TPU v7x, 32 devices: a whole 2x2x4 slice. The times are simulated.
32 devices in a mesh: freq: 2 (over y), gx: 4 (over z), gy: 2 (over x), col: 2 (over core).
Axes of the slice: x: 2, y: 2, z: 4, core: 2. Of those that a mesh axis runs over, the one named last changes fastest.
Arguments:
- source: bfloat16 [12, 64, 32, 256], P('freq', 'gx', 'gy', 'col'), parts along dimension 0, may hold values from -6 to 6
- warm: bfloat16 [12, 64, 32, 256], P('freq', 'gx', 'gy', 'col'), parts along dimension 0, may hold values from -2.1 to 2.6
- forward: bfloat16 [12, 64, 32, 256], P('freq', 'gx', 'gy', 'col'), parts along dimension 0, may hold values from -6 to 6
- density: bfloat16 [64, 32, 256], P('gx', 'gy', 'col'), may hold values from 1 to 3
- material_map: int32 [8, 4, 8], P('gx', 'gy', 'col'), may hold values from 0 to 7
- material_table: float32 [8, 2], replicated, may hold values from 0.5 to 2
- iface_cells: int32 [16, 256], P(('gx', 'gy', 'col')), may hold values from 0 to 32767, as said below
- impedance: float32 [2, 3], replicated, may hold values from 2 to 8
- omega2: float32 [2], P('freq'), parts along dimension 0, may hold values from 0.5 to 1
Outputs:
- adjoint: float32 [12, 64, 32, 256], P('freq', 'gx', 'gy', 'col'), parts along dimension 0
- coarse_gradient: float32 [32, 8], P('freq'), parts along dimension 0
There are 2 independent parts, one for each index of `freq`. A program takes and returns all parts, laid end to end along the dimension named above; an argument that names none is the same for every part. Nothing has to cross between parts.
Inputs may be any that keep to these rules, and one draw needn't show every extreme that they name: `iface_cells`: each row's entries are distinct, rising, and within the tile of 16 x 16 x 128 cells; row r belongs to the device of that index along gx, gy and col together.
All inputs are finite; a program needn't handle non-finite values.
Results may differ from a plain program's by a relative error of at most 0.0003.
Values may be sent and summed in bfloat16 or wider, within the bound.
No kernel may reach another device: no remote copies, remote signals or barrier semaphores. Data moves between devices by JAX's collectives and lax.ppermute only.
A program may use at most 64 MiB of HBM per device.

v0:
```python
import jax
import jax.numpy as jnp
from jax import lax
from jax.sharding import PartitionSpec as P

DAMPING = 0.5
RELAXATION = 0.6


def with_halo(array, sides, width):
    for axis, dim in sides:
        peers, length = (lax.axis_size(axis), array.shape[dim])
        up = [(i, (i + 1) % peers) for i in range(peers - 1)]
        down = [(j, i) for i, j in up]
        last = lax.slice_in_dim(array, length - width, length, axis=dim)
        initial = lax.slice_in_dim(array, 0, width, axis=dim)
        before = lax.ppermute(last, axis, up)
        after = lax.ppermute(initial, axis, down)
        array = jnp.concatenate([before, array, after], axis=dim)
    return array


def window(padded, offset):
    size_x = padded.shape[1] - 2
    size_y = padded.shape[2] - 2
    size_z = padded.shape[3] - 2
    return padded[
        :,
        1 + offset[0] : 1 + offset[0] + size_x,
        1 + offset[1] : 1 + offset[1] + size_y,
        1 + offset[2] : 1 + offset[2] + size_z,
    ]


def navier(padded, lame_first, shear):
    units = ((1, 0, 0), (0, 1, 0), (0, 0, 1))
    centre = window(padded, (0, 0, 0))
    second = []
    for axis_d in range(3):
        ahead = units[axis_d]
        behind = tuple((-value for value in ahead))
        second.append(window(padded, ahead) + window(padded, behind) - 2.0 * centre)
    laplace = second[0] + second[1] + second[2]
    result = []
    for part_index in range(2):
        for component in range(3):
            channel = part_index * 3 + component
            divergence = second[component][channel]
            for other_axis in range(3):
                if other_axis != component:
                    source_channel = part_index * 3 + other_axis
                    single = padded[source_channel : source_channel + 1]
                    first_unit = units[component]
                    other_unit = units[other_axis]
                    plus_plus = tuple((first_unit[k] + other_unit[k] for k in range(3)))
                    plus_minus = tuple((first_unit[k] - other_unit[k] for k in range(3)))
                    minus_plus = tuple((-first_unit[k] + other_unit[k] for k in range(3)))
                    minus_minus = tuple((-first_unit[k] - other_unit[k] for k in range(3)))
                    mixed = (
                        window(single, plus_plus)
                        - window(single, plus_minus)
                        - window(single, minus_plus)
                        + window(single, minus_minus)
                    )
                    divergence = divergence + 0.25 * mixed[0]
            result.append(shear * laplace[channel] + (lame_first + shear) * divergence)
    return jnp.stack(result)


def sweep(padded, lame_first, shear, density, mask, source, mean_field, omega_sq, impedance):
    field = window(padded, (0, 0, 0))
    elastic = navier(padded, lame_first, shear)
    real_part = field[:3]
    imag_part = field[3:]
    mean_real = mean_field[:3][:, None, None, None]
    mean_imag = mean_field[3:][:, None, None, None]
    imp_real = impedance[0][:, None, None, None]
    imp_imag = impedance[1][:, None, None, None]
    inertia = omega_sq * density
    diff_real = real_part - mean_real
    diff_imag = imag_part - mean_imag
    apply_real = (
        -elastic[:3]
        - inertia * (real_part - DAMPING * imag_part)
        + mask * (imp_real * diff_real - imp_imag * diff_imag)
    )
    apply_imag = (
        -elastic[3:]
        - inertia * (imag_part + DAMPING * real_part)
        + mask * (imp_real * diff_imag + imp_imag * diff_real)
    )
    resid_real = source[:3] - apply_real
    resid_imag = source[3:] - apply_imag
    diag_real = 8.0 * shear + 2.0 * lame_first - inertia + mask * imp_real
    diag_imag = -DAMPING * inertia + mask * imp_imag
    modulus = diag_real * diag_real + diag_imag * diag_imag
    new_real = real_part + RELAXATION * (resid_real * diag_real + resid_imag * diag_imag) / modulus
    new_imag = imag_part + RELAXATION * (resid_imag * diag_real - resid_real * diag_imag) / modulus
    return jnp.concatenate([new_real, new_imag], 0)


def expand(blocks):
    blocks_x, blocks_y, blocks_z = blocks.shape
    spread = jnp.broadcast_to(
        blocks[:, None, :, None, :, None], (blocks_x, 8, blocks_y, 8, blocks_z, 32)
    )
    return spread.reshape(blocks_x * 8, blocks_y * 8, blocks_z * 32)


def material(block_ids, table):
    lame_first = jnp.zeros(block_ids.shape, jnp.float32)
    shear = jnp.zeros(block_ids.shape, jnp.float32)
    for entry in range(table.shape[0]):
        chosen = block_ids == entry
        lame_first = jnp.where(chosen, table[entry, 0], lame_first)
        shear = jnp.where(chosen, table[entry, 1], shear)
    return (lame_first, shear)


def foundation(field, mask, count):
    total = lax.psum(jnp.sum(mask * field, axis=(1, 2, 3)), ("gx", "gy", "col"))
    return total / count


def shards(
    source, warm, forward, density, material_map, material_table, iface_cells, impedance, omega2
):
    omega_sq = omega2[0]
    tile_shape = density.shape
    tile_cells = tile_shape[0] * tile_shape[1] * tile_shape[2]
    mask = jnp.zeros((tile_cells,), jnp.float32).at[iface_cells[0]].set(1.0).reshape(tile_shape)
    block_ids = expand(material_map)
    lame_first, shear = material(block_ids, material_table)
    density_cells = density.astype(jnp.float32)
    source_cells = source.astype(jnp.float32)
    group_size = lax.axis_size("gx") * lax.axis_size("gy") * lax.axis_size("col")
    count = jnp.float32(group_size * iface_cells.shape[1])
    field = warm.astype(jnp.float32)
    for sweep_index in range(2):
        mean_field = foundation(field, mask, count)
        padded = with_halo(field, (("gx", 1), ("gy", 2), ("col", 3)), 1)
        field = sweep(
            padded,
            lame_first,
            shear,
            density_cells,
            mask,
            source_cells,
            mean_field,
            omega_sq,
            impedance,
        )
    forward_cells = forward.astype(jnp.float32)
    correlation = (
        field[:3] * forward_cells[:3]
        - field[3:] * forward_cells[3:]
        - DAMPING * (field[:3] * forward_cells[3:] + field[3:] * forward_cells[:3])
    )
    cell_terms = -omega_sq * jnp.sum(correlation, axis=0)
    coarse_x = tile_shape[0] // 4
    coarse_y = tile_shape[1] // 4
    local_sums = cell_terms.reshape(coarse_x, 4, coarse_y, 4, tile_shape[2]).sum(axis=(1, 3, 4))
    paired = lax.psum(local_sums, "col")
    gathered = lax.all_gather(paired[None], ("gx", "gy"), axis=0, tiled=True)
    grid_sums = gathered.reshape(lax.axis_size("gx"), lax.axis_size("gy"), coarse_x, coarse_y)
    coarse = (
        grid_sums.transpose(0, 2, 1, 3).reshape(
            lax.axis_size("gx") * coarse_x, lax.axis_size("gy") * coarse_y
        )
        / 64.0
    )
    return (field, coarse)


def solution(mesh):
    in_specs = (
        P("freq", "gx", "gy", "col"),
        P("freq", "gx", "gy", "col"),
        P("freq", "gx", "gy", "col"),
        P("gx", "gy", "col"),
        P("gx", "gy", "col"),
        P(),
        P(("gx", "gy", "col"), None),
        P(),
        P("freq"),
    )
    out_specs = (P("freq", "gx", "gy", "col"), P("freq", None))
    return jax.shard_map(shards, mesh=mesh, in_specs=in_specs, out_specs=out_specs, check_vma=False)
```

profile of v0, /device:TPU:0, one launch (start us, length us, event | category | flops | bytes accessed | tf_op | source)
XLA Modules:
  0.0 208.3 jit_solution(2462226845284078183)
XLA Ops:
  1.4 1.3 collective-permute-start
  2.7 5.6 %collective-permute-start.1 = (f32[6,1,16,128]{3,2,1,0:T(8,128)S(1)}, f32[6,1,16,128]{3,2,1,0:T(8,128)S(1)}, u32[]{:S(2)}, u32[]{:S(2)}) collective-permute-start(f32[6,1,16,128]{3,2,1,0:T(8,128)S(1)} %get-tuple-element.40), channel_id=1, source_target_pairs={{0,4},{4,8},{8,12},{1,5},{5,9},{9,13},{2,6},{6,10},{10,14},{3,7},{... | collective-permute-start | bytes 147464 | tf_op jit(solution)/shard_map/ppermute | solution.py:17
  8.3 2.0 fusion.108
  11.0 1.9 broadcast_select_fusion
  12.9 4.6 %select_select_fusion.1 = f32[2,8,2,8,4,32]{5,4,3,2,1,0:T(4,128)S(1)} fusion(f32[]{:T(128)} %bitcast, f32[]{:T(128)} %bitcast.1, f32[]{:T(128)} %bitcast.2, f32[]{:T(128)} %bitcast.3, f32[]{:T(128)} %bitcast.4, f32[2,2,4]{2,1,0:T(2,128)S(1)} %get-tuple-element.46, f32[]{:T(128)} %bitcast.6, f32[]{:T(128)} %bitcast.5, ...), kind=kLoop, calls=%fused_computation.41 | loop fusion | flops 229376 | bytes 131276 | tf_op jit(solution)/shard_map/jit(_where)/select_n | solution.py:116
  17.4 4.5 %select_select_fusion = f32[2,8,2,8,4,32]{5,4,3,2,1,0:T(4,128)S(1)} fusion(f32[]{:T(128)} %bitcast.8, f32[]{:T(128)} %bitcast.9, f32[]{:T(128)} %bitcast.10, f32[]{:T(128)} %bitcast.11, f32[]{:T(128)} %bitcast.12, f32[2,2,4]{2,1,0:T(2,128)S(1)} %get-tuple-element.45, f32[]{:T(128)} %bitcast.14, f32[]{:T(128)} %bitcast.13, ...), kind=kLoop, calls=%fused_computation.40 | loop fusion | flops 229376 | bytes 131276 | tf_op jit(solution)/shard_map/jit(_where)/select_n | solution.py:115
  22.0 8.9 %multiply_add_fusion = f32[2,8,2,8,4,32]{5,4,3,2,1,0:T(4,128)S(1)} fusion(f32[2,2,4]{2,1,0:T(2,128)S(1)} %get-tuple-element.46, f32[]{:T(128)} %bitcast.6, pred[2,2,4]{2,1,0:T(4,128)(4,1)S(1)} %get-tuple-element.53, f32[]{:T(128)} %bitcast.5, pred[2,2,4]{2,1,0:T(4,128)(4,1)S(1)} %get-tuple-element.48, f32[]{:T(128)} %bitcast.4, ...), kind=kLoop, calls=%fused_computation.39 | loop fusion | flops 557056 | bytes 131368 | tf_op jit(solution)/shard_map/add | solution.py:94
  32.8 1.3 collective-permute-start.2
  34.1 5.8 %collective-permute-start.3 = (f32[6,18,1,128]{3,2,1,0:T(1,128)S(1)}, f32[6,18,1,128]{3,2,1,0:T(1,128)}, u32[]{:S(2)}, u32[]{:S(2)}) collective-permute-start(f32[6,18,1,128]{3,2,1,0:T(1,128)S(1)} %get-tuple-element.34), channel_id=1, source_target_pairs={{0,2},{1,3},{4,6},{5,7},{8,10},{9,11},{12,14},{13,15},{16,18},{17,... | collective-permute-start | bytes 165896 | tf_op jit(solution)/shard_map/ppermute | solution.py:17
  41.7 1.0 convert_element_type.13
  42.7 2.0 scatter_custom_fusion
  44.7 1.0 pad_maximum_fusion.3
  46.2 1.6 copy.44
  47.8 1.3 collective-permute-start.4
  50.0 3.6 %collective-permute-start.5 = (f32[6,18,18,1]{2,1,3,0:T(8,128)S(1)}, f32[6,18,18,1]{2,1,3,0:T(8,128)}, u32[]{:S(2)}, u32[]{:S(2)}) collective-permute-start(f32[6,18,18,1]{2,1,3,0:T(8,128)S(1)} %copy.46), channel_id=1, source_target_pairs={{0,1},{2,3},{4,5},{6,7},{8,9},{10,11},{12,13},{14,15},{16,17},{18,... | collective-permute-start | bytes 23336 | tf_op jit(solution)/shard_map/ppermute | solution.py:17
  53.7 2.6 %pad_maximum_fusion.2 = (f32[6,18,17,128]{3,2,1,0:T(8,128)}, f32[6,18,17,128]{3,2,1,0:T(8,128)}) fusion(f32[6,18,1,128]{3,2,1,0:T(1,128)} %collective-permute-done.2, f32[6,1,16,128]{3,2,1,0:T(8,128)S(1)} %collective-permute-done, f32[6,16,16,128]{3,2,1,0:T(8,128)S(1)} %convert_element_type.12, f32[6,1,16,128]{3,2,1,0:T(8,128)S(1)} %collective-permute-done.1, ...), kind=kLoop, calls=%fused_computation.5 | loop fusion | flops 1410048 | bytes 2875392 | tf_op jit(solution)/shard_map/concatenate | solution.py:19
  57.0 1.7 copy.47
  58.7 3.1 %pad_maximum_fusion = (f32[6,18,18,129]{3,2,1,0:T(8,128)S(1)}, f32[6,18,18,129]{3,2,1,0:T(8,128)S(1)}) fusion(f32[6,18,18,1]{3,2,1,0:T(8,128)S(1)} %copy.45, f32[6,18,1,128]{3,2,1,0:T(1,128)} %collective-permute-done.2, f32[6,1,16,128]{3,2,1,0:T(8,128)S(1)} %collective-permute-done, f32[6,16,16,128]{3,2,1,0:T(8,128)S(1)} %convert_element_type.12, ...), kind=kLoop, calls=%fused_computation.1 | loop fusion | flops 2507760 | bytes 3017088 | tf_op jit(solution)/shard_map/concatenate | solution.py:19
  61.8 2.3 %add_add_fusion.1 = (f32[6,16,16,128]{3,2,1,0:T(8,128)}, f32[6,16,16,128]{3,2,1,0:T(8,128)}, f32[6,16,16,128]{3,2,1,0:T(8,128)}, f32[6,16,16,128]{3,2,1,0:T(8,128)}, f32[6]{0:T(128)S(1)}) fusion(bf16[6,16,16,128]{3,2,1,0:T(8,128)(2,1)S(1)} %copy-done.28, f32[6,18,17,128]{3,2,1,0:T(8,128)S(1)} %copy-done.17, f32[6,18,17,128]{3,2,1,0:T(8,128)S(1)} %copy-done.16, ...), kind=kLoop, calls=%fused_computation.38 | loop fusion | flops 2949114 | bytes 7700504 | tf_op jit(solution)/shard_map/add | solution.py:43
  64.2 29.5 %psum.21 = f32[6]{0:T(128)S(1)} all-reduce(f32[6]{0:T(128)S(1)} %get-tuple-element.39), channel_id=1, replica_groups=mesh['freq'=2,'gx'=4,'gy'=2,'col'=2] {'gx','gy','col'}, use_global_device_ids=true, to_apply=%region_2.3 | all-reduce | flops 6 | bytes 48 | tf_op jit(solution)/shard_map/psum | solution.py:121
  93.7 1.6 fusion.71
  95.4 1.4 fusion.89
  96.8 1.4 fusion.83
  98.3 1.4 fusion.65
  99.7 1.7 fusion.77
  101.5 1.7 fusion.59
  104.1 1.4 collective-permute-start.6
  105.5 4.5 %collective-permute-start.7 = (f32[6,1,16,128]{3,2,1,0:T(8,128)S(1)}, f32[6,1,16,128]{3,2,1,0:T(8,128)S(1)}, u32[]{:S(2)}, u32[]{:S(2)}) collective-permute-start(f32[6,1,16,128]{3,2,1,0:T(8,128)S(1)} %get-tuple-element.37), channel_id=1, source_target_pairs={{0,4},{4,8},{8,12},{1,5},{5,9},{9,13},{2,6},{6,10},{10,14},{3,7},{... | collective-permute-start | bytes 147464 | tf_op jit(solution)/shard_map/ppermute | solution.py:17
  110.2 1.6 collective-permute-done.7
  111.9 1.3 collective-permute-start.8
  113.2 4.7 %collective-permute-start.9 = (f32[6,18,1,128]{3,2,1,0:T(1,128)S(1)}, f32[6,18,1,128]{3,2,1,0:T(1,128)S(1)}, u32[]{:S(2)}, u32[]{:S(2)}) collective-permute-start(f32[6,18,1,128]{3,2,1,0:T(1,128)S(1)} %get-tuple-element.30), channel_id=1, source_target_pairs={{0,2},{1,3},{4,6},{5,7},{8,10},{9,11},{12,14},{13,15},{16,18},{17,... | collective-permute-start | bytes 165896 | tf_op jit(solution)/shard_map/ppermute | solution.py:17
  118.0 1.0 convert_element_type.15
  120.8 1.6 copy.48
  122.4 1.4 collective-permute-start.10
  124.8 3.6 %collective-permute-start.11 = (f32[6,18,18,1]{2,1,3,0:T(8,128)S(1)}, f32[6,18,18,1]{2,1,3,0:T(8,128)}, u32[]{:S(2)}, u32[]{:S(2)}) collective-permute-start(f32[6,18,18,1]{2,1,3,0:T(8,128)S(1)} %copy.50), channel_id=1, source_target_pairs={{0,1},{2,3},{4,5},{6,7},{8,9},{10,11},{12,13},{14,15},{16,17},{18,... | collective-permute-start | bytes 23336 | tf_op jit(solution)/shard_map/ppermute | solution.py:17
  128.4 1.7 pad_maximum_fusion.4
  130.9 1.7 copy.51
  132.6 3.6 %pad_maximum_fusion.1 = (f32[6,18,18,129]{3,2,1,0:T(8,128)S(1)}, f32[6,18,18,129]{3,2,1,0:T(8,128)S(1)}) fusion(f32[6,18,18,1]{3,2,1,0:T(8,128)S(1)} %copy.49, f32[6,18,1,128]{3,2,1,0:T(1,128)} %copy-done.10, f32[6,1,16,128]{3,2,1,0:T(8,128)S(1)} %collective-permute-done.6, f32[3,16,16,128]{3,2,1,0:T(8,128)S(1)} %divide_add_fusion.2, ...), kind=kLoop, calls=%fused_computation.3 | loop fusion | flops 3009312 | bytes 3017088 | tf_op jit(solution)/shard_map/concatenate | solution.py:19
  136.3 2.3 %add_add_fusion = (f32[6,16,16,128]{3,2,1,0:T(8,128)}, f32[6,16,16,128]{3,2,1,0:T(8,128)}, f32[6,16,16,128]{3,2,1,0:T(8,128)}, f32[6,16,16,128]{3,2,1,0:T(8,128)}, f32[6]{0:T(128)S(1)}) fusion(f32[3,16,16,128]{3,2,1,0:T(8,128)S(1)} %divide_add_fusion.2, f32[3,16,16,128]{3,2,1,0:T(8,128)S(1)} %get-tuple-element.11, f32[6,18,17,128]{3,2,1,0:T(8,128)S(1)} %copy-done.19, ...), kind=kLoop, calls=%fused_computation.36 | loop fusion | flops 3145722 | bytes 7307288 | tf_op jit(solution)/shard_map/add | solution.py:43
  138.6 29.5 %psum.22 = f32[6]{0:T(128)S(1)} all-reduce(f32[6]{0:T(128)S(1)} %get-tuple-element.36), channel_id=1, replica_groups=mesh['freq'=2,'gx'=4,'gy'=2,'col'=2] {'gx','gy','col'}, use_global_device_ids=true, to_apply=%region_4.5 | all-reduce | flops 6 | bytes 48 | tf_op jit(solution)/shard_map/psum | solution.py:121
  168.1 1.6 fusion.53
  169.8 1.3 fusion.35
  171.0 1.3 fusion.47
  172.3 1.3 fusion.29
  173.6 1.6 fusion.41
  175.3 1.7 fusion.23
  178.1 2.4 %psum.23 = f32[1,4,4]{2,1,0:T(4,128)S(1)} all-reduce(f32[1,4,4]{2,1,0:T(4,128)S(1)} %bitcast.39), channel_id=1, replica_groups=mesh['freq'=2,'gx'=4,'gy'=2,'col'=2] {'col'}, use_global_device_ids=true, to_apply=%region_8.9 | all-reduce | flops 16 | bytes 128 | tf_op jit(solution)/shard_map/psum | solution.py:163
  180.5 26.0 %all_gather.3 = f32[8,4,4]{2,1,0:T(4,128)S(1)} all-gather(f32[1,4,4]{2,1,0:T(4,128)S(1)} %psum.23), channel_id=1, replica_groups=mesh['freq'=2,'gx'=4,'gy'=2,'col'=2] {'gx','gy'}, dimensions={0}, use_global_device_ids=true | all-gather | bytes 576 | tf_op jit(solution)/shard_map/all_gather | solution.py:164
  (117 shorter events, 14.4 us)
Async XLA Ops:
  0.6 31.2 %copy-start.33 = (bf16[16,16,128]{2,1,0:T(8,128)(2,1)S(1)}, bf16[16,16,128]{2,1,0:T(8,128)(2,1)}, u32[]{:S(2)}) copy-start(bf16[16,16,128]{2,1,0:T(8,128)(2,1)} %param.12) | copy-start | bytes 196612
  1.4 31.2 %collective-permute-start = (f32[6,1,16,128]{3,2,1,0:T(8,128)S(1)}, f32[6,1,16,128]{3,2,1,0:T(8,128)S(1)}, u32[]{:S(2)}, u32[]{:S(2)}) collective-permute-start(f32[6,1,16,128]{3,2,1,0:T(8,128)S(1)} %get-tuple-element.41), channel_id=1, source_target_pairs={{4,0},{8,4},{12,8},{5,1},{9,5},{13,9},{6,2},{10,6},{14,10},{7,3},{... | collective-permute-start | bytes 147464 | tf_op jit(solution)/shard_map/ppermute | solution.py:18
  2.7 30.0 %collective-permute-start.1 = (f32[6,1,16,128]{3,2,1,0:T(8,128)S(1)}, f32[6,1,16,128]{3,2,1,0:T(8,128)S(1)}, u32[]{:S(2)}, u32[]{:S(2)}) collective-permute-start(f32[6,1,16,128]{3,2,1,0:T(8,128)S(1)} %get-tuple-element.40), channel_id=1, source_target_pairs={{0,4},{4,8},{8,12},{1,5},{5,9},{9,13},{2,6},{6,10},{10,14},{3,7},{... | collective-permute-start | bytes 147464 | tf_op jit(solution)/shard_map/ppermute | solution.py:17
  12.9 19.7 %copy-start.34 = (s32[1,256]{1,0:T(1,128)S(1)}, s32[1,256]{1,0:T(1,128)}, u32[]{:S(2)}) copy-start(s32[1,256]{1,0:T(1,128)} %param.15) | copy-start | bytes 3076
  12.9 19.7 %copy-start.27 = (bf16[6,16,16,128]{3,2,1,0:T(8,128)(2,1)S(1)}, bf16[6,16,16,128]{3,2,1,0:T(8,128)(2,1)}, u32[]{:S(2)}) copy-start(bf16[6,16,16,128]{3,2,1,0:T(8,128)(2,1)} %param.10) | copy-start | bytes 1179652
  31.8 8.1 %copy-start.35 = (f32[2,3]{1,0:T(2,128)S(1)}, f32[2,3]{1,0:T(2,128)}, u32[]{:S(2)}) copy-start(f32[2,3]{1,0:T(2,128)} %param.16) | copy-start | bytes 76
  32.7 9.0 %copy-start.31 = (bf16[6,16,16,128]{3,2,1,0:T(8,128)(2,1)S(1)}, bf16[6,16,16,128]{3,2,1,0:T(8,128)(2,1)}, u32[]{:S(2)}) copy-start(bf16[6,16,16,128]{3,2,1,0:T(8,128)(2,1)} %param.9) | copy-start | bytes 1179652
  32.8 11.9 %collective-permute-start.2 = (f32[6,18,1,128]{3,2,1,0:T(1,128)S(1)}, f32[6,18,1,128]{3,2,1,0:T(1,128)}, u32[]{:S(2)}, u32[]{:S(2)}) collective-permute-start(f32[6,18,1,128]{3,2,1,0:T(1,128)S(1)} %get-tuple-element.35), channel_id=1, source_target_pairs={{2,0},{3,1},{6,4},{7,5},{10,8},{11,9},{14,12},{15,13},{18,16},{19,... | collective-permute-start | bytes 165896 | tf_op jit(solution)/shard_map/ppermute | solution.py:18
  34.1 10.6 %collective-permute-start.3 = (f32[6,18,1,128]{3,2,1,0:T(1,128)S(1)}, f32[6,18,1,128]{3,2,1,0:T(1,128)}, u32[]{:S(2)}, u32[]{:S(2)}) collective-permute-start(f32[6,18,1,128]{3,2,1,0:T(1,128)S(1)} %get-tuple-element.34), channel_id=1, source_target_pairs={{0,2},{1,3},{4,6},{5,7},{8,10},{9,11},{12,14},{13,15},{16,18},{17,... | collective-permute-start | bytes 165896 | tf_op jit(solution)/shard_map/ppermute | solution.py:17
  47.8 8.5 %collective-permute-start.4 = (f32[6,18,18,1]{2,1,3,0:T(8,128)}, f32[6,18,18,1]{2,1,3,0:T(8,128)S(1)}, u32[]{:S(2)}, u32[]{:S(2)}) collective-permute-start(f32[6,18,18,1]{2,1,3,0:T(8,128)} %copy.44), channel_id=1, source_target_pairs={{1,0},{3,2},{5,4},{7,6},{9,8},{11,10},{13,12},{15,14},{17,16},{19,... | collective-permute-start | bytes 23336 | tf_op jit(solution)/shard_map/ppermute | solution.py:18
  50.0 7.0 %collective-permute-start.5 = (f32[6,18,18,1]{2,1,3,0:T(8,128)S(1)}, f32[6,18,18,1]{2,1,3,0:T(8,128)}, u32[]{:S(2)}, u32[]{:S(2)}) collective-permute-start(f32[6,18,18,1]{2,1,3,0:T(8,128)S(1)} %copy.46), channel_id=1, source_target_pairs={{0,1},{2,3},{4,5},{6,7},{8,9},{10,11},{12,13},{14,15},{16,17},{18,... | collective-permute-start | bytes 23336 | tf_op jit(solution)/shard_map/ppermute | solution.py:17
  58.7 3.1 %copy-start.6 = (f32[32768]{0:T(1024)S(1)}, f32[32768]{0:T(1024)}, u32[]{:S(2)}) copy-start(f32[32768]{0:T(1024)} %scatter_custom_fusion) | copy-start | bytes 393220
  58.7 3.1 %copy-start.16 = (f32[6,18,17,128]{3,2,1,0:T(8,128)S(1)}, f32[6,18,17,128]{3,2,1,0:T(8,128)}, u32[]{:S(2)}) copy-start(f32[6,18,17,128]{3,2,1,0:T(8,128)} %get-tuple-element.32) | copy-start | bytes 2820100
  58.7 3.1 %copy-start.17 = (f32[6,18,17,128]{3,2,1,0:T(8,128)S(1)}, f32[6,18,17,128]{3,2,1,0:T(8,128)}, u32[]{:S(2)}) copy-start(f32[6,18,17,128]{3,2,1,0:T(8,128)} %get-tuple-element.33) | copy-start | bytes 2820100
  58.7 3.1 %copy-start.28 = (bf16[6,16,16,128]{3,2,1,0:T(8,128)(2,1)S(1)}, bf16[6,16,16,128]{3,2,1,0:T(8,128)(2,1)}, u32[]{:S(2)}) copy-start(bf16[6,16,16,128]{3,2,1,0:T(8,128)(2,1)} %param.10) | copy-start | bytes 1179652
  93.7 1.6 copy-start
  93.7 1.7 copy-start.20
  95.3 6.1 %copy-start.2 = (f32[1,16,16,128]{3,2,1,0:T(8,128)}, f32[1,16,16,128]{3,2,1,0:T(8,128)S(1)}, u32[]{:S(2)}) copy-start(f32[1,16,16,128]{3,2,1,0:T(8,128)S(1)} %get-tuple-element.15) | copy-start | bytes 393220
  101.4 1.8 copy-start.4
  101.4 1.8 copy-start.7
  101.5 1.8 copy-start.23
  101.5 1.8 copy-start.25
  101.5 1.8 copy-start.29
  104.1 13.9 %copy-start.32 = (bf16[6,16,16,128]{3,2,1,0:T(8,128)(2,1)S(1)}, bf16[6,16,16,128]{3,2,1,0:T(8,128)(2,1)}, u32[]{:S(2)}) copy-start(bf16[6,16,16,128]{3,2,1,0:T(8,128)(2,1)} %param.11) | copy-start | bytes 1179652
  104.1 6.1 %collective-permute-start.6 = (f32[6,1,16,128]{3,2,1,0:T(8,128)S(1)}, f32[6,1,16,128]{3,2,1,0:T(8,128)S(1)}, u32[]{:S(2)}, u32[]{:S(2)}) collective-permute-start(f32[6,1,16,128]{3,2,1,0:T(8,128)S(1)} %get-tuple-element.38), channel_id=1, source_target_pairs={{4,0},{8,4},{12,8},{5,1},{9,5},{13,9},{6,2},{10,6},{14,10},{7,3},{... | collective-permute-start | bytes 147464 | tf_op jit(solution)/shard_map/ppermute | solution.py:18
  105.5 6.3 %collective-permute-start.7 = (f32[6,1,16,128]{3,2,1,0:T(8,128)S(1)}, f32[6,1,16,128]{3,2,1,0:T(8,128)S(1)}, u32[]{:S(2)}, u32[]{:S(2)}) collective-permute-start(f32[6,1,16,128]{3,2,1,0:T(8,128)S(1)} %get-tuple-element.37), channel_id=1, source_target_pairs={{0,4},{4,8},{8,12},{1,5},{5,9},{9,13},{2,6},{6,10},{10,14},{3,7},{... | collective-permute-start | bytes 147464 | tf_op jit(solution)/shard_map/ppermute | solution.py:17
  111.9 7.0 %collective-permute-start.8 = (f32[6,18,1,128]{3,2,1,0:T(1,128)S(1)}, f32[6,18,1,128]{3,2,1,0:T(1,128)S(1)}, u32[]{:S(2)}, u32[]{:S(2)}) collective-permute-start(f32[6,18,1,128]{3,2,1,0:T(1,128)S(1)} %get-tuple-element.31), channel_id=1, source_target_pairs={{2,0},{3,1},{6,4},{7,5},{10,8},{11,9},{14,12},{15,13},{18,16},{19,... | collective-permute-start | bytes 165896 | tf_op jit(solution)/shard_map/ppermute | solution.py:18
  113.2 6.3 %collective-permute-start.9 = (f32[6,18,1,128]{3,2,1,0:T(1,128)S(1)}, f32[6,18,1,128]{3,2,1,0:T(1,128)S(1)}, u32[]{:S(2)}, u32[]{:S(2)}) collective-permute-start(f32[6,18,1,128]{3,2,1,0:T(1,128)S(1)} %get-tuple-element.30), channel_id=1, source_target_pairs={{0,2},{1,3},{4,6},{5,7},{8,10},{9,11},{12,14},{13,15},{16,18},{17,... | collective-permute-start | bytes 165896 | tf_op jit(solution)/shard_map/ppermute | solution.py:17
  118.9 0.6 copy-start.10
  119.6 0.6 copy-start.13
  122.4 6.0 %copy-start.11 = (f32[6,18,1,128]{3,2,1,0:T(1,128)S(1)}, f32[6,18,1,128]{3,2,1,0:T(1,128)}, u32[]{:S(2)}) copy-start(f32[6,18,1,128]{3,2,1,0:T(1,128)} %copy-done.10) | copy-start | bytes 165892
  122.4 6.0 %copy-start.14 = (f32[6,18,1,128]{3,2,1,0:T(1,128)S(1)}, f32[6,18,1,128]{3,2,1,0:T(1,128)}, u32[]{:S(2)}) copy-start(f32[6,18,1,128]{3,2,1,0:T(1,128)} %copy-done.13) | copy-start | bytes 165892
  122.4 7.8 %collective-permute-start.10 = (f32[6,18,18,1]{2,1,3,0:T(8,128)}, f32[6,18,18,1]{2,1,3,0:T(8,128)S(1)}, u32[]{:S(2)}, u32[]{:S(2)}) collective-permute-start(f32[6,18,18,1]{2,1,3,0:T(8,128)} %copy.48), channel_id=1, source_target_pairs={{1,0},{3,2},{5,4},{7,6},{9,8},{11,10},{13,12},{15,14},{17,16},{19,... | collective-permute-start | bytes 23336 | tf_op jit(solution)/shard_map/ppermute | solution.py:18
  124.8 6.2 %collective-permute-start.11 = (f32[6,18,18,1]{2,1,3,0:T(8,128)S(1)}, f32[6,18,18,1]{2,1,3,0:T(8,128)}, u32[]{:S(2)}, u32[]{:S(2)}) collective-permute-start(f32[6,18,18,1]{2,1,3,0:T(8,128)S(1)} %copy.50), channel_id=1, source_target_pairs={{0,1},{2,3},{4,5},{6,7},{8,9},{10,11},{12,13},{14,15},{16,17},{18,... | collective-permute-start | bytes 23336 | tf_op jit(solution)/shard_map/ppermute | solution.py:17
  132.6 3.7 %copy-start.8 = (f32[32768]{0:T(1024)S(1)}, f32[32768]{0:T(1024)}, u32[]{:S(2)}) copy-start(f32[32768]{0:T(1024)} %scatter_custom_fusion) | copy-start | bytes 393220
  132.6 3.7 %copy-start.18 = (f32[6,18,17,128]{3,2,1,0:T(8,128)S(1)}, f32[6,18,17,128]{3,2,1,0:T(8,128)}, u32[]{:S(2)}) copy-start(f32[6,18,17,128]{3,2,1,0:T(8,128)} %get-tuple-element.28) | copy-start | bytes 2820100
  132.6 3.7 %copy-start.19 = (f32[6,18,17,128]{3,2,1,0:T(8,128)S(1)}, f32[6,18,17,128]{3,2,1,0:T(8,128)}, u32[]{:S(2)}) copy-start(f32[6,18,17,128]{3,2,1,0:T(8,128)} %get-tuple-element.29) | copy-start | bytes 2820100
  168.1 1.6 copy-start.1
  168.1 1.6 copy-start.3
  168.1 1.6 copy-start.12
  168.1 1.6 copy-start.15
  168.1 1.6 copy-start.22
  175.2 1.8 copy-start.5
  175.2 1.8 copy-start.9
  175.2 1.8 copy-start.21
  175.2 1.8 copy-start.24
  175.3 1.8 copy-start.26
  175.3 1.8 copy-start.30
where the time goes:
time: 210 us; the launch traced here: 208 us
  blocking collectives  87.4 us (42%)
  other arithmetic  61.2 us (29%)
  starting transfers between devices  35.9 us (17%)
  local copies, waits for them, and re-layouts  19.4 us (9%)
  waiting for transfers between devices  2.4 us (1%)
    psum x2, blocking collectives, foundation(): total = lax.psum(jnp.sum(mask * field, axis=(1, 2, 3)), ('gx', 'gy', 'col'))  58.9 us
    ppermute x6, starting transfers between devices, with_halo(): before = lax.ppermute(last, axis, up)  27.9 us
    all_gather x1, blocking collectives, shards(): gathered = lax.all_gather(paired[None], ('gx', 'gy'), axis=0, tiled=True)  26 us
    add x12, other arithmetic, navier(): result.append(shear * laplace[channel] + (lame_first + shear) * divergence)  18.1 us
    concatenate x8, other arithmetic, with_halo(): array = jnp.concatenate([before, array, after], axis=dim)  12.4 us
    add x1, other arithmetic, sweep(): diag_real = 8.0 * shear + 2.0 * lame_first - inertia + mask * imp_real  8.89 us
    ppermute x6, starting transfers between devices, with_halo(): after = lax.ppermute(initial, axis, down)  7.99 us
    select_n x2, other arithmetic, material(): lame_first = jnp.where(chosen, table[entry, 0], lame_first)  6.44 us
  transfers between devices with their start and end apart: 12, of which 3 were waited for; matrix products, arithmetic and copies ran while one was open for 18% of the time, Pallas kernels for 0%

commit v1 on v0

--- a/solution.py
+++ b/solution.py
@@ -67,27 +67,23 @@
     return jnp.stack(result)
 
 
-def sweep(padded, lame_first, shear, density, mask, source, mean_field, omega_sq, impedance):
+def sweep(padded, lame_first, shear, density, mask, source, omega_sq, impedance):
     field = window(padded, (0, 0, 0))
     elastic = navier(padded, lame_first, shear)
     real_part = field[:3]
     imag_part = field[3:]
-    mean_real = mean_field[:3][:, None, None, None]
-    mean_imag = mean_field[3:][:, None, None, None]
     imp_real = impedance[0][:, None, None, None]
     imp_imag = impedance[1][:, None, None, None]
     inertia = omega_sq * density
-    diff_real = real_part - mean_real
-    diff_imag = imag_part - mean_imag
     apply_real = (
         -elastic[:3]
         - inertia * (real_part - DAMPING * imag_part)
-        + mask * (imp_real * diff_real - imp_imag * diff_imag)
+        + mask * (imp_real * real_part - imp_imag * imag_part)
     )
     apply_imag = (
         -elastic[3:]
         - inertia * (imag_part + DAMPING * real_part)
-        + mask * (imp_real * diff_imag + imp_imag * diff_real)
+        + mask * (imp_real * imag_part + imp_imag * real_part)
     )
     resid_real = source[:3] - apply_real
     resid_imag = source[3:] - apply_imag
@@ -99,6 +95,47 @@
     return jnp.concatenate([new_real, new_imag], 0)
 
 
+def mean_gain(lame_first, shear, density, mask, omega_sq, impedance):
+    imp_real = impedance[0][:, None, None, None]
+    imp_imag = impedance[1][:, None, None, None]
+    inertia = omega_sq * density
+    diag_real = 8.0 * shear + 2.0 * lame_first - inertia + mask * imp_real
+    diag_imag = -DAMPING * inertia + mask * imp_imag
+    scale = RELAXATION * mask / (diag_real * diag_real + diag_imag * diag_imag)
+    gain_real = scale * (imp_real * diag_real + imp_imag * diag_imag)
+    gain_imag = scale * (imp_imag * diag_real - imp_real * diag_imag)
+    return gain_real, gain_imag
+
+
+def add_mean(field, gain_real, gain_imag, mean_field):
+    mean_real = mean_field[:3][:, None, None, None]
+    mean_imag = mean_field[3:][:, None, None, None]
+    new_real = field[:3] + (gain_real * mean_real - gain_imag * mean_imag)
+    new_imag = field[3:] + (gain_real * mean_imag + gain_imag * mean_real)
+    return jnp.concatenate([new_real, new_imag], 0)
+
+
+def group_sum(value, axes):
+    size = 1
+    for axis in axes:
+        size *= lax.axis_size(axis)
+    if size & (size - 1):
+        return lax.psum(value, axes)
+    stride = 1
+    while stride < size:
+        if stride * 4 <= size:
+            got = [
+                lax.ppermute(value, axes, [(i, i ^ (m * stride)) for i in range(size)])
+                for m in (1, 2, 3)
+            ]
+            value = (value + got[0]) + (got[1] + got[2])
+            stride *= 4
+        else:
+            value = value + lax.ppermute(value, axes, [(i, i ^ stride) for i in range(size)])
+            stride *= 2
+    return value
+
+
 def expand(blocks):
     blocks_x, blocks_y, blocks_z = blocks.shape
     spread = jnp.broadcast_to(
@@ -118,7 +155,7 @@
 
 
 def foundation(field, mask, count):
-    total = lax.psum(jnp.sum(mask * field, axis=(1, 2, 3)), ("gx", "gy", "col"))
+    total = group_sum(jnp.sum(mask * field, axis=(1, 2, 3)), ("gx", "gy", "col"))
     return total / count
 
 
@@ -129,12 +166,14 @@
     tile_shape = density.shape
     tile_cells = tile_shape[0] * tile_shape[1] * tile_shape[2]
     mask = jnp.zeros((tile_cells,), jnp.float32).at[iface_cells[0]].set(1.0).reshape(tile_shape)
-    block_ids = expand(material_map)
-    lame_first, shear = material(block_ids, material_table)
+    lame_tiles, shear_tiles = material(material_map, material_table)
+    lame_first = expand(lame_tiles)
+    shear = expand(shear_tiles)
     density_cells = density.astype(jnp.float32)
     source_cells = source.astype(jnp.float32)
     group_size = lax.axis_size("gx") * lax.axis_size("gy") * lax.axis_size("col")
     count = jnp.float32(group_size * iface_cells.shape[1])
+    gain_real, gain_imag = mean_gain(lame_first, shear, density_cells, mask, omega_sq, impedance)
     field = warm.astype(jnp.float32)
     for sweep_index in range(2):
         mean_field = foundation(field, mask, count)
@@ -146,10 +185,10 @@
             density_cells,
             mask,
             source_cells,
-            mean_field,
             omega_sq,
             impedance,
         )
+        field = add_mean(field, gain_real, gain_imag, mean_field)
     forward_cells = forward.astype(jnp.float32)
     correlation = (
         field[:3] * forward_cells[:3]
@@ -160,15 +199,13 @@
     coarse_x = tile_shape[0] // 4
     coarse_y = tile_shape[1] // 4
     local_sums = cell_terms.reshape(coarse_x, 4, coarse_y, 4, tile_shape[2]).sum(axis=(1, 3, 4))
-    paired = lax.psum(local_sums, "col")
-    gathered = lax.all_gather(paired[None], ("gx", "gy"), axis=0, tiled=True)
-    grid_sums = gathered.reshape(lax.axis_size("gx"), lax.axis_size("gy"), coarse_x, coarse_y)
-    coarse = (
-        grid_sums.transpose(0, 2, 1, 3).reshape(
-            lax.axis_size("gx") * coarse_x, lax.axis_size("gy") * coarse_y
-        )
-        / 64.0
-    )
+    grid = jnp.zeros(
+        (lax.axis_size("gx") * coarse_x, lax.axis_size("gy") * coarse_y), jnp.float32
+    )
+    grid = lax.dynamic_update_slice(
+        grid, local_sums, (lax.axis_index("gx") * coarse_x, lax.axis_index("gy") * coarse_y)
+    )
+    coarse = group_sum(grid, ("gx", "gy", "col")) / 64.0
     return (field, coarse)
 
 

time: 210 us -> 145 us (0.69)
  blocking collectives: 87.4 us -> 0 us
  starting transfers between devices: 35.9 us -> 57.5 us
  waiting for transfers between devices: 2.4 us -> 14.6 us
  other arithmetic: 61.2 us -> 50 us
    psum x3 -> x0, blocking collectives: 61.4 us -> none  [the longest x2 58.9 us: foundation(): total = lax.psum(jnp.sum(mask * field, axis=(1, 2, 3)), ('gx', 'gy', 'col'))]
    all_gather x1 -> x0, blocking collectives: 26 us -> none  [shards(): gathered = lax.all_gather(paired[None], ('gx', 'gy'), axis=0, tiled=True)]
    ppermute x0 -> x18, starting transfers between devices: none -> 20.4 us  [group_sum(): lax.ppermute(value, axes, [(i, i ^ m * stride) for i in range(size)])]
    ppermute x0 -> x18, waiting for transfers between devices: none -> 12.6 us  [group_sum(): lax.ppermute(value, axes, [(i, i ^ m * stride) for i in range(size)])]
    select_n x3 -> x0, other arithmetic: 11 us -> none  [the longest x2 6.44 us: material(): lame_first = jnp.where(chosen, table[entry, 0], lame_first)]
    add x2, other arithmetic: 4.62 us -> 1.32 us  [navier(): laplace = second[0] + second[1] + second[2]]
  transfers between devices with their start and end apart: 12 -> 30, of which waited for: 3 -> 9; matrix products, arithmetic and copies ran while one was open for 18% -> 33% of each run, Pallas kernels for 0% -> 0%
where the time goes in v1:
time: 145 us; the launch traced here: 143 us
  starting transfers between devices  57.5 us (40%)
  other arithmetic  50 us (34%)
  local copies, waits for them, and re-layouts  19.2 us (13%)
  waiting for transfers between devices  14.6 us (10%)
  between operations  2.04 us (1%)
    ppermute x6, starting transfers between devices, with_halo(): before = lax.ppermute(last, axis, up)  28.9 us
    ppermute x18, starting transfers between devices, group_sum(): lax.ppermute(value, axes, [(i, i ^ m * stride) for i in range(size)])  20.4 us
    add x12, other arithmetic, navier(): result.append(shear * laplace[channel] + (lame_first + shear) * divergence)  16.5 us
    concatenate x8, other arithmetic, with_halo(): array = jnp.concatenate([before, array, after], axis=dim)  14 us
    ppermute x18, waiting for transfers between devices, group_sum(): lax.ppermute(value, axes, [(i, i ^ m * stride) for i in range(size)])  12.6 us
    add x1, other arithmetic, sweep(): diag_real = 8.0 * shear + 2.0 * lame_first - inertia + mask * imp_real  10.7 us
    ppermute x6, starting transfers between devices, with_halo(): after = lax.ppermute(initial, axis, down)  8.17 us
    slice x4, local copies, waits for them, and re-layouts, with_halo(): initial = lax.slice_in_dim(array, 0, width, axis=dim)  3.96 us
  transfers between devices with their start and end apart: 30, of which 9 were waited for; matrix products, arithmetic and copies ran while one was open for 33% of the time, Pallas kernels for 0%

profile of v1, /device:TPU:0, one launch (start us, length us, event | category | flops | bytes accessed | tf_op | source)
XLA Modules:
  0.0 143.2 jit_solution(9365155517474968842)
XLA Ops:
  1.5 1.3 collective-permute-start
  2.8 5.6 %collective-permute-start.1 = (f32[6,1,16,128]{3,2,1,0:T(8,128)S(1)}, f32[6,1,16,128]{3,2,1,0:T(8,128)S(1)}, u32[]{:S(2)}, u32[]{:S(2)}) collective-permute-start(f32[6,1,16,128]{3,2,1,0:T(8,128)S(1)} %get-tuple-element.45), channel_id=1, source_target_pairs={{0,4},{4,8},{8,12},{1,5},{5,9},{9,13},{2,6},{6,10},{10,14},{3,7},{... | collective-permute-start | bytes 147464 | tf_op jit(solution)/shard_map/ppermute | solution.py:17
  9.0 2.0 %fusion.109 = (f32[1,1]{0,1:T(1,128)}, f32[1,1]{0,1:T(1,128)}, f32[1,1]{0,1:T(1,128)}, f32[1,1]{0,1:T(1,128)}, f32[1,1]{0,1:T(1,128)}, /*index=5*/f32[1,1]{0,1:T...) fusion(f32[8,2]{0,1:T(2,128)} %param.14), kind=kLoop, calls=%fused_computation.262 | loop fusion | bytes 128 | tf_op jit(solution)/shard_map/slice | solution.py:152
  11.0 10.7 %multiply_add_fusion.3 = (f32[2,2,4]{2,1,0:T(2,128)S(1)}, f32[2,2,4]{2,1,0:T(2,128)S(1)}, f32[2,2,4]{2,1,0:T(2,128)S(1)}) fusion(f32[]{:T(128)} %bitcast.7, s32[2,2,4]{2,1,0:T(2,128)} %param.13, f32[]{:T(128)} %bitcast.6, f32[]{:T(128)} %bitcast.5, f32[]{:T(128)} %bitcast.4, f32[]{:T(128)} %bitcast.3, f32[]{:T(128)} %bitcast.2, f32[]{:T(128)} %bitcast.1, ...), kind=kLoop, calls=%fused_computation.242 | loop fusion | flops 432 | bytes 320 | tf_op jit(solution)/shard_map/add | solution.py:90
  22.8 1.5 %scatter_custom_fusion = f32[32768]{0:T(1024)S(1)} fusion(s32[256]{0:T(256)S(1)} %bitcast.33, f32[256]{0:T(256)S(1)} %broadcast.133, f32[]{:T(128)} %constant.8.clone.1), kind=kCustom, calls=%fused_computation.226 | custom fusion | bytes 131076 | tf_op jit(solution)/shard_map/scatter | solution.py:168
  26.0 1.4 collective-permute-start.2
  27.4 5.8 %collective-permute-start.3 = (f32[6,18,1,128]{3,2,1,0:T(1,128)S(1)}, f32[6,18,1,128]{3,2,1,0:T(1,128)}, u32[]{:S(2)}, u32[]{:S(2)}) collective-permute-start(f32[6,18,1,128]{3,2,1,0:T(1,128)S(1)} %get-tuple-element.39), channel_id=1, source_target_pairs={{0,2},{1,3},{4,6},{5,7},{8,10},{9,11},{12,14},{13,15},{16,18},{17,... | collective-permute-start | bytes 165896 | tf_op jit(solution)/shard_map/ppermute | solution.py:17
  37.7 1.6 %copy.28 = f32[6,18,18,1]{2,1,3,0:T(8,128)} copy(f32[6,18,18,1]{3,2,1,0:T(8,128)S(1)} %get-tuple-element.27) | data formatting | bytes 15552 | tf_op jit(solution)/shard_map/slice | solution.py:16
  39.3 1.3 collective-permute-start.4
  41.5 3.6 %collective-permute-start.5 = (f32[6,18,18,1]{2,1,3,0:T(8,128)S(1)}, f32[6,18,18,1]{2,1,3,0:T(8,128)}, u32[]{:S(2)}, u32[]{:S(2)}) collective-permute-start(f32[6,18,18,1]{2,1,3,0:T(8,128)S(1)} %copy.30), channel_id=1, source_target_pairs={{0,1},{2,3},{4,5},{6,7},{8,9},{10,11},{12,13},{14,15},{16,17},{18,... | collective-permute-start | bytes 23336 | tf_op jit(solution)/shard_map/ppermute | solution.py:17
  45.2 2.5 %pad_maximum_fusion.2 = (f32[6,18,17,128]{3,2,1,0:T(8,128)}, f32[6,18,17,128]{3,2,1,0:T(8,128)}) fusion(f32[6,18,1,128]{3,2,1,0:T(1,128)} %collective-permute-done.2, f32[6,1,16,128]{3,2,1,0:T(8,128)S(1)} %collective-permute-done, f32[6,16,16,128]{3,2,1,0:T(8,128)S(1)} %convert_element_type.12, f32[6,1,16,128]{3,2,1,0:T(8,128)S(1)} %collective-permute-done.1, ...), kind=kLoop, calls=%fused_computation.5 | loop fusion | flops 1410048 | bytes 2875392 | tf_op jit(solution)/shard_map/concatenate | solution.py:19
  48.5 1.7 %copy.31 = f32[6,18,18,1]{3,2,1,0:T(8,128)S(1)} copy(f32[6,18,18,1]{2,1,3,0:T(8,128)} %collective-permute-done.5) | data formatting | bytes 15552 | tf_op jit(solution)/shard_map/ppermute | solution.py:17
  50.2 3.1 %pad_maximum_fusion = (f32[6,18,18,129]{3,2,1,0:T(8,128)S(1)}, f32[6,18,18,129]{3,2,1,0:T(8,128)S(1)}) fusion(f32[6,18,18,1]{3,2,1,0:T(8,128)S(1)} %copy.29, f32[6,18,1,128]{3,2,1,0:T(1,128)} %collective-permute-done.2, f32[6,1,16,128]{3,2,1,0:T(8,128)S(1)} %collective-permute-done, f32[6,16,16,128]{3,2,1,0:T(8,128)S(1)} %convert_element_type.12, ...), kind=kLoop, calls=%fused_computation.1 | loop fusion | flops 2507760 | bytes 3017088 | tf_op jit(solution)/shard_map/concatenate | solution.py:19
  54.7 1.3 collective-permute-start.8
  56.0 1.2 fusion.72
  58.4 1.3 fusion.84
  59.8 1.3 fusion.66
  61.0 1.6 %fusion.78 = f32[1,16,16,128]{3,2,1,0:T(8,128)S(1)} fusion(f32[1,16,16,128]{3,2,1,0:T(8,128)S(1)} %get-tuple-element.20, f32[6,18,18,1]{3,2,1,0:T(8,128)S(1)} %copy.31, f32[6,18,1,128]{3,2,1,0:T(1,128)} %collective-permute-done.2, f32[6,18,1,128]{3,2,1,0:T(1,128)} %collective-permute-done.3, f32[6,1,16,128]{3,2,1,0:T(8,128)S(1)} %collective-permute-done, ...), kind=kLoop, calls=%fused_computation.187 | loop fusion | flops 1736704 | bytes 1666240 | tf_op jit(solution)/shard_map/add | solution.py:66
  62.7 1.6 %fusion.60 = f32[1,16,16,128]{3,2,1,0:T(8,128)S(1)} fusion(f32[1,16,16,128]{3,2,1,0:T(8,128)S(1)} %get-tuple-element.20, f32[6,18,18,1]{3,2,1,0:T(8,128)S(1)} %copy.31, f32[6,18,1,128]{3,2,1,0:T(1,128)} %collective-permute-done.2, f32[6,18,1,128]{3,2,1,0:T(1,128)} %collective-permute-done.3, f32[6,1,16,128]{3,2,1,0:T(8,128)S(1)} %collective-permute-done, ...), kind=kLoop, calls=%fused_computation.148 | loop fusion | flops 1736704 | bytes 1666240 | tf_op jit(solution)/shard_map/add | solution.py:66
  64.4 3.1 %collective-permute-start.10 = (f32[6]{0:T(128)S(1)}, f32[6]{0:T(128)S(1)}, u32[]{:S(2)}, u32[]{:S(2)}) collective-permute-start(f32[6]{0:T(128)S(1)} %add_add_fusion.6), channel_id=1, source_target_pairs={{0,8},{1,9},{2,10},{3,11},{4,12},{5,13},{6,14},{7,15},{8,0},{9,1},... | collective-permute-start | bytes 80 | tf_op jit(solution)/shard_map/ppermute | solution.py:128
  67.5 1.4 collective-permute-start.11
  69.0 3.8 %collective-permute-done.11 = f32[6]{0:T(128)S(1)} collective-permute-done((f32[6]{0:T(128)S(1)}, f32[6]{0:T(128)S(1)}, u32[]{:S(2)}, u32[]{:S(2)}) %collective-permute-start.11) | collective-permute-done | bytes 56 | tf_op jit(solution)/shard_map/ppermute | solution.py:128
  74.1 1.6 %collective-permute-start.12 = (f32[6,1,16,128]{3,2,1,0:T(8,128)S(1)}, f32[6,1,16,128]{3,2,1,0:T(8,128)S(1)}, u32[]{:S(2)}, u32[]{:S(2)}) collective-permute-start(f32[6,1,16,128]{3,2,1,0:T(8,128)S(1)} %get-tuple-element.43), channel_id=1, source_target_pairs={{4,0},{8,4},{12,8},{5,1},{9,5},{13,9},{6,2},{10,6},{14,10},{7,3},{... | collective-permute-start | bytes 147464 | tf_op jit(solution)/shard_map/ppermute | solution.py:18
  75.7 4.5 %collective-permute-start.13 = (f32[6,1,16,128]{3,2,1,0:T(8,128)S(1)}, f32[6,1,16,128]{3,2,1,0:T(8,128)S(1)}, u32[]{:S(2)}, u32[]{:S(2)}) collective-permute-start(f32[6,1,16,128]{3,2,1,0:T(8,128)S(1)} %get-tuple-element.42), channel_id=1, source_target_pairs={{0,4},{4,8},{8,12},{1,5},{5,9},{9,13},{2,6},{6,10},{10,14},{3,7},{... | collective-permute-start | bytes 147464 | tf_op jit(solution)/shard_map/ppermute | solution.py:17
  80.3 1.7 %collective-permute-done.13 = f32[6,1,16,128]{3,2,1,0:T(8,128)S(1)} collective-permute-done((f32[6,1,16,128]{3,2,1,0:T(8,128)S(1)}, f32[6,1,16,128]{3,2,1,0:T(8,128)S(1)}, u32[]{:S(2)}, u32[]{:S(2)}) %collective-permute-start.13) | collective-permute-done | bytes 49184 | tf_op jit(solution)/shard_map/ppermute | solution.py:17
  82.1 1.3 collective-permute-start.14
  83.4 5.8 %collective-permute-start.15 = (f32[6,18,1,128]{3,2,1,0:T(1,128)S(1)}, f32[6,18,1,128]{3,2,1,0:T(1,128)}, u32[]{:S(2)}, u32[]{:S(2)}) collective-permute-start(f32[6,18,1,128]{3,2,1,0:T(1,128)S(1)} %get-tuple-element.35), channel_id=1, source_target_pairs={{0,2},{1,3},{4,6},{5,7},{8,10},{9,11},{12,14},{13,15},{16,18},{17,... | collective-permute-start | bytes 165896 | tf_op jit(solution)/shard_map/ppermute | solution.py:17
  91.8 1.6 %copy.32 = f32[6,18,18,1]{2,1,3,0:T(8,128)} copy(f32[6,18,18,1]{3,2,1,0:T(8,128)S(1)} %get-tuple-element.25) | data formatting | bytes 15552 | tf_op jit(solution)/shard_map/slice | solution.py:16
  93.3 1.3 collective-permute-start.16
  95.6 3.6 %collective-permute-start.17 = (f32[6,18,18,1]{2,1,3,0:T(8,128)S(1)}, f32[6,18,18,1]{2,1,3,0:T(8,128)}, u32[]{:S(2)}, u32[]{:S(2)}) collective-permute-start(f32[6,18,18,1]{2,1,3,0:T(8,128)S(1)} %copy.34), channel_id=1, source_target_pairs={{0,1},{2,3},{4,5},{6,7},{8,9},{10,11},{12,13},{14,15},{16,17},{18,... | collective-permute-start | bytes 23336 | tf_op jit(solution)/shard_map/ppermute | solution.py:17
  99.2 2.5 %pad_maximum_fusion.4 = (f32[6,18,17,128]{3,2,1,0:T(8,128)}, f32[6,18,17,128]{3,2,1,0:T(8,128)}) fusion(f32[6,18,1,128]{3,2,1,0:T(1,128)} %collective-permute-done.14, f32[6,1,16,128]{3,2,1,0:T(8,128)S(1)} %collective-permute-done.12, f32[3,16,16,128]{3,2,1,0:T(8,128)S(1)} %add_add_fusion.3, f32[3,16,16,128]{3,2,1,0:T(8,128)S(1)} %get-tuple-element.13, ...), kind=kLoop, calls=%fused_computation.8 | loop fusion | flops 1880064 | bytes 2875392 | tf_op jit(solution)/shard_map/concatenate | solution.py:19
  102.5 1.7 %copy.35 = f32[6,18,18,1]{3,2,1,0:T(8,128)S(1)} copy(f32[6,18,18,1]{2,1,3,0:T(8,128)} %collective-permute-done.17) | data formatting | bytes 15552 | tf_op jit(solution)/shard_map/ppermute | solution.py:17
  104.2 3.6 %pad_maximum_fusion.1 = (f32[6,18,18,129]{3,2,1,0:T(8,128)S(1)}, f32[6,18,18,129]{3,2,1,0:T(8,128)S(1)}) fusion(f32[6,18,18,1]{3,2,1,0:T(8,128)S(1)} %copy.33, f32[6,18,1,128]{3,2,1,0:T(1,128)} %collective-permute-done.14, f32[6,1,16,128]{3,2,1,0:T(8,128)S(1)} %collective-permute-done.12, f32[3,16,16,128]{3,2,1,0:T(8,128)S(1)} %add_add_fusion.3, ...), kind=kLoop, calls=%fused_computation.3 | loop fusion | flops 3009312 | bytes 3017088 | tf_op jit(solution)/shard_map/concatenate | solution.py:19
  108.6 2.5 %collective-permute-start.19 = (f32[6]{0:T(128)S(1)}, f32[6]{0:T(128)S(1)}, u32[]{:S(2)}, u32[]{:S(2)}) collective-permute-start(f32[6]{0:T(128)S(1)} %get-tuple-element.41), channel_id=1, source_target_pairs={{0,2},{1,3},{2,0},{3,1},{4,6},{5,7},{6,4},{7,5},{8,10},{9,11},{10,... | collective-permute-start | bytes 80 | tf_op jit(solution)/shard_map/ppermute | solution.py:128
  113.6 1.3 fusion.48
  114.9 1.3 fusion.30
  116.2 1.6 %fusion.42 = f32[1,16,16,128]{3,2,1,0:T(8,128)S(1)} fusion(f32[1,16,16,128]{3,2,1,0:T(8,128)S(1)} %copy-done.3, f32[6,18,18,1]{3,2,1,0:T(8,128)S(1)} %copy.35, f32[6,18,1,128]{3,2,1,0:T(1,128)} %collective-permute-done.14, f32[6,18,1,128]{3,2,1,0:T(1,128)} %collective-permute-done.15, f32[6,1,16,128]{3,2,1,0:T(8,128)S(1)} %collective-permute-done.12, ...), kind=kLoop, calls=%fused_computation.109 | loop fusion | flops 1998848 | bytes 1666240 | tf_op jit(solution)/shard_map/add | solution.py:66
  117.9 1.6 %fusion.24 = f32[1,16,16,128]{3,2,1,0:T(8,128)S(1)} fusion(f32[1,16,16,128]{3,2,1,0:T(8,128)S(1)} %copy-done.3, f32[6,18,18,1]{3,2,1,0:T(8,128)S(1)} %copy.35, f32[6,18,1,128]{3,2,1,0:T(1,128)} %collective-permute-done.14, f32[6,18,1,128]{3,2,1,0:T(1,128)} %collective-permute-done.15, f32[6,1,16,128]{3,2,1,0:T(8,128)S(1)} %collective-permute-done.12, ...), kind=kLoop, calls=%fused_computation.70 | loop fusion | flops 1998848 | bytes 1666240 | tf_op jit(solution)/shard_map/add | solution.py:66
  119.6 2.4 %collective-permute-start.21 = (f32[6]{0:T(128)S(1)}, f32[6]{0:T(128)S(1)}, u32[]{:S(2)}, u32[]{:S(2)}) collective-permute-start(f32[6]{0:T(128)S(1)} %add_add_fusion.5), channel_id=1, source_target_pairs={{0,4},{1,5},{2,6},{3,7},{4,0},{5,1},{6,2},{7,3},{8,12},{9,13},{10,... | collective-permute-start | bytes 80 | tf_op jit(solution)/shard_map/ppermute | solution.py:128
  122.5 1.9 %collective-permute-start.23 = (f32[6]{0:T(128)S(1)}, f32[6]{0:T(128)S(1)}, u32[]{:S(2)}, u32[]{:S(2)}) collective-permute-start(f32[6]{0:T(128)S(1)} %add_add_fusion.5), channel_id=1, source_target_pairs={{0,12},{1,13},{2,14},{3,15},{4,8},{5,9},{6,10},{7,11},{8,4},{9,5},... | collective-permute-start | bytes 80 | tf_op jit(solution)/shard_map/ppermute | solution.py:128
  124.4 2.0 %collective-permute-done.22 = f32[6]{0:T(128)S(1)} collective-permute-done((f32[6]{0:T(128)S(1)}, f32[6]{0:T(128)S(1)}, u32[]{:S(2)}, u32[]{:S(2)}) %collective-permute-start.22) | collective-permute-done | bytes 56 | tf_op jit(solution)/shard_map/ppermute | solution.py:128
  126.4 1.5 %collective-permute-done.23 = f32[6]{0:T(128)S(1)} collective-permute-done((f32[6]{0:T(128)S(1)}, f32[6]{0:T(128)S(1)}, u32[]{:S(2)}, u32[]{:S(2)}) %collective-permute-start.23) | collective-permute-done | bytes 56 | tf_op jit(solution)/shard_map/ppermute | solution.py:128
  129.7 2.0 %collective-permute-start.25 = (f32[16,8]{1,0:T(8,128)S(1)}, f32[16,8]{1,0:T(8,128)S(1)}, u32[]{:S(2)}, u32[]{:S(2)}) collective-permute-start(f32[16,8]{1,0:T(8,128)S(1)} %dynamic_update_slice.5), channel_id=1, source_target_pairs={{0,2},{1,3},{2,0},{3,1},{4,6},{5,7},{6,4},{7,5},{8,10},{9,11},{10,... | collective-permute-start | bytes 1544 | tf_op jit(solution)/shard_map/ppermute | solution.py:128
  132.1 1.3 collective-permute-done.25
  133.4 1.3 collective-permute-done.26
  134.7 2.4 %collective-permute-start.28 = (f32[16,8]{1,0:T(8,128)S(1)}, f32[16,8]{1,0:T(8,128)S(1)}, u32[]{:S(2)}, u32[]{:S(2)}) collective-permute-start(f32[16,8]{1,0:T(8,128)S(1)} %add_add_fusion.4), channel_id=1, source_target_pairs={{0,8},{1,9},{2,10},{3,11},{4,12},{5,13},{6,14},{7,15},{8,0},{9,1},... | collective-permute-start | bytes 1544 | tf_op jit(solution)/shard_map/ppermute | solution.py:128
  137.1 2.0 %collective-permute-start.29 = (f32[16,8]{1,0:T(8,128)S(1)}, f32[16,8]{1,0:T(8,128)S(1)}, u32[]{:S(2)}, u32[]{:S(2)}) collective-permute-start(f32[16,8]{1,0:T(8,128)S(1)} %add_add_fusion.4), channel_id=1, source_target_pairs={{0,12},{1,13},{2,14},{3,15},{4,8},{5,9},{6,10},{7,11},{8,4},{9,5},... | collective-permute-start | bytes 1544 | tf_op jit(solution)/shard_map/ppermute | solution.py:128
  140.0 2.5 %collective-permute-done.29 = f32[16,8]{1,0:T(8,128)S(1)} collective-permute-done((f32[16,8]{1,0:T(8,128)S(1)}, f32[16,8]{1,0:T(8,128)S(1)}, u32[]{:S(2)}, u32[]{:S(2)}) %collective-permute-start.29) | collective-permute-done | bytes 544 | tf_op jit(solution)/shard_map/ppermute | solution.py:128
  (141 shorter events, 25.9 us)
Async XLA Ops:
  0.6 25.2 %copy-start.20 = (bf16[6,16,16,128]{3,2,1,0:T(8,128)(2,1)S(1)}, bf16[6,16,16,128]{3,2,1,0:T(8,128)(2,1)}, u32[]{:S(2)}) copy-start(bf16[6,16,16,128]{3,2,1,0:T(8,128)(2,1)} %param.10) | copy-start | bytes 1179652
  0.6 23.7 %copy-start.27 = (bf16[16,16,128]{2,1,0:T(8,128)(2,1)S(1)}, bf16[16,16,128]{2,1,0:T(8,128)(2,1)}, u32[]{:S(2)}) copy-start(bf16[16,16,128]{2,1,0:T(8,128)(2,1)} %param.12) | copy-start | bytes 196612
  1.5 24.4 %collective-permute-start = (f32[6,1,16,128]{3,2,1,0:T(8,128)S(1)}, f32[6,1,16,128]{3,2,1,0:T(8,128)S(1)}, u32[]{:S(2)}, u32[]{:S(2)}) collective-permute-start(f32[6,1,16,128]{3,2,1,0:T(8,128)S(1)} %get-tuple-element.46), channel_id=1, source_target_pairs={{4,0},{8,4},{12,8},{5,1},{9,5},{13,9},{6,2},{10,6},{14,10},{7,3},{... | collective-permute-start | bytes 147464 | tf_op jit(solution)/shard_map/ppermute | solution.py:18
  2.8 23.1 %collective-permute-start.1 = (f32[6,1,16,128]{3,2,1,0:T(8,128)S(1)}, f32[6,1,16,128]{3,2,1,0:T(8,128)S(1)}, u32[]{:S(2)}, u32[]{:S(2)}) collective-permute-start(f32[6,1,16,128]{3,2,1,0:T(8,128)S(1)} %get-tuple-element.45), channel_id=1, source_target_pairs={{0,4},{4,8},{8,12},{1,5},{5,9},{9,13},{2,6},{6,10},{10,14},{3,7},{... | collective-permute-start | bytes 147464 | tf_op jit(solution)/shard_map/ppermute | solution.py:17
  25.1 8.1 %copy-start.28 = (f32[2,3]{1,0:T(2,128)S(1)}, f32[2,3]{1,0:T(2,128)}, u32[]{:S(2)}) copy-start(f32[2,3]{1,0:T(2,128)} %param.16) | copy-start | bytes 76
  26.0 9.4 %copy-start.25 = (bf16[6,16,16,128]{3,2,1,0:T(8,128)(2,1)S(1)}, bf16[6,16,16,128]{3,2,1,0:T(8,128)(2,1)}, u32[]{:S(2)}) copy-start(bf16[6,16,16,128]{3,2,1,0:T(8,128)(2,1)} %param.9) | copy-start | bytes 1179652
  26.0 10.3 %collective-permute-start.2 = (f32[6,18,1,128]{3,2,1,0:T(1,128)S(1)}, f32[6,18,1,128]{3,2,1,0:T(1,128)}, u32[]{:S(2)}, u32[]{:S(2)}) collective-permute-start(f32[6,18,1,128]{3,2,1,0:T(1,128)S(1)} %get-tuple-element.40), channel_id=1, source_target_pairs={{2,0},{3,1},{6,4},{7,5},{10,8},{11,9},{14,12},{15,13},{18,16},{19,... | collective-permute-start | bytes 165896 | tf_op jit(solution)/shard_map/ppermute | solution.py:18
  27.4 8.9 %collective-permute-start.3 = (f32[6,18,1,128]{3,2,1,0:T(1,128)S(1)}, f32[6,18,1,128]{3,2,1,0:T(1,128)}, u32[]{:S(2)}, u32[]{:S(2)}) collective-permute-start(f32[6,18,1,128]{3,2,1,0:T(1,128)S(1)} %get-tuple-element.39), channel_id=1, source_target_pairs={{0,2},{1,3},{4,6},{5,7},{8,10},{9,11},{12,14},{13,15},{16,18},{17,... | collective-permute-start | bytes 165896 | tf_op jit(solution)/shard_map/ppermute | solution.py:17
  39.3 8.4 %collective-permute-start.4 = (f32[6,18,18,1]{2,1,3,0:T(8,128)}, f32[6,18,18,1]{2,1,3,0:T(8,128)S(1)}, u32[]{:S(2)}, u32[]{:S(2)}) collective-permute-start(f32[6,18,18,1]{2,1,3,0:T(8,128)} %copy.28), channel_id=1, source_target_pairs={{1,0},{3,2},{5,4},{7,6},{9,8},{11,10},{13,12},{15,14},{17,16},{19,... | collective-permute-start | bytes 23336 | tf_op jit(solution)/shard_map/ppermute | solution.py:18
  41.5 7.0 %collective-permute-start.5 = (f32[6,18,18,1]{2,1,3,0:T(8,128)S(1)}, f32[6,18,18,1]{2,1,3,0:T(8,128)}, u32[]{:S(2)}, u32[]{:S(2)}) collective-permute-start(f32[6,18,18,1]{2,1,3,0:T(8,128)S(1)} %copy.30), channel_id=1, source_target_pairs={{0,1},{2,3},{4,5},{6,7},{8,9},{10,11},{12,13},{14,15},{16,17},{18,... | collective-permute-start | bytes 23336 | tf_op jit(solution)/shard_map/ppermute | solution.py:17
  54.0 10.3 %collective-permute-start.6 = (f32[6]{0:T(128)S(1)}, f32[6]{0:T(128)S(1)}, u32[]{:S(2)}, u32[]{:S(2)}) collective-permute-start(f32[6]{0:T(128)S(1)} %get-tuple-element.44), channel_id=1, source_target_pairs={{0,1},{1,0},{2,3},{3,2},{4,5},{5,4},{6,7},{7,6},{8,9},{9,8},{10,11... | collective-permute-start | bytes 80 | tf_op jit(solution)/shard_map/ppermute | solution.py:128
  54.1 10.2 %collective-permute-start.7 = (f32[6]{0:T(128)S(1)}, f32[6]{0:T(128)S(1)}, u32[]{:S(2)}, u32[]{:S(2)}) collective-permute-start(f32[6]{0:T(128)S(1)} %get-tuple-element.44), channel_id=1, source_target_pairs={{0,2},{1,3},{2,0},{3,1},{4,6},{5,7},{6,4},{7,5},{8,10},{9,11},{10,... | collective-permute-start | bytes 80 | tf_op jit(solution)/shard_map/ppermute | solution.py:128
  54.7 9.7 %collective-permute-start.8 = (f32[6]{0:T(128)S(1)}, f32[6]{0:T(128)S(1)}, u32[]{:S(2)}, u32[]{:S(2)}) collective-permute-start(f32[6]{0:T(128)S(1)} %get-tuple-element.44), channel_id=1, source_target_pairs={{0,3},{1,2},{2,1},{3,0},{4,7},{5,6},{6,5},{7,4},{8,11},{9,10},{10,... | collective-permute-start | bytes 80 | tf_op jit(solution)/shard_map/ppermute | solution.py:128
  57.2 5.5 %copy-start.2 = (f32[1,16,16,128]{3,2,1,0:T(8,128)}, f32[1,16,16,128]{3,2,1,0:T(8,128)S(1)}, u32[]{:S(2)}) copy-start(f32[1,16,16,128]{3,2,1,0:T(8,128)S(1)} %get-tuple-element.20) | copy-start | bytes 393220
  62.7 10.2 %copy-start.4 = (f32[6,16,16,128]{3,2,1,0:T(8,128)S(1)}, f32[6,16,16,128]{3,2,1,0:T(8,128)}, u32[]{:S(2)}) copy-start(f32[6,16,16,128]{3,2,1,0:T(8,128)} %convert_element_type.13) | copy-start | bytes 2359300
  62.7 10.2 %copy-start.14 = (f32[16,16,128]{2,1,0:T(8,128)S(1)}, f32[16,16,128]{2,1,0:T(8,128)}, u32[]{:S(2)}) copy-start(f32[16,16,128]{2,1,0:T(8,128)} %get-tuple-element.48) | copy-start | bytes 393220
  62.7 10.2 %copy-start.16 = (f32[16,16,128]{2,1,0:T(8,128)S(1)}, f32[16,16,128]{2,1,0:T(8,128)}, u32[]{:S(2)}) copy-start(f32[16,16,128]{2,1,0:T(8,128)} %get-tuple-element.49) | copy-start | bytes 393220
  62.7 10.2 %copy-start.18 = (f32[16,16,128]{2,1,0:T(8,128)S(1)}, f32[16,16,128]{2,1,0:T(8,128)}, u32[]{:S(2)}) copy-start(f32[16,16,128]{2,1,0:T(8,128)} %broadcast_multiply_fusion) | copy-start | bytes 393220
  62.7 10.2 %copy-start.22 = (f32[16,16,128]{2,1,0:T(8,128)S(1)}, f32[16,16,128]{2,1,0:T(8,128)}, u32[]{:S(2)}) copy-start(f32[16,16,128]{2,1,0:T(8,128)} %get-tuple-element.47) | copy-start | bytes 393220
  64.4 4.6 %collective-permute-start.10 = (f32[6]{0:T(128)S(1)}, f32[6]{0:T(128)S(1)}, u32[]{:S(2)}, u32[]{:S(2)}) collective-permute-start(f32[6]{0:T(128)S(1)} %add_add_fusion.6), channel_id=1, source_target_pairs={{0,8},{1,9},{2,10},{3,11},{4,12},{5,13},{6,14},{7,15},{8,0},{9,1},... | collective-permute-start | bytes 80 | tf_op jit(solution)/shard_map/ppermute | solution.py:128
  67.5 5.3 %collective-permute-start.11 = (f32[6]{0:T(128)S(1)}, f32[6]{0:T(128)S(1)}, u32[]{:S(2)}, u32[]{:S(2)}) collective-permute-start(f32[6]{0:T(128)S(1)} %add_add_fusion.6), channel_id=1, source_target_pairs={{0,12},{1,13},{2,14},{3,15},{4,8},{5,9},{6,10},{7,11},{8,4},{9,5},... | collective-permute-start | bytes 80 | tf_op jit(solution)/shard_map/ppermute | solution.py:128
  68.8 4.0 %collective-permute-start.9 = (f32[6]{0:T(128)S(1)}, f32[6]{0:T(128)S(1)}, u32[]{:S(2)}, u32[]{:S(2)}) collective-permute-start(f32[6]{0:T(128)S(1)} %add_add_fusion.6), channel_id=1, source_target_pairs={{0,4},{1,5},{2,6},{3,7},{4,0},{5,1},{6,2},{7,3},{8,12},{9,13},{10,... | collective-permute-start | bytes 80 | tf_op jit(solution)/shard_map/ppermute | solution.py:128
  74.0 15.1 %copy-start.26 = (bf16[6,16,16,128]{3,2,1,0:T(8,128)(2,1)S(1)}, bf16[6,16,16,128]{3,2,1,0:T(8,128)(2,1)}, u32[]{:S(2)}) copy-start(bf16[6,16,16,128]{3,2,1,0:T(8,128)(2,1)} %param.11) | copy-start | bytes 1179652
  74.1 6.2 %collective-permute-start.12 = (f32[6,1,16,128]{3,2,1,0:T(8,128)S(1)}, f32[6,1,16,128]{3,2,1,0:T(8,128)S(1)}, u32[]{:S(2)}, u32[]{:S(2)}) collective-permute-start(f32[6,1,16,128]{3,2,1,0:T(8,128)S(1)} %get-tuple-element.43), channel_id=1, source_target_pairs={{4,0},{8,4},{12,8},{5,1},{9,5},{13,9},{6,2},{10,6},{14,10},{7,3},{... | collective-permute-start | bytes 147464 | tf_op jit(solution)/shard_map/ppermute | solution.py:18
  75.7 6.3 %collective-permute-start.13 = (f32[6,1,16,128]{3,2,1,0:T(8,128)S(1)}, f32[6,1,16,128]{3,2,1,0:T(8,128)S(1)}, u32[]{:S(2)}, u32[]{:S(2)}) collective-permute-start(f32[6,1,16,128]{3,2,1,0:T(8,128)S(1)} %get-tuple-element.42), channel_id=1, source_target_pairs={{0,4},{4,8},{8,12},{1,5},{5,9},{9,13},{2,6},{6,10},{10,14},{3,7},{... | collective-permute-start | bytes 147464 | tf_op jit(solution)/shard_map/ppermute | solution.py:17
  82.1 8.0 %collective-permute-start.14 = (f32[6,18,1,128]{3,2,1,0:T(1,128)S(1)}, f32[6,18,1,128]{3,2,1,0:T(1,128)}, u32[]{:S(2)}, u32[]{:S(2)}) collective-permute-start(f32[6,18,1,128]{3,2,1,0:T(1,128)S(1)} %get-tuple-element.36), channel_id=1, source_target_pairs={{2,0},{3,1},{6,4},{7,5},{10,8},{11,9},{14,12},{15,13},{18,16},{19,... | collective-permute-start | bytes 165896 | tf_op jit(solution)/shard_map/ppermute | solution.py:18
  83.4 6.9 %collective-permute-start.15 = (f32[6,18,1,128]{3,2,1,0:T(1,128)S(1)}, f32[6,18,1,128]{3,2,1,0:T(1,128)}, u32[]{:S(2)}, u32[]{:S(2)}) collective-permute-start(f32[6,18,1,128]{3,2,1,0:T(1,128)S(1)} %get-tuple-element.35), channel_id=1, source_target_pairs={{0,2},{1,3},{4,6},{5,7},{8,10},{9,11},{12,14},{13,15},{16,18},{17,... | collective-permute-start | bytes 165896 | tf_op jit(solution)/shard_map/ppermute | solution.py:17
  93.3 8.4 %collective-permute-start.16 = (f32[6,18,18,1]{2,1,3,0:T(8,128)}, f32[6,18,18,1]{2,1,3,0:T(8,128)S(1)}, u32[]{:S(2)}, u32[]{:S(2)}) collective-permute-start(f32[6,18,18,1]{2,1,3,0:T(8,128)} %copy.32), channel_id=1, source_target_pairs={{1,0},{3,2},{5,4},{7,6},{9,8},{11,10},{13,12},{15,14},{17,16},{19,... | collective-permute-start | bytes 23336 | tf_op jit(solution)/shard_map/ppermute | solution.py:18
  95.6 7.0 %collective-permute-start.17 = (f32[6,18,18,1]{2,1,3,0:T(8,128)S(1)}, f32[6,18,18,1]{2,1,3,0:T(8,128)}, u32[]{:S(2)}, u32[]{:S(2)}) collective-permute-start(f32[6,18,18,1]{2,1,3,0:T(8,128)S(1)} %copy.34), channel_id=1, source_target_pairs={{0,1},{2,3},{4,5},{6,7},{8,9},{10,11},{12,13},{14,15},{16,17},{18,... | collective-permute-start | bytes 23336 | tf_op jit(solution)/shard_map/ppermute | solution.py:17
  104.2 3.7 %copy-start.12 = (f32[6,18,17,128]{3,2,1,0:T(8,128)S(1)}, f32[6,18,17,128]{3,2,1,0:T(8,128)}, u32[]{:S(2)}) copy-start(f32[6,18,17,128]{3,2,1,0:T(8,128)} %get-tuple-element.34) | copy-start | bytes 2820100
  108.5 11.0 %collective-permute-start.18 = (f32[6]{0:T(128)S(1)}, f32[6]{0:T(128)S(1)}, u32[]{:S(2)}, u32[]{:S(2)}) collective-permute-start(f32[6]{0:T(128)S(1)} %get-tuple-element.41), channel_id=1, source_target_pairs={{0,1},{1,0},{2,3},{3,2},{4,5},{5,4},{6,7},{7,6},{8,9},{9,8},{10,11... | collective-permute-start | bytes 80 | tf_op jit(solution)/shard_map/ppermute | solution.py:128
  108.6 10.9 %collective-permute-start.19 = (f32[6]{0:T(128)S(1)}, f32[6]{0:T(128)S(1)}, u32[]{:S(2)}, u32[]{:S(2)}) collective-permute-start(f32[6]{0:T(128)S(1)} %get-tuple-element.41), channel_id=1, source_target_pairs={{0,2},{1,3},{2,0},{3,1},{4,6},{5,7},{6,4},{7,5},{8,10},{9,11},{10,... | collective-permute-start | bytes 80 | tf_op jit(solution)/shard_map/ppermute | solution.py:128
  111.1 8.4 %collective-permute-start.20 = (f32[6]{0:T(128)S(1)}, f32[6]{0:T(128)S(1)}, u32[]{:S(2)}, u32[]{:S(2)}) collective-permute-start(f32[6]{0:T(128)S(1)} %get-tuple-element.41), channel_id=1, source_target_pairs={{0,3},{1,2},{2,1},{3,0},{4,7},{5,6},{6,5},{7,4},{8,11},{9,10},{10,... | collective-permute-start | bytes 80 | tf_op jit(solution)/shard_map/ppermute | solution.py:128
  117.9 10.1 %copy-start.5 = (f32[6,16,16,128]{3,2,1,0:T(8,128)S(1)}, f32[6,16,16,128]{3,2,1,0:T(8,128)}, u32[]{:S(2)}) copy-start(f32[6,16,16,128]{3,2,1,0:T(8,128)} %convert_element_type.13) | copy-start | bytes 2359300
  117.9 10.1 %copy-start.13 = (f32[6,16,16,128]{3,2,1,0:T(8,128)S(1)}, f32[6,16,16,128]{3,2,1,0:T(8,128)}, u32[]{:S(2)}) copy-start(f32[6,16,16,128]{3,2,1,0:T(8,128)} %convert_element_type.15) | copy-start | bytes 2359300
  117.9 10.1 %copy-start.15 = (f32[16,16,128]{2,1,0:T(8,128)S(1)}, f32[16,16,128]{2,1,0:T(8,128)}, u32[]{:S(2)}) copy-start(f32[16,16,128]{2,1,0:T(8,128)} %get-tuple-element.48) | copy-start | bytes 393220
  117.9 10.1 %copy-start.17 = (f32[16,16,128]{2,1,0:T(8,128)S(1)}, f32[16,16,128]{2,1,0:T(8,128)}, u32[]{:S(2)}) copy-start(f32[16,16,128]{2,1,0:T(8,128)} %get-tuple-element.49) | copy-start | bytes 393220
  117.9 10.1 %copy-start.19 = (f32[16,16,128]{2,1,0:T(8,128)S(1)}, f32[16,16,128]{2,1,0:T(8,128)}, u32[]{:S(2)}) copy-start(f32[16,16,128]{2,1,0:T(8,128)} %broadcast_multiply_fusion) | copy-start | bytes 393220
  117.9 10.1 %copy-start.23 = (f32[16,16,128]{2,1,0:T(8,128)S(1)}, f32[16,16,128]{2,1,0:T(8,128)}, u32[]{:S(2)}) copy-start(f32[16,16,128]{2,1,0:T(8,128)} %get-tuple-element.47) | copy-start | bytes 393220
  119.6 4.8 %collective-permute-start.21 = (f32[6]{0:T(128)S(1)}, f32[6]{0:T(128)S(1)}, u32[]{:S(2)}, u32[]{:S(2)}) collective-permute-start(f32[6]{0:T(128)S(1)} %add_add_fusion.5), channel_id=1, source_target_pairs={{0,4},{1,5},{2,6},{3,7},{4,0},{5,1},{6,2},{7,3},{8,12},{9,13},{10,... | collective-permute-start | bytes 80 | tf_op jit(solution)/shard_map/ppermute | solution.py:128
  122.0 4.4 %collective-permute-start.22 = (f32[6]{0:T(128)S(1)}, f32[6]{0:T(128)S(1)}, u32[]{:S(2)}, u32[]{:S(2)}) collective-permute-start(f32[6]{0:T(128)S(1)} %add_add_fusion.5), channel_id=1, source_target_pairs={{0,8},{1,9},{2,10},{3,11},{4,12},{5,13},{6,14},{7,15},{8,0},{9,1},... | collective-permute-start | bytes 80 | tf_op jit(solution)/shard_map/ppermute | solution.py:128
  122.5 5.3 %collective-permute-start.23 = (f32[6]{0:T(128)S(1)}, f32[6]{0:T(128)S(1)}, u32[]{:S(2)}, u32[]{:S(2)}) collective-permute-start(f32[6]{0:T(128)S(1)} %add_add_fusion.5), channel_id=1, source_target_pairs={{0,12},{1,13},{2,14},{3,15},{4,8},{5,9},{6,10},{7,11},{8,4},{9,5},... | collective-permute-start | bytes 80 | tf_op jit(solution)/shard_map/ppermute | solution.py:128
  129.6 2.1 %collective-permute-start.24 = (f32[16,8]{1,0:T(8,128)S(1)}, f32[16,8]{1,0:T(8,128)S(1)}, u32[]{:S(2)}, u32[]{:S(2)}) collective-permute-start(f32[16,8]{1,0:T(8,128)S(1)} %dynamic_update_slice.5), channel_id=1, source_target_pairs={{0,1},{1,0},{2,3},{3,2},{4,5},{5,4},{6,7},{7,6},{8,9},{9,8},{10,11... | collective-permute-start | bytes 1544 | tf_op jit(solution)/shard_map/ppermute | solution.py:128
  129.7 3.7 %collective-permute-start.25 = (f32[16,8]{1,0:T(8,128)S(1)}, f32[16,8]{1,0:T(8,128)S(1)}, u32[]{:S(2)}, u32[]{:S(2)}) collective-permute-start(f32[16,8]{1,0:T(8,128)S(1)} %dynamic_update_slice.5), channel_id=1, source_target_pairs={{0,2},{1,3},{2,0},{3,1},{4,6},{5,7},{6,4},{7,5},{8,10},{9,11},{10,... | collective-permute-start | bytes 1544 | tf_op jit(solution)/shard_map/ppermute | solution.py:128
  131.6 3.1 %collective-permute-start.26 = (f32[16,8]{1,0:T(8,128)S(1)}, f32[16,8]{1,0:T(8,128)S(1)}, u32[]{:S(2)}, u32[]{:S(2)}) collective-permute-start(f32[16,8]{1,0:T(8,128)S(1)} %dynamic_update_slice.5), channel_id=1, source_target_pairs={{0,3},{1,2},{2,1},{3,0},{4,7},{5,6},{6,5},{7,4},{8,11},{9,10},{10,... | collective-permute-start | bytes 1544 | tf_op jit(solution)/shard_map/ppermute | solution.py:128
  134.7 5.3 %collective-permute-start.27 = (f32[16,8]{1,0:T(8,128)S(1)}, f32[16,8]{1,0:T(8,128)S(1)}, u32[]{:S(2)}, u32[]{:S(2)}) collective-permute-start(f32[16,8]{1,0:T(8,128)S(1)} %add_add_fusion.4), channel_id=1, source_target_pairs={{0,4},{1,5},{2,6},{3,7},{4,0},{5,1},{6,2},{7,3},{8,12},{9,13},{10,... | collective-permute-start | bytes 1544 | tf_op jit(solution)/shard_map/ppermute | solution.py:128
  134.7 5.3 %collective-permute-start.28 = (f32[16,8]{1,0:T(8,128)S(1)}, f32[16,8]{1,0:T(8,128)S(1)}, u32[]{:S(2)}, u32[]{:S(2)}) collective-permute-start(f32[16,8]{1,0:T(8,128)S(1)} %add_add_fusion.4), channel_id=1, source_target_pairs={{0,8},{1,9},{2,10},{3,11},{4,12},{5,13},{6,14},{7,15},{8,0},{9,1},... | collective-permute-start | bytes 1544 | tf_op jit(solution)/shard_map/ppermute | solution.py:128
  137.1 5.4 %collective-permute-start.29 = (f32[16,8]{1,0:T(8,128)S(1)}, f32[16,8]{1,0:T(8,128)S(1)}, u32[]{:S(2)}, u32[]{:S(2)}) collective-permute-start(f32[16,8]{1,0:T(8,128)S(1)} %add_add_fusion.4), channel_id=1, source_target_pairs={{0,12},{1,13},{2,14},{3,15},{4,8},{5,9},{6,10},{7,11},{8,4},{9,5},... | collective-permute-start | bytes 1544 | tf_op jit(solution)/shard_map/ppermute | solution.py:128
  (11 other events, 32.5 us)

commit v2 on v1

--- a/solution.py
+++ b/solution.py
@@ -10,12 +10,19 @@
 def with_halo(array, sides, width):
     for axis, dim in sides:
         peers, length = (lax.axis_size(axis), array.shape[dim])
-        up = [(i, (i + 1) % peers) for i in range(peers - 1)]
-        down = [(j, i) for i, j in up]
         last = lax.slice_in_dim(array, length - width, length, axis=dim)
         initial = lax.slice_in_dim(array, 0, width, axis=dim)
-        before = lax.ppermute(last, axis, up)
-        after = lax.ppermute(initial, axis, down)
+        if peers == 2:
+            first = lax.axis_index(axis) == 0
+            got = lax.ppermute(jnp.where(first, last, initial), axis, [(0, 1), (1, 0)])
+            zero = jnp.zeros_like(got)
+            before = jnp.where(first, zero, got)
+            after = jnp.where(first, got, zero)
+        else:
+            up = [(i, (i + 1) % peers) for i in range(peers - 1)]
+            down = [(j, i) for i, j in up]
+            before = lax.ppermute(last, axis, up)
+            after = lax.ppermute(initial, axis, down)
         array = jnp.concatenate([before, array, after], axis=dim)
     return array
 
@@ -145,18 +152,11 @@
 
 
 def material(block_ids, table):
-    lame_first = jnp.zeros(block_ids.shape, jnp.float32)
-    shear = jnp.zeros(block_ids.shape, jnp.float32)
-    for entry in range(table.shape[0]):
-        chosen = block_ids == entry
-        lame_first = jnp.where(chosen, table[entry, 0], lame_first)
-        shear = jnp.where(chosen, table[entry, 1], shear)
+    entries = lax.broadcasted_iota(jnp.int32, block_ids.shape + (table.shape[0],), block_ids.ndim)
+    chosen = block_ids[..., None] == entries
+    lame_first = jnp.sum(jnp.where(chosen, table[:, 0], 0.0), axis=-1)
+    shear = jnp.sum(jnp.where(chosen, table[:, 1], 0.0), axis=-1)
     return (lame_first, shear)
-
-
-def foundation(field, mask, count):
-    total = group_sum(jnp.sum(mask * field, axis=(1, 2, 3)), ("gx", "gy", "col"))
-    return total / count
 
 
 def shards(
@@ -174,21 +174,33 @@
     group_size = lax.axis_size("gx") * lax.axis_size("gy") * lax.axis_size("col")
     count = jnp.float32(group_size * iface_cells.shape[1])
     gain_real, gain_imag = mean_gain(lame_first, shear, density_cells, mask, omega_sq, impedance)
+    axes = ("gx", "gy", "col")
     field = warm.astype(jnp.float32)
-    for sweep_index in range(2):
-        mean_field = foundation(field, mask, count)
-        padded = with_halo(field, (("gx", 1), ("gy", 2), ("col", 3)), 1)
-        field = sweep(
-            padded,
-            lame_first,
-            shear,
-            density_cells,
-            mask,
-            source_cells,
-            omega_sq,
-            impedance,
-        )
-        field = add_mean(field, gain_real, gain_imag, mean_field)
+    first = group_sum(
+        jnp.concatenate(
+            [
+                jnp.sum(mask * field, axis=(1, 2, 3)),
+                jnp.sum(gain_real, axis=(1, 2, 3)),
+                jnp.sum(gain_imag, axis=(1, 2, 3)),
+            ]
+        ),
+        axes,
+    )
+    mean_field = first[:6] / count
+    gain_total_real = first[6:9]
+    gain_total_imag = first[9:12]
+    sweep_args = (lame_first, shear, density_cells, mask, source_cells, omega_sq, impedance)
+    padded = with_halo(field, (("gx", 1), ("gy", 2), ("col", 3)), 1)
+    field = sweep(padded, *sweep_args)
+    second = group_sum(jnp.sum(mask * field, axis=(1, 2, 3)), axes)
+    field = add_mean(field, gain_real, gain_imag, mean_field)
+    padded = with_halo(field, (("gx", 1), ("gy", 2), ("col", 3)), 1)
+    field = sweep(padded, *sweep_args)
+    mean_real = mean_field[:3]
+    mean_imag = mean_field[3:]
+    total_real = second[:3] + (gain_total_real * mean_real - gain_total_imag * mean_imag)
+    total_imag = second[3:] + (gain_total_real * mean_imag + gain_total_imag * mean_real)
+    field = add_mean(field, gain_real, gain_imag, jnp.concatenate([total_real, total_imag]) / count)
     forward_cells = forward.astype(jnp.float32)
     correlation = (
         field[:3] * forward_cells[:3]

time: 145 us -> 105 us (0.72)
  other arithmetic: 50 us -> 27.4 us
  starting transfers between devices: 57.5 us -> 35.1 us
  local copies, waits for them, and re-layouts: 19.2 us -> 23.8 us
    ppermute x6 -> x2, starting transfers between devices: 28.9 us -> 10.3 us  [with_halo(): before = lax.ppermute(last, axis, up)]
    add x12, other arithmetic: 16.5 us -> 5.61 us  [navier(): result.append(shear * laplace[channel] + (lame_first + shear) * divergence)]
    add x1, other arithmetic: 10.7 us -> 0.01 us  [sweep(): diag_real = 8.0 * shear + 2.0 * lame_first - inertia + mask * imp_real]
    unnamed x59 -> x82, local copies, waits for them, and re-layouts: 0.8 us -> 9.46 us
    ppermute x6 -> x2, starting transfers between devices: 8.17 us -> 2.58 us  [with_halo(): after = lax.ppermute(initial, axis, down)]
    select_n x0 -> x6, local copies, waits for them, and re-layouts: none -> 4.87 us  [the longest x2 3.31 us: with_halo(): before = jnp.where(first, zero, got)]
    ppermute x4 -> x0, local copies, waits for them, and re-layouts: 4.86 us -> none  [the longest x2 3.31 us: with_halo(): before = lax.ppermute(last, axis, up)]
    concatenate x8 -> x6, other arithmetic: 14 us -> 10.5 us  [with_halo(): array = jnp.concatenate([before, array, after], axis=dim)]
  transfers between devices with their start and end apart: 30 -> 26, of which waited for: 9 -> 11; matrix products, arithmetic and copies ran while one was open for 33% -> 13% of each run, Pallas kernels for 0% -> 0%
where the time goes in v2:
time: 105 us; the launch traced here: 104 us
  starting transfers between devices  35.1 us (33%)
  other arithmetic  27.4 us (26%)
  local copies, waits for them, and re-layouts  23.8 us (23%)
  waiting for transfers between devices  16 us (15%)
  between operations  2.04 us (2%)
    ppermute x18, starting transfers between devices, group_sum(): lax.ppermute(value, axes, [(i, i ^ m * stride) for i in range(size)])  18.8 us
    ppermute x18, waiting for transfers between devices, group_sum(): lax.ppermute(value, axes, [(i, i ^ m * stride) for i in range(size)])  11.6 us
    concatenate x6, other arithmetic, with_halo(): array = jnp.concatenate([before, array, after], axis=dim)  10.5 us
    ppermute x2, starting transfers between devices, with_halo(): before = lax.ppermute(last, axis, up)  10.3 us
    unnamed x82, local copies, waits for them, and re-layouts  9.46 us
    add x12, other arithmetic, navier(): result.append(shear * laplace[channel] + (lame_first + shear) * divergence)  5.61 us
    ppermute x4, starting transfers between devices, with_halo(): got = lax.ppermute(jnp.where(first, last, initial), axis, [(0, 1), (1, 0)])  3.41 us
    select_n x2, local copies, waits for them, and re-layouts, with_halo(): before = jnp.where(first, zero, got)  3.31 us
  transfers between devices with their start and end apart: 26, of which 11 were waited for; matrix products, arithmetic and copies ran while one was open for 13% of the time, Pallas kernels for 0%

profile of v2, /device:TPU:0, one launch (start us, length us, event | category | flops | bytes accessed | tf_op | source)
XLA Modules:
  0.0 104.2 jit_solution(9971021291604055470)
XLA Ops:
  0.7 0.8 fusion.112
  1.5 1.3 %collective-permute-start = (f32[6,1,16,128]{3,2,1,0:T(8,128)S(1)}, f32[6,1,16,128]{3,2,1,0:T(8,128)S(1)}, u32[]{:S(2)}, u32[]{:S(2)}) collective-permute-start(f32[6,1,16,128]{3,2,1,0:T(8,128)S(1)} %get-tuple-element.54), channel_id=1, source_target_pairs={{4,0},{8,4},{12,8},{5,1},{9,5},{13,9},{6,2},{10,6},{14,10},{7,3},{... | collective-permute-start | bytes 147464 | tf_op jit(solution)/shard_map/ppermute | solution.py:25
  2.8 5.6 %collective-permute-start.1 = (f32[6,1,16,128]{3,2,1,0:T(8,128)S(1)}, f32[6,1,16,128]{3,2,1,0:T(8,128)S(1)}, u32[]{:S(2)}, u32[]{:S(2)}) collective-permute-start(f32[6,1,16,128]{3,2,1,0:T(8,128)S(1)} %get-tuple-element.53), channel_id=1, source_target_pairs={{0,4},{4,8},{8,12},{1,5},{5,9},{9,13},{2,6},{6,10},{10,14},{3,7},{... | collective-permute-start | bytes 147464 | tf_op jit(solution)/shard_map/ppermute | solution.py:24
  8.3 0.8 slice_bitcast_fusion.2
  9.1 0.8 select_reduce_fusion.1
  11.1 0.8 convert_multiply_fusion
  11.9 1.5 %scatter_custom_fusion = f32[32768]{0:T(1024)S(1)} fusion(s32[256]{0:T(256)S(1)} %bitcast.21, f32[256]{0:T(256)S(1)} %broadcast.106, f32[]{:T(128)} %constant.18.clone.1), kind=kCustom, calls=%fused_computation.238 | custom fusion | bytes 131076 | tf_op jit(solution)/shard_map/scatter | solution.py:168
  14.8 2.0 %collective-permute-start.2 = (f32[6,18,1,128]{3,2,1,0:T(1,128)S(1)}, f32[6,18,1,128]{3,2,1,0:T(1,128)S(1)}, u32[]{:S(2)}, u32[]{:S(2)}) collective-permute-start(f32[6,18,1,128]{3,2,1,0:T(1,128)S(1)} %broadcast_select_fusion.7), channel_id=1, source_target_pairs={{0,2},{2,0},{1,3},{3,1},{4,6},{6,4},{5,7},{7,5},{8,10},{10,8},{9,1... | collective-permute-start | bytes 165896 | tf_op jit(solution)/shard_map/ppermute | solution.py:17
  17.0 0.9 reshape.104
  18.1 0.9 reshape.105
  19.0 1.0 convert_element_type.13
  20.0 0.9 convert_element_type.15
  21.2 1.5 %fusion.111 = (f32[6,18,18,1]{3,2,1,0:T(8,128)S(1)}, f32[6,18,18,1]{3,2,1,0:T(8,128)}) fusion(f32[6,18,18,128]{3,2,1,0:T(8,128)S(1)} %pad_maximum_fusion.3), kind=kLoop, calls=%fused_computation.276 | loop fusion | bytes 31104 | tf_op jit(solution)/shard_map/slice | solution.py:14
  22.8 2.0 %copy.175 = f32[6,18,18,1]{2,3,1,0:T(1,128)S(1)} copy(f32[6,18,18,1]{3,2,1,0:T(8,128)} %get-tuple-element.37) | data formatting | bytes 15552
  25.7 1.7 %pad_maximum_fusion.2 = (f32[6,18,17,128]{3,2,1,0:T(8,128)}, f32[6,18,17,128]{3,2,1,0:T(8,128)}) fusion(f32[6,18,1,128]{3,2,1,0:T(1,128)S(1)} %get-tuple-element.65, f32[6,1,16,128]{3,2,1,0:T(8,128)S(1)} %collective-permute-done, f32[6,16,16,128]{3,2,1,0:T(8,128)S(1)} %convert_element_type.12, f32[6,1,16,128]{3,2,1,0:T(8,128)S(1)} %collective-permute-done.1, ...), kind=kLoop, calls=%fused_computation.5 | loop fusion | flops 1410048 | bytes 2875392 | tf_op jit(solution)/shard_map/concatenate | solution.py:26
  28.1 0.8 copy.157
  28.8 1.7 %copy.160 = f32[6,18,18,1]{3,2,1,0:T(8,128)S(1)} copy(f32[6,18,18,1]{2,1,3,0:T(8,128)} %get-tuple-element.58) | data formatting | bytes 15552 | tf_op jit(solution)/shard_map/jit(_where)/select_n | solution.py:19
  30.5 3.1 %pad_maximum_fusion = (f32[6,18,18,129]{3,2,1,0:T(8,128)S(1)}, f32[6,18,18,129]{3,2,1,0:T(8,128)S(1)}) fusion(f32[6,18,18,1]{3,2,1,0:T(8,128)S(1)} %copy.157, f32[6,18,1,128]{3,2,1,0:T(1,128)} %copy-done.15, f32[6,1,16,128]{3,2,1,0:T(8,128)S(1)} %collective-permute-done, f32[6,16,16,128]{3,2,1,0:T(8,128)S(1)} %convert_element_type.12, ...), kind=kLoop, calls=%fused_computation.1 | loop fusion | flops 2507760 | bytes 3017088 | tf_op jit(solution)/shard_map/concatenate | solution.py:26
  38.1 0.8 fusion.100
  40.1 1.3 %collective-permute-start.6 = (f32[12]{0:T(128)S(1)}, f32[12]{0:T(128)S(1)}, u32[]{:S(2)}, u32[]{:S(2)}) collective-permute-start(f32[12]{0:T(128)S(1)} %pad_maximum_fusion.19), channel_id=1, source_target_pairs={{0,3},{1,2},{2,1},{3,0},{4,7},{5,6},{6,5},{7,4},{8,11},{9,10},{10,... | collective-permute-start | bytes 152 | tf_op jit(solution)/shard_map/ppermute | solution.py:135
  43.5 2.2 %collective-permute-done.15 = f32[6]{0:T(128)S(1)} collective-permute-done((f32[6]{0:T(128)S(1)}, f32[6]{0:T(128)S(1)}, u32[]{:S(2)}, u32[]{:S(2)}) %collective-permute-start.15) | collective-permute-done | bytes 56 | tf_op jit(solution)/shard_map/ppermute | solution.py:135
  45.9 1.6 %collective-permute-start.17 = (f32[6]{0:T(128)S(1)}, f32[6]{0:T(128)S(1)}, u32[]{:S(2)}, u32[]{:S(2)}) collective-permute-start(f32[6]{0:T(128)S(1)} %add_add_fusion.7), channel_id=1, source_target_pairs={{0,4},{1,5},{2,6},{3,7},{4,0},{5,1},{6,2},{7,3},{8,12},{9,13},{10,... | collective-permute-start | bytes 80 | tf_op jit(solution)/shard_map/ppermute | solution.py:135
  47.5 1.1 %collective-permute-start.18 = (f32[6]{0:T(128)S(1)}, f32[6]{0:T(128)S(1)}, u32[]{:S(2)}, u32[]{:S(2)}) collective-permute-start(f32[6]{0:T(128)S(1)} %add_add_fusion.7), channel_id=1, source_target_pairs={{0,8},{1,9},{2,10},{3,11},{4,12},{5,13},{6,14},{7,15},{8,0},{9,1},... | collective-permute-start | bytes 80 | tf_op jit(solution)/shard_map/ppermute | solution.py:135
  48.6 1.7 %collective-permute-start.19 = (f32[6]{0:T(128)S(1)}, f32[6]{0:T(128)S(1)}, u32[]{:S(2)}, u32[]{:S(2)}) collective-permute-start(f32[6]{0:T(128)S(1)} %add_add_fusion.7), channel_id=1, source_target_pairs={{0,12},{1,13},{2,14},{3,15},{4,8},{5,9},{6,10},{7,11},{8,4},{9,5},... | collective-permute-start | bytes 80 | tf_op jit(solution)/shard_map/ppermute | solution.py:135
  50.3 0.7 collective-permute-start.7
  51.1 2.0 %collective-permute-start.8 = (f32[12]{0:T(128)S(1)}, f32[12]{0:T(128)S(1)}, u32[]{:S(2)}, u32[]{:S(2)}) collective-permute-start(f32[12]{0:T(128)S(1)} %add_add_fusion.9), channel_id=1, source_target_pairs={{0,8},{1,9},{2,10},{3,11},{4,12},{5,13},{6,14},{7,15},{8,0},{9,1},... | collective-permute-start | bytes 152 | tf_op jit(solution)/shard_map/ppermute | solution.py:135
  53.1 1.7 %collective-permute-start.9 = (f32[12]{0:T(128)S(1)}, f32[12]{0:T(128)S(1)}, u32[]{:S(2)}, u32[]{:S(2)}) collective-permute-start(f32[12]{0:T(128)S(1)} %add_add_fusion.9), channel_id=1, source_target_pairs={{0,12},{1,13},{2,14},{3,15},{4,8},{5,9},{6,10},{7,11},{8,4},{9,5},... | collective-permute-start | bytes 152 | tf_op jit(solution)/shard_map/ppermute | solution.py:135
  55.5 2.9 %collective-permute-done.9 = f32[12]{0:T(128)S(1)} collective-permute-done((f32[12]{0:T(128)S(1)}, f32[12]{0:T(128)S(1)}, u32[]{:S(2)}, u32[]{:S(2)}) %collective-permute-start.9) | collective-permute-done | bytes 80 | tf_op jit(solution)/shard_map/ppermute | solution.py:135
  58.9 1.3 %collective-permute-start.10 = (f32[6,1,16,128]{3,2,1,0:T(8,128)S(1)}, f32[6,1,16,128]{3,2,1,0:T(8,128)S(1)}, u32[]{:S(2)}, u32[]{:S(2)}) collective-permute-start(f32[6,1,16,128]{3,2,1,0:T(8,128)S(1)} %get-tuple-element.47), channel_id=1, source_target_pairs={{4,0},{8,4},{12,8},{5,1},{9,5},{13,9},{6,2},{10,6},{14,10},{7,3},{... | collective-permute-start | bytes 147464 | tf_op jit(solution)/shard_map/ppermute | solution.py:25
  60.2 4.7 %collective-permute-start.11 = (f32[6,1,16,128]{3,2,1,0:T(8,128)S(1)}, f32[6,1,16,128]{3,2,1,0:T(8,128)S(1)}, u32[]{:S(2)}, u32[]{:S(2)}) collective-permute-start(f32[6,1,16,128]{3,2,1,0:T(8,128)S(1)} %get-tuple-element.46), channel_id=1, source_target_pairs={{0,4},{4,8},{8,12},{1,5},{5,9},{9,13},{2,6},{6,10},{10,14},{3,7},{... | collective-permute-start | bytes 147464 | tf_op jit(solution)/shard_map/ppermute | solution.py:24
  65.0 1.5 %collective-permute-done.11 = f32[6,1,16,128]{3,2,1,0:T(8,128)S(1)} collective-permute-done((f32[6,1,16,128]{3,2,1,0:T(8,128)S(1)}, f32[6,1,16,128]{3,2,1,0:T(8,128)S(1)}, u32[]{:S(2)}, u32[]{:S(2)}) %collective-permute-start.11) | collective-permute-done | bytes 49184 | tf_op jit(solution)/shard_map/ppermute | solution.py:24
  66.6 1.3 %collective-permute-start.12 = (f32[6,18,1,128]{3,2,1,0:T(1,128)S(1)}, f32[6,18,1,128]{3,2,1,0:T(1,128)S(1)}, u32[]{:S(2)}, u32[]{:S(2)}) collective-permute-start(f32[6,18,1,128]{3,2,1,0:T(1,128)S(1)} %broadcast_select_fusion.4), channel_id=1, source_target_pairs={{0,2},{2,0},{1,3},{3,1},{4,6},{6,4},{5,7},{7,5},{8,10},{10,8},{9,1... | collective-permute-start | bytes 165896 | tf_op jit(solution)/shard_map/ppermute | solution.py:17
  67.9 2.9 %collective-permute-done.12 = f32[6,18,1,128]{3,2,1,0:T(1,128)S(1)} collective-permute-done((f32[6,18,1,128]{3,2,1,0:T(1,128)S(1)}, f32[6,18,1,128]{3,2,1,0:T(1,128)S(1)}, u32[]{:S(2)}, u32[]{:S(2)}) %collective-permute-start.12) | collective-permute-done | bytes 55328 | tf_op jit(solution)/shard_map/ppermute | solution.py:17
  71.1 1.5 %fusion.110 = (f32[6,18,18,1]{3,2,1,0:T(8,128)S(1)}, f32[6,18,18,1]{3,2,1,0:T(8,128)}) fusion(f32[6,18,18,128]{3,2,1,0:T(8,128)S(1)} %pad_maximum_fusion.5), kind=kLoop, calls=%fused_computation.275 | loop fusion | bytes 31104 | tf_op jit(solution)/shard_map/slice | solution.py:14
  72.6 2.0 %copy.177 = f32[6,18,18,1]{2,3,1,0:T(1,128)S(1)} copy(f32[6,18,18,1]{3,2,1,0:T(8,128)} %get-tuple-element.35) | data formatting | bytes 15552
  75.6 1.7 %pad_maximum_fusion.4 = (f32[6,18,17,128]{3,2,1,0:T(8,128)}, f32[6,18,17,128]{3,2,1,0:T(8,128)}) fusion(f32[6,18,1,128]{3,2,1,0:T(1,128)S(1)} %get-tuple-element.63, f32[6,1,16,128]{3,2,1,0:T(8,128)S(1)} %collective-permute-done.10, f32[3,16,16,128]{3,2,1,0:T(8,128)S(1)} %get-tuple-element.48, f32[3,16,16,128]{3,2,1,0:T(8,128)S(1)} %get-tuple-element.49, ...), kind=kLoop, calls=%fused_computation.8 | loop fusion | flops 1880064 | bytes 2875392 | tf_op jit(solution)/shard_map/concatenate | solution.py:26
  77.9 0.8 copy.166
  78.7 1.7 %copy.169 = f32[6,18,18,1]{3,2,1,0:T(8,128)S(1)} copy(f32[6,18,18,1]{2,1,3,0:T(8,128)} %get-tuple-element.56) | data formatting | bytes 15552 | tf_op jit(solution)/shard_map/jit(_where)/select_n | solution.py:19
  80.3 3.6 %pad_maximum_fusion.1 = (f32[6,18,18,129]{3,2,1,0:T(8,128)S(1)}, f32[6,18,18,129]{3,2,1,0:T(8,128)S(1)}) fusion(f32[6,18,18,1]{3,2,1,0:T(8,128)S(1)} %copy.166, f32[6,18,1,128]{3,2,1,0:T(1,128)} %copy-done.11, f32[6,1,16,128]{3,2,1,0:T(8,128)S(1)} %collective-permute-done.10, f32[3,16,16,128]{3,2,1,0:T(8,128)S(1)} %get-tuple-element.48, ...), kind=kLoop, calls=%fused_computation.3 | loop fusion | flops 3009312 | bytes 3017088 | tf_op jit(solution)/shard_map/concatenate | solution.py:26
  88.7 0.9 subtract_reduce_fusion
  91.2 1.4 %collective-permute-start.21 = (f32[16,8]{1,0:T(8,128)S(1)}, f32[16,8]{1,0:T(8,128)S(1)}, u32[]{:S(2)}, u32[]{:S(2)}) collective-permute-start(f32[16,8]{1,0:T(8,128)S(1)} %dynamic_update_slice.5), channel_id=1, source_target_pairs={{0,2},{1,3},{2,0},{3,1},{4,6},{5,7},{6,4},{7,5},{8,10},{9,11},{10,... | collective-permute-start | bytes 1544 | tf_op jit(solution)/shard_map/ppermute | solution.py:135
  93.0 1.8 %collective-permute-done.21 = f32[16,8]{1,0:T(8,128)S(1)} collective-permute-done((f32[16,8]{1,0:T(8,128)S(1)}, f32[16,8]{1,0:T(8,128)S(1)}, u32[]{:S(2)}, u32[]{:S(2)}) %collective-permute-start.21) | collective-permute-done | bytes 544 | tf_op jit(solution)/shard_map/ppermute | solution.py:135
  94.8 0.9 collective-permute-done.22
  95.7 2.3 %collective-permute-start.23 = (f32[16,8]{1,0:T(8,128)S(1)}, f32[16,8]{1,0:T(8,128)S(1)}, u32[]{:S(2)}, u32[]{:S(2)}) collective-permute-start(f32[16,8]{1,0:T(8,128)S(1)} %add_add_fusion.4), channel_id=1, source_target_pairs={{0,4},{1,5},{2,6},{3,7},{4,0},{5,1},{6,2},{7,3},{8,12},{9,13},{10,... | collective-permute-start | bytes 1544 | tf_op jit(solution)/shard_map/ppermute | solution.py:135
  98.1 2.4 %collective-permute-start.25 = (f32[16,8]{1,0:T(8,128)S(1)}, f32[16,8]{1,0:T(8,128)S(1)}, u32[]{:S(2)}, u32[]{:S(2)}) collective-permute-start(f32[16,8]{1,0:T(8,128)S(1)} %add_add_fusion.4), channel_id=1, source_target_pairs={{0,12},{1,13},{2,14},{3,15},{4,8},{5,9},{6,10},{7,11},{8,4},{9,5},... | collective-permute-start | bytes 1544 | tf_op jit(solution)/shard_map/ppermute | solution.py:135
  100.4 0.9 pad_maximum_fusion.13
  101.3 1.3 %collective-permute-done.24 = f32[16,8]{1,0:T(8,128)S(1)} collective-permute-done((f32[16,8]{1,0:T(8,128)S(1)}, f32[16,8]{1,0:T(8,128)S(1)}, u32[]{:S(2)}, u32[]{:S(2)}) %collective-permute-start.24) | collective-permute-done | bytes 544 | tf_op jit(solution)/shard_map/ppermute | solution.py:135
  102.6 0.9 collective-permute-done.25
  (166 shorter events, 22.4 us)
Async XLA Ops:
  0.6 14.0 %copy-start.17 = (bf16[6,16,16,128]{3,2,1,0:T(8,128)(2,1)S(1)}, bf16[6,16,16,128]{3,2,1,0:T(8,128)(2,1)}, u32[]{:S(2)}) copy-start(bf16[6,16,16,128]{3,2,1,0:T(8,128)(2,1)} %param.10) | copy-start | bytes 1179652
  0.6 10.4 %copy-start.36 = (s32[1,256]{1,0:T(1,128)S(1)}, s32[1,256]{1,0:T(1,128)}, u32[]{:S(2)}) copy-start(s32[1,256]{1,0:T(1,128)} %param.15) | copy-start | bytes 3076
  0.7 10.4 %copy-start.35 = (bf16[16,16,128]{2,1,0:T(8,128)(2,1)S(1)}, bf16[16,16,128]{2,1,0:T(8,128)(2,1)}, u32[]{:S(2)}) copy-start(bf16[16,16,128]{2,1,0:T(8,128)(2,1)} %param.12) | copy-start | bytes 196612
  1.5 13.3 %collective-permute-start = (f32[6,1,16,128]{3,2,1,0:T(8,128)S(1)}, f32[6,1,16,128]{3,2,1,0:T(8,128)S(1)}, u32[]{:S(2)}, u32[]{:S(2)}) collective-permute-start(f32[6,1,16,128]{3,2,1,0:T(8,128)S(1)} %get-tuple-element.54), channel_id=1, source_target_pairs={{4,0},{8,4},{12,8},{5,1},{9,5},{13,9},{6,2},{10,6},{14,10},{7,3},{... | collective-permute-start | bytes 147464 | tf_op jit(solution)/shard_map/ppermute | solution.py:25
  2.8 12.0 %collective-permute-start.1 = (f32[6,1,16,128]{3,2,1,0:T(8,128)S(1)}, f32[6,1,16,128]{3,2,1,0:T(8,128)S(1)}, u32[]{:S(2)}, u32[]{:S(2)}) collective-permute-start(f32[6,1,16,128]{3,2,1,0:T(8,128)S(1)} %get-tuple-element.53), channel_id=1, source_target_pairs={{0,4},{4,8},{8,12},{1,5},{5,9},{9,13},{2,6},{6,10},{10,14},{3,7},{... | collective-permute-start | bytes 147464 | tf_op jit(solution)/shard_map/ppermute | solution.py:24
  11.9 5.0 %copy-start.37 = (f32[2,3]{1,0:T(2,128)S(1)}, f32[2,3]{1,0:T(2,128)}, u32[]{:S(2)}) copy-start(f32[2,3]{1,0:T(2,128)} %param.16) | copy-start | bytes 76
  14.8 4.2 %copy-start.33 = (bf16[6,16,16,128]{3,2,1,0:T(8,128)(2,1)S(1)}, bf16[6,16,16,128]{3,2,1,0:T(8,128)(2,1)}, u32[]{:S(2)}) copy-start(bf16[6,16,16,128]{3,2,1,0:T(8,128)(2,1)} %param.9) | copy-start | bytes 1179652
  14.8 6.1 %collective-permute-start.2 = (f32[6,18,1,128]{3,2,1,0:T(1,128)S(1)}, f32[6,18,1,128]{3,2,1,0:T(1,128)S(1)}, u32[]{:S(2)}, u32[]{:S(2)}) collective-permute-start(f32[6,18,1,128]{3,2,1,0:T(1,128)S(1)} %broadcast_select_fusion.7), channel_id=1, source_target_pairs={{0,2},{2,0},{1,3},{3,1},{4,6},{6,4},{5,7},{7,5},{8,10},{10,8},{9,1... | collective-permute-start | bytes 165896 | tf_op jit(solution)/shard_map/ppermute | solution.py:17
  17.9 2.1 %copy-start.34 = (bf16[6,16,16,128]{3,2,1,0:T(8,128)(2,1)S(1)}, bf16[6,16,16,128]{3,2,1,0:T(8,128)(2,1)}, u32[]{:S(2)}) copy-start(bf16[6,16,16,128]{3,2,1,0:T(8,128)(2,1)} %param.11) | copy-start | bytes 1179652
  21.0 4.7 %copy-start.13 = (f32[6,18,1,128]{3,2,1,0:T(1,128)}, f32[6,18,1,128]{3,2,1,0:T(1,128)S(1)}, u32[]{:S(2)}) copy-start(f32[6,18,1,128]{3,2,1,0:T(1,128)S(1)} %get-tuple-element.64) | copy-start | bytes 165892
  21.0 4.7 %copy-start.15 = (f32[6,18,1,128]{3,2,1,0:T(1,128)}, f32[6,18,1,128]{3,2,1,0:T(1,128)S(1)}, u32[]{:S(2)}) copy-start(f32[6,18,1,128]{3,2,1,0:T(1,128)S(1)} %get-tuple-element.65) | copy-start | bytes 165892
  25.6 1.8 %collective-permute-start.3 = (f32[6,18,18,1]{2,1,3,0:T(8,128)S(1)}, f32[6,18,18,1]{2,1,3,0:T(8,128)S(1)}, u32[]{:S(2)}, u32[]{:S(2)}) collective-permute-start(f32[6,18,18,1]{2,1,3,0:T(8,128)S(1)} %copy.154), channel_id=1, source_target_pairs={{0,1},{1,0},{2,3},{3,2},{4,5},{5,4},{6,7},{7,6},{8,9},{9,8},{10,11... | collective-permute-start | bytes 23336 | tf_op jit(solution)/shard_map/ppermute | solution.py:17
  30.5 3.1 %copy-start.18 = (bf16[6,16,16,128]{3,2,1,0:T(8,128)(2,1)S(1)}, bf16[6,16,16,128]{3,2,1,0:T(8,128)(2,1)}, u32[]{:S(2)}) copy-start(bf16[6,16,16,128]{3,2,1,0:T(8,128)(2,1)} %param.10) | copy-start | bytes 1179652
  30.5 3.1 %copy-start.21 = (f32[6,18,17,128]{3,2,1,0:T(8,128)S(1)}, f32[6,18,17,128]{3,2,1,0:T(8,128)}, u32[]{:S(2)}) copy-start(f32[6,18,17,128]{3,2,1,0:T(8,128)} %get-tuple-element.44) | copy-start | bytes 2820100
  30.5 3.1 %copy-start.22 = (f32[6,18,17,128]{3,2,1,0:T(8,128)S(1)}, f32[6,18,17,128]{3,2,1,0:T(8,128)}, u32[]{:S(2)}) copy-start(f32[6,18,17,128]{3,2,1,0:T(8,128)} %get-tuple-element.45) | copy-start | bytes 2820100
  35.0 1.8 %copy-start.2 = (f32[1,16,16,128]{3,2,1,0:T(8,128)}, f32[1,16,16,128]{3,2,1,0:T(8,128)S(1)}, u32[]{:S(2)}) copy-start(f32[1,16,16,128]{3,2,1,0:T(8,128)S(1)} %get-tuple-element.29) | copy-start | bytes 393220
  36.9 1.2 %copy-start.28 = (f32[16,16,128]{2,1,0:T(8,128)S(1)}, f32[16,16,128]{2,1,0:T(8,128)}, u32[]{:S(2)}) copy-start(f32[16,16,128]{2,1,0:T(8,128)} %broadcast_multiply_fusion) | copy-start | bytes 393220
  36.9 1.3 %copy-start.30 = (f32[16,16,128]{2,1,0:T(8,128)S(1)}, f32[16,16,128]{2,1,0:T(8,128)}, u32[]{:S(2)}) copy-start(f32[16,16,128]{2,1,0:T(8,128)} %get-tuple-element.59) | copy-start | bytes 393220
  39.5 9.1 %collective-permute-start.4 = (f32[12]{0:T(128)S(1)}, f32[12]{0:T(128)S(1)}, u32[]{:S(2)}, u32[]{:S(2)}) collective-permute-start(f32[12]{0:T(128)S(1)} %pad_maximum_fusion.19), channel_id=1, source_target_pairs={{0,1},{1,0},{2,3},{3,2},{4,5},{5,4},{6,7},{7,6},{8,9},{9,8},{10,11... | collective-permute-start | bytes 152 | tf_op jit(solution)/shard_map/ppermute | solution.py:135
  40.0 10.3 %collective-permute-start.5 = (f32[12]{0:T(128)S(1)}, f32[12]{0:T(128)S(1)}, u32[]{:S(2)}, u32[]{:S(2)}) collective-permute-start(f32[12]{0:T(128)S(1)} %pad_maximum_fusion.19), channel_id=1, source_target_pairs={{0,2},{1,3},{2,0},{3,1},{4,6},{5,7},{6,4},{7,5},{8,10},{9,11},{10,... | collective-permute-start | bytes 152 | tf_op jit(solution)/shard_map/ppermute | solution.py:135
  40.1 10.2 %collective-permute-start.6 = (f32[12]{0:T(128)S(1)}, f32[12]{0:T(128)S(1)}, u32[]{:S(2)}, u32[]{:S(2)}) collective-permute-start(f32[12]{0:T(128)S(1)} %pad_maximum_fusion.19), channel_id=1, source_target_pairs={{0,3},{1,2},{2,1},{3,0},{4,7},{5,6},{6,5},{7,4},{8,11},{9,10},{10,... | collective-permute-start | bytes 152 | tf_op jit(solution)/shard_map/ppermute | solution.py:135
  41.4 1.5 %collective-permute-start.14 = (f32[6]{0:T(128)S(1)}, f32[6]{0:T(128)S(1)}, u32[]{:S(2)}, u32[]{:S(2)}) collective-permute-start(f32[6]{0:T(128)S(1)} %get-tuple-element.14), channel_id=1, source_target_pairs={{0,1},{1,0},{2,3},{3,2},{4,5},{5,4},{6,7},{7,6},{8,9},{9,8},{10,11... | collective-permute-start | bytes 80 | tf_op jit(solution)/shard_map/ppermute | solution.py:135
  42.1 3.5 %collective-permute-start.15 = (f32[6]{0:T(128)S(1)}, f32[6]{0:T(128)S(1)}, u32[]{:S(2)}, u32[]{:S(2)}) collective-permute-start(f32[6]{0:T(128)S(1)} %get-tuple-element.14), channel_id=1, source_target_pairs={{0,2},{1,3},{2,0},{3,1},{4,6},{5,7},{6,4},{7,5},{8,10},{9,11},{10,... | collective-permute-start | bytes 80 | tf_op jit(solution)/shard_map/ppermute | solution.py:135
  43.0 3.0 %collective-permute-start.16 = (f32[6]{0:T(128)S(1)}, f32[6]{0:T(128)S(1)}, u32[]{:S(2)}, u32[]{:S(2)}) collective-permute-start(f32[6]{0:T(128)S(1)} %get-tuple-element.14), channel_id=1, source_target_pairs={{0,3},{1,2},{2,1},{3,0},{4,7},{5,6},{6,5},{7,4},{8,11},{9,10},{10,... | collective-permute-start | bytes 80 | tf_op jit(solution)/shard_map/ppermute | solution.py:135
  45.9 7.1 %collective-permute-start.17 = (f32[6]{0:T(128)S(1)}, f32[6]{0:T(128)S(1)}, u32[]{:S(2)}, u32[]{:S(2)}) collective-permute-start(f32[6]{0:T(128)S(1)} %add_add_fusion.7), channel_id=1, source_target_pairs={{0,4},{1,5},{2,6},{3,7},{4,0},{5,1},{6,2},{7,3},{8,12},{9,13},{10,... | collective-permute-start | bytes 80 | tf_op jit(solution)/shard_map/ppermute | solution.py:135
  47.5 7.3 %collective-permute-start.18 = (f32[6]{0:T(128)S(1)}, f32[6]{0:T(128)S(1)}, u32[]{:S(2)}, u32[]{:S(2)}) collective-permute-start(f32[6]{0:T(128)S(1)} %add_add_fusion.7), channel_id=1, source_target_pairs={{0,8},{1,9},{2,10},{3,11},{4,12},{5,13},{6,14},{7,15},{8,0},{9,1},... | collective-permute-start | bytes 80 | tf_op jit(solution)/shard_map/ppermute | solution.py:135
  48.6 6.2 %collective-permute-start.19 = (f32[6]{0:T(128)S(1)}, f32[6]{0:T(128)S(1)}, u32[]{:S(2)}, u32[]{:S(2)}) collective-permute-start(f32[6]{0:T(128)S(1)} %add_add_fusion.7), channel_id=1, source_target_pairs={{0,12},{1,13},{2,14},{3,15},{4,8},{5,9},{6,10},{7,11},{8,4},{9,5},... | collective-permute-start | bytes 80 | tf_op jit(solution)/shard_map/ppermute | solution.py:135
  50.3 4.5 %collective-permute-start.7 = (f32[12]{0:T(128)S(1)}, f32[12]{0:T(128)S(1)}, u32[]{:S(2)}, u32[]{:S(2)}) collective-permute-start(f32[12]{0:T(128)S(1)} %add_add_fusion.9), channel_id=1, source_target_pairs={{0,4},{1,5},{2,6},{3,7},{4,0},{5,1},{6,2},{7,3},{8,12},{9,13},{10,... | collective-permute-start | bytes 152 | tf_op jit(solution)/shard_map/ppermute | solution.py:135
  51.1 4.4 %collective-permute-start.8 = (f32[12]{0:T(128)S(1)}, f32[12]{0:T(128)S(1)}, u32[]{:S(2)}, u32[]{:S(2)}) collective-permute-start(f32[12]{0:T(128)S(1)} %add_add_fusion.9), channel_id=1, source_target_pairs={{0,8},{1,9},{2,10},{3,11},{4,12},{5,13},{6,14},{7,15},{8,0},{9,1},... | collective-permute-start | bytes 152 | tf_op jit(solution)/shard_map/ppermute | solution.py:135
  53.1 5.3 %collective-permute-start.9 = (f32[12]{0:T(128)S(1)}, f32[12]{0:T(128)S(1)}, u32[]{:S(2)}, u32[]{:S(2)}) collective-permute-start(f32[12]{0:T(128)S(1)} %add_add_fusion.9), channel_id=1, source_target_pairs={{0,12},{1,13},{2,14},{3,15},{4,8},{5,9},{6,10},{7,11},{8,4},{9,5},... | collective-permute-start | bytes 152 | tf_op jit(solution)/shard_map/ppermute | solution.py:135
  58.9 6.1 %collective-permute-start.10 = (f32[6,1,16,128]{3,2,1,0:T(8,128)S(1)}, f32[6,1,16,128]{3,2,1,0:T(8,128)S(1)}, u32[]{:S(2)}, u32[]{:S(2)}) collective-permute-start(f32[6,1,16,128]{3,2,1,0:T(8,128)S(1)} %get-tuple-element.47), channel_id=1, source_target_pairs={{4,0},{8,4},{12,8},{5,1},{9,5},{13,9},{6,2},{10,6},{14,10},{7,3},{... | collective-permute-start | bytes 147464 | tf_op jit(solution)/shard_map/ppermute | solution.py:25
  60.2 6.3 %collective-permute-start.11 = (f32[6,1,16,128]{3,2,1,0:T(8,128)S(1)}, f32[6,1,16,128]{3,2,1,0:T(8,128)S(1)}, u32[]{:S(2)}, u32[]{:S(2)}) collective-permute-start(f32[6,1,16,128]{3,2,1,0:T(8,128)S(1)} %get-tuple-element.46), channel_id=1, source_target_pairs={{0,4},{4,8},{8,12},{1,5},{5,9},{9,13},{2,6},{6,10},{10,14},{3,7},{... | collective-permute-start | bytes 147464 | tf_op jit(solution)/shard_map/ppermute | solution.py:24
  66.6 4.2 %collective-permute-start.12 = (f32[6,18,1,128]{3,2,1,0:T(1,128)S(1)}, f32[6,18,1,128]{3,2,1,0:T(1,128)S(1)}, u32[]{:S(2)}, u32[]{:S(2)}) collective-permute-start(f32[6,18,1,128]{3,2,1,0:T(1,128)S(1)} %broadcast_select_fusion.4), channel_id=1, source_target_pairs={{0,2},{2,0},{1,3},{3,1},{4,6},{6,4},{5,7},{7,5},{8,10},{10,8},{9,1... | collective-permute-start | bytes 165896 | tf_op jit(solution)/shard_map/ppermute | solution.py:17
  70.9 4.7 %copy-start.9 = (f32[6,18,1,128]{3,2,1,0:T(1,128)}, f32[6,18,1,128]{3,2,1,0:T(1,128)S(1)}, u32[]{:S(2)}) copy-start(f32[6,18,1,128]{3,2,1,0:T(1,128)S(1)} %get-tuple-element.62) | copy-start | bytes 165892
  70.9 4.7 %copy-start.11 = (f32[6,18,1,128]{3,2,1,0:T(1,128)}, f32[6,18,1,128]{3,2,1,0:T(1,128)S(1)}, u32[]{:S(2)}) copy-start(f32[6,18,1,128]{3,2,1,0:T(1,128)S(1)} %get-tuple-element.63) | copy-start | bytes 165892
  75.5 1.8 %collective-permute-start.13 = (f32[6,18,18,1]{2,1,3,0:T(8,128)S(1)}, f32[6,18,18,1]{2,1,3,0:T(8,128)S(1)}, u32[]{:S(2)}, u32[]{:S(2)}) collective-permute-start(f32[6,18,18,1]{2,1,3,0:T(8,128)S(1)} %copy.163), channel_id=1, source_target_pairs={{0,1},{1,0},{2,3},{3,2},{4,5},{5,4},{6,7},{7,6},{8,9},{9,8},{10,11... | collective-permute-start | bytes 23336 | tf_op jit(solution)/shard_map/ppermute | solution.py:17
  80.3 3.6 %copy-start.19 = (f32[6,18,17,128]{3,2,1,0:T(8,128)S(1)}, f32[6,18,17,128]{3,2,1,0:T(8,128)}, u32[]{:S(2)}) copy-start(f32[6,18,17,128]{3,2,1,0:T(8,128)} %get-tuple-element.42) | copy-start | bytes 2820100
  80.3 3.7 %copy-start.20 = (f32[6,18,17,128]{3,2,1,0:T(8,128)S(1)}, f32[6,18,17,128]{3,2,1,0:T(8,128)}, u32[]{:S(2)}) copy-start(f32[6,18,17,128]{3,2,1,0:T(8,128)} %get-tuple-element.43) | copy-start | bytes 2820100
  87.2 1.2 %copy-start.26 = (f32[16,16,128]{2,1,0:T(8,128)S(1)}, f32[16,16,128]{2,1,0:T(8,128)}, u32[]{:S(2)}) copy-start(f32[16,16,128]{2,1,0:T(8,128)} %get-tuple-element.61) | copy-start | bytes 393220
  87.2 1.5 %copy-start.27 = (f32[6,16,16,128]{3,2,1,0:T(8,128)S(1)}, f32[6,16,16,128]{3,2,1,0:T(8,128)}, u32[]{:S(2)}) copy-start(f32[6,16,16,128]{3,2,1,0:T(8,128)} %convert_element_type.15) | copy-start | bytes 2359300
  87.2 1.4 %copy-start.29 = (f32[16,16,128]{2,1,0:T(8,128)S(1)}, f32[16,16,128]{2,1,0:T(8,128)}, u32[]{:S(2)}) copy-start(f32[16,16,128]{2,1,0:T(8,128)} %broadcast_multiply_fusion) | copy-start | bytes 393220
  87.2 1.5 %copy-start.31 = (f32[16,16,128]{2,1,0:T(8,128)S(1)}, f32[16,16,128]{2,1,0:T(8,128)}, u32[]{:S(2)}) copy-start(f32[16,16,128]{2,1,0:T(8,128)} %get-tuple-element.59) | copy-start | bytes 393220
  90.6 2.0 %collective-permute-start.20 = (f32[16,8]{1,0:T(8,128)S(1)}, f32[16,8]{1,0:T(8,128)S(1)}, u32[]{:S(2)}, u32[]{:S(2)}) collective-permute-start(f32[16,8]{1,0:T(8,128)S(1)} %dynamic_update_slice.5), channel_id=1, source_target_pairs={{0,1},{1,0},{2,3},{3,2},{4,5},{5,4},{6,7},{7,6},{8,9},{9,8},{10,11... | collective-permute-start | bytes 1544 | tf_op jit(solution)/shard_map/ppermute | solution.py:135
  91.2 3.7 %collective-permute-start.21 = (f32[16,8]{1,0:T(8,128)S(1)}, f32[16,8]{1,0:T(8,128)S(1)}, u32[]{:S(2)}, u32[]{:S(2)}) collective-permute-start(f32[16,8]{1,0:T(8,128)S(1)} %dynamic_update_slice.5), channel_id=1, source_target_pairs={{0,2},{1,3},{2,0},{3,1},{4,6},{5,7},{6,4},{7,5},{8,10},{9,11},{10,... | collective-permute-start | bytes 1544 | tf_op jit(solution)/shard_map/ppermute | solution.py:135
  92.6 3.1 %collective-permute-start.22 = (f32[16,8]{1,0:T(8,128)S(1)}, f32[16,8]{1,0:T(8,128)S(1)}, u32[]{:S(2)}, u32[]{:S(2)}) collective-permute-start(f32[16,8]{1,0:T(8,128)S(1)} %dynamic_update_slice.5), channel_id=1, source_target_pairs={{0,3},{1,2},{2,1},{3,0},{4,7},{5,6},{6,5},{7,4},{8,11},{9,10},{10,... | collective-permute-start | bytes 1544 | tf_op jit(solution)/shard_map/ppermute | solution.py:135
  95.7 5.6 %collective-permute-start.23 = (f32[16,8]{1,0:T(8,128)S(1)}, f32[16,8]{1,0:T(8,128)S(1)}, u32[]{:S(2)}, u32[]{:S(2)}) collective-permute-start(f32[16,8]{1,0:T(8,128)S(1)} %add_add_fusion.4), channel_id=1, source_target_pairs={{0,4},{1,5},{2,6},{3,7},{4,0},{5,1},{6,2},{7,3},{8,12},{9,13},{10,... | collective-permute-start | bytes 1544 | tf_op jit(solution)/shard_map/ppermute | solution.py:135
  98.0 4.5 %collective-permute-start.24 = (f32[16,8]{1,0:T(8,128)S(1)}, f32[16,8]{1,0:T(8,128)S(1)}, u32[]{:S(2)}, u32[]{:S(2)}) collective-permute-start(f32[16,8]{1,0:T(8,128)S(1)} %add_add_fusion.4), channel_id=1, source_target_pairs={{0,8},{1,9},{2,10},{3,11},{4,12},{5,13},{6,14},{7,15},{8,0},{9,1},... | collective-permute-start | bytes 1544 | tf_op jit(solution)/shard_map/ppermute | solution.py:135
  98.1 5.4 %collective-permute-start.25 = (f32[16,8]{1,0:T(8,128)S(1)}, f32[16,8]{1,0:T(8,128)S(1)}, u32[]{:S(2)}, u32[]{:S(2)}) collective-permute-start(f32[16,8]{1,0:T(8,128)S(1)} %add_add_fusion.4), channel_id=1, source_target_pairs={{0,12},{1,13},{2,14},{3,15},{4,8},{5,9},{6,10},{7,11},{8,4},{9,5},... | collective-permute-start | bytes 1544 | tf_op jit(solution)/shard_map/ppermute | solution.py:135
  (16 other events, 16.2 us)

commit v3 on v2

--- a/solution.py
+++ b/solution.py
@@ -7,11 +7,14 @@
 RELAXATION = 0.6
 
 
-def with_halo(array, sides, width):
+def with_halo(array, sides, width, tie=None):
     for axis, dim in sides:
         peers, length = (lax.axis_size(axis), array.shape[dim])
         last = lax.slice_in_dim(array, length - width, length, axis=dim)
         initial = lax.slice_in_dim(array, 0, width, axis=dim)
+        if tie is not None and axis == sides[-1][0]:
+            last = last + tie
+            initial = initial + tie
         if peers == 2:
             first = lax.axis_index(axis) == 0
             got = lax.ppermute(jnp.where(first, last, initial), axis, [(0, 1), (1, 0)])
@@ -190,7 +193,8 @@
     gain_total_real = first[6:9]
     gain_total_imag = first[9:12]
     sweep_args = (lame_first, shear, density_cells, mask, source_cells, omega_sq, impedance)
-    padded = with_halo(field, (("gx", 1), ("gy", 2), ("col", 3)), 1)
+    tie = 0.0 * jnp.sum(mean_field)
+    padded = with_halo(field, (("gx", 1), ("gy", 2), ("col", 3)), 1, tie)
     field = sweep(padded, *sweep_args)
     second = group_sum(jnp.sum(mask * field, axis=(1, 2, 3)), axes)
     field = add_mean(field, gain_real, gain_imag, mean_field)

time: 105 us -> 106 us (level)
    select_n x2, local copies, waits for them, and re-layouts: 1.55 us -> 3.31 us  [with_halo(): after = jnp.where(first, got, zero)]
    select_n x2, local copies, waits for them, and re-layouts: 3.31 us -> 1.55 us  [with_halo(): before = jnp.where(first, zero, got)]
    slice x2 -> x1, local copies, waits for them, and re-layouts: 3.02 us -> 1.51 us  [with_halo(): initial = lax.slice_in_dim(array, 0, width, axis=dim)]
    ppermute x2, waiting for transfers between devices: 1.47 us -> 0.01 us  [with_halo(): before = lax.ppermute(last, axis, up)]
    ppermute x4, waiting for transfers between devices: 2.88 us -> 4.02 us  [with_halo(): got = lax.ppermute(jnp.where(first, last, initial), axis, [(0, 1), (1, 0)])]
    unnamed x82 -> x88, local copies, waits for them, and re-layouts: 9.46 us -> 9.45 us
  transfers between devices with their start and end apart: 26 -> 26, of which waited for: 11 -> 11; matrix products, arithmetic and copies ran while one was open for 13% -> 10% of each run, Pallas kernels for 0% -> 0%
where the time goes in v3:
time: 106 us; the launch traced here: 105 us
  starting transfers between devices  34.4 us (32%)
  other arithmetic  28.2 us (27%)
  local copies, waits for them, and re-layouts  24.3 us (23%)
  waiting for transfers between devices  15.9 us (15%)
  between operations  2.73 us (3%)
    ppermute x18, starting transfers between devices, group_sum(): lax.ppermute(value, axes, [(i, i ^ m * stride) for i in range(size)])  19 us
    ppermute x18, waiting for transfers between devices, group_sum(): lax.ppermute(value, axes, [(i, i ^ m * stride) for i in range(size)])  11.9 us
    concatenate x6, other arithmetic, with_halo(): array = jnp.concatenate([before, array, after], axis=dim)  10.5 us
    ppermute x2, starting transfers between devices, with_halo(): before = lax.ppermute(last, axis, up)  9.52 us
    unnamed x88, local copies, waits for them, and re-layouts  9.45 us
    add x12, other arithmetic, navier(): result.append(shear * laplace[channel] + (lame_first + shear) * divergence)  5.61 us
    ppermute x4, waiting for transfers between devices, with_halo(): got = lax.ppermute(jnp.where(first, last, initial), axis, [(0, 1), (1, 0)])  4.02 us
    select_n x2, local copies, waits for them, and re-layouts, with_halo(): after = jnp.where(first, got, zero)  3.31 us
  transfers between devices with their start and end apart: 26, of which 11 were waited for; matrix products, arithmetic and copies ran while one was open for 10% of the time, Pallas kernels for 0%

profile of v3, /device:TPU:0, one launch (start us, length us, event | category | flops | bytes accessed | tf_op | source)
XLA Modules:
  0.0 105.4 jit_solution(9028274155144225032)
XLA Ops:
  0.7 0.8 slice_bitcast_fusion.1
  2.1 0.8 slice_bitcast_fusion.2
  2.8 0.8 select_reduce_fusion.1
  4.8 1.5 %scatter_custom_fusion = f32[32768]{0:T(1024)S(1)} fusion(s32[256]{0:T(256)S(1)} %bitcast.22, f32[256]{0:T(256)S(1)} %broadcast.106, f32[]{:T(128)} %constant.18.clone.1), kind=kCustom, calls=%fused_computation.238 | custom fusion | bytes 131076 | tf_op jit(solution)/shard_map/scatter | solution.py:171
  6.5 0.7 convert_multiply_fusion
  7.7 2.9 %collective-permute-start.4 = (f32[12]{0:T(128)S(1)}, f32[12]{0:T(128)S(1)}, u32[]{:S(2)}, u32[]{:S(2)}) collective-permute-start(f32[12]{0:T(128)S(1)} %pad_maximum_fusion.19), channel_id=1, source_target_pairs={{0,2},{1,3},{2,0},{3,1},{4,6},{5,7},{6,4},{7,5},{8,10},{9,11},{10,... | collective-permute-start | bytes 152 | tf_op jit(solution)/shard_map/ppermute | solution.py:138
  10.8 1.3 %collective-permute-start = (f32[6,1,16,128]{3,2,1,0:T(8,128)S(1)}, f32[6,1,16,128]{3,2,1,0:T(8,128)S(1)}, u32[]{:S(2)}, u32[]{:S(2)}) collective-permute-start(f32[6,1,16,128]{3,2,1,0:T(8,128)S(1)} %get-tuple-element.50), channel_id=1, source_target_pairs={{4,0},{8,4},{12,8},{5,1},{9,5},{13,9},{6,2},{10,6},{14,10},{7,3},{... | collective-permute-start | bytes 147464 | tf_op jit(solution)/shard_map/ppermute | solution.py:28
  12.2 4.7 %collective-permute-start.1 = (f32[6,1,16,128]{3,2,1,0:T(8,128)S(1)}, f32[6,1,16,128]{3,2,1,0:T(8,128)S(1)}, u32[]{:S(2)}, u32[]{:S(2)}) collective-permute-start(f32[6,1,16,128]{3,2,1,0:T(8,128)S(1)} %get-tuple-element.49), channel_id=1, source_target_pairs={{0,4},{4,8},{8,12},{1,5},{5,9},{9,13},{2,6},{6,10},{10,14},{3,7},{... | collective-permute-start | bytes 147464 | tf_op jit(solution)/shard_map/ppermute | solution.py:27
  17.0 0.9 convert_element_type.15
  18.1 0.9 reshape.104
  19.2 0.9 reshape.105
  20.1 1.0 convert_element_type.13
  21.1 3.1 %collective-permute-start.7 = (f32[12]{0:T(128)S(1)}, f32[12]{0:T(128)S(1)}, u32[]{:S(2)}, u32[]{:S(2)}) collective-permute-start(f32[12]{0:T(128)S(1)} %add_add_fusion.9), channel_id=1, source_target_pairs={{0,8},{1,9},{2,10},{3,11},{4,12},{5,13},{6,14},{7,15},{8,0},{9,1},... | collective-permute-start | bytes 152 | tf_op jit(solution)/shard_map/ppermute | solution.py:138
  24.2 1.4 %collective-permute-start.8 = (f32[12]{0:T(128)S(1)}, f32[12]{0:T(128)S(1)}, u32[]{:S(2)}, u32[]{:S(2)}) collective-permute-start(f32[12]{0:T(128)S(1)} %add_add_fusion.9), channel_id=1, source_target_pairs={{0,12},{1,13},{2,14},{3,15},{4,8},{5,9},{6,10},{7,11},{8,4},{9,5},... | collective-permute-start | bytes 152 | tf_op jit(solution)/shard_map/ppermute | solution.py:138
  25.7 3.8 %collective-permute-done.8 = f32[12]{0:T(128)S(1)} collective-permute-done((f32[12]{0:T(128)S(1)}, f32[12]{0:T(128)S(1)}, u32[]{:S(2)}, u32[]{:S(2)}) %collective-permute-start.8) | collective-permute-done | bytes 80 | tf_op jit(solution)/shard_map/ppermute | solution.py:138
  30.2 1.6 %collective-permute-start.2 = (f32[6,18,1,128]{3,2,1,0:T(1,128)S(1)}, f32[6,18,1,128]{3,2,1,0:T(1,128)S(1)}, u32[]{:S(2)}, u32[]{:S(2)}) collective-permute-start(f32[6,18,1,128]{3,2,1,0:T(1,128)S(1)} %broadcast_select_fusion.7), channel_id=1, source_target_pairs={{0,2},{2,0},{1,3},{3,1},{4,6},{6,4},{5,7},{7,5},{8,10},{10,8},{9,1... | collective-permute-start | bytes 165896 | tf_op jit(solution)/shard_map/ppermute | solution.py:20
  33.0 1.4 %collective-permute-done.2 = f32[6,18,1,128]{3,2,1,0:T(1,128)S(1)} collective-permute-done((f32[6,18,1,128]{3,2,1,0:T(1,128)S(1)}, f32[6,18,1,128]{3,2,1,0:T(1,128)S(1)}, u32[]{:S(2)}, u32[]{:S(2)}) %collective-permute-start.2) | collective-permute-done | bytes 55328 | tf_op jit(solution)/shard_map/ppermute | solution.py:20
  34.8 1.5 %fusion.112 = (f32[6,18,18,1]{3,2,1,0:T(8,128)S(1)}, f32[6,18,18,1]{3,2,1,0:T(8,128)}) fusion(f32[6,18,18,128]{3,2,1,0:T(8,128)S(1)} %pad_maximum_fusion.3), kind=kLoop, calls=%fused_computation.277 | loop fusion | bytes 31104 | tf_op jit(solution)/shard_map/slice | solution.py:13
  36.3 2.0 %copy.176 = f32[6,18,18,1]{2,3,1,0:T(1,128)S(1)} copy(f32[6,18,18,1]{3,2,1,0:T(8,128)} %get-tuple-element.38) | data formatting | bytes 15552
  38.3 0.7 copy.175
  39.3 1.7 %pad_maximum_fusion.2 = (f32[6,18,17,128]{3,2,1,0:T(8,128)}, f32[6,18,17,128]{3,2,1,0:T(8,128)}) fusion(f32[6,18,1,128]{3,2,1,0:T(1,128)S(1)} %get-tuple-element.61, f32[6,1,16,128]{3,2,1,0:T(8,128)S(1)} %collective-permute-done, f32[6,16,16,128]{3,2,1,0:T(8,128)S(1)} %convert_element_type.12, f32[6,1,16,128]{3,2,1,0:T(8,128)S(1)} %collective-permute-done.1, ...), kind=kLoop, calls=%fused_computation.5 | loop fusion | flops 1410048 | bytes 2875392 | tf_op jit(solution)/shard_map/concatenate | solution.py:29
  41.6 0.8 copy.160
  42.4 1.7 %copy.157 = f32[6,18,18,1]{3,2,1,0:T(8,128)S(1)} copy(f32[6,18,18,1]{2,1,3,0:T(8,128)} %get-tuple-element.53) | data formatting | bytes 15552 | tf_op jit(solution)/shard_map/jit(_where)/select_n | solution.py:23
  44.1 3.1 %pad_maximum_fusion = (f32[6,18,18,129]{3,2,1,0:T(8,128)S(1)}, f32[6,18,18,129]{3,2,1,0:T(8,128)S(1)}) fusion(f32[6,18,18,1]{3,2,1,0:T(8,128)S(1)} %copy.157, f32[6,18,1,128]{3,2,1,0:T(1,128)} %copy-done.11, f32[6,1,16,128]{3,2,1,0:T(8,128)S(1)} %collective-permute-done, f32[6,16,16,128]{3,2,1,0:T(8,128)S(1)} %convert_element_type.12, ...), kind=kLoop, calls=%fused_computation.1 | loop fusion | flops 2507760 | bytes 3017088 | tf_op jit(solution)/shard_map/concatenate | solution.py:29
  53.3 1.5 %collective-permute-start.15 = (f32[6]{0:T(128)S(1)}, f32[6]{0:T(128)S(1)}, u32[]{:S(2)}, u32[]{:S(2)}) collective-permute-start(f32[6]{0:T(128)S(1)} %fusion.9), channel_id=1, source_target_pairs={{0,2},{1,3},{2,0},{3,1},{4,6},{5,7},{6,4},{7,5},{8,10},{9,11},{10,... | collective-permute-start | bytes 80 | tf_op jit(solution)/shard_map/ppermute | solution.py:138
  55.5 1.3 %collective-permute-start.10 = (f32[6,1,16,128]{3,2,1,0:T(8,128)S(1)}, f32[6,1,16,128]{3,2,1,0:T(8,128)S(1)}, u32[]{:S(2)}, u32[]{:S(2)}) collective-permute-start(f32[6,1,16,128]{3,2,1,0:T(8,128)S(1)} %get-tuple-element.48), channel_id=1, source_target_pairs={{4,0},{8,4},{12,8},{5,1},{9,5},{13,9},{6,2},{10,6},{14,10},{7,3},{... | collective-permute-start | bytes 147464 | tf_op jit(solution)/shard_map/ppermute | solution.py:28
  56.8 4.8 %collective-permute-start.11 = (f32[6,1,16,128]{3,2,1,0:T(8,128)S(1)}, f32[6,1,16,128]{3,2,1,0:T(8,128)S(1)}, u32[]{:S(2)}, u32[]{:S(2)}) collective-permute-start(f32[6,1,16,128]{3,2,1,0:T(8,128)S(1)} %get-tuple-element.47), channel_id=1, source_target_pairs={{0,4},{4,8},{8,12},{1,5},{5,9},{9,13},{2,6},{6,10},{10,14},{3,7},{... | collective-permute-start | bytes 147464 | tf_op jit(solution)/shard_map/ppermute | solution.py:27
  62.3 1.8 %collective-permute-start.19 = (f32[6]{0:T(128)S(1)}, f32[6]{0:T(128)S(1)}, u32[]{:S(2)}, u32[]{:S(2)}) collective-permute-start(f32[6]{0:T(128)S(1)} %add_add_fusion.7), channel_id=1, source_target_pairs={{0,12},{1,13},{2,14},{3,15},{4,8},{5,9},{6,10},{7,11},{8,4},{9,5},... | collective-permute-start | bytes 80 | tf_op jit(solution)/shard_map/ppermute | solution.py:138
  64.1 1.1 %collective-permute-start.17 = (f32[6]{0:T(128)S(1)}, f32[6]{0:T(128)S(1)}, u32[]{:S(2)}, u32[]{:S(2)}) collective-permute-start(f32[6]{0:T(128)S(1)} %add_add_fusion.7), channel_id=1, source_target_pairs={{0,4},{1,5},{2,6},{3,7},{4,0},{5,1},{6,2},{7,3},{8,12},{9,13},{10,... | collective-permute-start | bytes 80 | tf_op jit(solution)/shard_map/ppermute | solution.py:138
  65.2 0.9 collective-permute-done.18
  66.1 1.5 %collective-permute-done.19 = f32[6]{0:T(128)S(1)} collective-permute-done((f32[6]{0:T(128)S(1)}, f32[6]{0:T(128)S(1)}, u32[]{:S(2)}, u32[]{:S(2)}) %collective-permute-start.19) | collective-permute-done | bytes 56 | tf_op jit(solution)/shard_map/ppermute | solution.py:138
  67.9 1.6 %collective-permute-start.12 = (f32[6,18,1,128]{3,2,1,0:T(1,128)S(1)}, f32[6,18,1,128]{3,2,1,0:T(1,128)S(1)}, u32[]{:S(2)}, u32[]{:S(2)}) collective-permute-start(f32[6,18,1,128]{3,2,1,0:T(1,128)S(1)} %broadcast_select_fusion.4), channel_id=1, source_target_pairs={{0,2},{2,0},{1,3},{3,1},{4,6},{6,4},{5,7},{7,5},{8,10},{10,8},{9,1... | collective-permute-start | bytes 165896 | tf_op jit(solution)/shard_map/ppermute | solution.py:20
  69.5 2.6 %collective-permute-done.12 = f32[6,18,1,128]{3,2,1,0:T(1,128)S(1)} collective-permute-done((f32[6,18,1,128]{3,2,1,0:T(1,128)S(1)}, f32[6,18,1,128]{3,2,1,0:T(1,128)S(1)}, u32[]{:S(2)}, u32[]{:S(2)}) %collective-permute-start.12) | collective-permute-done | bytes 55328 | tf_op jit(solution)/shard_map/ppermute | solution.py:20
  72.4 1.5 %fusion.111 = (f32[6,18,18,1]{3,2,1,0:T(8,128)S(1)}, f32[6,18,18,1]{3,2,1,0:T(8,128)}) fusion(f32[6,18,18,128]{3,2,1,0:T(8,128)S(1)} %pad_maximum_fusion.5), kind=kLoop, calls=%fused_computation.276 | loop fusion | bytes 31104 | tf_op jit(solution)/shard_map/slice | solution.py:14
  73.9 2.0 %copy.177 = f32[6,18,18,1]{2,3,1,0:T(1,128)S(1)} copy(f32[6,18,18,1]{3,2,1,0:T(8,128)} %get-tuple-element.36) | data formatting | bytes 15552
  76.0 0.7 copy.178
  76.9 1.7 %pad_maximum_fusion.4 = (f32[6,18,17,128]{3,2,1,0:T(8,128)}, f32[6,18,17,128]{3,2,1,0:T(8,128)}) fusion(f32[6,18,1,128]{3,2,1,0:T(1,128)S(1)} %get-tuple-element.59, f32[6,1,16,128]{3,2,1,0:T(8,128)S(1)} %collective-permute-done.10, f32[3,16,16,128]{3,2,1,0:T(8,128)S(1)} %get-tuple-element.27, f32[3,16,16,128]{3,2,1,0:T(8,128)S(1)} %get-tuple-element.23, ...), kind=kLoop, calls=%fused_computation.8 | loop fusion | flops 1880064 | bytes 2875392 | tf_op jit(solution)/shard_map/concatenate | solution.py:29
  79.2 0.8 copy.169
  80.0 1.7 %copy.166 = f32[6,18,18,1]{3,2,1,0:T(8,128)S(1)} copy(f32[6,18,18,1]{2,1,3,0:T(8,128)} %get-tuple-element.51) | data formatting | bytes 15552 | tf_op jit(solution)/shard_map/jit(_where)/select_n | solution.py:23
  81.7 3.6 %pad_maximum_fusion.1 = (f32[6,18,18,129]{3,2,1,0:T(8,128)S(1)}, f32[6,18,18,129]{3,2,1,0:T(8,128)S(1)}) fusion(f32[6,18,18,1]{3,2,1,0:T(8,128)S(1)} %copy.166, f32[6,18,1,128]{3,2,1,0:T(1,128)} %copy-done.15, f32[6,1,16,128]{3,2,1,0:T(8,128)S(1)} %collective-permute-done.10, f32[3,16,16,128]{3,2,1,0:T(8,128)S(1)} %get-tuple-element.27, ...), kind=kLoop, calls=%fused_computation.3 | loop fusion | flops 3009312 | bytes 3017088 | tf_op jit(solution)/shard_map/concatenate | solution.py:29
  90.3 0.9 subtract_reduce_fusion
  92.8 1.7 %collective-permute-start.21 = (f32[16,8]{1,0:T(8,128)S(1)}, f32[16,8]{1,0:T(8,128)S(1)}, u32[]{:S(2)}, u32[]{:S(2)}) collective-permute-start(f32[16,8]{1,0:T(8,128)S(1)} %dynamic_update_slice.5), channel_id=1, source_target_pairs={{0,2},{1,3},{2,0},{3,1},{4,6},{5,7},{6,4},{7,5},{8,10},{9,11},{10,... | collective-permute-start | bytes 1544 | tf_op jit(solution)/shard_map/ppermute | solution.py:138
  94.9 1.6 %collective-permute-done.21 = f32[16,8]{1,0:T(8,128)S(1)} collective-permute-done((f32[16,8]{1,0:T(8,128)S(1)}, f32[16,8]{1,0:T(8,128)S(1)}, u32[]{:S(2)}, u32[]{:S(2)}) %collective-permute-start.21) | collective-permute-done | bytes 544 | tf_op jit(solution)/shard_map/ppermute | solution.py:138
  96.5 1.2 %collective-permute-done.22 = f32[16,8]{1,0:T(8,128)S(1)} collective-permute-done((f32[16,8]{1,0:T(8,128)S(1)}, f32[16,8]{1,0:T(8,128)S(1)}, u32[]{:S(2)}, u32[]{:S(2)}) %collective-permute-start.22) | collective-permute-done | bytes 544 | tf_op jit(solution)/shard_map/ppermute | solution.py:138
  98.1 3.0 %collective-permute-start.25 = (f32[16,8]{1,0:T(8,128)S(1)}, f32[16,8]{1,0:T(8,128)S(1)}, u32[]{:S(2)}, u32[]{:S(2)}) collective-permute-start(f32[16,8]{1,0:T(8,128)S(1)} %add_add_fusion.4), channel_id=1, source_target_pairs={{0,12},{1,13},{2,14},{3,15},{4,8},{5,9},{6,10},{7,11},{8,4},{9,5},... | collective-permute-start | bytes 1544 | tf_op jit(solution)/shard_map/ppermute | solution.py:138
  101.1 0.9 pad_maximum_fusion.13
  102.2 1.4 %collective-permute-done.25 = f32[16,8]{1,0:T(8,128)S(1)} collective-permute-done((f32[16,8]{1,0:T(8,128)S(1)}, f32[16,8]{1,0:T(8,128)S(1)}, u32[]{:S(2)}, u32[]{:S(2)}) %collective-permute-start.25) | collective-permute-done | bytes 544 | tf_op jit(solution)/shard_map/ppermute | solution.py:138
  103.6 1.2 %collective-permute-done.23 = f32[16,8]{1,0:T(8,128)S(1)} collective-permute-done((f32[16,8]{1,0:T(8,128)S(1)}, f32[16,8]{1,0:T(8,128)S(1)}, u32[]{:S(2)}, u32[]{:S(2)}) %collective-permute-start.23) | collective-permute-done | bytes 544 | tf_op jit(solution)/shard_map/ppermute | solution.py:138
  (173 shorter events, 21.8 us)
Async XLA Ops:
  0.6 5.6 %copy-start.17 = (bf16[6,16,16,128]{3,2,1,0:T(8,128)(2,1)S(1)}, bf16[6,16,16,128]{3,2,1,0:T(8,128)(2,1)}, u32[]{:S(2)}) copy-start(bf16[6,16,16,128]{3,2,1,0:T(8,128)(2,1)} %param.10) | copy-start | bytes 1179652
  0.6 5.8 %copy-start.38 = (bf16[16,16,128]{2,1,0:T(8,128)(2,1)S(1)}, bf16[16,16,128]{2,1,0:T(8,128)(2,1)}, u32[]{:S(2)}) copy-start(bf16[16,16,128]{2,1,0:T(8,128)(2,1)} %param.12) | copy-start | bytes 196612
  6.3 5.9 %copy-start.4 = (f32[32768]{0:T(1024)}, f32[32768]{0:T(1024)S(1)}, u32[]{:S(2)}) copy-start(f32[32768]{0:T(1024)S(1)} %scatter_custom_fusion) | copy-start | bytes 393220
  6.5 10.6 %copy-start.36 = (bf16[6,16,16,128]{3,2,1,0:T(8,128)(2,1)S(1)}, bf16[6,16,16,128]{3,2,1,0:T(8,128)(2,1)}, u32[]{:S(2)}) copy-start(bf16[6,16,16,128]{3,2,1,0:T(8,128)(2,1)} %param.11) | copy-start | bytes 1179652
  7.2 5.0 %copy-start.23 = (f32[16,16,128]{2,1,0:T(8,128)}, f32[16,16,128]{2,1,0:T(8,128)S(1)}, u32[]{:S(2)}) copy-start(f32[16,16,128]{2,1,0:T(8,128)S(1)} %get-tuple-element.56) | copy-start | bytes 393220
  7.2 5.0 %copy-start.26 = (f32[16,16,128]{2,1,0:T(8,128)}, f32[16,16,128]{2,1,0:T(8,128)S(1)}, u32[]{:S(2)}) copy-start(f32[16,16,128]{2,1,0:T(8,128)S(1)} %get-tuple-element.57) | copy-start | bytes 393220
  7.2 5.0 %copy-start.29 = (f32[16,16,128]{2,1,0:T(8,128)}, f32[16,16,128]{2,1,0:T(8,128)S(1)}, u32[]{:S(2)}) copy-start(f32[16,16,128]{2,1,0:T(8,128)S(1)} %get-tuple-element.74) | copy-start | bytes 393220
  7.7 13.4 %collective-permute-start.4 = (f32[12]{0:T(128)S(1)}, f32[12]{0:T(128)S(1)}, u32[]{:S(2)}, u32[]{:S(2)}) collective-permute-start(f32[12]{0:T(128)S(1)} %pad_maximum_fusion.19), channel_id=1, source_target_pairs={{0,2},{1,3},{2,0},{3,1},{4,6},{5,7},{6,4},{7,5},{8,10},{9,11},{10,... | collective-permute-start | bytes 152 | tf_op jit(solution)/shard_map/ppermute | solution.py:138
  10.6 10.5 %collective-permute-start.5 = (f32[12]{0:T(128)S(1)}, f32[12]{0:T(128)S(1)}, u32[]{:S(2)}, u32[]{:S(2)}) collective-permute-start(f32[12]{0:T(128)S(1)} %pad_maximum_fusion.19), channel_id=1, source_target_pairs={{0,3},{1,2},{2,1},{3,0},{4,7},{5,6},{6,5},{7,4},{8,11},{9,10},{10,... | collective-permute-start | bytes 152 | tf_op jit(solution)/shard_map/ppermute | solution.py:138
  10.6 10.5 %collective-permute-start.3 = (f32[12]{0:T(128)S(1)}, f32[12]{0:T(128)S(1)}, u32[]{:S(2)}, u32[]{:S(2)}) collective-permute-start(f32[12]{0:T(128)S(1)} %pad_maximum_fusion.19), channel_id=1, source_target_pairs={{0,1},{1,0},{2,3},{3,2},{4,5},{5,4},{6,7},{7,6},{8,9},{9,8},{10,11... | collective-permute-start | bytes 152 | tf_op jit(solution)/shard_map/ppermute | solution.py:138
  10.8 19.3 %collective-permute-start = (f32[6,1,16,128]{3,2,1,0:T(8,128)S(1)}, f32[6,1,16,128]{3,2,1,0:T(8,128)S(1)}, u32[]{:S(2)}, u32[]{:S(2)}) collective-permute-start(f32[6,1,16,128]{3,2,1,0:T(8,128)S(1)} %get-tuple-element.50), channel_id=1, source_target_pairs={{4,0},{8,4},{12,8},{5,1},{9,5},{13,9},{6,2},{10,6},{14,10},{7,3},{... | collective-permute-start | bytes 147464 | tf_op jit(solution)/shard_map/ppermute | solution.py:28
  12.2 18.0 %collective-permute-start.1 = (f32[6,1,16,128]{3,2,1,0:T(8,128)S(1)}, f32[6,1,16,128]{3,2,1,0:T(8,128)S(1)}, u32[]{:S(2)}, u32[]{:S(2)}) collective-permute-start(f32[6,1,16,128]{3,2,1,0:T(8,128)S(1)} %get-tuple-element.49), channel_id=1, source_target_pairs={{0,4},{4,8},{8,12},{1,5},{5,9},{9,13},{2,6},{6,10},{10,14},{3,7},{... | collective-permute-start | bytes 147464 | tf_op jit(solution)/shard_map/ppermute | solution.py:27
  18.0 2.2 %copy-start.37 = (bf16[6,16,16,128]{3,2,1,0:T(8,128)(2,1)S(1)}, bf16[6,16,16,128]{3,2,1,0:T(8,128)(2,1)}, u32[]{:S(2)}) copy-start(bf16[6,16,16,128]{3,2,1,0:T(8,128)(2,1)} %param.9) | copy-start | bytes 1179652
  21.1 4.6 %collective-permute-start.7 = (f32[12]{0:T(128)S(1)}, f32[12]{0:T(128)S(1)}, u32[]{:S(2)}, u32[]{:S(2)}) collective-permute-start(f32[12]{0:T(128)S(1)} %add_add_fusion.9), channel_id=1, source_target_pairs={{0,8},{1,9},{2,10},{3,11},{4,12},{5,13},{6,14},{7,15},{8,0},{9,1},... | collective-permute-start | bytes 152 | tf_op jit(solution)/shard_map/ppermute | solution.py:138
  24.2 5.3 %collective-permute-start.8 = (f32[12]{0:T(128)S(1)}, f32[12]{0:T(128)S(1)}, u32[]{:S(2)}, u32[]{:S(2)}) collective-permute-start(f32[12]{0:T(128)S(1)} %add_add_fusion.9), channel_id=1, source_target_pairs={{0,12},{1,13},{2,14},{3,15},{4,8},{5,9},{6,10},{7,11},{8,4},{9,5},... | collective-permute-start | bytes 152 | tf_op jit(solution)/shard_map/ppermute | solution.py:138
  25.6 4.0 %collective-permute-start.6 = (f32[12]{0:T(128)S(1)}, f32[12]{0:T(128)S(1)}, u32[]{:S(2)}, u32[]{:S(2)}) collective-permute-start(f32[12]{0:T(128)S(1)} %add_add_fusion.9), channel_id=1, source_target_pairs={{0,4},{1,5},{2,6},{3,7},{4,0},{5,1},{6,2},{7,3},{8,12},{9,13},{10,... | collective-permute-start | bytes 152 | tf_op jit(solution)/shard_map/ppermute | solution.py:138
  30.2 4.2 %collective-permute-start.2 = (f32[6,18,1,128]{3,2,1,0:T(1,128)S(1)}, f32[6,18,1,128]{3,2,1,0:T(1,128)S(1)}, u32[]{:S(2)}, u32[]{:S(2)}) collective-permute-start(f32[6,18,1,128]{3,2,1,0:T(1,128)S(1)} %broadcast_select_fusion.7), channel_id=1, source_target_pairs={{0,2},{2,0},{1,3},{3,1},{4,6},{6,4},{5,7},{7,5},{8,10},{10,8},{9,1... | collective-permute-start | bytes 165896 | tf_op jit(solution)/shard_map/ppermute | solution.py:20
  34.5 4.7 %copy-start.9 = (f32[6,18,1,128]{3,2,1,0:T(1,128)}, f32[6,18,1,128]{3,2,1,0:T(1,128)S(1)}, u32[]{:S(2)}) copy-start(f32[6,18,1,128]{3,2,1,0:T(1,128)S(1)} %get-tuple-element.60) | copy-start | bytes 165892
  34.6 4.7 %copy-start.11 = (f32[6,18,1,128]{3,2,1,0:T(1,128)}, f32[6,18,1,128]{3,2,1,0:T(1,128)S(1)}, u32[]{:S(2)}) copy-start(f32[6,18,1,128]{3,2,1,0:T(1,128)S(1)} %get-tuple-element.61) | copy-start | bytes 165892
  39.2 1.8 %collective-permute-start.9 = (f32[6,18,18,1]{2,1,3,0:T(8,128)S(1)}, f32[6,18,18,1]{2,1,3,0:T(8,128)S(1)}, u32[]{:S(2)}, u32[]{:S(2)}) collective-permute-start(f32[6,18,18,1]{2,1,3,0:T(8,128)S(1)} %copy.154), channel_id=1, source_target_pairs={{0,1},{1,0},{2,3},{3,2},{4,5},{5,4},{6,7},{7,6},{8,9},{9,8},{10,11... | collective-permute-start | bytes 23336 | tf_op jit(solution)/shard_map/ppermute | solution.py:20
  44.0 3.1 %copy-start.18 = (bf16[6,16,16,128]{3,2,1,0:T(8,128)(2,1)S(1)}, bf16[6,16,16,128]{3,2,1,0:T(8,128)(2,1)}, u32[]{:S(2)}) copy-start(bf16[6,16,16,128]{3,2,1,0:T(8,128)(2,1)} %param.10) | copy-start | bytes 1179652
  44.0 3.1 %copy-start.21 = (f32[6,18,17,128]{3,2,1,0:T(8,128)S(1)}, f32[6,18,17,128]{3,2,1,0:T(8,128)}, u32[]{:S(2)}) copy-start(f32[6,18,17,128]{3,2,1,0:T(8,128)} %get-tuple-element.45) | copy-start | bytes 2820100
  44.0 3.1 %copy-start.22 = (f32[6,18,17,128]{3,2,1,0:T(8,128)S(1)}, f32[6,18,17,128]{3,2,1,0:T(8,128)}, u32[]{:S(2)}) copy-start(f32[6,18,17,128]{3,2,1,0:T(8,128)} %get-tuple-element.46) | copy-start | bytes 2820100
  48.6 2.1 %copy-start.2 = (f32[1,16,16,128]{3,2,1,0:T(8,128)}, f32[1,16,16,128]{3,2,1,0:T(8,128)S(1)}, u32[]{:S(2)}) copy-start(f32[1,16,16,128]{3,2,1,0:T(8,128)S(1)} %get-tuple-element.30) | copy-start | bytes 393220
  50.7 1.3 %copy-start.33 = (f32[16,16,128]{2,1,0:T(8,128)S(1)}, f32[16,16,128]{2,1,0:T(8,128)}, u32[]{:S(2)}) copy-start(f32[16,16,128]{2,1,0:T(8,128)} %get-tuple-element.55) | copy-start | bytes 393220
  50.7 1.3 %copy-start.39 = (f32[3]{0:T(128)S(1)}, f32[3]{0:T(128)}, u32[]{:S(2)}) copy-start(f32[3]{0:T(128)} %get-tuple-element.72) | copy-start | bytes 40
  53.3 8.3 %collective-permute-start.15 = (f32[6]{0:T(128)S(1)}, f32[6]{0:T(128)S(1)}, u32[]{:S(2)}, u32[]{:S(2)}) collective-permute-start(f32[6]{0:T(128)S(1)} %fusion.9), channel_id=1, source_target_pairs={{0,2},{1,3},{2,0},{3,1},{4,6},{5,7},{6,4},{7,5},{8,10},{9,11},{10,... | collective-permute-start | bytes 80 | tf_op jit(solution)/shard_map/ppermute | solution.py:138
  54.9 6.7 %collective-permute-start.16 = (f32[6]{0:T(128)S(1)}, f32[6]{0:T(128)S(1)}, u32[]{:S(2)}, u32[]{:S(2)}) collective-permute-start(f32[6]{0:T(128)S(1)} %fusion.9), channel_id=1, source_target_pairs={{0,3},{1,2},{2,1},{3,0},{4,7},{5,6},{6,5},{7,4},{8,11},{9,10},{10,... | collective-permute-start | bytes 80 | tf_op jit(solution)/shard_map/ppermute | solution.py:138
  55.2 6.4 %collective-permute-start.14 = (f32[6]{0:T(128)S(1)}, f32[6]{0:T(128)S(1)}, u32[]{:S(2)}, u32[]{:S(2)}) collective-permute-start(f32[6]{0:T(128)S(1)} %fusion.9), channel_id=1, source_target_pairs={{0,1},{1,0},{2,3},{3,2},{4,5},{5,4},{6,7},{7,6},{8,9},{9,8},{10,11... | collective-permute-start | bytes 80 | tf_op jit(solution)/shard_map/ppermute | solution.py:138
  55.5 12.3 %collective-permute-start.10 = (f32[6,1,16,128]{3,2,1,0:T(8,128)S(1)}, f32[6,1,16,128]{3,2,1,0:T(8,128)S(1)}, u32[]{:S(2)}, u32[]{:S(2)}) collective-permute-start(f32[6,1,16,128]{3,2,1,0:T(8,128)S(1)} %get-tuple-element.48), channel_id=1, source_target_pairs={{4,0},{8,4},{12,8},{5,1},{9,5},{13,9},{6,2},{10,6},{14,10},{7,3},{... | collective-permute-start | bytes 147464 | tf_op jit(solution)/shard_map/ppermute | solution.py:28
  56.8 11.0 %collective-permute-start.11 = (f32[6,1,16,128]{3,2,1,0:T(8,128)S(1)}, f32[6,1,16,128]{3,2,1,0:T(8,128)S(1)}, u32[]{:S(2)}, u32[]{:S(2)}) collective-permute-start(f32[6,1,16,128]{3,2,1,0:T(8,128)S(1)} %get-tuple-element.47), channel_id=1, source_target_pairs={{0,4},{4,8},{8,12},{1,5},{5,9},{9,13},{2,6},{6,10},{10,14},{3,7},{... | collective-permute-start | bytes 147464 | tf_op jit(solution)/shard_map/ppermute | solution.py:27
  61.6 4.5 %collective-permute-start.18 = (f32[6]{0:T(128)S(1)}, f32[6]{0:T(128)S(1)}, u32[]{:S(2)}, u32[]{:S(2)}) collective-permute-start(f32[6]{0:T(128)S(1)} %add_add_fusion.7), channel_id=1, source_target_pairs={{0,8},{1,9},{2,10},{3,11},{4,12},{5,13},{6,14},{7,15},{8,0},{9,1},... | collective-permute-start | bytes 80 | tf_op jit(solution)/shard_map/ppermute | solution.py:138
  62.3 5.3 %collective-permute-start.19 = (f32[6]{0:T(128)S(1)}, f32[6]{0:T(128)S(1)}, u32[]{:S(2)}, u32[]{:S(2)}) collective-permute-start(f32[6]{0:T(128)S(1)} %add_add_fusion.7), channel_id=1, source_target_pairs={{0,12},{1,13},{2,14},{3,15},{4,8},{5,9},{6,10},{7,11},{8,4},{9,5},... | collective-permute-start | bytes 80 | tf_op jit(solution)/shard_map/ppermute | solution.py:138
  64.1 3.5 %collective-permute-start.17 = (f32[6]{0:T(128)S(1)}, f32[6]{0:T(128)S(1)}, u32[]{:S(2)}, u32[]{:S(2)}) collective-permute-start(f32[6]{0:T(128)S(1)} %add_add_fusion.7), channel_id=1, source_target_pairs={{0,4},{1,5},{2,6},{3,7},{4,0},{5,1},{6,2},{7,3},{8,12},{9,13},{10,... | collective-permute-start | bytes 80 | tf_op jit(solution)/shard_map/ppermute | solution.py:138
  67.9 4.2 %collective-permute-start.12 = (f32[6,18,1,128]{3,2,1,0:T(1,128)S(1)}, f32[6,18,1,128]{3,2,1,0:T(1,128)S(1)}, u32[]{:S(2)}, u32[]{:S(2)}) collective-permute-start(f32[6,18,1,128]{3,2,1,0:T(1,128)S(1)} %broadcast_select_fusion.4), channel_id=1, source_target_pairs={{0,2},{2,0},{1,3},{3,1},{4,6},{6,4},{5,7},{7,5},{8,10},{10,8},{9,1... | collective-permute-start | bytes 165896 | tf_op jit(solution)/shard_map/ppermute | solution.py:20
  72.2 4.7 %copy-start.13 = (f32[6,18,1,128]{3,2,1,0:T(1,128)}, f32[6,18,1,128]{3,2,1,0:T(1,128)S(1)}, u32[]{:S(2)}) copy-start(f32[6,18,1,128]{3,2,1,0:T(1,128)S(1)} %get-tuple-element.58) | copy-start | bytes 165892
  72.2 4.7 %copy-start.15 = (f32[6,18,1,128]{3,2,1,0:T(1,128)}, f32[6,18,1,128]{3,2,1,0:T(1,128)S(1)}, u32[]{:S(2)}) copy-start(f32[6,18,1,128]{3,2,1,0:T(1,128)S(1)} %get-tuple-element.59) | copy-start | bytes 165892
  76.8 1.8 %collective-permute-start.13 = (f32[6,18,18,1]{2,1,3,0:T(8,128)S(1)}, f32[6,18,18,1]{2,1,3,0:T(8,128)S(1)}, u32[]{:S(2)}, u32[]{:S(2)}) collective-permute-start(f32[6,18,18,1]{2,1,3,0:T(8,128)S(1)} %copy.163), channel_id=1, source_target_pairs={{0,1},{1,0},{2,3},{3,2},{4,5},{5,4},{6,7},{7,6},{8,9},{9,8},{10,11... | collective-permute-start | bytes 23336 | tf_op jit(solution)/shard_map/ppermute | solution.py:20
  81.7 3.6 %copy-start.19 = (f32[6,18,17,128]{3,2,1,0:T(8,128)S(1)}, f32[6,18,17,128]{3,2,1,0:T(8,128)}, u32[]{:S(2)}) copy-start(f32[6,18,17,128]{3,2,1,0:T(8,128)} %get-tuple-element.43) | copy-start | bytes 2820100
  81.7 3.7 %copy-start.20 = (f32[6,18,17,128]{3,2,1,0:T(8,128)S(1)}, f32[6,18,17,128]{3,2,1,0:T(8,128)}, u32[]{:S(2)}) copy-start(f32[6,18,17,128]{3,2,1,0:T(8,128)} %get-tuple-element.44) | copy-start | bytes 2820100
  88.8 1.5 %copy-start.32 = (f32[6,16,16,128]{3,2,1,0:T(8,128)S(1)}, f32[6,16,16,128]{3,2,1,0:T(8,128)}, u32[]{:S(2)}) copy-start(f32[6,16,16,128]{3,2,1,0:T(8,128)} %convert_element_type.15) | copy-start | bytes 2359300
  88.8 1.5 %copy-start.34 = (f32[16,16,128]{2,1,0:T(8,128)S(1)}, f32[16,16,128]{2,1,0:T(8,128)}, u32[]{:S(2)}) copy-start(f32[16,16,128]{2,1,0:T(8,128)} %get-tuple-element.55) | copy-start | bytes 393220
  92.3 2.2 %collective-permute-start.20 = (f32[16,8]{1,0:T(8,128)S(1)}, f32[16,8]{1,0:T(8,128)S(1)}, u32[]{:S(2)}, u32[]{:S(2)}) collective-permute-start(f32[16,8]{1,0:T(8,128)S(1)} %dynamic_update_slice.5), channel_id=1, source_target_pairs={{0,1},{1,0},{2,3},{3,2},{4,5},{5,4},{6,7},{7,6},{8,9},{9,8},{10,11... | collective-permute-start | bytes 1544 | tf_op jit(solution)/shard_map/ppermute | solution.py:138
  92.8 3.7 %collective-permute-start.21 = (f32[16,8]{1,0:T(8,128)S(1)}, f32[16,8]{1,0:T(8,128)S(1)}, u32[]{:S(2)}, u32[]{:S(2)}) collective-permute-start(f32[16,8]{1,0:T(8,128)S(1)} %dynamic_update_slice.5), channel_id=1, source_target_pairs={{0,2},{1,3},{2,0},{3,1},{4,6},{5,7},{6,4},{7,5},{8,10},{9,11},{10,... | collective-permute-start | bytes 1544 | tf_op jit(solution)/shard_map/ppermute | solution.py:138
  94.5 3.1 %collective-permute-start.22 = (f32[16,8]{1,0:T(8,128)S(1)}, f32[16,8]{1,0:T(8,128)S(1)}, u32[]{:S(2)}, u32[]{:S(2)}) collective-permute-start(f32[16,8]{1,0:T(8,128)S(1)} %dynamic_update_slice.5), channel_id=1, source_target_pairs={{0,3},{1,2},{2,1},{3,0},{4,7},{5,6},{6,5},{7,4},{8,11},{9,10},{10,... | collective-permute-start | bytes 1544 | tf_op jit(solution)/shard_map/ppermute | solution.py:138
  97.6 4.5 %collective-permute-start.24 = (f32[16,8]{1,0:T(8,128)S(1)}, f32[16,8]{1,0:T(8,128)S(1)}, u32[]{:S(2)}, u32[]{:S(2)}) collective-permute-start(f32[16,8]{1,0:T(8,128)S(1)} %add_add_fusion.4), channel_id=1, source_target_pairs={{0,8},{1,9},{2,10},{3,11},{4,12},{5,13},{6,14},{7,15},{8,0},{9,1},... | collective-permute-start | bytes 1544 | tf_op jit(solution)/shard_map/ppermute | solution.py:138
  98.1 5.4 %collective-permute-start.25 = (f32[16,8]{1,0:T(8,128)S(1)}, f32[16,8]{1,0:T(8,128)S(1)}, u32[]{:S(2)}, u32[]{:S(2)}) collective-permute-start(f32[16,8]{1,0:T(8,128)S(1)} %add_add_fusion.4), channel_id=1, source_target_pairs={{0,12},{1,13},{2,14},{3,15},{4,8},{5,9},{6,10},{7,11},{8,4},{9,5},... | collective-permute-start | bytes 1544 | tf_op jit(solution)/shard_map/ppermute | solution.py:138
  101.1 3.7 %collective-permute-start.23 = (f32[16,8]{1,0:T(8,128)S(1)}, f32[16,8]{1,0:T(8,128)S(1)}, u32[]{:S(2)}, u32[]{:S(2)}) collective-permute-start(f32[16,8]{1,0:T(8,128)S(1)} %add_add_fusion.4), channel_id=1, source_target_pairs={{0,4},{1,5},{2,6},{3,7},{4,0},{5,1},{6,2},{7,3},{8,12},{9,13},{10,... | collective-permute-start | bytes 1544 | tf_op jit(solution)/shard_map/ppermute | solution.py:138
  (19 other events, 20.3 us)

commit v4 on v3

--- a/solution.py
+++ b/solution.py
@@ -133,16 +133,8 @@
         return lax.psum(value, axes)
     stride = 1
     while stride < size:
-        if stride * 4 <= size:
-            got = [
-                lax.ppermute(value, axes, [(i, i ^ (m * stride)) for i in range(size)])
-                for m in (1, 2, 3)
-            ]
-            value = (value + got[0]) + (got[1] + got[2])
-            stride *= 4
-        else:
-            value = value + lax.ppermute(value, axes, [(i, i ^ stride) for i in range(size)])
-            stride *= 2
+        value = value + lax.ppermute(value, axes, [(i, i ^ stride) for i in range(size)])
+        stride *= 2
     return value
 
 

time: 106 us -> 112 us (1.057)
  starting transfers between devices: 34.4 us -> 38.3 us
  waiting for transfers between devices: 15.9 us -> 18.1 us
    ppermute x18 -> x12, starting transfers between devices: 19 us -> 22 us  [group_sum(): lax.ppermute(value, axes, [(i, i ^ stride) for i in range(size)])]
    ppermute x18 -> x12, waiting for transfers between devices: 11.9 us -> 14.7 us  [group_sum(): lax.ppermute(value, axes, [(i, i ^ stride) for i in range(size)])]
    unnamed x88 -> x90, local copies, waits for them, and re-layouts: 9.45 us -> 9.46 us
  transfers between devices with their start and end apart: 26 -> 20, of which waited for: 11 -> 12; matrix products, arithmetic and copies ran while one was open for 10% -> 9% of each run, Pallas kernels for 0% -> 0%
where the time goes in v4:
time: 112 us
  starting transfers between devices  38.3 us (34%)
  other arithmetic  28.2 us (25%)
  local copies, waits for them, and re-layouts  24.3 us (22%)
  waiting for transfers between devices  18.1 us (16%)
  between operations  2.7 us (2%)
    ppermute x12, starting transfers between devices, group_sum(): lax.ppermute(value, axes, [(i, i ^ stride) for i in range(size)])  22 us
    ppermute x12, waiting for transfers between devices, group_sum(): lax.ppermute(value, axes, [(i, i ^ stride) for i in range(size)])  14.7 us
    concatenate x6, other arithmetic, with_halo(): array = jnp.concatenate([before, array, after], axis=dim)  10.5 us
    ppermute x2, starting transfers between devices, with_halo(): before = lax.ppermute(last, axis, up)  9.85 us
    unnamed x90, local copies, waits for them, and re-layouts  9.46 us
    add x12, other arithmetic, navier(): result.append(shear * laplace[channel] + (lame_first + shear) * divergence)  5.61 us
    ppermute x4, starting transfers between devices, with_halo(): got = lax.ppermute(jnp.where(first, last, initial), axis, [(0, 1), (1, 0)])  3.92 us
    ppermute x4, waiting for transfers between devices, with_halo(): got = lax.ppermute(jnp.where(first, last, initial), axis, [(0, 1), (1, 0)])  3.35 us
  transfers between devices with their start and end apart: 20, of which 12 were waited for; matrix products, arithmetic and copies ran while one was open for 9% of the time, Pallas kernels for 0%

profile of v4, /device:TPU:0, one launch (start us, length us, event | category | flops | bytes accessed | tf_op | source)
XLA Modules:
  0.0 111.6 jit_solution(7751140185578130765)
XLA Ops:
  2.1 0.8 slice_bitcast_fusion.2
  2.8 0.8 select_reduce_fusion.1
  4.8 1.5 %scatter_custom_fusion = f32[32768]{0:T(1024)S(1)} fusion(s32[256]{0:T(256)S(1)} %bitcast.22, f32[256]{0:T(256)S(1)} %broadcast.106, f32[]{:T(128)} %constant.18.clone.1), kind=kCustom, calls=%fused_computation.238 | custom fusion | bytes 131076 | tf_op jit(solution)/shard_map/scatter | solution.py:163
  8.2 1.3 %collective-permute-start = (f32[6,1,16,128]{3,2,1,0:T(8,128)S(1)}, f32[6,1,16,128]{3,2,1,0:T(8,128)S(1)}, u32[]{:S(2)}, u32[]{:S(2)}) collective-permute-start(f32[6,1,16,128]{3,2,1,0:T(8,128)S(1)} %get-tuple-element.50), channel_id=1, source_target_pairs={{4,0},{8,4},{12,8},{5,1},{9,5},{13,9},{6,2},{10,6},{14,10},{7,3},{... | collective-permute-start | bytes 147464 | tf_op jit(solution)/shard_map/ppermute | solution.py:28
  9.5 5.1 %collective-permute-start.1 = (f32[6,1,16,128]{3,2,1,0:T(8,128)S(1)}, f32[6,1,16,128]{3,2,1,0:T(8,128)S(1)}, u32[]{:S(2)}, u32[]{:S(2)}) collective-permute-start(f32[6,1,16,128]{3,2,1,0:T(8,128)S(1)} %get-tuple-element.49), channel_id=1, source_target_pairs={{0,4},{4,8},{8,12},{1,5},{5,9},{9,13},{2,6},{6,10},{10,14},{3,7},{... | collective-permute-start | bytes 147464 | tf_op jit(solution)/shard_map/ppermute | solution.py:27
  14.7 0.9 convert_element_type.15
  15.8 0.9 reshape.104
  16.9 0.9 reshape.105
  17.8 1.0 convert_element_type.13
  18.9 1.9 %collective-permute-start.4 = (f32[12]{0:T(128)S(1)}, f32[12]{0:T(128)S(1)}, u32[]{:S(2)}, u32[]{:S(2)}) collective-permute-start(f32[12]{0:T(128)S(1)} %fusion.116), channel_id=1, source_target_pairs={{0,2},{1,3},{2,0},{3,1},{4,6},{5,7},{6,4},{7,5},{8,10},{9,11},{10,... | collective-permute-start | bytes 152 | tf_op jit(solution)/shard_map/ppermute | solution.py:136
  20.8 1.6 %collective-permute-done.4 = f32[12]{0:T(128)S(1)} collective-permute-done((f32[12]{0:T(128)S(1)}, f32[12]{0:T(128)S(1)}, u32[]{:S(2)}, u32[]{:S(2)}) %collective-permute-start.4) | collective-permute-done | bytes 80 | tf_op jit(solution)/shard_map/ppermute | solution.py:136
  22.4 2.0 %collective-permute-start.5 = (f32[12]{0:T(128)S(1)}, f32[12]{0:T(128)S(1)}, u32[]{:S(2)}, u32[]{:S(2)}) collective-permute-start(f32[12]{0:T(128)S(1)} %add.479), channel_id=1, source_target_pairs={{0,4},{1,5},{2,6},{3,7},{4,0},{5,1},{6,2},{7,3},{8,12},{9,13},{10,... | collective-permute-start | bytes 152 | tf_op jit(solution)/shard_map/ppermute | solution.py:136
  24.5 1.5 %collective-permute-done.5 = f32[12]{0:T(128)S(1)} collective-permute-done((f32[12]{0:T(128)S(1)}, f32[12]{0:T(128)S(1)}, u32[]{:S(2)}, u32[]{:S(2)}) %collective-permute-start.5) | collective-permute-done | bytes 80 | tf_op jit(solution)/shard_map/ppermute | solution.py:136
  26.0 3.0 %collective-permute-start.6 = (f32[12]{0:T(128)S(1)}, f32[12]{0:T(128)S(1)}, u32[]{:S(2)}, u32[]{:S(2)}) collective-permute-start(f32[12]{0:T(128)S(1)} %add.480), channel_id=1, source_target_pairs={{0,8},{1,9},{2,10},{3,11},{4,12},{5,13},{6,14},{7,15},{8,0},{9,1},... | collective-permute-start | bytes 152 | tf_op jit(solution)/shard_map/ppermute | solution.py:136
  29.0 1.5 %collective-permute-done.6 = f32[12]{0:T(128)S(1)} collective-permute-done((f32[12]{0:T(128)S(1)}, f32[12]{0:T(128)S(1)}, u32[]{:S(2)}, u32[]{:S(2)}) %collective-permute-start.6) | collective-permute-done | bytes 80 | tf_op jit(solution)/shard_map/ppermute | solution.py:136
  31.2 1.9 %collective-permute-start.2 = (f32[6,18,1,128]{3,2,1,0:T(1,128)S(1)}, f32[6,18,1,128]{3,2,1,0:T(1,128)S(1)}, u32[]{:S(2)}, u32[]{:S(2)}) collective-permute-start(f32[6,18,1,128]{3,2,1,0:T(1,128)S(1)} %broadcast_select_fusion.7), channel_id=1, source_target_pairs={{0,2},{2,0},{1,3},{3,1},{4,6},{6,4},{5,7},{7,5},{8,10},{10,8},{9,1... | collective-permute-start | bytes 165896 | tf_op jit(solution)/shard_map/ppermute | solution.py:20
  34.4 1.1 collective-permute-done.2
  35.7 1.5 %fusion.112 = (f32[6,18,18,1]{3,2,1,0:T(8,128)S(1)}, f32[6,18,18,1]{3,2,1,0:T(8,128)}) fusion(f32[6,18,18,128]{3,2,1,0:T(8,128)S(1)} %pad_maximum_fusion.3), kind=kLoop, calls=%fused_computation.272 | loop fusion | bytes 31104 | tf_op jit(solution)/shard_map/slice | solution.py:13
  37.3 2.0 %copy.176 = f32[6,18,18,1]{2,3,1,0:T(1,128)S(1)} copy(f32[6,18,18,1]{3,2,1,0:T(8,128)} %get-tuple-element.38) | data formatting | bytes 15552
  40.2 1.7 %pad_maximum_fusion.2 = (f32[6,18,17,128]{3,2,1,0:T(8,128)}, f32[6,18,17,128]{3,2,1,0:T(8,128)}) fusion(f32[6,18,1,128]{3,2,1,0:T(1,128)S(1)} %get-tuple-element.61, f32[6,1,16,128]{3,2,1,0:T(8,128)S(1)} %collective-permute-done, f32[6,16,16,128]{3,2,1,0:T(8,128)S(1)} %convert_element_type.12, f32[6,1,16,128]{3,2,1,0:T(8,128)S(1)} %collective-permute-done.1, ...), kind=kLoop, calls=%fused_computation.5 | loop fusion | flops 1410048 | bytes 2875392 | tf_op jit(solution)/shard_map/concatenate | solution.py:29
  42.6 0.8 copy.160
  43.3 1.7 %copy.157 = f32[6,18,18,1]{3,2,1,0:T(8,128)S(1)} copy(f32[6,18,18,1]{2,1,3,0:T(8,128)} %get-tuple-element.53) | data formatting | bytes 15552 | tf_op jit(solution)/shard_map/jit(_where)/select_n | solution.py:23
  45.0 3.1 %pad_maximum_fusion = (f32[6,18,18,129]{3,2,1,0:T(8,128)S(1)}, f32[6,18,18,129]{3,2,1,0:T(8,128)S(1)}) fusion(f32[6,18,18,1]{3,2,1,0:T(8,128)S(1)} %copy.157, f32[6,18,1,128]{3,2,1,0:T(1,128)} %copy-done.11, f32[6,1,16,128]{3,2,1,0:T(8,128)S(1)} %collective-permute-done, f32[6,16,16,128]{3,2,1,0:T(8,128)S(1)} %convert_element_type.12, ...), kind=kLoop, calls=%fused_computation.1 | loop fusion | flops 2507760 | bytes 3017088 | tf_op jit(solution)/shard_map/concatenate | solution.py:29
  54.8 1.3 %collective-permute-start.8 = (f32[6,1,16,128]{3,2,1,0:T(8,128)S(1)}, f32[6,1,16,128]{3,2,1,0:T(8,128)S(1)}, u32[]{:S(2)}, u32[]{:S(2)}) collective-permute-start(f32[6,1,16,128]{3,2,1,0:T(8,128)S(1)} %get-tuple-element.48), channel_id=1, source_target_pairs={{4,0},{8,4},{12,8},{5,1},{9,5},{13,9},{6,2},{10,6},{14,10},{7,3},{... | collective-permute-start | bytes 147464 | tf_op jit(solution)/shard_map/ppermute | solution.py:28
  56.1 4.7 %collective-permute-start.9 = (f32[6,1,16,128]{3,2,1,0:T(8,128)S(1)}, f32[6,1,16,128]{3,2,1,0:T(8,128)S(1)}, u32[]{:S(2)}, u32[]{:S(2)}) collective-permute-start(f32[6,1,16,128]{3,2,1,0:T(8,128)S(1)} %get-tuple-element.47), channel_id=1, source_target_pairs={{0,4},{4,8},{8,12},{1,5},{5,9},{9,13},{2,6},{6,10},{10,14},{3,7},{... | collective-permute-start | bytes 147464 | tf_op jit(solution)/shard_map/ppermute | solution.py:27
  60.9 1.9 %collective-permute-start.13 = (f32[6]{0:T(128)S(1)}, f32[6]{0:T(128)S(1)}, u32[]{:S(2)}, u32[]{:S(2)}) collective-permute-start(f32[6]{0:T(128)S(1)} %add.569), channel_id=1, source_target_pairs={{0,2},{1,3},{2,0},{3,1},{4,6},{5,7},{6,4},{7,5},{8,10},{9,11},{10,... | collective-permute-start | bytes 80 | tf_op jit(solution)/shard_map/ppermute | solution.py:136
  62.8 1.7 %collective-permute-done.13 = f32[6]{0:T(128)S(1)} collective-permute-done((f32[6]{0:T(128)S(1)}, f32[6]{0:T(128)S(1)}, u32[]{:S(2)}, u32[]{:S(2)}) %collective-permute-start.13) | collective-permute-done | bytes 56 | tf_op jit(solution)/shard_map/ppermute | solution.py:136
  64.5 1.9 %collective-permute-start.14 = (f32[6]{0:T(128)S(1)}, f32[6]{0:T(128)S(1)}, u32[]{:S(2)}, u32[]{:S(2)}) collective-permute-start(f32[6]{0:T(128)S(1)} %add.570), channel_id=1, source_target_pairs={{0,4},{1,5},{2,6},{3,7},{4,0},{5,1},{6,2},{7,3},{8,12},{9,13},{10,... | collective-permute-start | bytes 80 | tf_op jit(solution)/shard_map/ppermute | solution.py:136
  66.4 1.6 %collective-permute-done.14 = f32[6]{0:T(128)S(1)} collective-permute-done((f32[6]{0:T(128)S(1)}, f32[6]{0:T(128)S(1)}, u32[]{:S(2)}, u32[]{:S(2)}) %collective-permute-start.14) | collective-permute-done | bytes 56 | tf_op jit(solution)/shard_map/ppermute | solution.py:136
  68.0 2.9 %collective-permute-start.15 = (f32[6]{0:T(128)S(1)}, f32[6]{0:T(128)S(1)}, u32[]{:S(2)}, u32[]{:S(2)}) collective-permute-start(f32[6]{0:T(128)S(1)} %add.571), channel_id=1, source_target_pairs={{0,8},{1,9},{2,10},{3,11},{4,12},{5,13},{6,14},{7,15},{8,0},{9,1},... | collective-permute-start | bytes 80 | tf_op jit(solution)/shard_map/ppermute | solution.py:136
  71.0 1.5 %collective-permute-done.15 = f32[6]{0:T(128)S(1)} collective-permute-done((f32[6]{0:T(128)S(1)}, f32[6]{0:T(128)S(1)}, u32[]{:S(2)}, u32[]{:S(2)}) %collective-permute-start.15) | collective-permute-done | bytes 56 | tf_op jit(solution)/shard_map/ppermute | solution.py:136
  72.7 1.9 %collective-permute-start.10 = (f32[6,18,1,128]{3,2,1,0:T(1,128)S(1)}, f32[6,18,1,128]{3,2,1,0:T(1,128)S(1)}, u32[]{:S(2)}, u32[]{:S(2)}) collective-permute-start(f32[6,18,1,128]{3,2,1,0:T(1,128)S(1)} %broadcast_select_fusion.4), channel_id=1, source_target_pairs={{0,2},{2,0},{1,3},{3,1},{4,6},{6,4},{5,7},{7,5},{8,10},{10,8},{9,1... | collective-permute-start | bytes 165896 | tf_op jit(solution)/shard_map/ppermute | solution.py:20
  74.7 2.3 %collective-permute-done.10 = f32[6,18,1,128]{3,2,1,0:T(1,128)S(1)} collective-permute-done((f32[6,18,1,128]{3,2,1,0:T(1,128)S(1)}, f32[6,18,1,128]{3,2,1,0:T(1,128)S(1)}, u32[]{:S(2)}, u32[]{:S(2)}) %collective-permute-start.10) | collective-permute-done | bytes 55328 | tf_op jit(solution)/shard_map/ppermute | solution.py:20
  77.2 1.5 %fusion.111 = (f32[6,18,18,1]{3,2,1,0:T(8,128)S(1)}, f32[6,18,18,1]{3,2,1,0:T(8,128)}) fusion(f32[6,18,18,128]{3,2,1,0:T(8,128)S(1)} %pad_maximum_fusion.5), kind=kLoop, calls=%fused_computation.271 | loop fusion | bytes 31104 | tf_op jit(solution)/shard_map/slice | solution.py:14
  78.8 2.0 %copy.177 = f32[6,18,18,1]{2,3,1,0:T(1,128)S(1)} copy(f32[6,18,18,1]{3,2,1,0:T(8,128)} %get-tuple-element.36) | data formatting | bytes 15552
  81.7 1.7 %pad_maximum_fusion.4 = (f32[6,18,17,128]{3,2,1,0:T(8,128)}, f32[6,18,17,128]{3,2,1,0:T(8,128)}) fusion(f32[6,18,1,128]{3,2,1,0:T(1,128)S(1)} %get-tuple-element.59, f32[6,1,16,128]{3,2,1,0:T(8,128)S(1)} %collective-permute-done.8, f32[3,16,16,128]{3,2,1,0:T(8,128)S(1)} %get-tuple-element.27, f32[3,16,16,128]{3,2,1,0:T(8,128)S(1)} %get-tuple-element.23, ...), kind=kLoop, calls=%fused_computation.8 | loop fusion | flops 1880064 | bytes 2875392 | tf_op jit(solution)/shard_map/concatenate | solution.py:29
  84.1 0.8 copy.169
  84.8 1.7 %copy.166 = f32[6,18,18,1]{3,2,1,0:T(8,128)S(1)} copy(f32[6,18,18,1]{2,1,3,0:T(8,128)} %get-tuple-element.51) | data formatting | bytes 15552 | tf_op jit(solution)/shard_map/jit(_where)/select_n | solution.py:23
  86.5 3.6 %pad_maximum_fusion.1 = (f32[6,18,18,129]{3,2,1,0:T(8,128)S(1)}, f32[6,18,18,129]{3,2,1,0:T(8,128)S(1)}) fusion(f32[6,18,18,1]{3,2,1,0:T(8,128)S(1)} %copy.166, f32[6,18,1,128]{3,2,1,0:T(1,128)} %copy-done.15, f32[6,1,16,128]{3,2,1,0:T(8,128)S(1)} %collective-permute-done.8, f32[3,16,16,128]{3,2,1,0:T(8,128)S(1)} %get-tuple-element.27, ...), kind=kLoop, calls=%fused_computation.3 | loop fusion | flops 3009312 | bytes 3017088 | tf_op jit(solution)/shard_map/concatenate | solution.py:29
  95.2 0.9 subtract_reduce_fusion
  97.7 0.8 collective-permute-done.16
  98.8 2.2 %collective-permute-start.17 = (f32[16,8]{1,0:T(8,128)S(1)}, f32[16,8]{1,0:T(8,128)S(1)}, u32[]{:S(2)}, u32[]{:S(2)}) collective-permute-start(f32[16,8]{1,0:T(8,128)S(1)} %add.583), channel_id=1, source_target_pairs={{0,2},{1,3},{2,0},{3,1},{4,6},{5,7},{6,4},{7,5},{8,10},{9,11},{10,... | collective-permute-start | bytes 1544 | tf_op jit(solution)/shard_map/ppermute | solution.py:136
  101.1 1.6 %collective-permute-done.17 = f32[16,8]{1,0:T(8,128)S(1)} collective-permute-done((f32[16,8]{1,0:T(8,128)S(1)}, f32[16,8]{1,0:T(8,128)S(1)}, u32[]{:S(2)}, u32[]{:S(2)}) %collective-permute-start.17) | collective-permute-done | bytes 544 | tf_op jit(solution)/shard_map/ppermute | solution.py:136
  102.7 1.8 %collective-permute-start.18 = (f32[16,8]{1,0:T(8,128)S(1)}, f32[16,8]{1,0:T(8,128)S(1)}, u32[]{:S(2)}, u32[]{:S(2)}) collective-permute-start(f32[16,8]{1,0:T(8,128)S(1)} %add.584), channel_id=1, source_target_pairs={{0,4},{1,5},{2,6},{3,7},{4,0},{5,1},{6,2},{7,3},{8,12},{9,13},{10,... | collective-permute-start | bytes 1544 | tf_op jit(solution)/shard_map/ppermute | solution.py:136
  104.5 1.9 %collective-permute-done.18 = f32[16,8]{1,0:T(8,128)S(1)} collective-permute-done((f32[16,8]{1,0:T(8,128)S(1)}, f32[16,8]{1,0:T(8,128)S(1)}, u32[]{:S(2)}, u32[]{:S(2)}) %collective-permute-start.18) | collective-permute-done | bytes 544 | tf_op jit(solution)/shard_map/ppermute | solution.py:136
  106.4 2.7 %collective-permute-start.19 = (f32[16,8]{1,0:T(8,128)S(1)}, f32[16,8]{1,0:T(8,128)S(1)}, u32[]{:S(2)}, u32[]{:S(2)}) collective-permute-start(f32[16,8]{1,0:T(8,128)S(1)} %add.585), channel_id=1, source_target_pairs={{0,8},{1,9},{2,10},{3,11},{4,12},{5,13},{6,14},{7,15},{8,0},{9,1},... | collective-permute-start | bytes 1544 | tf_op jit(solution)/shard_map/ppermute | solution.py:136
  109.1 0.9 pad_maximum_fusion.13
  110.0 0.9 collective-permute-done.19
  (168 shorter events, 23.4 us)
Async XLA Ops:
  0.6 5.6 %copy-start.17 = (bf16[6,16,16,128]{3,2,1,0:T(8,128)(2,1)S(1)}, bf16[6,16,16,128]{3,2,1,0:T(8,128)(2,1)}, u32[]{:S(2)}) copy-start(bf16[6,16,16,128]{3,2,1,0:T(8,128)(2,1)} %param.10) | copy-start | bytes 1179652
  0.6 5.8 %copy-start.38 = (bf16[16,16,128]{2,1,0:T(8,128)(2,1)S(1)}, bf16[16,16,128]{2,1,0:T(8,128)(2,1)}, u32[]{:S(2)}) copy-start(bf16[16,16,128]{2,1,0:T(8,128)(2,1)} %param.12) | copy-start | bytes 196612
  6.3 3.2 %copy-start.4 = (f32[32768]{0:T(1024)}, f32[32768]{0:T(1024)S(1)}, u32[]{:S(2)}) copy-start(f32[32768]{0:T(1024)S(1)} %scatter_custom_fusion) | copy-start | bytes 393220
  6.5 8.2 %copy-start.36 = (bf16[6,16,16,128]{3,2,1,0:T(8,128)(2,1)S(1)}, bf16[6,16,16,128]{3,2,1,0:T(8,128)(2,1)}, u32[]{:S(2)}) copy-start(bf16[6,16,16,128]{3,2,1,0:T(8,128)(2,1)} %param.11) | copy-start | bytes 1179652
  7.2 2.3 %copy-start.23 = (f32[16,16,128]{2,1,0:T(8,128)}, f32[16,16,128]{2,1,0:T(8,128)S(1)}, u32[]{:S(2)}) copy-start(f32[16,16,128]{2,1,0:T(8,128)S(1)} %get-tuple-element.56) | copy-start | bytes 393220
  7.2 2.3 %copy-start.26 = (f32[16,16,128]{2,1,0:T(8,128)}, f32[16,16,128]{2,1,0:T(8,128)S(1)}, u32[]{:S(2)}) copy-start(f32[16,16,128]{2,1,0:T(8,128)S(1)} %get-tuple-element.57) | copy-start | bytes 393220
  7.2 2.3 %copy-start.29 = (f32[16,16,128]{2,1,0:T(8,128)}, f32[16,16,128]{2,1,0:T(8,128)S(1)}, u32[]{:S(2)}) copy-start(f32[16,16,128]{2,1,0:T(8,128)S(1)} %get-tuple-element.74) | copy-start | bytes 393220
  7.7 11.1 %collective-permute-start.3 = (f32[12]{0:T(128)S(1)}, f32[12]{0:T(128)S(1)}, u32[]{:S(2)}, u32[]{:S(2)}) collective-permute-start(f32[12]{0:T(128)S(1)} %pad_maximum_fusion.19), channel_id=1, source_target_pairs={{0,1},{1,0},{2,3},{3,2},{4,5},{5,4},{6,7},{7,6},{8,9},{9,8},{10,11... | collective-permute-start | bytes 152 | tf_op jit(solution)/shard_map/ppermute | solution.py:136
  8.2 23.0 %collective-permute-start = (f32[6,1,16,128]{3,2,1,0:T(8,128)S(1)}, f32[6,1,16,128]{3,2,1,0:T(8,128)S(1)}, u32[]{:S(2)}, u32[]{:S(2)}) collective-permute-start(f32[6,1,16,128]{3,2,1,0:T(8,128)S(1)} %get-tuple-element.50), channel_id=1, source_target_pairs={{4,0},{8,4},{12,8},{5,1},{9,5},{13,9},{6,2},{10,6},{14,10},{7,3},{... | collective-permute-start | bytes 147464 | tf_op jit(solution)/shard_map/ppermute | solution.py:28
  9.5 21.6 %collective-permute-start.1 = (f32[6,1,16,128]{3,2,1,0:T(8,128)S(1)}, f32[6,1,16,128]{3,2,1,0:T(8,128)S(1)}, u32[]{:S(2)}, u32[]{:S(2)}) collective-permute-start(f32[6,1,16,128]{3,2,1,0:T(8,128)S(1)} %get-tuple-element.49), channel_id=1, source_target_pairs={{0,4},{4,8},{8,12},{1,5},{5,9},{9,13},{2,6},{6,10},{10,14},{3,7},{... | collective-permute-start | bytes 147464 | tf_op jit(solution)/shard_map/ppermute | solution.py:27
  15.7 2.2 %copy-start.37 = (bf16[6,16,16,128]{3,2,1,0:T(8,128)(2,1)S(1)}, bf16[6,16,16,128]{3,2,1,0:T(8,128)(2,1)}, u32[]{:S(2)}) copy-start(bf16[6,16,16,128]{3,2,1,0:T(8,128)(2,1)} %param.9) | copy-start | bytes 1179652
  18.9 3.5 %collective-permute-start.4 = (f32[12]{0:T(128)S(1)}, f32[12]{0:T(128)S(1)}, u32[]{:S(2)}, u32[]{:S(2)}) collective-permute-start(f32[12]{0:T(128)S(1)} %fusion.116), channel_id=1, source_target_pairs={{0,2},{1,3},{2,0},{3,1},{4,6},{5,7},{6,4},{7,5},{8,10},{9,11},{10,... | collective-permute-start | bytes 152 | tf_op jit(solution)/shard_map/ppermute | solution.py:136
  22.4 3.5 %collective-permute-start.5 = (f32[12]{0:T(128)S(1)}, f32[12]{0:T(128)S(1)}, u32[]{:S(2)}, u32[]{:S(2)}) collective-permute-start(f32[12]{0:T(128)S(1)} %add.479), channel_id=1, source_target_pairs={{0,4},{1,5},{2,6},{3,7},{4,0},{5,1},{6,2},{7,3},{8,12},{9,13},{10,... | collective-permute-start | bytes 152 | tf_op jit(solution)/shard_map/ppermute | solution.py:136
  26.0 4.5 %collective-permute-start.6 = (f32[12]{0:T(128)S(1)}, f32[12]{0:T(128)S(1)}, u32[]{:S(2)}, u32[]{:S(2)}) collective-permute-start(f32[12]{0:T(128)S(1)} %add.480), channel_id=1, source_target_pairs={{0,8},{1,9},{2,10},{3,11},{4,12},{5,13},{6,14},{7,15},{8,0},{9,1},... | collective-permute-start | bytes 152 | tf_op jit(solution)/shard_map/ppermute | solution.py:136
  31.2 4.2 %collective-permute-start.2 = (f32[6,18,1,128]{3,2,1,0:T(1,128)S(1)}, f32[6,18,1,128]{3,2,1,0:T(1,128)S(1)}, u32[]{:S(2)}, u32[]{:S(2)}) collective-permute-start(f32[6,18,1,128]{3,2,1,0:T(1,128)S(1)} %broadcast_select_fusion.7), channel_id=1, source_target_pairs={{0,2},{2,0},{1,3},{3,1},{4,6},{6,4},{5,7},{7,5},{8,10},{10,8},{9,1... | collective-permute-start | bytes 165896 | tf_op jit(solution)/shard_map/ppermute | solution.py:20
  35.5 4.7 %copy-start.9 = (f32[6,18,1,128]{3,2,1,0:T(1,128)}, f32[6,18,1,128]{3,2,1,0:T(1,128)S(1)}, u32[]{:S(2)}) copy-start(f32[6,18,1,128]{3,2,1,0:T(1,128)S(1)} %get-tuple-element.60) | copy-start | bytes 165892
  35.5 4.7 %copy-start.11 = (f32[6,18,1,128]{3,2,1,0:T(1,128)}, f32[6,18,1,128]{3,2,1,0:T(1,128)S(1)}, u32[]{:S(2)}) copy-start(f32[6,18,1,128]{3,2,1,0:T(1,128)S(1)} %get-tuple-element.61) | copy-start | bytes 165892
  40.1 1.8 %collective-permute-start.7 = (f32[6,18,18,1]{2,1,3,0:T(8,128)S(1)}, f32[6,18,18,1]{2,1,3,0:T(8,128)S(1)}, u32[]{:S(2)}, u32[]{:S(2)}) collective-permute-start(f32[6,18,18,1]{2,1,3,0:T(8,128)S(1)} %copy.154), channel_id=1, source_target_pairs={{0,1},{1,0},{2,3},{3,2},{4,5},{5,4},{6,7},{7,6},{8,9},{9,8},{10,11... | collective-permute-start | bytes 23336 | tf_op jit(solution)/shard_map/ppermute | solution.py:20
  45.0 3.1 %copy-start.18 = (bf16[6,16,16,128]{3,2,1,0:T(8,128)(2,1)S(1)}, bf16[6,16,16,128]{3,2,1,0:T(8,128)(2,1)}, u32[]{:S(2)}) copy-start(bf16[6,16,16,128]{3,2,1,0:T(8,128)(2,1)} %param.10) | copy-start | bytes 1179652
  45.0 3.1 %copy-start.21 = (f32[6,18,17,128]{3,2,1,0:T(8,128)S(1)}, f32[6,18,17,128]{3,2,1,0:T(8,128)}, u32[]{:S(2)}) copy-start(f32[6,18,17,128]{3,2,1,0:T(8,128)} %get-tuple-element.45) | copy-start | bytes 2820100
  45.0 3.1 %copy-start.22 = (f32[6,18,17,128]{3,2,1,0:T(8,128)S(1)}, f32[6,18,17,128]{3,2,1,0:T(8,128)}, u32[]{:S(2)}) copy-start(f32[6,18,17,128]{3,2,1,0:T(8,128)} %get-tuple-element.46) | copy-start | bytes 2820100
  49.5 2.1 %copy-start.2 = (f32[1,16,16,128]{3,2,1,0:T(8,128)}, f32[1,16,16,128]{3,2,1,0:T(8,128)S(1)}, u32[]{:S(2)}) copy-start(f32[1,16,16,128]{3,2,1,0:T(8,128)S(1)} %get-tuple-element.30) | copy-start | bytes 393220
  51.7 1.2 %copy-start.27 = (f32[16,16,128]{2,1,0:T(8,128)S(1)}, f32[16,16,128]{2,1,0:T(8,128)}, u32[]{:S(2)}) copy-start(f32[16,16,128]{2,1,0:T(8,128)} %copy-done.26) | copy-start | bytes 393220
  51.7 1.3 %copy-start.30 = (f32[16,16,128]{2,1,0:T(8,128)S(1)}, f32[16,16,128]{2,1,0:T(8,128)}, u32[]{:S(2)}) copy-start(f32[16,16,128]{2,1,0:T(8,128)} %copy-done.29) | copy-start | bytes 393220
  51.7 1.3 %copy-start.33 = (f32[16,16,128]{2,1,0:T(8,128)S(1)}, f32[16,16,128]{2,1,0:T(8,128)}, u32[]{:S(2)}) copy-start(f32[16,16,128]{2,1,0:T(8,128)} %get-tuple-element.55) | copy-start | bytes 393220
  51.7 1.3 %copy-start.39 = (f32[3]{0:T(128)S(1)}, f32[3]{0:T(128)}, u32[]{:S(2)}) copy-start(f32[3]{0:T(128)} %get-tuple-element.73) | copy-start | bytes 40
  54.1 18.4 %copy-start.41 = (f32[12]{0:T(128)S(1)}, f32[12]{0:T(128)}, u32[]{:S(2)}) copy-start(f32[12]{0:T(128)} %copy-done.40) | copy-start | bytes 148
  54.3 6.6 %collective-permute-start.12 = (f32[6]{0:T(128)S(1)}, f32[6]{0:T(128)S(1)}, u32[]{:S(2)}, u32[]{:S(2)}) collective-permute-start(f32[6]{0:T(128)S(1)} %fusion.9), channel_id=1, source_target_pairs={{0,1},{1,0},{2,3},{3,2},{4,5},{5,4},{6,7},{7,6},{8,9},{9,8},{10,11... | collective-permute-start | bytes 80 | tf_op jit(solution)/shard_map/ppermute | solution.py:136
  54.8 17.8 %collective-permute-start.8 = (f32[6,1,16,128]{3,2,1,0:T(8,128)S(1)}, f32[6,1,16,128]{3,2,1,0:T(8,128)S(1)}, u32[]{:S(2)}, u32[]{:S(2)}) collective-permute-start(f32[6,1,16,128]{3,2,1,0:T(8,128)S(1)} %get-tuple-element.48), channel_id=1, source_target_pairs={{4,0},{8,4},{12,8},{5,1},{9,5},{13,9},{6,2},{10,6},{14,10},{7,3},{... | collective-permute-start | bytes 147464 | tf_op jit(solution)/shard_map/ppermute | solution.py:28
  56.1 16.5 %collective-permute-start.9 = (f32[6,1,16,128]{3,2,1,0:T(8,128)S(1)}, f32[6,1,16,128]{3,2,1,0:T(8,128)S(1)}, u32[]{:S(2)}, u32[]{:S(2)}) collective-permute-start(f32[6,1,16,128]{3,2,1,0:T(8,128)S(1)} %get-tuple-element.47), channel_id=1, source_target_pairs={{0,4},{4,8},{8,12},{1,5},{5,9},{9,13},{2,6},{6,10},{10,14},{3,7},{... | collective-permute-start | bytes 147464 | tf_op jit(solution)/shard_map/ppermute | solution.py:27
  60.9 3.6 %collective-permute-start.13 = (f32[6]{0:T(128)S(1)}, f32[6]{0:T(128)S(1)}, u32[]{:S(2)}, u32[]{:S(2)}) collective-permute-start(f32[6]{0:T(128)S(1)} %add.569), channel_id=1, source_target_pairs={{0,2},{1,3},{2,0},{3,1},{4,6},{5,7},{6,4},{7,5},{8,10},{9,11},{10,... | collective-permute-start | bytes 80 | tf_op jit(solution)/shard_map/ppermute | solution.py:136
  64.5 3.5 %collective-permute-start.14 = (f32[6]{0:T(128)S(1)}, f32[6]{0:T(128)S(1)}, u32[]{:S(2)}, u32[]{:S(2)}) collective-permute-start(f32[6]{0:T(128)S(1)} %add.570), channel_id=1, source_target_pairs={{0,4},{1,5},{2,6},{3,7},{4,0},{5,1},{6,2},{7,3},{8,12},{9,13},{10,... | collective-permute-start | bytes 80 | tf_op jit(solution)/shard_map/ppermute | solution.py:136
  68.0 4.4 %collective-permute-start.15 = (f32[6]{0:T(128)S(1)}, f32[6]{0:T(128)S(1)}, u32[]{:S(2)}, u32[]{:S(2)}) collective-permute-start(f32[6]{0:T(128)S(1)} %add.571), channel_id=1, source_target_pairs={{0,8},{1,9},{2,10},{3,11},{4,12},{5,13},{6,14},{7,15},{8,0},{9,1},... | collective-permute-start | bytes 80 | tf_op jit(solution)/shard_map/ppermute | solution.py:136
  72.7 4.2 %collective-permute-start.10 = (f32[6,18,1,128]{3,2,1,0:T(1,128)S(1)}, f32[6,18,1,128]{3,2,1,0:T(1,128)S(1)}, u32[]{:S(2)}, u32[]{:S(2)}) collective-permute-start(f32[6,18,1,128]{3,2,1,0:T(1,128)S(1)} %broadcast_select_fusion.4), channel_id=1, source_target_pairs={{0,2},{2,0},{1,3},{3,1},{4,6},{6,4},{5,7},{7,5},{8,10},{10,8},{9,1... | collective-permute-start | bytes 165896 | tf_op jit(solution)/shard_map/ppermute | solution.py:20
  77.0 4.7 %copy-start.13 = (f32[6,18,1,128]{3,2,1,0:T(1,128)}, f32[6,18,1,128]{3,2,1,0:T(1,128)S(1)}, u32[]{:S(2)}) copy-start(f32[6,18,1,128]{3,2,1,0:T(1,128)S(1)} %get-tuple-element.58) | copy-start | bytes 165892
  77.0 4.7 %copy-start.15 = (f32[6,18,1,128]{3,2,1,0:T(1,128)}, f32[6,18,1,128]{3,2,1,0:T(1,128)S(1)}, u32[]{:S(2)}) copy-start(f32[6,18,1,128]{3,2,1,0:T(1,128)S(1)} %get-tuple-element.59) | copy-start | bytes 165892
  81.6 1.8 %collective-permute-start.11 = (f32[6,18,18,1]{2,1,3,0:T(8,128)S(1)}, f32[6,18,18,1]{2,1,3,0:T(8,128)S(1)}, u32[]{:S(2)}, u32[]{:S(2)}) collective-permute-start(f32[6,18,18,1]{2,1,3,0:T(8,128)S(1)} %copy.163), channel_id=1, source_target_pairs={{0,1},{1,0},{2,3},{3,2},{4,5},{5,4},{6,7},{7,6},{8,9},{9,8},{10,11... | collective-permute-start | bytes 23336 | tf_op jit(solution)/shard_map/ppermute | solution.py:20
  86.5 3.6 %copy-start.19 = (f32[6,18,17,128]{3,2,1,0:T(8,128)S(1)}, f32[6,18,17,128]{3,2,1,0:T(8,128)}, u32[]{:S(2)}) copy-start(f32[6,18,17,128]{3,2,1,0:T(8,128)} %get-tuple-element.43) | copy-start | bytes 2820100
  86.5 3.7 %copy-start.20 = (f32[6,18,17,128]{3,2,1,0:T(8,128)S(1)}, f32[6,18,17,128]{3,2,1,0:T(8,128)}, u32[]{:S(2)}) copy-start(f32[6,18,17,128]{3,2,1,0:T(8,128)} %get-tuple-element.44) | copy-start | bytes 2820100
  93.6 1.2 %copy-start.8 = (f32[6,16,16,128]{3,2,1,0:T(8,128)S(1)}, f32[6,16,16,128]{3,2,1,0:T(8,128)}, u32[]{:S(2)}) copy-start(f32[6,16,16,128]{3,2,1,0:T(8,128)} %convert_element_type.13) | copy-start | bytes 2359300
  93.6 1.2 %copy-start.28 = (f32[16,16,128]{2,1,0:T(8,128)S(1)}, f32[16,16,128]{2,1,0:T(8,128)}, u32[]{:S(2)}) copy-start(f32[16,16,128]{2,1,0:T(8,128)} %copy-done.26) | copy-start | bytes 393220
  93.6 1.3 %copy-start.31 = (f32[16,16,128]{2,1,0:T(8,128)S(1)}, f32[16,16,128]{2,1,0:T(8,128)}, u32[]{:S(2)}) copy-start(f32[16,16,128]{2,1,0:T(8,128)} %copy-done.29) | copy-start | bytes 393220
  93.7 1.5 %copy-start.32 = (f32[6,16,16,128]{3,2,1,0:T(8,128)S(1)}, f32[6,16,16,128]{3,2,1,0:T(8,128)}, u32[]{:S(2)}) copy-start(f32[6,16,16,128]{3,2,1,0:T(8,128)} %convert_element_type.15) | copy-start | bytes 2359300
  93.7 1.5 %copy-start.34 = (f32[16,16,128]{2,1,0:T(8,128)S(1)}, f32[16,16,128]{2,1,0:T(8,128)}, u32[]{:S(2)}) copy-start(f32[16,16,128]{2,1,0:T(8,128)} %get-tuple-element.55) | copy-start | bytes 393220
  97.1 1.4 %collective-permute-start.16 = (f32[16,8]{1,0:T(8,128)S(1)}, f32[16,8]{1,0:T(8,128)S(1)}, u32[]{:S(2)}, u32[]{:S(2)}) collective-permute-start(f32[16,8]{1,0:T(8,128)S(1)} %dynamic_update_slice.5), channel_id=1, source_target_pairs={{0,1},{1,0},{2,3},{3,2},{4,5},{5,4},{6,7},{7,6},{8,9},{9,8},{10,11... | collective-permute-start | bytes 1544 | tf_op jit(solution)/shard_map/ppermute | solution.py:136
  98.8 3.9 %collective-permute-start.17 = (f32[16,8]{1,0:T(8,128)S(1)}, f32[16,8]{1,0:T(8,128)S(1)}, u32[]{:S(2)}, u32[]{:S(2)}) collective-permute-start(f32[16,8]{1,0:T(8,128)S(1)} %add.583), channel_id=1, source_target_pairs={{0,2},{1,3},{2,0},{3,1},{4,6},{5,7},{6,4},{7,5},{8,10},{9,11},{10,... | collective-permute-start | bytes 1544 | tf_op jit(solution)/shard_map/ppermute | solution.py:136
  102.7 3.7 %collective-permute-start.18 = (f32[16,8]{1,0:T(8,128)S(1)}, f32[16,8]{1,0:T(8,128)S(1)}, u32[]{:S(2)}, u32[]{:S(2)}) collective-permute-start(f32[16,8]{1,0:T(8,128)S(1)} %add.584), channel_id=1, source_target_pairs={{0,4},{1,5},{2,6},{3,7},{4,0},{5,1},{6,2},{7,3},{8,12},{9,13},{10,... | collective-permute-start | bytes 1544 | tf_op jit(solution)/shard_map/ppermute | solution.py:136
  106.4 4.5 %collective-permute-start.19 = (f32[16,8]{1,0:T(8,128)S(1)}, f32[16,8]{1,0:T(8,128)S(1)}, u32[]{:S(2)}, u32[]{:S(2)}) collective-permute-start(f32[16,8]{1,0:T(8,128)S(1)} %add.585), channel_id=1, source_target_pairs={{0,8},{1,9},{2,10},{3,11},{4,12},{5,13},{6,14},{7,15},{8,0},{9,1},... | collective-permute-start | bytes 1544 | tf_op jit(solution)/shard_map/ppermute | solution.py:136
  (14 other events, 13.5 us)

commit v5 on v2

--- a/solution.py
+++ b/solution.py
@@ -175,6 +175,26 @@
     count = jnp.float32(group_size * iface_cells.shape[1])
     gain_real, gain_imag = mean_gain(lame_first, shear, density_cells, mask, omega_sq, impedance)
     axes = ("gx", "gy", "col")
+    coarse_x = tile_shape[0] // 4
+    coarse_y = tile_shape[1] // 4
+    grid_shape = (lax.axis_size("gx") * coarse_x, lax.axis_size("gy") * coarse_y)
+    grid_at = (lax.axis_index("gx") * coarse_x, lax.axis_index("gy") * coarse_y)
+
+    def block_sums(cells):
+        lead = cells.shape[:-3]
+        local = cells.reshape(lead + (coarse_x, 4, coarse_y, 4, tile_shape[2]))
+        local = local.sum(axis=(-4, -2, -1))
+        grid = jnp.zeros(lead + grid_shape, jnp.float32)
+        return lax.dynamic_update_slice(grid, local, (0,) * len(lead) + grid_at)
+
+    forward_cells = forward.astype(jnp.float32)
+    forward_real = forward_cells[:3]
+    forward_imag = forward_cells[3:]
+    plain_real = gain_real * forward_real - gain_imag * forward_imag
+    plain_imag = gain_real * forward_imag + gain_imag * forward_real
+    response_real = plain_real - DAMPING * plain_imag
+    response_imag = plain_imag + DAMPING * plain_real
+    response = block_sums(jnp.concatenate([response_real, response_imag]))
     field = warm.astype(jnp.float32)
     first = group_sum(
         jnp.concatenate(
@@ -182,6 +202,7 @@
                 jnp.sum(mask * field, axis=(1, 2, 3)),
                 jnp.sum(gain_real, axis=(1, 2, 3)),
                 jnp.sum(gain_imag, axis=(1, 2, 3)),
+                response.reshape(-1),
             ]
         ),
         axes,
@@ -189,35 +210,32 @@
     mean_field = first[:6] / count
     gain_total_real = first[6:9]
     gain_total_imag = first[9:12]
+    response = first[12:].reshape(response.shape)
     sweep_args = (lame_first, shear, density_cells, mask, source_cells, omega_sq, impedance)
     padded = with_halo(field, (("gx", 1), ("gy", 2), ("col", 3)), 1)
     field = sweep(padded, *sweep_args)
-    second = group_sum(jnp.sum(mask * field, axis=(1, 2, 3)), axes)
+    second_local = jnp.sum(mask * field, axis=(1, 2, 3))
     field = add_mean(field, gain_real, gain_imag, mean_field)
     padded = with_halo(field, (("gx", 1), ("gy", 2), ("col", 3)), 1)
     field = sweep(padded, *sweep_args)
+    correlation = (
+        field[:3] * forward_real
+        - field[3:] * forward_imag
+        - DAMPING * (field[:3] * forward_imag + field[3:] * forward_real)
+    )
+    cell_terms = -omega_sq * jnp.sum(correlation, axis=0)
+    last = group_sum(jnp.concatenate([second_local, block_sums(cell_terms).reshape(-1)]), axes)
+    second = last[:6]
     mean_real = mean_field[:3]
     mean_imag = mean_field[3:]
     total_real = second[:3] + (gain_total_real * mean_real - gain_total_imag * mean_imag)
     total_imag = second[3:] + (gain_total_real * mean_imag + gain_total_imag * mean_real)
-    field = add_mean(field, gain_real, gain_imag, jnp.concatenate([total_real, total_imag]) / count)
-    forward_cells = forward.astype(jnp.float32)
-    correlation = (
-        field[:3] * forward_cells[:3]
-        - field[3:] * forward_cells[3:]
-        - DAMPING * (field[:3] * forward_cells[3:] + field[3:] * forward_cells[:3])
-    )
-    cell_terms = -omega_sq * jnp.sum(correlation, axis=0)
-    coarse_x = tile_shape[0] // 4
-    coarse_y = tile_shape[1] // 4
-    local_sums = cell_terms.reshape(coarse_x, 4, coarse_y, 4, tile_shape[2]).sum(axis=(1, 3, 4))
-    grid = jnp.zeros(
-        (lax.axis_size("gx") * coarse_x, lax.axis_size("gy") * coarse_y), jnp.float32
-    )
-    grid = lax.dynamic_update_slice(
-        grid, local_sums, (lax.axis_index("gx") * coarse_x, lax.axis_index("gy") * coarse_y)
-    )
-    coarse = group_sum(grid, ("gx", "gy", "col")) / 64.0
+    late_mean = jnp.concatenate([total_real, total_imag]) / count
+    field = add_mean(field, gain_real, gain_imag, late_mean)
+    late_terms = jnp.sum(
+        late_mean[:3, None, None] * response[:3] - late_mean[3:, None, None] * response[3:], axis=0
+    )
+    coarse = (last[6:].reshape(grid_shape) - omega_sq * late_terms) / 64.0
     return (field, coarse)
 
 

time: 105 us -> 103 us (0.981)
  starting transfers between devices: 35.1 us -> 29 us
  local copies, waits for them, and re-layouts: 23.8 us -> 25.7 us
  waiting for transfers between devices: 16 us -> 17.2 us
    ppermute x18 -> x12, starting transfers between devices: 18.8 us -> 13.3 us  [group_sum(): lax.ppermute(value, axes, [(i, i ^ m * stride) for i in range(size)])]
    unnamed x82 -> x96, local copies, waits for them, and re-layouts: 9.46 us -> 10.4 us
    ppermute x18 -> x12, waiting for transfers between devices: 11.6 us -> 12.1 us  [group_sum(): lax.ppermute(value, axes, [(i, i ^ m * stride) for i in range(size)])]
  transfers between devices with their start and end apart: 26 -> 20, of which waited for: 11 -> 10; matrix products, arithmetic and copies ran while one was open for 13% -> 12% of each run, Pallas kernels for 0% -> 0%
where the time goes in v5:
time: 103 us; the launch traced here: 102 us
  starting transfers between devices  29 us (28%)
  other arithmetic  28.4 us (28%)
  local copies, waits for them, and re-layouts  25.7 us (25%)
  waiting for transfers between devices  17.2 us (17%)
  between operations  2.17 us (2%)
    ppermute x12, starting transfers between devices, group_sum(): lax.ppermute(value, axes, [(i, i ^ m * stride) for i in range(size)])  13.3 us
    ppermute x12, waiting for transfers between devices, group_sum(): lax.ppermute(value, axes, [(i, i ^ m * stride) for i in range(size)])  12.1 us
    concatenate x6, other arithmetic, with_halo(): array = jnp.concatenate([before, array, after], axis=dim)  10.5 us
    unnamed x96, local copies, waits for them, and re-layouts  10.4 us
    ppermute x2, starting transfers between devices, with_halo(): before = lax.ppermute(last, axis, up)  10.3 us
    add x12, other arithmetic, navier(): result.append(shear * laplace[channel] + (lame_first + shear) * divergence)  5.61 us
    ppermute x4, waiting for transfers between devices, with_halo(): got = lax.ppermute(jnp.where(first, last, initial), axis, [(0, 1), (1, 0)])  3.53 us
    select_n x2, local copies, waits for them, and re-layouts, with_halo(): before = jnp.where(first, zero, got)  3.31 us
  transfers between devices with their start and end apart: 20, of which 10 were waited for; matrix products, arithmetic and copies ran while one was open for 12% of the time, Pallas kernels for 0%

profile of v5, /device:TPU:0, one launch (start us, length us, event | category | flops | bytes accessed | tf_op | source)
XLA Modules:
  0.0 102.5 jit_solution(72587772332354197)
XLA Ops:
  0.7 0.8 fusion.112
  1.5 1.3 %collective-permute-start = (f32[6,1,16,128]{3,2,1,0:T(8,128)S(1)}, f32[6,1,16,128]{3,2,1,0:T(8,128)S(1)}, u32[]{:S(2)}, u32[]{:S(2)}) collective-permute-start(f32[6,1,16,128]{3,2,1,0:T(8,128)S(1)} %get-tuple-element.67), channel_id=1, source_target_pairs={{4,0},{8,4},{12,8},{5,1},{9,5},{13,9},{6,2},{10,6},{14,10},{7,3},{... | collective-permute-start | bytes 147464 | tf_op jit(solution)/shard_map/ppermute | solution.py:25
  2.8 5.6 %collective-permute-start.1 = (f32[6,1,16,128]{3,2,1,0:T(8,128)S(1)}, f32[6,1,16,128]{3,2,1,0:T(8,128)S(1)}, u32[]{:S(2)}, u32[]{:S(2)}) collective-permute-start(f32[6,1,16,128]{3,2,1,0:T(8,128)S(1)} %get-tuple-element.66), channel_id=1, source_target_pairs={{0,4},{4,8},{8,12},{1,5},{5,9},{9,13},{2,6},{6,10},{10,14},{3,7},{... | collective-permute-start | bytes 147464 | tf_op jit(solution)/shard_map/ppermute | solution.py:24
  8.3 0.8 slice_bitcast_fusion.2
  9.1 0.8 select_reduce_fusion.1
  11.1 0.8 convert_multiply_fusion
  11.8 1.5 %scatter_custom_fusion = f32[32768]{0:T(1024)S(1)} fusion(s32[256]{0:T(256)S(1)} %bitcast.21, f32[256]{0:T(256)S(1)} %broadcast.108, f32[]{:T(128)} %constant.18.clone.1), kind=kCustom, calls=%fused_computation.245 | custom fusion | bytes 131076 | tf_op jit(solution)/shard_map/scatter | solution.py:168
  14.8 2.0 %collective-permute-start.2 = (f32[6,18,1,128]{3,2,1,0:T(1,128)S(1)}, f32[6,18,1,128]{3,2,1,0:T(1,128)S(1)}, u32[]{:S(2)}, u32[]{:S(2)}) collective-permute-start(f32[6,18,1,128]{3,2,1,0:T(1,128)S(1)} %broadcast_select_fusion.7), channel_id=1, source_target_pairs={{0,2},{2,0},{1,3},{3,1},{4,6},{6,4},{5,7},{7,5},{8,10},{10,8},{9,1... | collective-permute-start | bytes 165896 | tf_op jit(solution)/shard_map/ppermute | solution.py:17
  17.0 0.9 reshape.124
  18.1 0.9 reshape.125
  19.0 1.0 convert_element_type.13
  20.0 0.9 convert_element_type.15
  21.2 1.5 %fusion.111 = (f32[6,18,18,1]{3,2,1,0:T(8,128)S(1)}, f32[6,18,18,1]{3,2,1,0:T(8,128)}) fusion(f32[6,18,18,128]{3,2,1,0:T(8,128)S(1)} %pad_maximum_fusion.3), kind=kLoop, calls=%fused_computation.283 | loop fusion | bytes 31104 | tf_op jit(solution)/shard_map/slice | solution.py:14
  22.7 2.0 %copy.179 = f32[6,18,18,1]{2,3,1,0:T(1,128)S(1)} copy(f32[6,18,18,1]{3,2,1,0:T(8,128)} %get-tuple-element.48) | data formatting | bytes 15552
  24.8 0.7 copy.180
  25.7 1.7 %pad_maximum_fusion.2 = (f32[6,18,17,128]{3,2,1,0:T(8,128)}, f32[6,18,17,128]{3,2,1,0:T(8,128)}) fusion(f32[6,18,1,128]{3,2,1,0:T(1,128)S(1)} %get-tuple-element.78, f32[6,1,16,128]{3,2,1,0:T(8,128)S(1)} %collective-permute-done, f32[6,16,16,128]{3,2,1,0:T(8,128)S(1)} %convert_element_type.12, f32[6,1,16,128]{3,2,1,0:T(8,128)S(1)} %collective-permute-done.1, ...), kind=kLoop, calls=%fused_computation.5 | loop fusion | flops 1410048 | bytes 2875392 | tf_op jit(solution)/shard_map/concatenate | solution.py:26
  28.1 0.8 copy.161
  28.8 1.7 %copy.164 = f32[6,18,18,1]{3,2,1,0:T(8,128)S(1)} copy(f32[6,18,18,1]{2,1,3,0:T(8,128)} %get-tuple-element.71) | data formatting | bytes 15552 | tf_op jit(solution)/shard_map/jit(_where)/select_n | solution.py:19
  30.5 3.1 %pad_maximum_fusion = (f32[6,18,18,129]{3,2,1,0:T(8,128)S(1)}, f32[6,18,18,129]{3,2,1,0:T(8,128)S(1)}) fusion(f32[6,18,18,1]{3,2,1,0:T(8,128)S(1)} %copy.161, f32[6,18,1,128]{3,2,1,0:T(1,128)} %copy-done.18, f32[6,1,16,128]{3,2,1,0:T(8,128)S(1)} %collective-permute-done, f32[6,16,16,128]{3,2,1,0:T(8,128)S(1)} %convert_element_type.12, ...), kind=kLoop, calls=%fused_computation.1 | loop fusion | flops 2507760 | bytes 3017088 | tf_op jit(solution)/shard_map/concatenate | solution.py:26
  41.5 0.8 fusion.9
  42.9 1.7 %collective-permute-start.5 = (f32[780]{0:T(1024)S(1)}, f32[780]{0:T(1024)S(1)}, u32[]{:S(2)}, u32[]{:S(2)}) collective-permute-start(f32[780]{0:T(1024)S(1)} %pad_maximum_fusion.19), channel_id=1, source_target_pairs={{0,2},{1,3},{2,0},{3,1},{4,6},{5,7},{6,4},{7,5},{8,10},{9,11},{10,... | collective-permute-start | bytes 9368 | tf_op jit(solution)/shard_map/ppermute | solution.py:135
  44.6 1.9 %collective-permute-done.5 = f32[780]{0:T(1024)S(1)} collective-permute-done((f32[780]{0:T(1024)S(1)}, f32[780]{0:T(1024)S(1)}, u32[]{:S(2)}, u32[]{:S(2)}) %collective-permute-start.5) | collective-permute-done | bytes 3152 | tf_op jit(solution)/shard_map/ppermute | solution.py:135
  46.5 1.2 %collective-permute-done.6 = f32[780]{0:T(1024)S(1)} collective-permute-done((f32[780]{0:T(1024)S(1)}, f32[780]{0:T(1024)S(1)}, u32[]{:S(2)}, u32[]{:S(2)}) %collective-permute-start.6) | collective-permute-done | bytes 3152 | tf_op jit(solution)/shard_map/ppermute | solution.py:135
  47.6 2.0 %collective-permute-start.7 = (f32[780]{0:T(1024)S(1)}, f32[780]{0:T(1024)S(1)}, u32[]{:S(2)}, u32[]{:S(2)}) collective-permute-start(f32[780]{0:T(1024)S(1)} %add_add_fusion.5), channel_id=1, source_target_pairs={{0,4},{1,5},{2,6},{3,7},{4,0},{5,1},{6,2},{7,3},{8,12},{9,13},{10,... | collective-permute-start | bytes 9368 | tf_op jit(solution)/shard_map/ppermute | solution.py:135
  49.7 1.0 collective-permute-start.8
  50.7 1.4 %collective-permute-start.9 = (f32[780]{0:T(1024)S(1)}, f32[780]{0:T(1024)S(1)}, u32[]{:S(2)}, u32[]{:S(2)}) collective-permute-start(f32[780]{0:T(1024)S(1)} %add_add_fusion.5), channel_id=1, source_target_pairs={{0,12},{1,13},{2,14},{3,15},{4,8},{5,9},{6,10},{7,11},{8,4},{9,5},... | collective-permute-start | bytes 9368 | tf_op jit(solution)/shard_map/ppermute | solution.py:135
  52.1 2.1 %collective-permute-done.8 = f32[780]{0:T(1024)S(1)} collective-permute-done((f32[780]{0:T(1024)S(1)}, f32[780]{0:T(1024)S(1)}, u32[]{:S(2)}, u32[]{:S(2)}) %collective-permute-start.8) | collective-permute-done | bytes 3152 | tf_op jit(solution)/shard_map/ppermute | solution.py:135
  54.2 1.9 %collective-permute-done.9 = f32[780]{0:T(1024)S(1)} collective-permute-done((f32[780]{0:T(1024)S(1)}, f32[780]{0:T(1024)S(1)}, u32[]{:S(2)}, u32[]{:S(2)}) %collective-permute-start.9) | collective-permute-done | bytes 3152 | tf_op jit(solution)/shard_map/ppermute | solution.py:135
  56.4 1.3 %collective-permute-start.10 = (f32[6,1,16,128]{3,2,1,0:T(8,128)S(1)}, f32[6,1,16,128]{3,2,1,0:T(8,128)S(1)}, u32[]{:S(2)}, u32[]{:S(2)}) collective-permute-start(f32[6,1,16,128]{3,2,1,0:T(8,128)S(1)} %get-tuple-element.62), channel_id=1, source_target_pairs={{4,0},{8,4},{12,8},{5,1},{9,5},{13,9},{6,2},{10,6},{14,10},{7,3},{... | collective-permute-start | bytes 147464 | tf_op jit(solution)/shard_map/ppermute | solution.py:25
  57.7 4.7 %collective-permute-start.11 = (f32[6,1,16,128]{3,2,1,0:T(8,128)S(1)}, f32[6,1,16,128]{3,2,1,0:T(8,128)S(1)}, u32[]{:S(2)}, u32[]{:S(2)}) collective-permute-start(f32[6,1,16,128]{3,2,1,0:T(8,128)S(1)} %get-tuple-element.61), channel_id=1, source_target_pairs={{0,4},{4,8},{8,12},{1,5},{5,9},{9,13},{2,6},{6,10},{10,14},{3,7},{... | collective-permute-start | bytes 147464 | tf_op jit(solution)/shard_map/ppermute | solution.py:24
  62.4 1.5 %collective-permute-done.11 = f32[6,1,16,128]{3,2,1,0:T(8,128)S(1)} collective-permute-done((f32[6,1,16,128]{3,2,1,0:T(8,128)S(1)}, f32[6,1,16,128]{3,2,1,0:T(8,128)S(1)}, u32[]{:S(2)}, u32[]{:S(2)}) %collective-permute-start.11) | collective-permute-done | bytes 49184 | tf_op jit(solution)/shard_map/ppermute | solution.py:24
  64.1 0.7 collective-permute-start.12
  64.7 3.5 %collective-permute-done.12 = f32[6,18,1,128]{3,2,1,0:T(1,128)S(1)} collective-permute-done((f32[6,18,1,128]{3,2,1,0:T(1,128)S(1)}, f32[6,18,1,128]{3,2,1,0:T(1,128)S(1)}, u32[]{:S(2)}, u32[]{:S(2)}) %collective-permute-start.12) | collective-permute-done | bytes 55328 | tf_op jit(solution)/shard_map/ppermute | solution.py:17
  68.6 1.5 %fusion.110 = (f32[6,18,18,1]{3,2,1,0:T(8,128)S(1)}, f32[6,18,18,1]{3,2,1,0:T(8,128)}) fusion(f32[6,18,18,128]{3,2,1,0:T(8,128)S(1)} %pad_maximum_fusion.5), kind=kLoop, calls=%fused_computation.282 | loop fusion | bytes 31104 | tf_op jit(solution)/shard_map/slice | solution.py:14
  70.1 2.0 %copy.181 = f32[6,18,18,1]{2,3,1,0:T(1,128)S(1)} copy(f32[6,18,18,1]{3,2,1,0:T(8,128)} %get-tuple-element.46) | data formatting | bytes 15552
  72.1 0.7 copy.182
  73.1 1.7 %pad_maximum_fusion.4 = (f32[6,18,17,128]{3,2,1,0:T(8,128)}, f32[6,18,17,128]{3,2,1,0:T(8,128)}) fusion(f32[6,18,1,128]{3,2,1,0:T(1,128)S(1)} %get-tuple-element.76, f32[6,1,16,128]{3,2,1,0:T(8,128)S(1)} %collective-permute-done.10, f32[3,16,16,128]{3,2,1,0:T(8,128)S(1)} %get-tuple-element.59, f32[3,16,16,128]{3,2,1,0:T(8,128)S(1)} %get-tuple-element.60, ...), kind=kLoop, calls=%fused_computation.8 | loop fusion | flops 1880064 | bytes 2875392 | tf_op jit(solution)/shard_map/concatenate | solution.py:26
  75.4 0.8 copy.170
  76.2 1.7 %copy.173 = f32[6,18,18,1]{3,2,1,0:T(8,128)S(1)} copy(f32[6,18,18,1]{2,1,3,0:T(8,128)} %get-tuple-element.69) | data formatting | bytes 15552 | tf_op jit(solution)/shard_map/jit(_where)/select_n | solution.py:19
  77.8 3.6 %pad_maximum_fusion.1 = (f32[6,18,18,129]{3,2,1,0:T(8,128)S(1)}, f32[6,18,18,129]{3,2,1,0:T(8,128)S(1)}) fusion(f32[6,18,18,1]{3,2,1,0:T(8,128)S(1)} %copy.170, f32[6,18,1,128]{3,2,1,0:T(1,128)} %copy-done.14, f32[6,1,16,128]{3,2,1,0:T(8,128)S(1)} %collective-permute-done.10, f32[3,16,16,128]{3,2,1,0:T(8,128)S(1)} %get-tuple-element.59, ...), kind=kLoop, calls=%fused_computation.3 | loop fusion | flops 3009312 | bytes 3017088 | tf_op jit(solution)/shard_map/concatenate | solution.py:26
  86.2 0.7 subtract_reduce_fusion
  88.6 0.8 collective-permute-start.15
  90.0 2.1 %collective-permute-done.15 = f32[134]{0:T(256)S(1)} collective-permute-done((f32[134]{0:T(256)S(1)}, f32[134]{0:T(256)S(1)}, u32[]{:S(2)}, u32[]{:S(2)}) %collective-permute-start.15) | collective-permute-done | bytes 568 | tf_op jit(solution)/shard_map/ppermute | solution.py:135
  92.4 2.3 %collective-permute-start.17 = (f32[134]{0:T(256)S(1)}, f32[134]{0:T(256)S(1)}, u32[]{:S(2)}, u32[]{:S(2)}) collective-permute-start(f32[134]{0:T(256)S(1)} %add_add_fusion.7), channel_id=1, source_target_pairs={{0,4},{1,5},{2,6},{3,7},{4,0},{5,1},{6,2},{7,3},{8,12},{9,13},{10,... | collective-permute-start | bytes 1616 | tf_op jit(solution)/shard_map/ppermute | solution.py:135
  94.8 2.4 %collective-permute-start.19 = (f32[134]{0:T(256)S(1)}, f32[134]{0:T(256)S(1)}, u32[]{:S(2)}, u32[]{:S(2)}) collective-permute-start(f32[134]{0:T(256)S(1)} %add_add_fusion.7), channel_id=1, source_target_pairs={{0,12},{1,13},{2,14},{3,15},{4,8},{5,9},{6,10},{7,11},{8,4},{9,5},... | collective-permute-start | bytes 1616 | tf_op jit(solution)/shard_map/ppermute | solution.py:135
  97.5 1.8 %collective-permute-done.18 = f32[134]{0:T(256)S(1)} collective-permute-done((f32[134]{0:T(256)S(1)}, f32[134]{0:T(256)S(1)}, u32[]{:S(2)}, u32[]{:S(2)}) %collective-permute-start.18) | collective-permute-done | bytes 568 | tf_op jit(solution)/shard_map/ppermute | solution.py:135
  99.2 0.9 collective-permute-done.19
  101.6 0.9 pad_maximum_fusion.13
  (183 shorter events, 21.7 us)
Async XLA Ops:
  0.6 14.0 %copy-start.24 = (bf16[6,16,16,128]{3,2,1,0:T(8,128)(2,1)S(1)}, bf16[6,16,16,128]{3,2,1,0:T(8,128)(2,1)}, u32[]{:S(2)}) copy-start(bf16[6,16,16,128]{3,2,1,0:T(8,128)(2,1)} %param.10) | copy-start | bytes 1179652
  0.6 10.4 %copy-start.43 = (s32[1,256]{1,0:T(1,128)S(1)}, s32[1,256]{1,0:T(1,128)}, u32[]{:S(2)}) copy-start(s32[1,256]{1,0:T(1,128)} %param.15) | copy-start | bytes 3076
  0.7 10.4 %copy-start.41 = (bf16[16,16,128]{2,1,0:T(8,128)(2,1)S(1)}, bf16[16,16,128]{2,1,0:T(8,128)(2,1)}, u32[]{:S(2)}) copy-start(bf16[16,16,128]{2,1,0:T(8,128)(2,1)} %param.12) | copy-start | bytes 196612
  1.5 13.2 %collective-permute-start = (f32[6,1,16,128]{3,2,1,0:T(8,128)S(1)}, f32[6,1,16,128]{3,2,1,0:T(8,128)S(1)}, u32[]{:S(2)}, u32[]{:S(2)}) collective-permute-start(f32[6,1,16,128]{3,2,1,0:T(8,128)S(1)} %get-tuple-element.67), channel_id=1, source_target_pairs={{4,0},{8,4},{12,8},{5,1},{9,5},{13,9},{6,2},{10,6},{14,10},{7,3},{... | collective-permute-start | bytes 147464 | tf_op jit(solution)/shard_map/ppermute | solution.py:25
  2.8 12.0 %collective-permute-start.1 = (f32[6,1,16,128]{3,2,1,0:T(8,128)S(1)}, f32[6,1,16,128]{3,2,1,0:T(8,128)S(1)}, u32[]{:S(2)}, u32[]{:S(2)}) collective-permute-start(f32[6,1,16,128]{3,2,1,0:T(8,128)S(1)} %get-tuple-element.66), channel_id=1, source_target_pairs={{0,4},{4,8},{8,12},{1,5},{5,9},{9,13},{2,6},{6,10},{10,14},{3,7},{... | collective-permute-start | bytes 147464 | tf_op jit(solution)/shard_map/ppermute | solution.py:24
  11.8 5.0 %copy-start.44 = (f32[2,3]{1,0:T(2,128)S(1)}, f32[2,3]{1,0:T(2,128)}, u32[]{:S(2)}) copy-start(f32[2,3]{1,0:T(2,128)} %param.16) | copy-start | bytes 76
  14.8 4.2 %copy-start.39 = (bf16[6,16,16,128]{3,2,1,0:T(8,128)(2,1)S(1)}, bf16[6,16,16,128]{3,2,1,0:T(8,128)(2,1)}, u32[]{:S(2)}) copy-start(bf16[6,16,16,128]{3,2,1,0:T(8,128)(2,1)} %param.9) | copy-start | bytes 1179652
  14.8 6.1 %collective-permute-start.2 = (f32[6,18,1,128]{3,2,1,0:T(1,128)S(1)}, f32[6,18,1,128]{3,2,1,0:T(1,128)S(1)}, u32[]{:S(2)}, u32[]{:S(2)}) collective-permute-start(f32[6,18,1,128]{3,2,1,0:T(1,128)S(1)} %broadcast_select_fusion.7), channel_id=1, source_target_pairs={{0,2},{2,0},{1,3},{3,1},{4,6},{6,4},{5,7},{7,5},{8,10},{10,8},{9,1... | collective-permute-start | bytes 165896 | tf_op jit(solution)/shard_map/ppermute | solution.py:17
  17.9 2.1 %copy-start.40 = (bf16[6,16,16,128]{3,2,1,0:T(8,128)(2,1)S(1)}, bf16[6,16,16,128]{3,2,1,0:T(8,128)(2,1)}, u32[]{:S(2)}) copy-start(bf16[6,16,16,128]{3,2,1,0:T(8,128)(2,1)} %param.11) | copy-start | bytes 1179652
  21.0 4.7 %copy-start.16 = (f32[6,18,1,128]{3,2,1,0:T(1,128)}, f32[6,18,1,128]{3,2,1,0:T(1,128)S(1)}, u32[]{:S(2)}) copy-start(f32[6,18,1,128]{3,2,1,0:T(1,128)S(1)} %get-tuple-element.77) | copy-start | bytes 165892
  21.0 4.7 %copy-start.18 = (f32[6,18,1,128]{3,2,1,0:T(1,128)}, f32[6,18,1,128]{3,2,1,0:T(1,128)S(1)}, u32[]{:S(2)}) copy-start(f32[6,18,1,128]{3,2,1,0:T(1,128)S(1)} %get-tuple-element.78) | copy-start | bytes 165892
  25.6 1.8 %collective-permute-start.3 = (f32[6,18,18,1]{2,1,3,0:T(8,128)S(1)}, f32[6,18,18,1]{2,1,3,0:T(8,128)S(1)}, u32[]{:S(2)}, u32[]{:S(2)}) collective-permute-start(f32[6,18,18,1]{2,1,3,0:T(8,128)S(1)} %copy.158), channel_id=1, source_target_pairs={{0,1},{1,0},{2,3},{3,2},{4,5},{5,4},{6,7},{7,6},{8,9},{9,8},{10,11... | collective-permute-start | bytes 23336 | tf_op jit(solution)/shard_map/ppermute | solution.py:17
  30.5 3.1 %copy-start.25 = (bf16[6,16,16,128]{3,2,1,0:T(8,128)(2,1)S(1)}, bf16[6,16,16,128]{3,2,1,0:T(8,128)(2,1)}, u32[]{:S(2)}) copy-start(bf16[6,16,16,128]{3,2,1,0:T(8,128)(2,1)} %param.10) | copy-start | bytes 1179652
  30.5 3.1 %copy-start.29 = (f32[6,18,17,128]{3,2,1,0:T(8,128)S(1)}, f32[6,18,17,128]{3,2,1,0:T(8,128)}, u32[]{:S(2)}) copy-start(f32[6,18,17,128]{3,2,1,0:T(8,128)} %get-tuple-element.55) | copy-start | bytes 2820100
  30.5 3.1 %copy-start.30 = (f32[6,18,17,128]{3,2,1,0:T(8,128)S(1)}, f32[6,18,17,128]{3,2,1,0:T(8,128)}, u32[]{:S(2)}) copy-start(f32[6,18,17,128]{3,2,1,0:T(8,128)} %get-tuple-element.56) | copy-start | bytes 2820100
  35.0 1.8 %copy-start.2 = (f32[1,16,16,128]{3,2,1,0:T(8,128)}, f32[1,16,16,128]{3,2,1,0:T(8,128)S(1)}, u32[]{:S(2)}) copy-start(f32[1,16,16,128]{3,2,1,0:T(8,128)S(1)} %get-tuple-element.40) | copy-start | bytes 393220
  36.9 1.2 %copy-start.35 = (f32[16,16,128]{2,1,0:T(8,128)S(1)}, f32[16,16,128]{2,1,0:T(8,128)}, u32[]{:S(2)}) copy-start(f32[16,16,128]{2,1,0:T(8,128)} %get-tuple-element.72) | copy-start | bytes 393220
  39.5 16.6 %copy-start.8 = (f32[3,16,16,128]{3,2,1,0:T(8,128)}, f32[3,16,16,128]{3,2,1,0:T(8,128)S(1)}, u32[]{:S(2)}) copy-start(f32[3,16,16,128]{3,2,1,0:T(8,128)S(1)} %get-tuple-element.33) | copy-start | bytes 1179652
  39.6 16.6 %copy-start.10 = (f32[3,16,16,128]{3,2,1,0:T(8,128)}, f32[3,16,16,128]{3,2,1,0:T(8,128)S(1)}, u32[]{:S(2)}) copy-start(f32[3,16,16,128]{3,2,1,0:T(8,128)S(1)} %get-tuple-element.64) | copy-start | bytes 1179652
  40.3 1.3 %copy-start.22 = (f32[32768]{0:T(1024)S(1)}, f32[32768]{0:T(1024)}, u32[]{:S(2)}) copy-start(f32[32768]{0:T(1024)} %copy-done.20) | copy-start | bytes 393220
  40.3 1.3 %copy-start.26 = (bf16[6,16,16,128]{3,2,1,0:T(8,128)(2,1)S(1)}, bf16[6,16,16,128]{3,2,1,0:T(8,128)(2,1)}, u32[]{:S(2)}) copy-start(bf16[6,16,16,128]{3,2,1,0:T(8,128)(2,1)} %param.10) | copy-start | bytes 1179652
  42.4 2.2 %collective-permute-start.4 = (f32[780]{0:T(1024)S(1)}, f32[780]{0:T(1024)S(1)}, u32[]{:S(2)}, u32[]{:S(2)}) collective-permute-start(f32[780]{0:T(1024)S(1)} %pad_maximum_fusion.19), channel_id=1, source_target_pairs={{0,1},{1,0},{2,3},{3,2},{4,5},{5,4},{6,7},{7,6},{8,9},{9,8},{10,11... | collective-permute-start | bytes 9368 | tf_op jit(solution)/shard_map/ppermute | solution.py:135
  42.9 3.6 %collective-permute-start.5 = (f32[780]{0:T(1024)S(1)}, f32[780]{0:T(1024)S(1)}, u32[]{:S(2)}, u32[]{:S(2)}) collective-permute-start(f32[780]{0:T(1024)S(1)} %pad_maximum_fusion.19), channel_id=1, source_target_pairs={{0,2},{1,3},{2,0},{3,1},{4,6},{5,7},{6,4},{7,5},{8,10},{9,11},{10,... | collective-permute-start | bytes 9368 | tf_op jit(solution)/shard_map/ppermute | solution.py:135
  44.6 3.1 %collective-permute-start.6 = (f32[780]{0:T(1024)S(1)}, f32[780]{0:T(1024)S(1)}, u32[]{:S(2)}, u32[]{:S(2)}) collective-permute-start(f32[780]{0:T(1024)S(1)} %pad_maximum_fusion.19), channel_id=1, source_target_pairs={{0,3},{1,2},{2,1},{3,0},{4,7},{5,6},{6,5},{7,4},{8,11},{9,10},{10,... | collective-permute-start | bytes 9368 | tf_op jit(solution)/shard_map/ppermute | solution.py:135
  47.6 4.5 %collective-permute-start.7 = (f32[780]{0:T(1024)S(1)}, f32[780]{0:T(1024)S(1)}, u32[]{:S(2)}, u32[]{:S(2)}) collective-permute-start(f32[780]{0:T(1024)S(1)} %add_add_fusion.5), channel_id=1, source_target_pairs={{0,4},{1,5},{2,6},{3,7},{4,0},{5,1},{6,2},{7,3},{8,12},{9,13},{10,... | collective-permute-start | bytes 9368 | tf_op jit(solution)/shard_map/ppermute | solution.py:135
  49.7 4.5 %collective-permute-start.8 = (f32[780]{0:T(1024)S(1)}, f32[780]{0:T(1024)S(1)}, u32[]{:S(2)}, u32[]{:S(2)}) collective-permute-start(f32[780]{0:T(1024)S(1)} %add_add_fusion.5), channel_id=1, source_target_pairs={{0,8},{1,9},{2,10},{3,11},{4,12},{5,13},{6,14},{7,15},{8,0},{9,1},... | collective-permute-start | bytes 9368 | tf_op jit(solution)/shard_map/ppermute | solution.py:135
  50.7 5.4 %collective-permute-start.9 = (f32[780]{0:T(1024)S(1)}, f32[780]{0:T(1024)S(1)}, u32[]{:S(2)}, u32[]{:S(2)}) collective-permute-start(f32[780]{0:T(1024)S(1)} %add_add_fusion.5), channel_id=1, source_target_pairs={{0,12},{1,13},{2,14},{3,15},{4,8},{5,9},{6,10},{7,11},{8,4},{9,5},... | collective-permute-start | bytes 9368 | tf_op jit(solution)/shard_map/ppermute | solution.py:135
  56.4 6.0 %collective-permute-start.10 = (f32[6,1,16,128]{3,2,1,0:T(8,128)S(1)}, f32[6,1,16,128]{3,2,1,0:T(8,128)S(1)}, u32[]{:S(2)}, u32[]{:S(2)}) collective-permute-start(f32[6,1,16,128]{3,2,1,0:T(8,128)S(1)} %get-tuple-element.62), channel_id=1, source_target_pairs={{4,0},{8,4},{12,8},{5,1},{9,5},{13,9},{6,2},{10,6},{14,10},{7,3},{... | collective-permute-start | bytes 147464 | tf_op jit(solution)/shard_map/ppermute | solution.py:25
  57.7 6.3 %collective-permute-start.11 = (f32[6,1,16,128]{3,2,1,0:T(8,128)S(1)}, f32[6,1,16,128]{3,2,1,0:T(8,128)S(1)}, u32[]{:S(2)}, u32[]{:S(2)}) collective-permute-start(f32[6,1,16,128]{3,2,1,0:T(8,128)S(1)} %get-tuple-element.61), channel_id=1, source_target_pairs={{0,4},{4,8},{8,12},{1,5},{5,9},{9,13},{2,6},{6,10},{10,14},{3,7},{... | collective-permute-start | bytes 147464 | tf_op jit(solution)/shard_map/ppermute | solution.py:24
  64.1 4.2 %collective-permute-start.12 = (f32[6,18,1,128]{3,2,1,0:T(1,128)S(1)}, f32[6,18,1,128]{3,2,1,0:T(1,128)S(1)}, u32[]{:S(2)}, u32[]{:S(2)}) collective-permute-start(f32[6,18,1,128]{3,2,1,0:T(1,128)S(1)} %broadcast_select_fusion.4), channel_id=1, source_target_pairs={{0,2},{2,0},{1,3},{3,1},{4,6},{6,4},{5,7},{7,5},{8,10},{10,8},{9,1... | collective-permute-start | bytes 165896 | tf_op jit(solution)/shard_map/ppermute | solution.py:17
  68.4 4.7 %copy-start.12 = (f32[6,18,1,128]{3,2,1,0:T(1,128)}, f32[6,18,1,128]{3,2,1,0:T(1,128)S(1)}, u32[]{:S(2)}) copy-start(f32[6,18,1,128]{3,2,1,0:T(1,128)S(1)} %get-tuple-element.75) | copy-start | bytes 165892
  68.4 4.7 %copy-start.14 = (f32[6,18,1,128]{3,2,1,0:T(1,128)}, f32[6,18,1,128]{3,2,1,0:T(1,128)S(1)}, u32[]{:S(2)}) copy-start(f32[6,18,1,128]{3,2,1,0:T(1,128)S(1)} %get-tuple-element.76) | copy-start | bytes 165892
  73.0 1.8 %collective-permute-start.13 = (f32[6,18,18,1]{2,1,3,0:T(8,128)S(1)}, f32[6,18,18,1]{2,1,3,0:T(8,128)S(1)}, u32[]{:S(2)}, u32[]{:S(2)}) collective-permute-start(f32[6,18,18,1]{2,1,3,0:T(8,128)S(1)} %copy.167), channel_id=1, source_target_pairs={{0,1},{1,0},{2,3},{3,2},{4,5},{5,4},{6,7},{7,6},{8,9},{9,8},{10,11... | collective-permute-start | bytes 23336 | tf_op jit(solution)/shard_map/ppermute | solution.py:17
  77.8 3.6 %copy-start.27 = (f32[6,18,17,128]{3,2,1,0:T(8,128)S(1)}, f32[6,18,17,128]{3,2,1,0:T(8,128)}, u32[]{:S(2)}) copy-start(f32[6,18,17,128]{3,2,1,0:T(8,128)} %get-tuple-element.53) | copy-start | bytes 2820100
  77.8 3.7 %copy-start.28 = (f32[6,18,17,128]{3,2,1,0:T(8,128)S(1)}, f32[6,18,17,128]{3,2,1,0:T(8,128)}, u32[]{:S(2)}) copy-start(f32[6,18,17,128]{3,2,1,0:T(8,128)} %get-tuple-element.54) | copy-start | bytes 2820100
  84.7 1.4 %copy-start.7 = (f32[6,16,16,128]{3,2,1,0:T(8,128)S(1)}, f32[6,16,16,128]{3,2,1,0:T(8,128)}, u32[]{:S(2)}) copy-start(f32[6,16,16,128]{3,2,1,0:T(8,128)} %convert_element_type.15) | copy-start | bytes 2359300
  84.7 1.4 %copy-start.23 = (f32[32768]{0:T(1024)S(1)}, f32[32768]{0:T(1024)}, u32[]{:S(2)}) copy-start(f32[32768]{0:T(1024)} %copy-done.20) | copy-start | bytes 393220
  84.7 1.4 %copy-start.32 = (f32[16,16,128]{2,1,0:T(8,128)S(1)}, f32[16,16,128]{2,1,0:T(8,128)}, u32[]{:S(2)}) copy-start(f32[16,16,128]{2,1,0:T(8,128)} %get-tuple-element.73) | copy-start | bytes 393220
  84.7 1.4 %copy-start.34 = (f32[16,16,128]{2,1,0:T(8,128)S(1)}, f32[16,16,128]{2,1,0:T(8,128)}, u32[]{:S(2)}) copy-start(f32[16,16,128]{2,1,0:T(8,128)} %get-tuple-element.74) | copy-start | bytes 393220
  84.7 1.4 %copy-start.36 = (f32[16,16,128]{2,1,0:T(8,128)S(1)}, f32[16,16,128]{2,1,0:T(8,128)}, u32[]{:S(2)}) copy-start(f32[16,16,128]{2,1,0:T(8,128)} %get-tuple-element.72) | copy-start | bytes 393220
  86.9 14.5 %copy-start.9 = (f32[3,16,16,128]{3,2,1,0:T(8,128)S(1)}, f32[3,16,16,128]{3,2,1,0:T(8,128)}, u32[]{:S(2)}) copy-start(f32[3,16,16,128]{3,2,1,0:T(8,128)} %copy-done.8) | copy-start | bytes 1179652
  86.9 14.5 %copy-start.11 = (f32[3,16,16,128]{3,2,1,0:T(8,128)S(1)}, f32[3,16,16,128]{3,2,1,0:T(8,128)}, u32[]{:S(2)}) copy-start(f32[3,16,16,128]{3,2,1,0:T(8,128)} %copy-done.10) | copy-start | bytes 1179652
  88.1 1.9 %collective-permute-start.14 = (f32[134]{0:T(256)S(1)}, f32[134]{0:T(256)S(1)}, u32[]{:S(2)}, u32[]{:S(2)}) collective-permute-start(f32[134]{0:T(256)S(1)} %pad_maximum_fusion.20), channel_id=1, source_target_pairs={{0,1},{1,0},{2,3},{3,2},{4,5},{5,4},{6,7},{7,6},{8,9},{9,8},{10,11... | collective-permute-start | bytes 1616 | tf_op jit(solution)/shard_map/ppermute | solution.py:135
  88.6 3.6 %collective-permute-start.15 = (f32[134]{0:T(256)S(1)}, f32[134]{0:T(256)S(1)}, u32[]{:S(2)}, u32[]{:S(2)}) collective-permute-start(f32[134]{0:T(256)S(1)} %pad_maximum_fusion.20), channel_id=1, source_target_pairs={{0,2},{1,3},{2,0},{3,1},{4,6},{5,7},{6,4},{7,5},{8,10},{9,11},{10,... | collective-permute-start | bytes 1616 | tf_op jit(solution)/shard_map/ppermute | solution.py:135
  89.4 3.0 %collective-permute-start.16 = (f32[134]{0:T(256)S(1)}, f32[134]{0:T(256)S(1)}, u32[]{:S(2)}, u32[]{:S(2)}) collective-permute-start(f32[134]{0:T(256)S(1)} %pad_maximum_fusion.20), channel_id=1, source_target_pairs={{0,3},{1,2},{2,1},{3,0},{4,7},{5,6},{6,5},{7,4},{8,11},{9,10},{10,... | collective-permute-start | bytes 1616 | tf_op jit(solution)/shard_map/ppermute | solution.py:135
  92.4 5.0 %collective-permute-start.17 = (f32[134]{0:T(256)S(1)}, f32[134]{0:T(256)S(1)}, u32[]{:S(2)}, u32[]{:S(2)}) collective-permute-start(f32[134]{0:T(256)S(1)} %add_add_fusion.7), channel_id=1, source_target_pairs={{0,4},{1,5},{2,6},{3,7},{4,0},{5,1},{6,2},{7,3},{8,12},{9,13},{10,... | collective-permute-start | bytes 1616 | tf_op jit(solution)/shard_map/ppermute | solution.py:135
  94.8 4.5 %collective-permute-start.18 = (f32[134]{0:T(256)S(1)}, f32[134]{0:T(256)S(1)}, u32[]{:S(2)}, u32[]{:S(2)}) collective-permute-start(f32[134]{0:T(256)S(1)} %add_add_fusion.7), channel_id=1, source_target_pairs={{0,8},{1,9},{2,10},{3,11},{4,12},{5,13},{6,14},{7,15},{8,0},{9,1},... | collective-permute-start | bytes 1616 | tf_op jit(solution)/shard_map/ppermute | solution.py:135
  94.8 5.4 %collective-permute-start.19 = (f32[134]{0:T(256)S(1)}, f32[134]{0:T(256)S(1)}, u32[]{:S(2)}, u32[]{:S(2)}) collective-permute-start(f32[134]{0:T(256)S(1)} %add_add_fusion.7), channel_id=1, source_target_pairs={{0,12},{1,13},{2,14},{3,15},{4,8},{5,9},{6,10},{7,11},{8,4},{9,5},... | collective-permute-start | bytes 1616 | tf_op jit(solution)/shard_map/ppermute | solution.py:135
  (17 other events, 17.0 us)

commit v6 on v5

--- a/solution.py
+++ b/solution.py
@@ -7,11 +7,14 @@
 RELAXATION = 0.6
 
 
-def with_halo(array, sides, width):
+def with_halo(array, sides, width, tie=None):
     for axis, dim in sides:
         peers, length = (lax.axis_size(axis), array.shape[dim])
         last = lax.slice_in_dim(array, length - width, length, axis=dim)
         initial = lax.slice_in_dim(array, 0, width, axis=dim)
+        if tie is not None:
+            last = last + tie
+            initial = initial + tie
         if peers == 2:
             first = lax.axis_index(axis) == 0
             got = lax.ppermute(jnp.where(first, last, initial), axis, [(0, 1), (1, 0)])
@@ -196,6 +199,8 @@
     response_imag = plain_imag + DAMPING * plain_real
     response = block_sums(jnp.concatenate([response_real, response_imag]))
     field = warm.astype(jnp.float32)
+    padded = with_halo(field, (("gx", 1),), 1)
+    after_x = 0.0 * padded[0, 0, 0, 0]
     first = group_sum(
         jnp.concatenate(
             [
@@ -204,7 +209,8 @@
                 jnp.sum(gain_imag, axis=(1, 2, 3)),
                 response.reshape(-1),
             ]
-        ),
+        )
+        + after_x,
         axes,
     )
     mean_field = first[:6] / count
@@ -212,7 +218,8 @@
     gain_total_imag = first[9:12]
     response = first[12:].reshape(response.shape)
     sweep_args = (lame_first, shear, density_cells, mask, source_cells, omega_sq, impedance)
-    padded = with_halo(field, (("gx", 1), ("gy", 2), ("col", 3)), 1)
+    padded = with_halo(padded, (("gy", 2),), 1)
+    padded = with_halo(padded, (("col", 3),), 1, 0.0 * jnp.sum(mean_field))
     field = sweep(padded, *sweep_args)
     second_local = jnp.sum(mask * field, axis=(1, 2, 3))
     field = add_mean(field, gain_real, gain_imag, mean_field)

time: 103 us -> 104 us (level)
  waiting for transfers between devices: 17.2 us -> 12.5 us
  starting transfers between devices: 29 us -> 32 us
  local copies, waits for them, and re-layouts: 25.7 us -> 27.5 us
  between operations: 2.17 us -> 3.47 us
    ppermute x12, waiting for transfers between devices: 12.1 us -> 9.2 us  [group_sum(): lax.ppermute(value, axes, [(i, i ^ m * stride) for i in range(size)])]
    ppermute x12, starting transfers between devices: 13.3 us -> 15.7 us  [group_sum(): lax.ppermute(value, axes, [(i, i ^ m * stride) for i in range(size)])]
    ppermute x4, waiting for transfers between devices: 3.53 us -> 1.79 us  [with_halo(): got = lax.ppermute(jnp.where(first, last, initial), axis, [(0, 1), (1, 0)])]
    unnamed x96 -> x104, local copies, waits for them, and re-layouts: 10.4 us -> 11 us
  transfers between devices with their start and end apart: 20 -> 20, of which waited for: 10 -> 8; matrix products, arithmetic and copies ran while one was open for 12% -> 15% of each run, Pallas kernels for 0% -> 0%
where the time goes in v6:
time: 104 us
  starting transfers between devices  32 us (31%)
  other arithmetic  28.4 us (27%)
  local copies, waits for them, and re-layouts  27.5 us (26%)
  waiting for transfers between devices  12.5 us (12%)
  between operations  3.47 us (3%)
    ppermute x12, starting transfers between devices, group_sum(): lax.ppermute(value, axes, [(i, i ^ m * stride) for i in range(size)])  15.7 us
    unnamed x104, local copies, waits for them, and re-layouts  11 us
    concatenate x6, other arithmetic, with_halo(): array = jnp.concatenate([before, array, after], axis=dim)  10.5 us
    ppermute x2, starting transfers between devices, with_halo(): before = lax.ppermute(last, axis, up)  9.69 us
    ppermute x12, waiting for transfers between devices, group_sum(): lax.ppermute(value, axes, [(i, i ^ m * stride) for i in range(size)])  9.2 us
    add x12, other arithmetic, navier(): result.append(shear * laplace[channel] + (lame_first + shear) * divergence)  5.61 us
    ppermute x4, starting transfers between devices, with_halo(): got = lax.ppermute(jnp.where(first, last, initial), axis, [(0, 1), (1, 0)])  3.73 us
    select_n x2, local copies, waits for them, and re-layouts, with_halo(): before = jnp.where(first, zero, got)  3.31 us
  transfers between devices with their start and end apart: 20, of which 8 were waited for; matrix products, arithmetic and copies ran while one was open for 15% of the time, Pallas kernels for 0%

profile of v6, /device:TPU:0, one launch (start us, length us, event | category | flops | bytes accessed | tf_op | source)
XLA Modules:
  0.0 103.8 jit_solution(3377343174081468190)
XLA Ops:
  0.7 0.8 fusion.113
  1.5 4.9 %collective-permute-start.1 = (f32[6,1,16,128]{3,2,1,0:T(8,128)S(1)}, f32[6,1,16,128]{3,2,1,0:T(8,128)S(1)}, u32[]{:S(2)}, u32[]{:S(2)}) collective-permute-start(f32[6,1,16,128]{3,2,1,0:T(8,128)S(1)} %get-tuple-element.65), channel_id=1, source_target_pairs={{0,4},{4,8},{8,12},{1,5},{5,9},{9,13},{2,6},{6,10},{10,14},{3,7},{... | collective-permute-start | bytes 147464 | tf_op jit(solution)/shard_map/ppermute | solution.py:27
  6.4 0.8 slice_bitcast_fusion.2
  7.2 0.8 select_reduce_fusion.1
  9.1 1.5 %scatter_custom_fusion = f32[32768]{0:T(1024)S(1)} fusion(s32[256]{0:T(256)S(1)} %bitcast.24, f32[256]{0:T(256)S(1)} %broadcast.108, f32[]{:T(128)} %constant.19.clone.1), kind=kCustom, calls=%fused_computation.245 | custom fusion | bytes 131076 | tf_op jit(solution)/shard_map/scatter | solution.py:171
  10.8 0.8 convert_multiply_fusion
  16.0 3.2 %collective-permute-start.4 = (f32[780]{0:T(1024)S(1)}, f32[780]{0:T(1024)S(1)}, u32[]{:S(2)}, u32[]{:S(2)}) collective-permute-start(f32[780]{0:T(1024)S(1)} %maximum_add_fusion.24), channel_id=1, source_target_pairs={{0,2},{1,3},{2,0},{3,1},{4,6},{5,7},{6,4},{7,5},{8,10},{9,11},{10,... | collective-permute-start | bytes 9368 | tf_op jit(solution)/shard_map/ppermute | solution.py:138
  19.2 1.5 %collective-permute-start = (f32[6,1,16,128]{3,2,1,0:T(8,128)S(1)}, f32[6,1,16,128]{3,2,1,0:T(8,128)S(1)}, u32[]{:S(2)}, u32[]{:S(2)}) collective-permute-start(f32[6,1,16,128]{3,2,1,0:T(8,128)S(1)} %get-tuple-element.64), channel_id=1, source_target_pairs={{4,0},{8,4},{12,8},{5,1},{9,5},{13,9},{6,2},{10,6},{14,10},{7,3},{... | collective-permute-start | bytes 147464 | tf_op jit(solution)/shard_map/ppermute | solution.py:28
  20.9 0.9 reshape.126
  22.0 0.9 reshape.128
  23.0 1.0 convert_element_type.13
  23.9 2.7 %collective-permute-start.6 = (f32[780]{0:T(1024)S(1)}, f32[780]{0:T(1024)S(1)}, u32[]{:S(2)}, u32[]{:S(2)}) collective-permute-start(f32[780]{0:T(1024)S(1)} %add_add_fusion.5), channel_id=1, source_target_pairs={{0,4},{1,5},{2,6},{3,7},{4,0},{5,1},{6,2},{7,3},{8,12},{9,13},{10,... | collective-permute-start | bytes 9368 | tf_op jit(solution)/shard_map/ppermute | solution.py:138
  26.7 2.5 %collective-permute-start.7 = (f32[780]{0:T(1024)S(1)}, f32[780]{0:T(1024)S(1)}, u32[]{:S(2)}, u32[]{:S(2)}) collective-permute-start(f32[780]{0:T(1024)S(1)} %add_add_fusion.5), channel_id=1, source_target_pairs={{0,8},{1,9},{2,10},{3,11},{4,12},{5,13},{6,14},{7,15},{8,0},{9,1},... | collective-permute-start | bytes 9368 | tf_op jit(solution)/shard_map/ppermute | solution.py:138
  29.3 1.8 %collective-permute-start.2 = (f32[6,18,1,128]{3,2,1,0:T(1,128)S(1)}, f32[6,18,1,128]{3,2,1,0:T(1,128)S(1)}, u32[]{:S(2)}, u32[]{:S(2)}) collective-permute-start(f32[6,18,1,128]{3,2,1,0:T(1,128)S(1)} %broadcast_select_fusion.7), channel_id=1, source_target_pairs={{0,2},{2,0},{1,3},{3,1},{4,6},{6,4},{5,7},{7,5},{8,10},{10,8},{9,1... | collective-permute-start | bytes 165896 | tf_op jit(solution)/shard_map/ppermute | solution.py:20
  31.2 3.4 %collective-permute-done.8 = f32[780]{0:T(1024)S(1)} collective-permute-done((f32[780]{0:T(1024)S(1)}, f32[780]{0:T(1024)S(1)}, u32[]{:S(2)}, u32[]{:S(2)}) %collective-permute-start.8) | collective-permute-done | bytes 3152 | tf_op jit(solution)/shard_map/ppermute | solution.py:138
  36.8 1.5 %fusion.112 = (f32[6,18,18,1]{3,2,1,0:T(8,128)}, f32[6,18,18,1]{3,2,1,0:T(8,128)S(1)}) fusion(f32[6,18,18,128]{3,2,1,0:T(8,128)S(1)} %pad_maximum_fusion.3), kind=kLoop, calls=%fused_computation.284 | loop fusion | bytes 31104 | tf_op jit(solution)/shard_map/slice | solution.py:13
  38.3 2.0 %copy.179 = f32[6,18,18,1]{2,3,1,0:T(1,128)S(1)} copy(f32[6,18,18,1]{3,2,1,0:T(8,128)} %get-tuple-element.48) | data formatting | bytes 15552
  40.3 0.7 copy.180
  41.2 1.7 %pad_maximum_fusion.2 = (f32[6,18,17,128]{3,2,1,0:T(8,128)}, f32[6,18,17,128]{3,2,1,0:T(8,128)}) fusion(f32[6,18,1,128]{3,2,1,0:T(1,128)S(1)} %get-tuple-element.76, f32[6,1,16,128]{3,2,1,0:T(8,128)S(1)} %collective-permute-done, f32[6,16,16,128]{3,2,1,0:T(8,128)S(1)} %convert_element_type.12, f32[6,1,16,128]{3,2,1,0:T(8,128)S(1)} %collective-permute-done.1, ...), kind=kLoop, calls=%fused_computation.5 | loop fusion | flops 1410048 | bytes 2875392 | tf_op jit(solution)/shard_map/concatenate | solution.py:29
  43.6 0.8 copy.161
  44.4 1.7 %copy.164 = f32[6,18,18,1]{3,2,1,0:T(8,128)S(1)} copy(f32[6,18,18,1]{2,1,3,0:T(8,128)} %get-tuple-element.69) | data formatting | bytes 15552 | tf_op jit(solution)/shard_map/jit(_where)/select_n | solution.py:22
  46.0 3.1 %pad_maximum_fusion = (f32[6,18,18,129]{3,2,1,0:T(8,128)S(1)}, f32[6,18,18,129]{3,2,1,0:T(8,128)S(1)}) fusion(f32[6,18,18,1]{3,2,1,0:T(8,128)S(1)} %copy.161, f32[6,18,1,128]{3,2,1,0:T(1,128)} %copy-done.20, f32[6,1,16,128]{3,2,1,0:T(8,128)S(1)} %collective-permute-done, f32[6,16,16,128]{3,2,1,0:T(8,128)S(1)} %convert_element_type.12, ...), kind=kLoop, calls=%fused_computation.1 | loop fusion | flops 2507760 | bytes 3017088 | tf_op jit(solution)/shard_map/concatenate | solution.py:29
  52.5 0.7 fusion.62
  54.9 1.4 %collective-permute-start.10 = (f32[6,1,16,128]{3,2,1,0:T(8,128)S(1)}, f32[6,1,16,128]{3,2,1,0:T(8,128)S(1)}, u32[]{:S(2)}, u32[]{:S(2)}) collective-permute-start(f32[6,1,16,128]{3,2,1,0:T(8,128)S(1)} %get-tuple-element.61), channel_id=1, source_target_pairs={{4,0},{8,4},{12,8},{5,1},{9,5},{13,9},{6,2},{10,6},{14,10},{7,3},{... | collective-permute-start | bytes 147464 | tf_op jit(solution)/shard_map/ppermute | solution.py:28
  56.3 4.8 %collective-permute-start.11 = (f32[6,1,16,128]{3,2,1,0:T(8,128)S(1)}, f32[6,1,16,128]{3,2,1,0:T(8,128)S(1)}, u32[]{:S(2)}, u32[]{:S(2)}) collective-permute-start(f32[6,1,16,128]{3,2,1,0:T(8,128)S(1)} %get-tuple-element.60), channel_id=1, source_target_pairs={{0,4},{4,8},{8,12},{1,5},{5,9},{9,13},{2,6},{6,10},{10,14},{3,7},{... | collective-permute-start | bytes 147464 | tf_op jit(solution)/shard_map/ppermute | solution.py:27
  61.1 1.5 %collective-permute-done.11 = f32[6,1,16,128]{3,2,1,0:T(8,128)S(1)} collective-permute-done((f32[6,1,16,128]{3,2,1,0:T(8,128)S(1)}, f32[6,1,16,128]{3,2,1,0:T(8,128)S(1)}, u32[]{:S(2)}, u32[]{:S(2)}) %collective-permute-start.11) | collective-permute-done | bytes 49184 | tf_op jit(solution)/shard_map/ppermute | solution.py:27
  62.6 1.8 %collective-permute-start.12 = (f32[6,18,1,128]{3,2,1,0:T(1,128)S(1)}, f32[6,18,1,128]{3,2,1,0:T(1,128)S(1)}, u32[]{:S(2)}, u32[]{:S(2)}) collective-permute-start(f32[6,18,1,128]{3,2,1,0:T(1,128)S(1)} %broadcast_select_fusion.4), channel_id=1, source_target_pairs={{0,2},{2,0},{1,3},{3,1},{4,6},{6,4},{5,7},{7,5},{8,10},{10,8},{9,1... | collective-permute-start | bytes 165896 | tf_op jit(solution)/shard_map/ppermute | solution.py:20
  65.1 1.8 %collective-permute-done.12 = f32[6,18,1,128]{3,2,1,0:T(1,128)S(1)} collective-permute-done((f32[6,18,1,128]{3,2,1,0:T(1,128)S(1)}, f32[6,18,1,128]{3,2,1,0:T(1,128)S(1)}, u32[]{:S(2)}, u32[]{:S(2)}) %collective-permute-start.12) | collective-permute-done | bytes 55328 | tf_op jit(solution)/shard_map/ppermute | solution.py:20
  67.2 1.5 %fusion.111 = (f32[6,18,18,1]{3,2,1,0:T(8,128)S(1)}, f32[6,18,18,1]{3,2,1,0:T(8,128)}) fusion(f32[6,18,18,128]{3,2,1,0:T(8,128)S(1)} %pad_maximum_fusion.5), kind=kLoop, calls=%fused_computation.283 | loop fusion | bytes 31104 | tf_op jit(solution)/shard_map/slice | solution.py:14
  68.7 2.0 %copy.181 = f32[6,18,18,1]{2,3,1,0:T(1,128)S(1)} copy(f32[6,18,18,1]{3,2,1,0:T(8,128)} %get-tuple-element.47) | data formatting | bytes 15552
  70.7 0.7 copy.182
  71.7 1.7 %pad_maximum_fusion.4 = (f32[6,18,17,128]{3,2,1,0:T(8,128)}, f32[6,18,17,128]{3,2,1,0:T(8,128)}) fusion(f32[6,18,1,128]{3,2,1,0:T(1,128)S(1)} %get-tuple-element.74, f32[6,1,16,128]{3,2,1,0:T(8,128)S(1)} %collective-permute-done.10, f32[3,16,16,128]{3,2,1,0:T(8,128)S(1)} %get-tuple-element.31, f32[3,16,16,128]{3,2,1,0:T(8,128)S(1)} %get-tuple-element.27, ...), kind=kLoop, calls=%fused_computation.8 | loop fusion | flops 1880064 | bytes 2875392 | tf_op jit(solution)/shard_map/concatenate | solution.py:29
  74.0 0.8 copy.170
  74.8 1.7 %copy.173 = f32[6,18,18,1]{3,2,1,0:T(8,128)S(1)} copy(f32[6,18,18,1]{2,1,3,0:T(8,128)} %get-tuple-element.67) | data formatting | bytes 15552 | tf_op jit(solution)/shard_map/jit(_where)/select_n | solution.py:22
  76.4 3.6 %pad_maximum_fusion.1 = (f32[6,18,18,129]{3,2,1,0:T(8,128)S(1)}, f32[6,18,18,129]{3,2,1,0:T(8,128)S(1)}) fusion(f32[6,18,18,1]{3,2,1,0:T(8,128)S(1)} %copy.170, f32[6,18,1,128]{3,2,1,0:T(1,128)} %copy-done.24, f32[6,1,16,128]{3,2,1,0:T(8,128)S(1)} %collective-permute-done.10, f32[3,16,16,128]{3,2,1,0:T(8,128)S(1)} %get-tuple-element.31, ...), kind=kLoop, calls=%fused_computation.3 | loop fusion | flops 3009312 | bytes 3017088 | tf_op jit(solution)/shard_map/concatenate | solution.py:29
  82.6 0.7 fusion.44
  83.3 0.7 fusion.26
  84.8 1.4 %subtract_reduce_fusion = (f32[16,16,128]{2,1,0:T(8,128)}, f32[3,16,16,128]{3,2,1,0:T(8,128)S(1)}, f32[3,16,16,128]{3,2,1,0:T(8,128)S(1)}) fusion(f32[6,16,16,128]{3,2,1,0:T(8,128)S(1)} %copy-done.17, f32[3,16,16,128]{3,2,1,0:T(8,128)S(1)} %get-tuple-element.27, f32[16,16,128]{2,1,0:T(8,128)S(1)} %copy-done.37, f32[3,16,16,128]{3,2,1,0:T(8,128)S(1)} %get-tuple-element.31, ...), kind=kLoop, calls=%fused_computation.61 | loop fusion | flops 5275648 | bytes 4587544 | tf_op jit(solution)/shard_map/reduce_sum | solution.py:233
  86.2 1.3 %copy.177 = f32[16,16,128]{1,2,0:T(8,128)S(1)} copy(f32[16,16,128]{2,1,0:T(8,128)} %get-tuple-element.20) | data formatting | bytes 262144
  88.8 1.9 %collective-permute-start.15 = (f32[134]{0:T(256)S(1)}, f32[134]{0:T(256)S(1)}, u32[]{:S(2)}, u32[]{:S(2)}) collective-permute-start(f32[134]{0:T(256)S(1)} %pad_maximum_fusion.19), channel_id=1, source_target_pairs={{0,2},{1,3},{2,0},{3,1},{4,6},{5,7},{6,4},{7,5},{8,10},{9,11},{10,... | collective-permute-start | bytes 1616 | tf_op jit(solution)/shard_map/ppermute | solution.py:138
  90.7 1.7 %collective-permute-done.15 = f32[134]{0:T(256)S(1)} collective-permute-done((f32[134]{0:T(256)S(1)}, f32[134]{0:T(256)S(1)}, u32[]{:S(2)}, u32[]{:S(2)}) %collective-permute-start.15) | collective-permute-done | bytes 568 | tf_op jit(solution)/shard_map/ppermute | solution.py:138
  92.4 1.3 %collective-permute-done.16 = f32[134]{0:T(256)S(1)} collective-permute-done((f32[134]{0:T(256)S(1)}, f32[134]{0:T(256)S(1)}, u32[]{:S(2)}, u32[]{:S(2)}) %collective-permute-start.16) | collective-permute-done | bytes 568 | tf_op jit(solution)/shard_map/ppermute | solution.py:138
  93.8 2.3 %collective-permute-start.17 = (f32[134]{0:T(256)S(1)}, f32[134]{0:T(256)S(1)}, u32[]{:S(2)}, u32[]{:S(2)}) collective-permute-start(f32[134]{0:T(256)S(1)} %add_add_fusion.7), channel_id=1, source_target_pairs={{0,4},{1,5},{2,6},{3,7},{4,0},{5,1},{6,2},{7,3},{8,12},{9,13},{10,... | collective-permute-start | bytes 1616 | tf_op jit(solution)/shard_map/ppermute | solution.py:138
  96.1 2.4 %collective-permute-start.19 = (f32[134]{0:T(256)S(1)}, f32[134]{0:T(256)S(1)}, u32[]{:S(2)}, u32[]{:S(2)}) collective-permute-start(f32[134]{0:T(256)S(1)} %add_add_fusion.7), channel_id=1, source_target_pairs={{0,12},{1,13},{2,14},{3,15},{4,8},{5,9},{6,10},{7,11},{8,4},{9,5},... | collective-permute-start | bytes 1616 | tf_op jit(solution)/shard_map/ppermute | solution.py:138
  98.8 1.8 %collective-permute-done.18 = f32[134]{0:T(256)S(1)} collective-permute-done((f32[134]{0:T(256)S(1)}, f32[134]{0:T(256)S(1)}, u32[]{:S(2)}, u32[]{:S(2)}) %collective-permute-start.18) | collective-permute-done | bytes 568 | tf_op jit(solution)/shard_map/ppermute | solution.py:138
  100.6 0.9 collective-permute-done.19
  102.0 0.7 copy.176
  102.8 0.9 pad_maximum_fusion.13
  (193 shorter events, 19.4 us)
Async XLA Ops:
  0.6 8.5 %copy-start.47 = (s32[1,256]{1,0:T(1,128)S(1)}, s32[1,256]{1,0:T(1,128)}, u32[]{:S(2)}) copy-start(s32[1,256]{1,0:T(1,128)} %param.15) | copy-start | bytes 3076
  0.6 10.0 %copy-start.48 = (f32[2,3]{1,0:T(2,128)S(1)}, f32[2,3]{1,0:T(2,128)}, u32[]{:S(2)}) copy-start(f32[2,3]{1,0:T(2,128)} %param.16) | copy-start | bytes 76
  0.7 10.0 %copy-start.41 = (bf16[6,16,16,128]{3,2,1,0:T(8,128)(2,1)S(1)}, bf16[6,16,16,128]{3,2,1,0:T(8,128)(2,1)}, u32[]{:S(2)}) copy-start(bf16[6,16,16,128]{3,2,1,0:T(8,128)(2,1)} %param.11) | copy-start | bytes 1179652
  1.5 13.2 %collective-permute-start.1 = (f32[6,1,16,128]{3,2,1,0:T(8,128)S(1)}, f32[6,1,16,128]{3,2,1,0:T(8,128)S(1)}, u32[]{:S(2)}, u32[]{:S(2)}) collective-permute-start(f32[6,1,16,128]{3,2,1,0:T(8,128)S(1)} %get-tuple-element.65), channel_id=1, source_target_pairs={{0,4},{4,8},{8,12},{1,5},{5,9},{9,13},{2,6},{6,10},{10,14},{3,7},{... | collective-permute-start | bytes 147464 | tf_op jit(solution)/shard_map/ppermute | solution.py:27
  8.0 2.7 %copy-start.43 = (bf16[16,16,128]{2,1,0:T(8,128)(2,1)S(1)}, bf16[16,16,128]{2,1,0:T(8,128)(2,1)}, u32[]{:S(2)}) copy-start(bf16[16,16,128]{2,1,0:T(8,128)(2,1)} %param.12) | copy-start | bytes 196612
  10.6 2.4 %copy-start.10 = (f32[32768]{0:T(1024)}, f32[32768]{0:T(1024)S(1)}, u32[]{:S(2)}) copy-start(f32[32768]{0:T(1024)S(1)} %scatter_custom_fusion) | copy-start | bytes 393220
  10.8 1.7 %copy-start.16 = (f32[6,16,16,128]{3,2,1,0:T(8,128)}, f32[6,16,16,128]{3,2,1,0:T(8,128)S(1)}, u32[]{:S(2)}) copy-start(f32[6,16,16,128]{3,2,1,0:T(8,128)S(1)} %convert_element_type.15) | copy-start | bytes 2359300
  15.9 8.0 %collective-permute-start.3 = (f32[780]{0:T(1024)S(1)}, f32[780]{0:T(1024)S(1)}, u32[]{:S(2)}, u32[]{:S(2)}) collective-permute-start(f32[780]{0:T(1024)S(1)} %maximum_add_fusion.24), channel_id=1, source_target_pairs={{0,1},{1,0},{2,3},{3,2},{4,5},{5,4},{6,7},{7,6},{8,9},{9,8},{10,11... | collective-permute-start | bytes 9368 | tf_op jit(solution)/shard_map/ppermute | solution.py:138
  16.0 8.0 %collective-permute-start.4 = (f32[780]{0:T(1024)S(1)}, f32[780]{0:T(1024)S(1)}, u32[]{:S(2)}, u32[]{:S(2)}) collective-permute-start(f32[780]{0:T(1024)S(1)} %maximum_add_fusion.24), channel_id=1, source_target_pairs={{0,2},{1,3},{2,0},{3,1},{4,6},{5,7},{6,4},{7,5},{8,10},{9,11},{10,... | collective-permute-start | bytes 9368 | tf_op jit(solution)/shard_map/ppermute | solution.py:138
  19.1 4.8 %collective-permute-start.5 = (f32[780]{0:T(1024)S(1)}, f32[780]{0:T(1024)S(1)}, u32[]{:S(2)}, u32[]{:S(2)}) collective-permute-start(f32[780]{0:T(1024)S(1)} %maximum_add_fusion.24), channel_id=1, source_target_pairs={{0,3},{1,2},{2,1},{3,0},{4,7},{5,6},{6,5},{7,4},{8,11},{9,10},{10,... | collective-permute-start | bytes 9368 | tf_op jit(solution)/shard_map/ppermute | solution.py:138
  19.2 10.0 %collective-permute-start = (f32[6,1,16,128]{3,2,1,0:T(8,128)S(1)}, f32[6,1,16,128]{3,2,1,0:T(8,128)S(1)}, u32[]{:S(2)}, u32[]{:S(2)}) collective-permute-start(f32[6,1,16,128]{3,2,1,0:T(8,128)S(1)} %get-tuple-element.64), channel_id=1, source_target_pairs={{4,0},{8,4},{12,8},{5,1},{9,5},{13,9},{6,2},{10,6},{14,10},{7,3},{... | collective-permute-start | bytes 147464 | tf_op jit(solution)/shard_map/ppermute | solution.py:28
  20.8 2.2 %copy-start.42 = (bf16[6,16,16,128]{3,2,1,0:T(8,128)(2,1)S(1)}, bf16[6,16,16,128]{3,2,1,0:T(8,128)(2,1)}, u32[]{:S(2)}) copy-start(bf16[6,16,16,128]{3,2,1,0:T(8,128)(2,1)} %param.9) | copy-start | bytes 1179652
  23.9 7.1 %collective-permute-start.6 = (f32[780]{0:T(1024)S(1)}, f32[780]{0:T(1024)S(1)}, u32[]{:S(2)}, u32[]{:S(2)}) collective-permute-start(f32[780]{0:T(1024)S(1)} %add_add_fusion.5), channel_id=1, source_target_pairs={{0,4},{1,5},{2,6},{3,7},{4,0},{5,1},{6,2},{7,3},{8,12},{9,13},{10,... | collective-permute-start | bytes 9368 | tf_op jit(solution)/shard_map/ppermute | solution.py:138
  26.7 4.5 %collective-permute-start.7 = (f32[780]{0:T(1024)S(1)}, f32[780]{0:T(1024)S(1)}, u32[]{:S(2)}, u32[]{:S(2)}) collective-permute-start(f32[780]{0:T(1024)S(1)} %add_add_fusion.5), channel_id=1, source_target_pairs={{0,8},{1,9},{2,10},{3,11},{4,12},{5,13},{6,14},{7,15},{8,0},{9,1},... | collective-permute-start | bytes 9368 | tf_op jit(solution)/shard_map/ppermute | solution.py:138
  29.2 5.4 %collective-permute-start.8 = (f32[780]{0:T(1024)S(1)}, f32[780]{0:T(1024)S(1)}, u32[]{:S(2)}, u32[]{:S(2)}) collective-permute-start(f32[780]{0:T(1024)S(1)} %add_add_fusion.5), channel_id=1, source_target_pairs={{0,12},{1,13},{2,14},{3,15},{4,8},{5,9},{6,10},{7,11},{8,4},{9,5},... | collective-permute-start | bytes 9368 | tf_op jit(solution)/shard_map/ppermute | solution.py:138
  29.3 7.2 %collective-permute-start.2 = (f32[6,18,1,128]{3,2,1,0:T(1,128)S(1)}, f32[6,18,1,128]{3,2,1,0:T(1,128)S(1)}, u32[]{:S(2)}, u32[]{:S(2)}) collective-permute-start(f32[6,18,1,128]{3,2,1,0:T(1,128)S(1)} %broadcast_select_fusion.7), channel_id=1, source_target_pairs={{0,2},{2,0},{1,3},{3,1},{4,6},{6,4},{5,7},{7,5},{8,10},{10,8},{9,1... | collective-permute-start | bytes 165896 | tf_op jit(solution)/shard_map/ppermute | solution.py:20
  36.5 4.7 %copy-start.18 = (f32[6,18,1,128]{3,2,1,0:T(1,128)}, f32[6,18,1,128]{3,2,1,0:T(1,128)S(1)}, u32[]{:S(2)}) copy-start(f32[6,18,1,128]{3,2,1,0:T(1,128)S(1)} %get-tuple-element.75) | copy-start | bytes 165892
  36.5 4.7 %copy-start.20 = (f32[6,18,1,128]{3,2,1,0:T(1,128)}, f32[6,18,1,128]{3,2,1,0:T(1,128)S(1)}, u32[]{:S(2)}) copy-start(f32[6,18,1,128]{3,2,1,0:T(1,128)S(1)} %get-tuple-element.76) | copy-start | bytes 165892
  41.1 1.8 %collective-permute-start.9 = (f32[6,18,18,1]{2,1,3,0:T(8,128)S(1)}, f32[6,18,18,1]{2,1,3,0:T(8,128)S(1)}, u32[]{:S(2)}, u32[]{:S(2)}) collective-permute-start(f32[6,18,18,1]{2,1,3,0:T(8,128)S(1)} %copy.158), channel_id=1, source_target_pairs={{0,1},{1,0},{2,3},{3,2},{4,5},{5,4},{6,7},{7,6},{8,9},{9,8},{10,11... | collective-permute-start | bytes 23336 | tf_op jit(solution)/shard_map/ppermute | solution.py:20
  46.0 3.1 %copy-start.27 = (bf16[6,16,16,128]{3,2,1,0:T(8,128)(2,1)S(1)}, bf16[6,16,16,128]{3,2,1,0:T(8,128)(2,1)}, u32[]{:S(2)}) copy-start(bf16[6,16,16,128]{3,2,1,0:T(8,128)(2,1)} %param.10) | copy-start | bytes 1179652
  46.0 3.1 %copy-start.30 = (f32[6,18,17,128]{3,2,1,0:T(8,128)S(1)}, f32[6,18,17,128]{3,2,1,0:T(8,128)}, u32[]{:S(2)}) copy-start(f32[6,18,17,128]{3,2,1,0:T(8,128)} %get-tuple-element.56) | copy-start | bytes 2820100
  46.0 3.1 %copy-start.31 = (f32[6,18,17,128]{3,2,1,0:T(8,128)S(1)}, f32[6,18,17,128]{3,2,1,0:T(8,128)}, u32[]{:S(2)}) copy-start(f32[6,18,17,128]{3,2,1,0:T(8,128)} %get-tuple-element.57) | copy-start | bytes 2820100
  50.5 1.8 %copy-start.2 = (f32[1,16,16,128]{3,2,1,0:T(8,128)}, f32[1,16,16,128]{3,2,1,0:T(8,128)S(1)}, u32[]{:S(2)}) copy-start(f32[1,16,16,128]{3,2,1,0:T(8,128)S(1)} %get-tuple-element.34) | copy-start | bytes 393220
  52.4 1.4 %copy-start.38 = (f32[16,16,128]{2,1,0:T(8,128)S(1)}, f32[16,16,128]{2,1,0:T(8,128)}, u32[]{:S(2)}) copy-start(f32[16,16,128]{2,1,0:T(8,128)} %get-tuple-element.70) | copy-start | bytes 393220
  52.4 1.4 %copy-start.45 = (f32[3]{0:T(128)S(1)}, f32[3]{0:T(128)}, u32[]{:S(2)}) copy-start(f32[3]{0:T(128)} %get-tuple-element.89) | copy-start | bytes 40
  52.5 1.4 %copy-start.46 = (f32[3]{0:T(128)S(1)}, f32[3]{0:T(128)}, u32[]{:S(2)}) copy-start(f32[3]{0:T(128)} %get-tuple-element.90) | copy-start | bytes 40
  54.8 9.6 %copy-start.12 = (f32[32768]{0:T(1024)S(1)}, f32[32768]{0:T(1024)}, u32[]{:S(2)}) copy-start(f32[32768]{0:T(1024)} %copy-done.10) | copy-start | bytes 393220
  54.9 6.2 %collective-permute-start.10 = (f32[6,1,16,128]{3,2,1,0:T(8,128)S(1)}, f32[6,1,16,128]{3,2,1,0:T(8,128)S(1)}, u32[]{:S(2)}, u32[]{:S(2)}) collective-permute-start(f32[6,1,16,128]{3,2,1,0:T(8,128)S(1)} %get-tuple-element.61), channel_id=1, source_target_pairs={{4,0},{8,4},{12,8},{5,1},{9,5},{13,9},{6,2},{10,6},{14,10},{7,3},{... | collective-permute-start | bytes 147464 | tf_op jit(solution)/shard_map/ppermute | solution.py:28
  56.3 6.3 %collective-permute-start.11 = (f32[6,1,16,128]{3,2,1,0:T(8,128)S(1)}, f32[6,1,16,128]{3,2,1,0:T(8,128)S(1)}, u32[]{:S(2)}, u32[]{:S(2)}) collective-permute-start(f32[6,1,16,128]{3,2,1,0:T(8,128)S(1)} %get-tuple-element.60), channel_id=1, source_target_pairs={{0,4},{4,8},{8,12},{1,5},{5,9},{9,13},{2,6},{6,10},{10,14},{3,7},{... | collective-permute-start | bytes 147464 | tf_op jit(solution)/shard_map/ppermute | solution.py:27
  62.6 4.2 %collective-permute-start.12 = (f32[6,18,1,128]{3,2,1,0:T(1,128)S(1)}, f32[6,18,1,128]{3,2,1,0:T(1,128)S(1)}, u32[]{:S(2)}, u32[]{:S(2)}) collective-permute-start(f32[6,18,1,128]{3,2,1,0:T(1,128)S(1)} %broadcast_select_fusion.4), channel_id=1, source_target_pairs={{0,2},{2,0},{1,3},{3,1},{4,6},{6,4},{5,7},{7,5},{8,10},{10,8},{9,1... | collective-permute-start | bytes 165896 | tf_op jit(solution)/shard_map/ppermute | solution.py:20
  66.9 4.7 %copy-start.22 = (f32[6,18,1,128]{3,2,1,0:T(1,128)}, f32[6,18,1,128]{3,2,1,0:T(1,128)S(1)}, u32[]{:S(2)}) copy-start(f32[6,18,1,128]{3,2,1,0:T(1,128)S(1)} %get-tuple-element.73) | copy-start | bytes 165892
  67.0 4.7 %copy-start.24 = (f32[6,18,1,128]{3,2,1,0:T(1,128)}, f32[6,18,1,128]{3,2,1,0:T(1,128)S(1)}, u32[]{:S(2)}) copy-start(f32[6,18,1,128]{3,2,1,0:T(1,128)S(1)} %get-tuple-element.74) | copy-start | bytes 165892
  71.6 1.8 %collective-permute-start.13 = (f32[6,18,18,1]{2,1,3,0:T(8,128)S(1)}, f32[6,18,18,1]{2,1,3,0:T(8,128)S(1)}, u32[]{:S(2)}, u32[]{:S(2)}) collective-permute-start(f32[6,18,18,1]{2,1,3,0:T(8,128)S(1)} %copy.167), channel_id=1, source_target_pairs={{0,1},{1,0},{2,3},{3,2},{4,5},{5,4},{6,7},{7,6},{8,9},{9,8},{10,11... | collective-permute-start | bytes 23336 | tf_op jit(solution)/shard_map/ppermute | solution.py:20
  76.4 3.6 %copy-start.28 = (f32[6,18,17,128]{3,2,1,0:T(8,128)S(1)}, f32[6,18,17,128]{3,2,1,0:T(8,128)}, u32[]{:S(2)}) copy-start(f32[6,18,17,128]{3,2,1,0:T(8,128)} %get-tuple-element.54) | copy-start | bytes 2820100
  76.4 3.7 %copy-start.29 = (f32[6,18,17,128]{3,2,1,0:T(8,128)S(1)}, f32[6,18,17,128]{3,2,1,0:T(8,128)}, u32[]{:S(2)}) copy-start(f32[6,18,17,128]{3,2,1,0:T(8,128)} %get-tuple-element.55) | copy-start | bytes 2820100
  83.3 1.4 %copy-start.17 = (f32[6,16,16,128]{3,2,1,0:T(8,128)S(1)}, f32[6,16,16,128]{3,2,1,0:T(8,128)}, u32[]{:S(2)}) copy-start(f32[6,16,16,128]{3,2,1,0:T(8,128)} %copy-done.16) | copy-start | bytes 2359300
  83.3 1.4 %copy-start.34 = (f32[16,16,128]{2,1,0:T(8,128)S(1)}, f32[16,16,128]{2,1,0:T(8,128)}, u32[]{:S(2)}) copy-start(f32[16,16,128]{2,1,0:T(8,128)} %copy-done.32) | copy-start | bytes 393220
  83.3 1.5 %copy-start.37 = (f32[16,16,128]{2,1,0:T(8,128)S(1)}, f32[16,16,128]{2,1,0:T(8,128)}, u32[]{:S(2)}) copy-start(f32[16,16,128]{2,1,0:T(8,128)} %copy-done.35) | copy-start | bytes 393220
  83.3 1.5 %copy-start.39 = (f32[16,16,128]{2,1,0:T(8,128)S(1)}, f32[16,16,128]{2,1,0:T(8,128)}, u32[]{:S(2)}) copy-start(f32[16,16,128]{2,1,0:T(8,128)} %get-tuple-element.70) | copy-start | bytes 393220
  86.2 2.1 %copy-start.44 = (f32[6]{0:T(128)S(1)}, f32[6]{0:T(128)}, u32[]{:S(2)}) copy-start(f32[6]{0:T(128)} %fusion.9) | copy-start | bytes 76
  86.2 16.5 %copy-start.6 = (f32[3,16,16,128]{3,2,1,0:T(8,128)S(1)}, f32[3,16,16,128]{3,2,1,0:T(8,128)}, u32[]{:S(2)}) copy-start(f32[3,16,16,128]{3,2,1,0:T(8,128)} %copy-done.4) | copy-start | bytes 1179652
  86.2 16.5 %copy-start.9 = (f32[3,16,16,128]{3,2,1,0:T(8,128)S(1)}, f32[3,16,16,128]{3,2,1,0:T(8,128)}, u32[]{:S(2)}) copy-start(f32[3,16,16,128]{3,2,1,0:T(8,128)} %copy-done.7) | copy-start | bytes 1179652
  88.3 2.4 %collective-permute-start.14 = (f32[134]{0:T(256)S(1)}, f32[134]{0:T(256)S(1)}, u32[]{:S(2)}, u32[]{:S(2)}) collective-permute-start(f32[134]{0:T(256)S(1)} %pad_maximum_fusion.19), channel_id=1, source_target_pairs={{0,1},{1,0},{2,3},{3,2},{4,5},{5,4},{6,7},{7,6},{8,9},{9,8},{10,11... | collective-permute-start | bytes 1616 | tf_op jit(solution)/shard_map/ppermute | solution.py:138
  88.8 3.6 %collective-permute-start.15 = (f32[134]{0:T(256)S(1)}, f32[134]{0:T(256)S(1)}, u32[]{:S(2)}, u32[]{:S(2)}) collective-permute-start(f32[134]{0:T(256)S(1)} %pad_maximum_fusion.19), channel_id=1, source_target_pairs={{0,2},{1,3},{2,0},{3,1},{4,6},{5,7},{6,4},{7,5},{8,10},{9,11},{10,... | collective-permute-start | bytes 1616 | tf_op jit(solution)/shard_map/ppermute | solution.py:138
  90.7 3.0 %collective-permute-start.16 = (f32[134]{0:T(256)S(1)}, f32[134]{0:T(256)S(1)}, u32[]{:S(2)}, u32[]{:S(2)}) collective-permute-start(f32[134]{0:T(256)S(1)} %pad_maximum_fusion.19), channel_id=1, source_target_pairs={{0,3},{1,2},{2,1},{3,0},{4,7},{5,6},{6,5},{7,4},{8,11},{9,10},{10,... | collective-permute-start | bytes 1616 | tf_op jit(solution)/shard_map/ppermute | solution.py:138
  93.8 5.0 %collective-permute-start.17 = (f32[134]{0:T(256)S(1)}, f32[134]{0:T(256)S(1)}, u32[]{:S(2)}, u32[]{:S(2)}) collective-permute-start(f32[134]{0:T(256)S(1)} %add_add_fusion.7), channel_id=1, source_target_pairs={{0,4},{1,5},{2,6},{3,7},{4,0},{5,1},{6,2},{7,3},{8,12},{9,13},{10,... | collective-permute-start | bytes 1616 | tf_op jit(solution)/shard_map/ppermute | solution.py:138
  96.1 4.5 %collective-permute-start.18 = (f32[134]{0:T(256)S(1)}, f32[134]{0:T(256)S(1)}, u32[]{:S(2)}, u32[]{:S(2)}) collective-permute-start(f32[134]{0:T(256)S(1)} %add_add_fusion.7), channel_id=1, source_target_pairs={{0,8},{1,9},{2,10},{3,11},{4,12},{5,13},{6,14},{7,15},{8,0},{9,1},... | collective-permute-start | bytes 1616 | tf_op jit(solution)/shard_map/ppermute | solution.py:138
  96.1 5.4 %collective-permute-start.19 = (f32[134]{0:T(256)S(1)}, f32[134]{0:T(256)S(1)}, u32[]{:S(2)}, u32[]{:S(2)}) collective-permute-start(f32[134]{0:T(256)S(1)} %add_add_fusion.7), channel_id=1, source_target_pairs={{0,12},{1,13},{2,14},{3,15},{4,8},{5,9},{6,10},{7,11},{8,4},{9,5},... | collective-permute-start | bytes 1616 | tf_op jit(solution)/shard_map/ppermute | solution.py:138
  (21 other events, 21.1 us)

commit v7 on v5

--- a/solution.py
+++ b/solution.py
@@ -12,7 +12,15 @@
         peers, length = (lax.axis_size(axis), array.shape[dim])
         last = lax.slice_in_dim(array, length - width, length, axis=dim)
         initial = lax.slice_in_dim(array, 0, width, axis=dim)
-        if peers == 2:
+        if peers == 2 and dim == array.ndim - 1:
+            first = lax.axis_index(axis) == 0
+            got = lax.ppermute(array, axis, [(0, 1), (1, 0)])
+            got_last = lax.slice_in_dim(got, length - width, length, axis=dim)
+            got_initial = lax.slice_in_dim(got, 0, width, axis=dim)
+            zero = jnp.zeros_like(got_last)
+            before = jnp.where(first, zero, got_last)
+            after = jnp.where(first, got_initial, zero)
+        elif peers == 2:
             first = lax.axis_index(axis) == 0
             got = lax.ppermute(jnp.where(first, last, initial), axis, [(0, 1), (1, 0)])
             zero = jnp.zeros_like(got)

time: 103 us -> 101 us (0.981)
  local copies, waits for them, and re-layouts: 25.7 us -> 13.3 us
  other arithmetic: 28.4 us -> 35.2 us
  waiting for transfers between devices: 17.2 us -> 21.1 us
    unnamed x96 -> x49, local copies, waits for them, and re-layouts: 10.4 us -> 2.03 us
    select_n x6 -> x0, local copies, waits for them, and re-layouts: 4.87 us -> none  [the longest x2 3.31 us: with_halo(): before = jnp.where(first, zero, got)]
    ppermute x0 -> x2, waiting for transfers between devices: none -> 3.83 us  [with_halo(): got = lax.ppermute(array, axis, [(0, 1), (1, 0)])]
    select_n x2, other arithmetic: 1.29 us -> 4.35 us  [with_halo(): after = jnp.where(first, got_initial, zero)]
    slice x2 -> x0, local copies, waits for them, and re-layouts: 3.04 us -> none  [with_halo(): initial = lax.slice_in_dim(array, 0, width, axis=dim)]
    concatenate x6, other arithmetic: 10.5 us -> 8.68 us  [with_halo(): array = jnp.concatenate([before, array, after], axis=dim)]
    dynamic_update_slice x2, local copies, waits for them, and re-layouts: 0.84 us -> 2.5 us  [block_sums(): return lax.dynamic_update_slice(grid, local, (0,) * len(lead) + grid_at)]
    reduce_sum x4, other arithmetic: 0.63 us -> 2.15 us  [block_sums(): local = local.sum(axis=(-4, -2, -1))]
  transfers between devices with their start and end apart: 20 -> 20, of which waited for: 10 -> 12; matrix products, arithmetic and copies ran while one was open for 12% -> 9% of each run, Pallas kernels for 0% -> 0%
where the time goes in v7:
time: 101 us; the launch traced here: 100 us
  other arithmetic  35.2 us (35%)
  starting transfers between devices  28.5 us (28%)
  waiting for transfers between devices  21.1 us (21%)
  local copies, waits for them, and re-layouts  13.3 us (13%)
  between operations  2 us (2%)
    ppermute x12, starting transfers between devices, group_sum(): lax.ppermute(value, axes, [(i, i ^ m * stride) for i in range(size)])  12.9 us
    ppermute x12, waiting for transfers between devices, group_sum(): lax.ppermute(value, axes, [(i, i ^ m * stride) for i in range(size)])  12.2 us
    ppermute x2, starting transfers between devices, with_halo(): before = lax.ppermute(last, axis, up)  10.3 us
    concatenate x6, other arithmetic, with_halo(): array = jnp.concatenate([before, array, after], axis=dim)  8.68 us
    add x12, other arithmetic, navier(): result.append(shear * laplace[channel] + (lame_first + shear) * divergence)  5.61 us
    select_n x2, other arithmetic, with_halo(): after = jnp.where(first, got_initial, zero)  4.35 us
    ppermute x2, waiting for transfers between devices, with_halo(): got = lax.ppermute(array, axis, [(0, 1), (1, 0)])  3.83 us
    ppermute x2, waiting for transfers between devices, with_halo(): got = lax.ppermute(jnp.where(first, last, initial), axis, [(0, 1), (1, 0)])  3.51 us
  transfers between devices with their start and end apart: 20, of which 12 were waited for; matrix products, arithmetic and copies ran while one was open for 9% of the time, Pallas kernels for 0%

profile of v7, /device:TPU:0, one launch (start us, length us, event | category | flops | bytes accessed | tf_op | source)
XLA Modules:
  0.0 100.0 jit_solution(6614971633527542874)
XLA Ops:
  0.6 0.8 fusion.110
  1.4 1.3 %collective-permute-start = (f32[6,1,16,128]{3,2,1,0:T(8,128)S(1)}, f32[6,1,16,128]{3,2,1,0:T(8,128)S(1)}, u32[]{:S(2)}, u32[]{:S(2)}) collective-permute-start(f32[6,1,16,128]{3,2,1,0:T(8,128)S(1)} %get-tuple-element.57), channel_id=1, source_target_pairs={{4,0},{8,4},{12,8},{5,1},{9,5},{13,9},{6,2},{10,6},{14,10},{7,3},{... | collective-permute-start | bytes 147464 | tf_op jit(solution)/shard_map/ppermute | solution.py:33
  2.7 5.6 %collective-permute-start.1 = (f32[6,1,16,128]{3,2,1,0:T(8,128)S(1)}, f32[6,1,16,128]{3,2,1,0:T(8,128)S(1)}, u32[]{:S(2)}, u32[]{:S(2)}) collective-permute-start(f32[6,1,16,128]{3,2,1,0:T(8,128)S(1)} %get-tuple-element.56), channel_id=1, source_target_pairs={{0,4},{4,8},{8,12},{1,5},{5,9},{9,13},{2,6},{6,10},{10,14},{3,7},{... | collective-permute-start | bytes 147464 | tf_op jit(solution)/shard_map/ppermute | solution.py:32
  8.3 0.8 slice_bitcast_fusion.2
  9.0 0.8 select_reduce_fusion.1
  9.9 1.1 %convert_element_type.12 = f32[6,16,16,128]{3,2,1,0:T(8,128)S(1)} convert(bf16[6,16,16,128]{3,2,1,0:T(8,128)(2,1)} %param.10) | non-fusion elementwise | flops 196608 | bytes 1179648 | tf_op jit(solution)/shard_map/convert_element_type | solution.py:206
  11.0 2.0 %collective-permute-start.2 = (f32[6,18,1,128]{3,2,1,0:T(1,128)S(1)}, f32[6,18,1,128]{3,2,1,0:T(1,128)S(1)}, u32[]{:S(2)}, u32[]{:S(2)}) collective-permute-start(f32[6,18,1,128]{3,2,1,0:T(1,128)S(1)} %broadcast_select_fusion.5), channel_id=1, source_target_pairs={{0,2},{2,0},{1,3},{3,1},{4,6},{6,4},{5,7},{7,5},{8,10},{10,8},{9,1... | collective-permute-start | bytes 165896 | tf_op jit(solution)/shard_map/ppermute | solution.py:25
  13.6 0.9 reshape.125
  15.7 1.1 %convert_element_type.15 = f32[6,16,16,128]{3,2,1,0:T(8,128)S(1)} convert(bf16[6,16,16,128]{3,2,1,0:T(8,128)(2,1)} %param.11) | non-fusion elementwise | flops 196608 | bytes 1179648 | tf_op jit(solution)/shard_map/convert_element_type | solution.py:198
  16.9 1.3 %pad_maximum_fusion.3 = f32[6,18,18,128]{3,2,1,0:T(8,128)} fusion(f32[6,18,1,128]{3,2,1,0:T(1,128)S(1)} %get-tuple-element.64, f32[6,1,16,128]{3,2,1,0:T(8,128)S(1)} %collective-permute-done, f32[6,16,16,128]{3,2,1,0:T(8,128)S(1)} %convert_element_type.12, f32[6,1,16,128]{3,2,1,0:T(8,128)S(1)} %collective-permute-done.1, ...), kind=kLoop, calls=%fused_computation.11 | loop fusion | flops 995328 | bytes 1990656 | tf_op jit(solution)/shard_map/concatenate | solution.py:34
  18.2 1.5 %scatter_custom_fusion = f32[32768]{0:T(1024)S(1)} fusion(s32[256]{0:T(256)S(1)} %bitcast.21, f32[256]{0:T(256)S(1)} %broadcast.108, f32[]{:T(128)} %constant.18.clone.1), kind=kCustom, calls=%fused_computation.247 | custom fusion | bytes 131076 | tf_op jit(solution)/shard_map/scatter | solution.py:176
  20.1 1.5 %collective-permute-done.3 = f32[6,18,18,128]{3,2,1,0:T(8,128)} collective-permute-done((f32[6,18,18,128]{3,2,1,0:T(8,128)}, f32[6,18,18,128]{3,2,1,0:T(8,128)}, u32[]{:S(2)}, u32[]{:S(2)}) %collective-permute-start.3) | collective-permute-done | bytes 995360 | tf_op jit(solution)/shard_map/ppermute | solution.py:17
  21.6 2.2 %slice_select_fusion.3 = (f32[6,18,18,1]{3,2,1,0:T(8,128)S(1)}, f32[6,18,18,1]{3,2,1,0:T(8,128)S(1)}) fusion(f32[6,18,18,128]{3,2,1,0:T(8,128)} %collective-permute-done.3, pred[]{:T(512)S(6)} %eq.19), kind=kLoop, calls=%fused_computation.8 | loop fusion | flops 3888 | bytes 31105 | tf_op jit(solution)/shard_map/jit(_where)/select_n | solution.py:22
  23.8 2.1 %pad_maximum_fusion = (f32[6,18,18,129]{3,2,1,0:T(8,128)S(1)}, f32[6,18,18,129]{3,2,1,0:T(8,128)S(1)}) fusion(f32[6,18,18,1]{3,2,1,0:T(8,128)S(1)} %get-tuple-element.37, f32[6,18,1,128]{3,2,1,0:T(1,128)S(1)} %get-tuple-element.64, f32[6,1,16,128]{3,2,1,0:T(8,128)S(1)} %collective-permute-done, f32[6,16,16,128]{3,2,1,0:T(8,128)S(1)} %convert_element_type.12, ...), kind=kLoop, calls=%fused_computation.1 | loop fusion | flops 2507760 | bytes 3017088 | tf_op jit(solution)/shard_map/concatenate | solution.py:34
  29.7 1.3 %divide_add_fusion.3 = (f32[3,16,16,128]{3,2,1,0:T(8,128)}, f32[3,16,16,128]{3,2,1,0:T(8,128)S(1)}, f32[3,16,16,128]{3,2,1,0:T(8,128)S(1)}) fusion(f32[6,16,16,128]{3,2,1,0:T(8,128)S(1)} %convert_element_type.12, f32[16,16,128]{2,1,0:T(8,128)S(1)} %get-tuple-element.60, f32[16,16,128]{2,1,0:T(8,128)S(1)} %get-tuple-element.59, f32[3]{0:T(128)S(1)} %get-tuple-element.70, ...), kind=kLoop, calls=%fused_computation.76 | loop fusion | flops 3833856 | bytes 4063256 | tf_op jit(solution)/shard_map/add | solution.py:108
  31.0 1.8 %fusion.105 = (f32[3]{0:T(128)}, f32[3,16,16,128]{3,2,1,0:T(8,128)S(1)}, f32[3]{0:T(128)}, f32[3,16,16,128]{3,2,1,0:T(8,128)S(1)}, f32[3,16,16,128]{3,2,1,0:T(8,128)}) fusion(f32[3]{0:T(128)S(1)} %get-tuple-element.70, f32[16,16,128]{2,1,0:T(8,128)S(1)} %get-tuple-element.60, f32[3]{0:T(128)S(1)} %get-tuple-element.69, f32[16,16,128]{2,1,0:T(8,128)S(1)} %bitcast.18, ...), kind=kLoop, calls=%fused_computation.278 | loop fusion | flops 2359290 | bytes 2883632 | tf_op jit(solution)/shard_map/reduce_sum | solution.py:211
  33.0 0.9 maximum_reduce_fusion
  33.9 1.6 %reduce_sum.110 = f32[6,4,4,4,4]{4,3,2,1,0:T(4,128)} reshape(f32[6,16,16]{2,1,0:T(8,128)} %maximum_reduce_fusion) | data formatting | bytes 12288 | tf_op jit(solution)/shard_map/reduce_sum | solution.py:194
  35.5 1.1 %reduce_sum.111 = f32[6,4,4]{2,1,0:T(4,128)S(1)} reduce(f32[6,4,4,4,4]{4,3,2,1,0:T(4,128)} %reduce_sum.110, f32[]{:T(128)} %constant.18.clone.1), dimensions={2,4}, to_apply=%region_7.8 | reduce | flops 1440 | bytes 6532 | tf_op jit(solution)/shard_map/reduce_sum | solution.py:194
  37.2 2.2 %dynamic_update_slice.6 = f32[6,16,8]{2,1,0:T(8,128)} dynamic-update-slice(f32[6,16,8]{2,1,0:T(8,128)} %broadcast_in_dim.34, f32[6,4,4]{2,1,0:T(4,128)S(1)} %reduce_sum.111, s32[]{:T(128)} %constant.21.clone.1, s32[]{:T(128)S(6)} %select_n.83, s32[]{:T(128)S(6)} %select_n.84) | dynamic-update-slice | bytes 772 | tf_op jit(solution)/shard_map/dynamic_update_slice | solution.py:196
  39.4 0.9 reshape.126
  40.3 1.3 %fusion.9 = (f32[6]{0:T(128)S(1)}, f32[6]{0:T(128)S(1)}) fusion(f32[3,16,16,128]{3,2,1,0:T(8,128)} %get-tuple-element.55, f32[3,16,16,128]{3,2,1,0:T(8,128)S(1)} %copy-done.8, f32[16,16,128]{2,1,0:T(8,128)S(1)} %bitcast.19, bf16[6,16,16,128]{3,2,1,0:T(8,128)(2,1)S(1)} %copy-done.7), kind=kLoop, calls=%fused_computation.41 | loop fusion | flops 1179636 | bytes 1310768 | tf_op jit(solution)/shard_map/reduce_sum | solution.py:225
  41.6 0.8 pad_maximum_fusion.19
  42.5 1.2 %collective-permute-start.5 = (f32[780]{0:T(1024)S(1)}, f32[780]{0:T(1024)S(1)}, u32[]{:S(2)}, u32[]{:S(2)}) collective-permute-start(f32[780]{0:T(1024)S(1)} %pad_maximum_fusion.19), channel_id=1, source_target_pairs={{0,2},{1,3},{2,0},{3,1},{4,6},{5,7},{6,4},{7,5},{8,10},{9,11},{10,... | collective-permute-start | bytes 9368 | tf_op jit(solution)/shard_map/ppermute | solution.py:143
  44.3 1.9 %collective-permute-done.5 = f32[780]{0:T(1024)S(1)} collective-permute-done((f32[780]{0:T(1024)S(1)}, f32[780]{0:T(1024)S(1)}, u32[]{:S(2)}, u32[]{:S(2)}) %collective-permute-start.5) | collective-permute-done | bytes 3152 | tf_op jit(solution)/shard_map/ppermute | solution.py:143
  46.8 1.8 %collective-permute-start.7 = (f32[780]{0:T(1024)S(1)}, f32[780]{0:T(1024)S(1)}, u32[]{:S(2)}, u32[]{:S(2)}) collective-permute-start(f32[780]{0:T(1024)S(1)} %add_add_fusion.5), channel_id=1, source_target_pairs={{0,4},{1,5},{2,6},{3,7},{4,0},{5,1},{6,2},{7,3},{8,12},{9,13},{10,... | collective-permute-start | bytes 9368 | tf_op jit(solution)/shard_map/ppermute | solution.py:143
  48.6 2.1 %collective-permute-start.8 = (f32[780]{0:T(1024)S(1)}, f32[780]{0:T(1024)S(1)}, u32[]{:S(2)}, u32[]{:S(2)}) collective-permute-start(f32[780]{0:T(1024)S(1)} %add_add_fusion.5), channel_id=1, source_target_pairs={{0,8},{1,9},{2,10},{3,11},{4,12},{5,13},{6,14},{7,15},{8,0},{9,1},... | collective-permute-start | bytes 9368 | tf_op jit(solution)/shard_map/ppermute | solution.py:143
  51.2 1.9 %collective-permute-done.8 = f32[780]{0:T(1024)S(1)} collective-permute-done((f32[780]{0:T(1024)S(1)}, f32[780]{0:T(1024)S(1)}, u32[]{:S(2)}, u32[]{:S(2)}) %collective-permute-start.8) | collective-permute-done | bytes 3152 | tf_op jit(solution)/shard_map/ppermute | solution.py:143
  53.1 3.0 %collective-permute-done.9 = f32[780]{0:T(1024)S(1)} collective-permute-done((f32[780]{0:T(1024)S(1)}, f32[780]{0:T(1024)S(1)}, u32[]{:S(2)}, u32[]{:S(2)}) %collective-permute-start.9) | collective-permute-done | bytes 3152 | tf_op jit(solution)/shard_map/ppermute | solution.py:143
  56.4 1.3 %collective-permute-start.10 = (f32[6,1,16,128]{3,2,1,0:T(8,128)S(1)}, f32[6,1,16,128]{3,2,1,0:T(8,128)S(1)}, u32[]{:S(2)}, u32[]{:S(2)}) collective-permute-start(f32[6,1,16,128]{3,2,1,0:T(8,128)S(1)} %get-tuple-element.52), channel_id=1, source_target_pairs={{4,0},{8,4},{12,8},{5,1},{9,5},{13,9},{6,2},{10,6},{14,10},{7,3},{... | collective-permute-start | bytes 147464 | tf_op jit(solution)/shard_map/ppermute | solution.py:33
  57.7 4.7 %collective-permute-start.11 = (f32[6,1,16,128]{3,2,1,0:T(8,128)S(1)}, f32[6,1,16,128]{3,2,1,0:T(8,128)S(1)}, u32[]{:S(2)}, u32[]{:S(2)}) collective-permute-start(f32[6,1,16,128]{3,2,1,0:T(8,128)S(1)} %get-tuple-element.51), channel_id=1, source_target_pairs={{0,4},{4,8},{8,12},{1,5},{5,9},{9,13},{2,6},{6,10},{10,14},{3,7},{... | collective-permute-start | bytes 147464 | tf_op jit(solution)/shard_map/ppermute | solution.py:32
  62.4 1.5 %collective-permute-done.11 = f32[6,1,16,128]{3,2,1,0:T(8,128)S(1)} collective-permute-done((f32[6,1,16,128]{3,2,1,0:T(8,128)S(1)}, f32[6,1,16,128]{3,2,1,0:T(8,128)S(1)}, u32[]{:S(2)}, u32[]{:S(2)}) %collective-permute-start.11) | collective-permute-done | bytes 49184 | tf_op jit(solution)/shard_map/ppermute | solution.py:32
  64.8 3.5 %collective-permute-done.12 = f32[6,18,1,128]{3,2,1,0:T(1,128)S(1)} collective-permute-done((f32[6,18,1,128]{3,2,1,0:T(1,128)S(1)}, f32[6,18,1,128]{3,2,1,0:T(1,128)S(1)}, u32[]{:S(2)}, u32[]{:S(2)}) %collective-permute-start.12) | collective-permute-done | bytes 55328 | tf_op jit(solution)/shard_map/ppermute | solution.py:25
  69.0 1.3 %pad_maximum_fusion.5 = f32[6,18,18,128]{3,2,1,0:T(8,128)} fusion(f32[6,18,1,128]{3,2,1,0:T(1,128)S(1)} %get-tuple-element.62, f32[6,1,16,128]{3,2,1,0:T(8,128)S(1)} %collective-permute-done.10, f32[3,16,16,128]{3,2,1,0:T(8,128)S(1)} %get-tuple-element.49, f32[3,16,16,128]{3,2,1,0:T(8,128)S(1)} %get-tuple-element.50, ...), kind=kLoop, calls=%fused_computation.14 | loop fusion | flops 1244160 | bytes 1990656 | tf_op jit(solution)/shard_map/concatenate | solution.py:34
  70.3 1.1 %pad_maximum_fusion.4 = (f32[6,18,17,128]{3,2,1,0:T(8,128)S(1)}, f32[6,18,17,128]{3,2,1,0:T(8,128)S(1)}) fusion(f32[6,18,1,128]{3,2,1,0:T(1,128)} %copy-done.2, f32[6,1,16,128]{3,2,1,0:T(8,128)S(1)} %collective-permute-done.10, f32[3,16,16,128]{3,2,1,0:T(8,128)S(1)} %get-tuple-element.49, f32[3,16,16,128]{3,2,1,0:T(8,128)S(1)} %get-tuple-element.50, ...), kind=kLoop, calls=%fused_computation.12 | loop fusion | flops 1880064 | bytes 2875392 | tf_op jit(solution)/shard_map/concatenate | solution.py:34
  71.4 2.3 %collective-permute-done.13 = f32[6,18,18,128]{3,2,1,0:T(8,128)} collective-permute-done((f32[6,18,18,128]{3,2,1,0:T(8,128)}, f32[6,18,18,128]{3,2,1,0:T(8,128)}, u32[]{:S(2)}, u32[]{:S(2)}) %collective-permute-start.13) | collective-permute-done | bytes 995360 | tf_op jit(solution)/shard_map/ppermute | solution.py:17
  73.7 2.2 %slice_select_fusion.1 = (f32[6,18,18,1]{3,2,1,0:T(8,128)S(1)}, f32[6,18,18,1]{3,2,1,0:T(8,128)S(1)}) fusion(f32[6,18,18,128]{3,2,1,0:T(8,128)} %collective-permute-done.13, pred[]{:T(512)S(6)} %eq.19), kind=kLoop, calls=%fused_computation.6 | loop fusion | flops 3888 | bytes 31105 | tf_op jit(solution)/shard_map/jit(_where)/select_n | solution.py:22
  75.9 2.7 %pad_maximum_fusion.1 = (f32[6,18,18,129]{3,2,1,0:T(8,128)S(1)}, f32[6,18,18,129]{3,2,1,0:T(8,128)S(1)}) fusion(f32[6,18,18,1]{3,2,1,0:T(8,128)S(1)} %get-tuple-element.35, f32[6,18,1,128]{3,2,1,0:T(1,128)S(1)} %copy-done.3, f32[6,1,16,128]{3,2,1,0:T(8,128)S(1)} %collective-permute-done.10, f32[3,16,16,128]{3,2,1,0:T(8,128)S(1)} %get-tuple-element.49, ...), kind=kLoop, calls=%fused_computation.3 | loop fusion | flops 3009312 | bytes 3017088 | tf_op jit(solution)/shard_map/concatenate | solution.py:34
  82.4 1.6 %subtract_reduce_fusion = (f32[16,16,128]{2,1,0:T(8,128)S(1)}, f32[3,16,16,128]{3,2,1,0:T(8,128)}, f32[3,16,16,128]{3,2,1,0:T(8,128)}) fusion(f32[6,16,16,128]{3,2,1,0:T(8,128)S(1)} %convert_element_type.15, f32[3,16,16,128]{3,2,1,0:T(8,128)S(1)} %get-tuple-element.50, f32[16,16,128]{2,1,0:T(8,128)S(1)} %copy-done.14, ...), kind=kLoop, calls=%fused_computation.64 | loop fusion | flops 5275648 | bytes 4587544 | tf_op jit(solution)/shard_map/reduce_sum | solution.py:234
  85.0 0.8 collective-permute-start.15
  85.8 0.9 collective-permute-start.16
  86.7 1.9 %collective-permute-done.15 = f32[134]{0:T(256)S(1)} collective-permute-done((f32[134]{0:T(256)S(1)}, f32[134]{0:T(256)S(1)}, u32[]{:S(2)}, u32[]{:S(2)}) %collective-permute-start.15) | collective-permute-done | bytes 568 | tf_op jit(solution)/shard_map/ppermute | solution.py:143
  88.9 2.3 %collective-permute-start.17 = (f32[134]{0:T(256)S(1)}, f32[134]{0:T(256)S(1)}, u32[]{:S(2)}, u32[]{:S(2)}) collective-permute-start(f32[134]{0:T(256)S(1)} %add_add_fusion.7), channel_id=1, source_target_pairs={{0,4},{1,5},{2,6},{3,7},{4,0},{5,1},{6,2},{7,3},{8,12},{9,13},{10,... | collective-permute-start | bytes 1616 | tf_op jit(solution)/shard_map/ppermute | solution.py:143
  91.2 2.4 %collective-permute-start.19 = (f32[134]{0:T(256)S(1)}, f32[134]{0:T(256)S(1)}, u32[]{:S(2)}, u32[]{:S(2)}) collective-permute-start(f32[134]{0:T(256)S(1)} %add_add_fusion.7), channel_id=1, source_target_pairs={{0,12},{1,13},{2,14},{3,15},{4,8},{5,9},{6,10},{7,11},{8,4},{9,5},... | collective-permute-start | bytes 1616 | tf_op jit(solution)/shard_map/ppermute | solution.py:143
  93.9 1.8 %collective-permute-done.18 = f32[134]{0:T(256)S(1)} collective-permute-done((f32[134]{0:T(256)S(1)}, f32[134]{0:T(256)S(1)}, u32[]{:S(2)}, u32[]{:S(2)}) %collective-permute-start.18) | collective-permute-done | bytes 568 | tf_op jit(solution)/shard_map/ppermute | solution.py:143
  95.7 0.9 collective-permute-done.19
  97.8 1.3 %subtract_add_fusion = (f32[3,16,16,128]{3,2,1,0:T(8,128)S(1)}, f32[3,16,16,128]{3,2,1,0:T(8,128)S(1)}) fusion(f32[3,16,16,128]{3,2,1,0:T(8,128)} %get-tuple-element.13, f32[3,16,16,128]{3,2,1,0:T(8,128)S(1)} %get-tuple-element.54, f32[3,16,16,128]{3,2,1,0:T(8,128)S(1)} %get-tuple-element.23, f32[3]{0:T(128)S(1)} %get-tuple-element.74, ...), kind=kLoop, calls=%fused_computation.63 | loop fusion | flops 786432 | bytes 2359320 | tf_op jit(solution)/shard_map/add | solution.py:128
  99.1 1.0 pad_maximum_fusion.13
  (126 shorter events, 16.0 us)
Async XLA Ops:
  1.4 9.5 %collective-permute-start = (f32[6,1,16,128]{3,2,1,0:T(8,128)S(1)}, f32[6,1,16,128]{3,2,1,0:T(8,128)S(1)}, u32[]{:S(2)}, u32[]{:S(2)}) collective-permute-start(f32[6,1,16,128]{3,2,1,0:T(8,128)S(1)} %get-tuple-element.57), channel_id=1, source_target_pairs={{4,0},{8,4},{12,8},{5,1},{9,5},{13,9},{6,2},{10,6},{14,10},{7,3},{... | collective-permute-start | bytes 147464 | tf_op jit(solution)/shard_map/ppermute | solution.py:33
  2.7 8.3 %collective-permute-start.1 = (f32[6,1,16,128]{3,2,1,0:T(8,128)S(1)}, f32[6,1,16,128]{3,2,1,0:T(8,128)S(1)}, u32[]{:S(2)}, u32[]{:S(2)}) collective-permute-start(f32[6,1,16,128]{3,2,1,0:T(8,128)S(1)} %get-tuple-element.56), channel_id=1, source_target_pairs={{0,4},{4,8},{8,12},{1,5},{5,9},{9,13},{2,6},{6,10},{10,14},{3,7},{... | collective-permute-start | bytes 147464 | tf_op jit(solution)/shard_map/ppermute | solution.py:32
  11.0 5.8 %collective-permute-start.2 = (f32[6,18,1,128]{3,2,1,0:T(1,128)S(1)}, f32[6,18,1,128]{3,2,1,0:T(1,128)S(1)}, u32[]{:S(2)}, u32[]{:S(2)}) collective-permute-start(f32[6,18,1,128]{3,2,1,0:T(1,128)S(1)} %broadcast_select_fusion.5), channel_id=1, source_target_pairs={{0,2},{2,0},{1,3},{3,1},{4,6},{6,4},{5,7},{7,5},{8,10},{10,8},{9,1... | collective-permute-start | bytes 165896 | tf_op jit(solution)/shard_map/ppermute | solution.py:25
  13.5 2.2 %copy-start.18 = (bf16[6,16,16,128]{3,2,1,0:T(8,128)(2,1)S(1)}, bf16[6,16,16,128]{3,2,1,0:T(8,128)(2,1)}, u32[]{:S(2)}) copy-start(bf16[6,16,16,128]{3,2,1,0:T(8,128)(2,1)} %param.9) | copy-start | bytes 1179652
  16.8 1.4 %copy-start.22 = (s32[1,256]{1,0:T(1,128)S(1)}, s32[1,256]{1,0:T(1,128)}, u32[]{:S(2)}) copy-start(s32[1,256]{1,0:T(1,128)} %param.15) | copy-start | bytes 3076
  16.8 2.9 %copy-start.23 = (f32[2,3]{1,0:T(2,128)S(1)}, f32[2,3]{1,0:T(2,128)}, u32[]{:S(2)}) copy-start(f32[2,3]{1,0:T(2,128)} %param.16) | copy-start | bytes 76
  16.9 2.9 %copy-start.19 = (bf16[16,16,128]{2,1,0:T(8,128)(2,1)S(1)}, bf16[16,16,128]{2,1,0:T(8,128)(2,1)}, u32[]{:S(2)}) copy-start(bf16[16,16,128]{2,1,0:T(8,128)(2,1)} %param.12) | copy-start | bytes 196612
  18.2 3.4 %collective-permute-start.3 = (f32[6,18,18,128]{3,2,1,0:T(8,128)}, f32[6,18,18,128]{3,2,1,0:T(8,128)}, u32[]{:S(2)}, u32[]{:S(2)}) collective-permute-start(f32[6,18,18,128]{3,2,1,0:T(8,128)} %pad_maximum_fusion.3), channel_id=1, source_target_pairs={{0,1},{1,0},{2,3},{3,2},{4,5},{5,4},{6,7},{7,6},{8,9},{9,8},{10,11... | collective-permute-start | bytes 2985992 | tf_op jit(solution)/shard_map/ppermute | solution.py:17
  19.7 20.6 %copy-start.4 = (f32[32768]{0:T(1024)}, f32[32768]{0:T(1024)S(1)}, u32[]{:S(2)}) copy-start(f32[32768]{0:T(1024)S(1)} %scatter_custom_fusion) | copy-start | bytes 393220
  19.7 11.2 %copy-start.20 = (f32[3]{0:T(128)}, f32[3]{0:T(128)S(1)}, u32[]{:S(2)}) copy-start(f32[3]{0:T(128)S(1)} %get-tuple-element.70) | copy-start | bytes 40
  19.8 9.9 %copy-start.15 = (f32[16,16,128]{2,1,0:T(8,128)}, f32[16,16,128]{2,1,0:T(8,128)S(1)}, u32[]{:S(2)}) copy-start(f32[16,16,128]{2,1,0:T(8,128)S(1)} %get-tuple-element.58) | copy-start | bytes 393220
  19.8 11.1 %copy-start.11 = (f32[16,16,128]{2,1,0:T(8,128)}, f32[16,16,128]{2,1,0:T(8,128)S(1)}, u32[]{:S(2)}) copy-start(f32[16,16,128]{2,1,0:T(8,128)S(1)} %get-tuple-element.59) | copy-start | bytes 393220
  19.8 11.1 %copy-start.13 = (f32[16,16,128]{2,1,0:T(8,128)}, f32[16,16,128]{2,1,0:T(8,128)S(1)}, u32[]{:S(2)}) copy-start(f32[16,16,128]{2,1,0:T(8,128)S(1)} %get-tuple-element.60) | copy-start | bytes 393220
  23.8 2.1 %copy-start.6 = (bf16[6,16,16,128]{3,2,1,0:T(8,128)(2,1)S(1)}, bf16[6,16,16,128]{3,2,1,0:T(8,128)(2,1)}, u32[]{:S(2)}) copy-start(bf16[6,16,16,128]{3,2,1,0:T(8,128)(2,1)} %param.10) | copy-start | bytes 1179652
  25.9 0.9 copy-start.17
  32.9 7.4 %copy-start.7 = (bf16[6,16,16,128]{3,2,1,0:T(8,128)(2,1)S(1)}, bf16[6,16,16,128]{3,2,1,0:T(8,128)(2,1)}, u32[]{:S(2)}) copy-start(bf16[6,16,16,128]{3,2,1,0:T(8,128)(2,1)} %param.10) | copy-start | bytes 1179652
  32.9 7.4 %copy-start.8 = (f32[3,16,16,128]{3,2,1,0:T(8,128)S(1)}, f32[3,16,16,128]{3,2,1,0:T(8,128)}, u32[]{:S(2)}) copy-start(f32[3,16,16,128]{3,2,1,0:T(8,128)} %get-tuple-element.19) | copy-start | bytes 1179652
  40.3 15.9 %copy-start.9 = (f32[3,16,16,128]{3,2,1,0:T(8,128)S(1)}, f32[3,16,16,128]{3,2,1,0:T(8,128)}, u32[]{:S(2)}) copy-start(f32[3,16,16,128]{3,2,1,0:T(8,128)} %get-tuple-element.19) | copy-start | bytes 1179652
  40.3 15.9 %copy-start.10 = (f32[3,16,16,128]{3,2,1,0:T(8,128)S(1)}, f32[3,16,16,128]{3,2,1,0:T(8,128)}, u32[]{:S(2)}) copy-start(f32[3,16,16,128]{3,2,1,0:T(8,128)} %get-tuple-element.55) | copy-start | bytes 1179652
  42.4 1.9 %collective-permute-start.4 = (f32[780]{0:T(1024)S(1)}, f32[780]{0:T(1024)S(1)}, u32[]{:S(2)}, u32[]{:S(2)}) collective-permute-start(f32[780]{0:T(1024)S(1)} %pad_maximum_fusion.19), channel_id=1, source_target_pairs={{0,1},{1,0},{2,3},{3,2},{4,5},{5,4},{6,7},{7,6},{8,9},{9,8},{10,11... | collective-permute-start | bytes 9368 | tf_op jit(solution)/shard_map/ppermute | solution.py:143
  42.5 3.6 %collective-permute-start.5 = (f32[780]{0:T(1024)S(1)}, f32[780]{0:T(1024)S(1)}, u32[]{:S(2)}, u32[]{:S(2)}) collective-permute-start(f32[780]{0:T(1024)S(1)} %pad_maximum_fusion.19), channel_id=1, source_target_pairs={{0,2},{1,3},{2,0},{3,1},{4,6},{5,7},{6,4},{7,5},{8,10},{9,11},{10,... | collective-permute-start | bytes 9368 | tf_op jit(solution)/shard_map/ppermute | solution.py:143
  43.8 3.0 %collective-permute-start.6 = (f32[780]{0:T(1024)S(1)}, f32[780]{0:T(1024)S(1)}, u32[]{:S(2)}, u32[]{:S(2)}) collective-permute-start(f32[780]{0:T(1024)S(1)} %pad_maximum_fusion.19), channel_id=1, source_target_pairs={{0,3},{1,2},{2,1},{3,0},{4,7},{5,6},{6,5},{7,4},{8,11},{9,10},{10,... | collective-permute-start | bytes 9368 | tf_op jit(solution)/shard_map/ppermute | solution.py:143
  46.8 4.4 %collective-permute-start.7 = (f32[780]{0:T(1024)S(1)}, f32[780]{0:T(1024)S(1)}, u32[]{:S(2)}, u32[]{:S(2)}) collective-permute-start(f32[780]{0:T(1024)S(1)} %add_add_fusion.5), channel_id=1, source_target_pairs={{0,4},{1,5},{2,6},{3,7},{4,0},{5,1},{6,2},{7,3},{8,12},{9,13},{10,... | collective-permute-start | bytes 9368 | tf_op jit(solution)/shard_map/ppermute | solution.py:143
  48.6 4.5 %collective-permute-start.8 = (f32[780]{0:T(1024)S(1)}, f32[780]{0:T(1024)S(1)}, u32[]{:S(2)}, u32[]{:S(2)}) collective-permute-start(f32[780]{0:T(1024)S(1)} %add_add_fusion.5), channel_id=1, source_target_pairs={{0,8},{1,9},{2,10},{3,11},{4,12},{5,13},{6,14},{7,15},{8,0},{9,1},... | collective-permute-start | bytes 9368 | tf_op jit(solution)/shard_map/ppermute | solution.py:143
  50.7 5.4 %collective-permute-start.9 = (f32[780]{0:T(1024)S(1)}, f32[780]{0:T(1024)S(1)}, u32[]{:S(2)}, u32[]{:S(2)}) collective-permute-start(f32[780]{0:T(1024)S(1)} %add_add_fusion.5), channel_id=1, source_target_pairs={{0,12},{1,13},{2,14},{3,15},{4,8},{5,9},{6,10},{7,11},{8,4},{9,5},... | collective-permute-start | bytes 9368 | tf_op jit(solution)/shard_map/ppermute | solution.py:143
  56.4 6.0 %collective-permute-start.10 = (f32[6,1,16,128]{3,2,1,0:T(8,128)S(1)}, f32[6,1,16,128]{3,2,1,0:T(8,128)S(1)}, u32[]{:S(2)}, u32[]{:S(2)}) collective-permute-start(f32[6,1,16,128]{3,2,1,0:T(8,128)S(1)} %get-tuple-element.52), channel_id=1, source_target_pairs={{4,0},{8,4},{12,8},{5,1},{9,5},{13,9},{6,2},{10,6},{14,10},{7,3},{... | collective-permute-start | bytes 147464 | tf_op jit(solution)/shard_map/ppermute | solution.py:33
  57.7 6.3 %collective-permute-start.11 = (f32[6,1,16,128]{3,2,1,0:T(8,128)S(1)}, f32[6,1,16,128]{3,2,1,0:T(8,128)S(1)}, u32[]{:S(2)}, u32[]{:S(2)}) collective-permute-start(f32[6,1,16,128]{3,2,1,0:T(8,128)S(1)} %get-tuple-element.51), channel_id=1, source_target_pairs={{0,4},{4,8},{8,12},{1,5},{5,9},{9,13},{2,6},{6,10},{10,14},{3,7},{... | collective-permute-start | bytes 147464 | tf_op jit(solution)/shard_map/ppermute | solution.py:32
  64.0 4.2 %collective-permute-start.12 = (f32[6,18,1,128]{3,2,1,0:T(1,128)S(1)}, f32[6,18,1,128]{3,2,1,0:T(1,128)S(1)}, u32[]{:S(2)}, u32[]{:S(2)}) collective-permute-start(f32[6,18,1,128]{3,2,1,0:T(1,128)S(1)} %broadcast_select_fusion.2), channel_id=1, source_target_pairs={{0,2},{2,0},{1,3},{3,1},{4,6},{6,4},{5,7},{7,5},{8,10},{10,8},{9,1... | collective-permute-start | bytes 165896 | tf_op jit(solution)/shard_map/ppermute | solution.py:25
  68.3 0.6 copy-start
  68.4 1.9 %copy-start.2 = (f32[6,18,1,128]{3,2,1,0:T(1,128)}, f32[6,18,1,128]{3,2,1,0:T(1,128)S(1)}, u32[]{:S(2)}) copy-start(f32[6,18,1,128]{3,2,1,0:T(1,128)S(1)} %get-tuple-element.62) | copy-start | bytes 165892
  70.3 3.4 %collective-permute-start.13 = (f32[6,18,18,128]{3,2,1,0:T(8,128)}, f32[6,18,18,128]{3,2,1,0:T(8,128)}, u32[]{:S(2)}, u32[]{:S(2)}) collective-permute-start(f32[6,18,18,128]{3,2,1,0:T(8,128)} %pad_maximum_fusion.5), channel_id=1, source_target_pairs={{0,1},{1,0},{2,3},{3,2},{4,5},{5,4},{6,7},{7,6},{8,9},{9,8},{10,11... | collective-permute-start | bytes 2985992 | tf_op jit(solution)/shard_map/ppermute | solution.py:17
  71.3 4.5 %copy-start.1 = (f32[6,18,1,128]{3,2,1,0:T(1,128)S(1)}, f32[6,18,1,128]{3,2,1,0:T(1,128)}, u32[]{:S(2)}) copy-start(f32[6,18,1,128]{3,2,1,0:T(1,128)} %copy-done) | copy-start | bytes 165892
  71.3 4.5 %copy-start.3 = (f32[6,18,1,128]{3,2,1,0:T(1,128)S(1)}, f32[6,18,1,128]{3,2,1,0:T(1,128)}, u32[]{:S(2)}) copy-start(f32[6,18,1,128]{3,2,1,0:T(1,128)} %copy-done.2) | copy-start | bytes 165892
  81.3 0.9 copy-start.5
  81.3 1.0 copy-start.12
  81.4 1.0 %copy-start.14 = (f32[16,16,128]{2,1,0:T(8,128)S(1)}, f32[16,16,128]{2,1,0:T(8,128)}, u32[]{:S(2)}) copy-start(f32[16,16,128]{2,1,0:T(8,128)} %copy-done.13) | copy-start | bytes 393220
  81.4 1.1 %copy-start.16 = (f32[16,16,128]{2,1,0:T(8,128)S(1)}, f32[16,16,128]{2,1,0:T(8,128)}, u32[]{:S(2)}) copy-start(f32[16,16,128]{2,1,0:T(8,128)} %copy-done.15) | copy-start | bytes 393220
  81.4 1.1 %copy-start.21 = (f32[3]{0:T(128)S(1)}, f32[3]{0:T(128)}, u32[]{:S(2)}) copy-start(f32[3]{0:T(128)} %copy-done.20) | copy-start | bytes 40
  84.8 1.9 %collective-permute-start.14 = (f32[134]{0:T(256)S(1)}, f32[134]{0:T(256)S(1)}, u32[]{:S(2)}, u32[]{:S(2)}) collective-permute-start(f32[134]{0:T(256)S(1)} %pad_maximum_fusion.20), channel_id=1, source_target_pairs={{0,1},{1,0},{2,3},{3,2},{4,5},{5,4},{6,7},{7,6},{8,9},{9,8},{10,11... | collective-permute-start | bytes 1616 | tf_op jit(solution)/shard_map/ppermute | solution.py:143
  85.0 3.6 %collective-permute-start.15 = (f32[134]{0:T(256)S(1)}, f32[134]{0:T(256)S(1)}, u32[]{:S(2)}, u32[]{:S(2)}) collective-permute-start(f32[134]{0:T(256)S(1)} %pad_maximum_fusion.20), channel_id=1, source_target_pairs={{0,2},{1,3},{2,0},{3,1},{4,6},{5,7},{6,4},{7,5},{8,10},{9,11},{10,... | collective-permute-start | bytes 1616 | tf_op jit(solution)/shard_map/ppermute | solution.py:143
  85.8 3.0 %collective-permute-start.16 = (f32[134]{0:T(256)S(1)}, f32[134]{0:T(256)S(1)}, u32[]{:S(2)}, u32[]{:S(2)}) collective-permute-start(f32[134]{0:T(256)S(1)} %pad_maximum_fusion.20), channel_id=1, source_target_pairs={{0,3},{1,2},{2,1},{3,0},{4,7},{5,6},{6,5},{7,4},{8,11},{9,10},{10,... | collective-permute-start | bytes 1616 | tf_op jit(solution)/shard_map/ppermute | solution.py:143
  88.9 5.0 %collective-permute-start.17 = (f32[134]{0:T(256)S(1)}, f32[134]{0:T(256)S(1)}, u32[]{:S(2)}, u32[]{:S(2)}) collective-permute-start(f32[134]{0:T(256)S(1)} %add_add_fusion.7), channel_id=1, source_target_pairs={{0,4},{1,5},{2,6},{3,7},{4,0},{5,1},{6,2},{7,3},{8,12},{9,13},{10,... | collective-permute-start | bytes 1616 | tf_op jit(solution)/shard_map/ppermute | solution.py:143
  91.2 4.5 %collective-permute-start.18 = (f32[134]{0:T(256)S(1)}, f32[134]{0:T(256)S(1)}, u32[]{:S(2)}, u32[]{:S(2)}) collective-permute-start(f32[134]{0:T(256)S(1)} %add_add_fusion.7), channel_id=1, source_target_pairs={{0,8},{1,9},{2,10},{3,11},{4,12},{5,13},{6,14},{7,15},{8,0},{9,1},... | collective-permute-start | bytes 1616 | tf_op jit(solution)/shard_map/ppermute | solution.py:143
  91.2 5.4 %collective-permute-start.19 = (f32[134]{0:T(256)S(1)}, f32[134]{0:T(256)S(1)}, u32[]{:S(2)}, u32[]{:S(2)}) collective-permute-start(f32[134]{0:T(256)S(1)} %add_add_fusion.7), channel_id=1, source_target_pairs={{0,12},{1,13},{2,14},{3,15},{4,8},{5,9},{6,10},{7,11},{8,4},{9,5},... | collective-permute-start | bytes 1616 | tf_op jit(solution)/shard_map/ppermute | solution.py:143

commit v8 on v7

--- a/solution.py
+++ b/solution.py
@@ -210,7 +210,6 @@
                 jnp.sum(mask * field, axis=(1, 2, 3)),
                 jnp.sum(gain_real, axis=(1, 2, 3)),
                 jnp.sum(gain_imag, axis=(1, 2, 3)),
-                response.reshape(-1),
             ]
         ),
         axes,
@@ -218,7 +217,6 @@
     mean_field = first[:6] / count
     gain_total_real = first[6:9]
     gain_total_imag = first[9:12]
-    response = first[12:].reshape(response.shape)
     sweep_args = (lame_first, shear, density_cells, mask, source_cells, omega_sq, impedance)
     padded = with_halo(field, (("gx", 1), ("gy", 2), ("col", 3)), 1)
     field = sweep(padded, *sweep_args)
@@ -232,8 +230,13 @@
         - DAMPING * (field[:3] * forward_imag + field[3:] * forward_real)
     )
     cell_terms = -omega_sq * jnp.sum(correlation, axis=0)
-    last = group_sum(jnp.concatenate([second_local, block_sums(cell_terms).reshape(-1)]), axes)
+    last = group_sum(
+        jnp.concatenate([second_local, block_sums(cell_terms).reshape(-1), response.reshape(-1)]),
+        axes,
+    )
     second = last[:6]
+    grid_size = grid_shape[0] * grid_shape[1]
+    response = last[6 + grid_size :].reshape(response.shape)
     mean_real = mean_field[:3]
     mean_imag = mean_field[3:]
     total_real = second[:3] + (gain_total_real * mean_real - gain_total_imag * mean_imag)
@@ -243,7 +246,7 @@
     late_terms = jnp.sum(
         late_mean[:3, None, None] * response[:3] - late_mean[3:, None, None] * response[3:], axis=0
     )
-    coarse = (last[6:].reshape(grid_shape) - omega_sq * late_terms) / 64.0
+    coarse = (last[6 : 6 + grid_size].reshape(grid_shape) - omega_sq * late_terms) / 64.0
     return (field, coarse)
 
 

time: 101 us -> 101 us (level)
  waiting for transfers between devices: 21.1 us -> 18.6 us
  starting transfers between devices: 28.5 us -> 30.7 us
  other arithmetic: 35.2 us -> 37.3 us
  local copies, waits for them, and re-layouts: 13.3 us -> 11.6 us
    ppermute x2, waiting for transfers between devices: 3.83 us -> 1.52 us  [with_halo(): got = lax.ppermute(array, axis, [(0, 1), (1, 0)])]
    reduce_sum x1, other arithmetic: 1.85 us -> 0.14 us  [shards(): jnp.sum(gain_real, axis=(1, 2, 3))]
    sub x1, other arithmetic: 0.12 us -> 1.68 us  [shards(): response_real = plain_real - DAMPING * plain_imag]
    ppermute x12, starting transfers between devices: 12.9 us -> 14.4 us  [group_sum(): lax.ppermute(value, axes, [(i, i ^ m * stride) for i in range(size)])]
    add x1, other arithmetic: 0.05 us -> 1.22 us  [shards(): response_imag = plain_imag + DAMPING * plain_real]
    unnamed x49 -> x61, local copies, waits for them, and re-layouts: 2.03 us -> 2.52 us
  transfers between devices with their start and end apart: 20 -> 20, of which waited for: 12 -> 10; matrix products, arithmetic and copies ran while one was open for 9% -> 15% of each run, Pallas kernels for 0% -> 0%
where the time goes in v8:
time: 101 us; the launch traced here: 100 us
  other arithmetic  37.3 us (37%)
  starting transfers between devices  30.7 us (30%)
  waiting for transfers between devices  18.6 us (18%)
  local copies, waits for them, and re-layouts  11.6 us (11%)
  between operations  2.01 us (2%)
    ppermute x12, starting transfers between devices, group_sum(): lax.ppermute(value, axes, [(i, i ^ m * stride) for i in range(size)])  14.4 us
    ppermute x12, waiting for transfers between devices, group_sum(): lax.ppermute(value, axes, [(i, i ^ m * stride) for i in range(size)])  12.8 us
    ppermute x2, starting transfers between devices, with_halo(): before = lax.ppermute(last, axis, up)  10.3 us
    concatenate x6, other arithmetic, with_halo(): array = jnp.concatenate([before, array, after], axis=dim)  8.69 us
    add x12, other arithmetic, navier(): result.append(shear * laplace[channel] + (lame_first + shear) * divergence)  5.61 us
    select_n x2, other arithmetic, with_halo(): after = jnp.where(first, got_initial, zero)  4.35 us
    ppermute x2, starting transfers between devices, with_halo(): got = lax.ppermute(jnp.where(first, last, initial), axis, [(0, 1), (1, 0)])  3.44 us
    ppermute x2, waiting for transfers between devices, with_halo(): got = lax.ppermute(jnp.where(first, last, initial), axis, [(0, 1), (1, 0)])  2.78 us
  transfers between devices with their start and end apart: 20, of which 10 were waited for; matrix products, arithmetic and copies ran while one was open for 15% of the time, Pallas kernels for 0%

profile of v8, /device:TPU:0, one launch (start us, length us, event | category | flops | bytes accessed | tf_op | source)
XLA Modules:
  0.0 100.3 jit_solution(13389450307011950698)
XLA Ops:
  0.6 0.8 fusion.108
  1.4 1.3 %collective-permute-start = (f32[6,1,16,128]{3,2,1,0:T(8,128)S(1)}, f32[6,1,16,128]{3,2,1,0:T(8,128)S(1)}, u32[]{:S(2)}, u32[]{:S(2)}) collective-permute-start(f32[6,1,16,128]{3,2,1,0:T(8,128)S(1)} %get-tuple-element.53), channel_id=1, source_target_pairs={{4,0},{8,4},{12,8},{5,1},{9,5},{13,9},{6,2},{10,6},{14,10},{7,3},{... | collective-permute-start | bytes 147464 | tf_op jit(solution)/shard_map/ppermute | solution.py:33
  2.7 5.6 %collective-permute-start.1 = (f32[6,1,16,128]{3,2,1,0:T(8,128)S(1)}, f32[6,1,16,128]{3,2,1,0:T(8,128)S(1)}, u32[]{:S(2)}, u32[]{:S(2)}) collective-permute-start(f32[6,1,16,128]{3,2,1,0:T(8,128)S(1)} %get-tuple-element.52), channel_id=1, source_target_pairs={{0,4},{4,8},{8,12},{1,5},{5,9},{9,13},{2,6},{6,10},{10,14},{3,7},{... | collective-permute-start | bytes 147464 | tf_op jit(solution)/shard_map/ppermute | solution.py:32
  8.3 0.8 slice_bitcast_fusion.2
  9.0 0.8 select_reduce_fusion.1
  9.9 1.1 %convert_element_type.12 = f32[6,16,16,128]{3,2,1,0:T(8,128)S(1)} convert(bf16[6,16,16,128]{3,2,1,0:T(8,128)(2,1)} %param.10) | non-fusion elementwise | flops 196608 | bytes 1179648 | tf_op jit(solution)/shard_map/convert_element_type | solution.py:206
  11.0 2.0 %collective-permute-start.2 = (f32[6,18,1,128]{3,2,1,0:T(1,128)S(1)}, f32[6,18,1,128]{3,2,1,0:T(1,128)S(1)}, u32[]{:S(2)}, u32[]{:S(2)}) collective-permute-start(f32[6,18,1,128]{3,2,1,0:T(1,128)S(1)} %broadcast_select_fusion.5), channel_id=1, source_target_pairs={{0,2},{2,0},{1,3},{3,1},{4,6},{6,4},{5,7},{7,5},{8,10},{10,8},{9,1... | collective-permute-start | bytes 165896 | tf_op jit(solution)/shard_map/ppermute | solution.py:25
  13.6 0.9 reshape.125
  15.7 1.1 %convert_element_type.15 = f32[6,16,16,128]{3,2,1,0:T(8,128)S(1)} convert(bf16[6,16,16,128]{3,2,1,0:T(8,128)(2,1)} %param.11) | non-fusion elementwise | flops 196608 | bytes 1179648 | tf_op jit(solution)/shard_map/convert_element_type | solution.py:198
  16.9 1.3 %pad_maximum_fusion.3 = f32[6,18,18,128]{3,2,1,0:T(8,128)} fusion(f32[6,18,1,128]{3,2,1,0:T(1,128)S(1)} %get-tuple-element.60, f32[6,1,16,128]{3,2,1,0:T(8,128)S(1)} %collective-permute-done, f32[6,16,16,128]{3,2,1,0:T(8,128)S(1)} %convert_element_type.12, f32[6,1,16,128]{3,2,1,0:T(8,128)S(1)} %collective-permute-done.1, ...), kind=kLoop, calls=%fused_computation.11 | loop fusion | flops 995328 | bytes 1990656 | tf_op jit(solution)/shard_map/concatenate | solution.py:34
  18.2 1.5 %scatter_custom_fusion = f32[32768]{0:T(1024)S(1)} fusion(s32[256]{0:T(256)S(1)} %bitcast.21, f32[256]{0:T(256)S(1)} %broadcast.108, f32[]{:T(128)} %constant.18.clone.1), kind=kCustom, calls=%fused_computation.247 | custom fusion | bytes 131076 | tf_op jit(solution)/shard_map/scatter | solution.py:176
  20.1 1.5 %collective-permute-done.3 = f32[6,18,18,128]{3,2,1,0:T(8,128)} collective-permute-done((f32[6,18,18,128]{3,2,1,0:T(8,128)}, f32[6,18,18,128]{3,2,1,0:T(8,128)}, u32[]{:S(2)}, u32[]{:S(2)}) %collective-permute-start.3) | collective-permute-done | bytes 995360 | tf_op jit(solution)/shard_map/ppermute | solution.py:17
  21.6 2.2 %slice_select_fusion.3 = (f32[6,18,18,1]{3,2,1,0:T(8,128)S(1)}, f32[6,18,18,1]{3,2,1,0:T(8,128)S(1)}) fusion(f32[6,18,18,128]{3,2,1,0:T(8,128)} %collective-permute-done.3, pred[]{:T(512)S(6)} %eq.19), kind=kLoop, calls=%fused_computation.8 | loop fusion | flops 3888 | bytes 31105 | tf_op jit(solution)/shard_map/jit(_where)/select_n | solution.py:22
  23.8 2.1 %pad_maximum_fusion = (f32[6,18,18,129]{3,2,1,0:T(8,128)S(1)}, f32[6,18,18,129]{3,2,1,0:T(8,128)S(1)}) fusion(f32[6,18,18,1]{3,2,1,0:T(8,128)S(1)} %get-tuple-element.35, f32[6,18,1,128]{3,2,1,0:T(1,128)S(1)} %get-tuple-element.60, f32[6,1,16,128]{3,2,1,0:T(8,128)S(1)} %collective-permute-done, f32[6,16,16,128]{3,2,1,0:T(8,128)S(1)} %convert_element_type.12, ...), kind=kLoop, calls=%fused_computation.1 | loop fusion | flops 2507760 | bytes 3017088 | tf_op jit(solution)/shard_map/concatenate | solution.py:34
  29.7 1.3 %divide_add_fusion.3 = (f32[3,16,16,128]{3,2,1,0:T(8,128)}, f32[3,16,16,128]{3,2,1,0:T(8,128)S(1)}, f32[3,16,16,128]{3,2,1,0:T(8,128)S(1)}) fusion(f32[6,16,16,128]{3,2,1,0:T(8,128)S(1)} %convert_element_type.12, f32[16,16,128]{2,1,0:T(8,128)S(1)} %get-tuple-element.56, f32[16,16,128]{2,1,0:T(8,128)S(1)} %get-tuple-element.55, f32[3]{0:T(128)S(1)} %get-tuple-element.66, ...), kind=kLoop, calls=%fused_computation.76 | loop fusion | flops 3833856 | bytes 4063256 | tf_op jit(solution)/shard_map/add | solution.py:108
  31.0 1.7 %multiply_subtract_fusion = (f32[3,16,16,128]{3,2,1,0:T(8,128)}, f32[3,16,16,128]{3,2,1,0:T(8,128)}, f32[3,16,16,128]{3,2,1,0:T(8,128)}, f32[3,16,16,128]{3,2,1,...) fusion(f32[6,16,16,128]{3,2,1,0:T(8,128)S(1)} %convert_element_type.15, ...), kind=kLoop, calls=%fused_computation.65 | loop fusion | flops 2949120 | bytes 4849688 | tf_op jit(solution)/shard_map/sub | solution.py:203
  32.9 2.1 %fusion.9 = (f32[6]{0:T(128)}, f32[6]{0:T(128)S(1)}) fusion(f32[3,16,16,128]{3,2,1,0:T(8,128)} %get-tuple-element.51, f32[3,16,16,128]{3,2,1,0:T(8,128)} %get-tuple-element.24, f32[16,16,128]{2,1,0:T(8,128)S(1)} %bitcast.19, bf16[6,16,16,128]{3,2,1,0:T(8,128)(2,1)} %param.10), kind=kLoop, calls=%fused_computation.40 | loop fusion | flops 1179636 | bytes 1310768 | tf_op jit(solution)/shard_map/reduce_sum | solution.py:223
  35.6 1.4 %collective-permute-start.6 = (f32[12]{0:T(128)S(1)}, f32[12]{0:T(128)S(1)}, u32[]{:S(2)}, u32[]{:S(2)}) collective-permute-start(f32[12]{0:T(128)S(1)} %pad_maximum_fusion.20), channel_id=1, source_target_pairs={{0,3},{1,2},{2,1},{3,0},{4,7},{5,6},{6,5},{7,4},{8,11},{9,10},{10,... | collective-permute-start | bytes 152 | tf_op jit(solution)/shard_map/ppermute | solution.py:143
  36.9 1.8 %collective-permute-done.5 = f32[12]{0:T(128)S(1)} collective-permute-done((f32[12]{0:T(128)S(1)}, f32[12]{0:T(128)S(1)}, u32[]{:S(2)}, u32[]{:S(2)}) %collective-permute-start.5) | collective-permute-done | bytes 80 | tf_op jit(solution)/shard_map/ppermute | solution.py:143
  38.8 1.6 %collective-permute-start.7 = (f32[12]{0:T(128)S(1)}, f32[12]{0:T(128)S(1)}, u32[]{:S(2)}, u32[]{:S(2)}) collective-permute-start(f32[12]{0:T(128)S(1)} %add_add_fusion.8), channel_id=1, source_target_pairs={{0,4},{1,5},{2,6},{3,7},{4,0},{5,1},{6,2},{7,3},{8,12},{9,13},{10,... | collective-permute-start | bytes 152 | tf_op jit(solution)/shard_map/ppermute | solution.py:143
  40.4 2.4 %collective-permute-start.8 = (f32[12]{0:T(128)S(1)}, f32[12]{0:T(128)S(1)}, u32[]{:S(2)}, u32[]{:S(2)}) collective-permute-start(f32[12]{0:T(128)S(1)} %add_add_fusion.8), channel_id=1, source_target_pairs={{0,8},{1,9},{2,10},{3,11},{4,12},{5,13},{6,14},{7,15},{8,0},{9,1},... | collective-permute-start | bytes 152 | tf_op jit(solution)/shard_map/ppermute | solution.py:143
  43.2 1.6 %collective-permute-done.8 = f32[12]{0:T(128)S(1)} collective-permute-done((f32[12]{0:T(128)S(1)}, f32[12]{0:T(128)S(1)}, u32[]{:S(2)}, u32[]{:S(2)}) %collective-permute-start.8) | collective-permute-done | bytes 80 | tf_op jit(solution)/shard_map/ppermute | solution.py:143
  44.9 3.3 %collective-permute-done.9 = f32[12]{0:T(128)S(1)} collective-permute-done((f32[12]{0:T(128)S(1)}, f32[12]{0:T(128)S(1)}, u32[]{:S(2)}, u32[]{:S(2)}) %collective-permute-start.9) | collective-permute-done | bytes 80 | tf_op jit(solution)/shard_map/ppermute | solution.py:143
  48.7 1.2 %add_add_fusion.3 = (f32[3,16,16,128]{3,2,1,0:T(8,128)S(1)}, f32[3,16,16,128]{3,2,1,0:T(8,128)S(1)}) fusion(f32[3,16,16,128]{3,2,1,0:T(8,128)S(1)} %copy-done.7, f32[3,16,16,128]{3,2,1,0:T(8,128)S(1)} %get-tuple-element.19, f32[3,16,16,128]{3,2,1,0:T(8,128)S(1)} %get-tuple-element.18, f32[3]{0:T(128)S(1)} %get-tuple-element.72, f32[3]{0:T(128)S(1)} %get-tuple-element.71, ...), kind=kLoop, calls=%fused_computation.71 | loop fusion | flops 786432 | bytes 2359320 | tf_op jit(solution)/shard_map/add | solution.py:129
  49.9 1.3 %collective-permute-start.10 = (f32[6,1,16,128]{3,2,1,0:T(8,128)S(1)}, f32[6,1,16,128]{3,2,1,0:T(8,128)S(1)}, u32[]{:S(2)}, u32[]{:S(2)}) collective-permute-start(f32[6,1,16,128]{3,2,1,0:T(8,128)S(1)} %get-tuple-element.50), channel_id=1, source_target_pairs={{4,0},{8,4},{12,8},{5,1},{9,5},{13,9},{6,2},{10,6},{14,10},{7,3},{... | collective-permute-start | bytes 147464 | tf_op jit(solution)/shard_map/ppermute | solution.py:33
  51.2 4.7 %collective-permute-start.11 = (f32[6,1,16,128]{3,2,1,0:T(8,128)S(1)}, f32[6,1,16,128]{3,2,1,0:T(8,128)S(1)}, u32[]{:S(2)}, u32[]{:S(2)}) collective-permute-start(f32[6,1,16,128]{3,2,1,0:T(8,128)S(1)} %get-tuple-element.49), channel_id=1, source_target_pairs={{0,4},{4,8},{8,12},{1,5},{5,9},{9,13},{2,6},{6,10},{10,14},{3,7},{... | collective-permute-start | bytes 147464 | tf_op jit(solution)/shard_map/ppermute | solution.py:32
  56.0 1.5 %collective-permute-done.11 = f32[6,1,16,128]{3,2,1,0:T(8,128)S(1)} collective-permute-done((f32[6,1,16,128]{3,2,1,0:T(8,128)S(1)}, f32[6,1,16,128]{3,2,1,0:T(8,128)S(1)}, u32[]{:S(2)}, u32[]{:S(2)}) %collective-permute-start.11) | collective-permute-done | bytes 49184 | tf_op jit(solution)/shard_map/ppermute | solution.py:32
  57.6 1.4 %collective-permute-start.12 = (f32[6,18,1,128]{3,2,1,0:T(1,128)S(1)}, f32[6,18,1,128]{3,2,1,0:T(1,128)S(1)}, u32[]{:S(2)}, u32[]{:S(2)}) collective-permute-start(f32[6,18,1,128]{3,2,1,0:T(1,128)S(1)} %broadcast_select_fusion.2), channel_id=1, source_target_pairs={{0,2},{2,0},{1,3},{3,1},{4,6},{6,4},{5,7},{7,5},{8,10},{10,8},{9,1... | collective-permute-start | bytes 165896 | tf_op jit(solution)/shard_map/ppermute | solution.py:25
  59.0 2.8 %collective-permute-done.12 = f32[6,18,1,128]{3,2,1,0:T(1,128)S(1)} collective-permute-done((f32[6,18,1,128]{3,2,1,0:T(1,128)S(1)}, f32[6,18,1,128]{3,2,1,0:T(1,128)S(1)}, u32[]{:S(2)}, u32[]{:S(2)}) %collective-permute-start.12) | collective-permute-done | bytes 55328 | tf_op jit(solution)/shard_map/ppermute | solution.py:25
  62.5 1.3 %pad_maximum_fusion.5 = f32[6,18,18,128]{3,2,1,0:T(8,128)} fusion(f32[6,18,1,128]{3,2,1,0:T(1,128)S(1)} %get-tuple-element.58, f32[6,1,16,128]{3,2,1,0:T(8,128)S(1)} %collective-permute-done.10, f32[3,16,16,128]{3,2,1,0:T(8,128)S(1)} %get-tuple-element.47, f32[3,16,16,128]{3,2,1,0:T(8,128)S(1)} %get-tuple-element.48, ...), kind=kLoop, calls=%fused_computation.14 | loop fusion | flops 1244160 | bytes 1990656 | tf_op jit(solution)/shard_map/concatenate | solution.py:34
  63.8 1.2 %multiply_add_fusion = f32[3,16,16,128]{3,2,1,0:T(8,128)S(1)} fusion(f32[3,16,16,128]{3,2,1,0:T(8,128)} %get-tuple-element.17, f32[3,16,16,128]{3,2,1,0:T(8,128)} %get-tuple-element.16), kind=kLoop, calls=%fused_computation.64 | loop fusion | flops 196608 | bytes 1179648 | tf_op jit(solution)/shard_map/add | solution.py:204
  65.3 0.8 reduce_sum.115
  66.1 1.6 %reduce_sum.116 = f32[6,4,4]{2,1,0:T(4,128)} reduce(f32[6,4,4,4,4]{4,3,2,1,0:T(4,128)} %reduce_sum.115, f32[]{:T(128)} %constant.18.clone.1), dimensions={2,4}, to_apply=%region_11.12 | reduce | flops 1440 | bytes 6532 | tf_op jit(solution)/shard_map/reduce_sum | solution.py:194
  67.8 1.7 %dynamic_update_slice.7 = f32[6,16,8]{2,1,0:T(8,128)S(1)} dynamic-update-slice(f32[6,16,8]{2,1,0:T(8,128)S(1)} %broadcast_in_dim.66, f32[6,4,4]{2,1,0:T(4,128)} %reduce_sum.116, s32[]{:T(128)} %constant.21.clone.1, s32[]{:T(128)S(6)} %select_n.88, s32[]{:T(128)S(6)} %select_n.89) | dynamic-update-slice | bytes 772 | tf_op jit(solution)/shard_map/dynamic_update_slice | solution.py:196
  69.4 0.7 reshape.127
  70.1 1.1 %pad_maximum_fusion.4 = (f32[6,18,17,128]{3,2,1,0:T(8,128)S(1)}, f32[6,18,17,128]{3,2,1,0:T(8,128)S(1)}) fusion(f32[6,18,1,128]{3,2,1,0:T(1,128)} %copy-done.2, f32[6,1,16,128]{3,2,1,0:T(8,128)S(1)} %collective-permute-done.10, f32[3,16,16,128]{3,2,1,0:T(8,128)S(1)} %get-tuple-element.47, f32[3,16,16,128]{3,2,1,0:T(8,128)S(1)} %get-tuple-element.48, ...), kind=kLoop, calls=%fused_computation.12 | loop fusion | flops 1880064 | bytes 2875392 | tf_op jit(solution)/shard_map/concatenate | solution.py:34
  71.2 2.2 %slice_select_fusion.1 = (f32[6,18,18,1]{3,2,1,0:T(8,128)S(1)}, f32[6,18,18,1]{3,2,1,0:T(8,128)S(1)}) fusion(f32[6,18,18,128]{3,2,1,0:T(8,128)} %collective-permute-done.13, pred[]{:T(512)S(6)} %eq.19), kind=kLoop, calls=%fused_computation.6 | loop fusion | flops 3888 | bytes 31105 | tf_op jit(solution)/shard_map/jit(_where)/select_n | solution.py:22
  73.4 2.7 %pad_maximum_fusion.1 = (f32[6,18,18,129]{3,2,1,0:T(8,128)S(1)}, f32[6,18,18,129]{3,2,1,0:T(8,128)S(1)}) fusion(f32[6,18,18,1]{3,2,1,0:T(8,128)S(1)} %get-tuple-element.33, f32[6,18,1,128]{3,2,1,0:T(1,128)S(1)} %copy-done.3, f32[6,1,16,128]{3,2,1,0:T(8,128)S(1)} %collective-permute-done.10, f32[3,16,16,128]{3,2,1,0:T(8,128)S(1)} %get-tuple-element.47, ...), kind=kLoop, calls=%fused_computation.3 | loop fusion | flops 3009312 | bytes 3017088 | tf_op jit(solution)/shard_map/concatenate | solution.py:34
  80.0 1.6 %subtract_reduce_fusion = (f32[16,16,128]{2,1,0:T(8,128)S(1)}, f32[3,16,16,128]{3,2,1,0:T(8,128)}, f32[3,16,16,128]{3,2,1,0:T(8,128)}) fusion(f32[6,16,16,128]{3,2,1,0:T(8,128)S(1)} %convert_element_type.15, f32[3,16,16,128]{3,2,1,0:T(8,128)S(1)} %get-tuple-element.48, f32[16,16,128]{2,1,0:T(8,128)S(1)} %copy-done.11, ...), kind=kLoop, calls=%fused_computation.68 | loop fusion | flops 5275648 | bytes 4587544 | tf_op jit(solution)/shard_map/reduce_sum | solution.py:232
  83.0 2.8 %collective-permute-start.15 = (f32[902]{0:T(1024)S(1)}, f32[902]{0:T(1024)S(1)}, u32[]{:S(2)}, u32[]{:S(2)}) collective-permute-start(f32[902]{0:T(1024)S(1)} %pad_maximum_fusion.19), channel_id=1, source_target_pairs={{0,2},{1,3},{2,0},{3,1},{4,6},{5,7},{6,4},{7,5},{8,10},{9,11},{10,... | collective-permute-start | bytes 10832 | tf_op jit(solution)/shard_map/ppermute | solution.py:143
  85.8 1.6 %collective-permute-done.15 = f32[902]{0:T(1024)S(1)} collective-permute-done((f32[902]{0:T(1024)S(1)}, f32[902]{0:T(1024)S(1)}, u32[]{:S(2)}, u32[]{:S(2)}) %collective-permute-start.15) | collective-permute-done | bytes 3640 | tf_op jit(solution)/shard_map/ppermute | solution.py:143
  87.4 1.5 %collective-permute-done.16 = f32[902]{0:T(1024)S(1)} collective-permute-done((f32[902]{0:T(1024)S(1)}, f32[902]{0:T(1024)S(1)}, u32[]{:S(2)}, u32[]{:S(2)}) %collective-permute-start.16) | collective-permute-done | bytes 3640 | tf_op jit(solution)/shard_map/ppermute | solution.py:143
  88.9 2.3 %collective-permute-start.17 = (f32[902]{0:T(1024)S(1)}, f32[902]{0:T(1024)S(1)}, u32[]{:S(2)}, u32[]{:S(2)}) collective-permute-start(f32[902]{0:T(1024)S(1)} %add_add_fusion.5), channel_id=1, source_target_pairs={{0,4},{1,5},{2,6},{3,7},{4,0},{5,1},{6,2},{7,3},{8,12},{9,13},{10,... | collective-permute-start | bytes 10832 | tf_op jit(solution)/shard_map/ppermute | solution.py:143
  91.2 2.4 %collective-permute-start.19 = (f32[902]{0:T(1024)S(1)}, f32[902]{0:T(1024)S(1)}, u32[]{:S(2)}, u32[]{:S(2)}) collective-permute-start(f32[902]{0:T(1024)S(1)} %add_add_fusion.5), channel_id=1, source_target_pairs={{0,12},{1,13},{2,14},{3,15},{4,8},{5,9},{6,10},{7,11},{8,4},{9,5},... | collective-permute-start | bytes 10832 | tf_op jit(solution)/shard_map/ppermute | solution.py:143
  93.6 2.1 %collective-permute-done.18 = f32[902]{0:T(1024)S(1)} collective-permute-done((f32[902]{0:T(1024)S(1)}, f32[902]{0:T(1024)S(1)}, u32[]{:S(2)}, u32[]{:S(2)}) %collective-permute-start.18) | collective-permute-done | bytes 3640 | tf_op jit(solution)/shard_map/ppermute | solution.py:143
  95.7 0.9 collective-permute-done.19
  98.0 1.3 %subtract_add_fusion = (f32[3,16,16,128]{3,2,1,0:T(8,128)S(1)}, f32[3,16,16,128]{3,2,1,0:T(8,128)S(1)}) fusion(f32[3,16,16,128]{3,2,1,0:T(8,128)} %get-tuple-element.13, f32[3,16,16,128]{3,2,1,0:T(8,128)S(1)} %get-tuple-element.19, f32[3,16,16,128]{3,2,1,0:T(8,128)S(1)} %get-tuple-element.18, f32[3]{0:T(128)S(1)} %get-tuple-element.70, ...), kind=kLoop, calls=%fused_computation.63 | loop fusion | flops 786432 | bytes 2359320 | tf_op jit(solution)/shard_map/add | solution.py:128
  99.4 1.0 pad_maximum_fusion.13
  (139 shorter events, 14.7 us)
Async XLA Ops:
  1.4 9.5 %collective-permute-start = (f32[6,1,16,128]{3,2,1,0:T(8,128)S(1)}, f32[6,1,16,128]{3,2,1,0:T(8,128)S(1)}, u32[]{:S(2)}, u32[]{:S(2)}) collective-permute-start(f32[6,1,16,128]{3,2,1,0:T(8,128)S(1)} %get-tuple-element.53), channel_id=1, source_target_pairs={{4,0},{8,4},{12,8},{5,1},{9,5},{13,9},{6,2},{10,6},{14,10},{7,3},{... | collective-permute-start | bytes 147464 | tf_op jit(solution)/shard_map/ppermute | solution.py:33
  2.7 8.3 %collective-permute-start.1 = (f32[6,1,16,128]{3,2,1,0:T(8,128)S(1)}, f32[6,1,16,128]{3,2,1,0:T(8,128)S(1)}, u32[]{:S(2)}, u32[]{:S(2)}) collective-permute-start(f32[6,1,16,128]{3,2,1,0:T(8,128)S(1)} %get-tuple-element.52), channel_id=1, source_target_pairs={{0,4},{4,8},{8,12},{1,5},{5,9},{9,13},{2,6},{6,10},{10,14},{3,7},{... | collective-permute-start | bytes 147464 | tf_op jit(solution)/shard_map/ppermute | solution.py:32
  11.0 5.8 %collective-permute-start.2 = (f32[6,18,1,128]{3,2,1,0:T(1,128)S(1)}, f32[6,18,1,128]{3,2,1,0:T(1,128)S(1)}, u32[]{:S(2)}, u32[]{:S(2)}) collective-permute-start(f32[6,18,1,128]{3,2,1,0:T(1,128)S(1)} %broadcast_select_fusion.5), channel_id=1, source_target_pairs={{0,2},{2,0},{1,3},{3,1},{4,6},{6,4},{5,7},{7,5},{8,10},{10,8},{9,1... | collective-permute-start | bytes 165896 | tf_op jit(solution)/shard_map/ppermute | solution.py:25
  13.5 2.2 %copy-start.16 = (bf16[6,16,16,128]{3,2,1,0:T(8,128)(2,1)S(1)}, bf16[6,16,16,128]{3,2,1,0:T(8,128)(2,1)}, u32[]{:S(2)}) copy-start(bf16[6,16,16,128]{3,2,1,0:T(8,128)(2,1)} %param.9) | copy-start | bytes 1179652
  16.8 1.4 %copy-start.28 = (s32[1,256]{1,0:T(1,128)S(1)}, s32[1,256]{1,0:T(1,128)}, u32[]{:S(2)}) copy-start(s32[1,256]{1,0:T(1,128)} %param.15) | copy-start | bytes 3076
  16.8 2.9 %copy-start.29 = (f32[2,3]{1,0:T(2,128)S(1)}, f32[2,3]{1,0:T(2,128)}, u32[]{:S(2)}) copy-start(f32[2,3]{1,0:T(2,128)} %param.16) | copy-start | bytes 76
  16.9 2.9 %copy-start.17 = (bf16[16,16,128]{2,1,0:T(8,128)(2,1)S(1)}, bf16[16,16,128]{2,1,0:T(8,128)(2,1)}, u32[]{:S(2)}) copy-start(bf16[16,16,128]{2,1,0:T(8,128)(2,1)} %param.12) | copy-start | bytes 196612
  18.2 3.4 %collective-permute-start.3 = (f32[6,18,18,128]{3,2,1,0:T(8,128)}, f32[6,18,18,128]{3,2,1,0:T(8,128)}, u32[]{:S(2)}, u32[]{:S(2)}) collective-permute-start(f32[6,18,18,128]{3,2,1,0:T(8,128)} %pad_maximum_fusion.3), channel_id=1, source_target_pairs={{0,1},{1,0},{2,3},{3,2},{4,5},{5,4},{6,7},{7,6},{8,9},{9,8},{10,11... | collective-permute-start | bytes 2985992 | tf_op jit(solution)/shard_map/ppermute | solution.py:17
  19.7 13.2 %copy-start.4 = (f32[32768]{0:T(1024)}, f32[32768]{0:T(1024)S(1)}, u32[]{:S(2)}) copy-start(f32[32768]{0:T(1024)S(1)} %scatter_custom_fusion) | copy-start | bytes 393220
  19.7 11.2 %copy-start.21 = (f32[3]{0:T(128)}, f32[3]{0:T(128)S(1)}, u32[]{:S(2)}) copy-start(f32[3]{0:T(128)S(1)} %get-tuple-element.65) | copy-start | bytes 40
  19.7 11.2 %copy-start.23 = (f32[3]{0:T(128)}, f32[3]{0:T(128)S(1)}, u32[]{:S(2)}) copy-start(f32[3]{0:T(128)S(1)} %get-tuple-element.66) | copy-start | bytes 40
  19.8 9.8 %copy-start.13 = (f32[16,16,128]{2,1,0:T(8,128)}, f32[16,16,128]{2,1,0:T(8,128)S(1)}, u32[]{:S(2)}) copy-start(f32[16,16,128]{2,1,0:T(8,128)S(1)} %get-tuple-element.54) | copy-start | bytes 393220
  19.8 11.1 %copy-start.8 = (f32[16,16,128]{2,1,0:T(8,128)}, f32[16,16,128]{2,1,0:T(8,128)S(1)}, u32[]{:S(2)}) copy-start(f32[16,16,128]{2,1,0:T(8,128)S(1)} %get-tuple-element.55) | copy-start | bytes 393220
  19.8 11.1 %copy-start.10 = (f32[16,16,128]{2,1,0:T(8,128)}, f32[16,16,128]{2,1,0:T(8,128)S(1)}, u32[]{:S(2)}) copy-start(f32[16,16,128]{2,1,0:T(8,128)S(1)} %get-tuple-element.56) | copy-start | bytes 393220
  23.8 2.1 %copy-start.6 = (bf16[6,16,16,128]{3,2,1,0:T(8,128)(2,1)S(1)}, bf16[6,16,16,128]{3,2,1,0:T(8,128)(2,1)}, u32[]{:S(2)}) copy-start(bf16[6,16,16,128]{3,2,1,0:T(8,128)(2,1)} %param.10) | copy-start | bytes 1179652
  25.9 0.9 copy-start.15
  32.9 15.8 %copy-start.7 = (f32[3,16,16,128]{3,2,1,0:T(8,128)S(1)}, f32[3,16,16,128]{3,2,1,0:T(8,128)}, u32[]{:S(2)}) copy-start(f32[3,16,16,128]{3,2,1,0:T(8,128)} %get-tuple-element.51) | copy-start | bytes 1179652
  35.1 1.9 %collective-permute-start.4 = (f32[12]{0:T(128)S(1)}, f32[12]{0:T(128)S(1)}, u32[]{:S(2)}, u32[]{:S(2)}) collective-permute-start(f32[12]{0:T(128)S(1)} %pad_maximum_fusion.20), channel_id=1, source_target_pairs={{0,1},{1,0},{2,3},{3,2},{4,5},{5,4},{6,7},{7,6},{8,9},{9,8},{10,11... | collective-permute-start | bytes 152 | tf_op jit(solution)/shard_map/ppermute | solution.py:143
  35.2 3.6 %collective-permute-start.5 = (f32[12]{0:T(128)S(1)}, f32[12]{0:T(128)S(1)}, u32[]{:S(2)}, u32[]{:S(2)}) collective-permute-start(f32[12]{0:T(128)S(1)} %pad_maximum_fusion.20), channel_id=1, source_target_pairs={{0,2},{1,3},{2,0},{3,1},{4,6},{5,7},{6,4},{7,5},{8,10},{9,11},{10,... | collective-permute-start | bytes 152 | tf_op jit(solution)/shard_map/ppermute | solution.py:143
  35.6 3.2 %collective-permute-start.6 = (f32[12]{0:T(128)S(1)}, f32[12]{0:T(128)S(1)}, u32[]{:S(2)}, u32[]{:S(2)}) collective-permute-start(f32[12]{0:T(128)S(1)} %pad_maximum_fusion.20), channel_id=1, source_target_pairs={{0,3},{1,2},{2,1},{3,0},{4,7},{5,6},{6,5},{7,4},{8,11},{9,10},{10,... | collective-permute-start | bytes 152 | tf_op jit(solution)/shard_map/ppermute | solution.py:143
  38.8 4.5 %collective-permute-start.7 = (f32[12]{0:T(128)S(1)}, f32[12]{0:T(128)S(1)}, u32[]{:S(2)}, u32[]{:S(2)}) collective-permute-start(f32[12]{0:T(128)S(1)} %add_add_fusion.8), channel_id=1, source_target_pairs={{0,4},{1,5},{2,6},{3,7},{4,0},{5,1},{6,2},{7,3},{8,12},{9,13},{10,... | collective-permute-start | bytes 152 | tf_op jit(solution)/shard_map/ppermute | solution.py:143
  40.4 4.4 %collective-permute-start.8 = (f32[12]{0:T(128)S(1)}, f32[12]{0:T(128)S(1)}, u32[]{:S(2)}, u32[]{:S(2)}) collective-permute-start(f32[12]{0:T(128)S(1)} %add_add_fusion.8), channel_id=1, source_target_pairs={{0,8},{1,9},{2,10},{3,11},{4,12},{5,13},{6,14},{7,15},{8,0},{9,1},... | collective-permute-start | bytes 152 | tf_op jit(solution)/shard_map/ppermute | solution.py:143
  42.8 5.3 %collective-permute-start.9 = (f32[12]{0:T(128)S(1)}, f32[12]{0:T(128)S(1)}, u32[]{:S(2)}, u32[]{:S(2)}) collective-permute-start(f32[12]{0:T(128)S(1)} %add_add_fusion.8), channel_id=1, source_target_pairs={{0,12},{1,13},{2,14},{3,15},{4,8},{5,9},{6,10},{7,11},{8,4},{9,5},... | collective-permute-start | bytes 152 | tf_op jit(solution)/shard_map/ppermute | solution.py:143
  49.9 6.0 %collective-permute-start.10 = (f32[6,1,16,128]{3,2,1,0:T(8,128)S(1)}, f32[6,1,16,128]{3,2,1,0:T(8,128)S(1)}, u32[]{:S(2)}, u32[]{:S(2)}) collective-permute-start(f32[6,1,16,128]{3,2,1,0:T(8,128)S(1)} %get-tuple-element.50), channel_id=1, source_target_pairs={{4,0},{8,4},{12,8},{5,1},{9,5},{13,9},{6,2},{10,6},{14,10},{7,3},{... | collective-permute-start | bytes 147464 | tf_op jit(solution)/shard_map/ppermute | solution.py:33
  51.2 6.3 %collective-permute-start.11 = (f32[6,1,16,128]{3,2,1,0:T(8,128)S(1)}, f32[6,1,16,128]{3,2,1,0:T(8,128)S(1)}, u32[]{:S(2)}, u32[]{:S(2)}) collective-permute-start(f32[6,1,16,128]{3,2,1,0:T(8,128)S(1)} %get-tuple-element.49), channel_id=1, source_target_pairs={{0,4},{4,8},{8,12},{1,5},{5,9},{9,13},{2,6},{6,10},{10,14},{3,7},{... | collective-permute-start | bytes 147464 | tf_op jit(solution)/shard_map/ppermute | solution.py:32
  57.6 4.2 %collective-permute-start.12 = (f32[6,18,1,128]{3,2,1,0:T(1,128)S(1)}, f32[6,18,1,128]{3,2,1,0:T(1,128)S(1)}, u32[]{:S(2)}, u32[]{:S(2)}) collective-permute-start(f32[6,18,1,128]{3,2,1,0:T(1,128)S(1)} %broadcast_select_fusion.2), channel_id=1, source_target_pairs={{0,2},{2,0},{1,3},{3,1},{4,6},{6,4},{5,7},{7,5},{8,10},{10,8},{9,1... | collective-permute-start | bytes 165896 | tf_op jit(solution)/shard_map/ppermute | solution.py:25
  61.9 0.6 copy-start
  61.9 1.9 %copy-start.2 = (f32[6,18,1,128]{3,2,1,0:T(1,128)}, f32[6,18,1,128]{3,2,1,0:T(1,128)S(1)}, u32[]{:S(2)}) copy-start(f32[6,18,1,128]{3,2,1,0:T(1,128)S(1)} %get-tuple-element.58) | copy-start | bytes 165892
  63.8 7.4 %collective-permute-start.13 = (f32[6,18,18,128]{3,2,1,0:T(8,128)}, f32[6,18,18,128]{3,2,1,0:T(8,128)}, u32[]{:S(2)}, u32[]{:S(2)}) collective-permute-start(f32[6,18,18,128]{3,2,1,0:T(8,128)} %pad_maximum_fusion.5), channel_id=1, source_target_pairs={{0,1},{1,0},{2,3},{3,2},{4,5},{5,4},{6,7},{7,6},{8,9},{9,8},{10,11... | collective-permute-start | bytes 2985992 | tf_op jit(solution)/shard_map/ppermute | solution.py:17
  63.8 1.2 %copy-start.12 = (f32[3,16,16,128]{3,2,1,0:T(8,128)S(1)}, f32[3,16,16,128]{3,2,1,0:T(8,128)}, u32[]{:S(2)}) copy-start(f32[3,16,16,128]{3,2,1,0:T(8,128)} %get-tuple-element.15) | copy-start | bytes 1179652
  71.2 2.2 %copy-start.1 = (f32[6,18,1,128]{3,2,1,0:T(1,128)S(1)}, f32[6,18,1,128]{3,2,1,0:T(1,128)}, u32[]{:S(2)}) copy-start(f32[6,18,1,128]{3,2,1,0:T(1,128)} %copy-done) | copy-start | bytes 165892
  71.2 2.2 %copy-start.3 = (f32[6,18,1,128]{3,2,1,0:T(1,128)S(1)}, f32[6,18,1,128]{3,2,1,0:T(1,128)}, u32[]{:S(2)}) copy-start(f32[6,18,1,128]{3,2,1,0:T(1,128)} %copy-done.2) | copy-start | bytes 165892
  78.9 0.9 copy-start.5
  78.9 1.0 copy-start.9
  78.9 1.0 %copy-start.11 = (f32[16,16,128]{2,1,0:T(8,128)S(1)}, f32[16,16,128]{2,1,0:T(8,128)}, u32[]{:S(2)}) copy-start(f32[16,16,128]{2,1,0:T(8,128)} %copy-done.10) | copy-start | bytes 393220
  78.9 1.1 %copy-start.14 = (f32[16,16,128]{2,1,0:T(8,128)S(1)}, f32[16,16,128]{2,1,0:T(8,128)}, u32[]{:S(2)}) copy-start(f32[16,16,128]{2,1,0:T(8,128)} %copy-done.13) | copy-start | bytes 393220
  78.9 1.1 %copy-start.22 = (f32[3]{0:T(128)S(1)}, f32[3]{0:T(128)}, u32[]{:S(2)}) copy-start(f32[3]{0:T(128)} %copy-done.21) | copy-start | bytes 40
  79.0 1.1 %copy-start.24 = (f32[3]{0:T(128)S(1)}, f32[3]{0:T(128)}, u32[]{:S(2)}) copy-start(f32[3]{0:T(128)} %copy-done.23) | copy-start | bytes 40
  80.0 2.4 %copy-start.18 = (f32[768]{0:T(1024)S(1)}, f32[768]{0:T(1024)}, u32[]{:S(2)}) copy-start(f32[768]{0:T(1024)} %reshape.127) | copy-start | bytes 9220
  80.0 2.4 %copy-start.27 = (f32[6]{0:T(128)S(1)}, f32[6]{0:T(128)}, u32[]{:S(2)}) copy-start(f32[6]{0:T(128)} %get-tuple-element.8) | copy-start | bytes 76
  80.0 16.7 %copy-start.20 = (f32[6]{0:T(128)S(1)}, f32[6]{0:T(128)}, u32[]{:S(2)}) copy-start(f32[6]{0:T(128)} %copy-done.19) | copy-start | bytes 76
  80.0 16.7 %copy-start.26 = (f32[12]{0:T(128)S(1)}, f32[12]{0:T(128)}, u32[]{:S(2)}) copy-start(f32[12]{0:T(128)} %copy-done.25) | copy-start | bytes 148
  82.5 3.3 %collective-permute-start.14 = (f32[902]{0:T(1024)S(1)}, f32[902]{0:T(1024)S(1)}, u32[]{:S(2)}, u32[]{:S(2)}) collective-permute-start(f32[902]{0:T(1024)S(1)} %pad_maximum_fusion.19), channel_id=1, source_target_pairs={{0,1},{1,0},{2,3},{3,2},{4,5},{5,4},{6,7},{7,6},{8,9},{9,8},{10,11... | collective-permute-start | bytes 10832 | tf_op jit(solution)/shard_map/ppermute | solution.py:143
  83.0 4.4 %collective-permute-start.15 = (f32[902]{0:T(1024)S(1)}, f32[902]{0:T(1024)S(1)}, u32[]{:S(2)}, u32[]{:S(2)}) collective-permute-start(f32[902]{0:T(1024)S(1)} %pad_maximum_fusion.19), channel_id=1, source_target_pairs={{0,2},{1,3},{2,0},{3,1},{4,6},{5,7},{6,4},{7,5},{8,10},{9,11},{10,... | collective-permute-start | bytes 10832 | tf_op jit(solution)/shard_map/ppermute | solution.py:143
  85.8 3.1 %collective-permute-start.16 = (f32[902]{0:T(1024)S(1)}, f32[902]{0:T(1024)S(1)}, u32[]{:S(2)}, u32[]{:S(2)}) collective-permute-start(f32[902]{0:T(1024)S(1)} %pad_maximum_fusion.19), channel_id=1, source_target_pairs={{0,3},{1,2},{2,1},{3,0},{4,7},{5,6},{6,5},{7,4},{8,11},{9,10},{10,... | collective-permute-start | bytes 10832 | tf_op jit(solution)/shard_map/ppermute | solution.py:143
  88.9 4.8 %collective-permute-start.17 = (f32[902]{0:T(1024)S(1)}, f32[902]{0:T(1024)S(1)}, u32[]{:S(2)}, u32[]{:S(2)}) collective-permute-start(f32[902]{0:T(1024)S(1)} %add_add_fusion.5), channel_id=1, source_target_pairs={{0,4},{1,5},{2,6},{3,7},{4,0},{5,1},{6,2},{7,3},{8,12},{9,13},{10,... | collective-permute-start | bytes 10832 | tf_op jit(solution)/shard_map/ppermute | solution.py:143
  91.2 4.5 %collective-permute-start.18 = (f32[902]{0:T(1024)S(1)}, f32[902]{0:T(1024)S(1)}, u32[]{:S(2)}, u32[]{:S(2)}) collective-permute-start(f32[902]{0:T(1024)S(1)} %add_add_fusion.5), channel_id=1, source_target_pairs={{0,8},{1,9},{2,10},{3,11},{4,12},{5,13},{6,14},{7,15},{8,0},{9,1},... | collective-permute-start | bytes 10832 | tf_op jit(solution)/shard_map/ppermute | solution.py:143
  91.2 5.4 %collective-permute-start.19 = (f32[902]{0:T(1024)S(1)}, f32[902]{0:T(1024)S(1)}, u32[]{:S(2)}, u32[]{:S(2)}) collective-permute-start(f32[902]{0:T(1024)S(1)} %add_add_fusion.5), channel_id=1, source_target_pairs={{0,12},{1,13},{2,14},{3,15},{4,8},{5,9},{6,10},{7,11},{8,4},{9,5},... | collective-permute-start | bytes 10832 | tf_op jit(solution)/shard_map/ppermute | solution.py:143
  (2 other events, 1.2 us)

commit v9 on v8

--- a/solution.py
+++ b/solution.py
@@ -7,14 +7,15 @@
 RELAXATION = 0.6
 
 
-def with_halo(array, sides, width):
+def with_halo(array, sides, width, tie=None):
     for axis, dim in sides:
         peers, length = (lax.axis_size(axis), array.shape[dim])
         last = lax.slice_in_dim(array, length - width, length, axis=dim)
         initial = lax.slice_in_dim(array, 0, width, axis=dim)
         if peers == 2 and dim == array.ndim - 1:
             first = lax.axis_index(axis) == 0
-            got = lax.ppermute(array, axis, [(0, 1), (1, 0)])
+            sent = array if tie is None else array + tie
+            got = lax.ppermute(sent, axis, [(0, 1), (1, 0)])
             got_last = lax.slice_in_dim(got, length - width, length, axis=dim)
             got_initial = lax.slice_in_dim(got, 0, width, axis=dim)
             zero = jnp.zeros_like(got_last)
@@ -130,12 +131,13 @@
     return jnp.concatenate([new_real, new_imag], 0)
 
 
-def group_sum(value, axes):
+def group_rounds(value, axes):
     size = 1
     for axis in axes:
         size *= lax.axis_size(axis)
     if size & (size - 1):
-        return lax.psum(value, axes)
+        return [lax.psum(value, axes)]
+    rounds = []
     stride = 1
     while stride < size:
         if stride * 4 <= size:
@@ -148,7 +150,12 @@
         else:
             value = value + lax.ppermute(value, axes, [(i, i ^ stride) for i in range(size)])
             stride *= 2
-    return value
+        rounds.append(value)
+    return rounds
+
+
+def group_sum(value, axes):
+    return group_rounds(value, axes)[-1]
 
 
 def expand(blocks):
@@ -204,7 +211,7 @@
     response_imag = plain_imag + DAMPING * plain_real
     response = block_sums(jnp.concatenate([response_real, response_imag]))
     field = warm.astype(jnp.float32)
-    first = group_sum(
+    rounds = group_rounds(
         jnp.concatenate(
             [
                 jnp.sum(mask * field, axis=(1, 2, 3)),
@@ -214,12 +221,15 @@
         ),
         axes,
     )
+    first = rounds[-1]
     mean_field = first[:6] / count
     gain_total_real = first[6:9]
     gain_total_imag = first[9:12]
     sweep_args = (lame_first, shear, density_cells, mask, source_cells, omega_sq, impedance)
-    padded = with_halo(field, (("gx", 1), ("gy", 2), ("col", 3)), 1)
-    field = sweep(padded, *sweep_args)
+    padded = with_halo(field, (("gx", 1), ("gy", 2)), 1)
+    padded = with_halo(padded, (("col", 3),), 1, 0.0 * rounds[0][0])
+    tied_source = source_cells + 0.0 * first[0]
+    field = sweep(padded, lame_first, shear, density_cells, mask, tied_source, omega_sq, impedance)
     second_local = jnp.sum(mask * field, axis=(1, 2, 3))
     field = add_mean(field, gain_real, gain_imag, mean_field)
     padded = with_halo(field, (("gx", 1), ("gy", 2), ("col", 3)), 1)

time: 101 us -> 93.5 us (0.926)
  other arithmetic: 37.3 us -> 33.4 us
  waiting for transfers between devices: 18.6 us -> 15.4 us
  local copies, waits for them, and re-layouts: 11.6 us -> 12.8 us
  starting transfers between devices: 30.7 us -> 29.5 us
    ppermute x14, waiting for transfers between devices: 14.3 us -> 10.2 us  [the longest x12 10.2 us: group_rounds(): lax.ppermute(value, axes, [(i, i ^ m * stride) for i in range(size)])]
    concatenate x6 -> x5, other arithmetic: 8.69 us -> 6.54 us  [with_halo(): array = jnp.concatenate([before, array, after], axis=dim)]
    reshape x2, local copies, waits for them, and re-layouts: 1.17 us -> 3.23 us  [expand(): return spread.reshape(blocks_x * 8, blocks_y * 8, blocks_z * 32)]
    select_n x2, other arithmetic: 4.35 us -> 2.6 us  [with_halo(): after = jnp.where(first, got_initial, zero)]
    broadcast_in_dim x3, local copies, waits for them, and re-layouts: 0.48 us -> 2.02 us  [expand(): jnp.broadcast_to(blocks[:, None, :, None, :, None], (blocks_x, 8, blocks_...]
    reduce_sum x4, other arithmetic: 2.12 us -> 0.61 us  [block_sums(): local = local.sum(axis=(-4, -2, -1))]
    add x1 -> x2, other arithmetic: 1.31 us -> 2.64 us  [add_mean(): new_real = field[:3] + (gain_real * mean_real - gain_imag * mean_imag)]
    reduce_sum x0 -> x1, other arithmetic: none -> 1.21 us  [shards(): jnp.sum(mask * field, axis=(1, 2, 3))]
  transfers between devices with their start and end apart: 20 -> 20, of which waited for: 10 -> 8; matrix products, arithmetic and copies ran while one was open for 15% -> 20% of each run, Pallas kernels for 0% -> 0%
where the time goes in v9:
time: 93.5 us; the launch traced here: 93 us
  other arithmetic  33.4 us (36%)
  starting transfers between devices  29.5 us (32%)
  waiting for transfers between devices  15.4 us (16%)
  local copies, waits for them, and re-layouts  12.8 us (14%)
  between operations  1.96 us (2%)
    ppermute x12, starting transfers between devices, group_rounds(): lax.ppermute(value, axes, [(i, i ^ m * stride) for i in range(size)])  14.1 us
    ppermute x2, starting transfers between devices, with_halo(): before = lax.ppermute(last, axis, up)  10.3 us
    ppermute x12, waiting for transfers between devices, group_rounds(): lax.ppermute(value, axes, [(i, i ^ m * stride) for i in range(size)])  10.2 us
    concatenate x5, other arithmetic, with_halo(): array = jnp.concatenate([before, array, after], axis=dim)  6.54 us
    add x12, other arithmetic, navier(): result.append(shear * laplace[channel] + (lame_first + shear) * divergence)  5.61 us
    ppermute x2, waiting for transfers between devices, with_halo(): got = lax.ppermute(jnp.where(first, last, initial), axis, [(0, 1), (1, 0)])  3.62 us
    reshape x2, local copies, waits for them, and re-layouts, expand(): return spread.reshape(blocks_x * 8, blocks_y * 8, blocks_z * 32)  3.23 us
    add x2, other arithmetic, add_mean(): new_real = field[:3] + (gain_real * mean_real - gain_imag * mean_imag)  2.64 us
  transfers between devices with their start and end apart: 20, of which 8 were waited for; matrix products, arithmetic and copies ran while one was open for 20% of the time, Pallas kernels for 0%

profile of v9, /device:TPU:0, one launch (start us, length us, event | category | flops | bytes accessed | tf_op | source)
XLA Modules:
  0.0 93.0 jit_solution(17616813944947579630)
XLA Ops:
  0.6 1.4 %fusion.102 = (f32[6,1,16,128]{3,2,1,0:T(8,128)S(1)}, f32[6,1,16,128]{3,2,1,0:T(8,128)}) fusion(bf16[6,16,16,128]{3,2,1,0:T(8,128)(2,1)} %param.10), kind=kLoop, calls=%fused_computation.279 | loop fusion | bytes 196608 | tf_op jit(solution)/shard_map/slice | solution.py:13
  2.1 1.3 %collective-permute-start.6 = (f32[6,1,16,128]{3,2,1,0:T(8,128)}, f32[6,1,16,128]{3,2,1,0:T(8,128)S(1)}, u32[]{:S(2)}, u32[]{:S(2)}) collective-permute-start(f32[6,1,16,128]{3,2,1,0:T(8,128)} %get-tuple-element.51), channel_id=1, source_target_pairs={{4,0},{8,4},{12,8},{5,1},{9,5},{13,9},{6,2},{10,6},{14,10},{7,3},{... | collective-permute-start | bytes 147464 | tf_op jit(solution)/shard_map/ppermute | solution.py:34
  3.4 5.6 %collective-permute-start.7 = (f32[6,1,16,128]{3,2,1,0:T(8,128)S(1)}, f32[6,1,16,128]{3,2,1,0:T(8,128)S(1)}, u32[]{:S(2)}, u32[]{:S(2)}) collective-permute-start(f32[6,1,16,128]{3,2,1,0:T(8,128)S(1)} %get-tuple-element.50), channel_id=1, source_target_pairs={{0,4},{4,8},{8,12},{1,5},{5,9},{9,13},{2,6},{6,10},{10,14},{3,7},{... | collective-permute-start | bytes 147464 | tf_op jit(solution)/shard_map/ppermute | solution.py:33
  8.9 0.7 compare_select_fusion
  9.6 1.5 %scatter_custom_fusion = f32[32768]{0:T(1024)S(1)} fusion(s32[256]{0:T(256)S(1)} %bitcast.29, f32[256]{0:T(256)S(1)} %broadcast.108, f32[]{:T(128)} %constant.19.clone.1), kind=kCustom, calls=%fused_computation.248 | custom fusion | bytes 131076 | tf_op jit(solution)/shard_map/scatter | solution.py:183
  11.1 1.2 %multiply_reduce_fusion = f32[6]{0:T(128)S(1)} fusion(bf16[6,16,16,128]{3,2,1,0:T(8,128)(2,1)} %param.10, f32[16,16,128]{2,1,0:T(8,128)S(1)} %bitcast.21), kind=kLoop, calls=%fused_computation.45 | loop fusion | flops 589818 | bytes 524312 | tf_op jit(solution)/shard_map/reduce_sum | solution.py:217
  12.3 0.8 slice_bitcast_fusion.2
  13.1 0.8 select_reduce_fusion.1
  15.1 0.7 convert_multiply_fusion
  15.8 1.4 %multiply_subtract_fusion = (f32[3,16,16,128]{3,2,1,0:T(8,128)}, f32[3,16,16,128]{3,2,1,0:T(8,128)}, f32[3,16,16,128]{3,2,1,0:T(8,128)}, f32[3,16,16,128]{3,2,1,0:T(8,128)S(1)}, f32[3,16,16,128]{3,2,1,0:T(8,128)S(1)}) fusion(f32[6,16,16,128]{3,2,1,0:T(8,128)S(1)} %convert_element_type.15, f32[3]{0:T(128)S(1)} %get-tuple-element.66, ...), kind=kLoop, calls=%fused_computation.65 | loop fusion | flops 2359296 | bytes 3276824 | tf_op jit(solution)/shard_map/sub | solution.py:210
  17.6 2.0 %collective-permute-start.1 = (f32[12]{0:T(128)S(1)}, f32[12]{0:T(128)S(1)}, u32[]{:S(2)}, u32[]{:S(2)}) collective-permute-start(f32[12]{0:T(128)S(1)} %pad_maximum_fusion.19), channel_id=1, source_target_pairs={{0,2},{1,3},{2,0},{3,1},{4,6},{5,7},{6,4},{7,5},{8,10},{9,11},{10,... | collective-permute-start | bytes 152 | tf_op jit(solution)/shard_map/ppermute | solution.py:145
  19.7 0.9 broadcast_in_dim.32
  20.7 1.3 %reshape.128 = f32[1,16,16,128]{3,2,1,0:T(8,128)S(1)} reshape(f32[2,8,2,8,4,32]{5,4,3,2,1,0:T(4,128)} %broadcast_in_dim.32) | data formatting | bytes 262144 | tf_op jit(solution)/shard_map/reshape | solution.py:166
  22.0 0.9 broadcast_in_dim.33
  22.9 1.9 %reshape.129 = f32[1,16,16,128]{3,2,1,0:T(8,128)} reshape(f32[2,8,2,8,4,32]{5,4,3,2,1,0:T(4,128)} %broadcast_in_dim.33) | data formatting | bytes 262144 | tf_op jit(solution)/shard_map/reshape | solution.py:166
  24.9 1.8 %collective-permute-start.8 = (f32[6,18,1,128]{3,2,1,0:T(1,128)S(1)}, f32[6,18,1,128]{3,2,1,0:T(1,128)S(1)}, u32[]{:S(2)}, u32[]{:S(2)}) collective-permute-start(f32[6,18,1,128]{3,2,1,0:T(1,128)S(1)} %broadcast_select_fusion.5), channel_id=1, source_target_pairs={{0,2},{2,0},{1,3},{3,1},{4,6},{6,4},{5,7},{7,5},{8,10},{10,8},{9,1... | collective-permute-start | bytes 165896 | tf_op jit(solution)/shard_map/ppermute | solution.py:26
  26.7 1.6 %collective-permute-start.3 = (f32[12]{0:T(128)S(1)}, f32[12]{0:T(128)S(1)}, u32[]{:S(2)}, u32[]{:S(2)}) collective-permute-start(f32[12]{0:T(128)S(1)} %add_add_fusion.8), channel_id=1, source_target_pairs={{0,4},{1,5},{2,6},{3,7},{4,0},{5,1},{6,2},{7,3},{8,12},{9,13},{10,... | collective-permute-start | bytes 152 | tf_op jit(solution)/shard_map/ppermute | solution.py:145
  28.4 1.1 %collective-permute-start.4 = (f32[12]{0:T(128)S(1)}, f32[12]{0:T(128)S(1)}, u32[]{:S(2)}, u32[]{:S(2)}) collective-permute-start(f32[12]{0:T(128)S(1)} %add_add_fusion.8), channel_id=1, source_target_pairs={{0,8},{1,9},{2,10},{3,11},{4,12},{5,13},{6,14},{7,15},{8,0},{9,1},... | collective-permute-start | bytes 152 | tf_op jit(solution)/shard_map/ppermute | solution.py:145
  29.5 1.7 %collective-permute-start.5 = (f32[12]{0:T(128)S(1)}, f32[12]{0:T(128)S(1)}, u32[]{:S(2)}, u32[]{:S(2)}) collective-permute-start(f32[12]{0:T(128)S(1)} %add_add_fusion.8), channel_id=1, source_target_pairs={{0,12},{1,13},{2,14},{3,15},{4,8},{5,9},{6,10},{7,11},{8,4},{9,5},... | collective-permute-start | bytes 152 | tf_op jit(solution)/shard_map/ppermute | solution.py:145
  31.6 1.2 %collective-permute-done.4 = f32[12]{0:T(128)S(1)} collective-permute-done((f32[12]{0:T(128)S(1)}, f32[12]{0:T(128)S(1)}, u32[]{:S(2)}, u32[]{:S(2)}) %collective-permute-start.4) | collective-permute-done | bytes 80 | tf_op jit(solution)/shard_map/ppermute | solution.py:145
  32.8 2.0 %collective-permute-done.5 = f32[12]{0:T(128)S(1)} collective-permute-done((f32[12]{0:T(128)S(1)}, f32[12]{0:T(128)S(1)}, u32[]{:S(2)}, u32[]{:S(2)}) %collective-permute-start.5) | collective-permute-done | bytes 80 | tf_op jit(solution)/shard_map/ppermute | solution.py:145
  35.7 2.1 %pad_maximum_fusion = (f32[6,18,18,129]{3,2,1,0:T(8,128)S(1)}, f32[6,18,18,129]{3,2,1,0:T(8,128)S(1)}) fusion(f32[6,18,18,1]{3,2,1,0:T(8,128)S(1)} %get-tuple-element.36, f32[6,18,1,128]{3,2,1,0:T(1,128)S(1)} %get-tuple-element.58, f32[6,1,16,128]{3,2,1,0:T(8,128)S(1)} %collective-permute-done.6, f32[6,16,16,128]{3,2,1,0:T(8,128)S(1)} %convert_element_type.12, ...), kind=kLoop, calls=%fused_computation.1 | loop fusion | flops 2507760 | bytes 3017088 | tf_op jit(solution)/shard_map/concatenate | solution.py:35
  40.9 0.7 fusion.58
  41.9 1.3 %subtract_add_fusion.1 = (f32[3,16,16,128]{3,2,1,0:T(8,128)S(1)}, f32[3,16,16,128]{3,2,1,0:T(8,128)}, f32[3,16,16,128]{3,2,1,0:T(8,128)S(1)}, f32[3,16,16,128]{3,2,1,0:T(8,128)S(1)}) fusion(f32[3,16,16,128]{3,2,1,0:T(8,128)S(1)} %get-tuple-element.17, f32[3,16,16,128]{3,2,1,0:T(8,128)S(1)} %get-tuple-element.16, f32[3]{0:T(128)S(1)} %get-tuple-element.70, ...), kind=kLoop, calls=%fused_computation.73 | loop fusion | flops 4227072 | bytes 5242928 | tf_op jit(solution)/shard_map/add | solution.py:129
  43.2 2.0 %add_add_fusion.3 = (f32[3,16,16,128]{3,2,1,0:T(8,128)S(1)}, f32[3,16,16,128]{3,2,1,0:T(8,128)}) fusion(f32[3,16,16,128]{3,2,1,0:T(8,128)S(1)} %get-tuple-element.17, f32[3,16,16,128]{3,2,1,0:T(8,128)S(1)} %get-tuple-element.16, f32[3]{0:T(128)S(1)} %get-tuple-element.70, f32[3]{0:T(128)S(1)} %get-tuple-element.69, ...), kind=kLoop, calls=%fused_computation.71 | loop fusion | flops 1671168 | bytes 3145776 | tf_op jit(solution)/shard_map/add | solution.py:130
  45.2 1.3 %collective-permute-start.10 = (f32[6,1,16,128]{3,2,1,0:T(8,128)S(1)}, f32[6,1,16,128]{3,2,1,0:T(8,128)S(1)}, u32[]{:S(2)}, u32[]{:S(2)}) collective-permute-start(f32[6,1,16,128]{3,2,1,0:T(8,128)S(1)} %get-tuple-element.49), channel_id=1, source_target_pairs={{4,0},{8,4},{12,8},{5,1},{9,5},{13,9},{6,2},{10,6},{14,10},{7,3},{... | collective-permute-start | bytes 147464 | tf_op jit(solution)/shard_map/ppermute | solution.py:34
  46.5 4.7 %collective-permute-start.11 = (f32[6,1,16,128]{3,2,1,0:T(8,128)S(1)}, f32[6,1,16,128]{3,2,1,0:T(8,128)S(1)}, u32[]{:S(2)}, u32[]{:S(2)}) collective-permute-start(f32[6,1,16,128]{3,2,1,0:T(8,128)S(1)} %get-tuple-element.48), channel_id=1, source_target_pairs={{0,4},{4,8},{8,12},{1,5},{5,9},{9,13},{2,6},{6,10},{10,14},{3,7},{... | collective-permute-start | bytes 147464 | tf_op jit(solution)/shard_map/ppermute | solution.py:33
  51.3 1.5 %collective-permute-done.11 = f32[6,1,16,128]{3,2,1,0:T(8,128)S(1)} collective-permute-done((f32[6,1,16,128]{3,2,1,0:T(8,128)S(1)}, f32[6,1,16,128]{3,2,1,0:T(8,128)S(1)}, u32[]{:S(2)}, u32[]{:S(2)}) %collective-permute-start.11) | collective-permute-done | bytes 49184 | tf_op jit(solution)/shard_map/ppermute | solution.py:33
  53.5 3.6 %collective-permute-done.12 = f32[6,18,1,128]{3,2,1,0:T(1,128)S(1)} collective-permute-done((f32[6,18,1,128]{3,2,1,0:T(1,128)S(1)}, f32[6,18,1,128]{3,2,1,0:T(1,128)S(1)}, u32[]{:S(2)}, u32[]{:S(2)}) %collective-permute-start.12) | collective-permute-done | bytes 55328 | tf_op jit(solution)/shard_map/ppermute | solution.py:26
  57.2 1.3 %pad_maximum_fusion.4 = f32[6,18,18,128]{3,2,1,0:T(8,128)} fusion(f32[6,18,1,128]{3,2,1,0:T(1,128)S(1)} %get-tuple-element.56, f32[6,1,16,128]{3,2,1,0:T(8,128)S(1)} %collective-permute-done.10, f32[3,16,16,128]{3,2,1,0:T(8,128)S(1)} %get-tuple-element.26, f32[3,16,16,128]{3,2,1,0:T(8,128)S(1)} %get-tuple-element.22, ...), kind=kLoop, calls=%fused_computation.14 | loop fusion | flops 1244160 | bytes 1990656 | tf_op jit(solution)/shard_map/concatenate | solution.py:35
  58.5 1.0 %convert_element_type.13 = f32[6,16,16,128]{3,2,1,0:T(8,128)} convert(bf16[6,16,16,128]{3,2,1,0:T(8,128)(2,1)S(1)} %copy-done.8) | non-fusion elementwise | flops 196608 | bytes 1179648 | tf_op jit(solution)/shard_map/convert_element_type | solution.py:188
  59.4 1.2 %multiply_add_fusion = f32[3,16,16,128]{3,2,1,0:T(8,128)S(1)} fusion(f32[3,16,16,128]{3,2,1,0:T(8,128)} %get-tuple-element.15, f32[3,16,16,128]{3,2,1,0:T(8,128)} %get-tuple-element.14), kind=kLoop, calls=%fused_computation.64 | loop fusion | flops 196608 | bytes 1179648 | tf_op jit(solution)/shard_map/add | solution.py:211
  61.8 1.3 %fusion.9 = f32[6]{0:T(128)S(1)} fusion(f32[3,16,16,128]{3,2,1,0:T(8,128)} %get-tuple-element.27, f32[3,16,16,128]{3,2,1,0:T(8,128)} %get-tuple-element.23, f32[16,16,128]{2,1,0:T(8,128)S(1)} %bitcast.25), kind=kLoop, calls=%fused_computation.40 | loop fusion | flops 589818 | bytes 917528 | tf_op jit(solution)/shard_map/reduce_sum | solution.py:233
  63.3 2.2 %slice_select_fusion.1 = (f32[6,18,18,1]{3,2,1,0:T(8,128)S(1)}, f32[6,18,18,1]{3,2,1,0:T(8,128)S(1)}) fusion(f32[6,18,18,128]{3,2,1,0:T(8,128)} %collective-permute-done.13, pred[]{:T(512)S(6)} %eq.19), kind=kLoop, calls=%fused_computation.6 | loop fusion | flops 3888 | bytes 31105 | tf_op jit(solution)/shard_map/jit(_where)/select_n | solution.py:23
  65.4 2.7 %pad_maximum_fusion.1 = (f32[6,18,18,129]{3,2,1,0:T(8,128)S(1)}, f32[6,18,18,129]{3,2,1,0:T(8,128)S(1)}) fusion(f32[6,18,18,1]{3,2,1,0:T(8,128)S(1)} %get-tuple-element.34, f32[6,18,1,128]{3,2,1,0:T(1,128)S(1)} %get-tuple-element.56, f32[6,1,16,128]{3,2,1,0:T(8,128)S(1)} %collective-permute-done.10, f32[3,16,16,128]{3,2,1,0:T(8,128)S(1)} %get-tuple-element.26, ...), kind=kLoop, calls=%fused_computation.3 | loop fusion | flops 3009312 | bytes 3017088 | tf_op jit(solution)/shard_map/concatenate | solution.py:35
  71.0 0.7 fusion.22
  72.2 1.6 %subtract_reduce_fusion = (f32[16,16,128]{2,1,0:T(8,128)S(1)}, f32[3,16,16,128]{3,2,1,0:T(8,128)}, f32[3,16,16,128]{3,2,1,0:T(8,128)}) fusion(f32[6,16,16,128]{3,2,1,0:T(8,128)S(1)} %convert_element_type.15, f32[3,16,16,128]{3,2,1,0:T(8,128)S(1)} %get-tuple-element.22, f32[16,16,128]{2,1,0:T(8,128)S(1)} %copy-done.5, ...), kind=kLoop, calls=%fused_computation.68 | loop fusion | flops 5275648 | bytes 4587544 | tf_op jit(solution)/shard_map/reduce_sum | solution.py:242
  75.1 2.3 %collective-permute-start.15 = (f32[902]{0:T(1024)S(1)}, f32[902]{0:T(1024)S(1)}, u32[]{:S(2)}, u32[]{:S(2)}) collective-permute-start(f32[902]{0:T(1024)S(1)} %pad_maximum_fusion.18), channel_id=1, source_target_pairs={{0,2},{1,3},{2,0},{3,1},{4,6},{5,7},{6,4},{7,5},{8,10},{9,11},{10,... | collective-permute-start | bytes 10832 | tf_op jit(solution)/shard_map/ppermute | solution.py:145
  77.5 1.6 %collective-permute-done.15 = f32[902]{0:T(1024)S(1)} collective-permute-done((f32[902]{0:T(1024)S(1)}, f32[902]{0:T(1024)S(1)}, u32[]{:S(2)}, u32[]{:S(2)}) %collective-permute-start.15) | collective-permute-done | bytes 3640 | tf_op jit(solution)/shard_map/ppermute | solution.py:145
  79.0 1.5 %collective-permute-done.16 = f32[902]{0:T(1024)S(1)} collective-permute-done((f32[902]{0:T(1024)S(1)}, f32[902]{0:T(1024)S(1)}, u32[]{:S(2)}, u32[]{:S(2)}) %collective-permute-start.16) | collective-permute-done | bytes 3640 | tf_op jit(solution)/shard_map/ppermute | solution.py:145
  80.5 2.3 %collective-permute-start.17 = (f32[902]{0:T(1024)S(1)}, f32[902]{0:T(1024)S(1)}, u32[]{:S(2)}, u32[]{:S(2)}) collective-permute-start(f32[902]{0:T(1024)S(1)} %add_add_fusion.5), channel_id=1, source_target_pairs={{0,4},{1,5},{2,6},{3,7},{4,0},{5,1},{6,2},{7,3},{8,12},{9,13},{10,... | collective-permute-start | bytes 10832 | tf_op jit(solution)/shard_map/ppermute | solution.py:145
  82.9 1.0 %collective-permute-start.18 = (f32[902]{0:T(1024)S(1)}, f32[902]{0:T(1024)S(1)}, u32[]{:S(2)}, u32[]{:S(2)}) collective-permute-start(f32[902]{0:T(1024)S(1)} %add_add_fusion.5), channel_id=1, source_target_pairs={{0,8},{1,9},{2,10},{3,11},{4,12},{5,13},{6,14},{7,15},{8,0},{9,1},... | collective-permute-start | bytes 10832 | tf_op jit(solution)/shard_map/ppermute | solution.py:145
  83.9 1.4 %collective-permute-start.19 = (f32[902]{0:T(1024)S(1)}, f32[902]{0:T(1024)S(1)}, u32[]{:S(2)}, u32[]{:S(2)}) collective-permute-start(f32[902]{0:T(1024)S(1)} %add_add_fusion.5), channel_id=1, source_target_pairs={{0,12},{1,13},{2,14},{3,15},{4,8},{5,9},{6,10},{7,11},{8,4},{9,5},... | collective-permute-start | bytes 10832 | tf_op jit(solution)/shard_map/ppermute | solution.py:145
  85.3 2.1 %collective-permute-done.18 = f32[902]{0:T(1024)S(1)} collective-permute-done((f32[902]{0:T(1024)S(1)}, f32[902]{0:T(1024)S(1)}, u32[]{:S(2)}, u32[]{:S(2)}) %collective-permute-start.18) | collective-permute-done | bytes 3640 | tf_op jit(solution)/shard_map/ppermute | solution.py:145
  87.4 1.9 %collective-permute-done.19 = f32[902]{0:T(1024)S(1)} collective-permute-done((f32[902]{0:T(1024)S(1)}, f32[902]{0:T(1024)S(1)}, u32[]{:S(2)}, u32[]{:S(2)}) %collective-permute-start.19) | collective-permute-done | bytes 3640 | tf_op jit(solution)/shard_map/ppermute | solution.py:145
  90.0 0.7 copy.13
  90.7 1.3 %subtract_add_fusion = (f32[3,16,16,128]{3,2,1,0:T(8,128)S(1)}, f32[3,16,16,128]{3,2,1,0:T(8,128)S(1)}) fusion(f32[3,16,16,128]{3,2,1,0:T(8,128)} %get-tuple-element.11, f32[3,16,16,128]{3,2,1,0:T(8,128)S(1)} %get-tuple-element.17, f32[3,16,16,128]{3,2,1,0:T(8,128)S(1)} %get-tuple-element.16, f32[3]{0:T(128)S(1)} %get-tuple-element.68, ...), kind=kLoop, calls=%fused_computation.63 | loop fusion | flops 786432 | bytes 2359320 | tf_op jit(solution)/shard_map/add | solution.py:129
  92.0 1.0 %pad_maximum_fusion.12 = f32[6,16,16,128]{3,2,1,0:T(8,128)} fusion(f32[3,16,16,128]{3,2,1,0:T(8,128)S(1)} %get-tuple-element.47, f32[3,16,16,128]{3,2,1,0:T(8,128)S(1)} %get-tuple-element.46), kind=kLoop, calls=%fused_computation.42 | loop fusion | flops 196608 | bytes 1572864 | tf_op jit(solution)/shard_map/concatenate | solution.py:131
  (111 shorter events, 13.1 us)
Async XLA Ops:
  0.6 14.4 %copy-start.14 = (f32[2,3]{1,0:T(2,128)S(1)}, f32[2,3]{1,0:T(2,128)}, u32[]{:S(2)}) copy-start(f32[2,3]{1,0:T(2,128)} %param.16) | copy-start | bytes 76
  0.6 14.4 %copy-start.12 = (bf16[6,16,16,128]{3,2,1,0:T(8,128)(2,1)S(1)}, bf16[6,16,16,128]{3,2,1,0:T(8,128)(2,1)}, u32[]{:S(2)}) copy-start(bf16[6,16,16,128]{3,2,1,0:T(8,128)(2,1)} %param.11) | copy-start | bytes 1179652
  2.1 22.7 %collective-permute-start.6 = (f32[6,1,16,128]{3,2,1,0:T(8,128)}, f32[6,1,16,128]{3,2,1,0:T(8,128)S(1)}, u32[]{:S(2)}, u32[]{:S(2)}) collective-permute-start(f32[6,1,16,128]{3,2,1,0:T(8,128)} %get-tuple-element.51), channel_id=1, source_target_pairs={{4,0},{8,4},{12,8},{5,1},{9,5},{13,9},{6,2},{10,6},{14,10},{7,3},{... | collective-permute-start | bytes 147464 | tf_op jit(solution)/shard_map/ppermute | solution.py:34
  3.4 21.5 %collective-permute-start.7 = (f32[6,1,16,128]{3,2,1,0:T(8,128)S(1)}, f32[6,1,16,128]{3,2,1,0:T(8,128)S(1)}, u32[]{:S(2)}, u32[]{:S(2)}) collective-permute-start(f32[6,1,16,128]{3,2,1,0:T(8,128)S(1)} %get-tuple-element.50), channel_id=1, source_target_pairs={{0,4},{4,8},{8,12},{1,5},{5,9},{9,13},{2,6},{6,10},{10,14},{3,7},{... | collective-permute-start | bytes 147464 | tf_op jit(solution)/shard_map/ppermute | solution.py:33
  11.1 4.0 %copy-start.13 = (bf16[16,16,128]{2,1,0:T(8,128)(2,1)S(1)}, bf16[16,16,128]{2,1,0:T(8,128)(2,1)}, u32[]{:S(2)}) copy-start(bf16[16,16,128]{2,1,0:T(8,128)(2,1)} %param.12) | copy-start | bytes 196612
  15.8 1.4 %copy-start.3 = (f32[16,16,128]{2,1,0:T(8,128)}, f32[16,16,128]{2,1,0:T(8,128)S(1)}, u32[]{:S(2)}) copy-start(f32[16,16,128]{2,1,0:T(8,128)S(1)} %get-tuple-element.54) | copy-start | bytes 393220
  15.8 25.8 %copy-start.1 = (f32[16,16,128]{2,1,0:T(8,128)}, f32[16,16,128]{2,1,0:T(8,128)S(1)}, u32[]{:S(2)}) copy-start(f32[16,16,128]{2,1,0:T(8,128)S(1)} %get-tuple-element.53) | copy-start | bytes 393220
  15.8 3.8 %copy-start = (bf16[6,16,16,128]{3,2,1,0:T(8,128)(2,1)S(1)}, bf16[6,16,16,128]{3,2,1,0:T(8,128)(2,1)}, u32[]{:S(2)}) copy-start(bf16[6,16,16,128]{3,2,1,0:T(8,128)(2,1)} %param.10) | copy-start | bytes 1179652
  17.6 9.1 %collective-permute-start = (f32[12]{0:T(128)S(1)}, f32[12]{0:T(128)S(1)}, u32[]{:S(2)}, u32[]{:S(2)}) collective-permute-start(f32[12]{0:T(128)S(1)} %pad_maximum_fusion.19), channel_id=1, source_target_pairs={{0,1},{1,0},{2,3},{3,2},{4,5},{5,4},{6,7},{7,6},{8,9},{9,8},{10,11... | collective-permute-start | bytes 152 | tf_op jit(solution)/shard_map/ppermute | solution.py:145
  17.6 9.1 %collective-permute-start.1 = (f32[12]{0:T(128)S(1)}, f32[12]{0:T(128)S(1)}, u32[]{:S(2)}, u32[]{:S(2)}) collective-permute-start(f32[12]{0:T(128)S(1)} %pad_maximum_fusion.19), channel_id=1, source_target_pairs={{0,2},{1,3},{2,0},{3,1},{4,6},{5,7},{6,4},{7,5},{8,10},{9,11},{10,... | collective-permute-start | bytes 152 | tf_op jit(solution)/shard_map/ppermute | solution.py:145
  19.6 7.1 %collective-permute-start.2 = (f32[12]{0:T(128)S(1)}, f32[12]{0:T(128)S(1)}, u32[]{:S(2)}, u32[]{:S(2)}) collective-permute-start(f32[12]{0:T(128)S(1)} %pad_maximum_fusion.19), channel_id=1, source_target_pairs={{0,3},{1,2},{2,1},{3,0},{4,7},{5,6},{6,5},{7,4},{8,11},{9,10},{10,... | collective-permute-start | bytes 152 | tf_op jit(solution)/shard_map/ppermute | solution.py:145
  24.9 10.0 %copy-start.8 = (bf16[6,16,16,128]{3,2,1,0:T(8,128)(2,1)S(1)}, bf16[6,16,16,128]{3,2,1,0:T(8,128)(2,1)}, u32[]{:S(2)}) copy-start(bf16[6,16,16,128]{3,2,1,0:T(8,128)(2,1)} %param.9) | copy-start | bytes 1179652
  24.9 6.3 %collective-permute-start.8 = (f32[6,18,1,128]{3,2,1,0:T(1,128)S(1)}, f32[6,18,1,128]{3,2,1,0:T(1,128)S(1)}, u32[]{:S(2)}, u32[]{:S(2)}) collective-permute-start(f32[6,18,1,128]{3,2,1,0:T(1,128)S(1)} %broadcast_select_fusion.5), channel_id=1, source_target_pairs={{0,2},{2,0},{1,3},{3,1},{4,6},{6,4},{5,7},{7,5},{8,10},{10,8},{9,1... | collective-permute-start | bytes 165896 | tf_op jit(solution)/shard_map/ppermute | solution.py:26
  26.7 4.9 %collective-permute-start.3 = (f32[12]{0:T(128)S(1)}, f32[12]{0:T(128)S(1)}, u32[]{:S(2)}, u32[]{:S(2)}) collective-permute-start(f32[12]{0:T(128)S(1)} %add_add_fusion.8), channel_id=1, source_target_pairs={{0,4},{1,5},{2,6},{3,7},{4,0},{5,1},{6,2},{7,3},{8,12},{9,13},{10,... | collective-permute-start | bytes 152 | tf_op jit(solution)/shard_map/ppermute | solution.py:145
  28.4 4.4 %collective-permute-start.4 = (f32[12]{0:T(128)S(1)}, f32[12]{0:T(128)S(1)}, u32[]{:S(2)}, u32[]{:S(2)}) collective-permute-start(f32[12]{0:T(128)S(1)} %add_add_fusion.8), channel_id=1, source_target_pairs={{0,8},{1,9},{2,10},{3,11},{4,12},{5,13},{6,14},{7,15},{8,0},{9,1},... | collective-permute-start | bytes 152 | tf_op jit(solution)/shard_map/ppermute | solution.py:145
  29.5 5.3 %collective-permute-start.5 = (f32[12]{0:T(128)S(1)}, f32[12]{0:T(128)S(1)}, u32[]{:S(2)}, u32[]{:S(2)}) collective-permute-start(f32[12]{0:T(128)S(1)} %add_add_fusion.8), channel_id=1, source_target_pairs={{0,12},{1,13},{2,14},{3,15},{4,8},{5,9},{6,10},{7,11},{8,4},{9,5},... | collective-permute-start | bytes 152 | tf_op jit(solution)/shard_map/ppermute | solution.py:145
  31.5 3.7 %collective-permute-start.9 = (f32[6,18,18,128]{3,2,1,0:T(8,128)S(1)}, f32[6,18,18,128]{3,2,1,0:T(8,128)S(1)}, u32[]{:S(2)}, u32[]{:S(2)}) collective-permute-start(f32[6,18,18,128]{3,2,1,0:T(8,128)S(1)} %maximum_add_fusion), channel_id=1, source_target_pairs={{0,1},{1,0},{2,3},{3,2},{4,5},{5,4},{6,7},{7,6},{8,9},{9,8},{10,11... | collective-permute-start | bytes 2985992 | tf_op jit(solution)/shard_map/ppermute | solution.py:18
  37.8 0.9 copy-start.11
  40.9 0.9 copy-start.4
  40.9 1.0 %copy-start.9 = (f32[16,16,128]{2,1,0:T(8,128)S(1)}, f32[16,16,128]{2,1,0:T(8,128)}, u32[]{:S(2)}) copy-start(f32[16,16,128]{2,1,0:T(8,128)} %get-tuple-element.52) | copy-start | bytes 393220
  45.2 6.0 %collective-permute-start.10 = (f32[6,1,16,128]{3,2,1,0:T(8,128)S(1)}, f32[6,1,16,128]{3,2,1,0:T(8,128)S(1)}, u32[]{:S(2)}, u32[]{:S(2)}) collective-permute-start(f32[6,1,16,128]{3,2,1,0:T(8,128)S(1)} %get-tuple-element.49), channel_id=1, source_target_pairs={{4,0},{8,4},{12,8},{5,1},{9,5},{13,9},{6,2},{10,6},{14,10},{7,3},{... | collective-permute-start | bytes 147464 | tf_op jit(solution)/shard_map/ppermute | solution.py:34
  46.5 6.3 %collective-permute-start.11 = (f32[6,1,16,128]{3,2,1,0:T(8,128)S(1)}, f32[6,1,16,128]{3,2,1,0:T(8,128)S(1)}, u32[]{:S(2)}, u32[]{:S(2)}) collective-permute-start(f32[6,1,16,128]{3,2,1,0:T(8,128)S(1)} %get-tuple-element.48), channel_id=1, source_target_pairs={{0,4},{4,8},{8,12},{1,5},{5,9},{9,13},{2,6},{6,10},{10,14},{3,7},{... | collective-permute-start | bytes 147464 | tf_op jit(solution)/shard_map/ppermute | solution.py:33
  52.9 4.2 %collective-permute-start.12 = (f32[6,18,1,128]{3,2,1,0:T(1,128)S(1)}, f32[6,18,1,128]{3,2,1,0:T(1,128)S(1)}, u32[]{:S(2)}, u32[]{:S(2)}) collective-permute-start(f32[6,18,1,128]{3,2,1,0:T(1,128)S(1)} %broadcast_select_fusion.2), channel_id=1, source_target_pairs={{0,2},{2,0},{1,3},{3,1},{4,6},{6,4},{5,7},{7,5},{8,10},{10,8},{9,1... | collective-permute-start | bytes 165896 | tf_op jit(solution)/shard_map/ppermute | solution.py:26
  58.4 2.1 %copy-start.7 = (f32[3,16,16,128]{3,2,1,0:T(8,128)S(1)}, f32[3,16,16,128]{3,2,1,0:T(8,128)}, u32[]{:S(2)}) copy-start(f32[3,16,16,128]{3,2,1,0:T(8,128)} %get-tuple-element.13) | copy-start | bytes 1179652
  58.5 4.8 %collective-permute-start.13 = (f32[6,18,18,128]{3,2,1,0:T(8,128)}, f32[6,18,18,128]{3,2,1,0:T(8,128)}, u32[]{:S(2)}, u32[]{:S(2)}) collective-permute-start(f32[6,18,18,128]{3,2,1,0:T(8,128)} %pad_maximum_fusion.4), channel_id=1, source_target_pairs={{0,1},{1,0},{2,3},{3,2},{4,5},{5,4},{6,7},{7,6},{8,9},{9,8},{10,11... | collective-permute-start | bytes 2985992 | tf_op jit(solution)/shard_map/ppermute | solution.py:18
  70.9 0.9 copy-start.2
  70.9 1.0 %copy-start.5 = (f32[16,16,128]{2,1,0:T(8,128)S(1)}, f32[16,16,128]{2,1,0:T(8,128)}, u32[]{:S(2)}) copy-start(f32[16,16,128]{2,1,0:T(8,128)} %copy-done.3) | copy-start | bytes 393220
  70.9 1.3 %copy-start.6 = (f32[6,16,16,128]{3,2,1,0:T(8,128)S(1)}, f32[6,16,16,128]{3,2,1,0:T(8,128)}, u32[]{:S(2)}) copy-start(f32[6,16,16,128]{3,2,1,0:T(8,128)} %convert_element_type.13) | copy-start | bytes 2359300
  71.0 1.2 %copy-start.10 = (f32[16,16,128]{2,1,0:T(8,128)S(1)}, f32[16,16,128]{2,1,0:T(8,128)}, u32[]{:S(2)}) copy-start(f32[16,16,128]{2,1,0:T(8,128)} %get-tuple-element.52) | copy-start | bytes 393220
  74.6 2.9 %collective-permute-start.14 = (f32[902]{0:T(1024)S(1)}, f32[902]{0:T(1024)S(1)}, u32[]{:S(2)}, u32[]{:S(2)}) collective-permute-start(f32[902]{0:T(1024)S(1)} %pad_maximum_fusion.18), channel_id=1, source_target_pairs={{0,1},{1,0},{2,3},{3,2},{4,5},{5,4},{6,7},{7,6},{8,9},{9,8},{10,11... | collective-permute-start | bytes 10832 | tf_op jit(solution)/shard_map/ppermute | solution.py:145
  75.1 3.9 %collective-permute-start.15 = (f32[902]{0:T(1024)S(1)}, f32[902]{0:T(1024)S(1)}, u32[]{:S(2)}, u32[]{:S(2)}) collective-permute-start(f32[902]{0:T(1024)S(1)} %pad_maximum_fusion.18), channel_id=1, source_target_pairs={{0,2},{1,3},{2,0},{3,1},{4,6},{5,7},{6,4},{7,5},{8,10},{9,11},{10,... | collective-permute-start | bytes 10832 | tf_op jit(solution)/shard_map/ppermute | solution.py:145
  77.5 3.1 %collective-permute-start.16 = (f32[902]{0:T(1024)S(1)}, f32[902]{0:T(1024)S(1)}, u32[]{:S(2)}, u32[]{:S(2)}) collective-permute-start(f32[902]{0:T(1024)S(1)} %pad_maximum_fusion.18), channel_id=1, source_target_pairs={{0,3},{1,2},{2,1},{3,0},{4,7},{5,6},{6,5},{7,4},{8,11},{9,10},{10,... | collective-permute-start | bytes 10832 | tf_op jit(solution)/shard_map/ppermute | solution.py:145
  80.5 4.8 %collective-permute-start.17 = (f32[902]{0:T(1024)S(1)}, f32[902]{0:T(1024)S(1)}, u32[]{:S(2)}, u32[]{:S(2)}) collective-permute-start(f32[902]{0:T(1024)S(1)} %add_add_fusion.5), channel_id=1, source_target_pairs={{0,4},{1,5},{2,6},{3,7},{4,0},{5,1},{6,2},{7,3},{8,12},{9,13},{10,... | collective-permute-start | bytes 10832 | tf_op jit(solution)/shard_map/ppermute | solution.py:145
  82.9 4.5 %collective-permute-start.18 = (f32[902]{0:T(1024)S(1)}, f32[902]{0:T(1024)S(1)}, u32[]{:S(2)}, u32[]{:S(2)}) collective-permute-start(f32[902]{0:T(1024)S(1)} %add_add_fusion.5), channel_id=1, source_target_pairs={{0,8},{1,9},{2,10},{3,11},{4,12},{5,13},{6,14},{7,15},{8,0},{9,1},... | collective-permute-start | bytes 10832 | tf_op jit(solution)/shard_map/ppermute | solution.py:145
  83.9 5.4 %collective-permute-start.19 = (f32[902]{0:T(1024)S(1)}, f32[902]{0:T(1024)S(1)}, u32[]{:S(2)}, u32[]{:S(2)}) collective-permute-start(f32[902]{0:T(1024)S(1)} %add_add_fusion.5), channel_id=1, source_target_pairs={{0,12},{1,13},{2,14},{3,15},{4,8},{5,9},{6,10},{7,11},{8,4},{9,5},... | collective-permute-start | bytes 10832 | tf_op jit(solution)/shard_map/ppermute | solution.py:145

commit v10 on v9

--- a/solution.py
+++ b/solution.py
@@ -131,7 +131,7 @@
     return jnp.concatenate([new_real, new_imag], 0)
 
 
-def group_rounds(value, axes):
+def group_rounds(value, axes, radix=4):
     size = 1
     for axis in axes:
         size *= lax.axis_size(axis)
@@ -140,7 +140,7 @@
     rounds = []
     stride = 1
     while stride < size:
-        if stride * 4 <= size:
+        if radix == 4 and stride * 4 <= size:
             got = [
                 lax.ppermute(value, axes, [(i, i ^ (m * stride)) for i in range(size)])
                 for m in (1, 2, 3)
@@ -220,6 +220,7 @@
             ]
         ),
         axes,
+        radix=2,
     )
     first = rounds[-1]
     mean_field = first[:6] / count
@@ -227,7 +228,7 @@
     gain_total_imag = first[9:12]
     sweep_args = (lame_first, shear, density_cells, mask, source_cells, omega_sq, impedance)
     padded = with_halo(field, (("gx", 1), ("gy", 2)), 1)
-    padded = with_halo(padded, (("col", 3),), 1, 0.0 * rounds[0][0])
+    padded = with_halo(padded, (("col", 3),), 1, 0.0 * rounds[(len(rounds) - 1) // 2][0])
     tied_source = source_cells + 0.0 * first[0]
     field = sweep(padded, lame_first, shear, density_cells, mask, tied_source, omega_sq, impedance)
     second_local = jnp.sum(mask * field, axis=(1, 2, 3))

time: 93.5 us -> 102 us (1.091)
  waiting for transfers between devices: 15.4 us -> 19.8 us
  other arithmetic: 33.4 us -> 37.3 us
    ppermute x0 -> x4, waiting for transfers between devices: none -> 6.5 us  [group_rounds(): lax.ppermute(value, axes, [(i, i ^ stride) for i in range(size)])]
    ppermute x12 -> x6, starting transfers between devices: 14.1 us -> 8 us  [group_rounds(): lax.ppermute(value, axes, [(i, i ^ m * stride) for i in range(size)])]
    ppermute x0 -> x4, starting transfers between devices: none -> 5.04 us  [group_rounds(): lax.ppermute(value, axes, [(i, i ^ stride) for i in range(size)])]
    ppermute x12 -> x6, waiting for transfers between devices: 10.2 us -> 8.45 us  [group_rounds(): lax.ppermute(value, axes, [(i, i ^ m * stride) for i in range(size)])]
    select_n x2, other arithmetic: 2.6 us -> 4.31 us  [with_halo(): after = jnp.where(first, got_initial, zero)]
    add x1, other arithmetic: 0.23 us -> 1.31 us  [with_halo(): sent = array if tie is None else array + tie]
    unnamed x31 -> x39, local copies, waits for them, and re-layouts: 1.84 us -> 2.38 us
  transfers between devices with their start and end apart: 20 -> 18, of which waited for: 8 -> 9; matrix products, arithmetic and copies ran while one was open for 20% -> 19% of each run, Pallas kernels for 0% -> 0%
where the time goes in v10:
time: 102 us; the launch traced here: 101 us
  other arithmetic  37.3 us (37%)
  starting transfers between devices  28.8 us (28%)
  waiting for transfers between devices  19.8 us (19%)
  local copies, waits for them, and re-layouts  13.3 us (13%)
  between operations  1.95 us (2%)
    ppermute x2, starting transfers between devices, with_halo(): before = lax.ppermute(last, axis, up)  10.3 us
    ppermute x6, waiting for transfers between devices, group_rounds(): lax.ppermute(value, axes, [(i, i ^ m * stride) for i in range(size)])  8.45 us
    ppermute x6, starting transfers between devices, group_rounds(): lax.ppermute(value, axes, [(i, i ^ m * stride) for i in range(size)])  8 us
    concatenate x5, other arithmetic, with_halo(): array = jnp.concatenate([before, array, after], axis=dim)  6.55 us
    ppermute x4, waiting for transfers between devices, group_rounds(): lax.ppermute(value, axes, [(i, i ^ stride) for i in range(size)])  6.5 us
    add x12, other arithmetic, navier(): result.append(shear * laplace[channel] + (lame_first + shear) * divergence)  5.61 us
    ppermute x4, starting transfers between devices, group_rounds(): lax.ppermute(value, axes, [(i, i ^ stride) for i in range(size)])  5.04 us
    select_n x2, other arithmetic, with_halo(): after = jnp.where(first, got_initial, zero)  4.31 us
  transfers between devices with their start and end apart: 18, of which 9 were waited for; matrix products, arithmetic and copies ran while one was open for 19% of the time, Pallas kernels for 0%

profile of v10, /device:TPU:0, one launch (start us, length us, event | category | flops | bytes accessed | tf_op | source)
XLA Modules:
  0.0 101.2 jit_solution(14771920138423615078)
XLA Ops:
  0.6 1.4 %fusion.102 = (f32[6,1,16,128]{3,2,1,0:T(8,128)S(1)}, f32[6,1,16,128]{3,2,1,0:T(8,128)}) fusion(bf16[6,16,16,128]{3,2,1,0:T(8,128)(2,1)} %param.10), kind=kLoop, calls=%fused_computation.277 | loop fusion | bytes 196608 | tf_op jit(solution)/shard_map/slice | solution.py:13
  2.1 1.3 %collective-permute-start.4 = (f32[6,1,16,128]{3,2,1,0:T(8,128)}, f32[6,1,16,128]{3,2,1,0:T(8,128)S(1)}, u32[]{:S(2)}, u32[]{:S(2)}) collective-permute-start(f32[6,1,16,128]{3,2,1,0:T(8,128)} %get-tuple-element.51), channel_id=1, source_target_pairs={{4,0},{8,4},{12,8},{5,1},{9,5},{13,9},{6,2},{10,6},{14,10},{7,3},{... | collective-permute-start | bytes 147464 | tf_op jit(solution)/shard_map/ppermute | solution.py:34
  3.4 5.6 %collective-permute-start.5 = (f32[6,1,16,128]{3,2,1,0:T(8,128)S(1)}, f32[6,1,16,128]{3,2,1,0:T(8,128)S(1)}, u32[]{:S(2)}, u32[]{:S(2)}) collective-permute-start(f32[6,1,16,128]{3,2,1,0:T(8,128)S(1)} %get-tuple-element.50), channel_id=1, source_target_pairs={{0,4},{4,8},{8,12},{1,5},{5,9},{9,13},{2,6},{6,10},{10,14},{3,7},{... | collective-permute-start | bytes 147464 | tf_op jit(solution)/shard_map/ppermute | solution.py:33
  8.9 0.7 compare_select_fusion
  9.6 1.5 %scatter_custom_fusion = f32[32768]{0:T(1024)S(1)} fusion(s32[256]{0:T(256)S(1)} %bitcast.28, f32[256]{0:T(256)S(1)} %broadcast.108, f32[]{:T(128)} %constant.19.clone.1), kind=kCustom, calls=%fused_computation.248 | custom fusion | bytes 131076 | tf_op jit(solution)/shard_map/scatter | solution.py:183
  11.1 1.2 %multiply_reduce_fusion = f32[6]{0:T(128)S(1)} fusion(bf16[6,16,16,128]{3,2,1,0:T(8,128)(2,1)} %param.10, f32[16,16,128]{2,1,0:T(8,128)S(1)} %bitcast.21), kind=kLoop, calls=%fused_computation.45 | loop fusion | flops 589818 | bytes 524312 | tf_op jit(solution)/shard_map/reduce_sum | solution.py:217
  12.3 0.8 slice_bitcast_fusion.2
  13.1 0.8 select_reduce_fusion.1
  15.2 0.7 convert_multiply_fusion
  15.8 1.4 %multiply_subtract_fusion = (f32[3,16,16,128]{3,2,1,0:T(8,128)}, f32[3,16,16,128]{3,2,1,0:T(8,128)}, f32[3,16,16,128]{3,2,1,0:T(8,128)}, f32[3,16,16,128]{3,2,1,0:T(8,128)S(1)}, f32[3,16,16,128]{3,2,1,0:T(8,128)S(1)}) fusion(f32[6,16,16,128]{3,2,1,0:T(8,128)S(1)} %convert_element_type.15, f32[3]{0:T(128)S(1)} %get-tuple-element.66, ...), kind=kLoop, calls=%fused_computation.65 | loop fusion | flops 2359296 | bytes 3276824 | tf_op jit(solution)/shard_map/sub | solution.py:210
  17.8 2.0 %collective-permute-start.6 = (f32[6,18,1,128]{3,2,1,0:T(1,128)S(1)}, f32[6,18,1,128]{3,2,1,0:T(1,128)S(1)}, u32[]{:S(2)}, u32[]{:S(2)}) collective-permute-start(f32[6,18,1,128]{3,2,1,0:T(1,128)S(1)} %broadcast_select_fusion.5), channel_id=1, source_target_pairs={{0,2},{2,0},{1,3},{3,1},{4,6},{6,4},{5,7},{7,5},{8,10},{10,8},{9,1... | collective-permute-start | bytes 165896 | tf_op jit(solution)/shard_map/ppermute | solution.py:26
  19.9 0.9 collective-permute-start.1
  20.7 2.7 %collective-permute-done.1 = f32[12]{0:T(128)S(1)} collective-permute-done((f32[12]{0:T(128)S(1)}, f32[12]{0:T(128)S(1)}, u32[]{:S(2)}, u32[]{:S(2)}) %collective-permute-start.1) | collective-permute-done | bytes 80 | tf_op jit(solution)/shard_map/ppermute | solution.py:151
  23.6 1.3 %maximum_add_fusion = f32[6,18,18,128]{3,2,1,0:T(8,128)} fusion(f32[6,18,1,128]{3,2,1,0:T(1,128)S(1)} %get-tuple-element.58, f32[6,1,16,128]{3,2,1,0:T(8,128)S(1)} %collective-permute-done.4, f32[6,16,16,128]{3,2,1,0:T(8,128)S(1)} %convert_element_type.12, f32[6,1,16,128]{3,2,1,0:T(8,128)S(1)} %collective-permute-done.5, ...), kind=kLoop, calls=%fused_computation.11 | loop fusion | flops 1244160 | bytes 1990660 | tf_op jit(solution)/shard_map/add | solution.py:17
  24.9 0.9 broadcast_in_dim.32
  25.8 1.3 %reshape.128 = f32[1,16,16,128]{3,2,1,0:T(8,128)S(1)} reshape(f32[2,8,2,8,4,32]{5,4,3,2,1,0:T(4,128)} %broadcast_in_dim.32) | data formatting | bytes 262144 | tf_op jit(solution)/shard_map/reshape | solution.py:166
  27.1 0.9 broadcast_in_dim.33
  28.0 1.9 %reshape.129 = f32[1,16,16,128]{3,2,1,0:T(8,128)} reshape(f32[2,8,2,8,4,32]{5,4,3,2,1,0:T(4,128)} %broadcast_in_dim.33) | data formatting | bytes 262144 | tf_op jit(solution)/shard_map/reshape | solution.py:166
  30.0 1.6 %collective-permute-start.2 = (f32[12]{0:T(128)S(1)}, f32[12]{0:T(128)S(1)}, u32[]{:S(2)}, u32[]{:S(2)}) collective-permute-start(f32[12]{0:T(128)S(1)} %add.479), channel_id=1, source_target_pairs={{0,4},{1,5},{2,6},{3,7},{4,0},{5,1},{6,2},{7,3},{8,12},{9,13},{10,... | collective-permute-start | bytes 152 | tf_op jit(solution)/shard_map/ppermute | solution.py:151
  31.6 2.0 %collective-permute-done.2 = f32[12]{0:T(128)S(1)} collective-permute-done((f32[12]{0:T(128)S(1)}, f32[12]{0:T(128)S(1)}, u32[]{:S(2)}, u32[]{:S(2)}) %collective-permute-start.2) | collective-permute-done | bytes 80 | tf_op jit(solution)/shard_map/ppermute | solution.py:151
  33.5 2.6 %collective-permute-start.3 = (f32[12]{0:T(128)S(1)}, f32[12]{0:T(128)S(1)}, u32[]{:S(2)}, u32[]{:S(2)}) collective-permute-start(f32[12]{0:T(128)S(1)} %add.480), channel_id=1, source_target_pairs={{0,8},{1,9},{2,10},{3,11},{4,12},{5,13},{6,14},{7,15},{8,0},{9,1},... | collective-permute-start | bytes 152 | tf_op jit(solution)/shard_map/ppermute | solution.py:151
  36.1 1.9 %collective-permute-done.3 = f32[12]{0:T(128)S(1)} collective-permute-done((f32[12]{0:T(128)S(1)}, f32[12]{0:T(128)S(1)}, u32[]{:S(2)}, u32[]{:S(2)}) %collective-permute-start.3) | collective-permute-done | bytes 80 | tf_op jit(solution)/shard_map/ppermute | solution.py:151
  38.6 1.1 %broadcast_add_fusion = f32[6,16,16,128]{3,2,1,0:T(8,128)S(1)} fusion(f32[]{:T(128)} %bitcast.8, bf16[6,16,16,128]{3,2,1,0:T(8,128)(2,1)} %param.9), kind=kLoop, calls=%fused_computation.75 | loop fusion | flops 393216 | bytes 1179652 | tf_op jit(solution)/shard_map/add | solution.py:232
  39.9 2.2 %slice_select_fusion.3 = (f32[6,18,18,1]{3,2,1,0:T(8,128)S(1)}, f32[6,18,18,1]{3,2,1,0:T(8,128)S(1)}) fusion(f32[6,18,18,128]{3,2,1,0:T(8,128)} %collective-permute-done.7, pred[]{:T(512)S(6)} %eq.19), kind=kLoop, calls=%fused_computation.8 | loop fusion | flops 3888 | bytes 31105 | tf_op jit(solution)/shard_map/jit(_where)/select_n | solution.py:23
  42.1 2.1 %pad_maximum_fusion = (f32[6,18,18,129]{3,2,1,0:T(8,128)S(1)}, f32[6,18,18,129]{3,2,1,0:T(8,128)S(1)}) fusion(f32[6,18,18,1]{3,2,1,0:T(8,128)S(1)} %get-tuple-element.36, f32[6,18,1,128]{3,2,1,0:T(1,128)S(1)} %get-tuple-element.58, f32[6,1,16,128]{3,2,1,0:T(8,128)S(1)} %collective-permute-done.4, f32[6,16,16,128]{3,2,1,0:T(8,128)S(1)} %convert_element_type.12, ...), kind=kLoop, calls=%fused_computation.1 | loop fusion | flops 2507760 | bytes 3017088 | tf_op jit(solution)/shard_map/concatenate | solution.py:35
  48.3 1.4 %subtract_add_fusion.1 = (f32[3,16,16,128]{3,2,1,0:T(8,128)S(1)}, f32[3,16,16,128]{3,2,1,0:T(8,128)}, f32[3,16,16,128]{3,2,1,0:T(8,128)S(1)}, f32[3,16,16,128]{3,2,1,0:T(8,128)S(1)}) fusion(f32[3,16,16,128]{3,2,1,0:T(8,128)S(1)} %get-tuple-element.17, f32[3,16,16,128]{3,2,1,0:T(8,128)S(1)} %get-tuple-element.16, f32[3]{0:T(128)S(1)} %get-tuple-element.70, ...), kind=kLoop, calls=%fused_computation.73 | loop fusion | flops 4227072 | bytes 5242928 | tf_op jit(solution)/shard_map/add | solution.py:129
  49.6 2.0 %add_add_fusion.3 = (f32[3,16,16,128]{3,2,1,0:T(8,128)S(1)}, f32[3,16,16,128]{3,2,1,0:T(8,128)}) fusion(f32[3,16,16,128]{3,2,1,0:T(8,128)S(1)} %get-tuple-element.17, f32[3,16,16,128]{3,2,1,0:T(8,128)S(1)} %get-tuple-element.16, f32[3]{0:T(128)S(1)} %get-tuple-element.70, f32[3]{0:T(128)S(1)} %get-tuple-element.69, ...), kind=kLoop, calls=%fused_computation.71 | loop fusion | flops 1671168 | bytes 3145776 | tf_op jit(solution)/shard_map/add | solution.py:130
  51.6 1.3 %collective-permute-start.8 = (f32[6,1,16,128]{3,2,1,0:T(8,128)S(1)}, f32[6,1,16,128]{3,2,1,0:T(8,128)S(1)}, u32[]{:S(2)}, u32[]{:S(2)}) collective-permute-start(f32[6,1,16,128]{3,2,1,0:T(8,128)S(1)} %get-tuple-element.49), channel_id=1, source_target_pairs={{4,0},{8,4},{12,8},{5,1},{9,5},{13,9},{6,2},{10,6},{14,10},{7,3},{... | collective-permute-start | bytes 147464 | tf_op jit(solution)/shard_map/ppermute | solution.py:34
  52.9 4.7 %collective-permute-start.9 = (f32[6,1,16,128]{3,2,1,0:T(8,128)S(1)}, f32[6,1,16,128]{3,2,1,0:T(8,128)S(1)}, u32[]{:S(2)}, u32[]{:S(2)}) collective-permute-start(f32[6,1,16,128]{3,2,1,0:T(8,128)S(1)} %get-tuple-element.48), channel_id=1, source_target_pairs={{0,4},{4,8},{8,12},{1,5},{5,9},{9,13},{2,6},{6,10},{10,14},{3,7},{... | collective-permute-start | bytes 147464 | tf_op jit(solution)/shard_map/ppermute | solution.py:33
  57.7 1.5 %collective-permute-done.9 = f32[6,1,16,128]{3,2,1,0:T(8,128)S(1)} collective-permute-done((f32[6,1,16,128]{3,2,1,0:T(8,128)S(1)}, f32[6,1,16,128]{3,2,1,0:T(8,128)S(1)}, u32[]{:S(2)}, u32[]{:S(2)}) %collective-permute-start.9) | collective-permute-done | bytes 49184 | tf_op jit(solution)/shard_map/ppermute | solution.py:33
  59.3 0.9 collective-permute-start.10
  60.2 3.3 %collective-permute-done.10 = f32[6,18,1,128]{3,2,1,0:T(1,128)S(1)} collective-permute-done((f32[6,18,1,128]{3,2,1,0:T(1,128)S(1)}, f32[6,18,1,128]{3,2,1,0:T(1,128)S(1)}, u32[]{:S(2)}, u32[]{:S(2)}) %collective-permute-start.10) | collective-permute-done | bytes 55328 | tf_op jit(solution)/shard_map/ppermute | solution.py:26
  63.6 1.3 %pad_maximum_fusion.4 = f32[6,18,18,128]{3,2,1,0:T(8,128)} fusion(f32[6,18,1,128]{3,2,1,0:T(1,128)S(1)} %get-tuple-element.56, f32[6,1,16,128]{3,2,1,0:T(8,128)S(1)} %collective-permute-done.8, f32[3,16,16,128]{3,2,1,0:T(8,128)S(1)} %get-tuple-element.26, f32[3,16,16,128]{3,2,1,0:T(8,128)S(1)} %get-tuple-element.22, ...), kind=kLoop, calls=%fused_computation.14 | loop fusion | flops 1244160 | bytes 1990656 | tf_op jit(solution)/shard_map/concatenate | solution.py:35
  64.9 1.0 convert_element_type.13
  65.9 1.2 %multiply_add_fusion = f32[3,16,16,128]{3,2,1,0:T(8,128)S(1)} fusion(f32[3,16,16,128]{3,2,1,0:T(8,128)} %get-tuple-element.15, f32[3,16,16,128]{3,2,1,0:T(8,128)} %get-tuple-element.14), kind=kLoop, calls=%fused_computation.64 | loop fusion | flops 196608 | bytes 1179648 | tf_op jit(solution)/shard_map/add | solution.py:211
  68.2 1.3 %fusion.9 = f32[6]{0:T(128)S(1)} fusion(f32[3,16,16,128]{3,2,1,0:T(8,128)} %get-tuple-element.27, f32[3,16,16,128]{3,2,1,0:T(8,128)} %get-tuple-element.23, f32[16,16,128]{2,1,0:T(8,128)S(1)} %bitcast.25), kind=kLoop, calls=%fused_computation.40 | loop fusion | flops 589818 | bytes 917528 | tf_op jit(solution)/shard_map/reduce_sum | solution.py:234
  69.7 2.2 %slice_select_fusion.1 = (f32[6,18,18,1]{3,2,1,0:T(8,128)S(1)}, f32[6,18,18,1]{3,2,1,0:T(8,128)S(1)}) fusion(f32[6,18,18,128]{3,2,1,0:T(8,128)} %collective-permute-done.11, pred[]{:T(512)S(6)} %eq.19), kind=kLoop, calls=%fused_computation.6 | loop fusion | flops 3888 | bytes 31105 | tf_op jit(solution)/shard_map/jit(_where)/select_n | solution.py:23
  71.9 2.7 %pad_maximum_fusion.1 = (f32[6,18,18,129]{3,2,1,0:T(8,128)S(1)}, f32[6,18,18,129]{3,2,1,0:T(8,128)S(1)}) fusion(f32[6,18,18,1]{3,2,1,0:T(8,128)S(1)} %get-tuple-element.34, f32[6,18,1,128]{3,2,1,0:T(1,128)S(1)} %get-tuple-element.56, f32[6,1,16,128]{3,2,1,0:T(8,128)S(1)} %collective-permute-done.8, f32[3,16,16,128]{3,2,1,0:T(8,128)S(1)} %get-tuple-element.26, ...), kind=kLoop, calls=%fused_computation.3 | loop fusion | flops 3009312 | bytes 3017088 | tf_op jit(solution)/shard_map/concatenate | solution.py:35
  78.6 1.6 %subtract_reduce_fusion = (f32[16,16,128]{2,1,0:T(8,128)S(1)}, f32[3,16,16,128]{3,2,1,0:T(8,128)}, f32[3,16,16,128]{3,2,1,0:T(8,128)}) fusion(f32[6,16,16,128]{3,2,1,0:T(8,128)S(1)} %convert_element_type.15, f32[3,16,16,128]{3,2,1,0:T(8,128)S(1)} %get-tuple-element.22, f32[16,16,128]{2,1,0:T(8,128)S(1)} %copy-done.5, ...), kind=kLoop, calls=%fused_computation.68 | loop fusion | flops 5275648 | bytes 4587544 | tf_op jit(solution)/shard_map/reduce_sum | solution.py:243
  81.6 2.7 %collective-permute-start.13 = (f32[902]{0:T(1024)S(1)}, f32[902]{0:T(1024)S(1)}, u32[]{:S(2)}, u32[]{:S(2)}) collective-permute-start(f32[902]{0:T(1024)S(1)} %pad_maximum_fusion.18), channel_id=1, source_target_pairs={{0,2},{1,3},{2,0},{3,1},{4,6},{5,7},{6,4},{7,5},{8,10},{9,11},{10,... | collective-permute-start | bytes 10832 | tf_op jit(solution)/shard_map/ppermute | solution.py:145
  84.2 1.6 %collective-permute-done.13 = f32[902]{0:T(1024)S(1)} collective-permute-done((f32[902]{0:T(1024)S(1)}, f32[902]{0:T(1024)S(1)}, u32[]{:S(2)}, u32[]{:S(2)}) %collective-permute-start.13) | collective-permute-done | bytes 3640 | tf_op jit(solution)/shard_map/ppermute | solution.py:145
  85.8 1.5 %collective-permute-done.14 = f32[902]{0:T(1024)S(1)} collective-permute-done((f32[902]{0:T(1024)S(1)}, f32[902]{0:T(1024)S(1)}, u32[]{:S(2)}, u32[]{:S(2)}) %collective-permute-start.14) | collective-permute-done | bytes 3640 | tf_op jit(solution)/shard_map/ppermute | solution.py:145
  87.3 2.3 %collective-permute-start.15 = (f32[902]{0:T(1024)S(1)}, f32[902]{0:T(1024)S(1)}, u32[]{:S(2)}, u32[]{:S(2)}) collective-permute-start(f32[902]{0:T(1024)S(1)} %add_add_fusion.5), channel_id=1, source_target_pairs={{0,4},{1,5},{2,6},{3,7},{4,0},{5,1},{6,2},{7,3},{8,12},{9,13},{10,... | collective-permute-start | bytes 10832 | tf_op jit(solution)/shard_map/ppermute | solution.py:145
  89.6 2.5 %collective-permute-start.16 = (f32[902]{0:T(1024)S(1)}, f32[902]{0:T(1024)S(1)}, u32[]{:S(2)}, u32[]{:S(2)}) collective-permute-start(f32[902]{0:T(1024)S(1)} %add_add_fusion.5), channel_id=1, source_target_pairs={{0,8},{1,9},{2,10},{3,11},{4,12},{5,13},{6,14},{7,15},{8,0},{9,1},... | collective-permute-start | bytes 10832 | tf_op jit(solution)/shard_map/ppermute | solution.py:145
  92.1 2.0 %collective-permute-done.16 = f32[902]{0:T(1024)S(1)} collective-permute-done((f32[902]{0:T(1024)S(1)}, f32[902]{0:T(1024)S(1)}, u32[]{:S(2)}, u32[]{:S(2)}) %collective-permute-start.16) | collective-permute-done | bytes 3640 | tf_op jit(solution)/shard_map/ppermute | solution.py:145
  94.1 3.4 %collective-permute-done.17 = f32[902]{0:T(1024)S(1)} collective-permute-done((f32[902]{0:T(1024)S(1)}, f32[902]{0:T(1024)S(1)}, u32[]{:S(2)}, u32[]{:S(2)}) %collective-permute-start.17) | collective-permute-done | bytes 3640 | tf_op jit(solution)/shard_map/ppermute | solution.py:145
  98.9 1.3 %subtract_add_fusion = (f32[3,16,16,128]{3,2,1,0:T(8,128)S(1)}, f32[3,16,16,128]{3,2,1,0:T(8,128)S(1)}) fusion(f32[3,16,16,128]{3,2,1,0:T(8,128)} %get-tuple-element.11, f32[3,16,16,128]{3,2,1,0:T(8,128)S(1)} %get-tuple-element.17, f32[3,16,16,128]{3,2,1,0:T(8,128)S(1)} %get-tuple-element.16, f32[3]{0:T(128)S(1)} %get-tuple-element.68, ...), kind=kLoop, calls=%fused_computation.63 | loop fusion | flops 786432 | bytes 2359320 | tf_op jit(solution)/shard_map/add | solution.py:129
  100.2 1.0 pad_maximum_fusion.12
  (117 shorter events, 14.2 us)
Async XLA Ops:
  0.6 14.4 %copy-start.18 = (f32[2,3]{1,0:T(2,128)S(1)}, f32[2,3]{1,0:T(2,128)}, u32[]{:S(2)}) copy-start(f32[2,3]{1,0:T(2,128)} %param.16) | copy-start | bytes 76
  0.6 14.4 %copy-start.12 = (bf16[6,16,16,128]{3,2,1,0:T(8,128)(2,1)S(1)}, bf16[6,16,16,128]{3,2,1,0:T(8,128)(2,1)}, u32[]{:S(2)}) copy-start(bf16[6,16,16,128]{3,2,1,0:T(8,128)(2,1)} %param.11) | copy-start | bytes 1179652
  2.1 15.6 %collective-permute-start.4 = (f32[6,1,16,128]{3,2,1,0:T(8,128)}, f32[6,1,16,128]{3,2,1,0:T(8,128)S(1)}, u32[]{:S(2)}, u32[]{:S(2)}) collective-permute-start(f32[6,1,16,128]{3,2,1,0:T(8,128)} %get-tuple-element.51), channel_id=1, source_target_pairs={{4,0},{8,4},{12,8},{5,1},{9,5},{13,9},{6,2},{10,6},{14,10},{7,3},{... | collective-permute-start | bytes 147464 | tf_op jit(solution)/shard_map/ppermute | solution.py:34
  3.4 14.3 %collective-permute-start.5 = (f32[6,1,16,128]{3,2,1,0:T(8,128)S(1)}, f32[6,1,16,128]{3,2,1,0:T(8,128)S(1)}, u32[]{:S(2)}, u32[]{:S(2)}) collective-permute-start(f32[6,1,16,128]{3,2,1,0:T(8,128)S(1)} %get-tuple-element.50), channel_id=1, source_target_pairs={{0,4},{4,8},{8,12},{1,5},{5,9},{9,13},{2,6},{6,10},{10,14},{3,7},{... | collective-permute-start | bytes 147464 | tf_op jit(solution)/shard_map/ppermute | solution.py:33
  11.1 4.0 %copy-start.13 = (bf16[16,16,128]{2,1,0:T(8,128)(2,1)S(1)}, bf16[16,16,128]{2,1,0:T(8,128)(2,1)}, u32[]{:S(2)}) copy-start(bf16[16,16,128]{2,1,0:T(8,128)(2,1)} %param.12) | copy-start | bytes 196612
  12.3 5.2 %copy-start.14 = (f32[6]{0:T(128)}, f32[6]{0:T(128)S(1)}, u32[]{:S(2)}) copy-start(f32[6]{0:T(128)S(1)} %multiply_reduce_fusion) | copy-start | bytes 76
  15.8 1.4 %copy-start.3 = (f32[16,16,128]{2,1,0:T(8,128)}, f32[16,16,128]{2,1,0:T(8,128)S(1)}, u32[]{:S(2)}) copy-start(f32[16,16,128]{2,1,0:T(8,128)S(1)} %get-tuple-element.54) | copy-start | bytes 393220
  15.8 32.1 %copy-start.1 = (f32[16,16,128]{2,1,0:T(8,128)}, f32[16,16,128]{2,1,0:T(8,128)S(1)}, u32[]{:S(2)}) copy-start(f32[16,16,128]{2,1,0:T(8,128)S(1)} %get-tuple-element.53) | copy-start | bytes 393220
  15.8 1.8 %copy-start = (bf16[6,16,16,128]{3,2,1,0:T(8,128)(2,1)S(1)}, bf16[6,16,16,128]{3,2,1,0:T(8,128)(2,1)}, u32[]{:S(2)}) copy-start(bf16[6,16,16,128]{3,2,1,0:T(8,128)(2,1)} %param.10) | copy-start | bytes 1179652
  17.6 2.2 %copy-start.15 = (f32[6]{0:T(128)S(1)}, f32[6]{0:T(128)}, u32[]{:S(2)}) copy-start(f32[6]{0:T(128)} %copy-done.14) | copy-start | bytes 76
  17.6 2.2 %collective-permute-start = (f32[12]{0:T(128)S(1)}, f32[12]{0:T(128)S(1)}, u32[]{:S(2)}, u32[]{:S(2)}) collective-permute-start(f32[12]{0:T(128)S(1)} %pad_maximum_fusion.19), channel_id=1, source_target_pairs={{0,1},{1,0},{2,3},{3,2},{4,5},{5,4},{6,7},{7,6},{8,9},{9,8},{10,11... | collective-permute-start | bytes 152 | tf_op jit(solution)/shard_map/ppermute | solution.py:151
  17.8 5.7 %collective-permute-start.6 = (f32[6,18,1,128]{3,2,1,0:T(1,128)S(1)}, f32[6,18,1,128]{3,2,1,0:T(1,128)S(1)}, u32[]{:S(2)}, u32[]{:S(2)}) collective-permute-start(f32[6,18,1,128]{3,2,1,0:T(1,128)S(1)} %broadcast_select_fusion.5), channel_id=1, source_target_pairs={{0,2},{2,0},{1,3},{3,1},{4,6},{6,4},{5,7},{7,5},{8,10},{10,8},{9,1... | collective-permute-start | bytes 165896 | tf_op jit(solution)/shard_map/ppermute | solution.py:26
  19.9 3.5 %collective-permute-start.1 = (f32[12]{0:T(128)S(1)}, f32[12]{0:T(128)S(1)}, u32[]{:S(2)}, u32[]{:S(2)}) collective-permute-start(f32[12]{0:T(128)S(1)} %fusion.106), channel_id=1, source_target_pairs={{0,2},{1,3},{2,0},{3,1},{4,6},{5,7},{6,4},{7,5},{8,10},{9,11},{10,... | collective-permute-start | bytes 152 | tf_op jit(solution)/shard_map/ppermute | solution.py:151
  24.9 15.0 %collective-permute-start.7 = (f32[6,18,18,128]{3,2,1,0:T(8,128)}, f32[6,18,18,128]{3,2,1,0:T(8,128)}, u32[]{:S(2)}, u32[]{:S(2)}) collective-permute-start(f32[6,18,18,128]{3,2,1,0:T(8,128)} %maximum_add_fusion), channel_id=1, source_target_pairs={{0,1},{1,0},{2,3},{3,2},{4,5},{5,4},{6,7},{7,6},{8,9},{9,8},{10,11... | collective-permute-start | bytes 2985992 | tf_op jit(solution)/shard_map/ppermute | solution.py:18
  30.0 3.5 %collective-permute-start.2 = (f32[12]{0:T(128)S(1)}, f32[12]{0:T(128)S(1)}, u32[]{:S(2)}, u32[]{:S(2)}) collective-permute-start(f32[12]{0:T(128)S(1)} %add.479), channel_id=1, source_target_pairs={{0,4},{1,5},{2,6},{3,7},{4,0},{5,1},{6,2},{7,3},{8,12},{9,13},{10,... | collective-permute-start | bytes 152 | tf_op jit(solution)/shard_map/ppermute | solution.py:151
  33.5 4.4 %collective-permute-start.3 = (f32[12]{0:T(128)S(1)}, f32[12]{0:T(128)S(1)}, u32[]{:S(2)}, u32[]{:S(2)}) collective-permute-start(f32[12]{0:T(128)S(1)} %add.480), channel_id=1, source_target_pairs={{0,8},{1,9},{2,10},{3,11},{4,12},{5,13},{6,14},{7,15},{8,0},{9,1},... | collective-permute-start | bytes 152 | tf_op jit(solution)/shard_map/ppermute | solution.py:151
  38.0 0.6 copy-start.16
  44.2 0.9 copy-start.11
  47.3 0.9 copy-start.4
  47.3 1.0 copy-start.9
  51.6 6.0 %collective-permute-start.8 = (f32[6,1,16,128]{3,2,1,0:T(8,128)S(1)}, f32[6,1,16,128]{3,2,1,0:T(8,128)S(1)}, u32[]{:S(2)}, u32[]{:S(2)}) collective-permute-start(f32[6,1,16,128]{3,2,1,0:T(8,128)S(1)} %get-tuple-element.49), channel_id=1, source_target_pairs={{4,0},{8,4},{12,8},{5,1},{9,5},{13,9},{6,2},{10,6},{14,10},{7,3},{... | collective-permute-start | bytes 147464 | tf_op jit(solution)/shard_map/ppermute | solution.py:34
  52.9 6.3 %collective-permute-start.9 = (f32[6,1,16,128]{3,2,1,0:T(8,128)S(1)}, f32[6,1,16,128]{3,2,1,0:T(8,128)S(1)}, u32[]{:S(2)}, u32[]{:S(2)}) collective-permute-start(f32[6,1,16,128]{3,2,1,0:T(8,128)S(1)} %get-tuple-element.48), channel_id=1, source_target_pairs={{0,4},{4,8},{8,12},{1,5},{5,9},{9,13},{2,6},{6,10},{10,14},{3,7},{... | collective-permute-start | bytes 147464 | tf_op jit(solution)/shard_map/ppermute | solution.py:33
  59.3 5.6 %copy-start.8 = (bf16[6,16,16,128]{3,2,1,0:T(8,128)(2,1)S(1)}, bf16[6,16,16,128]{3,2,1,0:T(8,128)(2,1)}, u32[]{:S(2)}) copy-start(bf16[6,16,16,128]{3,2,1,0:T(8,128)(2,1)} %param.9) | copy-start | bytes 1179652
  59.3 4.2 %collective-permute-start.10 = (f32[6,18,1,128]{3,2,1,0:T(1,128)S(1)}, f32[6,18,1,128]{3,2,1,0:T(1,128)S(1)}, u32[]{:S(2)}, u32[]{:S(2)}) collective-permute-start(f32[6,18,1,128]{3,2,1,0:T(1,128)S(1)} %broadcast_select_fusion.2), channel_id=1, source_target_pairs={{0,2},{2,0},{1,3},{3,1},{4,6},{6,4},{5,7},{7,5},{8,10},{10,8},{9,1... | collective-permute-start | bytes 165896 | tf_op jit(solution)/shard_map/ppermute | solution.py:26
  64.9 2.1 %copy-start.7 = (f32[3,16,16,128]{3,2,1,0:T(8,128)S(1)}, f32[3,16,16,128]{3,2,1,0:T(8,128)}, u32[]{:S(2)}) copy-start(f32[3,16,16,128]{3,2,1,0:T(8,128)} %get-tuple-element.13) | copy-start | bytes 1179652
  64.9 4.8 %collective-permute-start.11 = (f32[6,18,18,128]{3,2,1,0:T(8,128)}, f32[6,18,18,128]{3,2,1,0:T(8,128)}, u32[]{:S(2)}, u32[]{:S(2)}) collective-permute-start(f32[6,18,18,128]{3,2,1,0:T(8,128)} %pad_maximum_fusion.4), channel_id=1, source_target_pairs={{0,1},{1,0},{2,3},{3,2},{4,5},{5,4},{6,7},{7,6},{8,9},{9,8},{10,11... | collective-permute-start | bytes 2985992 | tf_op jit(solution)/shard_map/ppermute | solution.py:18
  77.4 0.9 copy-start.2
  77.4 1.0 copy-start.5
  77.4 1.3 %copy-start.6 = (f32[6,16,16,128]{3,2,1,0:T(8,128)S(1)}, f32[6,16,16,128]{3,2,1,0:T(8,128)}, u32[]{:S(2)}) copy-start(f32[6,16,16,128]{3,2,1,0:T(8,128)} %convert_element_type.13) | copy-start | bytes 2359300
  77.4 1.2 %copy-start.10 = (f32[16,16,128]{2,1,0:T(8,128)S(1)}, f32[16,16,128]{2,1,0:T(8,128)}, u32[]{:S(2)}) copy-start(f32[16,16,128]{2,1,0:T(8,128)} %get-tuple-element.52) | copy-start | bytes 393220
  78.6 18.9 %copy-start.17 = (f32[12]{0:T(128)S(1)}, f32[12]{0:T(128)}, u32[]{:S(2)}) copy-start(f32[12]{0:T(128)} %copy-done.16) | copy-start | bytes 148
  81.0 3.2 %collective-permute-start.12 = (f32[902]{0:T(1024)S(1)}, f32[902]{0:T(1024)S(1)}, u32[]{:S(2)}, u32[]{:S(2)}) collective-permute-start(f32[902]{0:T(1024)S(1)} %pad_maximum_fusion.18), channel_id=1, source_target_pairs={{0,1},{1,0},{2,3},{3,2},{4,5},{5,4},{6,7},{7,6},{8,9},{9,8},{10,11... | collective-permute-start | bytes 10832 | tf_op jit(solution)/shard_map/ppermute | solution.py:145
  81.6 4.2 %collective-permute-start.13 = (f32[902]{0:T(1024)S(1)}, f32[902]{0:T(1024)S(1)}, u32[]{:S(2)}, u32[]{:S(2)}) collective-permute-start(f32[902]{0:T(1024)S(1)} %pad_maximum_fusion.18), channel_id=1, source_target_pairs={{0,2},{1,3},{2,0},{3,1},{4,6},{5,7},{6,4},{7,5},{8,10},{9,11},{10,... | collective-permute-start | bytes 10832 | tf_op jit(solution)/shard_map/ppermute | solution.py:145
  84.2 3.1 %collective-permute-start.14 = (f32[902]{0:T(1024)S(1)}, f32[902]{0:T(1024)S(1)}, u32[]{:S(2)}, u32[]{:S(2)}) collective-permute-start(f32[902]{0:T(1024)S(1)} %pad_maximum_fusion.18), channel_id=1, source_target_pairs={{0,3},{1,2},{2,1},{3,0},{4,7},{5,6},{6,5},{7,4},{8,11},{9,10},{10,... | collective-permute-start | bytes 10832 | tf_op jit(solution)/shard_map/ppermute | solution.py:145
  87.3 4.8 %collective-permute-start.15 = (f32[902]{0:T(1024)S(1)}, f32[902]{0:T(1024)S(1)}, u32[]{:S(2)}, u32[]{:S(2)}) collective-permute-start(f32[902]{0:T(1024)S(1)} %add_add_fusion.5), channel_id=1, source_target_pairs={{0,4},{1,5},{2,6},{3,7},{4,0},{5,1},{6,2},{7,3},{8,12},{9,13},{10,... | collective-permute-start | bytes 10832 | tf_op jit(solution)/shard_map/ppermute | solution.py:145
  89.6 4.5 %collective-permute-start.16 = (f32[902]{0:T(1024)S(1)}, f32[902]{0:T(1024)S(1)}, u32[]{:S(2)}, u32[]{:S(2)}) collective-permute-start(f32[902]{0:T(1024)S(1)} %add_add_fusion.5), channel_id=1, source_target_pairs={{0,8},{1,9},{2,10},{3,11},{4,12},{5,13},{6,14},{7,15},{8,0},{9,1},... | collective-permute-start | bytes 10832 | tf_op jit(solution)/shard_map/ppermute | solution.py:145
  92.1 5.4 %collective-permute-start.17 = (f32[902]{0:T(1024)S(1)}, f32[902]{0:T(1024)S(1)}, u32[]{:S(2)}, u32[]{:S(2)}) collective-permute-start(f32[902]{0:T(1024)S(1)} %add_add_fusion.5), channel_id=1, source_target_pairs={{0,12},{1,13},{2,14},{3,15},{4,8},{5,9},{6,10},{7,11},{8,4},{9,5},... | collective-permute-start | bytes 10832 | tf_op jit(solution)/shard_map/ppermute | solution.py:145

commit v11 on v9

--- a/solution.py
+++ b/solution.py
@@ -160,8 +160,12 @@
 
 def expand(blocks):
     blocks_x, blocks_y, blocks_z = blocks.shape
+    depth_tile = lax.broadcasted_iota(jnp.int32, (1, 1, blocks_z * 32), 2) // 32
+    rows = jnp.zeros((blocks_x, blocks_y, blocks_z * 32), blocks.dtype)
+    for tile in range(blocks_z):
+        rows = jnp.where(depth_tile == tile, blocks[:, :, tile : tile + 1], rows)
     spread = jnp.broadcast_to(
-        blocks[:, None, :, None, :, None], (blocks_x, 8, blocks_y, 8, blocks_z, 32)
+        rows[:, None, :, None, :], (blocks_x, 8, blocks_y, 8, blocks_z * 32)
     )
     return spread.reshape(blocks_x * 8, blocks_y * 8, blocks_z * 32)
 

time: 93.5 us -> 89 us (0.952)
  local copies, waits for them, and re-layouts: 12.8 us -> 8.17 us
    reshape x2 -> x0, local copies, waits for them, and re-layouts: 3.23 us -> none  [expand(): return spread.reshape(blocks_x * 8, blocks_y * 8, blocks_z * 32)]
    broadcast_in_dim x3, local copies, waits for them, and re-layouts: 2.02 us -> 0.03 us  [expand(): jnp.broadcast_to(rows[:, None, :, None, :], (blocks_x, 8, blocks_y, 8, bl...]
  transfers between devices with their start and end apart: 20 -> 20, of which waited for: 8 -> 9; matrix products, arithmetic and copies ran while one was open for 20% -> 15% of each run, Pallas kernels for 0% -> 0%
where the time goes in v11:
time: 89 us; the launch traced here: 88.5 us
  other arithmetic  32.8 us (37%)
  starting transfers between devices  29.6 us (33%)
  waiting for transfers between devices  16 us (18%)
  local copies, waits for them, and re-layouts  8.17 us (9%)
  between operations  1.97 us (2%)
    ppermute x12, starting transfers between devices, group_rounds(): lax.ppermute(value, axes, [(i, i ^ m * stride) for i in range(size)])  14.2 us
    ppermute x12, waiting for transfers between devices, group_rounds(): lax.ppermute(value, axes, [(i, i ^ m * stride) for i in range(size)])  10.9 us
    ppermute x2, starting transfers between devices, with_halo(): before = lax.ppermute(last, axis, up)  10.3 us
    concatenate x5, other arithmetic, with_halo(): array = jnp.concatenate([before, array, after], axis=dim)  6.55 us
    add x12, other arithmetic, navier(): result.append(shear * laplace[channel] + (lame_first + shear) * divergence)  5.61 us
    ppermute x2, waiting for transfers between devices, with_halo(): got = lax.ppermute(jnp.where(first, last, initial), axis, [(0, 1), (1, 0)])  3.5 us
    add x2, other arithmetic, add_mean(): new_real = field[:3] + (gain_real * mean_real - gain_imag * mean_imag)  2.64 us
    select_n x2, other arithmetic, with_halo(): after = jnp.where(first, got_initial, zero)  2.59 us
  transfers between devices with their start and end apart: 20, of which 9 were waited for; matrix products, arithmetic and copies ran while one was open for 15% of the time, Pallas kernels for 0%

profile of v11, /device:TPU:0, one launch (start us, length us, event | category | flops | bytes accessed | tf_op | source)
XLA Modules:
  0.0 88.5 jit_solution(13736792553273854931)
XLA Ops:
  0.7 1.4 %fusion.102 = (f32[6,1,16,128]{3,2,1,0:T(8,128)S(1)}, f32[6,1,16,128]{3,2,1,0:T(8,128)}) fusion(bf16[6,16,16,128]{3,2,1,0:T(8,128)(2,1)} %param.10), kind=kLoop, calls=%fused_computation.297 | loop fusion | bytes 196608 | tf_op jit(solution)/shard_map/slice | solution.py:13
  2.1 1.3 %collective-permute-start.6 = (f32[6,1,16,128]{3,2,1,0:T(8,128)}, f32[6,1,16,128]{3,2,1,0:T(8,128)S(1)}, u32[]{:S(2)}, u32[]{:S(2)}) collective-permute-start(f32[6,1,16,128]{3,2,1,0:T(8,128)} %get-tuple-element.64), channel_id=1, source_target_pairs={{4,0},{8,4},{12,8},{5,1},{9,5},{13,9},{6,2},{10,6},{14,10},{7,3},{... | collective-permute-start | bytes 147464 | tf_op jit(solution)/shard_map/ppermute | solution.py:34
  3.4 5.6 %collective-permute-start.7 = (f32[6,1,16,128]{3,2,1,0:T(8,128)S(1)}, f32[6,1,16,128]{3,2,1,0:T(8,128)S(1)}, u32[]{:S(2)}, u32[]{:S(2)}) collective-permute-start(f32[6,1,16,128]{3,2,1,0:T(8,128)S(1)} %get-tuple-element.63), channel_id=1, source_target_pairs={{0,4},{4,8},{8,12},{1,5},{5,9},{9,13},{2,6},{6,10},{10,14},{3,7},{... | collective-permute-start | bytes 147464 | tf_op jit(solution)/shard_map/ppermute | solution.py:33
  9.0 0.7 compare_select_fusion
  9.7 1.5 %scatter_custom_fusion = f32[32768]{0:T(1024)S(1)} fusion(s32[256]{0:T(256)S(1)} %bitcast.46, f32[256]{0:T(256)S(1)} %broadcast.308, f32[]{:T(128)} %constant.28.clone.1), kind=kCustom, calls=%fused_computation.248 | custom fusion | bytes 131076 | tf_op jit(solution)/shard_map/scatter | solution.py:187
  11.2 1.2 %multiply_reduce_fusion = f32[6]{0:T(128)S(1)} fusion(bf16[6,16,16,128]{3,2,1,0:T(8,128)(2,1)} %param.10, f32[16,16,128]{2,1,0:T(8,128)S(1)} %bitcast.36), kind=kLoop, calls=%fused_computation.45 | loop fusion | flops 589818 | bytes 524312 | tf_op jit(solution)/shard_map/reduce_sum | solution.py:221
  12.3 0.8 slice_bitcast_fusion.2
  13.7 0.8 slice_bitcast_fusion.1
  15.1 0.7 convert_multiply_fusion
  15.8 1.4 %multiply_subtract_fusion = (f32[3,16,16,128]{3,2,1,0:T(8,128)}, f32[3,16,16,128]{3,2,1,0:T(8,128)}, f32[3,16,16,128]{3,2,1,0:T(8,128)}, f32[3,16,16,128]{3,2,1,0:T(8,128)S(1)}, f32[3,16,16,128]{3,2,1,0:T(8,128)S(1)}) fusion(f32[6,16,16,128]{3,2,1,0:T(8,128)S(1)} %convert_element_type.15, f32[3]{0:T(128)S(1)} %get-tuple-element.79, ...), kind=kLoop, calls=%fused_computation.65 | loop fusion | flops 2359296 | bytes 3276824 | tf_op jit(solution)/shard_map/sub | solution.py:214
  17.5 2.0 %collective-permute-start.1 = (f32[12]{0:T(128)S(1)}, f32[12]{0:T(128)S(1)}, u32[]{:S(2)}, u32[]{:S(2)}) collective-permute-start(f32[12]{0:T(128)S(1)} %pad_maximum_fusion.19), channel_id=1, source_target_pairs={{0,2},{1,3},{2,0},{3,1},{4,6},{5,7},{6,4},{7,5},{8,10},{9,11},{10,... | collective-permute-start | bytes 152 | tf_op jit(solution)/shard_map/ppermute | solution.py:145
  19.8 1.8 %collective-permute-start.8 = (f32[6,18,1,128]{3,2,1,0:T(1,128)S(1)}, f32[6,18,1,128]{3,2,1,0:T(1,128)S(1)}, u32[]{:S(2)}, u32[]{:S(2)}) collective-permute-start(f32[6,18,1,128]{3,2,1,0:T(1,128)S(1)} %broadcast_select_fusion.5), channel_id=1, source_target_pairs={{0,2},{2,0},{1,3},{3,1},{4,6},{6,4},{5,7},{7,5},{8,10},{10,8},{9,1... | collective-permute-start | bytes 165896 | tf_op jit(solution)/shard_map/ppermute | solution.py:26
  21.6 0.9 %collective-permute-done.2 = f32[12]{0:T(128)S(1)} collective-permute-done((f32[12]{0:T(128)S(1)}, f32[12]{0:T(128)S(1)}, u32[]{:S(2)}, u32[]{:S(2)}) %collective-permute-start.2) | collective-permute-done | bytes 80 | tf_op jit(solution)/shard_map/ppermute | solution.py:145
  22.5 1.6 %collective-permute-start.3 = (f32[12]{0:T(128)S(1)}, f32[12]{0:T(128)S(1)}, u32[]{:S(2)}, u32[]{:S(2)}) collective-permute-start(f32[12]{0:T(128)S(1)} %add_add_fusion.8), channel_id=1, source_target_pairs={{0,4},{1,5},{2,6},{3,7},{4,0},{5,1},{6,2},{7,3},{8,12},{9,13},{10,... | collective-permute-start | bytes 152 | tf_op jit(solution)/shard_map/ppermute | solution.py:145
  24.0 1.1 %collective-permute-start.4 = (f32[12]{0:T(128)S(1)}, f32[12]{0:T(128)S(1)}, u32[]{:S(2)}, u32[]{:S(2)}) collective-permute-start(f32[12]{0:T(128)S(1)} %add_add_fusion.8), channel_id=1, source_target_pairs={{0,8},{1,9},{2,10},{3,11},{4,12},{5,13},{6,14},{7,15},{8,0},{9,1},... | collective-permute-start | bytes 152 | tf_op jit(solution)/shard_map/ppermute | solution.py:145
  25.1 1.7 %collective-permute-start.5 = (f32[12]{0:T(128)S(1)}, f32[12]{0:T(128)S(1)}, u32[]{:S(2)}, u32[]{:S(2)}) collective-permute-start(f32[12]{0:T(128)S(1)} %add_add_fusion.8), channel_id=1, source_target_pairs={{0,12},{1,13},{2,14},{3,15},{4,8},{5,9},{6,10},{7,11},{8,4},{9,5},... | collective-permute-start | bytes 152 | tf_op jit(solution)/shard_map/ppermute | solution.py:145
  27.3 1.2 %collective-permute-done.4 = f32[12]{0:T(128)S(1)} collective-permute-done((f32[12]{0:T(128)S(1)}, f32[12]{0:T(128)S(1)}, u32[]{:S(2)}, u32[]{:S(2)}) %collective-permute-start.4) | collective-permute-done | bytes 80 | tf_op jit(solution)/shard_map/ppermute | solution.py:145
  28.5 2.0 %collective-permute-done.5 = f32[12]{0:T(128)S(1)} collective-permute-done((f32[12]{0:T(128)S(1)}, f32[12]{0:T(128)S(1)}, u32[]{:S(2)}, u32[]{:S(2)}) %collective-permute-start.5) | collective-permute-done | bytes 80 | tf_op jit(solution)/shard_map/ppermute | solution.py:145
  31.6 2.1 %pad_maximum_fusion = (f32[6,18,18,129]{3,2,1,0:T(8,128)S(1)}, f32[6,18,18,129]{3,2,1,0:T(8,128)S(1)}) fusion(f32[6,18,18,1]{3,2,1,0:T(8,128)S(1)} %get-tuple-element.49, f32[6,18,1,128]{3,2,1,0:T(1,128)S(1)} %get-tuple-element.71, f32[6,1,16,128]{3,2,1,0:T(8,128)S(1)} %collective-permute-done.6, f32[6,16,16,128]{3,2,1,0:T(8,128)S(1)} %convert_element_type.12, ...), kind=kLoop, calls=%fused_computation.1 | loop fusion | flops 2507760 | bytes 3017088 | tf_op jit(solution)/shard_map/concatenate | solution.py:35
  35.9 0.7 fusion.76
  36.5 0.7 fusion.58
  37.5 1.3 %subtract_add_fusion.1 = (f32[3,16,16,128]{3,2,1,0:T(8,128)S(1)}, f32[3,16,16,128]{3,2,1,0:T(8,128)}, f32[3,16,16,128]{3,2,1,0:T(8,128)S(1)}, f32[3,16,16,128]{3,2,1,0:T(8,128)S(1)}) fusion(f32[3,16,16,128]{3,2,1,0:T(8,128)S(1)} %get-tuple-element.27, f32[3,16,16,128]{3,2,1,0:T(8,128)S(1)} %get-tuple-element.26, f32[3]{0:T(128)S(1)} %get-tuple-element.83, ...), kind=kLoop, calls=%fused_computation.73 | loop fusion | flops 4227072 | bytes 5242928 | tf_op jit(solution)/shard_map/add | solution.py:129
  38.8 2.0 %add_add_fusion.3 = (f32[3,16,16,128]{3,2,1,0:T(8,128)S(1)}, f32[3,16,16,128]{3,2,1,0:T(8,128)}) fusion(f32[3,16,16,128]{3,2,1,0:T(8,128)S(1)} %get-tuple-element.27, f32[3,16,16,128]{3,2,1,0:T(8,128)S(1)} %get-tuple-element.26, f32[3]{0:T(128)S(1)} %get-tuple-element.83, f32[3]{0:T(128)S(1)} %get-tuple-element.82, ...), kind=kLoop, calls=%fused_computation.71 | loop fusion | flops 1671168 | bytes 3145776 | tf_op jit(solution)/shard_map/add | solution.py:130
  40.8 1.3 %collective-permute-start.10 = (f32[6,1,16,128]{3,2,1,0:T(8,128)S(1)}, f32[6,1,16,128]{3,2,1,0:T(8,128)S(1)}, u32[]{:S(2)}, u32[]{:S(2)}) collective-permute-start(f32[6,1,16,128]{3,2,1,0:T(8,128)S(1)} %get-tuple-element.62), channel_id=1, source_target_pairs={{4,0},{8,4},{12,8},{5,1},{9,5},{13,9},{6,2},{10,6},{14,10},{7,3},{... | collective-permute-start | bytes 147464 | tf_op jit(solution)/shard_map/ppermute | solution.py:34
  42.1 4.7 %collective-permute-start.11 = (f32[6,1,16,128]{3,2,1,0:T(8,128)S(1)}, f32[6,1,16,128]{3,2,1,0:T(8,128)S(1)}, u32[]{:S(2)}, u32[]{:S(2)}) collective-permute-start(f32[6,1,16,128]{3,2,1,0:T(8,128)S(1)} %get-tuple-element.61), channel_id=1, source_target_pairs={{0,4},{4,8},{8,12},{1,5},{5,9},{9,13},{2,6},{6,10},{10,14},{3,7},{... | collective-permute-start | bytes 147464 | tf_op jit(solution)/shard_map/ppermute | solution.py:33
  46.9 1.5 %collective-permute-done.11 = f32[6,1,16,128]{3,2,1,0:T(8,128)S(1)} collective-permute-done((f32[6,1,16,128]{3,2,1,0:T(8,128)S(1)}, f32[6,1,16,128]{3,2,1,0:T(8,128)S(1)}, u32[]{:S(2)}, u32[]{:S(2)}) %collective-permute-start.11) | collective-permute-done | bytes 49184 | tf_op jit(solution)/shard_map/ppermute | solution.py:33
  48.5 0.7 collective-permute-start.12
  49.2 3.5 %collective-permute-done.12 = f32[6,18,1,128]{3,2,1,0:T(1,128)S(1)} collective-permute-done((f32[6,18,1,128]{3,2,1,0:T(1,128)S(1)}, f32[6,18,1,128]{3,2,1,0:T(1,128)S(1)}, u32[]{:S(2)}, u32[]{:S(2)}) %collective-permute-start.12) | collective-permute-done | bytes 55328 | tf_op jit(solution)/shard_map/ppermute | solution.py:26
  52.8 1.3 %pad_maximum_fusion.4 = f32[6,18,18,128]{3,2,1,0:T(8,128)} fusion(f32[6,18,1,128]{3,2,1,0:T(1,128)S(1)} %get-tuple-element.69, f32[6,1,16,128]{3,2,1,0:T(8,128)S(1)} %collective-permute-done.10, f32[3,16,16,128]{3,2,1,0:T(8,128)S(1)} %get-tuple-element.36, f32[3,16,16,128]{3,2,1,0:T(8,128)S(1)} %get-tuple-element.32, ...), kind=kLoop, calls=%fused_computation.14 | loop fusion | flops 1244160 | bytes 1990656 | tf_op jit(solution)/shard_map/concatenate | solution.py:35
  54.1 1.0 %convert_element_type.13 = f32[6,16,16,128]{3,2,1,0:T(8,128)} convert(bf16[6,16,16,128]{3,2,1,0:T(8,128)(2,1)S(1)} %copy-done.8) | non-fusion elementwise | flops 196608 | bytes 1179648 | tf_op jit(solution)/shard_map/convert_element_type | solution.py:192
  55.0 1.2 %multiply_add_fusion = f32[3,16,16,128]{3,2,1,0:T(8,128)S(1)} fusion(f32[3,16,16,128]{3,2,1,0:T(8,128)} %get-tuple-element.25, f32[3,16,16,128]{3,2,1,0:T(8,128)} %get-tuple-element.24), kind=kLoop, calls=%fused_computation.64 | loop fusion | flops 196608 | bytes 1179648 | tf_op jit(solution)/shard_map/add | solution.py:215
  57.4 1.3 %fusion.9 = f32[6]{0:T(128)S(1)} fusion(f32[3,16,16,128]{3,2,1,0:T(8,128)} %get-tuple-element.37, f32[3,16,16,128]{3,2,1,0:T(8,128)} %get-tuple-element.33, f32[16,16,128]{2,1,0:T(8,128)S(1)} %bitcast.40), kind=kLoop, calls=%fused_computation.40 | loop fusion | flops 589818 | bytes 917528 | tf_op jit(solution)/shard_map/reduce_sum | solution.py:237
  58.9 2.2 %slice_select_fusion.1 = (f32[6,18,18,1]{3,2,1,0:T(8,128)S(1)}, f32[6,18,18,1]{3,2,1,0:T(8,128)S(1)}) fusion(f32[6,18,18,128]{3,2,1,0:T(8,128)} %collective-permute-done.13, pred[]{:T(512)S(6)} %eq.67), kind=kLoop, calls=%fused_computation.6 | loop fusion | flops 3888 | bytes 31105 | tf_op jit(solution)/shard_map/jit(_where)/select_n | solution.py:23
  61.1 2.7 %pad_maximum_fusion.1 = (f32[6,18,18,129]{3,2,1,0:T(8,128)S(1)}, f32[6,18,18,129]{3,2,1,0:T(8,128)S(1)}) fusion(f32[6,18,18,1]{3,2,1,0:T(8,128)S(1)} %get-tuple-element.47, f32[6,18,1,128]{3,2,1,0:T(1,128)S(1)} %get-tuple-element.69, f32[6,1,16,128]{3,2,1,0:T(8,128)S(1)} %collective-permute-done.10, f32[3,16,16,128]{3,2,1,0:T(8,128)S(1)} %get-tuple-element.36, ...), kind=kLoop, calls=%fused_computation.3 | loop fusion | flops 3009312 | bytes 3017088 | tf_op jit(solution)/shard_map/concatenate | solution.py:35
  65.9 0.7 fusion.40
  66.6 0.7 fusion.22
  67.8 1.6 %subtract_reduce_fusion = (f32[16,16,128]{2,1,0:T(8,128)S(1)}, f32[3,16,16,128]{3,2,1,0:T(8,128)}, f32[3,16,16,128]{3,2,1,0:T(8,128)}) fusion(f32[6,16,16,128]{3,2,1,0:T(8,128)S(1)} %convert_element_type.15, f32[3,16,16,128]{3,2,1,0:T(8,128)S(1)} %get-tuple-element.32, f32[16,16,128]{2,1,0:T(8,128)S(1)} %copy-done.5, ...), kind=kLoop, calls=%fused_computation.68 | loop fusion | flops 5275648 | bytes 4587544 | tf_op jit(solution)/shard_map/reduce_sum | solution.py:246
  70.8 2.4 %collective-permute-start.15 = (f32[902]{0:T(1024)S(1)}, f32[902]{0:T(1024)S(1)}, u32[]{:S(2)}, u32[]{:S(2)}) collective-permute-start(f32[902]{0:T(1024)S(1)} %pad_maximum_fusion.18), channel_id=1, source_target_pairs={{0,2},{1,3},{2,0},{3,1},{4,6},{5,7},{6,4},{7,5},{8,10},{9,11},{10,... | collective-permute-start | bytes 10832 | tf_op jit(solution)/shard_map/ppermute | solution.py:145
  73.2 1.6 %collective-permute-done.15 = f32[902]{0:T(1024)S(1)} collective-permute-done((f32[902]{0:T(1024)S(1)}, f32[902]{0:T(1024)S(1)}, u32[]{:S(2)}, u32[]{:S(2)}) %collective-permute-start.15) | collective-permute-done | bytes 3640 | tf_op jit(solution)/shard_map/ppermute | solution.py:145
  74.8 1.5 %collective-permute-done.16 = f32[902]{0:T(1024)S(1)} collective-permute-done((f32[902]{0:T(1024)S(1)}, f32[902]{0:T(1024)S(1)}, u32[]{:S(2)}, u32[]{:S(2)}) %collective-permute-start.16) | collective-permute-done | bytes 3640 | tf_op jit(solution)/shard_map/ppermute | solution.py:145
  76.3 2.3 %collective-permute-start.17 = (f32[902]{0:T(1024)S(1)}, f32[902]{0:T(1024)S(1)}, u32[]{:S(2)}, u32[]{:S(2)}) collective-permute-start(f32[902]{0:T(1024)S(1)} %add_add_fusion.5), channel_id=1, source_target_pairs={{0,4},{1,5},{2,6},{3,7},{4,0},{5,1},{6,2},{7,3},{8,12},{9,13},{10,... | collective-permute-start | bytes 10832 | tf_op jit(solution)/shard_map/ppermute | solution.py:145
  78.6 0.8 collective-permute-start.18
  79.4 1.6 %collective-permute-start.19 = (f32[902]{0:T(1024)S(1)}, f32[902]{0:T(1024)S(1)}, u32[]{:S(2)}, u32[]{:S(2)}) collective-permute-start(f32[902]{0:T(1024)S(1)} %add_add_fusion.5), channel_id=1, source_target_pairs={{0,12},{1,13},{2,14},{3,15},{4,8},{5,9},{6,10},{7,11},{8,4},{9,5},... | collective-permute-start | bytes 10832 | tf_op jit(solution)/shard_map/ppermute | solution.py:145
  81.1 2.1 %collective-permute-done.18 = f32[902]{0:T(1024)S(1)} collective-permute-done((f32[902]{0:T(1024)S(1)}, f32[902]{0:T(1024)S(1)}, u32[]{:S(2)}, u32[]{:S(2)}) %collective-permute-start.18) | collective-permute-done | bytes 3640 | tf_op jit(solution)/shard_map/ppermute | solution.py:145
  83.1 1.7 %collective-permute-done.19 = f32[902]{0:T(1024)S(1)} collective-permute-done((f32[902]{0:T(1024)S(1)}, f32[902]{0:T(1024)S(1)}, u32[]{:S(2)}, u32[]{:S(2)}) %collective-permute-start.19) | collective-permute-done | bytes 3640 | tf_op jit(solution)/shard_map/ppermute | solution.py:145
  85.6 0.7 copy.14
  86.3 1.3 %subtract_add_fusion = (f32[3,16,16,128]{3,2,1,0:T(8,128)S(1)}, f32[3,16,16,128]{3,2,1,0:T(8,128)S(1)}) fusion(f32[3,16,16,128]{3,2,1,0:T(8,128)} %get-tuple-element.21, f32[3,16,16,128]{3,2,1,0:T(8,128)S(1)} %get-tuple-element.27, f32[3,16,16,128]{3,2,1,0:T(8,128)S(1)} %get-tuple-element.26, f32[3]{0:T(128)S(1)} %get-tuple-element.81, ...), kind=kLoop, calls=%fused_computation.63 | loop fusion | flops 786432 | bytes 2359320 | tf_op jit(solution)/shard_map/add | solution.py:129
  87.6 1.0 %pad_maximum_fusion.12 = f32[6,16,16,128]{3,2,1,0:T(8,128)} fusion(f32[3,16,16,128]{3,2,1,0:T(8,128)S(1)} %get-tuple-element.60, f32[3,16,16,128]{3,2,1,0:T(8,128)S(1)} %get-tuple-element.59), kind=kLoop, calls=%fused_computation.42 | loop fusion | flops 196608 | bytes 1572864 | tf_op jit(solution)/shard_map/concatenate | solution.py:131
  (117 shorter events, 11.2 us)
Async XLA Ops:
  0.6 13.9 %copy-start.11 = (bf16[6,16,16,128]{3,2,1,0:T(8,128)(2,1)S(1)}, bf16[6,16,16,128]{3,2,1,0:T(8,128)(2,1)}, u32[]{:S(2)}) copy-start(bf16[6,16,16,128]{3,2,1,0:T(8,128)(2,1)} %param.11) | copy-start | bytes 1179652
  0.6 13.9 %copy-start.17 = (s32[2,2,4]{2,1,0:T(2,128)S(1)}, s32[2,2,4]{2,1,0:T(2,128)}, u32[]{:S(2)}) copy-start(s32[2,2,4]{2,1,0:T(2,128)} %param.13) | copy-start | bytes 196
  0.7 14.4 %copy-start.12 = (bf16[16,16,128]{2,1,0:T(8,128)(2,1)S(1)}, bf16[16,16,128]{2,1,0:T(8,128)(2,1)}, u32[]{:S(2)}) copy-start(bf16[16,16,128]{2,1,0:T(8,128)(2,1)} %param.12) | copy-start | bytes 196612
  2.1 17.6 %collective-permute-start.6 = (f32[6,1,16,128]{3,2,1,0:T(8,128)}, f32[6,1,16,128]{3,2,1,0:T(8,128)S(1)}, u32[]{:S(2)}, u32[]{:S(2)}) collective-permute-start(f32[6,1,16,128]{3,2,1,0:T(8,128)} %get-tuple-element.64), channel_id=1, source_target_pairs={{4,0},{8,4},{12,8},{5,1},{9,5},{13,9},{6,2},{10,6},{14,10},{7,3},{... | collective-permute-start | bytes 147464 | tf_op jit(solution)/shard_map/ppermute | solution.py:34
  3.4 16.3 %collective-permute-start.7 = (f32[6,1,16,128]{3,2,1,0:T(8,128)S(1)}, f32[6,1,16,128]{3,2,1,0:T(8,128)S(1)}, u32[]{:S(2)}, u32[]{:S(2)}) collective-permute-start(f32[6,1,16,128]{3,2,1,0:T(8,128)S(1)} %get-tuple-element.63), channel_id=1, source_target_pairs={{0,4},{4,8},{8,12},{1,5},{5,9},{9,13},{2,6},{6,10},{10,14},{3,7},{... | collective-permute-start | bytes 147464 | tf_op jit(solution)/shard_map/ppermute | solution.py:33
  15.8 1.4 %copy-start.3 = (f32[16,16,128]{2,1,0:T(8,128)}, f32[16,16,128]{2,1,0:T(8,128)S(1)}, u32[]{:S(2)}) copy-start(f32[16,16,128]{2,1,0:T(8,128)S(1)} %get-tuple-element.67) | copy-start | bytes 393220
  15.8 21.4 %copy-start.1 = (f32[16,16,128]{2,1,0:T(8,128)}, f32[16,16,128]{2,1,0:T(8,128)S(1)}, u32[]{:S(2)}) copy-start(f32[16,16,128]{2,1,0:T(8,128)S(1)} %get-tuple-element.66) | copy-start | bytes 393220
  15.8 3.8 %copy-start = (bf16[6,16,16,128]{3,2,1,0:T(8,128)(2,1)S(1)}, bf16[6,16,16,128]{3,2,1,0:T(8,128)(2,1)}, u32[]{:S(2)}) copy-start(bf16[6,16,16,128]{3,2,1,0:T(8,128)(2,1)} %param.10) | copy-start | bytes 1179652
  17.5 4.1 %collective-permute-start = (f32[12]{0:T(128)S(1)}, f32[12]{0:T(128)S(1)}, u32[]{:S(2)}, u32[]{:S(2)}) collective-permute-start(f32[12]{0:T(128)S(1)} %pad_maximum_fusion.19), channel_id=1, source_target_pairs={{0,1},{1,0},{2,3},{3,2},{4,5},{5,4},{6,7},{7,6},{8,9},{9,8},{10,11... | collective-permute-start | bytes 152 | tf_op jit(solution)/shard_map/ppermute | solution.py:145
  17.5 4.1 %collective-permute-start.1 = (f32[12]{0:T(128)S(1)}, f32[12]{0:T(128)S(1)}, u32[]{:S(2)}, u32[]{:S(2)}) collective-permute-start(f32[12]{0:T(128)S(1)} %pad_maximum_fusion.19), channel_id=1, source_target_pairs={{0,2},{1,3},{2,0},{3,1},{4,6},{5,7},{6,4},{7,5},{8,10},{9,11},{10,... | collective-permute-start | bytes 152 | tf_op jit(solution)/shard_map/ppermute | solution.py:145
  19.5 3.0 %collective-permute-start.2 = (f32[12]{0:T(128)S(1)}, f32[12]{0:T(128)S(1)}, u32[]{:S(2)}, u32[]{:S(2)}) collective-permute-start(f32[12]{0:T(128)S(1)} %pad_maximum_fusion.19), channel_id=1, source_target_pairs={{0,3},{1,2},{2,1},{3,0},{4,7},{5,6},{6,5},{7,4},{8,11},{9,10},{10,... | collective-permute-start | bytes 152 | tf_op jit(solution)/shard_map/ppermute | solution.py:145
  19.7 10.9 %copy-start.8 = (bf16[6,16,16,128]{3,2,1,0:T(8,128)(2,1)S(1)}, bf16[6,16,16,128]{3,2,1,0:T(8,128)(2,1)}, u32[]{:S(2)}) copy-start(bf16[6,16,16,128]{3,2,1,0:T(8,128)(2,1)} %param.9) | copy-start | bytes 1179652
  19.8 7.1 %collective-permute-start.8 = (f32[6,18,1,128]{3,2,1,0:T(1,128)S(1)}, f32[6,18,1,128]{3,2,1,0:T(1,128)S(1)}, u32[]{:S(2)}, u32[]{:S(2)}) collective-permute-start(f32[6,18,1,128]{3,2,1,0:T(1,128)S(1)} %broadcast_select_fusion.5), channel_id=1, source_target_pairs={{0,2},{2,0},{1,3},{3,1},{4,6},{6,4},{5,7},{7,5},{8,10},{10,8},{9,1... | collective-permute-start | bytes 165896 | tf_op jit(solution)/shard_map/ppermute | solution.py:26
  22.5 4.8 %collective-permute-start.3 = (f32[12]{0:T(128)S(1)}, f32[12]{0:T(128)S(1)}, u32[]{:S(2)}, u32[]{:S(2)}) collective-permute-start(f32[12]{0:T(128)S(1)} %add_add_fusion.8), channel_id=1, source_target_pairs={{0,4},{1,5},{2,6},{3,7},{4,0},{5,1},{6,2},{7,3},{8,12},{9,13},{10,... | collective-permute-start | bytes 152 | tf_op jit(solution)/shard_map/ppermute | solution.py:145
  24.0 4.4 %collective-permute-start.4 = (f32[12]{0:T(128)S(1)}, f32[12]{0:T(128)S(1)}, u32[]{:S(2)}, u32[]{:S(2)}) collective-permute-start(f32[12]{0:T(128)S(1)} %add_add_fusion.8), channel_id=1, source_target_pairs={{0,8},{1,9},{2,10},{3,11},{4,12},{5,13},{6,14},{7,15},{8,0},{9,1},... | collective-permute-start | bytes 152 | tf_op jit(solution)/shard_map/ppermute | solution.py:145
  25.1 5.3 %collective-permute-start.5 = (f32[12]{0:T(128)S(1)}, f32[12]{0:T(128)S(1)}, u32[]{:S(2)}, u32[]{:S(2)}) collective-permute-start(f32[12]{0:T(128)S(1)} %add_add_fusion.8), channel_id=1, source_target_pairs={{0,12},{1,13},{2,14},{3,15},{4,8},{5,9},{6,10},{7,11},{8,4},{9,5},... | collective-permute-start | bytes 152 | tf_op jit(solution)/shard_map/ppermute | solution.py:145
  27.2 3.9 %collective-permute-start.9 = (f32[6,18,18,128]{3,2,1,0:T(8,128)S(1)}, f32[6,18,18,128]{3,2,1,0:T(8,128)S(1)}, u32[]{:S(2)}, u32[]{:S(2)}) collective-permute-start(f32[6,18,18,128]{3,2,1,0:T(8,128)S(1)} %maximum_add_fusion), channel_id=1, source_target_pairs={{0,1},{1,0},{2,3},{3,2},{4,5},{5,4},{6,7},{7,6},{8,9},{9,8},{10,11... | collective-permute-start | bytes 2985992 | tf_op jit(solution)/shard_map/ppermute | solution.py:18
  30.5 0.6 copy-start.15
  30.5 0.6 copy-start.13
  36.5 0.9 %copy-start.4 = (f32[16,16,128]{2,1,0:T(8,128)S(1)}, f32[16,16,128]{2,1,0:T(8,128)}, u32[]{:S(2)}) copy-start(f32[16,16,128]{2,1,0:T(8,128)} %copy-done.3) | copy-start | bytes 393220
  36.5 1.0 %copy-start.9 = (f32[16,16,128]{2,1,0:T(8,128)S(1)}, f32[16,16,128]{2,1,0:T(8,128)}, u32[]{:S(2)}) copy-start(f32[16,16,128]{2,1,0:T(8,128)} %get-tuple-element.65) | copy-start | bytes 393220
  40.8 6.0 %collective-permute-start.10 = (f32[6,1,16,128]{3,2,1,0:T(8,128)S(1)}, f32[6,1,16,128]{3,2,1,0:T(8,128)S(1)}, u32[]{:S(2)}, u32[]{:S(2)}) collective-permute-start(f32[6,1,16,128]{3,2,1,0:T(8,128)S(1)} %get-tuple-element.62), channel_id=1, source_target_pairs={{4,0},{8,4},{12,8},{5,1},{9,5},{13,9},{6,2},{10,6},{14,10},{7,3},{... | collective-permute-start | bytes 147464 | tf_op jit(solution)/shard_map/ppermute | solution.py:34
  42.1 6.3 %collective-permute-start.11 = (f32[6,1,16,128]{3,2,1,0:T(8,128)S(1)}, f32[6,1,16,128]{3,2,1,0:T(8,128)S(1)}, u32[]{:S(2)}, u32[]{:S(2)}) collective-permute-start(f32[6,1,16,128]{3,2,1,0:T(8,128)S(1)} %get-tuple-element.61), channel_id=1, source_target_pairs={{0,4},{4,8},{8,12},{1,5},{5,9},{9,13},{2,6},{6,10},{10,14},{3,7},{... | collective-permute-start | bytes 147464 | tf_op jit(solution)/shard_map/ppermute | solution.py:33
  48.5 4.2 %collective-permute-start.12 = (f32[6,18,1,128]{3,2,1,0:T(1,128)S(1)}, f32[6,18,1,128]{3,2,1,0:T(1,128)S(1)}, u32[]{:S(2)}, u32[]{:S(2)}) collective-permute-start(f32[6,18,1,128]{3,2,1,0:T(1,128)S(1)} %broadcast_select_fusion.2), channel_id=1, source_target_pairs={{0,2},{2,0},{1,3},{3,1},{4,6},{6,4},{5,7},{7,5},{8,10},{10,8},{9,1... | collective-permute-start | bytes 165896 | tf_op jit(solution)/shard_map/ppermute | solution.py:26
  54.1 2.1 %copy-start.7 = (f32[3,16,16,128]{3,2,1,0:T(8,128)S(1)}, f32[3,16,16,128]{3,2,1,0:T(8,128)}, u32[]{:S(2)}) copy-start(f32[3,16,16,128]{3,2,1,0:T(8,128)} %get-tuple-element.23) | copy-start | bytes 1179652
  54.1 4.8 %collective-permute-start.13 = (f32[6,18,18,128]{3,2,1,0:T(8,128)}, f32[6,18,18,128]{3,2,1,0:T(8,128)}, u32[]{:S(2)}, u32[]{:S(2)}) collective-permute-start(f32[6,18,18,128]{3,2,1,0:T(8,128)} %pad_maximum_fusion.4), channel_id=1, source_target_pairs={{0,1},{1,0},{2,3},{3,2},{4,5},{5,4},{6,7},{7,6},{8,9},{9,8},{10,11... | collective-permute-start | bytes 2985992 | tf_op jit(solution)/shard_map/ppermute | solution.py:18
  66.6 0.9 %copy-start.2 = (f32[16,16,128]{2,1,0:T(8,128)S(1)}, f32[16,16,128]{2,1,0:T(8,128)}, u32[]{:S(2)}) copy-start(f32[16,16,128]{2,1,0:T(8,128)} %copy-done.1) | copy-start | bytes 393220
  66.6 1.0 %copy-start.5 = (f32[16,16,128]{2,1,0:T(8,128)S(1)}, f32[16,16,128]{2,1,0:T(8,128)}, u32[]{:S(2)}) copy-start(f32[16,16,128]{2,1,0:T(8,128)} %copy-done.3) | copy-start | bytes 393220
  66.6 1.3 %copy-start.6 = (f32[6,16,16,128]{3,2,1,0:T(8,128)S(1)}, f32[6,16,16,128]{3,2,1,0:T(8,128)}, u32[]{:S(2)}) copy-start(f32[6,16,16,128]{3,2,1,0:T(8,128)} %convert_element_type.13) | copy-start | bytes 2359300
  66.6 1.2 %copy-start.10 = (f32[16,16,128]{2,1,0:T(8,128)S(1)}, f32[16,16,128]{2,1,0:T(8,128)}, u32[]{:S(2)}) copy-start(f32[16,16,128]{2,1,0:T(8,128)} %get-tuple-element.65) | copy-start | bytes 393220
  67.8 17.1 %copy-start.14 = (f32[6]{0:T(128)S(1)}, f32[6]{0:T(128)}, u32[]{:S(2)}) copy-start(f32[6]{0:T(128)} %copy-done.13) | copy-start | bytes 76
  67.8 17.1 %copy-start.16 = (f32[12]{0:T(128)S(1)}, f32[12]{0:T(128)}, u32[]{:S(2)}) copy-start(f32[12]{0:T(128)} %copy-done.15) | copy-start | bytes 148
  70.3 3.0 %collective-permute-start.14 = (f32[902]{0:T(1024)S(1)}, f32[902]{0:T(1024)S(1)}, u32[]{:S(2)}, u32[]{:S(2)}) collective-permute-start(f32[902]{0:T(1024)S(1)} %pad_maximum_fusion.18), channel_id=1, source_target_pairs={{0,1},{1,0},{2,3},{3,2},{4,5},{5,4},{6,7},{7,6},{8,9},{9,8},{10,11... | collective-permute-start | bytes 10832 | tf_op jit(solution)/shard_map/ppermute | solution.py:145
  70.8 4.0 %collective-permute-start.15 = (f32[902]{0:T(1024)S(1)}, f32[902]{0:T(1024)S(1)}, u32[]{:S(2)}, u32[]{:S(2)}) collective-permute-start(f32[902]{0:T(1024)S(1)} %pad_maximum_fusion.18), channel_id=1, source_target_pairs={{0,2},{1,3},{2,0},{3,1},{4,6},{5,7},{6,4},{7,5},{8,10},{9,11},{10,... | collective-permute-start | bytes 10832 | tf_op jit(solution)/shard_map/ppermute | solution.py:145
  73.2 3.1 %collective-permute-start.16 = (f32[902]{0:T(1024)S(1)}, f32[902]{0:T(1024)S(1)}, u32[]{:S(2)}, u32[]{:S(2)}) collective-permute-start(f32[902]{0:T(1024)S(1)} %pad_maximum_fusion.18), channel_id=1, source_target_pairs={{0,3},{1,2},{2,1},{3,0},{4,7},{5,6},{6,5},{7,4},{8,11},{9,10},{10,... | collective-permute-start | bytes 10832 | tf_op jit(solution)/shard_map/ppermute | solution.py:145
  76.3 4.8 %collective-permute-start.17 = (f32[902]{0:T(1024)S(1)}, f32[902]{0:T(1024)S(1)}, u32[]{:S(2)}, u32[]{:S(2)}) collective-permute-start(f32[902]{0:T(1024)S(1)} %add_add_fusion.5), channel_id=1, source_target_pairs={{0,4},{1,5},{2,6},{3,7},{4,0},{5,1},{6,2},{7,3},{8,12},{9,13},{10,... | collective-permute-start | bytes 10832 | tf_op jit(solution)/shard_map/ppermute | solution.py:145
  78.6 4.5 %collective-permute-start.18 = (f32[902]{0:T(1024)S(1)}, f32[902]{0:T(1024)S(1)}, u32[]{:S(2)}, u32[]{:S(2)}) collective-permute-start(f32[902]{0:T(1024)S(1)} %add_add_fusion.5), channel_id=1, source_target_pairs={{0,8},{1,9},{2,10},{3,11},{4,12},{5,13},{6,14},{7,15},{8,0},{9,1},... | collective-permute-start | bytes 10832 | tf_op jit(solution)/shard_map/ppermute | solution.py:145
  79.4 5.4 %collective-permute-start.19 = (f32[902]{0:T(1024)S(1)}, f32[902]{0:T(1024)S(1)}, u32[]{:S(2)}, u32[]{:S(2)}) collective-permute-start(f32[902]{0:T(1024)S(1)} %add_add_fusion.5), channel_id=1, source_target_pairs={{0,12},{1,13},{2,14},{3,15},{4,8},{5,9},{6,10},{7,11},{8,4},{9,5},... | collective-permute-start | bytes 10832 | tf_op jit(solution)/shard_map/ppermute | solution.py:145

commit v12 on v11

--- a/solution.py
+++ b/solution.py
@@ -124,11 +124,11 @@
 
 
 def add_mean(field, gain_real, gain_imag, mean_field):
-    mean_real = mean_field[:3][:, None, None, None]
-    mean_imag = mean_field[3:][:, None, None, None]
-    new_real = field[:3] + (gain_real * mean_real - gain_imag * mean_imag)
-    new_imag = field[3:] + (gain_real * mean_imag + gain_imag * mean_real)
-    return jnp.concatenate([new_real, new_imag], 0)
+    mean_real = mean_field[:3]
+    mean_imag = mean_field[3:]
+    straight = jnp.concatenate([mean_real, mean_imag])[:, None, None, None]
+    crossed = jnp.concatenate([-mean_imag, mean_real])[:, None, None, None]
+    return field + (gain_real * straight + gain_imag * crossed)
 
 
 def group_rounds(value, axes):
@@ -193,6 +193,8 @@
     group_size = lax.axis_size("gx") * lax.axis_size("gy") * lax.axis_size("col")
     count = jnp.float32(group_size * iface_cells.shape[1])
     gain_real, gain_imag = mean_gain(lame_first, shear, density_cells, mask, omega_sq, impedance)
+    gain_both_real = jnp.concatenate([gain_real, gain_real])
+    gain_both_imag = jnp.concatenate([gain_imag, gain_imag])
     axes = ("gx", "gy", "col")
     coarse_x = tile_shape[0] // 4
     coarse_y = tile_shape[1] // 4
@@ -235,7 +237,7 @@
     tied_source = source_cells + 0.0 * first[0]
     field = sweep(padded, lame_first, shear, density_cells, mask, tied_source, omega_sq, impedance)
     second_local = jnp.sum(mask * field, axis=(1, 2, 3))
-    field = add_mean(field, gain_real, gain_imag, mean_field)
+    field = add_mean(field, gain_both_real, gain_both_imag, mean_field)
     padded = with_halo(field, (("gx", 1), ("gy", 2), ("col", 3)), 1)
     field = sweep(padded, *sweep_args)
     correlation = (
@@ -256,7 +258,7 @@
     total_real = second[:3] + (gain_total_real * mean_real - gain_total_imag * mean_imag)
     total_imag = second[3:] + (gain_total_real * mean_imag + gain_total_imag * mean_real)
     late_mean = jnp.concatenate([total_real, total_imag]) / count
-    field = add_mean(field, gain_real, gain_imag, late_mean)
+    field = add_mean(field, gain_both_real, gain_both_imag, late_mean)
     late_terms = jnp.sum(
         late_mean[:3, None, None] * response[:3] - late_mean[3:, None, None] * response[3:], axis=0
     )

time: 89 us -> 87.4 us (0.982)
  other arithmetic: 32.8 us -> 30.4 us
    add x3, other arithmetic: 4.64 us -> 2.83 us  [the longest x1 2.05 us: add_mean(): return field + (gain_real * straight + gain_imag * crossed)]
    reduce_sum x4, other arithmetic: 0.61 us -> 1.82 us  [block_sums(): local = local.sum(axis=(-4, -2, -1))]
    dynamic_update_slice x2, local copies, waits for them, and re-layouts: 0.84 us -> 2 us  [block_sums(): return lax.dynamic_update_slice(grid, local, (0,) * len(lead) + grid_at)]
  transfers between devices with their start and end apart: 20 -> 20, of which waited for: 9 -> 9; matrix products, arithmetic and copies ran while one was open for 15% -> 18% of each run, Pallas kernels for 0% -> 0%
where the time goes in v12:
time: 87.4 us; the launch traced here: 86.7 us
  other arithmetic  30.4 us (35%)
  starting transfers between devices  29.3 us (34%)
  waiting for transfers between devices  16.1 us (18%)
  local copies, waits for them, and re-layouts  9.03 us (10%)
  between operations  1.99 us (2%)
    ppermute x12, starting transfers between devices, group_rounds(): lax.ppermute(value, axes, [(i, i ^ m * stride) for i in range(size)])  13.8 us
    ppermute x12, waiting for transfers between devices, group_rounds(): lax.ppermute(value, axes, [(i, i ^ m * stride) for i in range(size)])  11 us
    ppermute x2, starting transfers between devices, with_halo(): before = lax.ppermute(last, axis, up)  10.3 us
    concatenate x5, other arithmetic, with_halo(): array = jnp.concatenate([before, array, after], axis=dim)  5.97 us
    add x12, other arithmetic, navier(): result.append(shear * laplace[channel] + (lame_first + shear) * divergence)  5.61 us
    ppermute x2, waiting for transfers between devices, with_halo(): got = lax.ppermute(jnp.where(first, last, initial), axis, [(0, 1), (1, 0)])  3.5 us
    select_n x2, other arithmetic, with_halo(): after = jnp.where(first, got_initial, zero)  2.64 us
    ppermute x2, starting transfers between devices, with_halo(): after = lax.ppermute(initial, axis, down)  2.57 us
  transfers between devices with their start and end apart: 20, of which 9 were waited for; matrix products, arithmetic and copies ran while one was open for 18% of the time, Pallas kernels for 0%

profile of v12, /device:TPU:0, one launch (start us, length us, event | category | flops | bytes accessed | tf_op | source)
XLA Modules:
  0.0 86.7 jit_solution(1916125882051886230)
XLA Ops:
  0.7 0.8 fusion.107
  1.5 1.3 %collective-permute-start.6 = (f32[6,1,16,128]{3,2,1,0:T(8,128)S(1)}, f32[6,1,16,128]{3,2,1,0:T(8,128)S(1)}, u32[]{:S(2)}, u32[]{:S(2)}) collective-permute-start(f32[6,1,16,128]{3,2,1,0:T(8,128)S(1)} %get-tuple-element.63), channel_id=1, source_target_pairs={{4,0},{8,4},{12,8},{5,1},{9,5},{13,9},{6,2},{10,6},{14,10},{7,3},{... | collective-permute-start | bytes 147464 | tf_op jit(solution)/shard_map/ppermute | solution.py:34
  2.8 5.6 %collective-permute-start.7 = (f32[6,1,16,128]{3,2,1,0:T(8,128)S(1)}, f32[6,1,16,128]{3,2,1,0:T(8,128)S(1)}, u32[]{:S(2)}, u32[]{:S(2)}) collective-permute-start(f32[6,1,16,128]{3,2,1,0:T(8,128)S(1)} %get-tuple-element.62), channel_id=1, source_target_pairs={{0,4},{4,8},{8,12},{1,5},{5,9},{9,13},{2,6},{6,10},{10,14},{3,7},{... | collective-permute-start | bytes 147464 | tf_op jit(solution)/shard_map/ppermute | solution.py:33
  8.4 0.7 compare_select_fusion
  9.1 1.5 %scatter_custom_fusion = f32[32768]{0:T(1024)S(1)} fusion(s32[256]{0:T(256)S(1)} %bitcast.47, f32[256]{0:T(256)S(1)} %broadcast.308, f32[]{:T(128)} %constant.28.clone.1), kind=kCustom, calls=%fused_computation.245 | custom fusion | bytes 131076 | tf_op jit(solution)/shard_map/scatter | solution.py:187
  10.5 1.2 %multiply_reduce_fusion.1 = f32[6]{0:T(128)S(1)} fusion(bf16[6,16,16,128]{3,2,1,0:T(8,128)(2,1)} %param.10, f32[16,16,128]{2,1,0:T(8,128)S(1)} %bitcast.36), kind=kLoop, calls=%fused_computation.46 | loop fusion | flops 589818 | bytes 524312 | tf_op jit(solution)/shard_map/reduce_sum | solution.py:223
  11.7 0.8 slice_bitcast_fusion.2
  13.1 0.8 slice_bitcast_fusion.1
  14.4 0.7 convert_multiply_fusion
  15.1 1.4 %multiply_subtract_fusion = (f32[3,16,16,128]{3,2,1,0:T(8,128)}, f32[3,16,16,128]{3,2,1,0:T(8,128)}, f32[3,16,16,128]{3,2,1,0:T(8,128)}, f32[3,16,16,128]{3,2,1,0:T(8,128)S(1)}, f32[3,16,16,128]{3,2,1,0:T(8,128)S(1)}) fusion(f32[6,16,16,128]{3,2,1,0:T(8,128)S(1)} %convert_element_type.15, f32[3]{0:T(128)S(1)} %get-tuple-element.78, ...), kind=kLoop, calls=%fused_computation.64 | loop fusion | flops 2359296 | bytes 3276824 | tf_op jit(solution)/shard_map/sub | solution.py:216
  16.9 2.0 %collective-permute-start.1 = (f32[12]{0:T(128)S(1)}, f32[12]{0:T(128)S(1)}, u32[]{:S(2)}, u32[]{:S(2)}) collective-permute-start(f32[12]{0:T(128)S(1)} %pad_maximum_fusion.17), channel_id=1, source_target_pairs={{0,2},{1,3},{2,0},{3,1},{4,6},{5,7},{6,4},{7,5},{8,10},{9,11},{10,... | collective-permute-start | bytes 152 | tf_op jit(solution)/shard_map/ppermute | solution.py:145
  19.1 1.8 %collective-permute-start.8 = (f32[6,18,1,128]{3,2,1,0:T(1,128)S(1)}, f32[6,18,1,128]{3,2,1,0:T(1,128)S(1)}, u32[]{:S(2)}, u32[]{:S(2)}) collective-permute-start(f32[6,18,1,128]{3,2,1,0:T(1,128)S(1)} %broadcast_select_fusion.5), channel_id=1, source_target_pairs={{0,2},{2,0},{1,3},{3,1},{4,6},{6,4},{5,7},{7,5},{8,10},{10,8},{9,1... | collective-permute-start | bytes 165896 | tf_op jit(solution)/shard_map/ppermute | solution.py:26
  20.9 0.9 %collective-permute-done.2 = f32[12]{0:T(128)S(1)} collective-permute-done((f32[12]{0:T(128)S(1)}, f32[12]{0:T(128)S(1)}, u32[]{:S(2)}, u32[]{:S(2)}) %collective-permute-start.2) | collective-permute-done | bytes 80 | tf_op jit(solution)/shard_map/ppermute | solution.py:145
  21.9 1.6 %collective-permute-start.3 = (f32[12]{0:T(128)S(1)}, f32[12]{0:T(128)S(1)}, u32[]{:S(2)}, u32[]{:S(2)}) collective-permute-start(f32[12]{0:T(128)S(1)} %add_add_fusion.6), channel_id=1, source_target_pairs={{0,4},{1,5},{2,6},{3,7},{4,0},{5,1},{6,2},{7,3},{8,12},{9,13},{10,... | collective-permute-start | bytes 152 | tf_op jit(solution)/shard_map/ppermute | solution.py:145
  23.4 1.1 %collective-permute-start.4 = (f32[12]{0:T(128)S(1)}, f32[12]{0:T(128)S(1)}, u32[]{:S(2)}, u32[]{:S(2)}) collective-permute-start(f32[12]{0:T(128)S(1)} %add_add_fusion.6), channel_id=1, source_target_pairs={{0,8},{1,9},{2,10},{3,11},{4,12},{5,13},{6,14},{7,15},{8,0},{9,1},... | collective-permute-start | bytes 152 | tf_op jit(solution)/shard_map/ppermute | solution.py:145
  24.5 1.7 %collective-permute-start.5 = (f32[12]{0:T(128)S(1)}, f32[12]{0:T(128)S(1)}, u32[]{:S(2)}, u32[]{:S(2)}) collective-permute-start(f32[12]{0:T(128)S(1)} %add_add_fusion.6), channel_id=1, source_target_pairs={{0,12},{1,13},{2,14},{3,15},{4,8},{5,9},{6,10},{7,11},{8,4},{9,5},... | collective-permute-start | bytes 152 | tf_op jit(solution)/shard_map/ppermute | solution.py:145
  26.7 1.2 %collective-permute-done.4 = f32[12]{0:T(128)S(1)} collective-permute-done((f32[12]{0:T(128)S(1)}, f32[12]{0:T(128)S(1)}, u32[]{:S(2)}, u32[]{:S(2)}) %collective-permute-start.4) | collective-permute-done | bytes 80 | tf_op jit(solution)/shard_map/ppermute | solution.py:145
  27.9 2.0 %collective-permute-done.5 = f32[12]{0:T(128)S(1)} collective-permute-done((f32[12]{0:T(128)S(1)}, f32[12]{0:T(128)S(1)}, u32[]{:S(2)}, u32[]{:S(2)}) %collective-permute-start.5) | collective-permute-done | bytes 80 | tf_op jit(solution)/shard_map/ppermute | solution.py:145
  30.9 2.1 %pad_maximum_fusion = (f32[6,18,18,129]{3,2,1,0:T(8,128)S(1)}, f32[6,18,18,129]{3,2,1,0:T(8,128)S(1)}) fusion(f32[6,18,18,1]{3,2,1,0:T(8,128)S(1)} %get-tuple-element.48, f32[6,18,1,128]{3,2,1,0:T(1,128)S(1)} %get-tuple-element.70, f32[6,1,16,128]{3,2,1,0:T(8,128)S(1)} %collective-permute-done.6, f32[6,16,16,128]{3,2,1,0:T(8,128)S(1)} %convert_element_type.12, ...), kind=kLoop, calls=%fused_computation.1 | loop fusion | flops 2507760 | bytes 3017088 | tf_op jit(solution)/shard_map/concatenate | solution.py:35
  35.2 0.7 fusion.82
  35.8 0.7 fusion.64
  37.6 0.8 multiply_reduce_fusion
  38.3 1.3 %collective-permute-start.10 = (f32[6,1,16,128]{3,2,1,0:T(8,128)S(1)}, f32[6,1,16,128]{3,2,1,0:T(8,128)S(1)}, u32[]{:S(2)}, u32[]{:S(2)}) collective-permute-start(f32[6,1,16,128]{3,2,1,0:T(8,128)S(1)} %get-tuple-element.61), channel_id=1, source_target_pairs={{4,0},{8,4},{12,8},{5,1},{9,5},{13,9},{6,2},{10,6},{14,10},{7,3},{... | collective-permute-start | bytes 147464 | tf_op jit(solution)/shard_map/ppermute | solution.py:34
  39.6 4.7 %collective-permute-start.11 = (f32[6,1,16,128]{3,2,1,0:T(8,128)S(1)}, f32[6,1,16,128]{3,2,1,0:T(8,128)S(1)}, u32[]{:S(2)}, u32[]{:S(2)}) collective-permute-start(f32[6,1,16,128]{3,2,1,0:T(8,128)S(1)} %get-tuple-element.60), channel_id=1, source_target_pairs={{0,4},{4,8},{8,12},{1,5},{5,9},{9,13},{2,6},{6,10},{10,14},{3,7},{... | collective-permute-start | bytes 147464 | tf_op jit(solution)/shard_map/ppermute | solution.py:33
  44.4 1.5 %collective-permute-done.11 = f32[6,1,16,128]{3,2,1,0:T(8,128)S(1)} collective-permute-done((f32[6,1,16,128]{3,2,1,0:T(8,128)S(1)}, f32[6,1,16,128]{3,2,1,0:T(8,128)S(1)}, u32[]{:S(2)}, u32[]{:S(2)}) %collective-permute-start.11) | collective-permute-done | bytes 49184 | tf_op jit(solution)/shard_map/ppermute | solution.py:33
  46.0 0.7 collective-permute-start.12
  46.7 3.5 %collective-permute-done.12 = f32[6,18,1,128]{3,2,1,0:T(1,128)S(1)} collective-permute-done((f32[6,18,1,128]{3,2,1,0:T(1,128)S(1)}, f32[6,18,1,128]{3,2,1,0:T(1,128)S(1)}, u32[]{:S(2)}, u32[]{:S(2)}) %collective-permute-start.12) | collective-permute-done | bytes 55328 | tf_op jit(solution)/shard_map/ppermute | solution.py:26
  50.3 1.3 %pad_maximum_fusion.4 = f32[6,18,18,128]{3,2,1,0:T(8,128)} fusion(f32[6,18,1,128]{3,2,1,0:T(1,128)S(1)} %get-tuple-element.68, f32[6,1,16,128]{3,2,1,0:T(8,128)S(1)} %collective-permute-done.10, f32[6,16,16,128]{3,2,1,0:T(8,128)S(1)} %get-tuple-element.59, f32[6,1,16,128]{3,2,1,0:T(8,128)S(1)} %collective-permute-done.11, ...), kind=kLoop, calls=%fused_computation.14 | loop fusion | flops 995328 | bytes 1990656 | tf_op jit(solution)/shard_map/concatenate | solution.py:35
  51.6 1.0 %convert_element_type.13 = f32[6,16,16,128]{3,2,1,0:T(8,128)} convert(bf16[6,16,16,128]{3,2,1,0:T(8,128)(2,1)S(1)} %copy-done.3) | non-fusion elementwise | flops 196608 | bytes 1179648 | tf_op jit(solution)/shard_map/convert_element_type | solution.py:192
  52.5 1.2 %multiply_add_fusion = f32[3,16,16,128]{3,2,1,0:T(8,128)S(1)} fusion(f32[3,16,16,128]{3,2,1,0:T(8,128)} %get-tuple-element.25, f32[3,16,16,128]{3,2,1,0:T(8,128)} %get-tuple-element.24), kind=kLoop, calls=%fused_computation.63 | loop fusion | flops 196608 | bytes 1179648 | tf_op jit(solution)/shard_map/add | solution.py:217
  53.8 0.9 %maximum_reduce_fusion = f32[6,16,16]{2,1,0:T(8,128)} fusion(f32[3,16,16,128]{3,2,1,0:T(8,128)S(1)} %multiply_add_fusion, f32[3,16,16,128]{3,2,1,0:T(8,128)S(1)} %copy-done.2), kind=kLoop, calls=%fused_computation.42 | loop fusion | flops 391680 | bytes 792576 | tf_op jit(solution)/shard_map/reduce_sum | solution.py:207
  54.6 0.9 %reduce_sum.115 = f32[6,4,4,4,4]{4,3,2,1,0:T(4,128)S(1)} reshape(f32[6,16,16]{2,1,0:T(8,128)} %maximum_reduce_fusion) | data formatting | bytes 12288 | tf_op jit(solution)/shard_map/reduce_sum | solution.py:207
  55.6 0.7 reduce_sum.116
  56.3 1.7 %dynamic_update_slice.7 = f32[6,16,8]{2,1,0:T(8,128)S(1)} dynamic-update-slice(f32[6,16,8]{2,1,0:T(8,128)S(1)} %broadcast_in_dim.188, f32[6,4,4]{2,1,0:T(4,128)} %reduce_sum.116, s32[]{:T(128)} %constant.29.clone.1, s32[]{:T(128)S(6)} %select_n.188, s32[]{:T(128)S(6)} %select_n.189) | dynamic-update-slice | bytes 772 | tf_op jit(solution)/shard_map/dynamic_update_slice | solution.py:209
  58.3 2.2 %slice_select_fusion.1 = (f32[6,18,18,1]{3,2,1,0:T(8,128)S(1)}, f32[6,18,18,1]{3,2,1,0:T(8,128)S(1)}) fusion(f32[6,18,18,128]{3,2,1,0:T(8,128)} %collective-permute-done.13, pred[]{:T(512)S(6)} %eq.67), kind=kLoop, calls=%fused_computation.6 | loop fusion | flops 3888 | bytes 31105 | tf_op jit(solution)/shard_map/jit(_where)/select_n | solution.py:23
  60.5 2.1 %pad_maximum_fusion.1 = (f32[6,18,18,129]{3,2,1,0:T(8,128)S(1)}, f32[6,18,18,129]{3,2,1,0:T(8,128)S(1)}) fusion(f32[6,18,18,1]{3,2,1,0:T(8,128)S(1)} %get-tuple-element.46, f32[6,18,1,128]{3,2,1,0:T(1,128)S(1)} %get-tuple-element.68, f32[6,1,16,128]{3,2,1,0:T(8,128)S(1)} %collective-permute-done.10, f32[6,16,16,128]{3,2,1,0:T(8,128)S(1)} %get-tuple-element.59, ...), kind=kLoop, calls=%fused_computation.3 | loop fusion | flops 2507760 | bytes 3017088 | tf_op jit(solution)/shard_map/concatenate | solution.py:35
  64.7 0.7 fusion.28
  66.9 1.2 %subtract_reduce_fusion = (f32[16,16,128]{2,1,0:T(8,128)S(1)}, f32[3,16,16,128]{3,2,1,0:T(8,128)S(1)}, f32[3,16,16,128]{3,2,1,0:T(8,128)}) fusion(f32[6,16,16,128]{3,2,1,0:T(8,128)S(1)} %convert_element_type.15, f32[3,16,16,128]{3,2,1,0:T(8,128)S(1)} %get-tuple-element.45, f32[3]{0:T(128)S(1)} %copy-done.10, f32[16,16,128]{2,1,0:T(8,128)S(1)} %get-tuple-element.66, ...), kind=kLoop, calls=%fused_computation.67 | loop fusion | flops 2719744 | bytes 3670040 | tf_op jit(solution)/shard_map/reduce_sum | solution.py:248
  69.4 2.1 %collective-permute-start.15 = (f32[902]{0:T(1024)S(1)}, f32[902]{0:T(1024)S(1)}, u32[]{:S(2)}, u32[]{:S(2)}) collective-permute-start(f32[902]{0:T(1024)S(1)} %pad_maximum_fusion.16), channel_id=1, source_target_pairs={{0,2},{1,3},{2,0},{3,1},{4,6},{5,7},{6,4},{7,5},{8,10},{9,11},{10,... | collective-permute-start | bytes 10832 | tf_op jit(solution)/shard_map/ppermute | solution.py:145
  71.5 1.6 %collective-permute-done.15 = f32[902]{0:T(1024)S(1)} collective-permute-done((f32[902]{0:T(1024)S(1)}, f32[902]{0:T(1024)S(1)}, u32[]{:S(2)}, u32[]{:S(2)}) %collective-permute-start.15) | collective-permute-done | bytes 3640 | tf_op jit(solution)/shard_map/ppermute | solution.py:145
  73.1 1.5 %collective-permute-done.16 = f32[902]{0:T(1024)S(1)} collective-permute-done((f32[902]{0:T(1024)S(1)}, f32[902]{0:T(1024)S(1)}, u32[]{:S(2)}, u32[]{:S(2)}) %collective-permute-start.16) | collective-permute-done | bytes 3640 | tf_op jit(solution)/shard_map/ppermute | solution.py:145
  74.5 2.3 %collective-permute-start.17 = (f32[902]{0:T(1024)S(1)}, f32[902]{0:T(1024)S(1)}, u32[]{:S(2)}, u32[]{:S(2)}) collective-permute-start(f32[902]{0:T(1024)S(1)} %add_add_fusion.3), channel_id=1, source_target_pairs={{0,4},{1,5},{2,6},{3,7},{4,0},{5,1},{6,2},{7,3},{8,12},{9,13},{10,... | collective-permute-start | bytes 10832 | tf_op jit(solution)/shard_map/ppermute | solution.py:145
  76.9 0.9 %collective-permute-start.18 = (f32[902]{0:T(1024)S(1)}, f32[902]{0:T(1024)S(1)}, u32[]{:S(2)}, u32[]{:S(2)}) collective-permute-start(f32[902]{0:T(1024)S(1)} %add_add_fusion.3), channel_id=1, source_target_pairs={{0,8},{1,9},{2,10},{3,11},{4,12},{5,13},{6,14},{7,15},{8,0},{9,1},... | collective-permute-start | bytes 10832 | tf_op jit(solution)/shard_map/ppermute | solution.py:145
  77.8 1.5 %collective-permute-start.19 = (f32[902]{0:T(1024)S(1)}, f32[902]{0:T(1024)S(1)}, u32[]{:S(2)}, u32[]{:S(2)}) collective-permute-start(f32[902]{0:T(1024)S(1)} %add_add_fusion.3), channel_id=1, source_target_pairs={{0,12},{1,13},{2,14},{3,15},{4,8},{5,9},{6,10},{7,11},{8,4},{9,5},... | collective-permute-start | bytes 10832 | tf_op jit(solution)/shard_map/ppermute | solution.py:145
  79.3 2.1 %collective-permute-done.18 = f32[902]{0:T(1024)S(1)} collective-permute-done((f32[902]{0:T(1024)S(1)}, f32[902]{0:T(1024)S(1)}, u32[]{:S(2)}, u32[]{:S(2)}) %collective-permute-start.18) | collective-permute-done | bytes 3640 | tf_op jit(solution)/shard_map/ppermute | solution.py:145
  81.4 1.8 %collective-permute-done.19 = f32[902]{0:T(1024)S(1)} collective-permute-done((f32[902]{0:T(1024)S(1)}, f32[902]{0:T(1024)S(1)}, u32[]{:S(2)}, u32[]{:S(2)}) %collective-permute-start.19) | collective-permute-done | bytes 3640 | tf_op jit(solution)/shard_map/ppermute | solution.py:145
  84.0 0.7 copy.14
  84.7 2.0 %fusion.13 = f32[6,16,16,128]{3,2,1,0:T(8,128)} fusion(f32[3,16,16,128]{3,2,1,0:T(8,128)S(1)} %get-tuple-element.27, f32[3,16,16,128]{3,2,1,0:T(8,128)S(1)} %get-tuple-element.26, f32[3,16,16,128]{3,2,1,0:T(8,128)} %get-tuple-element.22, f32[3,16,16,128]{3,2,1,0:T(8,128)S(1)} %get-tuple-element.21, f32[6]{0:T(128)S(1)} %pad_maximum_fusion.19, ...), kind=kLoop, calls=%fused_computation.38 | loop fusion | flops 1376256 | bytes 2359344 | tf_op jit(solution)/shard_map/add | solution.py:131
  (117 shorter events, 11.7 us)
Async XLA Ops:
  0.6 13.3 %copy-start.5 = (bf16[6,16,16,128]{3,2,1,0:T(8,128)(2,1)S(1)}, bf16[6,16,16,128]{3,2,1,0:T(8,128)(2,1)}, u32[]{:S(2)}) copy-start(bf16[6,16,16,128]{3,2,1,0:T(8,128)(2,1)} %param.11) | copy-start | bytes 1179652
  0.6 13.3 %copy-start.16 = (s32[2,2,4]{2,1,0:T(2,128)S(1)}, s32[2,2,4]{2,1,0:T(2,128)}, u32[]{:S(2)}) copy-start(s32[2,2,4]{2,1,0:T(2,128)} %param.13) | copy-start | bytes 196
  0.7 13.8 %copy-start.6 = (bf16[16,16,128]{2,1,0:T(8,128)(2,1)S(1)}, bf16[16,16,128]{2,1,0:T(8,128)(2,1)}, u32[]{:S(2)}) copy-start(bf16[16,16,128]{2,1,0:T(8,128)(2,1)} %param.12) | copy-start | bytes 196612
  1.5 17.6 %collective-permute-start.6 = (f32[6,1,16,128]{3,2,1,0:T(8,128)S(1)}, f32[6,1,16,128]{3,2,1,0:T(8,128)S(1)}, u32[]{:S(2)}, u32[]{:S(2)}) collective-permute-start(f32[6,1,16,128]{3,2,1,0:T(8,128)S(1)} %get-tuple-element.63), channel_id=1, source_target_pairs={{4,0},{8,4},{12,8},{5,1},{9,5},{13,9},{6,2},{10,6},{14,10},{7,3},{... | collective-permute-start | bytes 147464 | tf_op jit(solution)/shard_map/ppermute | solution.py:34
  2.8 16.3 %collective-permute-start.7 = (f32[6,1,16,128]{3,2,1,0:T(8,128)S(1)}, f32[6,1,16,128]{3,2,1,0:T(8,128)S(1)}, u32[]{:S(2)}, u32[]{:S(2)}) collective-permute-start(f32[6,1,16,128]{3,2,1,0:T(8,128)S(1)} %get-tuple-element.62), channel_id=1, source_target_pairs={{0,4},{4,8},{8,12},{1,5},{5,9},{9,13},{2,6},{6,10},{10,14},{3,7},{... | collective-permute-start | bytes 147464 | tf_op jit(solution)/shard_map/ppermute | solution.py:33
  13.9 23.4 %copy-start.7 = (f32[3]{0:T(128)}, f32[3]{0:T(128)S(1)}, u32[]{:S(2)}) copy-start(f32[3]{0:T(128)S(1)} %get-tuple-element.77) | copy-start | bytes 40
  13.9 23.4 %copy-start.9 = (f32[3]{0:T(128)}, f32[3]{0:T(128)S(1)}, u32[]{:S(2)}) copy-start(f32[3]{0:T(128)S(1)} %get-tuple-element.78) | copy-start | bytes 40
  15.1 3.8 %copy-start = (bf16[6,16,16,128]{3,2,1,0:T(8,128)(2,1)S(1)}, bf16[6,16,16,128]{3,2,1,0:T(8,128)(2,1)}, u32[]{:S(2)}) copy-start(bf16[6,16,16,128]{3,2,1,0:T(8,128)(2,1)} %param.10) | copy-start | bytes 1179652
  16.9 4.1 %collective-permute-start = (f32[12]{0:T(128)S(1)}, f32[12]{0:T(128)S(1)}, u32[]{:S(2)}, u32[]{:S(2)}) collective-permute-start(f32[12]{0:T(128)S(1)} %pad_maximum_fusion.17), channel_id=1, source_target_pairs={{0,1},{1,0},{2,3},{3,2},{4,5},{5,4},{6,7},{7,6},{8,9},{9,8},{10,11... | collective-permute-start | bytes 152 | tf_op jit(solution)/shard_map/ppermute | solution.py:145
  16.9 4.1 %collective-permute-start.1 = (f32[12]{0:T(128)S(1)}, f32[12]{0:T(128)S(1)}, u32[]{:S(2)}, u32[]{:S(2)}) collective-permute-start(f32[12]{0:T(128)S(1)} %pad_maximum_fusion.17), channel_id=1, source_target_pairs={{0,2},{1,3},{2,0},{3,1},{4,6},{5,7},{6,4},{7,5},{8,10},{9,11},{10,... | collective-permute-start | bytes 152 | tf_op jit(solution)/shard_map/ppermute | solution.py:145
  18.9 3.0 %collective-permute-start.2 = (f32[12]{0:T(128)S(1)}, f32[12]{0:T(128)S(1)}, u32[]{:S(2)}, u32[]{:S(2)}) collective-permute-start(f32[12]{0:T(128)S(1)} %pad_maximum_fusion.17), channel_id=1, source_target_pairs={{0,3},{1,2},{2,1},{3,0},{4,7},{5,6},{6,5},{7,4},{8,11},{9,10},{10,... | collective-permute-start | bytes 152 | tf_op jit(solution)/shard_map/ppermute | solution.py:145
  19.1 10.9 %copy-start.3 = (bf16[6,16,16,128]{3,2,1,0:T(8,128)(2,1)S(1)}, bf16[6,16,16,128]{3,2,1,0:T(8,128)(2,1)}, u32[]{:S(2)}) copy-start(bf16[6,16,16,128]{3,2,1,0:T(8,128)(2,1)} %param.9) | copy-start | bytes 1179652
  19.1 7.1 %collective-permute-start.8 = (f32[6,18,1,128]{3,2,1,0:T(1,128)S(1)}, f32[6,18,1,128]{3,2,1,0:T(1,128)S(1)}, u32[]{:S(2)}, u32[]{:S(2)}) collective-permute-start(f32[6,18,1,128]{3,2,1,0:T(1,128)S(1)} %broadcast_select_fusion.5), channel_id=1, source_target_pairs={{0,2},{2,0},{1,3},{3,1},{4,6},{6,4},{5,7},{7,5},{8,10},{10,8},{9,1... | collective-permute-start | bytes 165896 | tf_op jit(solution)/shard_map/ppermute | solution.py:26
  21.9 4.8 %collective-permute-start.3 = (f32[12]{0:T(128)S(1)}, f32[12]{0:T(128)S(1)}, u32[]{:S(2)}, u32[]{:S(2)}) collective-permute-start(f32[12]{0:T(128)S(1)} %add_add_fusion.6), channel_id=1, source_target_pairs={{0,4},{1,5},{2,6},{3,7},{4,0},{5,1},{6,2},{7,3},{8,12},{9,13},{10,... | collective-permute-start | bytes 152 | tf_op jit(solution)/shard_map/ppermute | solution.py:145
  23.4 4.4 %collective-permute-start.4 = (f32[12]{0:T(128)S(1)}, f32[12]{0:T(128)S(1)}, u32[]{:S(2)}, u32[]{:S(2)}) collective-permute-start(f32[12]{0:T(128)S(1)} %add_add_fusion.6), channel_id=1, source_target_pairs={{0,8},{1,9},{2,10},{3,11},{4,12},{5,13},{6,14},{7,15},{8,0},{9,1},... | collective-permute-start | bytes 152 | tf_op jit(solution)/shard_map/ppermute | solution.py:145
  24.5 5.3 %collective-permute-start.5 = (f32[12]{0:T(128)S(1)}, f32[12]{0:T(128)S(1)}, u32[]{:S(2)}, u32[]{:S(2)}) collective-permute-start(f32[12]{0:T(128)S(1)} %add_add_fusion.6), channel_id=1, source_target_pairs={{0,12},{1,13},{2,14},{3,15},{4,8},{5,9},{6,10},{7,11},{8,4},{9,5},... | collective-permute-start | bytes 152 | tf_op jit(solution)/shard_map/ppermute | solution.py:145
  26.6 3.8 %collective-permute-start.9 = (f32[6,18,18,128]{3,2,1,0:T(8,128)S(1)}, f32[6,18,18,128]{3,2,1,0:T(8,128)S(1)}, u32[]{:S(2)}, u32[]{:S(2)}) collective-permute-start(f32[6,18,18,128]{3,2,1,0:T(8,128)S(1)} %maximum_add_fusion), channel_id=1, source_target_pairs={{0,1},{1,0},{2,3},{3,2},{4,5},{5,4},{6,7},{7,6},{8,9},{9,8},{10,11... | collective-permute-start | bytes 2985992 | tf_op jit(solution)/shard_map/ppermute | solution.py:18
  29.9 0.5 copy-start.13
  29.9 7.6 %copy-start.11 = (f32[6]{0:T(128)}, f32[6]{0:T(128)S(1)}, u32[]{:S(2)}) copy-start(f32[6]{0:T(128)S(1)} %slice_multiply_fusion.12) | copy-start | bytes 76
  35.8 0.9 %copy-start.4 = (f32[16,16,128]{2,1,0:T(8,128)S(1)}, f32[16,16,128]{2,1,0:T(8,128)}, u32[]{:S(2)}) copy-start(f32[16,16,128]{2,1,0:T(8,128)} %get-tuple-element.64) | copy-start | bytes 393220
  38.3 6.0 %collective-permute-start.10 = (f32[6,1,16,128]{3,2,1,0:T(8,128)S(1)}, f32[6,1,16,128]{3,2,1,0:T(8,128)S(1)}, u32[]{:S(2)}, u32[]{:S(2)}) collective-permute-start(f32[6,1,16,128]{3,2,1,0:T(8,128)S(1)} %get-tuple-element.61), channel_id=1, source_target_pairs={{4,0},{8,4},{12,8},{5,1},{9,5},{13,9},{6,2},{10,6},{14,10},{7,3},{... | collective-permute-start | bytes 147464 | tf_op jit(solution)/shard_map/ppermute | solution.py:34
  39.6 6.3 %collective-permute-start.11 = (f32[6,1,16,128]{3,2,1,0:T(8,128)S(1)}, f32[6,1,16,128]{3,2,1,0:T(8,128)S(1)}, u32[]{:S(2)}, u32[]{:S(2)}) collective-permute-start(f32[6,1,16,128]{3,2,1,0:T(8,128)S(1)} %get-tuple-element.60), channel_id=1, source_target_pairs={{0,4},{4,8},{8,12},{1,5},{5,9},{9,13},{2,6},{6,10},{10,14},{3,7},{... | collective-permute-start | bytes 147464 | tf_op jit(solution)/shard_map/ppermute | solution.py:33
  46.0 4.2 %collective-permute-start.12 = (f32[6,18,1,128]{3,2,1,0:T(1,128)S(1)}, f32[6,18,1,128]{3,2,1,0:T(1,128)S(1)}, u32[]{:S(2)}, u32[]{:S(2)}) collective-permute-start(f32[6,18,1,128]{3,2,1,0:T(1,128)S(1)} %broadcast_select_fusion.2), channel_id=1, source_target_pairs={{0,2},{2,0},{1,3},{3,1},{4,6},{6,4},{5,7},{7,5},{8,10},{10,8},{9,1... | collective-permute-start | bytes 165896 | tf_op jit(solution)/shard_map/ppermute | solution.py:26
  51.6 6.7 %collective-permute-start.13 = (f32[6,18,18,128]{3,2,1,0:T(8,128)}, f32[6,18,18,128]{3,2,1,0:T(8,128)}, u32[]{:S(2)}, u32[]{:S(2)}) collective-permute-start(f32[6,18,18,128]{3,2,1,0:T(8,128)} %pad_maximum_fusion.4), channel_id=1, source_target_pairs={{0,1},{1,0},{2,3},{3,2},{4,5},{5,4},{6,7},{7,6},{8,9},{9,8},{10,11... | collective-permute-start | bytes 2985992 | tf_op jit(solution)/shard_map/ppermute | solution.py:18
  52.5 1.2 %copy-start.2 = (f32[3,16,16,128]{3,2,1,0:T(8,128)S(1)}, f32[3,16,16,128]{3,2,1,0:T(8,128)}, u32[]{:S(2)}) copy-start(f32[3,16,16,128]{3,2,1,0:T(8,128)} %get-tuple-element.23) | copy-start | bytes 1179652
  65.4 1.1 %copy-start.1 = (f32[6,16,16,128]{3,2,1,0:T(8,128)S(1)}, f32[6,16,16,128]{3,2,1,0:T(8,128)}, u32[]{:S(2)}) copy-start(f32[6,16,16,128]{3,2,1,0:T(8,128)} %convert_element_type.13) | copy-start | bytes 2359300
  65.4 1.1 %copy-start.8 = (f32[3]{0:T(128)S(1)}, f32[3]{0:T(128)}, u32[]{:S(2)}) copy-start(f32[3]{0:T(128)} %copy-done.7) | copy-start | bytes 40
  65.4 1.1 %copy-start.10 = (f32[3]{0:T(128)S(1)}, f32[3]{0:T(128)}, u32[]{:S(2)}) copy-start(f32[3]{0:T(128)} %copy-done.9) | copy-start | bytes 40
  66.8 2.0 %copy-start.15 = (f32[6]{0:T(128)S(1)}, f32[6]{0:T(128)}, u32[]{:S(2)}) copy-start(f32[6]{0:T(128)} %get-tuple-element.58) | copy-start | bytes 76
  66.8 16.4 %copy-start.12 = (f32[6]{0:T(128)S(1)}, f32[6]{0:T(128)}, u32[]{:S(2)}) copy-start(f32[6]{0:T(128)} %copy-done.11) | copy-start | bytes 76
  66.9 16.4 %copy-start.14 = (f32[12]{0:T(128)S(1)}, f32[12]{0:T(128)}, u32[]{:S(2)}) copy-start(f32[12]{0:T(128)} %copy-done.13) | copy-start | bytes 148
  68.9 2.6 %collective-permute-start.14 = (f32[902]{0:T(1024)S(1)}, f32[902]{0:T(1024)S(1)}, u32[]{:S(2)}, u32[]{:S(2)}) collective-permute-start(f32[902]{0:T(1024)S(1)} %pad_maximum_fusion.16), channel_id=1, source_target_pairs={{0,1},{1,0},{2,3},{3,2},{4,5},{5,4},{6,7},{7,6},{8,9},{9,8},{10,11... | collective-permute-start | bytes 10832 | tf_op jit(solution)/shard_map/ppermute | solution.py:145
  69.4 3.7 %collective-permute-start.15 = (f32[902]{0:T(1024)S(1)}, f32[902]{0:T(1024)S(1)}, u32[]{:S(2)}, u32[]{:S(2)}) collective-permute-start(f32[902]{0:T(1024)S(1)} %pad_maximum_fusion.16), channel_id=1, source_target_pairs={{0,2},{1,3},{2,0},{3,1},{4,6},{5,7},{6,4},{7,5},{8,10},{9,11},{10,... | collective-permute-start | bytes 10832 | tf_op jit(solution)/shard_map/ppermute | solution.py:145
  71.5 3.1 %collective-permute-start.16 = (f32[902]{0:T(1024)S(1)}, f32[902]{0:T(1024)S(1)}, u32[]{:S(2)}, u32[]{:S(2)}) collective-permute-start(f32[902]{0:T(1024)S(1)} %pad_maximum_fusion.16), channel_id=1, source_target_pairs={{0,3},{1,2},{2,1},{3,0},{4,7},{5,6},{6,5},{7,4},{8,11},{9,10},{10,... | collective-permute-start | bytes 10832 | tf_op jit(solution)/shard_map/ppermute | solution.py:145
  74.5 4.8 %collective-permute-start.17 = (f32[902]{0:T(1024)S(1)}, f32[902]{0:T(1024)S(1)}, u32[]{:S(2)}, u32[]{:S(2)}) collective-permute-start(f32[902]{0:T(1024)S(1)} %add_add_fusion.3), channel_id=1, source_target_pairs={{0,4},{1,5},{2,6},{3,7},{4,0},{5,1},{6,2},{7,3},{8,12},{9,13},{10,... | collective-permute-start | bytes 10832 | tf_op jit(solution)/shard_map/ppermute | solution.py:145
  76.9 4.5 %collective-permute-start.18 = (f32[902]{0:T(1024)S(1)}, f32[902]{0:T(1024)S(1)}, u32[]{:S(2)}, u32[]{:S(2)}) collective-permute-start(f32[902]{0:T(1024)S(1)} %add_add_fusion.3), channel_id=1, source_target_pairs={{0,8},{1,9},{2,10},{3,11},{4,12},{5,13},{6,14},{7,15},{8,0},{9,1},... | collective-permute-start | bytes 10832 | tf_op jit(solution)/shard_map/ppermute | solution.py:145
  77.8 5.4 %collective-permute-start.19 = (f32[902]{0:T(1024)S(1)}, f32[902]{0:T(1024)S(1)}, u32[]{:S(2)}, u32[]{:S(2)}) collective-permute-start(f32[902]{0:T(1024)S(1)} %add_add_fusion.3), channel_id=1, source_target_pairs={{0,12},{1,13},{2,14},{3,15},{4,8},{5,9},{6,10},{7,11},{8,4},{9,5},... | collective-permute-start | bytes 10832 | tf_op jit(solution)/shard_map/ppermute | solution.py:145

commit v13 on v12

--- a/solution.py
+++ b/solution.py
@@ -205,8 +205,16 @@
         lead = cells.shape[:-3]
         local = cells.reshape(lead + (coarse_x, 4, coarse_y, 4, tile_shape[2]))
         local = local.sum(axis=(-4, -2, -1))
-        grid = jnp.zeros(lead + grid_shape, jnp.float32)
-        return lax.dynamic_update_slice(grid, local, (0,) * len(lead) + grid_at)
+        rows = lax.broadcasted_iota(jnp.int32, (grid_shape[0], coarse_x), 0)
+        cols = lax.broadcasted_iota(jnp.int32, (grid_shape[1], coarse_y), 0)
+        pick_x = (rows == grid_at[0] + lax.broadcasted_iota(jnp.int32, rows.shape, 1))
+        pick_y = (cols == grid_at[1] + lax.broadcasted_iota(jnp.int32, cols.shape, 1))
+        spread = (
+            local[..., None, None, :, :]
+            * pick_x.astype(jnp.float32)[:, None, :, None]
+            * pick_y.astype(jnp.float32)[None, :, None, :]
+        )
+        return spread.sum(axis=(-2, -1))
 
     forward_cells = forward.astype(jnp.float32)
     forward_real = forward_cells[:3]

time: 87.4 us -> 87.9 us (level)
  other arithmetic: 30.4 us -> 35.5 us
  waiting for transfers between devices: 16.1 us -> 14 us
  local copies, waits for them, and re-layouts: 9.03 us -> 7.18 us
    dynamic_update_slice x2 -> x0, local copies, waits for them, and re-layouts: 2 us -> none  [block_sums(): return lax.dynamic_update_slice(grid, local, (0,) * len(lead) + grid_at)]
    convert_element_type x0 -> x2, other arithmetic: none -> 1.36 us  [the longest x1 0.68 us: block_sums(): pick_y.astype(jnp.float32)[None, :, None, :]]
    reduce_sum x4, other arithmetic: 1.82 us -> 2.95 us  [block_sums(): local = local.sum(axis=(-4, -2, -1))]
    add x0 -> x2, other arithmetic: none -> 1.05 us  [the longest x1 0.53 us: block_sums(): pick_y = cols == grid_at[1] + lax.broadcasted_iota(jnp.int32, cols.shape, 1)]
    convert_element_type x1, other arithmetic: 0.95 us -> 1.95 us  [shards(): source_cells = source.astype(jnp.float32)]
  transfers between devices with their start and end apart: 20 -> 20, of which waited for: 9 -> 9; matrix products, arithmetic and copies ran while one was open for 18% -> 22% of each run, Pallas kernels for 0% -> 0%
where the time goes in v13:
time: 87.9 us; the launch traced here: 87.3 us
  other arithmetic  35.5 us (40%)
  starting transfers between devices  28.6 us (33%)
  waiting for transfers between devices  14 us (16%)
  local copies, waits for them, and re-layouts  7.18 us (8%)
  between operations  2.02 us (2%)
    ppermute x12, starting transfers between devices, group_rounds(): lax.ppermute(value, axes, [(i, i ^ m * stride) for i in range(size)])  13.2 us
    ppermute x12, waiting for transfers between devices, group_rounds(): lax.ppermute(value, axes, [(i, i ^ m * stride) for i in range(size)])  10.3 us
    ppermute x2, starting transfers between devices, with_halo(): before = lax.ppermute(last, axis, up)  10.3 us
    concatenate x5, other arithmetic, with_halo(): array = jnp.concatenate([before, array, after], axis=dim)  5.96 us
    add x12, other arithmetic, navier(): result.append(shear * laplace[channel] + (lame_first + shear) * divergence)  5.61 us
    ppermute x2, waiting for transfers between devices, with_halo(): got = lax.ppermute(jnp.where(first, last, initial), axis, [(0, 1), (1, 0)])  2.98 us
    reduce_sum x4, other arithmetic, block_sums(): local = local.sum(axis=(-4, -2, -1))  2.95 us
    select_n x2, other arithmetic, with_halo(): after = jnp.where(first, got_initial, zero)  2.64 us
  transfers between devices with their start and end apart: 20, of which 9 were waited for; matrix products, arithmetic and copies ran while one was open for 22% of the time, Pallas kernels for 0%

profile of v13, /device:TPU:0, one launch (start us, length us, event | category | flops | bytes accessed | tf_op | source)
XLA Modules:
  0.0 87.3 jit_solution(8303271866617649666)
XLA Ops:
  0.7 0.8 fusion.109
  1.5 1.3 %collective-permute-start.6 = (f32[6,1,16,128]{3,2,1,0:T(8,128)S(1)}, f32[6,1,16,128]{3,2,1,0:T(8,128)S(1)}, u32[]{:S(2)}, u32[]{:S(2)}) collective-permute-start(f32[6,1,16,128]{3,2,1,0:T(8,128)S(1)} %get-tuple-element.63), channel_id=1, source_target_pairs={{4,0},{8,4},{12,8},{5,1},{9,5},{13,9},{6,2},{10,6},{14,10},{7,3},{... | collective-permute-start | bytes 147464 | tf_op jit(solution)/shard_map/ppermute | solution.py:34
  2.8 5.6 %collective-permute-start.7 = (f32[6,1,16,128]{3,2,1,0:T(8,128)S(1)}, f32[6,1,16,128]{3,2,1,0:T(8,128)S(1)}, u32[]{:S(2)}, u32[]{:S(2)}) collective-permute-start(f32[6,1,16,128]{3,2,1,0:T(8,128)S(1)} %get-tuple-element.62), channel_id=1, source_target_pairs={{0,4},{4,8},{8,12},{1,5},{5,9},{9,13},{2,6},{6,10},{10,14},{3,7},{... | collective-permute-start | bytes 147464 | tf_op jit(solution)/shard_map/ppermute | solution.py:33
  8.4 0.7 compare_select_fusion
  9.1 1.5 %scatter_custom_fusion = f32[32768]{0:T(1024)S(1)} fusion(s32[256]{0:T(256)S(1)} %bitcast.47, f32[256]{0:T(256)S(1)} %broadcast.378, f32[]{:T(128)} %constant.28.clone.1), kind=kCustom, calls=%fused_computation.247 | custom fusion | bytes 131076 | tf_op jit(solution)/shard_map/scatter | solution.py:187
  10.5 1.2 %multiply_reduce_fusion.1 = f32[6]{0:T(128)S(1)} fusion(bf16[6,16,16,128]{3,2,1,0:T(8,128)(2,1)} %param.10, f32[16,16,128]{2,1,0:T(8,128)S(1)} %bitcast.36), kind=kLoop, calls=%fused_computation.46 | loop fusion | flops 589818 | bytes 524312 | tf_op jit(solution)/shard_map/reduce_sum | solution.py:231
  11.7 0.8 slice_bitcast_fusion.2
  13.1 0.8 slice_bitcast_fusion.1
  14.4 0.7 convert_multiply_fusion
  15.1 1.4 %multiply_subtract_fusion = (f32[3,16,16,128]{3,2,1,0:T(8,128)}, f32[3,16,16,128]{3,2,1,0:T(8,128)}, f32[3,16,16,128]{3,2,1,0:T(8,128)}, f32[3,16,16,128]{3,2,1,0:T(8,128)S(1)}, f32[3,16,16,128]{3,2,1,0:T(8,128)S(1)}) fusion(f32[6,16,16,128]{3,2,1,0:T(8,128)S(1)} %convert_element_type.39, f32[3]{0:T(128)S(1)} %get-tuple-element.78, ...), kind=kLoop, calls=%fused_computation.65 | loop fusion | flops 2359296 | bytes 3276824 | tf_op jit(solution)/shard_map/sub | solution.py:224
  16.8 2.0 %collective-permute-start.1 = (f32[12]{0:T(128)S(1)}, f32[12]{0:T(128)S(1)}, u32[]{:S(2)}, u32[]{:S(2)}) collective-permute-start(f32[12]{0:T(128)S(1)} %pad_maximum_fusion.17), channel_id=1, source_target_pairs={{0,2},{1,3},{2,0},{3,1},{4,6},{5,7},{6,4},{7,5},{8,10},{9,11},{10,... | collective-permute-start | bytes 152 | tf_op jit(solution)/shard_map/ppermute | solution.py:145
  19.1 1.8 %collective-permute-start.8 = (f32[6,18,1,128]{3,2,1,0:T(1,128)S(1)}, f32[6,18,1,128]{3,2,1,0:T(1,128)S(1)}, u32[]{:S(2)}, u32[]{:S(2)}) collective-permute-start(f32[6,18,1,128]{3,2,1,0:T(1,128)S(1)} %broadcast_select_fusion.5), channel_id=1, source_target_pairs={{0,2},{2,0},{1,3},{3,1},{4,6},{6,4},{5,7},{7,5},{8,10},{10,8},{9,1... | collective-permute-start | bytes 165896 | tf_op jit(solution)/shard_map/ppermute | solution.py:26
  20.9 0.9 %collective-permute-done.2 = f32[12]{0:T(128)S(1)} collective-permute-done((f32[12]{0:T(128)S(1)}, f32[12]{0:T(128)S(1)}, u32[]{:S(2)}, u32[]{:S(2)}) %collective-permute-start.2) | collective-permute-done | bytes 80 | tf_op jit(solution)/shard_map/ppermute | solution.py:145
  21.8 1.6 %collective-permute-start.3 = (f32[12]{0:T(128)S(1)}, f32[12]{0:T(128)S(1)}, u32[]{:S(2)}, u32[]{:S(2)}) collective-permute-start(f32[12]{0:T(128)S(1)} %add_add_fusion.6), channel_id=1, source_target_pairs={{0,4},{1,5},{2,6},{3,7},{4,0},{5,1},{6,2},{7,3},{8,12},{9,13},{10,... | collective-permute-start | bytes 152 | tf_op jit(solution)/shard_map/ppermute | solution.py:145
  23.4 1.1 %collective-permute-start.4 = (f32[12]{0:T(128)S(1)}, f32[12]{0:T(128)S(1)}, u32[]{:S(2)}, u32[]{:S(2)}) collective-permute-start(f32[12]{0:T(128)S(1)} %add_add_fusion.6), channel_id=1, source_target_pairs={{0,8},{1,9},{2,10},{3,11},{4,12},{5,13},{6,14},{7,15},{8,0},{9,1},... | collective-permute-start | bytes 152 | tf_op jit(solution)/shard_map/ppermute | solution.py:145
  24.5 1.7 %collective-permute-start.5 = (f32[12]{0:T(128)S(1)}, f32[12]{0:T(128)S(1)}, u32[]{:S(2)}, u32[]{:S(2)}) collective-permute-start(f32[12]{0:T(128)S(1)} %add_add_fusion.6), channel_id=1, source_target_pairs={{0,12},{1,13},{2,14},{3,15},{4,8},{5,9},{6,10},{7,11},{8,4},{9,5},... | collective-permute-start | bytes 152 | tf_op jit(solution)/shard_map/ppermute | solution.py:145
  26.7 1.2 %collective-permute-done.4 = f32[12]{0:T(128)S(1)} collective-permute-done((f32[12]{0:T(128)S(1)}, f32[12]{0:T(128)S(1)}, u32[]{:S(2)}, u32[]{:S(2)}) %collective-permute-start.4) | collective-permute-done | bytes 80 | tf_op jit(solution)/shard_map/ppermute | solution.py:145
  27.8 2.0 %collective-permute-done.5 = f32[12]{0:T(128)S(1)} collective-permute-done((f32[12]{0:T(128)S(1)}, f32[12]{0:T(128)S(1)}, u32[]{:S(2)}, u32[]{:S(2)}) %collective-permute-start.5) | collective-permute-done | bytes 80 | tf_op jit(solution)/shard_map/ppermute | solution.py:145
  30.8 2.1 %pad_maximum_fusion = (f32[6,18,18,129]{3,2,1,0:T(8,128)S(1)}, f32[6,18,18,129]{3,2,1,0:T(8,128)S(1)}) fusion(f32[6,18,18,1]{3,2,1,0:T(8,128)S(1)} %get-tuple-element.48, f32[6,18,1,128]{3,2,1,0:T(1,128)S(1)} %get-tuple-element.70, f32[6,1,16,128]{3,2,1,0:T(8,128)S(1)} %collective-permute-done.6, f32[6,16,16,128]{3,2,1,0:T(8,128)S(1)} %convert_element_type.36, ...), kind=kLoop, calls=%fused_computation.1 | loop fusion | flops 2507760 | bytes 3017088 | tf_op jit(solution)/shard_map/concatenate | solution.py:35
  35.8 0.7 fusion.64
  37.5 0.7 multiply_reduce_fusion
  38.3 1.3 %collective-permute-start.10 = (f32[6,1,16,128]{3,2,1,0:T(8,128)S(1)}, f32[6,1,16,128]{3,2,1,0:T(8,128)S(1)}, u32[]{:S(2)}, u32[]{:S(2)}) collective-permute-start(f32[6,1,16,128]{3,2,1,0:T(8,128)S(1)} %get-tuple-element.61), channel_id=1, source_target_pairs={{4,0},{8,4},{12,8},{5,1},{9,5},{13,9},{6,2},{10,6},{14,10},{7,3},{... | collective-permute-start | bytes 147464 | tf_op jit(solution)/shard_map/ppermute | solution.py:34
  39.6 4.7 %collective-permute-start.11 = (f32[6,1,16,128]{3,2,1,0:T(8,128)S(1)}, f32[6,1,16,128]{3,2,1,0:T(8,128)S(1)}, u32[]{:S(2)}, u32[]{:S(2)}) collective-permute-start(f32[6,1,16,128]{3,2,1,0:T(8,128)S(1)} %get-tuple-element.60), channel_id=1, source_target_pairs={{0,4},{4,8},{8,12},{1,5},{5,9},{9,13},{2,6},{6,10},{10,14},{3,7},{... | collective-permute-start | bytes 147464 | tf_op jit(solution)/shard_map/ppermute | solution.py:33
  44.3 0.8 multiply_add_fusion
  45.2 0.7 collective-permute-done.11
  45.9 0.7 collective-permute-start.12
  47.2 3.0 %collective-permute-done.12 = f32[6,18,1,128]{3,2,1,0:T(1,128)S(1)} collective-permute-done((f32[6,18,1,128]{3,2,1,0:T(1,128)S(1)}, f32[6,18,1,128]{3,2,1,0:T(1,128)S(1)}, u32[]{:S(2)}, u32[]{:S(2)}) %collective-permute-start.12) | collective-permute-done | bytes 55328 | tf_op jit(solution)/shard_map/ppermute | solution.py:26
  50.2 1.3 %pad_maximum_fusion.4 = f32[6,18,18,128]{3,2,1,0:T(8,128)} fusion(f32[6,18,1,128]{3,2,1,0:T(1,128)S(1)} %get-tuple-element.68, f32[6,1,16,128]{3,2,1,0:T(8,128)S(1)} %collective-permute-done.10, f32[6,16,16,128]{3,2,1,0:T(8,128)S(1)} %get-tuple-element.59, f32[6,1,16,128]{3,2,1,0:T(8,128)S(1)} %collective-permute-done.11, ...), kind=kLoop, calls=%fused_computation.14 | loop fusion | flops 995328 | bytes 1990656 | tf_op jit(solution)/shard_map/concatenate | solution.py:35
  52.0 1.9 %convert_element_type.37 = f32[6,16,16,128]{3,2,1,0:T(8,128)} convert(bf16[6,16,16,128]{3,2,1,0:T(8,128)(2,1)} %param.9) | non-fusion elementwise | flops 196608 | bytes 1179648 | tf_op jit(solution)/shard_map/convert_element_type | solution.py:192
  54.0 2.0 %maximum_reduce_fusion = f32[6,16,16]{2,1,0:T(8,128)} fusion(f32[3,16,16,128]{3,2,1,0:T(8,128)} %multiply_add_fusion, f32[3,16,16,128]{3,2,1,0:T(8,128)} %get-tuple-element.23), kind=kLoop, calls=%fused_computation.42 | loop fusion | flops 391680 | bytes 792576 | tf_op jit(solution)/shard_map/reduce_sum | solution.py:207
  56.0 0.9 %reduce_sum.134 = f32[6,4,4,4,4]{4,3,2,1,0:T(4,128)S(1)} reshape(f32[6,16,16]{2,1,0:T(8,128)} %maximum_reduce_fusion) | data formatting | bytes 12288 | tf_op jit(solution)/shard_map/reduce_sum | solution.py:207
  57.0 0.7 reduce_sum.135
  57.7 0.7 fusion.100
  58.4 0.7 fusion.101
  59.0 0.8 broadcast_multiply_fusion.2
  60.4 2.2 %slice_select_fusion.1 = (f32[6,18,18,1]{3,2,1,0:T(8,128)S(1)}, f32[6,18,18,1]{3,2,1,0:T(8,128)S(1)}) fusion(f32[6,18,18,128]{3,2,1,0:T(8,128)} %collective-permute-done.13, pred[]{:T(512)S(6)} %eq.91), kind=kLoop, calls=%fused_computation.6 | loop fusion | flops 3888 | bytes 31105 | tf_op jit(solution)/shard_map/jit(_where)/select_n | solution.py:23
  62.6 2.1 %pad_maximum_fusion.1 = (f32[6,18,18,129]{3,2,1,0:T(8,128)S(1)}, f32[6,18,18,129]{3,2,1,0:T(8,128)S(1)}) fusion(f32[6,18,18,1]{3,2,1,0:T(8,128)S(1)} %get-tuple-element.46, f32[6,18,1,128]{3,2,1,0:T(1,128)S(1)} %get-tuple-element.68, f32[6,1,16,128]{3,2,1,0:T(8,128)S(1)} %collective-permute-done.10, f32[6,16,16,128]{3,2,1,0:T(8,128)S(1)} %get-tuple-element.59, ...), kind=kLoop, calls=%fused_computation.3 | loop fusion | flops 2507760 | bytes 3017088 | tf_op jit(solution)/shard_map/concatenate | solution.py:35
  66.8 0.7 fusion.28
  68.9 1.2 %subtract_reduce_fusion = (f32[16,16,128]{2,1,0:T(8,128)S(1)}, f32[3,16,16,128]{3,2,1,0:T(8,128)S(1)}, f32[3,16,16,128]{3,2,1,0:T(8,128)}) fusion(f32[6,16,16,128]{3,2,1,0:T(8,128)S(1)} %convert_element_type.39, f32[3,16,16,128]{3,2,1,0:T(8,128)S(1)} %get-tuple-element.45, f32[3]{0:T(128)S(1)} %copy-done.11, f32[16,16,128]{2,1,0:T(8,128)S(1)} %get-tuple-element.66, ...), kind=kLoop, calls=%fused_computation.68 | loop fusion | flops 2719744 | bytes 3670040 | tf_op jit(solution)/shard_map/reduce_sum | solution.py:256
  72.0 0.8 collective-permute-start.16
  72.8 2.2 %collective-permute-done.15 = f32[902]{0:T(1024)S(1)} collective-permute-done((f32[902]{0:T(1024)S(1)}, f32[902]{0:T(1024)S(1)}, u32[]{:S(2)}, u32[]{:S(2)}) %collective-permute-start.15) | collective-permute-done | bytes 3640 | tf_op jit(solution)/shard_map/ppermute | solution.py:145
  75.0 2.3 %collective-permute-start.17 = (f32[902]{0:T(1024)S(1)}, f32[902]{0:T(1024)S(1)}, u32[]{:S(2)}, u32[]{:S(2)}) collective-permute-start(f32[902]{0:T(1024)S(1)} %add_add_fusion.3), channel_id=1, source_target_pairs={{0,4},{1,5},{2,6},{3,7},{4,0},{5,1},{6,2},{7,3},{8,12},{9,13},{10,... | collective-permute-start | bytes 10832 | tf_op jit(solution)/shard_map/ppermute | solution.py:145
  77.4 1.0 %collective-permute-start.18 = (f32[902]{0:T(1024)S(1)}, f32[902]{0:T(1024)S(1)}, u32[]{:S(2)}, u32[]{:S(2)}) collective-permute-start(f32[902]{0:T(1024)S(1)} %add_add_fusion.3), channel_id=1, source_target_pairs={{0,8},{1,9},{2,10},{3,11},{4,12},{5,13},{6,14},{7,15},{8,0},{9,1},... | collective-permute-start | bytes 10832 | tf_op jit(solution)/shard_map/ppermute | solution.py:145
  78.4 1.4 %collective-permute-start.19 = (f32[902]{0:T(1024)S(1)}, f32[902]{0:T(1024)S(1)}, u32[]{:S(2)}, u32[]{:S(2)}) collective-permute-start(f32[902]{0:T(1024)S(1)} %add_add_fusion.3), channel_id=1, source_target_pairs={{0,12},{1,13},{2,14},{3,15},{4,8},{5,9},{6,10},{7,11},{8,4},{9,5},... | collective-permute-start | bytes 10832 | tf_op jit(solution)/shard_map/ppermute | solution.py:145
  79.8 2.1 %collective-permute-done.18 = f32[902]{0:T(1024)S(1)} collective-permute-done((f32[902]{0:T(1024)S(1)}, f32[902]{0:T(1024)S(1)}, u32[]{:S(2)}, u32[]{:S(2)}) %collective-permute-start.18) | collective-permute-done | bytes 3640 | tf_op jit(solution)/shard_map/ppermute | solution.py:145
  81.9 1.9 %collective-permute-done.19 = f32[902]{0:T(1024)S(1)} collective-permute-done((f32[902]{0:T(1024)S(1)}, f32[902]{0:T(1024)S(1)}, u32[]{:S(2)}, u32[]{:S(2)}) %collective-permute-start.19) | collective-permute-done | bytes 3640 | tf_op jit(solution)/shard_map/ppermute | solution.py:145
  84.5 0.7 copy.18
  85.3 2.0 %fusion.13 = f32[6,16,16,128]{3,2,1,0:T(8,128)} fusion(f32[3,16,16,128]{3,2,1,0:T(8,128)S(1)} %get-tuple-element.27, f32[3,16,16,128]{3,2,1,0:T(8,128)S(1)} %get-tuple-element.26, f32[3,16,16,128]{3,2,1,0:T(8,128)} %get-tuple-element.22, f32[3,16,16,128]{3,2,1,0:T(8,128)S(1)} %get-tuple-element.21, f32[6]{0:T(128)S(1)} %pad_maximum_fusion.19, ...), kind=kLoop, calls=%fused_computation.38 | loop fusion | flops 1376256 | bytes 2359344 | tf_op jit(solution)/shard_map/add | solution.py:131
  (125 shorter events, 14.2 us)
Async XLA Ops:
  0.6 13.3 %copy-start.6 = (bf16[6,16,16,128]{3,2,1,0:T(8,128)(2,1)S(1)}, bf16[6,16,16,128]{3,2,1,0:T(8,128)(2,1)}, u32[]{:S(2)}) copy-start(bf16[6,16,16,128]{3,2,1,0:T(8,128)(2,1)} %param.11) | copy-start | bytes 1179652
  0.6 13.3 %copy-start.17 = (s32[2,2,4]{2,1,0:T(2,128)S(1)}, s32[2,2,4]{2,1,0:T(2,128)}, u32[]{:S(2)}) copy-start(s32[2,2,4]{2,1,0:T(2,128)} %param.13) | copy-start | bytes 196
  0.7 13.8 %copy-start.7 = (bf16[16,16,128]{2,1,0:T(8,128)(2,1)S(1)}, bf16[16,16,128]{2,1,0:T(8,128)(2,1)}, u32[]{:S(2)}) copy-start(bf16[16,16,128]{2,1,0:T(8,128)(2,1)} %param.12) | copy-start | bytes 196612
  1.5 17.5 %collective-permute-start.6 = (f32[6,1,16,128]{3,2,1,0:T(8,128)S(1)}, f32[6,1,16,128]{3,2,1,0:T(8,128)S(1)}, u32[]{:S(2)}, u32[]{:S(2)}) collective-permute-start(f32[6,1,16,128]{3,2,1,0:T(8,128)S(1)} %get-tuple-element.63), channel_id=1, source_target_pairs={{4,0},{8,4},{12,8},{5,1},{9,5},{13,9},{6,2},{10,6},{14,10},{7,3},{... | collective-permute-start | bytes 147464 | tf_op jit(solution)/shard_map/ppermute | solution.py:34
  2.8 16.2 %collective-permute-start.7 = (f32[6,1,16,128]{3,2,1,0:T(8,128)S(1)}, f32[6,1,16,128]{3,2,1,0:T(8,128)S(1)}, u32[]{:S(2)}, u32[]{:S(2)}) collective-permute-start(f32[6,1,16,128]{3,2,1,0:T(8,128)S(1)} %get-tuple-element.62), channel_id=1, source_target_pairs={{0,4},{4,8},{8,12},{1,5},{5,9},{9,13},{2,6},{6,10},{10,14},{3,7},{... | collective-permute-start | bytes 147464 | tf_op jit(solution)/shard_map/ppermute | solution.py:33
  13.9 23.3 %copy-start.8 = (f32[3]{0:T(128)}, f32[3]{0:T(128)S(1)}, u32[]{:S(2)}) copy-start(f32[3]{0:T(128)S(1)} %get-tuple-element.77) | copy-start | bytes 40
  13.9 23.3 %copy-start.10 = (f32[3]{0:T(128)}, f32[3]{0:T(128)S(1)}, u32[]{:S(2)}) copy-start(f32[3]{0:T(128)S(1)} %get-tuple-element.78) | copy-start | bytes 40
  15.1 3.8 %copy-start = (bf16[6,16,16,128]{3,2,1,0:T(8,128)(2,1)S(1)}, bf16[6,16,16,128]{3,2,1,0:T(8,128)(2,1)}, u32[]{:S(2)}) copy-start(bf16[6,16,16,128]{3,2,1,0:T(8,128)(2,1)} %param.10) | copy-start | bytes 1179652
  16.8 4.1 %collective-permute-start = (f32[12]{0:T(128)S(1)}, f32[12]{0:T(128)S(1)}, u32[]{:S(2)}, u32[]{:S(2)}) collective-permute-start(f32[12]{0:T(128)S(1)} %pad_maximum_fusion.17), channel_id=1, source_target_pairs={{0,1},{1,0},{2,3},{3,2},{4,5},{5,4},{6,7},{7,6},{8,9},{9,8},{10,11... | collective-permute-start | bytes 152 | tf_op jit(solution)/shard_map/ppermute | solution.py:145
  16.8 4.1 %collective-permute-start.1 = (f32[12]{0:T(128)S(1)}, f32[12]{0:T(128)S(1)}, u32[]{:S(2)}, u32[]{:S(2)}) collective-permute-start(f32[12]{0:T(128)S(1)} %pad_maximum_fusion.17), channel_id=1, source_target_pairs={{0,2},{1,3},{2,0},{3,1},{4,6},{5,7},{6,4},{7,5},{8,10},{9,11},{10,... | collective-permute-start | bytes 152 | tf_op jit(solution)/shard_map/ppermute | solution.py:145
  18.8 3.0 %collective-permute-start.2 = (f32[12]{0:T(128)S(1)}, f32[12]{0:T(128)S(1)}, u32[]{:S(2)}, u32[]{:S(2)}) collective-permute-start(f32[12]{0:T(128)S(1)} %pad_maximum_fusion.17), channel_id=1, source_target_pairs={{0,3},{1,2},{2,1},{3,0},{4,7},{5,6},{6,5},{7,4},{8,11},{9,10},{10,... | collective-permute-start | bytes 152 | tf_op jit(solution)/shard_map/ppermute | solution.py:145
  19.1 10.9 %copy-start.4 = (bf16[6,16,16,128]{3,2,1,0:T(8,128)(2,1)S(1)}, bf16[6,16,16,128]{3,2,1,0:T(8,128)(2,1)}, u32[]{:S(2)}) copy-start(bf16[6,16,16,128]{3,2,1,0:T(8,128)(2,1)} %param.9) | copy-start | bytes 1179652
  19.1 7.1 %collective-permute-start.8 = (f32[6,18,1,128]{3,2,1,0:T(1,128)S(1)}, f32[6,18,1,128]{3,2,1,0:T(1,128)S(1)}, u32[]{:S(2)}, u32[]{:S(2)}) collective-permute-start(f32[6,18,1,128]{3,2,1,0:T(1,128)S(1)} %broadcast_select_fusion.5), channel_id=1, source_target_pairs={{0,2},{2,0},{1,3},{3,1},{4,6},{6,4},{5,7},{7,5},{8,10},{10,8},{9,1... | collective-permute-start | bytes 165896 | tf_op jit(solution)/shard_map/ppermute | solution.py:26
  21.8 4.8 %collective-permute-start.3 = (f32[12]{0:T(128)S(1)}, f32[12]{0:T(128)S(1)}, u32[]{:S(2)}, u32[]{:S(2)}) collective-permute-start(f32[12]{0:T(128)S(1)} %add_add_fusion.6), channel_id=1, source_target_pairs={{0,4},{1,5},{2,6},{3,7},{4,0},{5,1},{6,2},{7,3},{8,12},{9,13},{10,... | collective-permute-start | bytes 152 | tf_op jit(solution)/shard_map/ppermute | solution.py:145
  23.4 4.4 %collective-permute-start.4 = (f32[12]{0:T(128)S(1)}, f32[12]{0:T(128)S(1)}, u32[]{:S(2)}, u32[]{:S(2)}) collective-permute-start(f32[12]{0:T(128)S(1)} %add_add_fusion.6), channel_id=1, source_target_pairs={{0,8},{1,9},{2,10},{3,11},{4,12},{5,13},{6,14},{7,15},{8,0},{9,1},... | collective-permute-start | bytes 152 | tf_op jit(solution)/shard_map/ppermute | solution.py:145
  24.5 5.3 %collective-permute-start.5 = (f32[12]{0:T(128)S(1)}, f32[12]{0:T(128)S(1)}, u32[]{:S(2)}, u32[]{:S(2)}) collective-permute-start(f32[12]{0:T(128)S(1)} %add_add_fusion.6), channel_id=1, source_target_pairs={{0,12},{1,13},{2,14},{3,15},{4,8},{5,9},{6,10},{7,11},{8,4},{9,5},... | collective-permute-start | bytes 152 | tf_op jit(solution)/shard_map/ppermute | solution.py:145
  26.6 3.8 %collective-permute-start.9 = (f32[6,18,18,128]{3,2,1,0:T(8,128)S(1)}, f32[6,18,18,128]{3,2,1,0:T(8,128)S(1)}, u32[]{:S(2)}, u32[]{:S(2)}) collective-permute-start(f32[6,18,18,128]{3,2,1,0:T(8,128)S(1)} %maximum_add_fusion), channel_id=1, source_target_pairs={{0,1},{1,0},{2,3},{3,2},{4,5},{5,4},{6,7},{7,6},{8,9},{9,8},{10,11... | collective-permute-start | bytes 2985992 | tf_op jit(solution)/shard_map/ppermute | solution.py:18
  29.8 0.5 copy-start.14
  29.9 7.6 %copy-start.12 = (f32[6]{0:T(128)}, f32[6]{0:T(128)S(1)}, u32[]{:S(2)}) copy-start(f32[6]{0:T(128)S(1)} %slice_multiply_fusion.12) | copy-start | bytes 76
  35.8 0.9 %copy-start.5 = (f32[16,16,128]{2,1,0:T(8,128)S(1)}, f32[16,16,128]{2,1,0:T(8,128)}, u32[]{:S(2)}) copy-start(f32[16,16,128]{2,1,0:T(8,128)} %get-tuple-element.64) | copy-start | bytes 393220
  37.5 6.8 %copy-start.2 = (f32[3,16,16,128]{3,2,1,0:T(8,128)S(1)}, f32[3,16,16,128]{3,2,1,0:T(8,128)}, u32[]{:S(2)}) copy-start(f32[3,16,16,128]{3,2,1,0:T(8,128)} %get-tuple-element.24) | copy-start | bytes 1179652
  37.5 6.8 %copy-start.3 = (f32[3,16,16,128]{3,2,1,0:T(8,128)S(1)}, f32[3,16,16,128]{3,2,1,0:T(8,128)}, u32[]{:S(2)}) copy-start(f32[3,16,16,128]{3,2,1,0:T(8,128)} %get-tuple-element.25) | copy-start | bytes 1179652
  38.3 6.9 %collective-permute-start.10 = (f32[6,1,16,128]{3,2,1,0:T(8,128)S(1)}, f32[6,1,16,128]{3,2,1,0:T(8,128)S(1)}, u32[]{:S(2)}, u32[]{:S(2)}) collective-permute-start(f32[6,1,16,128]{3,2,1,0:T(8,128)S(1)} %get-tuple-element.61), channel_id=1, source_target_pairs={{4,0},{8,4},{12,8},{5,1},{9,5},{13,9},{6,2},{10,6},{14,10},{7,3},{... | collective-permute-start | bytes 147464 | tf_op jit(solution)/shard_map/ppermute | solution.py:34
  39.6 6.3 %collective-permute-start.11 = (f32[6,1,16,128]{3,2,1,0:T(8,128)S(1)}, f32[6,1,16,128]{3,2,1,0:T(8,128)S(1)}, u32[]{:S(2)}, u32[]{:S(2)}) collective-permute-start(f32[6,1,16,128]{3,2,1,0:T(8,128)S(1)} %get-tuple-element.60), channel_id=1, source_target_pairs={{0,4},{4,8},{8,12},{1,5},{5,9},{9,13},{2,6},{6,10},{10,14},{3,7},{... | collective-permute-start | bytes 147464 | tf_op jit(solution)/shard_map/ppermute | solution.py:33
  45.9 4.2 %collective-permute-start.12 = (f32[6,18,1,128]{3,2,1,0:T(1,128)S(1)}, f32[6,18,1,128]{3,2,1,0:T(1,128)S(1)}, u32[]{:S(2)}, u32[]{:S(2)}) collective-permute-start(f32[6,18,1,128]{3,2,1,0:T(1,128)S(1)} %broadcast_select_fusion.2), channel_id=1, source_target_pairs={{0,2},{2,0},{1,3},{3,1},{4,6},{6,4},{5,7},{7,5},{8,10},{10,8},{9,1... | collective-permute-start | bytes 165896 | tf_op jit(solution)/shard_map/ppermute | solution.py:26
  51.5 8.8 %collective-permute-start.13 = (f32[6,18,18,128]{3,2,1,0:T(8,128)}, f32[6,18,18,128]{3,2,1,0:T(8,128)}, u32[]{:S(2)}, u32[]{:S(2)}) collective-permute-start(f32[6,18,18,128]{3,2,1,0:T(8,128)} %pad_maximum_fusion.4), channel_id=1, source_target_pairs={{0,1},{1,0},{2,3},{3,2},{4,5},{5,4},{6,7},{7,6},{8,9},{9,8},{10,11... | collective-permute-start | bytes 2985992 | tf_op jit(solution)/shard_map/ppermute | solution.py:18
  67.4 1.1 %copy-start.1 = (f32[6,16,16,128]{3,2,1,0:T(8,128)S(1)}, f32[6,16,16,128]{3,2,1,0:T(8,128)}, u32[]{:S(2)}) copy-start(f32[6,16,16,128]{3,2,1,0:T(8,128)} %convert_element_type.37) | copy-start | bytes 2359300
  67.5 1.1 %copy-start.9 = (f32[3]{0:T(128)S(1)}, f32[3]{0:T(128)}, u32[]{:S(2)}) copy-start(f32[3]{0:T(128)} %copy-done.8) | copy-start | bytes 40
  67.5 1.1 %copy-start.11 = (f32[3]{0:T(128)S(1)}, f32[3]{0:T(128)}, u32[]{:S(2)}) copy-start(f32[3]{0:T(128)} %copy-done.10) | copy-start | bytes 40
  68.9 1.8 %copy-start.16 = (f32[6]{0:T(128)S(1)}, f32[6]{0:T(128)}, u32[]{:S(2)}) copy-start(f32[6]{0:T(128)} %get-tuple-element.58) | copy-start | bytes 76
  68.9 15.0 %copy-start.13 = (f32[6]{0:T(128)S(1)}, f32[6]{0:T(128)}, u32[]{:S(2)}) copy-start(f32[6]{0:T(128)} %copy-done.12) | copy-start | bytes 76
  68.9 15.0 %copy-start.15 = (f32[12]{0:T(128)S(1)}, f32[12]{0:T(128)}, u32[]{:S(2)}) copy-start(f32[12]{0:T(128)} %copy-done.14) | copy-start | bytes 148
  70.8 1.9 %collective-permute-start.14 = (f32[902]{0:T(1024)S(1)}, f32[902]{0:T(1024)S(1)}, u32[]{:S(2)}, u32[]{:S(2)}) collective-permute-start(f32[902]{0:T(1024)S(1)} %pad_maximum_fusion.16), channel_id=1, source_target_pairs={{0,1},{1,0},{2,3},{3,2},{4,5},{5,4},{6,7},{7,6},{8,9},{9,8},{10,11... | collective-permute-start | bytes 10832 | tf_op jit(solution)/shard_map/ppermute | solution.py:145
  71.3 3.6 %collective-permute-start.15 = (f32[902]{0:T(1024)S(1)}, f32[902]{0:T(1024)S(1)}, u32[]{:S(2)}, u32[]{:S(2)}) collective-permute-start(f32[902]{0:T(1024)S(1)} %pad_maximum_fusion.16), channel_id=1, source_target_pairs={{0,2},{1,3},{2,0},{3,1},{4,6},{5,7},{6,4},{7,5},{8,10},{9,11},{10,... | collective-permute-start | bytes 10832 | tf_op jit(solution)/shard_map/ppermute | solution.py:145
  72.0 3.1 %collective-permute-start.16 = (f32[902]{0:T(1024)S(1)}, f32[902]{0:T(1024)S(1)}, u32[]{:S(2)}, u32[]{:S(2)}) collective-permute-start(f32[902]{0:T(1024)S(1)} %pad_maximum_fusion.16), channel_id=1, source_target_pairs={{0,3},{1,2},{2,1},{3,0},{4,7},{5,6},{6,5},{7,4},{8,11},{9,10},{10,... | collective-permute-start | bytes 10832 | tf_op jit(solution)/shard_map/ppermute | solution.py:145
  75.0 4.8 %collective-permute-start.17 = (f32[902]{0:T(1024)S(1)}, f32[902]{0:T(1024)S(1)}, u32[]{:S(2)}, u32[]{:S(2)}) collective-permute-start(f32[902]{0:T(1024)S(1)} %add_add_fusion.3), channel_id=1, source_target_pairs={{0,4},{1,5},{2,6},{3,7},{4,0},{5,1},{6,2},{7,3},{8,12},{9,13},{10,... | collective-permute-start | bytes 10832 | tf_op jit(solution)/shard_map/ppermute | solution.py:145
  77.4 4.5 %collective-permute-start.18 = (f32[902]{0:T(1024)S(1)}, f32[902]{0:T(1024)S(1)}, u32[]{:S(2)}, u32[]{:S(2)}) collective-permute-start(f32[902]{0:T(1024)S(1)} %add_add_fusion.3), channel_id=1, source_target_pairs={{0,8},{1,9},{2,10},{3,11},{4,12},{5,13},{6,14},{7,15},{8,0},{9,1},... | collective-permute-start | bytes 10832 | tf_op jit(solution)/shard_map/ppermute | solution.py:145
  78.4 5.4 %collective-permute-start.19 = (f32[902]{0:T(1024)S(1)}, f32[902]{0:T(1024)S(1)}, u32[]{:S(2)}, u32[]{:S(2)}) collective-permute-start(f32[902]{0:T(1024)S(1)} %add_add_fusion.3), channel_id=1, source_target_pairs={{0,12},{1,13},{2,14},{3,15},{4,8},{5,9},{6,10},{7,11},{8,4},{9,5},... | collective-permute-start | bytes 10832 | tf_op jit(solution)/shard_map/ppermute | solution.py:145

commit v14 on v12

--- a/solution.py
+++ b/solution.py
@@ -238,7 +238,37 @@
     field = sweep(padded, lame_first, shear, density_cells, mask, tied_source, omega_sq, impedance)
     second_local = jnp.sum(mask * field, axis=(1, 2, 3))
     field = add_mean(field, gain_both_real, gain_both_imag, mean_field)
-    padded = with_halo(field, (("gx", 1), ("gy", 2), ("col", 3)), 1)
+
+    def plane(start):
+        cut = slice(start, start + 1)
+        part = sweep(
+            padded[:, start : start + 3],
+            lame_first[cut],
+            shear[cut],
+            density_cells[cut],
+            mask[cut],
+            tied_source[:, cut],
+            omega_sq,
+            impedance,
+        )
+        return add_mean(part, gain_both_real[:, cut], gain_both_imag[:, cut], mean_field)
+
+    low_plane = plane(0)
+    high_plane = plane(tile_shape[0] - 1)
+    peers = lax.axis_size("gx")
+    if peers == 2:
+        first_x = lax.axis_index("gx") == 0
+        got = lax.ppermute(jnp.where(first_x, high_plane, low_plane), "gx", [(0, 1), (1, 0)])
+        zero = jnp.zeros_like(got)
+        before = jnp.where(first_x, zero, got)
+        after = jnp.where(first_x, got, zero)
+    else:
+        up = [(i, (i + 1) % peers) for i in range(peers - 1)]
+        down = [(j, i) for i, j in up]
+        before = lax.ppermute(high_plane, "gx", up)
+        after = lax.ppermute(low_plane, "gx", down)
+    padded = jnp.concatenate([before, field, after], axis=1)
+    padded = with_halo(padded, (("gy", 2), ("col", 3)), 1)
     field = sweep(padded, *sweep_args)
     correlation = (
         field[:3] * forward_real

time: 87.4 us -> 90.5 us (1.035)
  starting transfers between devices: 29.3 us -> 25.7 us
  other arithmetic: 30.4 us -> 33.4 us
  waiting for transfers between devices: 16.1 us -> 18.3 us
  local copies, waits for them, and re-layouts: 9.03 us -> 10.3 us
    ppermute x2 -> x1, starting transfers between devices: 10.3 us -> 3.72 us  [with_halo(): before = lax.ppermute(last, axis, up)]
    ppermute x0 -> x2, starting transfers between devices: none -> 4.3 us  [the longest x1 2.82 us: shards(): before = lax.ppermute(high_plane, 'gx', up)]
    ppermute x2 -> x1, waiting for transfers between devices: 0.01 us -> 4.15 us  [with_halo(): after = lax.ppermute(initial, axis, down)]
    ppermute x12, waiting for transfers between devices: 11 us -> 7.17 us  [group_rounds(): lax.ppermute(value, axes, [(i, i ^ m * stride) for i in range(size)])]
    ppermute x0 -> x2, waiting for transfers between devices: none -> 2.91 us  [the longest x1 2.91 us: shards(): after = lax.ppermute(low_plane, 'gx', down)]
    add x12, other arithmetic: 5.61 us -> 3.89 us  [navier(): result.append(shear * laplace[channel] + (lame_first + shear) * divergence)]
    ppermute x2 -> x1, waiting for transfers between devices: 1.54 us -> 0.03 us  [with_halo(): before = lax.ppermute(last, axis, up)]
    unnamed x35 -> x45, local copies, waits for them, and re-layouts: 1.43 us -> 2.91 us
  transfers between devices with their start and end apart: 20 -> 20, of which waited for: 9 -> 11; matrix products, arithmetic and copies ran while one was open for 18% -> 12% of each run, Pallas kernels for 0% -> 0%
where the time goes in v14:
time: 90.5 us; the launch traced here: 89.8 us
  other arithmetic  33.4 us (37%)
  starting transfers between devices  25.7 us (28%)
  waiting for transfers between devices  18.3 us (20%)
  local copies, waits for them, and re-layouts  10.3 us (11%)
  between operations  2.04 us (2%)
    ppermute x12, starting transfers between devices, group_rounds(): lax.ppermute(value, axes, [(i, i ^ m * stride) for i in range(size)])  14.2 us
    ppermute x12, waiting for transfers between devices, group_rounds(): lax.ppermute(value, axes, [(i, i ^ m * stride) for i in range(size)])  7.17 us
    concatenate x5, other arithmetic, with_halo(): array = jnp.concatenate([before, array, after], axis=dim)  5.98 us
    ppermute x1, waiting for transfers between devices, with_halo(): after = lax.ppermute(initial, axis, down)  4.15 us
    add x12, other arithmetic, navier(): result.append(shear * laplace[channel] + (lame_first + shear) * divergence)  3.89 us
    ppermute x1, starting transfers between devices, with_halo(): before = lax.ppermute(last, axis, up)  3.72 us
    ppermute x2, waiting for transfers between devices, with_halo(): got = lax.ppermute(jnp.where(first, last, initial), axis, [(0, 1), (1, 0)])  3.62 us
    ppermute x1, waiting for transfers between devices, shards(): after = lax.ppermute(low_plane, 'gx', down)  2.91 us
  transfers between devices with their start and end apart: 20, of which 11 were waited for; matrix products, arithmetic and copies ran while one was open for 12% of the time, Pallas kernels for 0%

profile of v14, /device:TPU:0, one launch (start us, length us, event | category | flops | bytes accessed | tf_op | source)
XLA Modules:
  0.0 89.8 jit_solution(10640600363715487253)
XLA Ops:
  1.4 0.7 compare_select_fusion
  2.0 0.8 slice_bitcast_fusion.16
  2.8 0.8 slice_bitcast_fusion.15
  3.6 1.5 %scatter_custom_fusion = f32[32768]{0:T(1024)S(1)} fusion(s32[256]{0:T(256)S(1)} %bitcast.285, f32[256]{0:T(256)S(1)} %broadcast.700, f32[]{:T(128)} %constant.28.clone.1), kind=kCustom, calls=%fused_computation.254 | custom fusion | bytes 131076 | tf_op jit(solution)/shard_map/scatter | solution.py:187
  5.1 1.2 %multiply_reduce_fusion.1 = f32[6]{0:T(128)S(1)} fusion(bf16[6,16,16,128]{3,2,1,0:T(8,128)(2,1)} %param.10, f32[16,16,128]{2,1,0:T(8,128)S(1)} %bitcast.261), kind=kLoop, calls=%fused_computation.54 | loop fusion | flops 589818 | bytes 524312 | tf_op jit(solution)/shard_map/reduce_sum | solution.py:223
  6.2 1.1 %convert_element_type.15 = f32[6,16,16,128]{3,2,1,0:T(8,128)S(1)} convert(bf16[6,16,16,128]{3,2,1,0:T(8,128)(2,1)} %param.11) | non-fusion elementwise | flops 196608 | bytes 1179648 | tf_op jit(solution)/shard_map/convert_element_type | solution.py:211
  7.8 0.7 broadcast_multiply_fusion.1
  8.5 1.4 %multiply_subtract_fusion = (f32[3,16,16,128]{3,2,1,0:T(8,128)}, f32[3,16,16,128]{3,2,1,0:T(8,128)}, f32[3,16,16,128]{3,2,1,0:T(8,128)}, f32[3,16,16,128]{3,2,1,0:T(8,128)S(1)}, f32[3,16,16,128]{3,2,1,0:T(8,128)S(1)}) fusion(f32[6,16,16,128]{3,2,1,0:T(8,128)S(1)} %convert_element_type.15, f32[3]{0:T(128)S(1)} %get-tuple-element.101, ...), kind=kLoop, calls=%fused_computation.72 | loop fusion | flops 2359296 | bytes 3276824 | tf_op jit(solution)/shard_map/sub | solution.py:216
  10.1 0.7 pad_maximum_fusion.17
  10.8 2.4 %collective-permute-start.2 = (f32[12]{0:T(128)}, f32[12]{0:T(128)}, u32[]{:S(2)}, u32[]{:S(2)}) collective-permute-start(f32[12]{0:T(128)} %pad_maximum_fusion.17), channel_id=1, source_target_pairs={{0,3},{1,2},{2,1},{3,0},{4,7},{5,6},{6,5},{7,4},{8,11},{9,10},{10,... | collective-permute-start | bytes 152 | tf_op jit(solution)/shard_map/ppermute | solution.py:145
  13.9 0.6 fusion.239
  14.5 3.7 %collective-permute-start.7 = (f32[6,1,16,128]{3,2,1,0:T(8,128)}, f32[6,1,16,128]{3,2,1,0:T(8,128)S(1)}, u32[]{:S(2)}, u32[]{:S(2)}) collective-permute-start(f32[6,1,16,128]{3,2,1,0:T(8,128)} %get-tuple-element.77), channel_id=1, source_target_pairs={{0,4},{4,8},{8,12},{1,5},{5,9},{9,13},{2,6},{6,10},{10,14},{3,7},{... | collective-permute-start | bytes 147464 | tf_op jit(solution)/shard_map/ppermute | solution.py:33
  18.2 1.3 %collective-permute-start.6 = (f32[6,1,16,128]{3,2,1,0:T(8,128)}, f32[6,1,16,128]{3,2,1,0:T(8,128)S(1)}, u32[]{:S(2)}, u32[]{:S(2)}) collective-permute-start(f32[6,1,16,128]{3,2,1,0:T(8,128)} %get-tuple-element.78), channel_id=1, source_target_pairs={{4,0},{8,4},{12,8},{5,1},{9,5},{13,9},{6,2},{10,6},{14,10},{7,3},{... | collective-permute-start | bytes 147464 | tf_op jit(solution)/shard_map/ppermute | solution.py:34
  20.3 4.1 %collective-permute-done.6 = f32[6,1,16,128]{3,2,1,0:T(8,128)S(1)} collective-permute-done((f32[6,1,16,128]{3,2,1,0:T(8,128)}, f32[6,1,16,128]{3,2,1,0:T(8,128)S(1)}, u32[]{:S(2)}, u32[]{:S(2)}) %collective-permute-start.6) | collective-permute-done | bytes 49184 | tf_op jit(solution)/shard_map/ppermute | solution.py:34
  24.5 1.6 %collective-permute-start.8 = (f32[6,18,1,128]{3,2,1,0:T(1,128)S(1)}, f32[6,18,1,128]{3,2,1,0:T(1,128)S(1)}, u32[]{:S(2)}, u32[]{:S(2)}) collective-permute-start(f32[6,18,1,128]{3,2,1,0:T(1,128)S(1)} %broadcast_select_fusion.5), channel_id=1, source_target_pairs={{0,2},{2,0},{1,3},{3,1},{4,6},{6,4},{5,7},{7,5},{8,10},{10,8},{9,1... | collective-permute-start | bytes 165896 | tf_op jit(solution)/shard_map/ppermute | solution.py:26
  26.1 0.7 add_add_fusion.8
  26.8 1.8 %collective-permute-start.5 = (f32[12]{0:T(128)S(1)}, f32[12]{0:T(128)S(1)}, u32[]{:S(2)}, u32[]{:S(2)}) collective-permute-start(f32[12]{0:T(128)S(1)} %add_add_fusion.8), channel_id=1, source_target_pairs={{0,12},{1,13},{2,14},{3,15},{4,8},{5,9},{6,10},{7,11},{8,4},{9,5},... | collective-permute-start | bytes 152 | tf_op jit(solution)/shard_map/ppermute | solution.py:145
  28.6 1.2 %collective-permute-start.4 = (f32[12]{0:T(128)S(1)}, f32[12]{0:T(128)S(1)}, u32[]{:S(2)}, u32[]{:S(2)}) collective-permute-start(f32[12]{0:T(128)S(1)} %add_add_fusion.8), channel_id=1, source_target_pairs={{0,8},{1,9},{2,10},{3,11},{4,12},{5,13},{6,14},{7,15},{8,0},{9,1},... | collective-permute-start | bytes 152 | tf_op jit(solution)/shard_map/ppermute | solution.py:145
  29.8 1.3 %collective-permute-start.3 = (f32[12]{0:T(128)S(1)}, f32[12]{0:T(128)S(1)}, u32[]{:S(2)}, u32[]{:S(2)}) collective-permute-start(f32[12]{0:T(128)S(1)} %add_add_fusion.8), channel_id=1, source_target_pairs={{0,4},{1,5},{2,6},{3,7},{4,0},{5,1},{6,2},{7,3},{8,12},{9,13},{10,... | collective-permute-start | bytes 152 | tf_op jit(solution)/shard_map/ppermute | solution.py:145
  32.1 0.9 %collective-permute-done.4 = f32[12]{0:T(128)S(1)} collective-permute-done((f32[12]{0:T(128)S(1)}, f32[12]{0:T(128)S(1)}, u32[]{:S(2)}, u32[]{:S(2)}) %collective-permute-start.4) | collective-permute-done | bytes 80 | tf_op jit(solution)/shard_map/ppermute | solution.py:145
  35.1 2.1 %pad_maximum_fusion = (f32[6,18,18,129]{3,2,1,0:T(8,128)S(1)}, f32[6,18,18,129]{3,2,1,0:T(8,128)S(1)}) fusion(f32[6,18,18,1]{3,2,1,0:T(8,128)S(1)} %get-tuple-element.59, f32[6,18,1,128]{3,2,1,0:T(1,128)S(1)} %get-tuple-element.91, f32[6,1,16,128]{3,2,1,0:T(8,128)S(1)} %collective-permute-done.6, f32[6,16,16,128]{3,2,1,0:T(8,128)S(1)} %convert_element_type.12, ...), kind=kLoop, calls=%fused_computation.1 | loop fusion | flops 2507760 | bytes 3017088 | tf_op jit(solution)/shard_map/concatenate | solution.py:35
  42.3 2.8 %collective-permute-start.11 = (f32[6,1,16,128]{3,2,1,0:T(8,128)S(1)}, f32[6,1,16,128]{3,2,1,0:T(8,128)S(1)}, u32[]{:S(2)}, u32[]{:S(2)}) collective-permute-start(f32[6,1,16,128]{3,2,1,0:T(8,128)S(1)} %get-tuple-element.69), channel_id=1, source_target_pairs={{0,4},{4,8},{8,12},{1,5},{5,9},{9,13},{2,6},{6,10},{10,14},{3,7},{... | collective-permute-start | bytes 147464 | tf_op jit(solution)/shard_map/ppermute | solution.py:268
  45.1 1.5 %collective-permute-start.10 = (f32[6,1,16,128]{3,2,1,0:T(8,128)S(1)}, f32[6,1,16,128]{3,2,1,0:T(8,128)S(1)}, u32[]{:S(2)}, u32[]{:S(2)}) collective-permute-start(f32[6,1,16,128]{3,2,1,0:T(8,128)S(1)} %get-tuple-element.70), channel_id=1, source_target_pairs={{4,0},{8,4},{12,8},{5,1},{9,5},{13,9},{6,2},{10,6},{14,10},{7,3},{... | collective-permute-start | bytes 147464 | tf_op jit(solution)/shard_map/ppermute | solution.py:269
  47.4 0.8 multiply_reduce_fusion
  48.2 2.9 %collective-permute-done.10 = f32[6,1,16,128]{3,2,1,0:T(8,128)S(1)} collective-permute-done((f32[6,1,16,128]{3,2,1,0:T(8,128)S(1)}, f32[6,1,16,128]{3,2,1,0:T(8,128)S(1)}, u32[]{:S(2)}, u32[]{:S(2)}) %collective-permute-start.10) | collective-permute-done | bytes 49184 | tf_op jit(solution)/shard_map/ppermute | solution.py:269
  51.8 3.6 %collective-permute-done.12 = f32[6,18,1,128]{3,2,1,0:T(1,128)S(1)} collective-permute-done((f32[6,18,1,128]{3,2,1,0:T(1,128)S(1)}, f32[6,18,1,128]{3,2,1,0:T(1,128)S(1)}, u32[]{:S(2)}, u32[]{:S(2)}) %collective-permute-start.12) | collective-permute-done | bytes 55328 | tf_op jit(solution)/shard_map/ppermute | solution.py:26
  55.5 1.3 %pad_maximum_fusion.4 = f32[6,18,18,128]{3,2,1,0:T(8,128)} fusion(f32[6,18,1,128]{3,2,1,0:T(1,128)S(1)} %get-tuple-element.89, f32[6,1,16,128]{3,2,1,0:T(8,128)S(1)} %collective-permute-done.10, f32[6,16,16,128]{3,2,1,0:T(8,128)S(1)} %get-tuple-element.74, f32[6,1,16,128]{3,2,1,0:T(8,128)S(1)} %collective-permute-done.11, ...), kind=kLoop, calls=%fused_computation.14 | loop fusion | flops 995328 | bytes 1990656 | tf_op jit(solution)/shard_map/concatenate | solution.py:35
  56.8 1.0 %convert_element_type.13 = f32[6,16,16,128]{3,2,1,0:T(8,128)} convert(bf16[6,16,16,128]{3,2,1,0:T(8,128)(2,1)S(1)} %copy-done.5) | non-fusion elementwise | flops 196608 | bytes 1179648 | tf_op jit(solution)/shard_map/convert_element_type | solution.py:192
  57.7 1.2 %multiply_add_fusion = f32[3,16,16,128]{3,2,1,0:T(8,128)S(1)} fusion(f32[3,16,16,128]{3,2,1,0:T(8,128)} %get-tuple-element.25, f32[3,16,16,128]{3,2,1,0:T(8,128)} %get-tuple-element.24), kind=kLoop, calls=%fused_computation.71 | loop fusion | flops 196608 | bytes 1179648 | tf_op jit(solution)/shard_map/add | solution.py:217
  59.0 0.9 maximum_reduce_fusion
  59.9 0.9 %reduce_sum.115 = f32[6,4,4,4,4]{4,3,2,1,0:T(4,128)S(1)} reshape(f32[6,16,16]{2,1,0:T(8,128)} %maximum_reduce_fusion) | data formatting | bytes 12288 | tf_op jit(solution)/shard_map/reduce_sum | solution.py:207
  60.8 0.7 reduce_sum.116
  61.5 1.7 %dynamic_update_slice.7 = f32[6,16,8]{2,1,0:T(8,128)S(1)} dynamic-update-slice(f32[6,16,8]{2,1,0:T(8,128)S(1)} %broadcast_in_dim.205, f32[6,4,4]{2,1,0:T(4,128)} %reduce_sum.116, s32[]{:T(128)} %constant.29.clone.1, s32[]{:T(128)S(6)} %select_n.188, s32[]{:T(128)S(6)} %select_n.189) | dynamic-update-slice | bytes 772 | tf_op jit(solution)/shard_map/dynamic_update_slice | solution.py:209
  63.5 2.2 %slice_select_fusion.1 = (f32[6,18,18,1]{3,2,1,0:T(8,128)S(1)}, f32[6,18,18,1]{3,2,1,0:T(8,128)S(1)}) fusion(f32[6,18,18,128]{3,2,1,0:T(8,128)} %collective-permute-done.13, pred[]{:T(512)S(6)} %eq.67), kind=kLoop, calls=%fused_computation.6 | loop fusion | flops 3888 | bytes 31105 | tf_op jit(solution)/shard_map/jit(_where)/select_n | solution.py:23
  65.7 2.1 %pad_maximum_fusion.1 = (f32[6,18,18,129]{3,2,1,0:T(8,128)S(1)}, f32[6,18,18,129]{3,2,1,0:T(8,128)S(1)}) fusion(f32[6,18,18,1]{3,2,1,0:T(8,128)S(1)} %get-tuple-element.57, f32[6,18,1,128]{3,2,1,0:T(1,128)S(1)} %get-tuple-element.89, f32[6,1,16,128]{3,2,1,0:T(8,128)S(1)} %collective-permute-done.10, f32[6,16,16,128]{3,2,1,0:T(8,128)S(1)} %get-tuple-element.74, ...), kind=kLoop, calls=%fused_computation.3 | loop fusion | flops 2507760 | bytes 3017088 | tf_op jit(solution)/shard_map/concatenate | solution.py:35
  69.9 0.7 fusion.46
  70.6 0.7 fusion.28
  72.0 1.2 %subtract_reduce_fusion = (f32[16,16,128]{2,1,0:T(8,128)S(1)}, f32[3,16,16,128]{3,2,1,0:T(8,128)S(1)}, f32[3,16,16,128]{3,2,1,0:T(8,128)}) fusion(f32[6,16,16,128]{3,2,1,0:T(8,128)S(1)} %convert_element_type.15, f32[3,16,16,128]{3,2,1,0:T(8,128)S(1)} %get-tuple-element.56, f32[3]{0:T(128)S(1)} %copy-done.13, f32[16,16,128]{2,1,0:T(8,128)S(1)} %get-tuple-element.87, ...), kind=kLoop, calls=%fused_computation.75 | loop fusion | flops 2719744 | bytes 3670040 | tf_op jit(solution)/shard_map/reduce_sum | solution.py:278
  74.1 2.1 %collective-permute-start.16 = (f32[902]{0:T(1024)S(1)}, f32[902]{0:T(1024)S(1)}, u32[]{:S(2)}, u32[]{:S(2)}) collective-permute-start(f32[902]{0:T(1024)S(1)} %pad_maximum_fusion.16), channel_id=1, source_target_pairs={{0,3},{1,2},{2,1},{3,0},{4,7},{5,6},{6,5},{7,4},{8,11},{9,10},{10,... | collective-permute-start | bytes 10832 | tf_op jit(solution)/shard_map/ppermute | solution.py:145
  76.4 1.1 %collective-permute-done.16 = f32[902]{0:T(1024)S(1)} collective-permute-done((f32[902]{0:T(1024)S(1)}, f32[902]{0:T(1024)S(1)}, u32[]{:S(2)}, u32[]{:S(2)}) %collective-permute-start.16) | collective-permute-done | bytes 3640 | tf_op jit(solution)/shard_map/ppermute | solution.py:145
  77.5 2.3 %collective-permute-done.15 = f32[902]{0:T(1024)S(1)} collective-permute-done((f32[902]{0:T(1024)S(1)}, f32[902]{0:T(1024)S(1)}, u32[]{:S(2)}, u32[]{:S(2)}) %collective-permute-start.15) | collective-permute-done | bytes 3640 | tf_op jit(solution)/shard_map/ppermute | solution.py:145
  79.8 0.9 collective-permute-start.19
  80.6 2.0 %collective-permute-start.18 = (f32[902]{0:T(1024)S(1)}, f32[902]{0:T(1024)S(1)}, u32[]{:S(2)}, u32[]{:S(2)}) collective-permute-start(f32[902]{0:T(1024)S(1)} %add_add_fusion.5), channel_id=1, source_target_pairs={{0,8},{1,9},{2,10},{3,11},{4,12},{5,13},{6,14},{7,15},{8,0},{9,1},... | collective-permute-start | bytes 10832 | tf_op jit(solution)/shard_map/ppermute | solution.py:145
  82.6 1.6 %collective-permute-start.17 = (f32[902]{0:T(1024)S(1)}, f32[902]{0:T(1024)S(1)}, u32[]{:S(2)}, u32[]{:S(2)}) collective-permute-start(f32[902]{0:T(1024)S(1)} %add_add_fusion.5), channel_id=1, source_target_pairs={{0,4},{1,5},{2,6},{3,7},{4,0},{5,1},{6,2},{7,3},{8,12},{9,13},{10,... | collective-permute-start | bytes 10832 | tf_op jit(solution)/shard_map/ppermute | solution.py:145
  84.2 1.0 %collective-permute-done.19 = f32[902]{0:T(1024)S(1)} collective-permute-done((f32[902]{0:T(1024)S(1)}, f32[902]{0:T(1024)S(1)}, u32[]{:S(2)}, u32[]{:S(2)}) %collective-permute-start.19) | collective-permute-done | bytes 3640 | tf_op jit(solution)/shard_map/ppermute | solution.py:145
  85.2 1.0 %collective-permute-done.17 = f32[902]{0:T(1024)S(1)} collective-permute-done((f32[902]{0:T(1024)S(1)}, f32[902]{0:T(1024)S(1)}, u32[]{:S(2)}, u32[]{:S(2)}) %collective-permute-start.17) | collective-permute-done | bytes 3640 | tf_op jit(solution)/shard_map/ppermute | solution.py:145
  87.1 0.7 copy.14
  87.7 2.0 %fusion.7 = f32[6,16,16,128]{3,2,1,0:T(8,128)} fusion(f32[3,16,16,128]{3,2,1,0:T(8,128)S(1)} %get-tuple-element.27, f32[3,16,16,128]{3,2,1,0:T(8,128)S(1)} %get-tuple-element.26, f32[3,16,16,128]{3,2,1,0:T(8,128)} %get-tuple-element.22, f32[3,16,16,128]{3,2,1,0:T(8,128)S(1)} %get-tuple-element.21, f32[6]{0:T(128)S(1)} %pad_maximum_fusion.19, ...), kind=kLoop, calls=%fused_computation.32 | loop fusion | flops 1376256 | bytes 2359344 | tf_op jit(solution)/shard_map/add | solution.py:131
  (146 shorter events, 16.6 us)
Async XLA Ops:
  0.6 6.7 %copy-start.21 = (s32[2,2,4]{2,1,0:T(2,128)S(1)}, s32[2,2,4]{2,1,0:T(2,128)}, u32[]{:S(2)}) copy-start(s32[2,2,4]{2,1,0:T(2,128)} %param.13) | copy-start | bytes 196
  0.6 7.1 %copy-start.7 = (bf16[16,16,128]{2,1,0:T(8,128)(2,1)S(1)}, bf16[16,16,128]{2,1,0:T(8,128)(2,1)}, u32[]{:S(2)}) copy-start(bf16[16,16,128]{2,1,0:T(8,128)(2,1)} %param.12) | copy-start | bytes 196612
  3.6 5.0 %copy-start.8 = (f32[3]{0:T(128)}, f32[3]{0:T(128)S(1)}, u32[]{:S(2)}) copy-start(f32[3]{0:T(128)S(1)} %get-tuple-element.100) | copy-start | bytes 40
  3.6 5.0 %copy-start.11 = (f32[3]{0:T(128)}, f32[3]{0:T(128)S(1)}, u32[]{:S(2)}) copy-start(f32[3]{0:T(128)S(1)} %get-tuple-element.101) | copy-start | bytes 40
  7.8 11.8 %copy-start.2 = (f32[2,8,2,8,128]{4,3,2,1,0:T(8,128)}, f32[2,8,2,8,128]{4,3,2,1,0:T(8,128)S(1)}, u32[]{:S(2)}) copy-start(f32[2,8,2,8,128]{4,3,2,1,0:T(8,128)S(1)} %broadcast_in_dim.203) | copy-start | bytes 393220
  8.5 5.4 %copy-start = (bf16[6,16,16,128]{3,2,1,0:T(8,128)(2,1)S(1)}, bf16[6,16,16,128]{3,2,1,0:T(8,128)(2,1)}, u32[]{:S(2)}) copy-start(bf16[6,16,16,128]{3,2,1,0:T(8,128)(2,1)} %param.10) | copy-start | bytes 1179652
  10.8 15.3 %collective-permute-start.2 = (f32[12]{0:T(128)}, f32[12]{0:T(128)}, u32[]{:S(2)}, u32[]{:S(2)}) collective-permute-start(f32[12]{0:T(128)} %pad_maximum_fusion.17), channel_id=1, source_target_pairs={{0,3},{1,2},{2,1},{3,0},{4,7},{5,6},{6,5},{7,4},{8,11},{9,10},{10,... | collective-permute-start | bytes 152 | tf_op jit(solution)/shard_map/ppermute | solution.py:145
  13.2 12.9 %collective-permute-start.1 = (f32[12]{0:T(128)}, f32[12]{0:T(128)}, u32[]{:S(2)}, u32[]{:S(2)}) collective-permute-start(f32[12]{0:T(128)} %pad_maximum_fusion.17), channel_id=1, source_target_pairs={{0,2},{1,3},{2,0},{3,1},{4,6},{5,7},{6,4},{7,5},{8,10},{9,11},{10,... | collective-permute-start | bytes 152 | tf_op jit(solution)/shard_map/ppermute | solution.py:145
  13.8 12.3 %collective-permute-start = (f32[12]{0:T(128)}, f32[12]{0:T(128)}, u32[]{:S(2)}, u32[]{:S(2)}) collective-permute-start(f32[12]{0:T(128)} %pad_maximum_fusion.17), channel_id=1, source_target_pairs={{0,1},{1,0},{2,3},{3,2},{4,5},{5,4},{6,7},{7,6},{8,9},{9,8},{10,11... | collective-permute-start | bytes 152 | tf_op jit(solution)/shard_map/ppermute | solution.py:145
  14.5 5.8 %collective-permute-start.7 = (f32[6,1,16,128]{3,2,1,0:T(8,128)}, f32[6,1,16,128]{3,2,1,0:T(8,128)S(1)}, u32[]{:S(2)}, u32[]{:S(2)}) collective-permute-start(f32[6,1,16,128]{3,2,1,0:T(8,128)} %get-tuple-element.77), channel_id=1, source_target_pairs={{0,4},{4,8},{8,12},{1,5},{5,9},{9,13},{2,6},{6,10},{10,14},{3,7},{... | collective-permute-start | bytes 147464 | tf_op jit(solution)/shard_map/ppermute | solution.py:33
  18.2 6.2 %collective-permute-start.6 = (f32[6,1,16,128]{3,2,1,0:T(8,128)}, f32[6,1,16,128]{3,2,1,0:T(8,128)S(1)}, u32[]{:S(2)}, u32[]{:S(2)}) collective-permute-start(f32[6,1,16,128]{3,2,1,0:T(8,128)} %get-tuple-element.78), channel_id=1, source_target_pairs={{4,0},{8,4},{12,8},{5,1},{9,5},{13,9},{6,2},{10,6},{14,10},{7,3},{... | collective-permute-start | bytes 147464 | tf_op jit(solution)/shard_map/ppermute | solution.py:34
  24.5 9.4 %copy-start.5 = (bf16[6,16,16,128]{3,2,1,0:T(8,128)(2,1)S(1)}, bf16[6,16,16,128]{3,2,1,0:T(8,128)(2,1)}, u32[]{:S(2)}) copy-start(bf16[6,16,16,128]{3,2,1,0:T(8,128)(2,1)} %param.9) | copy-start | bytes 1179652
  24.5 6.7 %collective-permute-start.8 = (f32[6,18,1,128]{3,2,1,0:T(1,128)S(1)}, f32[6,18,1,128]{3,2,1,0:T(1,128)S(1)}, u32[]{:S(2)}, u32[]{:S(2)}) collective-permute-start(f32[6,18,1,128]{3,2,1,0:T(1,128)S(1)} %broadcast_select_fusion.5), channel_id=1, source_target_pairs={{0,2},{2,0},{1,3},{3,1},{4,6},{6,4},{5,7},{7,5},{8,10},{10,8},{9,1... | collective-permute-start | bytes 165896 | tf_op jit(solution)/shard_map/ppermute | solution.py:26
  26.8 5.3 %collective-permute-start.5 = (f32[12]{0:T(128)S(1)}, f32[12]{0:T(128)S(1)}, u32[]{:S(2)}, u32[]{:S(2)}) collective-permute-start(f32[12]{0:T(128)S(1)} %add_add_fusion.8), channel_id=1, source_target_pairs={{0,12},{1,13},{2,14},{3,15},{4,8},{5,9},{6,10},{7,11},{8,4},{9,5},... | collective-permute-start | bytes 152 | tf_op jit(solution)/shard_map/ppermute | solution.py:145
  28.6 4.4 %collective-permute-start.4 = (f32[12]{0:T(128)S(1)}, f32[12]{0:T(128)S(1)}, u32[]{:S(2)}, u32[]{:S(2)}) collective-permute-start(f32[12]{0:T(128)S(1)} %add_add_fusion.8), channel_id=1, source_target_pairs={{0,8},{1,9},{2,10},{3,11},{4,12},{5,13},{6,14},{7,15},{8,0},{9,1},... | collective-permute-start | bytes 152 | tf_op jit(solution)/shard_map/ppermute | solution.py:145
  29.8 3.5 %collective-permute-start.3 = (f32[12]{0:T(128)S(1)}, f32[12]{0:T(128)S(1)}, u32[]{:S(2)}, u32[]{:S(2)}) collective-permute-start(f32[12]{0:T(128)S(1)} %add_add_fusion.8), channel_id=1, source_target_pairs={{0,4},{1,5},{2,6},{3,7},{4,0},{5,1},{6,2},{7,3},{8,12},{9,13},{10,... | collective-permute-start | bytes 152 | tf_op jit(solution)/shard_map/ppermute | solution.py:145
  31.5 3.1 %collective-permute-start.9 = (f32[6,18,18,128]{3,2,1,0:T(8,128)S(1)}, f32[6,18,18,128]{3,2,1,0:T(8,128)S(1)}, u32[]{:S(2)}, u32[]{:S(2)}) collective-permute-start(f32[6,18,18,128]{3,2,1,0:T(8,128)S(1)} %maximum_add_fusion), channel_id=1, source_target_pairs={{0,1},{1,0},{2,3},{3,2},{4,5},{5,4},{6,7},{7,6},{8,9},{9,8},{10,11... | collective-permute-start | bytes 2985992 | tf_op jit(solution)/shard_map/ppermute | solution.py:18
  33.4 0.5 copy-start.18
  33.4 14.0 %copy-start.16 = (f32[6]{0:T(128)}, f32[6]{0:T(128)S(1)}, u32[]{:S(2)}) copy-start(f32[6]{0:T(128)S(1)} %slice_multiply_fusion.14) | copy-start | bytes 76
  37.2 0.9 %copy-start.3 = (f32[2,8,2,8,128]{4,3,2,1,0:T(8,128)S(1)}, f32[2,8,2,8,128]{4,3,2,1,0:T(8,128)}, u32[]{:S(2)}) copy-start(f32[2,8,2,8,128]{4,3,2,1,0:T(8,128)} %copy-done.2) | copy-start | bytes 393220
  39.9 0.7 copy-start.9
  39.9 0.7 copy-start.12
  39.9 0.7 copy-start.15
  41.3 0.7 copy-start.14
  41.4 5.2 %copy-start.6 = (f32[16,16,128]{2,1,0:T(8,128)S(1)}, f32[16,16,128]{2,1,0:T(8,128)}, u32[]{:S(2)}) copy-start(f32[16,16,128]{2,1,0:T(8,128)} %get-tuple-element.85) | copy-start | bytes 393220
  42.3 5.9 %collective-permute-start.11 = (f32[6,1,16,128]{3,2,1,0:T(8,128)S(1)}, f32[6,1,16,128]{3,2,1,0:T(8,128)S(1)}, u32[]{:S(2)}, u32[]{:S(2)}) collective-permute-start(f32[6,1,16,128]{3,2,1,0:T(8,128)S(1)} %get-tuple-element.69), channel_id=1, source_target_pairs={{0,4},{4,8},{8,12},{1,5},{5,9},{9,13},{2,6},{6,10},{10,14},{3,7},{... | collective-permute-start | bytes 147464 | tf_op jit(solution)/shard_map/ppermute | solution.py:268
  45.1 6.0 %collective-permute-start.10 = (f32[6,1,16,128]{3,2,1,0:T(8,128)S(1)}, f32[6,1,16,128]{3,2,1,0:T(8,128)S(1)}, u32[]{:S(2)}, u32[]{:S(2)}) collective-permute-start(f32[6,1,16,128]{3,2,1,0:T(8,128)S(1)} %get-tuple-element.70), channel_id=1, source_target_pairs={{4,0},{8,4},{12,8},{5,1},{9,5},{13,9},{6,2},{10,6},{14,10},{7,3},{... | collective-permute-start | bytes 147464 | tf_op jit(solution)/shard_map/ppermute | solution.py:269
  51.2 4.2 %collective-permute-start.12 = (f32[6,18,1,128]{3,2,1,0:T(1,128)S(1)}, f32[6,18,1,128]{3,2,1,0:T(1,128)S(1)}, u32[]{:S(2)}, u32[]{:S(2)}) collective-permute-start(f32[6,18,1,128]{3,2,1,0:T(1,128)S(1)} %broadcast_select_fusion.2), channel_id=1, source_target_pairs={{0,2},{2,0},{1,3},{3,1},{4,6},{6,4},{5,7},{7,5},{8,10},{10,8},{9,1... | collective-permute-start | bytes 165896 | tf_op jit(solution)/shard_map/ppermute | solution.py:26
  56.8 6.7 %collective-permute-start.13 = (f32[6,18,18,128]{3,2,1,0:T(8,128)}, f32[6,18,18,128]{3,2,1,0:T(8,128)}, u32[]{:S(2)}, u32[]{:S(2)}) collective-permute-start(f32[6,18,18,128]{3,2,1,0:T(8,128)} %pad_maximum_fusion.4), channel_id=1, source_target_pairs={{0,1},{1,0},{2,3},{3,2},{4,5},{5,4},{6,7},{7,6},{8,9},{9,8},{10,11... | collective-permute-start | bytes 2985992 | tf_op jit(solution)/shard_map/ppermute | solution.py:18
  57.7 1.2 %copy-start.4 = (f32[3,16,16,128]{3,2,1,0:T(8,128)S(1)}, f32[3,16,16,128]{3,2,1,0:T(8,128)}, u32[]{:S(2)}) copy-start(f32[3,16,16,128]{3,2,1,0:T(8,128)} %get-tuple-element.23) | copy-start | bytes 1179652
  70.6 1.1 %copy-start.1 = (f32[6,16,16,128]{3,2,1,0:T(8,128)S(1)}, f32[6,16,16,128]{3,2,1,0:T(8,128)}, u32[]{:S(2)}) copy-start(f32[6,16,16,128]{3,2,1,0:T(8,128)} %convert_element_type.13) | copy-start | bytes 2359300
  70.6 1.1 %copy-start.10 = (f32[3]{0:T(128)S(1)}, f32[3]{0:T(128)}, u32[]{:S(2)}) copy-start(f32[3]{0:T(128)} %copy-done.8) | copy-start | bytes 40
  70.6 1.1 %copy-start.13 = (f32[3]{0:T(128)S(1)}, f32[3]{0:T(128)}, u32[]{:S(2)}) copy-start(f32[3]{0:T(128)} %copy-done.11) | copy-start | bytes 40
  72.0 2.0 %copy-start.20 = (f32[6]{0:T(128)S(1)}, f32[6]{0:T(128)}, u32[]{:S(2)}) copy-start(f32[6]{0:T(128)} %get-tuple-element.73) | copy-start | bytes 76
  72.0 14.2 %copy-start.17 = (f32[6]{0:T(128)S(1)}, f32[6]{0:T(128)}, u32[]{:S(2)}) copy-start(f32[6]{0:T(128)} %copy-done.16) | copy-start | bytes 76
  72.0 14.2 %copy-start.19 = (f32[12]{0:T(128)S(1)}, f32[12]{0:T(128)}, u32[]{:S(2)}) copy-start(f32[12]{0:T(128)} %copy-done.18) | copy-start | bytes 148
  74.1 3.4 %collective-permute-start.16 = (f32[902]{0:T(1024)S(1)}, f32[902]{0:T(1024)S(1)}, u32[]{:S(2)}, u32[]{:S(2)}) collective-permute-start(f32[902]{0:T(1024)S(1)} %pad_maximum_fusion.16), channel_id=1, source_target_pairs={{0,3},{1,2},{2,1},{3,0},{4,7},{5,6},{6,5},{7,4},{8,11},{9,10},{10,... | collective-permute-start | bytes 10832 | tf_op jit(solution)/shard_map/ppermute | solution.py:145
  76.1 3.6 %collective-permute-start.15 = (f32[902]{0:T(1024)S(1)}, f32[902]{0:T(1024)S(1)}, u32[]{:S(2)}, u32[]{:S(2)}) collective-permute-start(f32[902]{0:T(1024)S(1)} %pad_maximum_fusion.16), channel_id=1, source_target_pairs={{0,2},{1,3},{2,0},{3,1},{4,6},{5,7},{6,4},{7,5},{8,10},{9,11},{10,... | collective-permute-start | bytes 10832 | tf_op jit(solution)/shard_map/ppermute | solution.py:145
  76.2 3.6 %collective-permute-start.14 = (f32[902]{0:T(1024)S(1)}, f32[902]{0:T(1024)S(1)}, u32[]{:S(2)}, u32[]{:S(2)}) collective-permute-start(f32[902]{0:T(1024)S(1)} %pad_maximum_fusion.16), channel_id=1, source_target_pairs={{0,1},{1,0},{2,3},{3,2},{4,5},{5,4},{6,7},{7,6},{8,9},{9,8},{10,11... | collective-permute-start | bytes 10832 | tf_op jit(solution)/shard_map/ppermute | solution.py:145
  79.8 5.5 %collective-permute-start.19 = (f32[902]{0:T(1024)S(1)}, f32[902]{0:T(1024)S(1)}, u32[]{:S(2)}, u32[]{:S(2)}) collective-permute-start(f32[902]{0:T(1024)S(1)} %add_add_fusion.5), channel_id=1, source_target_pairs={{0,12},{1,13},{2,14},{3,15},{4,8},{5,9},{6,10},{7,11},{8,4},{9,5},... | collective-permute-start | bytes 10832 | tf_op jit(solution)/shard_map/ppermute | solution.py:145
  80.6 4.6 %collective-permute-start.18 = (f32[902]{0:T(1024)S(1)}, f32[902]{0:T(1024)S(1)}, u32[]{:S(2)}, u32[]{:S(2)}) collective-permute-start(f32[902]{0:T(1024)S(1)} %add_add_fusion.5), channel_id=1, source_target_pairs={{0,8},{1,9},{2,10},{3,11},{4,12},{5,13},{6,14},{7,15},{8,0},{9,1},... | collective-permute-start | bytes 10832 | tf_op jit(solution)/shard_map/ppermute | solution.py:145
  82.6 3.6 %collective-permute-start.17 = (f32[902]{0:T(1024)S(1)}, f32[902]{0:T(1024)S(1)}, u32[]{:S(2)}, u32[]{:S(2)}) collective-permute-start(f32[902]{0:T(1024)S(1)} %add_add_fusion.5), channel_id=1, source_target_pairs={{0,4},{1,5},{2,6},{3,7},{4,0},{5,1},{6,2},{7,3},{8,12},{9,13},{10,... | collective-permute-start | bytes 10832 | tf_op jit(solution)/shard_map/ppermute | solution.py:145

commit v15 on v12

--- a/solution.py
+++ b/solution.py
@@ -198,13 +198,13 @@
     axes = ("gx", "gy", "col")
     coarse_x = tile_shape[0] // 4
     coarse_y = tile_shape[1] // 4
-    grid_shape = (lax.axis_size("gx") * coarse_x, lax.axis_size("gy") * coarse_y)
-    grid_at = (lax.axis_index("gx") * coarse_x, lax.axis_index("gy") * coarse_y)
+    grid_shape = (lax.axis_size("gy") * coarse_y, lax.axis_size("gx") * coarse_x)
+    grid_at = (lax.axis_index("gy") * coarse_y, lax.axis_index("gx") * coarse_x)
 
     def block_sums(cells):
         lead = cells.shape[:-3]
         local = cells.reshape(lead + (coarse_x, 4, coarse_y, 4, tile_shape[2]))
-        local = local.sum(axis=(-4, -2, -1))
+        local = jnp.swapaxes(local.sum(axis=(-4, -2, -1)), -1, -2)
         grid = jnp.zeros(lead + grid_shape, jnp.float32)
         return lax.dynamic_update_slice(grid, local, (0,) * len(lead) + grid_at)
 
@@ -262,7 +262,7 @@
     late_terms = jnp.sum(
         late_mean[:3, None, None] * response[:3] - late_mean[3:, None, None] * response[3:], axis=0
     )
-    coarse = (last[6 : 6 + grid_size].reshape(grid_shape) - omega_sq * late_terms) / 64.0
+    coarse = ((last[6 : 6 + grid_size].reshape(grid_shape) - omega_sq * late_terms) / 64.0).T
     return (field, coarse)
 
 

time: 87.4 us -> 87.2 us (level)
  local copies, waits for them, and re-layouts: 9.03 us -> 7.92 us
  starting transfers between devices: 29.3 us -> 30.4 us
    dynamic_update_slice x2, local copies, waits for them, and re-layouts: 2 us -> 0.67 us  [block_sums(): return lax.dynamic_update_slice(grid, local, (0,) * len(lead) + grid_at)]
    ppermute x12, starting transfers between devices: 13.8 us -> 15 us  [group_rounds(): lax.ppermute(value, axes, [(i, i ^ m * stride) for i in range(size)])]
    transpose x0 -> x2, local copies, waits for them, and re-layouts: none -> 0.92 us  [block_sums(): local = jnp.swapaxes(local.sum(axis=(-4, -2, -1)), -1, -2)]
  transfers between devices with their start and end apart: 20 -> 20, of which waited for: 9 -> 9; matrix products, arithmetic and copies ran while one was open for 18% -> 17% of each run, Pallas kernels for 0% -> 0%
where the time goes in v15:
time: 87.2 us; the launch traced here: 86.6 us
  other arithmetic  31 us (36%)
  starting transfers between devices  30.4 us (35%)
  waiting for transfers between devices  15.4 us (18%)
  local copies, waits for them, and re-layouts  7.92 us (9%)
  between operations  1.96 us (2%)
    ppermute x12, starting transfers between devices, group_rounds(): lax.ppermute(value, axes, [(i, i ^ m * stride) for i in range(size)])  15 us
    ppermute x12, waiting for transfers between devices, group_rounds(): lax.ppermute(value, axes, [(i, i ^ m * stride) for i in range(size)])  10.3 us
    ppermute x2, starting transfers between devices, with_halo(): before = lax.ppermute(last, axis, up)  10.3 us
    concatenate x5, other arithmetic, with_halo(): array = jnp.concatenate([before, array, after], axis=dim)  5.97 us
    add x12, other arithmetic, navier(): result.append(shear * laplace[channel] + (lame_first + shear) * divergence)  5.61 us
    ppermute x2, waiting for transfers between devices, with_halo(): got = lax.ppermute(jnp.where(first, last, initial), axis, [(0, 1), (1, 0)])  3.5 us
    select_n x2, other arithmetic, with_halo(): after = jnp.where(first, got_initial, zero)  2.64 us
    ppermute x2, starting transfers between devices, with_halo(): after = lax.ppermute(initial, axis, down)  2.57 us
  transfers between devices with their start and end apart: 20, of which 9 were waited for; matrix products, arithmetic and copies ran while one was open for 17% of the time, Pallas kernels for 0%

profile of v15, /device:TPU:0, one launch (start us, length us, event | category | flops | bytes accessed | tf_op | source)
XLA Modules:
  0.0 86.6 jit_solution(8262071420094160322)
XLA Ops:
  0.7 0.8 fusion.107
  1.5 1.3 %collective-permute-start.6 = (f32[6,1,16,128]{3,2,1,0:T(8,128)S(1)}, f32[6,1,16,128]{3,2,1,0:T(8,128)S(1)}, u32[]{:S(2)}, u32[]{:S(2)}) collective-permute-start(f32[6,1,16,128]{3,2,1,0:T(8,128)S(1)} %get-tuple-element.55), channel_id=1, source_target_pairs={{4,0},{8,4},{12,8},{5,1},{9,5},{13,9},{6,2},{10,6},{14,10},{7,3},{... | collective-permute-start | bytes 147464 | tf_op jit(solution)/shard_map/ppermute | solution.py:34
  2.8 5.6 %collective-permute-start.7 = (f32[6,1,16,128]{3,2,1,0:T(8,128)S(1)}, f32[6,1,16,128]{3,2,1,0:T(8,128)S(1)}, u32[]{:S(2)}, u32[]{:S(2)}) collective-permute-start(f32[6,1,16,128]{3,2,1,0:T(8,128)S(1)} %get-tuple-element.54), channel_id=1, source_target_pairs={{0,4},{4,8},{8,12},{1,5},{5,9},{9,13},{2,6},{6,10},{10,14},{3,7},{... | collective-permute-start | bytes 147464 | tf_op jit(solution)/shard_map/ppermute | solution.py:33
  8.4 0.7 compare_select_fusion
  9.1 1.5 %scatter_custom_fusion = f32[32768]{0:T(1024)S(1)} fusion(s32[256]{0:T(256)S(1)} %bitcast.53, f32[256]{0:T(256)S(1)} %broadcast.308, f32[]{:T(128)} %constant.28.clone.1), kind=kCustom, calls=%fused_computation.245 | custom fusion | bytes 131076 | tf_op jit(solution)/shard_map/scatter | solution.py:187
  10.5 1.2 %multiply_reduce_fusion.1 = f32[6]{0:T(128)S(1)} fusion(bf16[6,16,16,128]{3,2,1,0:T(8,128)(2,1)} %param.10, f32[16,16,128]{2,1,0:T(8,128)S(1)} %bitcast.40), kind=kLoop, calls=%fused_computation.46 | loop fusion | flops 589818 | bytes 524312 | tf_op jit(solution)/shard_map/reduce_sum | solution.py:223
  11.7 0.8 slice_bitcast_fusion.2
  13.1 0.8 slice_bitcast_fusion.1
  14.4 0.7 convert_multiply_fusion
  15.1 1.4 %multiply_subtract_fusion = (f32[3,16,16,128]{3,2,1,0:T(8,128)}, f32[3,16,16,128]{3,2,1,0:T(8,128)}, f32[3,16,16,128]{3,2,1,0:T(8,128)}, f32[3,16,16,128]{3,2,1,0:T(8,128)S(1)}, f32[3,16,16,128]{3,2,1,0:T(8,128)S(1)}) fusion(f32[6,16,16,128]{3,2,1,0:T(8,128)S(1)} %convert_element_type.15, f32[3]{0:T(128)S(1)} %get-tuple-element.70, ...), kind=kLoop, calls=%fused_computation.64 | loop fusion | flops 2359296 | bytes 3276824 | tf_op jit(solution)/shard_map/sub | solution.py:216
  16.9 2.0 %collective-permute-start.1 = (f32[12]{0:T(128)S(1)}, f32[12]{0:T(128)S(1)}, u32[]{:S(2)}, u32[]{:S(2)}) collective-permute-start(f32[12]{0:T(128)S(1)} %pad_maximum_fusion.17), channel_id=1, source_target_pairs={{0,2},{1,3},{2,0},{3,1},{4,6},{5,7},{6,4},{7,5},{8,10},{9,11},{10,... | collective-permute-start | bytes 152 | tf_op jit(solution)/shard_map/ppermute | solution.py:145
  19.1 1.8 %collective-permute-start.8 = (f32[6,18,1,128]{3,2,1,0:T(1,128)S(1)}, f32[6,18,1,128]{3,2,1,0:T(1,128)S(1)}, u32[]{:S(2)}, u32[]{:S(2)}) collective-permute-start(f32[6,18,1,128]{3,2,1,0:T(1,128)S(1)} %broadcast_select_fusion.5), channel_id=1, source_target_pairs={{0,2},{2,0},{1,3},{3,1},{4,6},{6,4},{5,7},{7,5},{8,10},{10,8},{9,1... | collective-permute-start | bytes 165896 | tf_op jit(solution)/shard_map/ppermute | solution.py:26
  20.9 0.9 %collective-permute-done.2 = f32[12]{0:T(128)S(1)} collective-permute-done((f32[12]{0:T(128)S(1)}, f32[12]{0:T(128)S(1)}, u32[]{:S(2)}, u32[]{:S(2)}) %collective-permute-start.2) | collective-permute-done | bytes 80 | tf_op jit(solution)/shard_map/ppermute | solution.py:145
  21.8 1.6 %collective-permute-start.3 = (f32[12]{0:T(128)S(1)}, f32[12]{0:T(128)S(1)}, u32[]{:S(2)}, u32[]{:S(2)}) collective-permute-start(f32[12]{0:T(128)S(1)} %add_add_fusion.6), channel_id=1, source_target_pairs={{0,4},{1,5},{2,6},{3,7},{4,0},{5,1},{6,2},{7,3},{8,12},{9,13},{10,... | collective-permute-start | bytes 152 | tf_op jit(solution)/shard_map/ppermute | solution.py:145
  23.4 1.1 %collective-permute-start.4 = (f32[12]{0:T(128)S(1)}, f32[12]{0:T(128)S(1)}, u32[]{:S(2)}, u32[]{:S(2)}) collective-permute-start(f32[12]{0:T(128)S(1)} %add_add_fusion.6), channel_id=1, source_target_pairs={{0,8},{1,9},{2,10},{3,11},{4,12},{5,13},{6,14},{7,15},{8,0},{9,1},... | collective-permute-start | bytes 152 | tf_op jit(solution)/shard_map/ppermute | solution.py:145
  24.5 1.7 %collective-permute-start.5 = (f32[12]{0:T(128)S(1)}, f32[12]{0:T(128)S(1)}, u32[]{:S(2)}, u32[]{:S(2)}) collective-permute-start(f32[12]{0:T(128)S(1)} %add_add_fusion.6), channel_id=1, source_target_pairs={{0,12},{1,13},{2,14},{3,15},{4,8},{5,9},{6,10},{7,11},{8,4},{9,5},... | collective-permute-start | bytes 152 | tf_op jit(solution)/shard_map/ppermute | solution.py:145
  26.7 1.2 %collective-permute-done.4 = f32[12]{0:T(128)S(1)} collective-permute-done((f32[12]{0:T(128)S(1)}, f32[12]{0:T(128)S(1)}, u32[]{:S(2)}, u32[]{:S(2)}) %collective-permute-start.4) | collective-permute-done | bytes 80 | tf_op jit(solution)/shard_map/ppermute | solution.py:145
  27.9 2.0 %collective-permute-done.5 = f32[12]{0:T(128)S(1)} collective-permute-done((f32[12]{0:T(128)S(1)}, f32[12]{0:T(128)S(1)}, u32[]{:S(2)}, u32[]{:S(2)}) %collective-permute-start.5) | collective-permute-done | bytes 80 | tf_op jit(solution)/shard_map/ppermute | solution.py:145
  30.9 2.1 %pad_maximum_fusion = (f32[6,18,18,129]{3,2,1,0:T(8,128)S(1)}, f32[6,18,18,129]{3,2,1,0:T(8,128)S(1)}) fusion(f32[6,18,18,1]{3,2,1,0:T(8,128)S(1)} %get-tuple-element.40, f32[6,18,1,128]{3,2,1,0:T(1,128)S(1)} %get-tuple-element.62, f32[6,1,16,128]{3,2,1,0:T(8,128)S(1)} %collective-permute-done.6, f32[6,16,16,128]{3,2,1,0:T(8,128)S(1)} %convert_element_type.12, ...), kind=kLoop, calls=%fused_computation.1 | loop fusion | flops 2507760 | bytes 3017088 | tf_op jit(solution)/shard_map/concatenate | solution.py:35
  35.2 0.7 fusion.82
  35.8 0.7 fusion.64
  37.5 0.8 multiply_reduce_fusion
  38.3 1.3 %collective-permute-start.10 = (f32[6,1,16,128]{3,2,1,0:T(8,128)S(1)}, f32[6,1,16,128]{3,2,1,0:T(8,128)S(1)}, u32[]{:S(2)}, u32[]{:S(2)}) collective-permute-start(f32[6,1,16,128]{3,2,1,0:T(8,128)S(1)} %get-tuple-element.53), channel_id=1, source_target_pairs={{4,0},{8,4},{12,8},{5,1},{9,5},{13,9},{6,2},{10,6},{14,10},{7,3},{... | collective-permute-start | bytes 147464 | tf_op jit(solution)/shard_map/ppermute | solution.py:34
  39.6 4.7 %collective-permute-start.11 = (f32[6,1,16,128]{3,2,1,0:T(8,128)S(1)}, f32[6,1,16,128]{3,2,1,0:T(8,128)S(1)}, u32[]{:S(2)}, u32[]{:S(2)}) collective-permute-start(f32[6,1,16,128]{3,2,1,0:T(8,128)S(1)} %get-tuple-element.52), channel_id=1, source_target_pairs={{0,4},{4,8},{8,12},{1,5},{5,9},{9,13},{2,6},{6,10},{10,14},{3,7},{... | collective-permute-start | bytes 147464 | tf_op jit(solution)/shard_map/ppermute | solution.py:33
  44.4 1.5 %collective-permute-done.11 = f32[6,1,16,128]{3,2,1,0:T(8,128)S(1)} collective-permute-done((f32[6,1,16,128]{3,2,1,0:T(8,128)S(1)}, f32[6,1,16,128]{3,2,1,0:T(8,128)S(1)}, u32[]{:S(2)}, u32[]{:S(2)}) %collective-permute-start.11) | collective-permute-done | bytes 49184 | tf_op jit(solution)/shard_map/ppermute | solution.py:33
  46.0 0.7 collective-permute-start.12
  46.7 3.5 %collective-permute-done.12 = f32[6,18,1,128]{3,2,1,0:T(1,128)S(1)} collective-permute-done((f32[6,18,1,128]{3,2,1,0:T(1,128)S(1)}, f32[6,18,1,128]{3,2,1,0:T(1,128)S(1)}, u32[]{:S(2)}, u32[]{:S(2)}) %collective-permute-start.12) | collective-permute-done | bytes 55328 | tf_op jit(solution)/shard_map/ppermute | solution.py:26
  50.3 1.3 %pad_maximum_fusion.4 = f32[6,18,18,128]{3,2,1,0:T(8,128)} fusion(f32[6,18,1,128]{3,2,1,0:T(1,128)S(1)} %get-tuple-element.60, f32[6,1,16,128]{3,2,1,0:T(8,128)S(1)} %collective-permute-done.10, f32[6,16,16,128]{3,2,1,0:T(8,128)S(1)} %get-tuple-element.51, f32[6,1,16,128]{3,2,1,0:T(8,128)S(1)} %collective-permute-done.11, ...), kind=kLoop, calls=%fused_computation.14 | loop fusion | flops 995328 | bytes 1990656 | tf_op jit(solution)/shard_map/concatenate | solution.py:35
  51.6 1.0 %convert_element_type.13 = f32[6,16,16,128]{3,2,1,0:T(8,128)} convert(bf16[6,16,16,128]{3,2,1,0:T(8,128)(2,1)S(1)} %copy-done.3) | non-fusion elementwise | flops 196608 | bytes 1179648 | tf_op jit(solution)/shard_map/convert_element_type | solution.py:192
  52.5 1.2 %multiply_add_fusion = f32[3,16,16,128]{3,2,1,0:T(8,128)S(1)} fusion(f32[3,16,16,128]{3,2,1,0:T(8,128)} %get-tuple-element.17, f32[3,16,16,128]{3,2,1,0:T(8,128)} %get-tuple-element.16), kind=kLoop, calls=%fused_computation.63 | loop fusion | flops 196608 | bytes 1179648 | tf_op jit(solution)/shard_map/add | solution.py:217
  53.8 0.9 %maximum_reduce_fusion = f32[6,16,16]{2,1,0:T(8,128)} fusion(f32[3,16,16,128]{3,2,1,0:T(8,128)S(1)} %multiply_add_fusion, f32[3,16,16,128]{3,2,1,0:T(8,128)S(1)} %copy-done.2), kind=kLoop, calls=%fused_computation.42 | loop fusion | flops 391680 | bytes 792576 | tf_op jit(solution)/shard_map/reduce_sum | solution.py:207
  54.6 0.9 %reduce_sum.115 = f32[6,4,4,4,4]{4,3,2,1,0:T(4,128)S(1)} reshape(f32[6,16,16]{2,1,0:T(8,128)} %maximum_reduce_fusion) | data formatting | bytes 12288 | tf_op jit(solution)/shard_map/reduce_sum | solution.py:207
  55.6 0.7 reduce_sum.116
  56.3 0.8 copy.15
  57.9 2.2 %slice_select_fusion.1 = (f32[6,18,18,1]{3,2,1,0:T(8,128)S(1)}, f32[6,18,18,1]{3,2,1,0:T(8,128)S(1)}) fusion(f32[6,18,18,128]{3,2,1,0:T(8,128)} %collective-permute-done.13, pred[]{:T(512)S(6)} %eq.67), kind=kLoop, calls=%fused_computation.6 | loop fusion | flops 3888 | bytes 31105 | tf_op jit(solution)/shard_map/jit(_where)/select_n | solution.py:23
  60.1 2.1 %pad_maximum_fusion.1 = (f32[6,18,18,129]{3,2,1,0:T(8,128)S(1)}, f32[6,18,18,129]{3,2,1,0:T(8,128)S(1)}) fusion(f32[6,18,18,1]{3,2,1,0:T(8,128)S(1)} %get-tuple-element.38, f32[6,18,1,128]{3,2,1,0:T(1,128)S(1)} %get-tuple-element.60, f32[6,1,16,128]{3,2,1,0:T(8,128)S(1)} %collective-permute-done.10, f32[6,16,16,128]{3,2,1,0:T(8,128)S(1)} %get-tuple-element.51, ...), kind=kLoop, calls=%fused_computation.3 | loop fusion | flops 2507760 | bytes 3017088 | tf_op jit(solution)/shard_map/concatenate | solution.py:35
  64.3 0.7 fusion.28
  65.0 0.7 fusion.46
  66.4 1.2 %subtract_reduce_fusion = (f32[16,16,128]{2,1,0:T(8,128)S(1)}, f32[3,16,16,128]{3,2,1,0:T(8,128)S(1)}, f32[3,16,16,128]{3,2,1,0:T(8,128)}) fusion(f32[6,16,16,128]{3,2,1,0:T(8,128)S(1)} %convert_element_type.15, f32[3,16,16,128]{3,2,1,0:T(8,128)S(1)} %get-tuple-element.37, f32[3]{0:T(128)S(1)} %copy-done.10, f32[16,16,128]{2,1,0:T(8,128)S(1)} %get-tuple-element.58, ...), kind=kLoop, calls=%fused_computation.67 | loop fusion | flops 2719744 | bytes 3670040 | tf_op jit(solution)/shard_map/reduce_sum | solution.py:248
  68.9 0.7 collective-permute-start.15
  69.6 0.8 collective-permute-start.16
  70.4 2.2 %collective-permute-done.15 = f32[902]{0:T(1024)S(1)} collective-permute-done((f32[902]{0:T(1024)S(1)}, f32[902]{0:T(1024)S(1)}, u32[]{:S(2)}, u32[]{:S(2)}) %collective-permute-start.15) | collective-permute-done | bytes 3640 | tf_op jit(solution)/shard_map/ppermute | solution.py:145
  72.7 4.1 %collective-permute-start.17 = (f32[902]{0:T(1024)S(1)}, f32[902]{0:T(1024)S(1)}, u32[]{:S(2)}, u32[]{:S(2)}) collective-permute-start(f32[902]{0:T(1024)S(1)} %add_add_fusion.3), channel_id=1, source_target_pairs={{0,4},{1,5},{2,6},{3,7},{4,0},{5,1},{6,2},{7,3},{8,12},{9,13},{10,... | collective-permute-start | bytes 10832 | tf_op jit(solution)/shard_map/ppermute | solution.py:145
  76.8 1.0 %collective-permute-start.18 = (f32[902]{0:T(1024)S(1)}, f32[902]{0:T(1024)S(1)}, u32[]{:S(2)}, u32[]{:S(2)}) collective-permute-start(f32[902]{0:T(1024)S(1)} %add_add_fusion.3), channel_id=1, source_target_pairs={{0,8},{1,9},{2,10},{3,11},{4,12},{5,13},{6,14},{7,15},{8,0},{9,1},... | collective-permute-start | bytes 10832 | tf_op jit(solution)/shard_map/ppermute | solution.py:145
  77.8 1.4 %collective-permute-start.19 = (f32[902]{0:T(1024)S(1)}, f32[902]{0:T(1024)S(1)}, u32[]{:S(2)}, u32[]{:S(2)}) collective-permute-start(f32[902]{0:T(1024)S(1)} %add_add_fusion.3), channel_id=1, source_target_pairs={{0,12},{1,13},{2,14},{3,15},{4,8},{5,9},{6,10},{7,11},{8,4},{9,5},... | collective-permute-start | bytes 10832 | tf_op jit(solution)/shard_map/ppermute | solution.py:145
  79.2 2.1 %collective-permute-done.18 = f32[902]{0:T(1024)S(1)} collective-permute-done((f32[902]{0:T(1024)S(1)}, f32[902]{0:T(1024)S(1)}, u32[]{:S(2)}, u32[]{:S(2)}) %collective-permute-start.18) | collective-permute-done | bytes 3640 | tf_op jit(solution)/shard_map/ppermute | solution.py:145
  81.3 1.9 %collective-permute-done.19 = f32[902]{0:T(1024)S(1)} collective-permute-done((f32[902]{0:T(1024)S(1)}, f32[902]{0:T(1024)S(1)}, u32[]{:S(2)}, u32[]{:S(2)}) %collective-permute-start.19) | collective-permute-done | bytes 3640 | tf_op jit(solution)/shard_map/ppermute | solution.py:145
  84.6 2.0 %fusion.13 = f32[6,16,16,128]{3,2,1,0:T(8,128)} fusion(f32[3,16,16,128]{3,2,1,0:T(8,128)S(1)} %get-tuple-element.19, f32[3,16,16,128]{3,2,1,0:T(8,128)S(1)} %get-tuple-element.18, f32[3,16,16,128]{3,2,1,0:T(8,128)} %get-tuple-element.14, f32[3,16,16,128]{3,2,1,0:T(8,128)S(1)} %get-tuple-element.13, f32[6]{0:T(128)S(1)} %pad_maximum_fusion.19, ...), kind=kLoop, calls=%fused_computation.38 | loop fusion | flops 1376256 | bytes 2359344 | tf_op jit(solution)/shard_map/add | solution.py:131
  (118 shorter events, 12.1 us)
Async XLA Ops:
  0.6 13.3 %copy-start.5 = (bf16[6,16,16,128]{3,2,1,0:T(8,128)(2,1)S(1)}, bf16[6,16,16,128]{3,2,1,0:T(8,128)(2,1)}, u32[]{:S(2)}) copy-start(bf16[6,16,16,128]{3,2,1,0:T(8,128)(2,1)} %param.11) | copy-start | bytes 1179652
  0.6 13.3 %copy-start.16 = (s32[2,2,4]{2,1,0:T(2,128)S(1)}, s32[2,2,4]{2,1,0:T(2,128)}, u32[]{:S(2)}) copy-start(s32[2,2,4]{2,1,0:T(2,128)} %param.13) | copy-start | bytes 196
  0.7 13.8 %copy-start.6 = (bf16[16,16,128]{2,1,0:T(8,128)(2,1)S(1)}, bf16[16,16,128]{2,1,0:T(8,128)(2,1)}, u32[]{:S(2)}) copy-start(bf16[16,16,128]{2,1,0:T(8,128)(2,1)} %param.12) | copy-start | bytes 196612
  1.5 17.6 %collective-permute-start.6 = (f32[6,1,16,128]{3,2,1,0:T(8,128)S(1)}, f32[6,1,16,128]{3,2,1,0:T(8,128)S(1)}, u32[]{:S(2)}, u32[]{:S(2)}) collective-permute-start(f32[6,1,16,128]{3,2,1,0:T(8,128)S(1)} %get-tuple-element.55), channel_id=1, source_target_pairs={{4,0},{8,4},{12,8},{5,1},{9,5},{13,9},{6,2},{10,6},{14,10},{7,3},{... | collective-permute-start | bytes 147464 | tf_op jit(solution)/shard_map/ppermute | solution.py:34
  2.8 16.3 %collective-permute-start.7 = (f32[6,1,16,128]{3,2,1,0:T(8,128)S(1)}, f32[6,1,16,128]{3,2,1,0:T(8,128)S(1)}, u32[]{:S(2)}, u32[]{:S(2)}) collective-permute-start(f32[6,1,16,128]{3,2,1,0:T(8,128)S(1)} %get-tuple-element.54), channel_id=1, source_target_pairs={{0,4},{4,8},{8,12},{1,5},{5,9},{9,13},{2,6},{6,10},{10,14},{3,7},{... | collective-permute-start | bytes 147464 | tf_op jit(solution)/shard_map/ppermute | solution.py:33
  13.9 23.4 %copy-start.7 = (f32[3]{0:T(128)}, f32[3]{0:T(128)S(1)}, u32[]{:S(2)}) copy-start(f32[3]{0:T(128)S(1)} %get-tuple-element.69) | copy-start | bytes 40
  13.9 23.4 %copy-start.9 = (f32[3]{0:T(128)}, f32[3]{0:T(128)S(1)}, u32[]{:S(2)}) copy-start(f32[3]{0:T(128)S(1)} %get-tuple-element.70) | copy-start | bytes 40
  15.1 3.8 %copy-start = (bf16[6,16,16,128]{3,2,1,0:T(8,128)(2,1)S(1)}, bf16[6,16,16,128]{3,2,1,0:T(8,128)(2,1)}, u32[]{:S(2)}) copy-start(bf16[6,16,16,128]{3,2,1,0:T(8,128)(2,1)} %param.10) | copy-start | bytes 1179652
  16.9 4.1 %collective-permute-start = (f32[12]{0:T(128)S(1)}, f32[12]{0:T(128)S(1)}, u32[]{:S(2)}, u32[]{:S(2)}) collective-permute-start(f32[12]{0:T(128)S(1)} %pad_maximum_fusion.17), channel_id=1, source_target_pairs={{0,1},{1,0},{2,3},{3,2},{4,5},{5,4},{6,7},{7,6},{8,9},{9,8},{10,11... | collective-permute-start | bytes 152 | tf_op jit(solution)/shard_map/ppermute | solution.py:145
  16.9 4.1 %collective-permute-start.1 = (f32[12]{0:T(128)S(1)}, f32[12]{0:T(128)S(1)}, u32[]{:S(2)}, u32[]{:S(2)}) collective-permute-start(f32[12]{0:T(128)S(1)} %pad_maximum_fusion.17), channel_id=1, source_target_pairs={{0,2},{1,3},{2,0},{3,1},{4,6},{5,7},{6,4},{7,5},{8,10},{9,11},{10,... | collective-permute-start | bytes 152 | tf_op jit(solution)/shard_map/ppermute | solution.py:145
  18.9 3.0 %collective-permute-start.2 = (f32[12]{0:T(128)S(1)}, f32[12]{0:T(128)S(1)}, u32[]{:S(2)}, u32[]{:S(2)}) collective-permute-start(f32[12]{0:T(128)S(1)} %pad_maximum_fusion.17), channel_id=1, source_target_pairs={{0,3},{1,2},{2,1},{3,0},{4,7},{5,6},{6,5},{7,4},{8,11},{9,10},{10,... | collective-permute-start | bytes 152 | tf_op jit(solution)/shard_map/ppermute | solution.py:145
  19.1 10.9 %copy-start.3 = (bf16[6,16,16,128]{3,2,1,0:T(8,128)(2,1)S(1)}, bf16[6,16,16,128]{3,2,1,0:T(8,128)(2,1)}, u32[]{:S(2)}) copy-start(bf16[6,16,16,128]{3,2,1,0:T(8,128)(2,1)} %param.9) | copy-start | bytes 1179652
  19.1 7.1 %collective-permute-start.8 = (f32[6,18,1,128]{3,2,1,0:T(1,128)S(1)}, f32[6,18,1,128]{3,2,1,0:T(1,128)S(1)}, u32[]{:S(2)}, u32[]{:S(2)}) collective-permute-start(f32[6,18,1,128]{3,2,1,0:T(1,128)S(1)} %broadcast_select_fusion.5), channel_id=1, source_target_pairs={{0,2},{2,0},{1,3},{3,1},{4,6},{6,4},{5,7},{7,5},{8,10},{10,8},{9,1... | collective-permute-start | bytes 165896 | tf_op jit(solution)/shard_map/ppermute | solution.py:26
  21.8 4.8 %collective-permute-start.3 = (f32[12]{0:T(128)S(1)}, f32[12]{0:T(128)S(1)}, u32[]{:S(2)}, u32[]{:S(2)}) collective-permute-start(f32[12]{0:T(128)S(1)} %add_add_fusion.6), channel_id=1, source_target_pairs={{0,4},{1,5},{2,6},{3,7},{4,0},{5,1},{6,2},{7,3},{8,12},{9,13},{10,... | collective-permute-start | bytes 152 | tf_op jit(solution)/shard_map/ppermute | solution.py:145
  23.4 4.4 %collective-permute-start.4 = (f32[12]{0:T(128)S(1)}, f32[12]{0:T(128)S(1)}, u32[]{:S(2)}, u32[]{:S(2)}) collective-permute-start(f32[12]{0:T(128)S(1)} %add_add_fusion.6), channel_id=1, source_target_pairs={{0,8},{1,9},{2,10},{3,11},{4,12},{5,13},{6,14},{7,15},{8,0},{9,1},... | collective-permute-start | bytes 152 | tf_op jit(solution)/shard_map/ppermute | solution.py:145
  24.5 5.3 %collective-permute-start.5 = (f32[12]{0:T(128)S(1)}, f32[12]{0:T(128)S(1)}, u32[]{:S(2)}, u32[]{:S(2)}) collective-permute-start(f32[12]{0:T(128)S(1)} %add_add_fusion.6), channel_id=1, source_target_pairs={{0,12},{1,13},{2,14},{3,15},{4,8},{5,9},{6,10},{7,11},{8,4},{9,5},... | collective-permute-start | bytes 152 | tf_op jit(solution)/shard_map/ppermute | solution.py:145
  26.6 3.8 %collective-permute-start.9 = (f32[6,18,18,128]{3,2,1,0:T(8,128)S(1)}, f32[6,18,18,128]{3,2,1,0:T(8,128)S(1)}, u32[]{:S(2)}, u32[]{:S(2)}) collective-permute-start(f32[6,18,18,128]{3,2,1,0:T(8,128)S(1)} %maximum_add_fusion), channel_id=1, source_target_pairs={{0,1},{1,0},{2,3},{3,2},{4,5},{5,4},{6,7},{7,6},{8,9},{9,8},{10,11... | collective-permute-start | bytes 2985992 | tf_op jit(solution)/shard_map/ppermute | solution.py:18
  29.9 0.5 copy-start.13
  29.9 7.6 %copy-start.11 = (f32[6]{0:T(128)}, f32[6]{0:T(128)S(1)}, u32[]{:S(2)}) copy-start(f32[6]{0:T(128)S(1)} %slice_multiply_fusion.12) | copy-start | bytes 76
  35.8 0.9 %copy-start.4 = (f32[16,16,128]{2,1,0:T(8,128)S(1)}, f32[16,16,128]{2,1,0:T(8,128)}, u32[]{:S(2)}) copy-start(f32[16,16,128]{2,1,0:T(8,128)} %get-tuple-element.56) | copy-start | bytes 393220
  38.3 6.0 %collective-permute-start.10 = (f32[6,1,16,128]{3,2,1,0:T(8,128)S(1)}, f32[6,1,16,128]{3,2,1,0:T(8,128)S(1)}, u32[]{:S(2)}, u32[]{:S(2)}) collective-permute-start(f32[6,1,16,128]{3,2,1,0:T(8,128)S(1)} %get-tuple-element.53), channel_id=1, source_target_pairs={{4,0},{8,4},{12,8},{5,1},{9,5},{13,9},{6,2},{10,6},{14,10},{7,3},{... | collective-permute-start | bytes 147464 | tf_op jit(solution)/shard_map/ppermute | solution.py:34
  39.6 6.3 %collective-permute-start.11 = (f32[6,1,16,128]{3,2,1,0:T(8,128)S(1)}, f32[6,1,16,128]{3,2,1,0:T(8,128)S(1)}, u32[]{:S(2)}, u32[]{:S(2)}) collective-permute-start(f32[6,1,16,128]{3,2,1,0:T(8,128)S(1)} %get-tuple-element.52), channel_id=1, source_target_pairs={{0,4},{4,8},{8,12},{1,5},{5,9},{9,13},{2,6},{6,10},{10,14},{3,7},{... | collective-permute-start | bytes 147464 | tf_op jit(solution)/shard_map/ppermute | solution.py:33
  46.0 4.2 %collective-permute-start.12 = (f32[6,18,1,128]{3,2,1,0:T(1,128)S(1)}, f32[6,18,1,128]{3,2,1,0:T(1,128)S(1)}, u32[]{:S(2)}, u32[]{:S(2)}) collective-permute-start(f32[6,18,1,128]{3,2,1,0:T(1,128)S(1)} %broadcast_select_fusion.2), channel_id=1, source_target_pairs={{0,2},{2,0},{1,3},{3,1},{4,6},{6,4},{5,7},{7,5},{8,10},{10,8},{9,1... | collective-permute-start | bytes 165896 | tf_op jit(solution)/shard_map/ppermute | solution.py:26
  51.6 6.3 %collective-permute-start.13 = (f32[6,18,18,128]{3,2,1,0:T(8,128)}, f32[6,18,18,128]{3,2,1,0:T(8,128)}, u32[]{:S(2)}, u32[]{:S(2)}) collective-permute-start(f32[6,18,18,128]{3,2,1,0:T(8,128)} %pad_maximum_fusion.4), channel_id=1, source_target_pairs={{0,1},{1,0},{2,3},{3,2},{4,5},{5,4},{6,7},{7,6},{8,9},{9,8},{10,11... | collective-permute-start | bytes 2985992 | tf_op jit(solution)/shard_map/ppermute | solution.py:18
  52.5 1.2 %copy-start.2 = (f32[3,16,16,128]{3,2,1,0:T(8,128)S(1)}, f32[3,16,16,128]{3,2,1,0:T(8,128)}, u32[]{:S(2)}) copy-start(f32[3,16,16,128]{3,2,1,0:T(8,128)} %get-tuple-element.15) | copy-start | bytes 1179652
  65.0 1.1 %copy-start.1 = (f32[6,16,16,128]{3,2,1,0:T(8,128)S(1)}, f32[6,16,16,128]{3,2,1,0:T(8,128)}, u32[]{:S(2)}) copy-start(f32[6,16,16,128]{3,2,1,0:T(8,128)} %convert_element_type.13) | copy-start | bytes 2359300
  65.0 1.1 %copy-start.8 = (f32[3]{0:T(128)S(1)}, f32[3]{0:T(128)}, u32[]{:S(2)}) copy-start(f32[3]{0:T(128)} %copy-done.7) | copy-start | bytes 40
  65.0 1.1 %copy-start.10 = (f32[3]{0:T(128)S(1)}, f32[3]{0:T(128)}, u32[]{:S(2)}) copy-start(f32[3]{0:T(128)} %copy-done.9) | copy-start | bytes 40
  66.4 1.9 %copy-start.15 = (f32[6]{0:T(128)S(1)}, f32[6]{0:T(128)}, u32[]{:S(2)}) copy-start(f32[6]{0:T(128)} %get-tuple-element.50) | copy-start | bytes 76
  66.4 16.9 %copy-start.12 = (f32[6]{0:T(128)S(1)}, f32[6]{0:T(128)}, u32[]{:S(2)}) copy-start(f32[6]{0:T(128)} %copy-done.11) | copy-start | bytes 76
  66.4 16.9 %copy-start.14 = (f32[12]{0:T(128)S(1)}, f32[12]{0:T(128)}, u32[]{:S(2)}) copy-start(f32[12]{0:T(128)} %copy-done.13) | copy-start | bytes 148
  68.4 1.9 %collective-permute-start.14 = (f32[902]{0:T(1024)S(1)}, f32[902]{0:T(1024)S(1)}, u32[]{:S(2)}, u32[]{:S(2)}) collective-permute-start(f32[902]{0:T(1024)S(1)} %pad_maximum_fusion.16), channel_id=1, source_target_pairs={{0,1},{1,0},{2,3},{3,2},{4,5},{5,4},{6,7},{7,6},{8,9},{9,8},{10,11... | collective-permute-start | bytes 10832 | tf_op jit(solution)/shard_map/ppermute | solution.py:145
  68.9 3.6 %collective-permute-start.15 = (f32[902]{0:T(1024)S(1)}, f32[902]{0:T(1024)S(1)}, u32[]{:S(2)}, u32[]{:S(2)}) collective-permute-start(f32[902]{0:T(1024)S(1)} %pad_maximum_fusion.16), channel_id=1, source_target_pairs={{0,2},{1,3},{2,0},{3,1},{4,6},{5,7},{6,4},{7,5},{8,10},{9,11},{10,... | collective-permute-start | bytes 10832 | tf_op jit(solution)/shard_map/ppermute | solution.py:145
  69.6 3.1 %collective-permute-start.16 = (f32[902]{0:T(1024)S(1)}, f32[902]{0:T(1024)S(1)}, u32[]{:S(2)}, u32[]{:S(2)}) collective-permute-start(f32[902]{0:T(1024)S(1)} %pad_maximum_fusion.16), channel_id=1, source_target_pairs={{0,3},{1,2},{2,1},{3,0},{4,7},{5,6},{6,5},{7,4},{8,11},{9,10},{10,... | collective-permute-start | bytes 10832 | tf_op jit(solution)/shard_map/ppermute | solution.py:145
  72.7 6.6 %collective-permute-start.17 = (f32[902]{0:T(1024)S(1)}, f32[902]{0:T(1024)S(1)}, u32[]{:S(2)}, u32[]{:S(2)}) collective-permute-start(f32[902]{0:T(1024)S(1)} %add_add_fusion.3), channel_id=1, source_target_pairs={{0,4},{1,5},{2,6},{3,7},{4,0},{5,1},{6,2},{7,3},{8,12},{9,13},{10,... | collective-permute-start | bytes 10832 | tf_op jit(solution)/shard_map/ppermute | solution.py:145
  76.8 4.5 %collective-permute-start.18 = (f32[902]{0:T(1024)S(1)}, f32[902]{0:T(1024)S(1)}, u32[]{:S(2)}, u32[]{:S(2)}) collective-permute-start(f32[902]{0:T(1024)S(1)} %add_add_fusion.3), channel_id=1, source_target_pairs={{0,8},{1,9},{2,10},{3,11},{4,12},{5,13},{6,14},{7,15},{8,0},{9,1},... | collective-permute-start | bytes 10832 | tf_op jit(solution)/shard_map/ppermute | solution.py:145
  77.8 5.4 %collective-permute-start.19 = (f32[902]{0:T(1024)S(1)}, f32[902]{0:T(1024)S(1)}, u32[]{:S(2)}, u32[]{:S(2)}) collective-permute-start(f32[902]{0:T(1024)S(1)} %add_add_fusion.3), channel_id=1, source_target_pairs={{0,12},{1,13},{2,14},{3,15},{4,8},{5,9},{6,10},{7,11},{8,4},{9,5},... | collective-permute-start | bytes 10832 | tf_op jit(solution)/shard_map/ppermute | solution.py:145

commit v16 on v12

--- a/solution.py
+++ b/solution.py
@@ -16,8 +16,9 @@
             first = lax.axis_index(axis) == 0
             sent = array if tie is None else array + tie
             got = lax.ppermute(sent, axis, [(0, 1), (1, 0)])
-            got_last = lax.slice_in_dim(got, length - width, length, axis=dim)
-            got_initial = lax.slice_in_dim(got, 0, width, axis=dim)
+            lane = lax.broadcasted_iota(jnp.int32, got.shape, dim)
+            got_last = jnp.sum(jnp.where(lane == length - 1, got, 0.0), axis=dim, keepdims=True)
+            got_initial = jnp.sum(jnp.where(lane == 0, got, 0.0), axis=dim, keepdims=True)
             zero = jnp.zeros_like(got_last)
             before = jnp.where(first, zero, got_last)
             after = jnp.where(first, got_initial, zero)

time: 87.4 us -> 98.7 us (1.13)
  local copies, waits for them, and re-layouts: 9.03 us -> 14 us
  other arithmetic: 30.4 us -> 34.1 us
  waiting for transfers between devices: 16.1 us -> 17.6 us
    concatenate x5, other arithmetic: 5.97 us -> 10.9 us  [with_halo(): array = jnp.concatenate([before, array, after], axis=dim)]
    select_n x0 -> x4, local copies, waits for them, and re-layouts: none -> 4.86 us  [the longest x2 3.3 us: with_halo(): before = jnp.where(first, zero, got_last)]
    unnamed x35 -> x113, local copies, waits for them, and re-layouts: 1.43 us -> 4.35 us
    select_n x2, other arithmetic: 2.64 us -> 0.02 us  [with_halo(): after = jnp.where(first, got_initial, zero)]
    reduce_sum x0 -> x2, other arithmetic: none -> 2.16 us  [with_halo(): jnp.sum(jnp.where(lane == 0, got, 0.0), axis=dim, keepdims=True)]
    ppermute x12, starting transfers between devices: 13.8 us -> 15.7 us  [group_rounds(): lax.ppermute(value, axes, [(i, i ^ m * stride) for i in range(size)])]
    ppermute x2, waiting for transfers between devices: 1.54 us -> 3.12 us  [with_halo(): before = lax.ppermute(last, axis, up)]
    select_n x0 -> x2, other arithmetic: none -> 1.28 us  [with_halo(): before = jnp.where(first, zero, got_last)]
  transfers between devices with their start and end apart: 20 -> 20, of which waited for: 9 -> 9; matrix products, arithmetic and copies ran while one was open for 18% -> 8% of each run, Pallas kernels for 0% -> 0%
where the time goes in v16:
time: 98.7 us; the launch traced here: 98 us
  other arithmetic  34.1 us (35%)
  starting transfers between devices  30 us (30%)
  waiting for transfers between devices  17.6 us (18%)
  local copies, waits for them, and re-layouts  14 us (14%)
  between operations  2.27 us (2%)
    ppermute x12, starting transfers between devices, group_rounds(): lax.ppermute(value, axes, [(i, i ^ m * stride) for i in range(size)])  15.7 us
    ppermute x12, waiting for transfers between devices, group_rounds(): lax.ppermute(value, axes, [(i, i ^ m * stride) for i in range(size)])  10.9 us
    concatenate x5, other arithmetic, with_halo(): array = jnp.concatenate([before, array, after], axis=dim)  10.9 us
    ppermute x2, starting transfers between devices, with_halo(): before = lax.ppermute(last, axis, up)  9.28 us
    add x12, other arithmetic, navier(): result.append(shear * laplace[channel] + (lame_first + shear) * divergence)  5.59 us
    unnamed x113, local copies, waits for them, and re-layouts  4.35 us
    ppermute x2, waiting for transfers between devices, with_halo(): got = lax.ppermute(jnp.where(first, last, initial), axis, [(0, 1), (1, 0)])  3.62 us
    select_n x2, local copies, waits for them, and re-layouts, with_halo(): before = jnp.where(first, zero, got_last)  3.3 us
  transfers between devices with their start and end apart: 20, of which 9 were waited for; matrix products, arithmetic and copies ran while one was open for 8% of the time, Pallas kernels for 0%

profile of v16, /device:TPU:0, one launch (start us, length us, event | category | flops | bytes accessed | tf_op | source)
XLA Modules:
  0.0 98.0 jit_solution(17172744136687253010)
XLA Ops:
  0.7 0.8 slice_bitcast_fusion.2
  2.1 0.7 compare_select_fusion
  2.8 1.5 %scatter_custom_fusion = f32[32768]{0:T(1024)S(1)} fusion(s32[256]{0:T(256)S(1)} %bitcast.55, f32[256]{0:T(256)S(1)} %broadcast.391, f32[]{:T(128)} %constant.28.clone.1), kind=kCustom, calls=%fused_computation.249 | custom fusion | bytes 131076 | tf_op jit(solution)/shard_map/scatter | solution.py:188
  4.3 0.8 slice_bitcast_fusion.1
  5.0 1.1 %convert_element_type.15 = f32[6,16,16,128]{3,2,1,0:T(8,128)S(1)} convert(bf16[6,16,16,128]{3,2,1,0:T(8,128)(2,1)} %param.11) | non-fusion elementwise | flops 196608 | bytes 1179648 | tf_op jit(solution)/shard_map/convert_element_type | solution.py:212
  6.5 0.7 multiply_add_fusion.5
  7.2 0.7 convert_multiply_fusion
  7.8 1.4 %multiply_subtract_fusion = (f32[3,16,16,128]{3,2,1,0:T(8,128)}, f32[3,16,16,128]{3,2,1,0:T(8,128)}, f32[3,16,16,128]{3,2,1,0:T(8,128)}, f32[3,16,16,128]{3,2,1,0:T(8,128)S(1)}, f32[3,16,16,128]{3,2,1,0:T(8,128)S(1)}) fusion(f32[6,16,16,128]{3,2,1,0:T(8,128)S(1)} %convert_element_type.15, f32[3]{0:T(128)S(1)} %get-tuple-element.78, ...), kind=kLoop, calls=%fused_computation.64 | loop fusion | flops 2359296 | bytes 3276824 | tf_op jit(solution)/shard_map/sub | solution.py:217
  10.3 2.6 %collective-permute-start.1 = (f32[12]{0:T(128)S(1)}, f32[12]{0:T(128)S(1)}, u32[]{:S(2)}, u32[]{:S(2)}) collective-permute-start(f32[12]{0:T(128)S(1)} %pad_maximum_fusion.17), channel_id=1, source_target_pairs={{0,2},{1,3},{2,0},{3,1},{4,6},{5,7},{6,4},{7,5},{8,10},{9,11},{10,... | collective-permute-start | bytes 152 | tf_op jit(solution)/shard_map/ppermute | solution.py:146
  13.0 1.3 %collective-permute-start.6 = (f32[6,1,16,128]{3,2,1,0:T(8,128)S(1)}, f32[6,1,16,128]{3,2,1,0:T(8,128)S(1)}, u32[]{:S(2)}, u32[]{:S(2)}) collective-permute-start(f32[6,1,16,128]{3,2,1,0:T(8,128)S(1)} %get-tuple-element.63), channel_id=1, source_target_pairs={{4,0},{8,4},{12,8},{5,1},{9,5},{13,9},{6,2},{10,6},{14,10},{7,3},{... | collective-permute-start | bytes 147464 | tf_op jit(solution)/shard_map/ppermute | solution.py:35
  14.3 4.5 %collective-permute-start.7 = (f32[6,1,16,128]{3,2,1,0:T(8,128)S(1)}, f32[6,1,16,128]{3,2,1,0:T(8,128)S(1)}, u32[]{:S(2)}, u32[]{:S(2)}) collective-permute-start(f32[6,1,16,128]{3,2,1,0:T(8,128)S(1)} %get-tuple-element.62), channel_id=1, source_target_pairs={{0,4},{4,8},{8,12},{1,5},{5,9},{9,13},{2,6},{6,10},{10,14},{3,7},{... | collective-permute-start | bytes 147464 | tf_op jit(solution)/shard_map/ppermute | solution.py:34
  19.0 1.6 %collective-permute-done.7 = f32[6,1,16,128]{3,2,1,0:T(8,128)S(1)} collective-permute-done((f32[6,1,16,128]{3,2,1,0:T(8,128)S(1)}, f32[6,1,16,128]{3,2,1,0:T(8,128)S(1)}, u32[]{:S(2)}, u32[]{:S(2)}) %collective-permute-start.7) | collective-permute-done | bytes 49184 | tf_op jit(solution)/shard_map/ppermute | solution.py:34
  20.6 1.8 %collective-permute-start.8 = (f32[6,18,1,128]{3,2,1,0:T(1,128)S(1)}, f32[6,18,1,128]{3,2,1,0:T(1,128)S(1)}, u32[]{:S(2)}, u32[]{:S(2)}) collective-permute-start(f32[6,18,1,128]{3,2,1,0:T(1,128)S(1)} %broadcast_select_fusion.5), channel_id=1, source_target_pairs={{0,2},{2,0},{1,3},{3,1},{4,6},{6,4},{5,7},{7,5},{8,10},{10,8},{9,1... | collective-permute-start | bytes 165896 | tf_op jit(solution)/shard_map/ppermute | solution.py:27
  22.4 2.4 %collective-permute-start.3 = (f32[12]{0:T(128)S(1)}, f32[12]{0:T(128)S(1)}, u32[]{:S(2)}, u32[]{:S(2)}) collective-permute-start(f32[12]{0:T(128)S(1)} %add_add_fusion.6), channel_id=1, source_target_pairs={{0,4},{1,5},{2,6},{3,7},{4,0},{5,1},{6,2},{7,3},{8,12},{9,13},{10,... | collective-permute-start | bytes 152 | tf_op jit(solution)/shard_map/ppermute | solution.py:146
  24.9 2.6 %collective-permute-start.4 = (f32[12]{0:T(128)S(1)}, f32[12]{0:T(128)S(1)}, u32[]{:S(2)}, u32[]{:S(2)}) collective-permute-start(f32[12]{0:T(128)S(1)} %add_add_fusion.6), channel_id=1, source_target_pairs={{0,8},{1,9},{2,10},{3,11},{4,12},{5,13},{6,14},{7,15},{8,0},{9,1},... | collective-permute-start | bytes 152 | tf_op jit(solution)/shard_map/ppermute | solution.py:146
  27.9 1.4 %collective-permute-done.4 = f32[12]{0:T(128)S(1)} collective-permute-done((f32[12]{0:T(128)S(1)}, f32[12]{0:T(128)S(1)}, u32[]{:S(2)}, u32[]{:S(2)}) %collective-permute-start.4) | collective-permute-done | bytes 80 | tf_op jit(solution)/shard_map/ppermute | solution.py:146
  29.3 3.5 %collective-permute-done.5 = f32[12]{0:T(128)S(1)} collective-permute-done((f32[12]{0:T(128)S(1)}, f32[12]{0:T(128)S(1)}, u32[]{:S(2)}, u32[]{:S(2)}) %collective-permute-start.5) | collective-permute-done | bytes 80 | tf_op jit(solution)/shard_map/ppermute | solution.py:146
  32.9 0.7 pad_maximum_fusion.18
  33.6 1.0 broadcast_add_fusion
  34.5 1.7 %pad_maximum_fusion.2 = (f32[6,18,17,128]{3,2,1,0:T(8,128)}, f32[6,18,17,128]{3,2,1,0:T(8,128)}) fusion(f32[6,18,1,128]{3,2,1,0:T(1,128)S(1)} %get-tuple-element.70, f32[6,1,16,128]{3,2,1,0:T(8,128)S(1)} %collective-permute-done.6, f32[6,16,16,128]{3,2,1,0:T(8,128)S(1)} %convert_element_type.12, f32[6,1,16,128]{3,2,1,0:T(8,128)S(1)} %collective-permute-done.7, ...), kind=kLoop, calls=%fused_computation.5 | loop fusion | flops 1410048 | bytes 2875392 | tf_op jit(solution)/shard_map/concatenate | solution.py:36
  36.3 0.8 select_reduce_fusion.3
  37.1 0.8 copy.25
  38.5 1.7 %copy.26 = f32[6,18,18,1]{3,2,1,0:T(8,128)S(1)} copy(f32[6,18,18,1]{2,1,0,3:T(8,128)} %select_bitcast_fusion.2) | data formatting | bytes 15552 | tf_op jit(solution)/shard_map/jit(_where)/select_n | solution.py:23
  40.1 3.1 %pad_maximum_fusion = (f32[6,18,18,129]{3,2,1,0:T(8,128)S(1)}, f32[6,18,18,129]{3,2,1,0:T(8,128)S(1)}) fusion(f32[6,18,18,1]{3,2,1,0:T(8,128)S(1)} %copy.25, f32[6,18,1,128]{3,2,1,0:T(1,128)} %copy-done.17, f32[6,1,16,128]{3,2,1,0:T(8,128)S(1)} %collective-permute-done.6, f32[6,16,16,128]{3,2,1,0:T(8,128)S(1)} %convert_element_type.12, ...), kind=kLoop, calls=%fused_computation.1 | loop fusion | flops 2507760 | bytes 3017088 | tf_op jit(solution)/shard_map/concatenate | solution.py:36
  45.6 0.7 fusion.82
  48.5 0.7 copy-done.10
  49.3 0.8 multiply_reduce_fusion
  50.1 1.3 %collective-permute-start.10 = (f32[6,1,16,128]{3,2,1,0:T(8,128)S(1)}, f32[6,1,16,128]{3,2,1,0:T(8,128)S(1)}, u32[]{:S(2)}, u32[]{:S(2)}) collective-permute-start(f32[6,1,16,128]{3,2,1,0:T(8,128)S(1)} %get-tuple-element.61), channel_id=1, source_target_pairs={{4,0},{8,4},{12,8},{5,1},{9,5},{13,9},{6,2},{10,6},{14,10},{7,3},{... | collective-permute-start | bytes 147464 | tf_op jit(solution)/shard_map/ppermute | solution.py:35
  51.4 4.7 %collective-permute-start.11 = (f32[6,1,16,128]{3,2,1,0:T(8,128)S(1)}, f32[6,1,16,128]{3,2,1,0:T(8,128)S(1)}, u32[]{:S(2)}, u32[]{:S(2)}) collective-permute-start(f32[6,1,16,128]{3,2,1,0:T(8,128)S(1)} %get-tuple-element.60), channel_id=1, source_target_pairs={{0,4},{4,8},{8,12},{1,5},{5,9},{9,13},{2,6},{6,10},{10,14},{3,7},{... | collective-permute-start | bytes 147464 | tf_op jit(solution)/shard_map/ppermute | solution.py:34
  56.1 1.5 %collective-permute-done.11 = f32[6,1,16,128]{3,2,1,0:T(8,128)S(1)} collective-permute-done((f32[6,1,16,128]{3,2,1,0:T(8,128)S(1)}, f32[6,1,16,128]{3,2,1,0:T(8,128)S(1)}, u32[]{:S(2)}, u32[]{:S(2)}) %collective-permute-start.11) | collective-permute-done | bytes 49184 | tf_op jit(solution)/shard_map/ppermute | solution.py:34
  58.3 3.6 %collective-permute-done.12 = f32[6,18,1,128]{3,2,1,0:T(1,128)S(1)} collective-permute-done((f32[6,18,1,128]{3,2,1,0:T(1,128)S(1)}, f32[6,18,1,128]{3,2,1,0:T(1,128)S(1)}, u32[]{:S(2)}, u32[]{:S(2)}) %collective-permute-start.12) | collective-permute-done | bytes 55328 | tf_op jit(solution)/shard_map/ppermute | solution.py:27
  62.1 1.3 %pad_maximum_fusion.4 = f32[6,18,18,128]{3,2,1,0:T(8,128)} fusion(f32[6,18,1,128]{3,2,1,0:T(1,128)S(1)} %get-tuple-element.68, f32[6,1,16,128]{3,2,1,0:T(8,128)S(1)} %collective-permute-done.10, f32[6,16,16,128]{3,2,1,0:T(8,128)S(1)} %get-tuple-element.59, f32[6,1,16,128]{3,2,1,0:T(8,128)S(1)} %collective-permute-done.11, ...), kind=kLoop, calls=%fused_computation.10 | loop fusion | flops 995328 | bytes 1990656 | tf_op jit(solution)/shard_map/concatenate | solution.py:36
  63.4 1.0 convert_element_type.13
  65.6 1.7 %pad_maximum_fusion.3 = (f32[6,18,17,128]{3,2,1,0:T(8,128)}, f32[6,18,17,128]{3,2,1,0:T(8,128)}) fusion(f32[6,18,1,128]{3,2,1,0:T(1,128)S(1)} %get-tuple-element.68, f32[6,1,16,128]{3,2,1,0:T(8,128)S(1)} %collective-permute-done.10, f32[6,16,16,128]{3,2,1,0:T(8,128)S(1)} %get-tuple-element.59, f32[6,1,16,128]{3,2,1,0:T(8,128)S(1)} %collective-permute-done.11, ...), kind=kLoop, calls=%fused_computation.8 | loop fusion | flops 1410048 | bytes 2875392 | tf_op jit(solution)/shard_map/concatenate | solution.py:36
  67.3 1.4 %select_reduce_fusion.1 = (f32[6,18,18]{2,1,0:T(8,128)S(1)}, f32[6,18,18]{2,1,0:T(8,128)}) fusion(f32[6,18,18,128]{3,2,1,0:T(8,128)S(1)} %collective-permute-done.13, pred[128]{0:T(512)(128)(4,1)S(1)} %copy-done.52, pred[128]{0:T(512)(128)(4,1)S(1)} %copy-done.50), kind=kLoop, calls=%fused_computation.12 | loop fusion | flops 991440 | bytes 1011136 | tf_op jit(solution)/shard_map/reduce_sum | solution.py:21
  68.8 0.8 copy.27
  70.3 1.7 %copy.28 = f32[6,18,18,1]{3,2,1,0:T(8,128)S(1)} copy(f32[6,18,18,1]{2,1,0,3:T(8,128)} %select_bitcast_fusion) | data formatting | bytes 15552 | tf_op jit(solution)/shard_map/jit(_where)/select_n | solution.py:23
  71.9 3.1 %pad_maximum_fusion.1 = (f32[6,18,18,129]{3,2,1,0:T(8,128)S(1)}, f32[6,18,18,129]{3,2,1,0:T(8,128)S(1)}) fusion(f32[6,18,18,1]{3,2,1,0:T(8,128)S(1)} %copy.27, f32[6,18,1,128]{3,2,1,0:T(1,128)} %copy-done.21, f32[6,1,16,128]{3,2,1,0:T(8,128)S(1)} %collective-permute-done.10, f32[6,16,16,128]{3,2,1,0:T(8,128)S(1)} %get-tuple-element.59, ...), kind=kLoop, calls=%fused_computation.3 | loop fusion | flops 2507760 | bytes 3017088 | tf_op jit(solution)/shard_map/concatenate | solution.py:36
  79.7 0.8 copy-done.8
  82.4 2.3 %collective-permute-start.15 = (f32[902]{0:T(1024)S(1)}, f32[902]{0:T(1024)S(1)}, u32[]{:S(2)}, u32[]{:S(2)}) collective-permute-start(f32[902]{0:T(1024)S(1)} %pad_maximum_fusion.16), channel_id=1, source_target_pairs={{0,2},{1,3},{2,0},{3,1},{4,6},{5,7},{6,4},{7,5},{8,10},{9,11},{10,... | collective-permute-start | bytes 10832 | tf_op jit(solution)/shard_map/ppermute | solution.py:146
  84.7 1.6 %collective-permute-done.15 = f32[902]{0:T(1024)S(1)} collective-permute-done((f32[902]{0:T(1024)S(1)}, f32[902]{0:T(1024)S(1)}, u32[]{:S(2)}, u32[]{:S(2)}) %collective-permute-start.15) | collective-permute-done | bytes 3640 | tf_op jit(solution)/shard_map/ppermute | solution.py:146
  86.3 1.5 %collective-permute-done.16 = f32[902]{0:T(1024)S(1)} collective-permute-done((f32[902]{0:T(1024)S(1)}, f32[902]{0:T(1024)S(1)}, u32[]{:S(2)}, u32[]{:S(2)}) %collective-permute-start.16) | collective-permute-done | bytes 3640 | tf_op jit(solution)/shard_map/ppermute | solution.py:146
  87.7 2.3 %collective-permute-start.17 = (f32[902]{0:T(1024)S(1)}, f32[902]{0:T(1024)S(1)}, u32[]{:S(2)}, u32[]{:S(2)}) collective-permute-start(f32[902]{0:T(1024)S(1)} %add_add_fusion.3), channel_id=1, source_target_pairs={{0,4},{1,5},{2,6},{3,7},{4,0},{5,1},{6,2},{7,3},{8,12},{9,13},{10,... | collective-permute-start | bytes 10832 | tf_op jit(solution)/shard_map/ppermute | solution.py:146
  90.1 2.4 %collective-permute-start.19 = (f32[902]{0:T(1024)S(1)}, f32[902]{0:T(1024)S(1)}, u32[]{:S(2)}, u32[]{:S(2)}) collective-permute-start(f32[902]{0:T(1024)S(1)} %add_add_fusion.3), channel_id=1, source_target_pairs={{0,12},{1,13},{2,14},{3,15},{4,8},{5,9},{6,10},{7,11},{8,4},{9,5},... | collective-permute-start | bytes 10832 | tf_op jit(solution)/shard_map/ppermute | solution.py:146
  92.5 2.1 %collective-permute-done.18 = f32[902]{0:T(1024)S(1)} collective-permute-done((f32[902]{0:T(1024)S(1)}, f32[902]{0:T(1024)S(1)}, u32[]{:S(2)}, u32[]{:S(2)}) %collective-permute-start.18) | collective-permute-done | bytes 3640 | tf_op jit(solution)/shard_map/ppermute | solution.py:146
  94.6 0.9 collective-permute-done.19
  96.2 0.7 copy.29
  97.0 1.1 %fusion.13 = f32[6,16,16,128]{3,2,1,0:T(8,128)} fusion(f32[3,16,16,128]{3,2,1,0:T(8,128)S(1)} %copy-done.14, f32[3,16,16,128]{3,2,1,0:T(8,128)S(1)} %copy-done.11, f32[3,16,16,128]{3,2,1,0:T(8,128)S(1)} %get-tuple-element.26, f32[3,16,16,128]{3,2,1,0:T(8,128)S(1)} %get-tuple-element.25, f32[6]{0:T(128)S(1)} %pad_maximum_fusion.19, f32[6]{0:T(128)S(1)} %maximum_multiply_fusion), kind=kLoop, calls=%fused_computation.38 | loop fusion | flops 1376256 | bytes 2359344 | tf_op jit(solution)/shard_map/add | solution.py:132
  (204 shorter events, 17.2 us)
Async XLA Ops:
  0.6 5.5 %copy-start.54 = (s32[2,2,4]{2,1,0:T(2,128)S(1)}, s32[2,2,4]{2,1,0:T(2,128)}, u32[]{:S(2)}) copy-start(s32[2,2,4]{2,1,0:T(2,128)} %param.13) | copy-start | bytes 196
  0.6 6.5 %copy-start.45 = (bf16[16,16,128]{2,1,0:T(8,128)(2,1)S(1)}, bf16[16,16,128]{2,1,0:T(8,128)(2,1)}, u32[]{:S(2)}) copy-start(bf16[16,16,128]{2,1,0:T(8,128)(2,1)} %param.12) | copy-start | bytes 196612
  4.2 5.4 %copy-start.4 = (f32[32768]{0:T(1024)}, f32[32768]{0:T(1024)S(1)}, u32[]{:S(2)}) copy-start(f32[32768]{0:T(1024)S(1)} %scatter_custom_fusion) | copy-start | bytes 393220
  6.1 3.2 %copy-start.7 = (f32[6,16,16,128]{3,2,1,0:T(8,128)}, f32[6,16,16,128]{3,2,1,0:T(8,128)S(1)}, u32[]{:S(2)}) copy-start(f32[6,16,16,128]{3,2,1,0:T(8,128)S(1)} %convert_element_type.15) | copy-start | bytes 2359300
  7.8 1.7 %copy-start.23 = (bf16[6,16,16,128]{3,2,1,0:T(8,128)(2,1)S(1)}, bf16[6,16,16,128]{3,2,1,0:T(8,128)(2,1)}, u32[]{:S(2)}) copy-start(bf16[6,16,16,128]{3,2,1,0:T(8,128)(2,1)} %param.10) | copy-start | bytes 1179652
  9.3 9.5 %copy-start.9 = (f32[3,16,16,128]{3,2,1,0:T(8,128)}, f32[3,16,16,128]{3,2,1,0:T(8,128)S(1)}, u32[]{:S(2)}) copy-start(f32[3,16,16,128]{3,2,1,0:T(8,128)S(1)} %get-tuple-element.30) | copy-start | bytes 1179652
  9.3 9.5 %copy-start.12 = (f32[3,16,16,128]{3,2,1,0:T(8,128)}, f32[3,16,16,128]{3,2,1,0:T(8,128)S(1)}, u32[]{:S(2)}) copy-start(f32[3,16,16,128]{3,2,1,0:T(8,128)S(1)} %get-tuple-element.31) | copy-start | bytes 1179652
  9.9 12.6 %collective-permute-start = (f32[12]{0:T(128)S(1)}, f32[12]{0:T(128)S(1)}, u32[]{:S(2)}, u32[]{:S(2)}) collective-permute-start(f32[12]{0:T(128)S(1)} %pad_maximum_fusion.17), channel_id=1, source_target_pairs={{0,1},{1,0},{2,3},{3,2},{4,5},{5,4},{6,7},{7,6},{8,9},{9,8},{10,11... | collective-permute-start | bytes 152 | tf_op jit(solution)/shard_map/ppermute | solution.py:146
  10.3 12.1 %collective-permute-start.1 = (f32[12]{0:T(128)S(1)}, f32[12]{0:T(128)S(1)}, u32[]{:S(2)}, u32[]{:S(2)}) collective-permute-start(f32[12]{0:T(128)S(1)} %pad_maximum_fusion.17), channel_id=1, source_target_pairs={{0,2},{1,3},{2,0},{3,1},{4,6},{5,7},{6,4},{7,5},{8,10},{9,11},{10,... | collective-permute-start | bytes 152 | tf_op jit(solution)/shard_map/ppermute | solution.py:146
  12.9 9.5 %collective-permute-start.2 = (f32[12]{0:T(128)S(1)}, f32[12]{0:T(128)S(1)}, u32[]{:S(2)}, u32[]{:S(2)}) collective-permute-start(f32[12]{0:T(128)S(1)} %pad_maximum_fusion.17), channel_id=1, source_target_pairs={{0,3},{1,2},{2,1},{3,0},{4,7},{5,6},{6,5},{7,4},{8,11},{9,10},{10,... | collective-permute-start | bytes 152 | tf_op jit(solution)/shard_map/ppermute | solution.py:146
  13.0 6.0 %collective-permute-start.6 = (f32[6,1,16,128]{3,2,1,0:T(8,128)S(1)}, f32[6,1,16,128]{3,2,1,0:T(8,128)S(1)}, u32[]{:S(2)}, u32[]{:S(2)}) collective-permute-start(f32[6,1,16,128]{3,2,1,0:T(8,128)S(1)} %get-tuple-element.63), channel_id=1, source_target_pairs={{4,0},{8,4},{12,8},{5,1},{9,5},{13,9},{6,2},{10,6},{14,10},{7,3},{... | collective-permute-start | bytes 147464 | tf_op jit(solution)/shard_map/ppermute | solution.py:35
  14.3 6.3 %collective-permute-start.7 = (f32[6,1,16,128]{3,2,1,0:T(8,128)S(1)}, f32[6,1,16,128]{3,2,1,0:T(8,128)S(1)}, u32[]{:S(2)}, u32[]{:S(2)}) collective-permute-start(f32[6,1,16,128]{3,2,1,0:T(8,128)S(1)} %get-tuple-element.62), channel_id=1, source_target_pairs={{0,4},{4,8},{8,12},{1,5},{5,9},{9,13},{2,6},{6,10},{10,14},{3,7},{... | collective-permute-start | bytes 147464 | tf_op jit(solution)/shard_map/ppermute | solution.py:34
  18.9 17.4 %copy-start.49 = (pred[128]{0:T(512)(128)(4,1)}, pred[128]{0:T(512)(128)(4,1)S(1)}, u32[]{:S(2)}) copy-start(pred[128]{0:T(512)(128)(4,1)S(1)} %get-tuple-element.92) | copy-start | bytes 388
  18.9 17.4 %copy-start.51 = (pred[128]{0:T(512)(128)(4,1)}, pred[128]{0:T(512)(128)(4,1)S(1)}, u32[]{:S(2)}) copy-start(pred[128]{0:T(512)(128)(4,1)S(1)} %get-tuple-element.93) | copy-start | bytes 388
  20.6 13.0 %copy-start.40 = (bf16[6,16,16,128]{3,2,1,0:T(8,128)(2,1)S(1)}, bf16[6,16,16,128]{3,2,1,0:T(8,128)(2,1)}, u32[]{:S(2)}) copy-start(bf16[6,16,16,128]{3,2,1,0:T(8,128)(2,1)} %param.9) | copy-start | bytes 1179652
  20.6 6.9 %collective-permute-start.8 = (f32[6,18,1,128]{3,2,1,0:T(1,128)S(1)}, f32[6,18,1,128]{3,2,1,0:T(1,128)S(1)}, u32[]{:S(2)}, u32[]{:S(2)}) collective-permute-start(f32[6,18,1,128]{3,2,1,0:T(1,128)S(1)} %broadcast_select_fusion.5), channel_id=1, source_target_pairs={{0,2},{2,0},{1,3},{3,1},{4,6},{6,4},{5,7},{7,5},{8,10},{10,8},{9,1... | collective-permute-start | bytes 165896 | tf_op jit(solution)/shard_map/ppermute | solution.py:27
  22.4 5.5 %collective-permute-start.3 = (f32[12]{0:T(128)S(1)}, f32[12]{0:T(128)S(1)}, u32[]{:S(2)}, u32[]{:S(2)}) collective-permute-start(f32[12]{0:T(128)S(1)} %add_add_fusion.6), channel_id=1, source_target_pairs={{0,4},{1,5},{2,6},{3,7},{4,0},{5,1},{6,2},{7,3},{8,12},{9,13},{10,... | collective-permute-start | bytes 152 | tf_op jit(solution)/shard_map/ppermute | solution.py:146
  24.9 4.4 %collective-permute-start.4 = (f32[12]{0:T(128)S(1)}, f32[12]{0:T(128)S(1)}, u32[]{:S(2)}, u32[]{:S(2)}) collective-permute-start(f32[12]{0:T(128)S(1)} %add_add_fusion.6), channel_id=1, source_target_pairs={{0,8},{1,9},{2,10},{3,11},{4,12},{5,13},{6,14},{7,15},{8,0},{9,1},... | collective-permute-start | bytes 152 | tf_op jit(solution)/shard_map/ppermute | solution.py:146
  27.4 5.3 %collective-permute-start.5 = (f32[12]{0:T(128)S(1)}, f32[12]{0:T(128)S(1)}, u32[]{:S(2)}, u32[]{:S(2)}) collective-permute-start(f32[12]{0:T(128)S(1)} %add_add_fusion.6), channel_id=1, source_target_pairs={{0,12},{1,13},{2,14},{3,15},{4,8},{5,9},{6,10},{7,11},{8,4},{9,5},... | collective-permute-start | bytes 152 | tf_op jit(solution)/shard_map/ppermute | solution.py:146
  27.6 7.0 %copy-start.15 = (f32[6,18,1,128]{3,2,1,0:T(1,128)}, f32[6,18,1,128]{3,2,1,0:T(1,128)S(1)}, u32[]{:S(2)}) copy-start(f32[6,18,1,128]{3,2,1,0:T(1,128)S(1)} %get-tuple-element.69) | copy-start | bytes 165892
  27.6 7.0 %copy-start.17 = (f32[6,18,1,128]{3,2,1,0:T(1,128)}, f32[6,18,1,128]{3,2,1,0:T(1,128)S(1)}, u32[]{:S(2)}) copy-start(f32[6,18,1,128]{3,2,1,0:T(1,128)S(1)} %get-tuple-element.70) | copy-start | bytes 165892
  27.8 8.4 %collective-permute-start.9 = (f32[6,18,18,128]{3,2,1,0:T(8,128)S(1)}, f32[6,18,18,128]{3,2,1,0:T(8,128)S(1)}, u32[]{:S(2)}, u32[]{:S(2)}) collective-permute-start(f32[6,18,18,128]{3,2,1,0:T(8,128)S(1)} %maximum_add_fusion), channel_id=1, source_target_pairs={{0,1},{1,0},{2,3},{3,2},{4,5},{5,4},{6,7},{7,6},{8,9},{9,8},{10,11... | collective-permute-start | bytes 2985992 | tf_op jit(solution)/shard_map/ppermute | solution.py:18
  32.8 3.5 %copy-start.47 = (f32[12]{0:T(128)}, f32[12]{0:T(128)S(1)}, u32[]{:S(2)}) copy-start(f32[12]{0:T(128)S(1)} %add_add_fusion.5) | copy-start | bytes 148
  40.1 3.1 %copy-start.24 = (bf16[6,16,16,128]{3,2,1,0:T(8,128)(2,1)S(1)}, bf16[6,16,16,128]{3,2,1,0:T(8,128)(2,1)}, u32[]{:S(2)}) copy-start(bf16[6,16,16,128]{3,2,1,0:T(8,128)(2,1)} %param.10) | copy-start | bytes 1179652
  40.1 3.1 %copy-start.27 = (f32[6,18,17,128]{3,2,1,0:T(8,128)S(1)}, f32[6,18,17,128]{3,2,1,0:T(8,128)}, u32[]{:S(2)}) copy-start(f32[6,18,17,128]{3,2,1,0:T(8,128)} %get-tuple-element.56) | copy-start | bytes 2820100
  40.1 3.1 %copy-start.28 = (f32[6,18,17,128]{3,2,1,0:T(8,128)S(1)}, f32[6,18,17,128]{3,2,1,0:T(8,128)}, u32[]{:S(2)}) copy-start(f32[6,18,17,128]{3,2,1,0:T(8,128)} %get-tuple-element.57) | copy-start | bytes 2820100
  43.9 2.3 %copy-start = (f32[2,8,2,8,128]{4,3,2,1,0:T(8,128)}, f32[2,8,2,8,128]{4,3,2,1,0:T(8,128)S(1)}, u32[]{:S(2)}) copy-start(f32[2,8,2,8,128]{4,3,2,1,0:T(8,128)S(1)} %broadcast_in_dim.196) | copy-start | bytes 393220
  44.5 1.8 %copy-start.2 = (f32[1,16,16,128]{3,2,1,0:T(8,128)}, f32[1,16,16,128]{3,2,1,0:T(8,128)S(1)}, u32[]{:S(2)}) copy-start(f32[1,16,16,128]{3,2,1,0:T(8,128)S(1)} %get-tuple-element.40) | copy-start | bytes 393220
  50.1 6.0 %collective-permute-start.10 = (f32[6,1,16,128]{3,2,1,0:T(8,128)S(1)}, f32[6,1,16,128]{3,2,1,0:T(8,128)S(1)}, u32[]{:S(2)}, u32[]{:S(2)}) collective-permute-start(f32[6,1,16,128]{3,2,1,0:T(8,128)S(1)} %get-tuple-element.61), channel_id=1, source_target_pairs={{4,0},{8,4},{12,8},{5,1},{9,5},{13,9},{6,2},{10,6},{14,10},{7,3},{... | collective-permute-start | bytes 147464 | tf_op jit(solution)/shard_map/ppermute | solution.py:35
  51.4 6.3 %collective-permute-start.11 = (f32[6,1,16,128]{3,2,1,0:T(8,128)S(1)}, f32[6,1,16,128]{3,2,1,0:T(8,128)S(1)}, u32[]{:S(2)}, u32[]{:S(2)}) collective-permute-start(f32[6,1,16,128]{3,2,1,0:T(8,128)S(1)} %get-tuple-element.60), channel_id=1, source_target_pairs={{0,4},{4,8},{8,12},{1,5},{5,9},{9,13},{2,6},{6,10},{10,14},{3,7},{... | collective-permute-start | bytes 147464 | tf_op jit(solution)/shard_map/ppermute | solution.py:34
  57.7 5.6 %copy-start.41 = (bf16[6,16,16,128]{3,2,1,0:T(8,128)(2,1)S(1)}, bf16[6,16,16,128]{3,2,1,0:T(8,128)(2,1)}, u32[]{:S(2)}) copy-start(bf16[6,16,16,128]{3,2,1,0:T(8,128)(2,1)} %param.9) | copy-start | bytes 1179652
  57.7 4.2 %collective-permute-start.12 = (f32[6,18,1,128]{3,2,1,0:T(1,128)S(1)}, f32[6,18,1,128]{3,2,1,0:T(1,128)S(1)}, u32[]{:S(2)}, u32[]{:S(2)}) collective-permute-start(f32[6,18,1,128]{3,2,1,0:T(1,128)S(1)} %broadcast_select_fusion.2), channel_id=1, source_target_pairs={{0,2},{2,0},{1,3},{3,1},{4,6},{6,4},{5,7},{7,5},{8,10},{10,8},{9,1... | collective-permute-start | bytes 165896 | tf_op jit(solution)/shard_map/ppermute | solution.py:27
  62.0 3.5 %copy-start.19 = (f32[6,18,1,128]{3,2,1,0:T(1,128)}, f32[6,18,1,128]{3,2,1,0:T(1,128)S(1)}, u32[]{:S(2)}) copy-start(f32[6,18,1,128]{3,2,1,0:T(1,128)S(1)} %get-tuple-element.67) | copy-start | bytes 165892
  62.0 3.5 %copy-start.21 = (f32[6,18,1,128]{3,2,1,0:T(1,128)}, f32[6,18,1,128]{3,2,1,0:T(1,128)S(1)}, u32[]{:S(2)}) copy-start(f32[6,18,1,128]{3,2,1,0:T(1,128)S(1)} %get-tuple-element.68) | copy-start | bytes 165892
  62.1 2.3 %copy-start.38 = (f32[3,16,16,128]{3,2,1,0:T(8,128)S(1)}, f32[3,16,16,128]{3,2,1,0:T(8,128)}, u32[]{:S(2)}) copy-start(f32[3,16,16,128]{3,2,1,0:T(8,128)} %get-tuple-element.28) | copy-start | bytes 1179652
  62.1 2.3 %copy-start.39 = (f32[3,16,16,128]{3,2,1,0:T(8,128)S(1)}, f32[3,16,16,128]{3,2,1,0:T(8,128)}, u32[]{:S(2)}) copy-start(f32[3,16,16,128]{3,2,1,0:T(8,128)} %get-tuple-element.29) | copy-start | bytes 1179652
  63.4 4.0 %collective-permute-start.13 = (f32[6,18,18,128]{3,2,1,0:T(8,128)}, f32[6,18,18,128]{3,2,1,0:T(8,128)S(1)}, u32[]{:S(2)}, u32[]{:S(2)}) collective-permute-start(f32[6,18,18,128]{3,2,1,0:T(8,128)} %pad_maximum_fusion.4), channel_id=1, source_target_pairs={{0,1},{1,0},{2,3},{3,2},{4,5},{5,4},{6,7},{7,6},{8,9},{9,8},{10,11... | collective-permute-start | bytes 2985992 | tf_op jit(solution)/shard_map/ppermute | solution.py:18
  71.9 3.1 %copy-start.25 = (f32[6,18,17,128]{3,2,1,0:T(8,128)S(1)}, f32[6,18,17,128]{3,2,1,0:T(8,128)}, u32[]{:S(2)}) copy-start(f32[6,18,17,128]{3,2,1,0:T(8,128)} %get-tuple-element.54) | copy-start | bytes 2820100
  71.9 3.1 %copy-start.26 = (f32[6,18,17,128]{3,2,1,0:T(8,128)S(1)}, f32[6,18,17,128]{3,2,1,0:T(8,128)}, u32[]{:S(2)}) copy-start(f32[6,18,17,128]{3,2,1,0:T(8,128)} %get-tuple-element.55) | copy-start | bytes 2820100
  80.6 15.0 %copy-start.48 = (f32[12]{0:T(128)S(1)}, f32[12]{0:T(128)}, u32[]{:S(2)}) copy-start(f32[12]{0:T(128)} %copy-done.47) | copy-start | bytes 148
  80.6 16.4 %copy-start.11 = (f32[3,16,16,128]{3,2,1,0:T(8,128)S(1)}, f32[3,16,16,128]{3,2,1,0:T(8,128)}, u32[]{:S(2)}) copy-start(f32[3,16,16,128]{3,2,1,0:T(8,128)} %copy-done.9) | copy-start | bytes 1179652
  80.6 16.4 %copy-start.14 = (f32[3,16,16,128]{3,2,1,0:T(8,128)S(1)}, f32[3,16,16,128]{3,2,1,0:T(8,128)}, u32[]{:S(2)}) copy-start(f32[3,16,16,128]{3,2,1,0:T(8,128)} %copy-done.12) | copy-start | bytes 1179652
  81.8 2.8 %collective-permute-start.14 = (f32[902]{0:T(1024)S(1)}, f32[902]{0:T(1024)S(1)}, u32[]{:S(2)}, u32[]{:S(2)}) collective-permute-start(f32[902]{0:T(1024)S(1)} %pad_maximum_fusion.16), channel_id=1, source_target_pairs={{0,1},{1,0},{2,3},{3,2},{4,5},{5,4},{6,7},{7,6},{8,9},{9,8},{10,11... | collective-permute-start | bytes 10832 | tf_op jit(solution)/shard_map/ppermute | solution.py:146
  82.4 3.9 %collective-permute-start.15 = (f32[902]{0:T(1024)S(1)}, f32[902]{0:T(1024)S(1)}, u32[]{:S(2)}, u32[]{:S(2)}) collective-permute-start(f32[902]{0:T(1024)S(1)} %pad_maximum_fusion.16), channel_id=1, source_target_pairs={{0,2},{1,3},{2,0},{3,1},{4,6},{5,7},{6,4},{7,5},{8,10},{9,11},{10,... | collective-permute-start | bytes 10832 | tf_op jit(solution)/shard_map/ppermute | solution.py:146
  84.7 3.1 %collective-permute-start.16 = (f32[902]{0:T(1024)S(1)}, f32[902]{0:T(1024)S(1)}, u32[]{:S(2)}, u32[]{:S(2)}) collective-permute-start(f32[902]{0:T(1024)S(1)} %pad_maximum_fusion.16), channel_id=1, source_target_pairs={{0,3},{1,2},{2,1},{3,0},{4,7},{5,6},{6,5},{7,4},{8,11},{9,10},{10,... | collective-permute-start | bytes 10832 | tf_op jit(solution)/shard_map/ppermute | solution.py:146
  87.7 4.8 %collective-permute-start.17 = (f32[902]{0:T(1024)S(1)}, f32[902]{0:T(1024)S(1)}, u32[]{:S(2)}, u32[]{:S(2)}) collective-permute-start(f32[902]{0:T(1024)S(1)} %add_add_fusion.3), channel_id=1, source_target_pairs={{0,4},{1,5},{2,6},{3,7},{4,0},{5,1},{6,2},{7,3},{8,12},{9,13},{10,... | collective-permute-start | bytes 10832 | tf_op jit(solution)/shard_map/ppermute | solution.py:146
  90.1 4.5 %collective-permute-start.18 = (f32[902]{0:T(1024)S(1)}, f32[902]{0:T(1024)S(1)}, u32[]{:S(2)}, u32[]{:S(2)}) collective-permute-start(f32[902]{0:T(1024)S(1)} %add_add_fusion.3), channel_id=1, source_target_pairs={{0,8},{1,9},{2,10},{3,11},{4,12},{5,13},{6,14},{7,15},{8,0},{9,1},... | collective-permute-start | bytes 10832 | tf_op jit(solution)/shard_map/ppermute | solution.py:146
  90.1 5.4 %collective-permute-start.19 = (f32[902]{0:T(1024)S(1)}, f32[902]{0:T(1024)S(1)}, u32[]{:S(2)}, u32[]{:S(2)}) collective-permute-start(f32[902]{0:T(1024)S(1)} %add_add_fusion.3), channel_id=1, source_target_pairs={{0,12},{1,13},{2,14},{3,15},{4,8},{5,9},{6,10},{7,11},{8,4},{9,5},... | collective-permute-start | bytes 10832 | tf_op jit(solution)/shard_map/ppermute | solution.py:146
  (28 other events, 31.1 us)

commit v17 on v12

--- a/solution.py
+++ b/solution.py
@@ -221,16 +221,12 @@
         jnp.concatenate(
             [
                 jnp.sum(mask * field, axis=(1, 2, 3)),
-                jnp.sum(gain_real, axis=(1, 2, 3)),
-                jnp.sum(gain_imag, axis=(1, 2, 3)),
             ]
         ),
         axes,
     )
     first = rounds[-1]
     mean_field = first[:6] / count
-    gain_total_real = first[6:9]
-    gain_total_imag = first[9:12]
     sweep_args = (lame_first, shear, density_cells, mask, source_cells, omega_sq, impedance)
     padded = with_halo(field, (("gx", 1), ("gy", 2)), 1)
     padded = with_halo(padded, (("col", 3),), 1, 0.0 * rounds[0][0])
@@ -247,10 +243,21 @@
     )
     cell_terms = -omega_sq * jnp.sum(correlation, axis=0)
     last = group_sum(
-        jnp.concatenate([second_local, block_sums(cell_terms).reshape(-1), response.reshape(-1)]),
+        jnp.concatenate(
+            [
+                second_local,
+                jnp.sum(gain_real, axis=(1, 2, 3)),
+                jnp.sum(gain_imag, axis=(1, 2, 3)),
+                block_sums(cell_terms).reshape(-1),
+                response.reshape(-1),
+            ]
+        ),
         axes,
     )
     second = last[:6]
+    gain_total_real = last[6:9]
+    gain_total_imag = last[9:12]
+    last = last[6:]
     grid_size = grid_shape[0] * grid_shape[1]
     response = last[6 + grid_size :].reshape(response.shape)
     mean_real = mean_field[:3]

time: 87.4 us -> 95.9 us (1.097)
  other arithmetic: 30.4 us -> 36.9 us
  starting transfers between devices: 29.3 us -> 31 us
    ppermute x12, starting transfers between devices: 13.8 us -> 15.8 us  [group_rounds(): lax.ppermute(value, axes, [(i, i ^ m * stride) for i in range(size)])]
    ppermute x2, waiting for transfers between devices: 3.5 us -> 5.03 us  [with_halo(): got = lax.ppermute(jnp.where(first, last, initial), axis, [(0, 1), (1, 0)])]
    ppermute x12, waiting for transfers between devices: 11 us -> 9.87 us  [group_rounds(): lax.ppermute(value, axes, [(i, i ^ m * stride) for i in range(size)])]
    add x1, other arithmetic: 0.24 us -> 1.32 us  [with_halo(): sent = array if tie is None else array + tie]
    ppermute x2, starting transfers between devices: 10.3 us -> 9.28 us  [with_halo(): before = lax.ppermute(last, axis, up)]
    convert_element_type x1, other arithmetic: 0.07 us -> 1.06 us  [shards(): forward_cells = forward.astype(jnp.float32)]
    add x1, other arithmetic: 0.07 us -> 1.06 us  [shards(): tied_source = source_cells + 0.0 * first[0]]
  transfers between devices with their start and end apart: 20 -> 20, of which waited for: 9 -> 9; matrix products, arithmetic and copies ran while one was open for 18% -> 16% of each run, Pallas kernels for 0% -> 0%
where the time goes in v17:
time: 95.9 us; the launch traced here: 95.1 us
  other arithmetic  36.9 us (38%)
  starting transfers between devices  31 us (32%)
  waiting for transfers between devices  16.5 us (17%)
  local copies, waits for them, and re-layouts  8.76 us (9%)
  between operations  1.97 us (2%)
    ppermute x12, starting transfers between devices, group_rounds(): lax.ppermute(value, axes, [(i, i ^ m * stride) for i in range(size)])  15.8 us
    ppermute x12, waiting for transfers between devices, group_rounds(): lax.ppermute(value, axes, [(i, i ^ m * stride) for i in range(size)])  9.87 us
    ppermute x2, starting transfers between devices, with_halo(): before = lax.ppermute(last, axis, up)  9.28 us
    concatenate x5, other arithmetic, with_halo(): array = jnp.concatenate([before, array, after], axis=dim)  5.96 us
    add x12, other arithmetic, navier(): result.append(shear * laplace[channel] + (lame_first + shear) * divergence)  5.61 us
    ppermute x2, waiting for transfers between devices, with_halo(): got = lax.ppermute(jnp.where(first, last, initial), axis, [(0, 1), (1, 0)])  5.03 us
    ppermute x2, starting transfers between devices, with_halo(): got = lax.ppermute(jnp.where(first, last, initial), axis, [(0, 1), (1, 0)])  3.35 us
    select_n x2, other arithmetic, with_halo(): after = jnp.where(first, got_initial, zero)  2.6 us
  transfers between devices with their start and end apart: 20, of which 9 were waited for; matrix products, arithmetic and copies ran while one was open for 16% of the time, Pallas kernels for 0%

profile of v17, /device:TPU:0, one launch (start us, length us, event | category | flops | bytes accessed | tf_op | source)
XLA Modules:
  0.0 95.1 jit_solution(11217103111596806929)
XLA Ops:
  0.6 0.7 compare_select_fusion
  1.4 1.5 %scatter_custom_fusion = f32[32768]{0:T(1024)S(1)} fusion(s32[256]{0:T(256)S(1)} %bitcast.45, f32[256]{0:T(256)S(1)} %broadcast.308, f32[]{:T(128)} %constant.28.clone.1), kind=kCustom, calls=%fused_computation.245 | custom fusion | bytes 131076 | tf_op jit(solution)/shard_map/scatter | solution.py:187
  2.8 1.2 %multiply_reduce_fusion.1 = f32[6]{0:T(128)S(1)} fusion(bf16[6,16,16,128]{3,2,1,0:T(8,128)(2,1)} %param.10, f32[16,16,128]{2,1,0:T(8,128)S(1)} %bitcast.35), kind=kLoop, calls=%fused_computation.46 | loop fusion | flops 589818 | bytes 524312 | tf_op jit(solution)/shard_map/reduce_sum | solution.py:223
  4.5 2.6 %collective-permute-start.1 = (f32[6]{0:T(128)S(1)}, f32[6]{0:T(128)S(1)}, u32[]{:S(2)}, u32[]{:S(2)}) collective-permute-start(f32[6]{0:T(128)S(1)} %multiply_reduce_fusion.1), channel_id=1, source_target_pairs={{0,2},{1,3},{2,0},{3,1},{4,6},{5,7},{6,4},{7,5},{8,10},{9,11},{10,... | collective-permute-start | bytes 80 | tf_op jit(solution)/shard_map/ppermute | solution.py:145
  7.1 0.8 fusion.107
  7.9 1.3 %collective-permute-start.6 = (f32[6,1,16,128]{3,2,1,0:T(8,128)S(1)}, f32[6,1,16,128]{3,2,1,0:T(8,128)S(1)}, u32[]{:S(2)}, u32[]{:S(2)}) collective-permute-start(f32[6,1,16,128]{3,2,1,0:T(8,128)S(1)} %get-tuple-element.66), channel_id=1, source_target_pairs={{4,0},{8,4},{12,8},{5,1},{9,5},{13,9},{6,2},{10,6},{14,10},{7,3},{... | collective-permute-start | bytes 147464 | tf_op jit(solution)/shard_map/ppermute | solution.py:34
  9.2 4.5 %collective-permute-start.7 = (f32[6,1,16,128]{3,2,1,0:T(8,128)S(1)}, f32[6,1,16,128]{3,2,1,0:T(8,128)S(1)}, u32[]{:S(2)}, u32[]{:S(2)}) collective-permute-start(f32[6,1,16,128]{3,2,1,0:T(8,128)S(1)} %get-tuple-element.65), channel_id=1, source_target_pairs={{0,4},{4,8},{8,12},{1,5},{5,9},{9,13},{2,6},{6,10},{10,14},{3,7},{... | collective-permute-start | bytes 147464 | tf_op jit(solution)/shard_map/ppermute | solution.py:33
  13.8 0.8 slice_bitcast_fusion.2
  15.2 0.8 select_reduce_fusion.1
  16.3 1.6 %convert_multiply_fusion = (f32[16,16,128]{2,1,0:T(8,128)}, f32[16,16,128]{2,1,0:T(8,128)}, f32[16,16,128]{2,1,0:T(8,128)}) fusion(bf16[16,16,128]{2,1,0:T(8,128)(2,1)} %param.12, f32[]{:T(128)} %bitcast.20, f32[16,16,128]{2,1,0:T(8,128)S(1)} %bitcast.43), kind=kLoop, calls=%fused_computation.236 | loop fusion | flops 131072 | bytes 589828 | tf_op jit(solution)/shard_map/mul | solution.py:93
  18.8 1.8 %collective-permute-start.8 = (f32[6,18,1,128]{3,2,1,0:T(1,128)S(1)}, f32[6,18,1,128]{3,2,1,0:T(1,128)S(1)}, u32[]{:S(2)}, u32[]{:S(2)}) collective-permute-start(f32[6,18,1,128]{3,2,1,0:T(1,128)S(1)} %broadcast_select_fusion.5), channel_id=1, source_target_pairs={{0,2},{2,0},{1,3},{3,1},{4,6},{6,4},{5,7},{7,5},{8,10},{10,8},{9,1... | collective-permute-start | bytes 165896 | tf_op jit(solution)/shard_map/ppermute | solution.py:26
  20.6 2.4 %collective-permute-done.8 = f32[6,18,1,128]{3,2,1,0:T(1,128)S(1)} collective-permute-done((f32[6,18,1,128]{3,2,1,0:T(1,128)S(1)}, f32[6,18,1,128]{3,2,1,0:T(1,128)S(1)}, u32[]{:S(2)}, u32[]{:S(2)}) %collective-permute-start.8) | collective-permute-done | bytes 55328 | tf_op jit(solution)/shard_map/ppermute | solution.py:26
  23.1 1.3 %maximum_add_fusion = f32[6,18,18,128]{3,2,1,0:T(8,128)} fusion(f32[6,18,1,128]{3,2,1,0:T(1,128)S(1)} %get-tuple-element.73, f32[6,1,16,128]{3,2,1,0:T(8,128)S(1)} %collective-permute-done.6, f32[6,16,16,128]{3,2,1,0:T(8,128)S(1)} %convert_element_type.12, f32[6,1,16,128]{3,2,1,0:T(8,128)S(1)} %collective-permute-done.7, ...), kind=kLoop, calls=%fused_computation.11 | loop fusion | flops 1244160 | bytes 1990660 | tf_op jit(solution)/shard_map/add | solution.py:17
  24.4 1.1 %convert_element_type.15 = f32[6,16,16,128]{3,2,1,0:T(8,128)S(1)} convert(bf16[6,16,16,128]{3,2,1,0:T(8,128)(2,1)} %param.11) | non-fusion elementwise | flops 196608 | bytes 1179648 | tf_op jit(solution)/shard_map/convert_element_type | solution.py:211
  25.5 1.9 %collective-permute-start.3 = (f32[6]{0:T(128)S(1)}, f32[6]{0:T(128)S(1)}, u32[]{:S(2)}, u32[]{:S(2)}) collective-permute-start(f32[6]{0:T(128)S(1)} %add_add_fusion.6), channel_id=1, source_target_pairs={{0,4},{1,5},{2,6},{3,7},{4,0},{5,1},{6,2},{7,3},{8,12},{9,13},{10,... | collective-permute-start | bytes 80 | tf_op jit(solution)/shard_map/ppermute | solution.py:145
  27.4 1.1 %collective-permute-start.4 = (f32[6]{0:T(128)S(1)}, f32[6]{0:T(128)S(1)}, u32[]{:S(2)}, u32[]{:S(2)}) collective-permute-start(f32[6]{0:T(128)S(1)} %add_add_fusion.6), channel_id=1, source_target_pairs={{0,8},{1,9},{2,10},{3,11},{4,12},{5,13},{6,14},{7,15},{8,0},{9,1},... | collective-permute-start | bytes 80 | tf_op jit(solution)/shard_map/ppermute | solution.py:145
  28.5 1.5 %collective-permute-start.5 = (f32[6]{0:T(128)S(1)}, f32[6]{0:T(128)S(1)}, u32[]{:S(2)}, u32[]{:S(2)}) collective-permute-start(f32[6]{0:T(128)S(1)} %add_add_fusion.6), channel_id=1, source_target_pairs={{0,12},{1,13},{2,14},{3,15},{4,8},{5,9},{6,10},{7,11},{8,4},{9,5},... | collective-permute-start | bytes 80 | tf_op jit(solution)/shard_map/ppermute | solution.py:145
  30.0 1.8 %collective-permute-done.4 = f32[6]{0:T(128)S(1)} collective-permute-done((f32[6]{0:T(128)S(1)}, f32[6]{0:T(128)S(1)}, u32[]{:S(2)}, u32[]{:S(2)}) %collective-permute-start.4) | collective-permute-done | bytes 56 | tf_op jit(solution)/shard_map/ppermute | solution.py:145
  31.8 2.0 %collective-permute-done.5 = f32[6]{0:T(128)S(1)} collective-permute-done((f32[6]{0:T(128)S(1)}, f32[6]{0:T(128)S(1)}, u32[]{:S(2)}, u32[]{:S(2)}) %collective-permute-start.5) | collective-permute-done | bytes 56 | tf_op jit(solution)/shard_map/ppermute | solution.py:145
  34.0 1.1 %broadcast_add_fusion = f32[6,16,16,128]{3,2,1,0:T(8,128)S(1)} fusion(f32[]{:T(128)} %bitcast.3, bf16[6,16,16,128]{3,2,1,0:T(8,128)(2,1)} %param.9), kind=kLoop, calls=%fused_computation.78 | loop fusion | flops 393216 | bytes 1179652 | tf_op jit(solution)/shard_map/add | solution.py:233
  35.8 2.1 %pad_maximum_fusion = (f32[6,18,18,129]{3,2,1,0:T(8,128)S(1)}, f32[6,18,18,129]{3,2,1,0:T(8,128)S(1)}) fusion(f32[6,18,18,1]{3,2,1,0:T(8,128)S(1)} %get-tuple-element.50, f32[6,18,1,128]{3,2,1,0:T(1,128)S(1)} %get-tuple-element.73, f32[6,1,16,128]{3,2,1,0:T(8,128)S(1)} %collective-permute-done.6, f32[6,16,16,128]{3,2,1,0:T(8,128)S(1)} %convert_element_type.12, ...), kind=kLoop, calls=%fused_computation.1 | loop fusion | flops 2507760 | bytes 3017088 | tf_op jit(solution)/shard_map/concatenate | solution.py:35
  42.7 1.5 %multiply_subtract_fusion = (f32[3,16,16,128]{3,2,1,0:T(8,128)}, f32[3,16,16,128]{3,2,1,0:T(8,128)}, f32[3,16,16,128]{3,2,1,0:T(8,128)}, f32[3,16,16,128]{3,2,1,...) fusion(f32[6,16,16,128]{3,2,1,0:T(8,128)S(1)} %convert_element_type.15, ...), kind=kLoop, calls=%fused_computation.64 | loop fusion | flops 2949120 | bytes 4849688 | tf_op jit(solution)/shard_map/sub | solution.py:216
  44.2 0.8 multiply_reduce_fusion
  45.1 1.3 %collective-permute-start.10 = (f32[6,1,16,128]{3,2,1,0:T(8,128)S(1)}, f32[6,1,16,128]{3,2,1,0:T(8,128)S(1)}, u32[]{:S(2)}, u32[]{:S(2)}) collective-permute-start(f32[6,1,16,128]{3,2,1,0:T(8,128)S(1)} %get-tuple-element.63), channel_id=1, source_target_pairs={{4,0},{8,4},{12,8},{5,1},{9,5},{13,9},{6,2},{10,6},{14,10},{7,3},{... | collective-permute-start | bytes 147464 | tf_op jit(solution)/shard_map/ppermute | solution.py:34
  46.3 4.7 %collective-permute-start.11 = (f32[6,1,16,128]{3,2,1,0:T(8,128)S(1)}, f32[6,1,16,128]{3,2,1,0:T(8,128)S(1)}, u32[]{:S(2)}, u32[]{:S(2)}) collective-permute-start(f32[6,1,16,128]{3,2,1,0:T(8,128)S(1)} %get-tuple-element.62), channel_id=1, source_target_pairs={{0,4},{4,8},{8,12},{1,5},{5,9},{9,13},{2,6},{6,10},{10,14},{3,7},{... | collective-permute-start | bytes 147464 | tf_op jit(solution)/shard_map/ppermute | solution.py:33
  51.1 1.5 %collective-permute-done.11 = f32[6,1,16,128]{3,2,1,0:T(8,128)S(1)} collective-permute-done((f32[6,1,16,128]{3,2,1,0:T(8,128)S(1)}, f32[6,1,16,128]{3,2,1,0:T(8,128)S(1)}, u32[]{:S(2)}, u32[]{:S(2)}) %collective-permute-start.11) | collective-permute-done | bytes 49184 | tf_op jit(solution)/shard_map/ppermute | solution.py:33
  52.7 1.6 %collective-permute-start.12 = (f32[6,18,1,128]{3,2,1,0:T(1,128)S(1)}, f32[6,18,1,128]{3,2,1,0:T(1,128)S(1)}, u32[]{:S(2)}, u32[]{:S(2)}) collective-permute-start(f32[6,18,1,128]{3,2,1,0:T(1,128)S(1)} %broadcast_select_fusion.2), channel_id=1, source_target_pairs={{0,2},{2,0},{1,3},{3,1},{4,6},{6,4},{5,7},{7,5},{8,10},{10,8},{9,1... | collective-permute-start | bytes 165896 | tf_op jit(solution)/shard_map/ppermute | solution.py:26
  54.3 2.7 %collective-permute-done.12 = f32[6,18,1,128]{3,2,1,0:T(1,128)S(1)} collective-permute-done((f32[6,18,1,128]{3,2,1,0:T(1,128)S(1)}, f32[6,18,1,128]{3,2,1,0:T(1,128)S(1)}, u32[]{:S(2)}, u32[]{:S(2)}) %collective-permute-start.12) | collective-permute-done | bytes 55328 | tf_op jit(solution)/shard_map/ppermute | solution.py:26
  57.0 1.3 %pad_maximum_fusion.4 = f32[6,18,18,128]{3,2,1,0:T(8,128)} fusion(f32[6,18,1,128]{3,2,1,0:T(1,128)S(1)} %get-tuple-element.71, f32[6,1,16,128]{3,2,1,0:T(8,128)S(1)} %collective-permute-done.10, f32[6,16,16,128]{3,2,1,0:T(8,128)S(1)} %get-tuple-element.61, f32[6,1,16,128]{3,2,1,0:T(8,128)S(1)} %collective-permute-done.11, ...), kind=kLoop, calls=%fused_computation.14 | loop fusion | flops 995328 | bytes 1990656 | tf_op jit(solution)/shard_map/concatenate | solution.py:35
  58.3 0.9 convert_element_type.13
  59.3 0.7 reduce_sum.108
  60.0 0.7 reduce_sum.109
  60.7 1.2 %multiply_add_fusion = f32[3,16,16,128]{3,2,1,0:T(8,128)S(1)} fusion(f32[3,16,16,128]{3,2,1,0:T(8,128)} %get-tuple-element.22, f32[3,16,16,128]{3,2,1,0:T(8,128)} %get-tuple-element.21), kind=kLoop, calls=%fused_computation.63 | loop fusion | flops 196608 | bytes 1179648 | tf_op jit(solution)/shard_map/add | solution.py:217
  61.9 0.9 maximum_reduce_fusion
  62.8 0.9 reduce_sum.115
  63.7 0.7 reduce_sum.116
  64.5 1.7 %dynamic_update_slice.7 = f32[6,16,8]{2,1,0:T(8,128)S(1)} dynamic-update-slice(f32[6,16,8]{2,1,0:T(8,128)S(1)} %broadcast_in_dim.188, f32[6,4,4]{2,1,0:T(4,128)} %reduce_sum.116, s32[]{:T(128)} %constant.29.clone.1, s32[]{:T(128)S(6)} %select_n.188, s32[]{:T(128)S(6)} %select_n.189) | dynamic-update-slice | bytes 772 | tf_op jit(solution)/shard_map/dynamic_update_slice | solution.py:209
  66.5 2.2 %slice_select_fusion.1 = (f32[6,18,18,1]{3,2,1,0:T(8,128)S(1)}, f32[6,18,18,1]{3,2,1,0:T(8,128)S(1)}) fusion(f32[6,18,18,128]{3,2,1,0:T(8,128)} %collective-permute-done.13, pred[]{:T(512)S(6)} %eq.67), kind=kLoop, calls=%fused_computation.6 | loop fusion | flops 3888 | bytes 31105 | tf_op jit(solution)/shard_map/jit(_where)/select_n | solution.py:23
  68.6 2.1 %pad_maximum_fusion.1 = (f32[6,18,18,129]{3,2,1,0:T(8,128)S(1)}, f32[6,18,18,129]{3,2,1,0:T(8,128)S(1)}) fusion(f32[6,18,18,1]{3,2,1,0:T(8,128)S(1)} %get-tuple-element.48, f32[6,18,1,128]{3,2,1,0:T(1,128)S(1)} %get-tuple-element.71, f32[6,1,16,128]{3,2,1,0:T(8,128)S(1)} %collective-permute-done.10, f32[6,16,16,128]{3,2,1,0:T(8,128)S(1)} %get-tuple-element.61, ...), kind=kLoop, calls=%fused_computation.3 | loop fusion | flops 2507760 | bytes 3017088 | tf_op jit(solution)/shard_map/concatenate | solution.py:35
  75.0 1.3 %subtract_reduce_fusion = (f32[16,16,128]{2,1,0:T(8,128)S(1)}, f32[3,16,16,128]{3,2,1,0:T(8,128)}, f32[3,16,16,128]{3,2,1,0:T(8,128)}) fusion(f32[6,16,16,128]{3,2,1,0:T(8,128)S(1)} %convert_element_type.15, f32[3,16,16,128]{3,2,1,0:T(8,128)S(1)} %get-tuple-element.47, f32[3]{0:T(128)S(1)} %copy-done.14, f32[16,16,128]{2,1,0:T(8,128)S(1)} %copy-done.4, ...), kind=kLoop, calls=%fused_computation.67 | loop fusion | flops 2719744 | bytes 3670040 | tf_op jit(solution)/shard_map/reduce_sum | solution.py:244
  77.7 2.9 %collective-permute-start.15 = (f32[908]{0:T(1024)S(1)}, f32[908]{0:T(1024)S(1)}, u32[]{:S(2)}, u32[]{:S(2)}) collective-permute-start(f32[908]{0:T(1024)S(1)} %concatenate.201), channel_id=1, source_target_pairs={{0,2},{1,3},{2,0},{3,1},{4,6},{5,7},{6,4},{7,5},{8,10},{9,11},{10,... | collective-permute-start | bytes 10904 | tf_op jit(solution)/shard_map/ppermute | solution.py:145
  80.6 1.6 %collective-permute-done.15 = f32[908]{0:T(1024)S(1)} collective-permute-done((f32[908]{0:T(1024)S(1)}, f32[908]{0:T(1024)S(1)}, u32[]{:S(2)}, u32[]{:S(2)}) %collective-permute-start.15) | collective-permute-done | bytes 3664 | tf_op jit(solution)/shard_map/ppermute | solution.py:145
  82.2 1.5 %collective-permute-done.16 = f32[908]{0:T(1024)S(1)} collective-permute-done((f32[908]{0:T(1024)S(1)}, f32[908]{0:T(1024)S(1)}, u32[]{:S(2)}, u32[]{:S(2)}) %collective-permute-start.16) | collective-permute-done | bytes 3664 | tf_op jit(solution)/shard_map/ppermute | solution.py:145
  83.7 2.3 %collective-permute-start.17 = (f32[908]{0:T(1024)S(1)}, f32[908]{0:T(1024)S(1)}, u32[]{:S(2)}, u32[]{:S(2)}) collective-permute-start(f32[908]{0:T(1024)S(1)} %add_add_fusion.3), channel_id=1, source_target_pairs={{0,4},{1,5},{2,6},{3,7},{4,0},{5,1},{6,2},{7,3},{8,12},{9,13},{10,... | collective-permute-start | bytes 10904 | tf_op jit(solution)/shard_map/ppermute | solution.py:145
  86.0 2.4 %collective-permute-start.19 = (f32[908]{0:T(1024)S(1)}, f32[908]{0:T(1024)S(1)}, u32[]{:S(2)}, u32[]{:S(2)}) collective-permute-start(f32[908]{0:T(1024)S(1)} %add_add_fusion.3), channel_id=1, source_target_pairs={{0,12},{1,13},{2,14},{3,15},{4,8},{5,9},{6,10},{7,11},{8,4},{9,5},... | collective-permute-start | bytes 10904 | tf_op jit(solution)/shard_map/ppermute | solution.py:145
  88.4 2.1 %collective-permute-done.18 = f32[908]{0:T(1024)S(1)} collective-permute-done((f32[908]{0:T(1024)S(1)}, f32[908]{0:T(1024)S(1)}, u32[]{:S(2)}, u32[]{:S(2)}) %collective-permute-start.18) | collective-permute-done | bytes 3664 | tf_op jit(solution)/shard_map/ppermute | solution.py:145
  90.5 0.9 collective-permute-done.19
  92.9 2.2 %fusion.13 = f32[6,16,16,128]{3,2,1,0:T(8,128)} fusion(f32[3,16,16,128]{3,2,1,0:T(8,128)S(1)} %get-tuple-element.24, f32[3,16,16,128]{3,2,1,0:T(8,128)S(1)} %get-tuple-element.23, f32[3,16,16,128]{3,2,1,0:T(8,128)} %get-tuple-element.27, f32[3,16,16,128]{3,2,1,0:T(8,128)} %get-tuple-element.26, f32[6]{0:T(128)S(1)} %pad_maximum_fusion.17, ...), kind=kLoop, calls=%fused_computation.38 | loop fusion | flops 1376256 | bytes 2359344 | tf_op jit(solution)/shard_map/add | solution.py:131
  (118 shorter events, 14.6 us)
Async XLA Ops:
  0.6 18.0 %copy-start = (bf16[6,16,16,128]{3,2,1,0:T(8,128)(2,1)S(1)}, bf16[6,16,16,128]{3,2,1,0:T(8,128)(2,1)}, u32[]{:S(2)}) copy-start(bf16[6,16,16,128]{3,2,1,0:T(8,128)(2,1)} %param.10) | copy-start | bytes 1179652
  4.0 16.6 %collective-permute-start = (f32[6]{0:T(128)S(1)}, f32[6]{0:T(128)S(1)}, u32[]{:S(2)}, u32[]{:S(2)}) collective-permute-start(f32[6]{0:T(128)S(1)} %multiply_reduce_fusion.1), channel_id=1, source_target_pairs={{0,1},{1,0},{2,3},{3,2},{4,5},{5,4},{6,7},{7,6},{8,9},{9,8},{10,11... | collective-permute-start | bytes 80 | tf_op jit(solution)/shard_map/ppermute | solution.py:145
  4.5 16.1 %collective-permute-start.1 = (f32[6]{0:T(128)S(1)}, f32[6]{0:T(128)S(1)}, u32[]{:S(2)}, u32[]{:S(2)}) collective-permute-start(f32[6]{0:T(128)S(1)} %multiply_reduce_fusion.1), channel_id=1, source_target_pairs={{0,2},{1,3},{2,0},{3,1},{4,6},{5,7},{6,4},{7,5},{8,10},{9,11},{10,... | collective-permute-start | bytes 80 | tf_op jit(solution)/shard_map/ppermute | solution.py:145
  7.1 13.5 %collective-permute-start.2 = (f32[6]{0:T(128)S(1)}, f32[6]{0:T(128)S(1)}, u32[]{:S(2)}, u32[]{:S(2)}) collective-permute-start(f32[6]{0:T(128)S(1)} %multiply_reduce_fusion.1), channel_id=1, source_target_pairs={{0,3},{1,2},{2,1},{3,0},{4,7},{5,6},{6,5},{7,4},{8,11},{9,10},{10,... | collective-permute-start | bytes 80 | tf_op jit(solution)/shard_map/ppermute | solution.py:145
  7.9 10.8 %collective-permute-start.6 = (f32[6,1,16,128]{3,2,1,0:T(8,128)S(1)}, f32[6,1,16,128]{3,2,1,0:T(8,128)S(1)}, u32[]{:S(2)}, u32[]{:S(2)}) collective-permute-start(f32[6,1,16,128]{3,2,1,0:T(8,128)S(1)} %get-tuple-element.66), channel_id=1, source_target_pairs={{4,0},{8,4},{12,8},{5,1},{9,5},{13,9},{6,2},{10,6},{14,10},{7,3},{... | collective-permute-start | bytes 147464 | tf_op jit(solution)/shard_map/ppermute | solution.py:34
  9.2 9.5 %collective-permute-start.7 = (f32[6,1,16,128]{3,2,1,0:T(8,128)S(1)}, f32[6,1,16,128]{3,2,1,0:T(8,128)S(1)}, u32[]{:S(2)}, u32[]{:S(2)}) collective-permute-start(f32[6,1,16,128]{3,2,1,0:T(8,128)S(1)} %get-tuple-element.65), channel_id=1, source_target_pairs={{0,4},{4,8},{8,12},{1,5},{5,9},{9,13},{2,6},{6,10},{10,14},{3,7},{... | collective-permute-start | bytes 147464 | tf_op jit(solution)/shard_map/ppermute | solution.py:33
  18.8 5.6 %copy-start.18 = (f32[2,3]{1,0:T(2,128)S(1)}, f32[2,3]{1,0:T(2,128)}, u32[]{:S(2)}) copy-start(f32[2,3]{1,0:T(2,128)} %param.16) | copy-start | bytes 76
  18.8 4.2 %collective-permute-start.8 = (f32[6,18,1,128]{3,2,1,0:T(1,128)S(1)}, f32[6,18,1,128]{3,2,1,0:T(1,128)S(1)}, u32[]{:S(2)}, u32[]{:S(2)}) collective-permute-start(f32[6,18,1,128]{3,2,1,0:T(1,128)S(1)} %broadcast_select_fusion.5), channel_id=1, source_target_pairs={{0,2},{2,0},{1,3},{3,1},{4,6},{6,4},{5,7},{7,5},{8,10},{10,8},{9,1... | collective-permute-start | bytes 165896 | tf_op jit(solution)/shard_map/ppermute | solution.py:26
  24.4 10.9 %collective-permute-start.9 = (f32[6,18,18,128]{3,2,1,0:T(8,128)}, f32[6,18,18,128]{3,2,1,0:T(8,128)S(1)}, u32[]{:S(2)}, u32[]{:S(2)}) collective-permute-start(f32[6,18,18,128]{3,2,1,0:T(8,128)} %maximum_add_fusion), channel_id=1, source_target_pairs={{0,1},{1,0},{2,3},{3,2},{4,5},{5,4},{6,7},{7,6},{8,9},{9,8},{10,11... | collective-permute-start | bytes 2985992 | tf_op jit(solution)/shard_map/ppermute | solution.py:18
  24.4 17.9 %copy-start.11 = (f32[3]{0:T(128)}, f32[3]{0:T(128)S(1)}, u32[]{:S(2)}) copy-start(f32[3]{0:T(128)S(1)} %get-tuple-element.80) | copy-start | bytes 40
  24.4 17.9 %copy-start.13 = (f32[3]{0:T(128)}, f32[3]{0:T(128)S(1)}, u32[]{:S(2)}) copy-start(f32[3]{0:T(128)S(1)} %get-tuple-element.81) | copy-start | bytes 40
  25.5 4.5 %collective-permute-start.3 = (f32[6]{0:T(128)S(1)}, f32[6]{0:T(128)S(1)}, u32[]{:S(2)}, u32[]{:S(2)}) collective-permute-start(f32[6]{0:T(128)S(1)} %add_add_fusion.6), channel_id=1, source_target_pairs={{0,4},{1,5},{2,6},{3,7},{4,0},{5,1},{6,2},{7,3},{8,12},{9,13},{10,... | collective-permute-start | bytes 80 | tf_op jit(solution)/shard_map/ppermute | solution.py:145
  27.4 4.4 %collective-permute-start.4 = (f32[6]{0:T(128)S(1)}, f32[6]{0:T(128)S(1)}, u32[]{:S(2)}, u32[]{:S(2)}) collective-permute-start(f32[6]{0:T(128)S(1)} %add_add_fusion.6), channel_id=1, source_target_pairs={{0,8},{1,9},{2,10},{3,11},{4,12},{5,13},{6,14},{7,15},{8,0},{9,1},... | collective-permute-start | bytes 80 | tf_op jit(solution)/shard_map/ppermute | solution.py:145
  28.5 5.3 %collective-permute-start.5 = (f32[6]{0:T(128)S(1)}, f32[6]{0:T(128)S(1)}, u32[]{:S(2)}, u32[]{:S(2)}) collective-permute-start(f32[6]{0:T(128)S(1)} %add_add_fusion.6), channel_id=1, source_target_pairs={{0,12},{1,13},{2,14},{3,15},{4,8},{5,9},{6,10},{7,11},{8,4},{9,5},... | collective-permute-start | bytes 80 | tf_op jit(solution)/shard_map/ppermute | solution.py:145
  33.8 10.4 %copy-start.9 = (f32[6]{0:T(128)}, f32[6]{0:T(128)S(1)}, u32[]{:S(2)}) copy-start(f32[6]{0:T(128)S(1)} %get-tuple-element.32) | copy-start | bytes 76
  35.8 2.1 %copy-start.1 = (bf16[6,16,16,128]{3,2,1,0:T(8,128)(2,1)S(1)}, bf16[6,16,16,128]{3,2,1,0:T(8,128)(2,1)}, u32[]{:S(2)}) copy-start(bf16[6,16,16,128]{3,2,1,0:T(8,128)(2,1)} %param.10) | copy-start | bytes 1179652
  40.7 0.9 copy-start.3
  40.7 1.0 %copy-start.4 = (f32[16,16,128]{2,1,0:T(8,128)S(1)}, f32[16,16,128]{2,1,0:T(8,128)}, u32[]{:S(2)}) copy-start(f32[16,16,128]{2,1,0:T(8,128)} %get-tuple-element.69) | copy-start | bytes 393220
  40.7 1.0 %copy-start.7 = (f32[16,16,128]{2,1,0:T(8,128)S(1)}, f32[16,16,128]{2,1,0:T(8,128)}, u32[]{:S(2)}) copy-start(f32[16,16,128]{2,1,0:T(8,128)} %get-tuple-element.67) | copy-start | bytes 393220
  41.8 0.9 copy-start.8
  45.1 6.0 %collective-permute-start.10 = (f32[6,1,16,128]{3,2,1,0:T(8,128)S(1)}, f32[6,1,16,128]{3,2,1,0:T(8,128)S(1)}, u32[]{:S(2)}, u32[]{:S(2)}) collective-permute-start(f32[6,1,16,128]{3,2,1,0:T(8,128)S(1)} %get-tuple-element.63), channel_id=1, source_target_pairs={{4,0},{8,4},{12,8},{5,1},{9,5},{13,9},{6,2},{10,6},{14,10},{7,3},{... | collective-permute-start | bytes 147464 | tf_op jit(solution)/shard_map/ppermute | solution.py:34
  46.3 6.3 %collective-permute-start.11 = (f32[6,1,16,128]{3,2,1,0:T(8,128)S(1)}, f32[6,1,16,128]{3,2,1,0:T(8,128)S(1)}, u32[]{:S(2)}, u32[]{:S(2)}) collective-permute-start(f32[6,1,16,128]{3,2,1,0:T(8,128)S(1)} %get-tuple-element.62), channel_id=1, source_target_pairs={{0,4},{4,8},{8,12},{1,5},{5,9},{9,13},{2,6},{6,10},{10,14},{3,7},{... | collective-permute-start | bytes 147464 | tf_op jit(solution)/shard_map/ppermute | solution.py:33
  52.7 5.6 %copy-start.5 = (bf16[6,16,16,128]{3,2,1,0:T(8,128)(2,1)S(1)}, bf16[6,16,16,128]{3,2,1,0:T(8,128)(2,1)}, u32[]{:S(2)}) copy-start(bf16[6,16,16,128]{3,2,1,0:T(8,128)(2,1)} %param.9) | copy-start | bytes 1179652
  52.7 4.2 %collective-permute-start.12 = (f32[6,18,1,128]{3,2,1,0:T(1,128)S(1)}, f32[6,18,1,128]{3,2,1,0:T(1,128)S(1)}, u32[]{:S(2)}, u32[]{:S(2)}) collective-permute-start(f32[6,18,1,128]{3,2,1,0:T(1,128)S(1)} %broadcast_select_fusion.2), channel_id=1, source_target_pairs={{0,2},{2,0},{1,3},{3,1},{4,6},{6,4},{5,7},{7,5},{8,10},{10,8},{9,1... | collective-permute-start | bytes 165896 | tf_op jit(solution)/shard_map/ppermute | solution.py:26
  58.3 8.2 %collective-permute-start.13 = (f32[6,18,18,128]{3,2,1,0:T(8,128)}, f32[6,18,18,128]{3,2,1,0:T(8,128)}, u32[]{:S(2)}, u32[]{:S(2)}) collective-permute-start(f32[6,18,18,128]{3,2,1,0:T(8,128)} %pad_maximum_fusion.4), channel_id=1, source_target_pairs={{0,1},{1,0},{2,3},{3,2},{4,5},{5,4},{6,7},{7,6},{8,9},{9,8},{10,11... | collective-permute-start | bytes 2985992 | tf_op jit(solution)/shard_map/ppermute | solution.py:18
  60.7 1.2 %copy-start.6 = (f32[3,16,16,128]{3,2,1,0:T(8,128)S(1)}, f32[3,16,16,128]{3,2,1,0:T(8,128)}, u32[]{:S(2)}) copy-start(f32[3,16,16,128]{3,2,1,0:T(8,128)} %get-tuple-element.20) | copy-start | bytes 1179652
  73.5 1.1 %copy-start.2 = (f32[6,16,16,128]{3,2,1,0:T(8,128)S(1)}, f32[6,16,16,128]{3,2,1,0:T(8,128)}, u32[]{:S(2)}) copy-start(f32[6,16,16,128]{3,2,1,0:T(8,128)} %convert_element_type.13) | copy-start | bytes 2359300
  73.5 1.1 %copy-start.12 = (f32[3]{0:T(128)S(1)}, f32[3]{0:T(128)}, u32[]{:S(2)}) copy-start(f32[3]{0:T(128)} %copy-done.11) | copy-start | bytes 40
  73.5 1.1 %copy-start.14 = (f32[3]{0:T(128)S(1)}, f32[3]{0:T(128)}, u32[]{:S(2)}) copy-start(f32[3]{0:T(128)} %copy-done.13) | copy-start | bytes 40
  74.9 2.1 %copy-start.15 = (f32[6]{0:T(128)S(1)}, f32[6]{0:T(128)}, u32[]{:S(2)}) copy-start(f32[6]{0:T(128)} %get-tuple-element.60) | copy-start | bytes 76
  75.0 2.1 %copy-start.16 = (f32[3]{0:T(128)S(1)}, f32[3]{0:T(128)}, u32[]{:S(2)}) copy-start(f32[3]{0:T(128)} %reduce_sum.108) | copy-start | bytes 40
  75.0 2.1 %copy-start.17 = (f32[3]{0:T(128)S(1)}, f32[3]{0:T(128)}, u32[]{:S(2)}) copy-start(f32[3]{0:T(128)} %reduce_sum.109) | copy-start | bytes 40
  75.0 16.5 %copy-start.10 = (f32[6]{0:T(128)S(1)}, f32[6]{0:T(128)}, u32[]{:S(2)}) copy-start(f32[6]{0:T(128)} %copy-done.9) | copy-start | bytes 76
  77.2 3.4 %collective-permute-start.14 = (f32[908]{0:T(1024)S(1)}, f32[908]{0:T(1024)S(1)}, u32[]{:S(2)}, u32[]{:S(2)}) collective-permute-start(f32[908]{0:T(1024)S(1)} %concatenate.201), channel_id=1, source_target_pairs={{0,1},{1,0},{2,3},{3,2},{4,5},{5,4},{6,7},{7,6},{8,9},{9,8},{10,11... | collective-permute-start | bytes 10904 | tf_op jit(solution)/shard_map/ppermute | solution.py:145
  77.7 4.5 %collective-permute-start.15 = (f32[908]{0:T(1024)S(1)}, f32[908]{0:T(1024)S(1)}, u32[]{:S(2)}, u32[]{:S(2)}) collective-permute-start(f32[908]{0:T(1024)S(1)} %concatenate.201), channel_id=1, source_target_pairs={{0,2},{1,3},{2,0},{3,1},{4,6},{5,7},{6,4},{7,5},{8,10},{9,11},{10,... | collective-permute-start | bytes 10904 | tf_op jit(solution)/shard_map/ppermute | solution.py:145
  80.6 3.1 %collective-permute-start.16 = (f32[908]{0:T(1024)S(1)}, f32[908]{0:T(1024)S(1)}, u32[]{:S(2)}, u32[]{:S(2)}) collective-permute-start(f32[908]{0:T(1024)S(1)} %concatenate.201), channel_id=1, source_target_pairs={{0,3},{1,2},{2,1},{3,0},{4,7},{5,6},{6,5},{7,4},{8,11},{9,10},{10,... | collective-permute-start | bytes 10904 | tf_op jit(solution)/shard_map/ppermute | solution.py:145
  83.7 4.8 %collective-permute-start.17 = (f32[908]{0:T(1024)S(1)}, f32[908]{0:T(1024)S(1)}, u32[]{:S(2)}, u32[]{:S(2)}) collective-permute-start(f32[908]{0:T(1024)S(1)} %add_add_fusion.3), channel_id=1, source_target_pairs={{0,4},{1,5},{2,6},{3,7},{4,0},{5,1},{6,2},{7,3},{8,12},{9,13},{10,... | collective-permute-start | bytes 10904 | tf_op jit(solution)/shard_map/ppermute | solution.py:145
  86.0 4.5 %collective-permute-start.18 = (f32[908]{0:T(1024)S(1)}, f32[908]{0:T(1024)S(1)}, u32[]{:S(2)}, u32[]{:S(2)}) collective-permute-start(f32[908]{0:T(1024)S(1)} %add_add_fusion.3), channel_id=1, source_target_pairs={{0,8},{1,9},{2,10},{3,11},{4,12},{5,13},{6,14},{7,15},{8,0},{9,1},... | collective-permute-start | bytes 10904 | tf_op jit(solution)/shard_map/ppermute | solution.py:145
  86.0 5.4 %collective-permute-start.19 = (f32[908]{0:T(1024)S(1)}, f32[908]{0:T(1024)S(1)}, u32[]{:S(2)}, u32[]{:S(2)}) collective-permute-start(f32[908]{0:T(1024)S(1)} %add_add_fusion.3), channel_id=1, source_target_pairs={{0,12},{1,13},{2,14},{3,15},{4,8},{5,9},{6,10},{7,11},{8,4},{9,5},... | collective-permute-start | bytes 10904 | tf_op jit(solution)/shard_map/ppermute | solution.py:145

commit v18 on v12

--- a/solution.py
+++ b/solution.py
@@ -86,29 +86,21 @@
 def sweep(padded, lame_first, shear, density, mask, source, omega_sq, impedance):
     field = window(padded, (0, 0, 0))
     elastic = navier(padded, lame_first, shear)
-    real_part = field[:3]
-    imag_part = field[3:]
-    imp_real = impedance[0][:, None, None, None]
-    imp_imag = impedance[1][:, None, None, None]
+    cross = jnp.concatenate([-field[3:], field[:3]], 0)
+    imp_real = jnp.concatenate([impedance[0], impedance[0]])[:, None, None, None]
+    imp_imag = jnp.concatenate([impedance[1], impedance[1]])[:, None, None, None]
     inertia = omega_sq * density
-    apply_real = (
-        -elastic[:3]
-        - inertia * (real_part - DAMPING * imag_part)
-        + mask * (imp_real * real_part - imp_imag * imag_part)
-    )
-    apply_imag = (
-        -elastic[3:]
-        - inertia * (imag_part + DAMPING * real_part)
-        + mask * (imp_real * imag_part + imp_imag * real_part)
-    )
-    resid_real = source[:3] - apply_real
-    resid_imag = source[3:] - apply_imag
+    apply = (
+        -elastic
+        - inertia * (field + DAMPING * cross)
+        + mask * (imp_real * field + imp_imag * cross)
+    )
+    resid = source - apply
+    resid_cross = jnp.concatenate([resid[3:], -resid[:3]], 0)
     diag_real = 8.0 * shear + 2.0 * lame_first - inertia + mask * imp_real
     diag_imag = -DAMPING * inertia + mask * imp_imag
     modulus = diag_real * diag_real + diag_imag * diag_imag
-    new_real = real_part + RELAXATION * (resid_real * diag_real + resid_imag * diag_imag) / modulus
-    new_imag = imag_part + RELAXATION * (resid_imag * diag_real - resid_real * diag_imag) / modulus
-    return jnp.concatenate([new_real, new_imag], 0)
+    return field + RELAXATION * (resid * diag_real + resid_cross * diag_imag) / modulus
 
 
 def mean_gain(lame_first, shear, density, mask, omega_sq, impedance):

time: 87.4 us -> 92.2 us (1.055)
  waiting for transfers between devices: 16.1 us -> 21.6 us
  starting transfers between devices: 29.3 us -> 27.5 us
  other arithmetic: 30.4 us -> 31.5 us
    ppermute x2, waiting for transfers between devices: 0.01 us -> 7.99 us  [with_halo(): after = lax.ppermute(initial, axis, down)]
    add x15 -> x1, other arithmetic: 6.46 us -> 0.43 us  [sweep(): field + RELAXATION * (resid * diag_real + resid_cross * diag_imag) / modulus]
    unnamed x0 -> x10, other arithmetic: none -> 4.31 us
    ppermute x12, waiting for transfers between devices: 11 us -> 7.21 us  [group_rounds(): lax.ppermute(value, axes, [(i, i ^ m * stride) for i in range(size)])]
    ppermute x2, starting transfers between devices: 10.3 us -> 6.99 us  [with_halo(): before = lax.ppermute(last, axis, up)]
    unnamed x35 -> x43, local copies, waits for them, and re-layouts: 1.43 us -> 3.43 us
    ppermute x2, waiting for transfers between devices: 3.5 us -> 5.26 us  [with_halo(): got = lax.ppermute(jnp.where(first, last, initial), axis, [(0, 1), (1, 0)])]
    select_n x2, other arithmetic: 2.64 us -> 4.32 us  [with_halo(): after = jnp.where(first, got_initial, zero)]
  transfers between devices with their start and end apart: 20 -> 20, of which waited for: 9 -> 13; matrix products, arithmetic and copies ran while one was open for 18% -> 5% of each run, Pallas kernels for 0% -> 0%
where the time goes in v18:
time: 92.2 us; the launch traced here: 91.6 us
  other arithmetic  31.5 us (34%)
  starting transfers between devices  27.5 us (30%)
  waiting for transfers between devices  21.6 us (23%)
  local copies, waits for them, and re-layouts  9.04 us (10%)
  between operations  2 us (2%)
    ppermute x12, starting transfers between devices, group_rounds(): lax.ppermute(value, axes, [(i, i ^ m * stride) for i in range(size)])  14.6 us
    ppermute x2, waiting for transfers between devices, with_halo(): after = lax.ppermute(initial, axis, down)  7.99 us
    ppermute x12, waiting for transfers between devices, group_rounds(): lax.ppermute(value, axes, [(i, i ^ m * stride) for i in range(size)])  7.21 us
    ppermute x2, starting transfers between devices, with_halo(): before = lax.ppermute(last, axis, up)  6.99 us
    concatenate x5, other arithmetic, with_halo(): array = jnp.concatenate([before, array, after], axis=dim)  5.96 us
    ppermute x2, waiting for transfers between devices, with_halo(): got = lax.ppermute(jnp.where(first, last, initial), axis, [(0, 1), (1, 0)])  5.26 us
    select_n x2, other arithmetic, with_halo(): after = jnp.where(first, got_initial, zero)  4.32 us
    unnamed x10, other arithmetic  4.31 us
  transfers between devices with their start and end apart: 20, of which 13 were waited for; matrix products, arithmetic and copies ran while one was open for 5% of the time, Pallas kernels for 0%

profile of v18, /device:TPU:0, one launch (start us, length us, event | category | flops | bytes accessed | tf_op | source)
XLA Modules:
  0.0 91.6 jit_solution(16036845064907148410)
XLA Ops:
  1.4 0.7 compare_select_fusion
  2.0 0.8 slice_bitcast_fusion.2
  2.8 0.8 slice_bitcast_fusion.1
  3.6 1.5 %scatter_custom_fusion = f32[32768]{0:T(1024)S(1)} fusion(s32[256]{0:T(256)S(1)} %bitcast.47, f32[256]{0:T(256)S(1)} %broadcast.314, f32[]{:T(128)} %constant.28.clone.1), kind=kCustom, calls=%fused_computation.265 | custom fusion | bytes 131076 | tf_op jit(solution)/shard_map/scatter | solution.py:179
  5.0 1.2 %fusion.3 = f32[6]{0:T(128)S(1)} fusion(bf16[6,16,16,128]{3,2,1,0:T(8,128)(2,1)} %param.10, f32[16,16,128]{2,1,0:T(8,128)S(1)} %bitcast.37), kind=kLoop, calls=%fused_computation.25 | loop fusion | flops 589818 | bytes 524312 | tf_op jit(solution)/shard_map/reduce_sum | solution.py:215
  6.2 1.1 %convert_element_type.15 = f32[6,16,16,128]{3,2,1,0:T(8,128)S(1)} convert(bf16[6,16,16,128]{3,2,1,0:T(8,128)(2,1)} %param.11) | non-fusion elementwise | flops 196608 | bytes 1179648 | tf_op jit(solution)/shard_map/convert_element_type | solution.py:203
  7.8 0.7 convert_multiply_fusion.3
  8.4 1.4 %multiply_subtract_fusion = (f32[3,16,16,128]{3,2,1,0:T(8,128)}, f32[3,16,16,128]{3,2,1,0:T(8,128)}, f32[3,16,16,128]{3,2,1,0:T(8,128)}, f32[3,16,16,128]{3,2,1,0:T(8,128)S(1)}, f32[3,16,16,128]{3,2,1,0:T(8,128)S(1)}) fusion(f32[6,16,16,128]{3,2,1,0:T(8,128)S(1)} %convert_element_type.15, f32[3]{0:T(128)S(1)} %get-tuple-element.76, ...), kind=kLoop, calls=%fused_computation.78 | loop fusion | flops 2359296 | bytes 3276824 | tf_op jit(solution)/shard_map/sub | solution.py:208
  10.2 2.4 %collective-permute-start.2 = (f32[12]{0:T(128)S(1)}, f32[12]{0:T(128)S(1)}, u32[]{:S(2)}, u32[]{:S(2)}) collective-permute-start(f32[12]{0:T(128)S(1)} %pad_maximum_fusion.18), channel_id=1, source_target_pairs={{0,3},{1,2},{2,1},{3,0},{4,7},{5,6},{6,5},{7,4},{8,11},{9,10},{10,... | collective-permute-start | bytes 152 | tf_op jit(solution)/shard_map/ppermute | solution.py:137
  13.2 3.7 %collective-permute-start.7 = (f32[6,1,16,128]{3,2,1,0:T(8,128)S(1)}, f32[6,1,16,128]{3,2,1,0:T(8,128)S(1)}, u32[]{:S(2)}, u32[]{:S(2)}) collective-permute-start(f32[6,1,16,128]{3,2,1,0:T(8,128)S(1)} %get-tuple-element.60), channel_id=1, source_target_pairs={{0,4},{4,8},{8,12},{1,5},{5,9},{9,13},{2,6},{6,10},{10,14},{3,7},{... | collective-permute-start | bytes 147464 | tf_op jit(solution)/shard_map/ppermute | solution.py:33
  17.0 1.3 %collective-permute-start.6 = (f32[6,1,16,128]{3,2,1,0:T(8,128)S(1)}, f32[6,1,16,128]{3,2,1,0:T(8,128)S(1)}, u32[]{:S(2)}, u32[]{:S(2)}) collective-permute-start(f32[6,1,16,128]{3,2,1,0:T(8,128)S(1)} %get-tuple-element.61), channel_id=1, source_target_pairs={{4,0},{8,4},{12,8},{5,1},{9,5},{13,9},{6,2},{10,6},{14,10},{7,3},{... | collective-permute-start | bytes 147464 | tf_op jit(solution)/shard_map/ppermute | solution.py:34
  18.4 0.8 slice_negate_fusion.3
  19.2 3.7 %collective-permute-done.6 = f32[6,1,16,128]{3,2,1,0:T(8,128)S(1)} collective-permute-done((f32[6,1,16,128]{3,2,1,0:T(8,128)S(1)}, f32[6,1,16,128]{3,2,1,0:T(8,128)S(1)}, u32[]{:S(2)}, u32[]{:S(2)}) %collective-permute-start.6) | collective-permute-done | bytes 49184 | tf_op jit(solution)/shard_map/ppermute | solution.py:34
  23.0 1.6 %collective-permute-start.8 = (f32[6,18,1,128]{3,2,1,0:T(1,128)S(1)}, f32[6,18,1,128]{3,2,1,0:T(1,128)S(1)}, u32[]{:S(2)}, u32[]{:S(2)}) collective-permute-start(f32[6,18,1,128]{3,2,1,0:T(1,128)S(1)} %broadcast_select_fusion.5), channel_id=1, source_target_pairs={{0,2},{2,0},{1,3},{3,1},{4,6},{6,4},{5,7},{7,5},{8,10},{10,8},{9,1... | collective-permute-start | bytes 165896 | tf_op jit(solution)/shard_map/ppermute | solution.py:26
  24.6 2.6 %collective-permute-done.8 = f32[6,18,1,128]{3,2,1,0:T(1,128)S(1)} collective-permute-done((f32[6,18,1,128]{3,2,1,0:T(1,128)S(1)}, f32[6,18,1,128]{3,2,1,0:T(1,128)S(1)}, u32[]{:S(2)}, u32[]{:S(2)}) %collective-permute-start.8) | collective-permute-done | bytes 55328 | tf_op jit(solution)/shard_map/ppermute | solution.py:26
  27.3 1.3 %maximum_add_fusion = f32[6,18,18,128]{3,2,1,0:T(8,128)} fusion(f32[6,18,1,128]{3,2,1,0:T(1,128)S(1)} %get-tuple-element.68, f32[6,1,16,128]{3,2,1,0:T(8,128)S(1)} %collective-permute-done.6, f32[6,16,16,128]{3,2,1,0:T(8,128)S(1)} %convert_element_type.12, f32[6,1,16,128]{3,2,1,0:T(8,128)S(1)} %collective-permute-done.7, ...), kind=kLoop, calls=%fused_computation.11 | loop fusion | flops 1244160 | bytes 1990660 | tf_op jit(solution)/shard_map/add | solution.py:17
  28.7 0.8 slice.1051
  29.5 1.7 %collective-permute-start.5 = (f32[12]{0:T(128)S(1)}, f32[12]{0:T(128)S(1)}, u32[]{:S(2)}, u32[]{:S(2)}) collective-permute-start(f32[12]{0:T(128)S(1)} %add_add_fusion.6), channel_id=1, source_target_pairs={{0,12},{1,13},{2,14},{3,15},{4,8},{5,9},{6,10},{7,11},{8,4},{9,5},... | collective-permute-start | bytes 152 | tf_op jit(solution)/shard_map/ppermute | solution.py:137
  31.2 1.3 %collective-permute-start.4 = (f32[12]{0:T(128)S(1)}, f32[12]{0:T(128)S(1)}, u32[]{:S(2)}, u32[]{:S(2)}) collective-permute-start(f32[12]{0:T(128)S(1)} %add_add_fusion.6), channel_id=1, source_target_pairs={{0,8},{1,9},{2,10},{3,11},{4,12},{5,13},{6,14},{7,15},{8,0},{9,1},... | collective-permute-start | bytes 152 | tf_op jit(solution)/shard_map/ppermute | solution.py:137
  32.6 1.3 %collective-permute-start.3 = (f32[12]{0:T(128)S(1)}, f32[12]{0:T(128)S(1)}, u32[]{:S(2)}, u32[]{:S(2)}) collective-permute-start(f32[12]{0:T(128)S(1)} %add_add_fusion.6), channel_id=1, source_target_pairs={{0,4},{1,5},{2,6},{3,7},{4,0},{5,1},{6,2},{7,3},{8,12},{9,13},{10,... | collective-permute-start | bytes 152 | tf_op jit(solution)/shard_map/ppermute | solution.py:137
  33.9 0.9 %collective-permute-done.5 = f32[12]{0:T(128)S(1)} collective-permute-done((f32[12]{0:T(128)S(1)}, f32[12]{0:T(128)S(1)}, u32[]{:S(2)}, u32[]{:S(2)}) %collective-permute-start.5) | collective-permute-done | bytes 80 | tf_op jit(solution)/shard_map/ppermute | solution.py:137
  34.9 0.8 collective-permute-done.4
  36.6 2.2 %slice_select_fusion.3 = (f32[6,18,18,1]{3,2,1,0:T(8,128)S(1)}, f32[6,18,18,1]{3,2,1,0:T(8,128)S(1)}) fusion(f32[6,18,18,128]{3,2,1,0:T(8,128)} %collective-permute-done.9, pred[]{:T(512)S(6)} %eq.67), kind=kLoop, calls=%fused_computation.8 | loop fusion | flops 3888 | bytes 31105 | tf_op jit(solution)/shard_map/jit(_where)/select_n | solution.py:23
  38.8 2.1 %pad_maximum_fusion = (f32[6,18,18,129]{3,2,1,0:T(8,128)S(1)}, f32[6,18,18,129]{3,2,1,0:T(8,128)S(1)}) fusion(f32[6,18,18,1]{3,2,1,0:T(8,128)S(1)} %get-tuple-element.42, f32[6,18,1,128]{3,2,1,0:T(1,128)S(1)} %get-tuple-element.68, f32[6,1,16,128]{3,2,1,0:T(8,128)S(1)} %collective-permute-done.6, f32[6,16,16,128]{3,2,1,0:T(8,128)S(1)} %convert_element_type.12, ...), kind=kLoop, calls=%fused_computation.1 | loop fusion | flops 2507760 | bytes 3017088 | tf_op jit(solution)/shard_map/concatenate | solution.py:35
  43.8 0.7 fusion.76
  45.5 0.8 copy-done.6
  46.3 1.2 %multiply_reduce_fusion = (f32[6]{0:T(128)}, f32[6,16,16,128]{3,2,1,0:T(8,128)S(1)}) fusion(f32[16,16,128]{2,1,0:T(8,128)S(1)} %bitcast.40, f32[6]{0:T(128)S(1)} %pad_maximum_fusion.20, f32[16,16,128]{2,1,0:T(8,128)S(1)} %copy-done.6, f32[3,16,16,128]{3,2,1,0:T(8,128)S(1)} %get-tuple-element.59, f32[3,16,16,128]{3,2,1,0:T(8,128)S(1)} %get-tuple-element.58, ...), kind=kLoop, calls=%fused_computation.67 | loop fusion | flops 3342330 | bytes 3145800 | tf_op jit(solution)/shard_map/reduce_sum | solution.py:231
  47.8 3.3 %collective-permute-start.11 = (f32[6,1,16,128]{3,2,1,0:T(8,128)S(1)}, f32[6,1,16,128]{3,2,1,0:T(8,128)S(1)}, u32[]{:S(2)}, u32[]{:S(2)}) collective-permute-start(f32[6,1,16,128]{3,2,1,0:T(8,128)S(1)} %get-tuple-element.54), channel_id=1, source_target_pairs={{0,4},{4,8},{8,12},{1,5},{5,9},{9,13},{2,6},{6,10},{10,14},{3,7},{... | collective-permute-start | bytes 147464 | tf_op jit(solution)/shard_map/ppermute | solution.py:33
  51.0 1.5 %collective-permute-start.10 = (f32[6,1,16,128]{3,2,1,0:T(8,128)S(1)}, f32[6,1,16,128]{3,2,1,0:T(8,128)S(1)}, u32[]{:S(2)}, u32[]{:S(2)}) collective-permute-start(f32[6,1,16,128]{3,2,1,0:T(8,128)S(1)} %get-tuple-element.55), channel_id=1, source_target_pairs={{4,0},{8,4},{12,8},{5,1},{9,5},{13,9},{6,2},{10,6},{14,10},{7,3},{... | collective-permute-start | bytes 147464 | tf_op jit(solution)/shard_map/ppermute | solution.py:34
  52.7 4.3 %collective-permute-done.10 = f32[6,1,16,128]{3,2,1,0:T(8,128)S(1)} collective-permute-done((f32[6,1,16,128]{3,2,1,0:T(8,128)S(1)}, f32[6,1,16,128]{3,2,1,0:T(8,128)S(1)}, u32[]{:S(2)}, u32[]{:S(2)}) %collective-permute-start.10) | collective-permute-done | bytes 49184 | tf_op jit(solution)/shard_map/ppermute | solution.py:34
  57.1 1.6 %collective-permute-start.12 = (f32[6,18,1,128]{3,2,1,0:T(1,128)S(1)}, f32[6,18,1,128]{3,2,1,0:T(1,128)S(1)}, u32[]{:S(2)}, u32[]{:S(2)}) collective-permute-start(f32[6,18,1,128]{3,2,1,0:T(1,128)S(1)} %broadcast_select_fusion.2), channel_id=1, source_target_pairs={{0,2},{2,0},{1,3},{3,1},{4,6},{6,4},{5,7},{7,5},{8,10},{10,8},{9,1... | collective-permute-start | bytes 165896 | tf_op jit(solution)/shard_map/ppermute | solution.py:26
  58.6 2.7 %collective-permute-done.12 = f32[6,18,1,128]{3,2,1,0:T(1,128)S(1)} collective-permute-done((f32[6,18,1,128]{3,2,1,0:T(1,128)S(1)}, f32[6,18,1,128]{3,2,1,0:T(1,128)S(1)}, u32[]{:S(2)}, u32[]{:S(2)}) %collective-permute-start.12) | collective-permute-done | bytes 55328 | tf_op jit(solution)/shard_map/ppermute | solution.py:26
  61.4 1.3 %pad_maximum_fusion.4 = f32[6,18,18,128]{3,2,1,0:T(8,128)} fusion(f32[6,18,1,128]{3,2,1,0:T(1,128)S(1)} %get-tuple-element.66, f32[6,1,16,128]{3,2,1,0:T(8,128)S(1)} %collective-permute-done.10, f32[6,16,16,128]{3,2,1,0:T(8,128)S(1)} %fusion.21, f32[6,1,16,128]{3,2,1,0:T(8,128)S(1)} %collective-permute-done.11, f32[6,18,1,128]{3,2,1,0:T(1,128)S(1)} %get-tuple-element.65), kind=kLoop, calls=%fused_computation.14 | loop fusion | flops 995328 | bytes 1990656 | tf_op jit(solution)/shard_map/concatenate | solution.py:35
  62.7 1.0 %multiply_add_fusion.3 = f32[3,16,16,128]{3,2,1,0:T(8,128)S(1)} fusion(f32[3,16,16,128]{3,2,1,0:T(8,128)} %get-tuple-element.24, f32[3,16,16,128]{3,2,1,0:T(8,128)S(1)} %copy-done.9), kind=kLoop, calls=%fused_computation.77 | loop fusion | flops 196608 | bytes 1179648 | tf_op jit(solution)/shard_map/add | solution.py:209
  65.2 0.9 collective-permute-done.13
  66.1 2.2 %slice_select_fusion.1 = (f32[6,18,18,1]{3,2,1,0:T(8,128)S(1)}, f32[6,18,18,1]{3,2,1,0:T(8,128)S(1)}) fusion(f32[6,18,18,128]{3,2,1,0:T(8,128)} %collective-permute-done.13, pred[]{:T(512)S(6)} %eq.67), kind=kLoop, calls=%fused_computation.6 | loop fusion | flops 3888 | bytes 31105 | tf_op jit(solution)/shard_map/jit(_where)/select_n | solution.py:23
  68.3 2.1 %pad_maximum_fusion.1 = (f32[6,18,18,129]{3,2,1,0:T(8,128)S(1)}, f32[6,18,18,129]{3,2,1,0:T(8,128)S(1)}) fusion(f32[6,18,18,1]{3,2,1,0:T(8,128)S(1)} %get-tuple-element.40, f32[6,18,1,128]{3,2,1,0:T(1,128)S(1)} %get-tuple-element.66, f32[6,1,16,128]{3,2,1,0:T(8,128)S(1)} %collective-permute-done.10, f32[6,16,16,128]{3,2,1,0:T(8,128)S(1)} %fusion.21, ...), kind=kLoop, calls=%fused_computation.3 | loop fusion | flops 2507760 | bytes 3017088 | tf_op jit(solution)/shard_map/concatenate | solution.py:35
  73.1 0.7 fusion.34
  74.6 0.8 copy-done.4
  76.9 2.6 %collective-permute-start.16 = (f32[902]{0:T(1024)S(1)}, f32[902]{0:T(1024)S(1)}, u32[]{:S(2)}, u32[]{:S(2)}) collective-permute-start(f32[902]{0:T(1024)S(1)} %pad_maximum_fusion.17), channel_id=1, source_target_pairs={{0,3},{1,2},{2,1},{3,0},{4,7},{5,6},{6,5},{7,4},{8,11},{9,10},{10,... | collective-permute-start | bytes 10832 | tf_op jit(solution)/shard_map/ppermute | solution.py:137
  79.6 1.1 %collective-permute-done.16 = f32[902]{0:T(1024)S(1)} collective-permute-done((f32[902]{0:T(1024)S(1)}, f32[902]{0:T(1024)S(1)}, u32[]{:S(2)}, u32[]{:S(2)}) %collective-permute-start.16) | collective-permute-done | bytes 3640 | tf_op jit(solution)/shard_map/ppermute | solution.py:137
  80.7 2.3 %collective-permute-done.15 = f32[902]{0:T(1024)S(1)} collective-permute-done((f32[902]{0:T(1024)S(1)}, f32[902]{0:T(1024)S(1)}, u32[]{:S(2)}, u32[]{:S(2)}) %collective-permute-start.15) | collective-permute-done | bytes 3640 | tf_op jit(solution)/shard_map/ppermute | solution.py:137
  83.0 0.8 collective-permute-start.19
  83.8 1.6 %collective-permute-start.18 = (f32[902]{0:T(1024)S(1)}, f32[902]{0:T(1024)S(1)}, u32[]{:S(2)}, u32[]{:S(2)}) collective-permute-start(f32[902]{0:T(1024)S(1)} %add_add_fusion.3), channel_id=1, source_target_pairs={{0,8},{1,9},{2,10},{3,11},{4,12},{5,13},{6,14},{7,15},{8,0},{9,1},... | collective-permute-start | bytes 10832 | tf_op jit(solution)/shard_map/ppermute | solution.py:137
  85.4 2.1 %collective-permute-start.17 = (f32[902]{0:T(1024)S(1)}, f32[902]{0:T(1024)S(1)}, u32[]{:S(2)}, u32[]{:S(2)}) collective-permute-start(f32[902]{0:T(1024)S(1)} %add_add_fusion.3), channel_id=1, source_target_pairs={{0,4},{1,5},{2,6},{3,7},{4,0},{5,1},{6,2},{7,3},{8,12},{9,13},{10,... | collective-permute-start | bytes 10832 | tf_op jit(solution)/shard_map/ppermute | solution.py:137
  87.5 1.0 %collective-permute-done.19 = f32[902]{0:T(1024)S(1)} collective-permute-done((f32[902]{0:T(1024)S(1)}, f32[902]{0:T(1024)S(1)}, u32[]{:S(2)}, u32[]{:S(2)}) %collective-permute-start.19) | collective-permute-done | bytes 3640 | tf_op jit(solution)/shard_map/ppermute | solution.py:137
  89.5 1.1 %fusion.23 = f32[6,16,16,128]{3,2,1,0:T(8,128)} fusion(f32[6,16,16,128]{3,2,1,0:T(8,128)S(1)} %fusion.29, f32[3,16,16,128]{3,2,1,0:T(8,128)S(1)} %get-tuple-element.25, f32[3,16,16,128]{3,2,1,0:T(8,128)S(1)} %copy-done.2, f32[6]{0:T(128)S(1)} %pad_maximum_fusion.22, f32[6]{0:T(128)S(1)} %maximum_multiply_fusion.2), kind=kLoop, calls=%fused_computation.56 | loop fusion | flops 1179648 | bytes 2359344 | tf_op jit(solution)/shard_map/add | solution.py:123
  91.0 0.7 copy.14
  (131 shorter events, 15.1 us)
Async XLA Ops:
  0.6 6.7 %copy-start.20 = (s32[2,2,4]{2,1,0:T(2,128)S(1)}, s32[2,2,4]{2,1,0:T(2,128)}, u32[]{:S(2)}) copy-start(s32[2,2,4]{2,1,0:T(2,128)} %param.13) | copy-start | bytes 196
  0.6 7.1 %copy-start.16 = (bf16[16,16,128]{2,1,0:T(8,128)(2,1)S(1)}, bf16[16,16,128]{2,1,0:T(8,128)(2,1)}, u32[]{:S(2)}) copy-start(bf16[16,16,128]{2,1,0:T(8,128)(2,1)} %param.12) | copy-start | bytes 196612
  8.4 1.4 %copy-start.5 = (f32[16,16,128]{2,1,0:T(8,128)}, f32[16,16,128]{2,1,0:T(8,128)S(1)}, u32[]{:S(2)}) copy-start(f32[16,16,128]{2,1,0:T(8,128)S(1)} %get-tuple-element.64) | copy-start | bytes 393220
  8.4 37.1 %copy-start.3 = (f32[16,16,128]{2,1,0:T(8,128)}, f32[16,16,128]{2,1,0:T(8,128)S(1)}, u32[]{:S(2)}) copy-start(f32[16,16,128]{2,1,0:T(8,128)S(1)} %get-tuple-element.63) | copy-start | bytes 393220
  8.4 4.8 %copy-start = (bf16[6,16,16,128]{3,2,1,0:T(8,128)(2,1)S(1)}, bf16[6,16,16,128]{3,2,1,0:T(8,128)(2,1)}, u32[]{:S(2)}) copy-start(bf16[6,16,16,128]{3,2,1,0:T(8,128)(2,1)} %param.10) | copy-start | bytes 1179652
  9.8 37.7 %copy-start.1 = (f32[3,16,16,128]{3,2,1,0:T(8,128)}, f32[3,16,16,128]{3,2,1,0:T(8,128)S(1)}, u32[]{:S(2)}) copy-start(f32[3,16,16,128]{3,2,1,0:T(8,128)S(1)} %get-tuple-element.26) | copy-start | bytes 1179652
  10.2 14.4 %collective-permute-start.2 = (f32[12]{0:T(128)S(1)}, f32[12]{0:T(128)S(1)}, u32[]{:S(2)}, u32[]{:S(2)}) collective-permute-start(f32[12]{0:T(128)S(1)} %pad_maximum_fusion.18), channel_id=1, source_target_pairs={{0,3},{1,2},{2,1},{3,0},{4,7},{5,6},{6,5},{7,4},{8,11},{9,10},{10,... | collective-permute-start | bytes 152 | tf_op jit(solution)/shard_map/ppermute | solution.py:137
  12.5 12.0 %collective-permute-start.1 = (f32[12]{0:T(128)S(1)}, f32[12]{0:T(128)S(1)}, u32[]{:S(2)}, u32[]{:S(2)}) collective-permute-start(f32[12]{0:T(128)S(1)} %pad_maximum_fusion.18), channel_id=1, source_target_pairs={{0,2},{1,3},{2,0},{3,1},{4,6},{5,7},{6,4},{7,5},{8,10},{9,11},{10,... | collective-permute-start | bytes 152 | tf_op jit(solution)/shard_map/ppermute | solution.py:137
  13.2 11.4 %collective-permute-start = (f32[12]{0:T(128)S(1)}, f32[12]{0:T(128)S(1)}, u32[]{:S(2)}, u32[]{:S(2)}) collective-permute-start(f32[12]{0:T(128)S(1)} %pad_maximum_fusion.18), channel_id=1, source_target_pairs={{0,1},{1,0},{2,3},{3,2},{4,5},{5,4},{6,7},{7,6},{8,9},{9,8},{10,11... | collective-permute-start | bytes 152 | tf_op jit(solution)/shard_map/ppermute | solution.py:137
  13.2 6.0 %collective-permute-start.7 = (f32[6,1,16,128]{3,2,1,0:T(8,128)S(1)}, f32[6,1,16,128]{3,2,1,0:T(8,128)S(1)}, u32[]{:S(2)}, u32[]{:S(2)}) collective-permute-start(f32[6,1,16,128]{3,2,1,0:T(8,128)S(1)} %get-tuple-element.60), channel_id=1, source_target_pairs={{0,4},{4,8},{8,12},{1,5},{5,9},{9,13},{2,6},{6,10},{10,14},{3,7},{... | collective-permute-start | bytes 147464 | tf_op jit(solution)/shard_map/ppermute | solution.py:33
  17.0 6.0 %collective-permute-start.6 = (f32[6,1,16,128]{3,2,1,0:T(8,128)S(1)}, f32[6,1,16,128]{3,2,1,0:T(8,128)S(1)}, u32[]{:S(2)}, u32[]{:S(2)}) collective-permute-start(f32[6,1,16,128]{3,2,1,0:T(8,128)S(1)} %get-tuple-element.61), channel_id=1, source_target_pairs={{4,0},{8,4},{12,8},{5,1},{9,5},{13,9},{6,2},{10,6},{14,10},{7,3},{... | collective-permute-start | bytes 147464 | tf_op jit(solution)/shard_map/ppermute | solution.py:34
  23.0 4.2 %collective-permute-start.8 = (f32[6,18,1,128]{3,2,1,0:T(1,128)S(1)}, f32[6,18,1,128]{3,2,1,0:T(1,128)S(1)}, u32[]{:S(2)}, u32[]{:S(2)}) collective-permute-start(f32[6,18,1,128]{3,2,1,0:T(1,128)S(1)} %broadcast_select_fusion.5), channel_id=1, source_target_pairs={{0,2},{2,0},{1,3},{3,1},{4,6},{6,4},{5,7},{7,5},{8,10},{10,8},{9,1... | collective-permute-start | bytes 165896 | tf_op jit(solution)/shard_map/ppermute | solution.py:26
  28.7 8.0 %collective-permute-start.9 = (f32[6,18,18,128]{3,2,1,0:T(8,128)}, f32[6,18,18,128]{3,2,1,0:T(8,128)}, u32[]{:S(2)}, u32[]{:S(2)}) collective-permute-start(f32[6,18,18,128]{3,2,1,0:T(8,128)} %maximum_add_fusion), channel_id=1, source_target_pairs={{0,1},{1,0},{2,3},{3,2},{4,5},{5,4},{6,7},{7,6},{8,9},{9,8},{10,11... | collective-permute-start | bytes 2985992 | tf_op jit(solution)/shard_map/ppermute | solution.py:18
  29.5 5.3 %collective-permute-start.5 = (f32[12]{0:T(128)S(1)}, f32[12]{0:T(128)S(1)}, u32[]{:S(2)}, u32[]{:S(2)}) collective-permute-start(f32[12]{0:T(128)S(1)} %add_add_fusion.6), channel_id=1, source_target_pairs={{0,12},{1,13},{2,14},{3,15},{4,8},{5,9},{6,10},{7,11},{8,4},{9,5},... | collective-permute-start | bytes 152 | tf_op jit(solution)/shard_map/ppermute | solution.py:137
  31.2 4.4 %collective-permute-start.4 = (f32[12]{0:T(128)S(1)}, f32[12]{0:T(128)S(1)}, u32[]{:S(2)}, u32[]{:S(2)}) collective-permute-start(f32[12]{0:T(128)S(1)} %add_add_fusion.6), channel_id=1, source_target_pairs={{0,8},{1,9},{2,10},{3,11},{4,12},{5,13},{6,14},{7,15},{8,0},{9,1},... | collective-permute-start | bytes 152 | tf_op jit(solution)/shard_map/ppermute | solution.py:137
  32.6 3.5 %collective-permute-start.3 = (f32[12]{0:T(128)S(1)}, f32[12]{0:T(128)S(1)}, u32[]{:S(2)}, u32[]{:S(2)}) collective-permute-start(f32[12]{0:T(128)S(1)} %add_add_fusion.6), channel_id=1, source_target_pairs={{0,4},{1,5},{2,6},{3,7},{4,0},{5,1},{6,2},{7,3},{8,12},{9,13},{10,... | collective-permute-start | bytes 152 | tf_op jit(solution)/shard_map/ppermute | solution.py:137
  36.1 0.5 copy-start.17
  43.8 1.0 %copy-start.10 = (bf16[6,16,16,128]{3,2,1,0:T(8,128)(2,1)S(1)}, bf16[6,16,16,128]{3,2,1,0:T(8,128)(2,1)}, u32[]{:S(2)}) copy-start(bf16[6,16,16,128]{3,2,1,0:T(8,128)(2,1)} %param.9) | copy-start | bytes 1179652
  43.8 1.1 %copy-start.12 = (f32[3,16,16,128]{3,2,1,0:T(8,128)S(1)}, f32[3,16,16,128]{3,2,1,0:T(8,128)}, u32[]{:S(2)}) copy-start(f32[3,16,16,128]{3,2,1,0:T(8,128)} %slice_negate_fusion.3) | copy-start | bytes 1179652
  43.8 1.2 %copy-start.13 = (f32[3,16,16,128]{3,2,1,0:T(8,128)S(1)}, f32[3,16,16,128]{3,2,1,0:T(8,128)}, u32[]{:S(2)}) copy-start(f32[3,16,16,128]{3,2,1,0:T(8,128)} %slice.1051) | copy-start | bytes 1179652
  43.8 1.2 %copy-start.14 = (f32[16,16,128]{2,1,0:T(8,128)S(1)}, f32[16,16,128]{2,1,0:T(8,128)}, u32[]{:S(2)}) copy-start(f32[16,16,128]{2,1,0:T(8,128)} %get-tuple-element.62) | copy-start | bytes 393220
  45.4 0.9 copy-start.6
  47.8 5.0 %collective-permute-start.11 = (f32[6,1,16,128]{3,2,1,0:T(8,128)S(1)}, f32[6,1,16,128]{3,2,1,0:T(8,128)S(1)}, u32[]{:S(2)}, u32[]{:S(2)}) collective-permute-start(f32[6,1,16,128]{3,2,1,0:T(8,128)S(1)} %get-tuple-element.54), channel_id=1, source_target_pairs={{0,4},{4,8},{8,12},{1,5},{5,9},{9,13},{2,6},{6,10},{10,14},{3,7},{... | collective-permute-start | bytes 147464 | tf_op jit(solution)/shard_map/ppermute | solution.py:33
  51.0 6.0 %collective-permute-start.10 = (f32[6,1,16,128]{3,2,1,0:T(8,128)S(1)}, f32[6,1,16,128]{3,2,1,0:T(8,128)S(1)}, u32[]{:S(2)}, u32[]{:S(2)}) collective-permute-start(f32[6,1,16,128]{3,2,1,0:T(8,128)S(1)} %get-tuple-element.55), channel_id=1, source_target_pairs={{4,0},{8,4},{12,8},{5,1},{9,5},{13,9},{6,2},{10,6},{14,10},{7,3},{... | collective-permute-start | bytes 147464 | tf_op jit(solution)/shard_map/ppermute | solution.py:34
  57.1 5.6 %copy-start.9 = (f32[3,16,16,128]{3,2,1,0:T(8,128)S(1)}, f32[3,16,16,128]{3,2,1,0:T(8,128)}, u32[]{:S(2)}) copy-start(f32[3,16,16,128]{3,2,1,0:T(8,128)} %get-tuple-element.23) | copy-start | bytes 1179652
  57.1 4.2 %collective-permute-start.12 = (f32[6,18,1,128]{3,2,1,0:T(1,128)S(1)}, f32[6,18,1,128]{3,2,1,0:T(1,128)S(1)}, u32[]{:S(2)}, u32[]{:S(2)}) collective-permute-start(f32[6,18,1,128]{3,2,1,0:T(1,128)S(1)} %broadcast_select_fusion.2), channel_id=1, source_target_pairs={{0,2},{2,0},{1,3},{3,1},{4,6},{6,4},{5,7},{7,5},{8,10},{10,8},{9,1... | collective-permute-start | bytes 165896 | tf_op jit(solution)/shard_map/ppermute | solution.py:26
  61.4 2.4 %copy-start.8 = (f32[3,16,16,128]{3,2,1,0:T(8,128)S(1)}, f32[3,16,16,128]{3,2,1,0:T(8,128)}, u32[]{:S(2)}) copy-start(f32[3,16,16,128]{3,2,1,0:T(8,128)} %get-tuple-element.22) | copy-start | bytes 1179652
  62.7 3.4 %collective-permute-start.13 = (f32[6,18,18,128]{3,2,1,0:T(8,128)}, f32[6,18,18,128]{3,2,1,0:T(8,128)}, u32[]{:S(2)}, u32[]{:S(2)}) collective-permute-start(f32[6,18,18,128]{3,2,1,0:T(8,128)} %pad_maximum_fusion.4), channel_id=1, source_target_pairs={{0,1},{1,0},{2,3},{3,2},{4,5},{5,4},{6,7},{7,6},{8,9},{9,8},{10,11... | collective-permute-start | bytes 2985992 | tf_op jit(solution)/shard_map/ppermute | solution.py:18
  73.1 1.0 %copy-start.11 = (bf16[6,16,16,128]{3,2,1,0:T(8,128)(2,1)S(1)}, bf16[6,16,16,128]{3,2,1,0:T(8,128)(2,1)}, u32[]{:S(2)}) copy-start(bf16[6,16,16,128]{3,2,1,0:T(8,128)(2,1)} %param.9) | copy-start | bytes 1179652
  73.1 1.0 %copy-start.15 = (f32[16,16,128]{2,1,0:T(8,128)S(1)}, f32[16,16,128]{2,1,0:T(8,128)}, u32[]{:S(2)}) copy-start(f32[16,16,128]{2,1,0:T(8,128)} %get-tuple-element.62) | copy-start | bytes 393220
  74.5 0.9 copy-start.4
  74.5 1.0 %copy-start.7 = (f32[16,16,128]{2,1,0:T(8,128)S(1)}, f32[16,16,128]{2,1,0:T(8,128)}, u32[]{:S(2)}) copy-start(f32[16,16,128]{2,1,0:T(8,128)} %copy-done.5) | copy-start | bytes 393220
  75.9 0.9 copy-start.19
  75.9 13.2 %copy-start.18 = (f32[12]{0:T(128)S(1)}, f32[12]{0:T(128)}, u32[]{:S(2)}) copy-start(f32[12]{0:T(128)} %copy-done.17) | copy-start | bytes 148
  75.9 13.6 %copy-start.2 = (f32[3,16,16,128]{3,2,1,0:T(8,128)S(1)}, f32[3,16,16,128]{3,2,1,0:T(8,128)}, u32[]{:S(2)}) copy-start(f32[3,16,16,128]{3,2,1,0:T(8,128)} %copy-done.1) | copy-start | bytes 1179652
  76.9 3.9 %collective-permute-start.16 = (f32[902]{0:T(1024)S(1)}, f32[902]{0:T(1024)S(1)}, u32[]{:S(2)}, u32[]{:S(2)}) collective-permute-start(f32[902]{0:T(1024)S(1)} %pad_maximum_fusion.17), channel_id=1, source_target_pairs={{0,3},{1,2},{2,1},{3,0},{4,7},{5,6},{6,5},{7,4},{8,11},{9,10},{10,... | collective-permute-start | bytes 10832 | tf_op jit(solution)/shard_map/ppermute | solution.py:137
  79.4 3.6 %collective-permute-start.15 = (f32[902]{0:T(1024)S(1)}, f32[902]{0:T(1024)S(1)}, u32[]{:S(2)}, u32[]{:S(2)}) collective-permute-start(f32[902]{0:T(1024)S(1)} %pad_maximum_fusion.17), channel_id=1, source_target_pairs={{0,2},{1,3},{2,0},{3,1},{4,6},{5,7},{6,4},{7,5},{8,10},{9,11},{10,... | collective-permute-start | bytes 10832 | tf_op jit(solution)/shard_map/ppermute | solution.py:137
  79.4 3.6 %collective-permute-start.14 = (f32[902]{0:T(1024)S(1)}, f32[902]{0:T(1024)S(1)}, u32[]{:S(2)}, u32[]{:S(2)}) collective-permute-start(f32[902]{0:T(1024)S(1)} %pad_maximum_fusion.17), channel_id=1, source_target_pairs={{0,1},{1,0},{2,3},{3,2},{4,5},{5,4},{6,7},{7,6},{8,9},{9,8},{10,11... | collective-permute-start | bytes 10832 | tf_op jit(solution)/shard_map/ppermute | solution.py:137
  83.0 5.5 %collective-permute-start.19 = (f32[902]{0:T(1024)S(1)}, f32[902]{0:T(1024)S(1)}, u32[]{:S(2)}, u32[]{:S(2)}) collective-permute-start(f32[902]{0:T(1024)S(1)} %add_add_fusion.3), channel_id=1, source_target_pairs={{0,12},{1,13},{2,14},{3,15},{4,8},{5,9},{6,10},{7,11},{8,4},{9,5},... | collective-permute-start | bytes 10832 | tf_op jit(solution)/shard_map/ppermute | solution.py:137
  83.8 4.7 %collective-permute-start.18 = (f32[902]{0:T(1024)S(1)}, f32[902]{0:T(1024)S(1)}, u32[]{:S(2)}, u32[]{:S(2)}) collective-permute-start(f32[902]{0:T(1024)S(1)} %add_add_fusion.3), channel_id=1, source_target_pairs={{0,8},{1,9},{2,10},{3,11},{4,12},{5,13},{6,14},{7,15},{8,0},{9,1},... | collective-permute-start | bytes 10832 | tf_op jit(solution)/shard_map/ppermute | solution.py:137
  85.4 3.7 %collective-permute-start.17 = (f32[902]{0:T(1024)S(1)}, f32[902]{0:T(1024)S(1)}, u32[]{:S(2)}, u32[]{:S(2)}) collective-permute-start(f32[902]{0:T(1024)S(1)} %add_add_fusion.3), channel_id=1, source_target_pairs={{0,4},{1,5},{2,6},{3,7},{4,0},{5,1},{6,2},{7,3},{8,12},{9,13},{10,... | collective-permute-start | bytes 10832 | tf_op jit(solution)/shard_map/ppermute | solution.py:137

commit v19 on v12

--- a/solution.py
+++ b/solution.py
@@ -233,7 +233,7 @@
     gain_total_imag = first[9:12]
     sweep_args = (lame_first, shear, density_cells, mask, source_cells, omega_sq, impedance)
     padded = with_halo(field, (("gx", 1), ("gy", 2)), 1)
-    padded = with_halo(padded, (("col", 3),), 1, 0.0 * rounds[0][0])
+    padded = with_halo(padded, (("col", 3),), 1)
     tied_source = source_cells + 0.0 * first[0]
     field = sweep(padded, lame_first, shear, density_cells, mask, tied_source, omega_sq, impedance)
     second_local = jnp.sum(mask * field, axis=(1, 2, 3))

time: 87.4 us -> 91.3 us (1.045)
  waiting for transfers between devices: 16.1 us -> 21 us
  other arithmetic: 30.4 us -> 32.4 us
  starting transfers between devices: 29.3 us -> 27.3 us
  local copies, waits for them, and re-layouts: 9.03 us -> 8 us
    ppermute x2, waiting for transfers between devices: 0.01 us -> 6.02 us  [with_halo(): after = lax.ppermute(initial, axis, down)]
    ppermute x2, starting transfers between devices: 10.3 us -> 7.31 us  [with_halo(): before = lax.ppermute(last, axis, up)]
    ppermute x2, waiting for transfers between devices: 3.5 us -> 5.4 us  [with_halo(): got = lax.ppermute(jnp.where(first, last, initial), axis, [(0, 1), (1, 0)])]
    select_n x2, other arithmetic: 2.64 us -> 4.4 us  [with_halo(): after = jnp.where(first, got_initial, zero)]
    ppermute x12, waiting for transfers between devices: 11 us -> 9.27 us  [group_rounds(): lax.ppermute(value, axes, [(i, i ^ m * stride) for i in range(size)])]
    ppermute x2, waiting for transfers between devices: 1.54 us -> 0.25 us  [with_halo(): before = lax.ppermute(last, axis, up)]
    concatenate x5 -> x6, other arithmetic: 5.97 us -> 7.24 us  [with_halo(): array = jnp.concatenate([before, array, after], axis=dim)]
    reduce_sum x1 -> x0, other arithmetic: 1.18 us -> none  [shards(): jnp.sum(mask * field, axis=(1, 2, 3))]
  transfers between devices with their start and end apart: 20 -> 20, of which waited for: 9 -> 12; matrix products, arithmetic and copies ran while one was open for 18% -> 18% of each run, Pallas kernels for 0% -> 0%
where the time goes in v19:
time: 91.3 us; the launch traced here: 90.6 us
  other arithmetic  32.4 us (35%)
  starting transfers between devices  27.3 us (30%)
  waiting for transfers between devices  21 us (23%)
  local copies, waits for them, and re-layouts  8 us (9%)
  between operations  1.94 us (2%)
    ppermute x12, starting transfers between devices, group_rounds(): lax.ppermute(value, axes, [(i, i ^ m * stride) for i in range(size)])  14.2 us
    ppermute x12, waiting for transfers between devices, group_rounds(): lax.ppermute(value, axes, [(i, i ^ m * stride) for i in range(size)])  9.27 us
    ppermute x2, starting transfers between devices, with_halo(): before = lax.ppermute(last, axis, up)  7.31 us
    concatenate x6, other arithmetic, with_halo(): array = jnp.concatenate([before, array, after], axis=dim)  7.24 us
    ppermute x2, waiting for transfers between devices, with_halo(): after = lax.ppermute(initial, axis, down)  6.02 us
    add x12, other arithmetic, navier(): result.append(shear * laplace[channel] + (lame_first + shear) * divergence)  5.61 us
    ppermute x2, waiting for transfers between devices, with_halo(): got = lax.ppermute(jnp.where(first, last, initial), axis, [(0, 1), (1, 0)])  5.4 us
    select_n x2, other arithmetic, with_halo(): after = jnp.where(first, got_initial, zero)  4.4 us
  transfers between devices with their start and end apart: 20, of which 12 were waited for; matrix products, arithmetic and copies ran while one was open for 18% of the time, Pallas kernels for 0%

profile of v19, /device:TPU:0, one launch (start us, length us, event | category | flops | bytes accessed | tf_op | source)
XLA Modules:
  0.0 90.6 jit_solution(2513580753744020147)
XLA Ops:
  0.6 0.8 fusion.107
  1.4 4.9 %collective-permute-start.7 = (f32[6,1,16,128]{3,2,1,0:T(8,128)S(1)}, f32[6,1,16,128]{3,2,1,0:T(8,128)S(1)}, u32[]{:S(2)}, u32[]{:S(2)}) collective-permute-start(f32[6,1,16,128]{3,2,1,0:T(8,128)S(1)} %get-tuple-element.63), channel_id=1, source_target_pairs={{0,4},{4,8},{8,12},{1,5},{5,9},{9,13},{2,6},{6,10},{10,14},{3,7},{... | collective-permute-start | bytes 147464 | tf_op jit(solution)/shard_map/ppermute | solution.py:33
  6.3 1.3 %collective-permute-start.6 = (f32[6,1,16,128]{3,2,1,0:T(8,128)S(1)}, f32[6,1,16,128]{3,2,1,0:T(8,128)S(1)}, u32[]{:S(2)}, u32[]{:S(2)}) collective-permute-start(f32[6,1,16,128]{3,2,1,0:T(8,128)S(1)} %get-tuple-element.64), channel_id=1, source_target_pairs={{4,0},{8,4},{12,8},{5,1},{9,5},{13,9},{6,2},{10,6},{14,10},{7,3},{... | collective-permute-start | bytes 147464 | tf_op jit(solution)/shard_map/ppermute | solution.py:34
  7.7 0.8 slice_bitcast_fusion.2
  8.4 0.8 select_reduce_fusion.1
  9.5 1.1 %convert_element_type.12 = f32[6,16,16,128]{3,2,1,0:T(8,128)S(1)} convert(bf16[6,16,16,128]{3,2,1,0:T(8,128)(2,1)} %param.10) | non-fusion elementwise | flops 196608 | bytes 1179648 | tf_op jit(solution)/shard_map/convert_element_type | solution.py:219
  10.6 1.7 %collective-permute-done.6 = f32[6,1,16,128]{3,2,1,0:T(8,128)S(1)} collective-permute-done((f32[6,1,16,128]{3,2,1,0:T(8,128)S(1)}, f32[6,1,16,128]{3,2,1,0:T(8,128)S(1)}, u32[]{:S(2)}, u32[]{:S(2)}) %collective-permute-start.6) | collective-permute-done | bytes 49184 | tf_op jit(solution)/shard_map/ppermute | solution.py:34
  12.4 1.6 %collective-permute-start.8 = (f32[6,18,1,128]{3,2,1,0:T(1,128)S(1)}, f32[6,18,1,128]{3,2,1,0:T(1,128)S(1)}, u32[]{:S(2)}, u32[]{:S(2)}) collective-permute-start(f32[6,18,1,128]{3,2,1,0:T(1,128)S(1)} %broadcast_select_fusion.5), channel_id=1, source_target_pairs={{0,2},{2,0},{1,3},{3,1},{4,6},{6,4},{5,7},{7,5},{8,10},{10,8},{9,1... | collective-permute-start | bytes 165896 | tf_op jit(solution)/shard_map/ppermute | solution.py:26
  14.0 2.7 %collective-permute-done.8 = f32[6,18,1,128]{3,2,1,0:T(1,128)S(1)} collective-permute-done((f32[6,18,1,128]{3,2,1,0:T(1,128)S(1)}, f32[6,18,1,128]{3,2,1,0:T(1,128)S(1)}, u32[]{:S(2)}, u32[]{:S(2)}) %collective-permute-start.8) | collective-permute-done | bytes 55328 | tf_op jit(solution)/shard_map/ppermute | solution.py:26
  16.7 1.3 %pad_maximum_fusion.3 = f32[6,18,18,128]{3,2,1,0:T(8,128)} fusion(f32[6,18,1,128]{3,2,1,0:T(1,128)S(1)} %get-tuple-element.71, f32[6,1,16,128]{3,2,1,0:T(8,128)S(1)} %collective-permute-done.6, f32[6,16,16,128]{3,2,1,0:T(8,128)S(1)} %convert_element_type.12, f32[6,1,16,128]{3,2,1,0:T(8,128)S(1)} %collective-permute-done.7, ...), kind=kLoop, calls=%fused_computation.11 | loop fusion | flops 995328 | bytes 1990656 | tf_op jit(solution)/shard_map/concatenate | solution.py:35
  18.8 1.5 %scatter_custom_fusion = f32[32768]{0:T(1024)S(1)} fusion(s32[256]{0:T(256)S(1)} %bitcast.45, f32[256]{0:T(256)S(1)} %broadcast.308, f32[]{:T(128)} %constant.27.clone.1), kind=kCustom, calls=%fused_computation.245 | custom fusion | bytes 131076 | tf_op jit(solution)/shard_map/scatter | solution.py:187
  20.4 1.4 %multiply_subtract_fusion = (f32[3,16,16,128]{3,2,1,0:T(8,128)}, f32[3,16,16,128]{3,2,1,0:T(8,128)}, f32[3,16,16,128]{3,2,1,0:T(8,128)}, f32[3,16,16,128]{3,2,1,0:T(8,128)S(1)}, f32[3,16,16,128]{3,2,1,0:T(8,128)S(1)}) fusion(f32[6,16,16,128]{3,2,1,0:T(8,128)S(1)} %convert_element_type.15, f32[3]{0:T(128)S(1)} %get-tuple-element.79, ...), kind=kLoop, calls=%fused_computation.64 | loop fusion | flops 2359296 | bytes 3276824 | tf_op jit(solution)/shard_map/sub | solution.py:216
  22.3 2.2 %slice_select_fusion.3 = (f32[6,18,18,1]{3,2,1,0:T(8,128)S(1)}, f32[6,18,18,1]{3,2,1,0:T(8,128)S(1)}) fusion(f32[6,18,18,128]{3,2,1,0:T(8,128)} %collective-permute-done.9, pred[]{:T(512)S(6)} %eq.67), kind=kLoop, calls=%fused_computation.8 | loop fusion | flops 3888 | bytes 31105 | tf_op jit(solution)/shard_map/jit(_where)/select_n | solution.py:23
  24.5 2.1 %pad_maximum_fusion = (f32[6,18,18,129]{3,2,1,0:T(8,128)S(1)}, f32[6,18,18,129]{3,2,1,0:T(8,128)S(1)}) fusion(f32[6,18,18,1]{3,2,1,0:T(8,128)S(1)} %get-tuple-element.48, f32[6,18,1,128]{3,2,1,0:T(1,128)S(1)} %get-tuple-element.71, f32[6,1,16,128]{3,2,1,0:T(8,128)S(1)} %collective-permute-done.6, f32[6,16,16,128]{3,2,1,0:T(8,128)S(1)} %convert_element_type.12, ...), kind=kLoop, calls=%fused_computation.1 | loop fusion | flops 2507760 | bytes 3017088 | tf_op jit(solution)/shard_map/concatenate | solution.py:35
  26.6 0.7 add_add_fusion.1
  27.4 1.6 %collective-permute-start.2 = (f32[12]{0:T(128)S(1)}, f32[12]{0:T(128)S(1)}, u32[]{:S(2)}, u32[]{:S(2)}) collective-permute-start(f32[12]{0:T(128)S(1)} %pad_maximum_fusion.18), channel_id=1, source_target_pairs={{0,3},{1,2},{2,1},{3,0},{4,7},{5,6},{6,5},{7,4},{8,11},{9,10},{10,... | collective-permute-start | bytes 152 | tf_op jit(solution)/shard_map/ppermute | solution.py:145
  30.3 0.7 fusion.64
  32.5 3.0 %collective-permute-start.5 = (f32[12]{0:T(128)S(1)}, f32[12]{0:T(128)S(1)}, u32[]{:S(2)}, u32[]{:S(2)}) collective-permute-start(f32[12]{0:T(128)S(1)} %add_add_fusion.6), channel_id=1, source_target_pairs={{0,12},{1,13},{2,14},{3,15},{4,8},{5,9},{6,10},{7,11},{8,4},{9,5},... | collective-permute-start | bytes 152 | tf_op jit(solution)/shard_map/ppermute | solution.py:145
  35.6 1.3 %collective-permute-start.3 = (f32[12]{0:T(128)S(1)}, f32[12]{0:T(128)S(1)}, u32[]{:S(2)}, u32[]{:S(2)}) collective-permute-start(f32[12]{0:T(128)S(1)} %add_add_fusion.6), channel_id=1, source_target_pairs={{0,4},{1,5},{2,6},{3,7},{4,0},{5,1},{6,2},{7,3},{8,12},{9,13},{10,... | collective-permute-start | bytes 152 | tf_op jit(solution)/shard_map/ppermute | solution.py:145
  37.0 0.9 %collective-permute-done.5 = f32[12]{0:T(128)S(1)} collective-permute-done((f32[12]{0:T(128)S(1)}, f32[12]{0:T(128)S(1)}, u32[]{:S(2)}, u32[]{:S(2)}) %collective-permute-start.5) | collective-permute-done | bytes 80 | tf_op jit(solution)/shard_map/ppermute | solution.py:145
  37.9 2.1 %collective-permute-done.4 = f32[12]{0:T(128)S(1)} collective-permute-done((f32[12]{0:T(128)S(1)}, f32[12]{0:T(128)S(1)}, u32[]{:S(2)}, u32[]{:S(2)}) %collective-permute-start.4) | collective-permute-done | bytes 80 | tf_op jit(solution)/shard_map/ppermute | solution.py:145
  41.1 0.8 multiply_reduce_fusion
  41.9 2.4 %collective-permute-start.11 = (f32[6,1,16,128]{3,2,1,0:T(8,128)S(1)}, f32[6,1,16,128]{3,2,1,0:T(8,128)S(1)}, u32[]{:S(2)}, u32[]{:S(2)}) collective-permute-start(f32[6,1,16,128]{3,2,1,0:T(8,128)S(1)} %get-tuple-element.60), channel_id=1, source_target_pairs={{0,4},{4,8},{8,12},{1,5},{5,9},{9,13},{2,6},{6,10},{10,14},{3,7},{... | collective-permute-start | bytes 147464 | tf_op jit(solution)/shard_map/ppermute | solution.py:33
  44.3 1.5 %collective-permute-start.10 = (f32[6,1,16,128]{3,2,1,0:T(8,128)S(1)}, f32[6,1,16,128]{3,2,1,0:T(8,128)S(1)}, u32[]{:S(2)}, u32[]{:S(2)}) collective-permute-start(f32[6,1,16,128]{3,2,1,0:T(8,128)S(1)} %get-tuple-element.61), channel_id=1, source_target_pairs={{4,0},{8,4},{12,8},{5,1},{9,5},{13,9},{6,2},{10,6},{14,10},{7,3},{... | collective-permute-start | bytes 147464 | tf_op jit(solution)/shard_map/ppermute | solution.py:34
  46.0 4.3 %collective-permute-done.10 = f32[6,1,16,128]{3,2,1,0:T(8,128)S(1)} collective-permute-done((f32[6,1,16,128]{3,2,1,0:T(8,128)S(1)}, f32[6,1,16,128]{3,2,1,0:T(8,128)S(1)}, u32[]{:S(2)}, u32[]{:S(2)}) %collective-permute-start.10) | collective-permute-done | bytes 49184 | tf_op jit(solution)/shard_map/ppermute | solution.py:34
  50.4 1.5 %collective-permute-start.12 = (f32[6,18,1,128]{3,2,1,0:T(1,128)S(1)}, f32[6,18,1,128]{3,2,1,0:T(1,128)S(1)}, u32[]{:S(2)}, u32[]{:S(2)}) collective-permute-start(f32[6,18,1,128]{3,2,1,0:T(1,128)S(1)} %broadcast_select_fusion.2), channel_id=1, source_target_pairs={{0,2},{2,0},{1,3},{3,1},{4,6},{6,4},{5,7},{7,5},{8,10},{10,8},{9,1... | collective-permute-start | bytes 165896 | tf_op jit(solution)/shard_map/ppermute | solution.py:26
  51.9 2.7 %collective-permute-done.12 = f32[6,18,1,128]{3,2,1,0:T(1,128)S(1)} collective-permute-done((f32[6,18,1,128]{3,2,1,0:T(1,128)S(1)}, f32[6,18,1,128]{3,2,1,0:T(1,128)S(1)}, u32[]{:S(2)}, u32[]{:S(2)}) %collective-permute-start.12) | collective-permute-done | bytes 55328 | tf_op jit(solution)/shard_map/ppermute | solution.py:26
  54.7 1.3 %pad_maximum_fusion.5 = f32[6,18,18,128]{3,2,1,0:T(8,128)} fusion(f32[6,18,1,128]{3,2,1,0:T(1,128)S(1)} %get-tuple-element.69, f32[6,1,16,128]{3,2,1,0:T(8,128)S(1)} %collective-permute-done.10, f32[6,16,16,128]{3,2,1,0:T(8,128)S(1)} %get-tuple-element.59, f32[6,1,16,128]{3,2,1,0:T(8,128)S(1)} %collective-permute-done.11, ...), kind=kLoop, calls=%fused_computation.14 | loop fusion | flops 995328 | bytes 1990656 | tf_op jit(solution)/shard_map/concatenate | solution.py:35
  56.0 0.9 %convert_element_type.13 = f32[6,16,16,128]{3,2,1,0:T(8,128)} convert(bf16[6,16,16,128]{3,2,1,0:T(8,128)(2,1)S(1)} %copy-done.3) | non-fusion elementwise | flops 196608 | bytes 1179648 | tf_op jit(solution)/shard_map/convert_element_type | solution.py:192
  57.0 1.2 %multiply_add_fusion = f32[3,16,16,128]{3,2,1,0:T(8,128)S(1)} fusion(f32[3,16,16,128]{3,2,1,0:T(8,128)} %get-tuple-element.25, f32[3,16,16,128]{3,2,1,0:T(8,128)} %get-tuple-element.24), kind=kLoop, calls=%fused_computation.63 | loop fusion | flops 196608 | bytes 1179648 | tf_op jit(solution)/shard_map/add | solution.py:217
  58.2 0.9 maximum_reduce_fusion
  59.1 0.9 %reduce_sum.115 = f32[6,4,4,4,4]{4,3,2,1,0:T(4,128)S(1)} reshape(f32[6,16,16]{2,1,0:T(8,128)} %maximum_reduce_fusion) | data formatting | bytes 12288 | tf_op jit(solution)/shard_map/reduce_sum | solution.py:207
  60.0 0.7 reduce_sum.116
  60.8 1.7 %dynamic_update_slice.7 = f32[6,16,8]{2,1,0:T(8,128)S(1)} dynamic-update-slice(f32[6,16,8]{2,1,0:T(8,128)S(1)} %broadcast_in_dim.188, f32[6,4,4]{2,1,0:T(4,128)} %reduce_sum.116, s32[]{:T(128)} %constant.28.clone.1, s32[]{:T(128)S(6)} %select_n.188, s32[]{:T(128)S(6)} %select_n.189) | dynamic-update-slice | bytes 772 | tf_op jit(solution)/shard_map/dynamic_update_slice | solution.py:209
  62.8 2.2 %slice_select_fusion.1 = (f32[6,18,18,1]{3,2,1,0:T(8,128)S(1)}, f32[6,18,18,1]{3,2,1,0:T(8,128)S(1)}) fusion(f32[6,18,18,128]{3,2,1,0:T(8,128)} %collective-permute-done.13, pred[]{:T(512)S(6)} %eq.67), kind=kLoop, calls=%fused_computation.6 | loop fusion | flops 3888 | bytes 31105 | tf_op jit(solution)/shard_map/jit(_where)/select_n | solution.py:23
  65.0 2.1 %pad_maximum_fusion.1 = (f32[6,18,18,129]{3,2,1,0:T(8,128)S(1)}, f32[6,18,18,129]{3,2,1,0:T(8,128)S(1)}) fusion(f32[6,18,18,1]{3,2,1,0:T(8,128)S(1)} %get-tuple-element.46, f32[6,18,1,128]{3,2,1,0:T(1,128)S(1)} %get-tuple-element.69, f32[6,1,16,128]{3,2,1,0:T(8,128)S(1)} %collective-permute-done.10, f32[6,16,16,128]{3,2,1,0:T(8,128)S(1)} %get-tuple-element.59, ...), kind=kLoop, calls=%fused_computation.3 | loop fusion | flops 2507760 | bytes 3017088 | tf_op jit(solution)/shard_map/concatenate | solution.py:35
  69.9 0.7 fusion.28
  71.3 1.2 %subtract_reduce_fusion = (f32[16,16,128]{2,1,0:T(8,128)S(1)}, f32[3,16,16,128]{3,2,1,0:T(8,128)S(1)}, f32[3,16,16,128]{3,2,1,0:T(8,128)}) fusion(f32[6,16,16,128]{3,2,1,0:T(8,128)S(1)} %convert_element_type.15, f32[3,16,16,128]{3,2,1,0:T(8,128)S(1)} %get-tuple-element.45, f32[3]{0:T(128)S(1)} %copy-done.9, f32[16,16,128]{2,1,0:T(8,128)S(1)} %get-tuple-element.67, ...), kind=kLoop, calls=%fused_computation.67 | loop fusion | flops 2719744 | bytes 3670040 | tf_op jit(solution)/shard_map/reduce_sum | solution.py:248
  73.3 3.0 %collective-permute-start.16 = (f32[902]{0:T(1024)S(1)}, f32[902]{0:T(1024)S(1)}, u32[]{:S(2)}, u32[]{:S(2)}) collective-permute-start(f32[902]{0:T(1024)S(1)} %pad_maximum_fusion.17), channel_id=1, source_target_pairs={{0,3},{1,2},{2,1},{3,0},{4,7},{5,6},{6,5},{7,4},{8,11},{9,10},{10,... | collective-permute-start | bytes 10832 | tf_op jit(solution)/shard_map/ppermute | solution.py:145
  76.5 1.1 %collective-permute-done.16 = f32[902]{0:T(1024)S(1)} collective-permute-done((f32[902]{0:T(1024)S(1)}, f32[902]{0:T(1024)S(1)}, u32[]{:S(2)}, u32[]{:S(2)}) %collective-permute-start.16) | collective-permute-done | bytes 3640 | tf_op jit(solution)/shard_map/ppermute | solution.py:145
  77.6 2.3 %collective-permute-done.15 = f32[902]{0:T(1024)S(1)} collective-permute-done((f32[902]{0:T(1024)S(1)}, f32[902]{0:T(1024)S(1)}, u32[]{:S(2)}, u32[]{:S(2)}) %collective-permute-start.15) | collective-permute-done | bytes 3640 | tf_op jit(solution)/shard_map/ppermute | solution.py:145
  79.9 0.7 collective-permute-start.19
  80.7 2.8 %collective-permute-start.18 = (f32[902]{0:T(1024)S(1)}, f32[902]{0:T(1024)S(1)}, u32[]{:S(2)}, u32[]{:S(2)}) collective-permute-start(f32[902]{0:T(1024)S(1)} %add_add_fusion.3), channel_id=1, source_target_pairs={{0,8},{1,9},{2,10},{3,11},{4,12},{5,13},{6,14},{7,15},{8,0},{9,1},... | collective-permute-start | bytes 10832 | tf_op jit(solution)/shard_map/ppermute | solution.py:145
  83.5 0.9 %collective-permute-start.17 = (f32[902]{0:T(1024)S(1)}, f32[902]{0:T(1024)S(1)}, u32[]{:S(2)}, u32[]{:S(2)}) collective-permute-start(f32[902]{0:T(1024)S(1)} %add_add_fusion.3), channel_id=1, source_target_pairs={{0,4},{1,5},{2,6},{3,7},{4,0},{5,1},{6,2},{7,3},{8,12},{9,13},{10,... | collective-permute-start | bytes 10832 | tf_op jit(solution)/shard_map/ppermute | solution.py:145
  84.4 1.0 %collective-permute-done.19 = f32[902]{0:T(1024)S(1)} collective-permute-done((f32[902]{0:T(1024)S(1)}, f32[902]{0:T(1024)S(1)}, u32[]{:S(2)}, u32[]{:S(2)}) %collective-permute-start.19) | collective-permute-done | bytes 3640 | tf_op jit(solution)/shard_map/ppermute | solution.py:145
  85.4 1.7 %collective-permute-done.17 = f32[902]{0:T(1024)S(1)} collective-permute-done((f32[902]{0:T(1024)S(1)}, f32[902]{0:T(1024)S(1)}, u32[]{:S(2)}, u32[]{:S(2)}) %collective-permute-start.17) | collective-permute-done | bytes 3640 | tf_op jit(solution)/shard_map/ppermute | solution.py:145
  87.9 0.7 copy.14
  88.6 2.0 %fusion.13 = f32[6,16,16,128]{3,2,1,0:T(8,128)} fusion(f32[3,16,16,128]{3,2,1,0:T(8,128)S(1)} %get-tuple-element.27, f32[3,16,16,128]{3,2,1,0:T(8,128)S(1)} %get-tuple-element.26, f32[3,16,16,128]{3,2,1,0:T(8,128)} %get-tuple-element.22, f32[3,16,16,128]{3,2,1,0:T(8,128)S(1)} %get-tuple-element.21, f32[6]{0:T(128)S(1)} %pad_maximum_fusion.20, ...), kind=kLoop, calls=%fused_computation.38 | loop fusion | flops 1376256 | bytes 2359344 | tf_op jit(solution)/shard_map/add | solution.py:131
  (116 shorter events, 11.0 us)
Async XLA Ops:
  0.6 13.3 %copy-start.15 = (s32[1,256]{1,0:T(1,128)S(1)}, s32[1,256]{1,0:T(1,128)}, u32[]{:S(2)}) copy-start(s32[1,256]{1,0:T(1,128)} %param.15) | copy-start | bytes 3076
  1.4 9.2 %collective-permute-start.7 = (f32[6,1,16,128]{3,2,1,0:T(8,128)S(1)}, f32[6,1,16,128]{3,2,1,0:T(8,128)S(1)}, u32[]{:S(2)}, u32[]{:S(2)}) collective-permute-start(f32[6,1,16,128]{3,2,1,0:T(8,128)S(1)} %get-tuple-element.63), channel_id=1, source_target_pairs={{0,4},{4,8},{8,12},{1,5},{5,9},{9,13},{2,6},{6,10},{10,14},{3,7},{... | collective-permute-start | bytes 147464 | tf_op jit(solution)/shard_map/ppermute | solution.py:33
  6.3 6.0 %collective-permute-start.6 = (f32[6,1,16,128]{3,2,1,0:T(8,128)S(1)}, f32[6,1,16,128]{3,2,1,0:T(8,128)S(1)}, u32[]{:S(2)}, u32[]{:S(2)}) collective-permute-start(f32[6,1,16,128]{3,2,1,0:T(8,128)S(1)} %get-tuple-element.64), channel_id=1, source_target_pairs={{4,0},{8,4},{12,8},{5,1},{9,5},{13,9},{6,2},{10,6},{14,10},{7,3},{... | collective-permute-start | bytes 147464 | tf_op jit(solution)/shard_map/ppermute | solution.py:34
  12.4 5.6 %copy-start.16 = (f32[2,3]{1,0:T(2,128)S(1)}, f32[2,3]{1,0:T(2,128)}, u32[]{:S(2)}) copy-start(f32[2,3]{1,0:T(2,128)} %param.16) | copy-start | bytes 76
  12.4 6.3 %copy-start.4 = (bf16[6,16,16,128]{3,2,1,0:T(8,128)(2,1)S(1)}, bf16[6,16,16,128]{3,2,1,0:T(8,128)(2,1)}, u32[]{:S(2)}) copy-start(bf16[6,16,16,128]{3,2,1,0:T(8,128)(2,1)} %param.11) | copy-start | bytes 1179652
  12.4 4.2 %collective-permute-start.8 = (f32[6,18,1,128]{3,2,1,0:T(1,128)S(1)}, f32[6,18,1,128]{3,2,1,0:T(1,128)S(1)}, u32[]{:S(2)}, u32[]{:S(2)}) collective-permute-start(f32[6,18,1,128]{3,2,1,0:T(1,128)S(1)} %broadcast_select_fusion.5), channel_id=1, source_target_pairs={{0,2},{2,0},{1,3},{3,1},{4,6},{6,4},{5,7},{7,5},{8,10},{10,8},{9,1... | collective-permute-start | bytes 165896 | tf_op jit(solution)/shard_map/ppermute | solution.py:26
  18.0 2.3 %copy-start.5 = (bf16[16,16,128]{2,1,0:T(8,128)(2,1)S(1)}, bf16[16,16,128]{2,1,0:T(8,128)(2,1)}, u32[]{:S(2)}) copy-start(bf16[16,16,128]{2,1,0:T(8,128)(2,1)} %param.12) | copy-start | bytes 196612
  18.0 4.2 %collective-permute-start.9 = (f32[6,18,18,128]{3,2,1,0:T(8,128)}, f32[6,18,18,128]{3,2,1,0:T(8,128)}, u32[]{:S(2)}, u32[]{:S(2)}) collective-permute-start(f32[6,18,18,128]{3,2,1,0:T(8,128)} %pad_maximum_fusion.3), channel_id=1, source_target_pairs={{0,1},{1,0},{2,3},{3,2},{4,5},{5,4},{6,7},{7,6},{8,9},{9,8},{10,11... | collective-permute-start | bytes 2985992 | tf_op jit(solution)/shard_map/ppermute | solution.py:18
  18.0 22.8 %copy-start.6 = (f32[3]{0:T(128)}, f32[3]{0:T(128)S(1)}, u32[]{:S(2)}) copy-start(f32[3]{0:T(128)S(1)} %get-tuple-element.78) | copy-start | bytes 40
  18.0 22.8 %copy-start.8 = (f32[3]{0:T(128)}, f32[3]{0:T(128)S(1)}, u32[]{:S(2)}) copy-start(f32[3]{0:T(128)S(1)} %get-tuple-element.79) | copy-start | bytes 40
  24.5 2.1 %copy-start.1 = (bf16[6,16,16,128]{3,2,1,0:T(8,128)(2,1)S(1)}, bf16[6,16,16,128]{3,2,1,0:T(8,128)(2,1)}, u32[]{:S(2)}) copy-start(bf16[6,16,16,128]{3,2,1,0:T(8,128)(2,1)} %param.10) | copy-start | bytes 1179652
  27.4 5.0 %collective-permute-start.2 = (f32[12]{0:T(128)S(1)}, f32[12]{0:T(128)S(1)}, u32[]{:S(2)}, u32[]{:S(2)}) collective-permute-start(f32[12]{0:T(128)S(1)} %pad_maximum_fusion.18), channel_id=1, source_target_pairs={{0,3},{1,2},{2,1},{3,0},{4,7},{5,6},{6,5},{7,4},{8,11},{9,10},{10,... | collective-permute-start | bytes 152 | tf_op jit(solution)/shard_map/ppermute | solution.py:145
  29.0 3.5 %collective-permute-start.1 = (f32[12]{0:T(128)S(1)}, f32[12]{0:T(128)S(1)}, u32[]{:S(2)}, u32[]{:S(2)}) collective-permute-start(f32[12]{0:T(128)S(1)} %pad_maximum_fusion.18), channel_id=1, source_target_pairs={{0,2},{1,3},{2,0},{3,1},{4,6},{5,7},{6,4},{7,5},{8,10},{9,11},{10,... | collective-permute-start | bytes 152 | tf_op jit(solution)/shard_map/ppermute | solution.py:145
  29.5 3.0 %collective-permute-start = (f32[12]{0:T(128)S(1)}, f32[12]{0:T(128)S(1)}, u32[]{:S(2)}, u32[]{:S(2)}) collective-permute-start(f32[12]{0:T(128)S(1)} %pad_maximum_fusion.18), channel_id=1, source_target_pairs={{0,1},{1,0},{2,3},{3,2},{4,5},{5,4},{6,7},{7,6},{8,9},{9,8},{10,11... | collective-permute-start | bytes 152 | tf_op jit(solution)/shard_map/ppermute | solution.py:145
  32.0 8.3 %copy-start.3 = (bf16[6,16,16,128]{3,2,1,0:T(8,128)(2,1)S(1)}, bf16[6,16,16,128]{3,2,1,0:T(8,128)(2,1)}, u32[]{:S(2)}) copy-start(bf16[6,16,16,128]{3,2,1,0:T(8,128)(2,1)} %param.9) | copy-start | bytes 1179652
  32.5 5.4 %collective-permute-start.5 = (f32[12]{0:T(128)S(1)}, f32[12]{0:T(128)S(1)}, u32[]{:S(2)}, u32[]{:S(2)}) collective-permute-start(f32[12]{0:T(128)S(1)} %add_add_fusion.6), channel_id=1, source_target_pairs={{0,12},{1,13},{2,14},{3,15},{4,8},{5,9},{6,10},{7,11},{8,4},{9,5},... | collective-permute-start | bytes 152 | tf_op jit(solution)/shard_map/ppermute | solution.py:145
  35.6 4.4 %collective-permute-start.4 = (f32[12]{0:T(128)S(1)}, f32[12]{0:T(128)S(1)}, u32[]{:S(2)}, u32[]{:S(2)}) collective-permute-start(f32[12]{0:T(128)S(1)} %add_add_fusion.6), channel_id=1, source_target_pairs={{0,8},{1,9},{2,10},{3,11},{4,12},{5,13},{6,14},{7,15},{8,0},{9,1},... | collective-permute-start | bytes 152 | tf_op jit(solution)/shard_map/ppermute | solution.py:145
  35.6 4.4 %collective-permute-start.3 = (f32[12]{0:T(128)S(1)}, f32[12]{0:T(128)S(1)}, u32[]{:S(2)}, u32[]{:S(2)}) collective-permute-start(f32[12]{0:T(128)S(1)} %add_add_fusion.6), channel_id=1, source_target_pairs={{0,4},{1,5},{2,6},{3,7},{4,0},{5,1},{6,2},{7,3},{8,12},{9,13},{10,... | collective-permute-start | bytes 152 | tf_op jit(solution)/shard_map/ppermute | solution.py:145
  40.0 0.8 copy-start.12
  40.0 1.1 %copy-start.10 = (f32[6]{0:T(128)}, f32[6]{0:T(128)S(1)}, u32[]{:S(2)}) copy-start(f32[6]{0:T(128)S(1)} %slice_multiply_fusion.12) | copy-start | bytes 76
  41.9 4.1 %collective-permute-start.11 = (f32[6,1,16,128]{3,2,1,0:T(8,128)S(1)}, f32[6,1,16,128]{3,2,1,0:T(8,128)S(1)}, u32[]{:S(2)}, u32[]{:S(2)}) collective-permute-start(f32[6,1,16,128]{3,2,1,0:T(8,128)S(1)} %get-tuple-element.60), channel_id=1, source_target_pairs={{0,4},{4,8},{8,12},{1,5},{5,9},{9,13},{2,6},{6,10},{10,14},{3,7},{... | collective-permute-start | bytes 147464 | tf_op jit(solution)/shard_map/ppermute | solution.py:33
  44.3 6.1 %collective-permute-start.10 = (f32[6,1,16,128]{3,2,1,0:T(8,128)S(1)}, f32[6,1,16,128]{3,2,1,0:T(8,128)S(1)}, u32[]{:S(2)}, u32[]{:S(2)}) collective-permute-start(f32[6,1,16,128]{3,2,1,0:T(8,128)S(1)} %get-tuple-element.61), channel_id=1, source_target_pairs={{4,0},{8,4},{12,8},{5,1},{9,5},{13,9},{6,2},{10,6},{14,10},{7,3},{... | collective-permute-start | bytes 147464 | tf_op jit(solution)/shard_map/ppermute | solution.py:34
  50.4 4.2 %collective-permute-start.12 = (f32[6,18,1,128]{3,2,1,0:T(1,128)S(1)}, f32[6,18,1,128]{3,2,1,0:T(1,128)S(1)}, u32[]{:S(2)}, u32[]{:S(2)}) collective-permute-start(f32[6,18,1,128]{3,2,1,0:T(1,128)S(1)} %broadcast_select_fusion.2), channel_id=1, source_target_pairs={{0,2},{2,0},{1,3},{3,1},{4,6},{6,4},{5,7},{7,5},{8,10},{10,8},{9,1... | collective-permute-start | bytes 165896 | tf_op jit(solution)/shard_map/ppermute | solution.py:26
  56.0 6.7 %collective-permute-start.13 = (f32[6,18,18,128]{3,2,1,0:T(8,128)}, f32[6,18,18,128]{3,2,1,0:T(8,128)}, u32[]{:S(2)}, u32[]{:S(2)}) collective-permute-start(f32[6,18,18,128]{3,2,1,0:T(8,128)} %pad_maximum_fusion.5), channel_id=1, source_target_pairs={{0,1},{1,0},{2,3},{3,2},{4,5},{5,4},{6,7},{7,6},{8,9},{9,8},{10,11... | collective-permute-start | bytes 2985992 | tf_op jit(solution)/shard_map/ppermute | solution.py:18
  57.0 1.2 %copy-start.2 = (f32[3,16,16,128]{3,2,1,0:T(8,128)S(1)}, f32[3,16,16,128]{3,2,1,0:T(8,128)}, u32[]{:S(2)}) copy-start(f32[3,16,16,128]{3,2,1,0:T(8,128)} %get-tuple-element.23) | copy-start | bytes 1179652
  69.8 1.1 %copy-start = (f32[6,16,16,128]{3,2,1,0:T(8,128)S(1)}, f32[6,16,16,128]{3,2,1,0:T(8,128)}, u32[]{:S(2)}) copy-start(f32[6,16,16,128]{3,2,1,0:T(8,128)} %convert_element_type.13) | copy-start | bytes 2359300
  69.9 1.1 %copy-start.7 = (f32[3]{0:T(128)S(1)}, f32[3]{0:T(128)}, u32[]{:S(2)}) copy-start(f32[3]{0:T(128)} %copy-done.6) | copy-start | bytes 40
  69.9 1.1 %copy-start.9 = (f32[3]{0:T(128)S(1)}, f32[3]{0:T(128)}, u32[]{:S(2)}) copy-start(f32[3]{0:T(128)} %copy-done.8) | copy-start | bytes 40
  71.3 2.0 %copy-start.14 = (f32[6]{0:T(128)S(1)}, f32[6]{0:T(128)}, u32[]{:S(2)}) copy-start(f32[6]{0:T(128)} %get-tuple-element.58) | copy-start | bytes 76
  71.3 15.8 %copy-start.11 = (f32[6]{0:T(128)S(1)}, f32[6]{0:T(128)}, u32[]{:S(2)}) copy-start(f32[6]{0:T(128)} %copy-done.10) | copy-start | bytes 76
  71.3 15.8 %copy-start.13 = (f32[12]{0:T(128)S(1)}, f32[12]{0:T(128)}, u32[]{:S(2)}) copy-start(f32[12]{0:T(128)} %copy-done.12) | copy-start | bytes 148
  73.3 4.3 %collective-permute-start.16 = (f32[902]{0:T(1024)S(1)}, f32[902]{0:T(1024)S(1)}, u32[]{:S(2)}, u32[]{:S(2)}) collective-permute-start(f32[902]{0:T(1024)S(1)} %pad_maximum_fusion.17), channel_id=1, source_target_pairs={{0,3},{1,2},{2,1},{3,0},{4,7},{5,6},{6,5},{7,4},{8,11},{9,10},{10,... | collective-permute-start | bytes 10832 | tf_op jit(solution)/shard_map/ppermute | solution.py:145
  76.3 3.6 %collective-permute-start.15 = (f32[902]{0:T(1024)S(1)}, f32[902]{0:T(1024)S(1)}, u32[]{:S(2)}, u32[]{:S(2)}) collective-permute-start(f32[902]{0:T(1024)S(1)} %pad_maximum_fusion.17), channel_id=1, source_target_pairs={{0,2},{1,3},{2,0},{3,1},{4,6},{5,7},{6,4},{7,5},{8,10},{9,11},{10,... | collective-permute-start | bytes 10832 | tf_op jit(solution)/shard_map/ppermute | solution.py:145
  76.3 3.6 %collective-permute-start.14 = (f32[902]{0:T(1024)S(1)}, f32[902]{0:T(1024)S(1)}, u32[]{:S(2)}, u32[]{:S(2)}) collective-permute-start(f32[902]{0:T(1024)S(1)} %pad_maximum_fusion.17), channel_id=1, source_target_pairs={{0,1},{1,0},{2,3},{3,2},{4,5},{5,4},{6,7},{7,6},{8,9},{9,8},{10,11... | collective-permute-start | bytes 10832 | tf_op jit(solution)/shard_map/ppermute | solution.py:145
  79.9 5.5 %collective-permute-start.19 = (f32[902]{0:T(1024)S(1)}, f32[902]{0:T(1024)S(1)}, u32[]{:S(2)}, u32[]{:S(2)}) collective-permute-start(f32[902]{0:T(1024)S(1)} %add_add_fusion.3), channel_id=1, source_target_pairs={{0,12},{1,13},{2,14},{3,15},{4,8},{5,9},{6,10},{7,11},{8,4},{9,5},... | collective-permute-start | bytes 10832 | tf_op jit(solution)/shard_map/ppermute | solution.py:145
  80.7 4.7 %collective-permute-start.18 = (f32[902]{0:T(1024)S(1)}, f32[902]{0:T(1024)S(1)}, u32[]{:S(2)}, u32[]{:S(2)}) collective-permute-start(f32[902]{0:T(1024)S(1)} %add_add_fusion.3), channel_id=1, source_target_pairs={{0,8},{1,9},{2,10},{3,11},{4,12},{5,13},{6,14},{7,15},{8,0},{9,1},... | collective-permute-start | bytes 10832 | tf_op jit(solution)/shard_map/ppermute | solution.py:145
  83.5 3.6 %collective-permute-start.17 = (f32[902]{0:T(1024)S(1)}, f32[902]{0:T(1024)S(1)}, u32[]{:S(2)}, u32[]{:S(2)}) collective-permute-start(f32[902]{0:T(1024)S(1)} %add_add_fusion.3), channel_id=1, source_target_pairs={{0,4},{1,5},{2,6},{3,7},{4,0},{5,1},{6,2},{7,3},{8,12},{9,13},{10,... | collective-permute-start | bytes 10832 | tf_op jit(solution)/shard_map/ppermute | solution.py:145
